TPU v7x, 32 devices: a whole 2x2x4 slice. The times are simulated.
32 devices in a mesh: groups: 2 (over x), ctx: 8 (over z, y), dp: 2 (over core).
Axes of the slice: x: 2, y: 2, z: 4, core: 2. Of those that a mesh axis runs over, the one named last changes fastest.
Arguments:
- query_rows: bfloat16 [4, 3072, 4096], P(('groups', 'dp'), 'ctx'), parts along dimension 0, may hold values from -6 to 6
- key_rows: bfloat16 [4, 3072, 4096], P(('groups', 'dp'), 'ctx'), parts along dimension 0, may hold values from -6 to 6
- value_rows: bfloat16 [4, 3072, 4096], P(('groups', 'dp'), 'ctx'), parts along dimension 0, may hold values from -6 to 6
- gain: float32 [4096], P('dp'), may hold values from 0.5 to 1.5
Outputs:
- normed: bfloat16 [4, 3072, 4096], P(('groups', 'dp'), 'ctx'), parts along dimension 0
There are 2 independent parts, one for each index of `groups`. A program takes and returns all parts, laid end to end along the dimension named above; an argument that names none is the same for every part. Nothing has to cross between parts.
All inputs are finite; a program needn't handle non-finite values.
Results may differ from a plain program's by a relative error of at most 0.0049.
Values may be sent and summed in bfloat16 or wider, within the bound.
No kernel may reach another device: no remote copies, remote signals or barrier semaphores. Data moves between devices by JAX's collectives and lax.ppermute only.
A program may use at most 192 MiB of HBM per device.

v0:
```python
import jax
import jax.numpy as jnp
from jax import lax
from jax.sharding import PartitionSpec as P

H = 32


def carried_in(value, axis, join, neutral):
    count, mine = (lax.axis_size(axis), lax.axis_index(axis))
    pieces = lax.all_gather(value, axis)
    so_far = jnp.full_like(value, 0) + jnp.asarray(neutral, value.dtype)

    def step(position, so_far):
        longer = join(so_far, pieces[position])
        return jnp.where(position < mine, longer, so_far)

    return lax.fori_loop(0, count - 1, step, so_far)


def attend_local(query, keyset, valset, state_bf):
    row_count = query.shape[1]
    causal_mask = jnp.arange(row_count)[:, None] >= jnp.arange(row_count)[None, :]
    scores = jnp.einsum("sthd,suhd->shtu", query, keyset, preferred_element_type=jnp.float32)
    weights = jnp.where(causal_mask, scores, 0.0).astype(jnp.bfloat16)
    within = jnp.einsum("shtu,suhe->sthe", weights, valset, preferred_element_type=jnp.float32)
    carried = jnp.einsum("sthd,shde->sthe", query, state_bf, preferred_element_type=jnp.float32)
    return within + carried


def add_states(earlier, later):
    return earlier + later


def shards(query_rows, key_rows, value_rows, gain):
    seq_count, row_count, feat_count = query_rows.shape
    head_size = feat_count // H
    full_gain = lax.all_gather(gain, "dp", axis=0, tiled=True)
    query = query_rows.reshape(seq_count, row_count, H, head_size)
    keyset = key_rows.reshape(seq_count, row_count, H, head_size)
    valset = value_rows.reshape(seq_count, row_count, H, head_size)
    state_terms = jnp.einsum("sthd,sthe->shde", keyset, valset, preferred_element_type=jnp.float32)
    prefix = carried_in(state_terms, "ctx", add_states, jnp.zeros_like(state_terms))
    attended = attend_local(query, keyset, valset, prefix.astype(jnp.bfloat16))
    attended = attended.reshape(seq_count, row_count, feat_count)
    scale = lax.rsqrt(jnp.mean(attended * attended, axis=-1, keepdims=True) + 1e-05)
    return (attended * scale * full_gain).astype(jnp.bfloat16)


def solution(mesh):
    in_specs = (
        P(("groups", "dp"), "ctx", None),
        P(("groups", "dp"), "ctx", None),
        P(("groups", "dp"), "ctx", None),
        P("dp"),
    )
    out_specs = P(("groups", "dp"), "ctx", None)
    return jax.shard_map(shards, mesh=mesh, in_specs=in_specs, out_specs=out_specs, check_vma=False)
```

profile of v0, /device:TPU:30, one launch (start us, length us, event | category | flops | bytes accessed | tf_op | source)
XLA Modules:
  0.0 290.7 jit_solution(6800529169445532872)
XLA Ops:
  6.5 0.0 all-gather.3.cloned.1.call-start
  6.5 4.7 %copy.20 = bf16[1,384,4096]{1,2,0:T(8,128)(2,1)} copy(bf16[1,384,4096]{2,1,0:T(8,128)(2,1)} %param.7) | data formatting | bytes 6291456 | tf_op jit(solution)/shard_map/reshape.1
  11.2 0.0 copy-start
  11.2 2.9 copy.22
  14.1 0.0 copy-start.1
  14.1 1.6 copy-done.1
  15.8 0.0 copy-done
  15.8 3.8 %fusion.11 = f32[32,128,128]{2,1,0:T(8,128)} fusion(bf16[384,32,128]{0,2,1:T(8,128)(2,1)S(1)} %bitcast.35, bf16[384,32,128]{2,1,0:T(8,128)(2,1)S(1)} %bitcast.36), kind=kOutput, calls=%fused_computation.14 | convolution fusion | flops 402653184 | bytes 8388608 | tf_op jit(solution)/shard_map/sthd,sthe->shde/dot_general | solution.py:42
  19.6 0.0 all-gather.3.cloned.1.call-update
  19.6 0.0 copy-start.2
  19.6 4.4 %copy.21 = bf16[48,8,32,128]{3,2,1,0:T(8,128)(2,1)} copy(bf16[48,8,32,128]{3,1,2,0:T(8,128)(2,1)} %bitcast.40) | data formatting | bytes 6291456
  24.0 0.0 copy-done.2
  24.0 2.0 all_gather.11
  26.1 10.4 %fusion = f32[32,384,128]{1,2,0:T(8,128)} fusion(pred[384,384]{1,0:T(8,128)(4,1)S(1)} %iota_compare_fusion, bf16[384,32,128]{0,2,1:T(8,128)(2,1)} %bitcast.34, bf16[384,32,128]{2,1,0:T(8,128)(2,1)} %bitcast.32, bf16[384,32,128]{2,1,0:T(8,128)(2,1)} %bitcast.37), kind=kOutput, calls=%fused_computation.2 | convolution fusion | flops 2425356288 | bytes 15876096 | tf_op jit(solution)/shard_map/shtu,suhe->sthe/dot_general | solution.py:26
  36.5 208.9 %all-gather.3.cloned.1.call-done = f32[256,128,128]{2,1,0:T(8,128)} async-done(((f32[32,128,128]{2,1,0:T(8,128)}), f32[256,128,128]{2,1,0:T(8,128)}) %all-gather.3.cloned.1.call-update) | async-done | bytes 16777232 | tf_op jit(solution)/shard_map/all_gather | solution.py:11
  245.4 16.3 %while.14 = (s32[]{:T(128)}, f32[1,32,128,128]{3,2,1,0:T(8,128)S(1)}, s32[]{:T(128)}, f32[8,1,32,128,128]{4,3,2,1,0:T(8,128)}, s32[]{:T(128)}, /*index=5*/s32[]{:T(128)}) while((s32[]{:T(128)}, f32[1,32,128,128]{3,2,1,0:T(8,128)S(1)}, s32[]{:T(128)}, f32[8,1,32,128,128]{4,3,2,1,0:T(8,128)}, s32[]{:T(128)}, ...), condition=%wide.region_1.2_spmd.clone, body=%wide.region_0.1_spmd.clone.sunk | while | flops 1572868 | bytes 6291549 | solution.py:18
  245.4 2.3 add_select_fusion.2
  247.7 2.3 add_select_fusion.2
  250.1 2.3 add_select_fusion.2
  252.4 2.3 add_select_fusion.2
  254.8 2.3 add_select_fusion.2
  257.1 2.3 add_select_fusion.2
  259.4 2.3 add_select_fusion.2
  261.8 10.1 %fusion.3 = (f32[384]{0:T(512)S(1)}, f32[32,128,384]{2,1,0:T(8,128)}) fusion(bf16[384,32,128]{2,1,0:T(8,128)(2,1)} %bitcast.33, f32[1,32,128,128]{3,2,1,0:T(8,128)S(1)} %get-tuple-element.84, f32[32,384,128]{1,2,0:T(8,128)} %fusion), kind=kOutput, calls=%fused_computation.6 | convolution fusion | flops 407895680 | bytes 17827328 | tf_op jit(solution)/shard_map/sthd,shde->sthe/dot_general | solution.py:27
  271.9 6.6 %copy.18 = f32[1,384,4096]{2,1,0:T(8,128)} copy(f32[1,384,4096]{1,2,0:T(8,128)} %bitcast.31) | data formatting | bytes 12582912 | tf_op jit(solution)/shard_map/reshape | solution.py:45
  278.5 5.4 %multiply_convert_fusion = bf16[1,384,4096]{2,1,0:T(8,128)(2,1)} fusion(f32[1,384,4096]{2,1,0:T(8,128)} %copy.18, f32[4096]{0:T(1024)S(1)} %all_gather.11, f32[384]{0:T(512)S(1)} %add_rsqrt_fusion), kind=kLoop, calls=%fused_computation.8 | loop fusion | flops 4718592 | bytes 9455104 | tf_op jit(solution)/shard_map/convert_element_type | solution.py:47
  (3 shorter events, 0.1 us)
Async XLA Ops:
  6.5 238.9 %all-gather.3.cloned.1.call-start = ((), (), s32[]{:S(2)}) async-start(), calls=%async_computation | async-start | bytes 18874368 | tf_op jit(solution)/shard_map/all_gather | solution.py:11
  11.2 4.5 %copy-start = (bf16[1,384,4096]{1,2,0:T(8,128)(2,1)S(1)}, bf16[1,384,4096]{1,2,0:T(8,128)(2,1)}, u32[]{:S(2)}) copy-start(bf16[1,384,4096]{1,2,0:T(8,128)(2,1)} %copy.20) | copy-start | bytes 9437188
  14.1 1.6 copy-start.1
  19.6 4.4 %copy-start.2 = (f32[2048]{0:T(1024)S(1)}, f32[2048]{0:T(1024)}, u32[]{:S(2)}) copy-start(f32[2048]{0:T(1024)} %param.9) | copy-start | bytes 24580
Sparse Core Ops, SparseCore 0:
  19.7 225.6 all-gather.2
where the time goes:
time: 296 us; the launch traced here: 291 us
  waiting for transfers between devices  209 us (71%)
  matrix products  24.4 us (8%)
  other arithmetic  21.6 us (7%)
  local copies, waits for them, and re-layouts  20.2 us (7%)
  between operations  13.4 us (5%)
    all_gather x1, waiting for transfers between devices, carried_in(): pieces = lax.all_gather(value, axis)  209 us
    select_n x7, other arithmetic, step(): return jnp.where(position < mine, longer, so_far)  16.2 us
    dot_general x1, matrix products, attend_local(): jnp.einsum('shtu,suhe->sthe', weights, valset, preferred_element_type=jnp...  10.4 us
    dot_general x1, matrix products, attend_local(): jnp.einsum('sthd,shde->sthe', query, state_bf, preferred_element_type=jnp...  10.1 us
    unnamed x8, local copies, waits for them, and re-layouts  8.93 us
    reshape x1, local copies, waits for them, and re-layouts, shards(): attended = attended.reshape(seq_count, row_count, feat_count)  6.58 us
  transfers between devices with their start and end apart: 1, of which 1 were waited for; matrix products, arithmetic and copies ran while one was open for 5% of the time, Pallas kernels for 0%

commit v1 on v0

v1 whole, which is shorter than its diff:
```python
import jax
import jax.numpy as jnp
from jax import lax
from jax.sharding import PartitionSpec as P

H = 32


def pair_chain_prefix(terms, axis):
    count = lax.axis_size(axis)
    mine_at = lax.axis_index(axis) % 2
    half = terms.shape[0] // 2
    pairs = count // 2
    mine = lax.dynamic_slice_in_dim(terms, mine_at * half, half, 0)
    other = lax.dynamic_slice_in_dim(terms, (1 - mine_at) * half, half, 0)
    swap = [(2 * i, 2 * i + 1) for i in range(pairs)] + [(2 * i + 1, 2 * i) for i in range(pairs)]
    got = lax.ppermute(other, axis, swap)
    total = mine + got
    carried = jnp.zeros_like(total)
    for hop in range(1, pairs):
        links = [(2 * (hop - 1) + side, 2 * hop + side) for side in range(2)]
        carried = carried + lax.ppermute(carried + total, axis, links)
    first = mine_at == 0
    keep = (carried + jnp.where(first, 0.0, got)).astype(jnp.bfloat16)
    send = (carried + jnp.where(first, mine, 0.0)).astype(jnp.bfloat16)
    back = lax.ppermute(send, axis, swap)
    low = jnp.where(first, keep, back)
    high = jnp.where(first, back, keep)
    return jnp.concatenate([low, high], axis=0)


def shards(query_rows, key_rows, value_rows, gain):
    seq_count, row_count, feat_count = query_rows.shape
    head_size = feat_count // H
    full_gain = lax.all_gather(gain, "dp", axis=0, tiled=True)
    query = query_rows.reshape(row_count, H, head_size)
    keyset = key_rows.reshape(row_count, H, head_size)
    valset = value_rows.reshape(row_count, H, head_size)
    state_terms = jnp.einsum("thd,the->hde", keyset, valset, preferred_element_type=jnp.float32)
    prefix_bf = pair_chain_prefix(state_terms, "ctx")
    causal_mask = jnp.arange(row_count)[:, None] >= jnp.arange(row_count)[None, :]
    scores = jnp.einsum("thd,uhd->htu", query, keyset, preferred_element_type=jnp.float32)
    weights = jnp.where(causal_mask, scores, 0.0).astype(jnp.bfloat16)
    within = jnp.einsum("htu,uhe->the", weights, valset, preferred_element_type=jnp.float32)
    carried = jnp.einsum("thd,hde->the", query, prefix_bf, preferred_element_type=jnp.float32)
    attended = (within + carried).reshape(seq_count, row_count, feat_count)
    scale = lax.rsqrt(jnp.mean(attended * attended, axis=-1, keepdims=True) + 1e-05)
    return (attended * scale * full_gain).astype(jnp.bfloat16)


def solution(mesh):
    in_specs = (
        P(("groups", "dp"), "ctx", None),
        P(("groups", "dp"), "ctx", None),
        P(("groups", "dp"), "ctx", None),
        P("dp"),
    )
    out_specs = P(("groups", "dp"), "ctx", None)
    return jax.shard_map(shards, mesh=mesh, in_specs=in_specs, out_specs=out_specs, check_vma=False)
```

time: 296 us -> 149 us (0.50); the launches traced: 291 us -> 147 us
  waiting for transfers between devices: 209 us -> 87.2 us
  between operations: 13.4 us -> 0.1 us
  other arithmetic: 21.6 us -> 10.9 us
  starting transfers between devices: 0.01 us -> 3.72 us
    all_gather x1 -> x0, waiting for transfers between devices: 209 us -> none  [carried_in(): pieces = lax.all_gather(value, axis)]
    ppermute x0 -> x5, waiting for transfers between devices: none -> 87.2 us  [the longest x3 62.5 us: pair_chain_prefix(): carried = carried + lax.ppermute(carried + total, axis, links)]
    select_n x7 -> x2, other arithmetic: 16.2 us -> 1.74 us  [the longest x1 1.67 us: pair_chain_prefix(): low = jnp.where(first, keep, back)]
    reshape x1 -> x2, local copies, waits for them, and re-layouts: 6.58 us -> 11.6 us  [the longest x1 6.64 us: shards(): attended = (within + carried).reshape(seq_count, row_count, feat_count)]
    another operation x1 -> x0, local copies, waits for them, and re-layouts: 4.71 us -> none
    ppermute x0 -> x5, starting transfers between devices: none -> 3.72 us  [the longest x3 2.72 us: pair_chain_prefix(): carried = carried + lax.ppermute(carried + total, axis, links)]
    unnamed x8 -> x12, local copies, waits for them, and re-layouts: 8.93 us -> 7.34 us
  transfers between devices with their start and end apart: 1 -> 5, of which waited for: 1 -> 3; matrix products, arithmetic and copies ran while one was open for 5% -> 10% of each run, Pallas kernels for 0% -> 0%
where the time goes in v1:
time: 149 us; the launch traced here: 147 us
  waiting for transfers between devices  87.2 us (59%)
  matrix products  23.5 us (16%)
  local copies, waits for them, and re-layouts  19.9 us (13%)
  other arithmetic  10.9 us (7%)
  starting transfers between devices  3.72 us (2%)
  blocking collectives  1.98 us (1%)
    ppermute x3, waiting for transfers between devices, pair_chain_prefix(): carried = carried + lax.ppermute(carried + total, axis, links)  62.5 us
    ppermute x1, waiting for transfers between devices, pair_chain_prefix(): got = lax.ppermute(other, axis, swap)  24.6 us
    dot_general x1, matrix products, shards(): jnp.einsum('htu,uhe->the', weights, valset, preferred_element_type=jnp.fl...  10.2 us
    dot_general x1, matrix products, shards(): jnp.einsum('thd,hde->the', query, prefix_bf, preferred_element_type=jnp.f...  8 us
    unnamed x12, local copies, waits for them, and re-layouts  7.34 us
    reshape x1, local copies, waits for them, and re-layouts, shards(): attended = (within + carried).reshape(seq_count, row_count, feat_count)  6.64 us
    convert_element_type x1, other arithmetic, shards(): return (attended * scale * full_gain).astype(jnp.bfloat16)  5.42 us
    dot_general x1, matrix products, shards(): jnp.einsum('thd,the->hde', keyset, valset, preferred_element_type=jnp.flo...  5.3 us
  transfers between devices with their start and end apart: 5, of which 3 were waited for; matrix products, arithmetic and copies ran while one was open for 10% of the time, Pallas kernels for 0%

profile of v1, /device:TPU:30, one launch (start us, length us, event | category | flops | bytes accessed | tf_op | source)
XLA Modules:
  0.0 147.3 jit_solution(9963254534458489159)
XLA Ops:
  0.0 0.0 copy-start.3
  0.0 4.9 %copy.18 = bf16[1,384,4096]{1,2,0:T(8,128)(2,1)} copy(bf16[1,384,4096]{2,1,0:T(8,128)(2,1)} %param.5) | data formatting | bytes 6291456 | tf_op jit(solution)/shard_map/reshape | solution.py:37
  4.9 0.0 copy-done.3
  4.9 2.5 %copy.20 = bf16[48,8,32,128]{3,2,1,0:T(8,128)(2,1)} copy(bf16[48,8,32,128]{3,1,2,0:T(8,128)(2,1)S(1)} %bitcast.21) | data formatting | bytes 6291456
  7.4 5.3 %fusion.10 = f32[32,128,128]{2,1,0:T(8,128)S(1)} fusion(bf16[384,32,128]{0,2,1:T(8,128)(2,1)} %bitcast.17, bf16[384,32,128]{2,1,0:T(8,128)(2,1)} %bitcast.19), kind=kOutput, calls=%fused_computation.12 | convolution fusion | flops 402653184 | bytes 8388608 | tf_op jit(solution)/shard_map/thd,the->hde/dot_general | solution.py:39
  12.7 1.0 constant_dynamic-slice_fusion
  13.8 0.5 collective-permute-start
  14.3 24.6 %collective-permute-done = f32[16,128,128]{2,1,0:T(8,128)S(1)} collective-permute-done((f32[16,128,128]{2,1,0:T(8,128)}, f32[16,128,128]{2,1,0:T(8,128)S(1)}, u32[]{:S(2)}, u32[]{:S(2)}) %collective-permute-start) | collective-permute-done | bytes 1048608 | tf_op jit(solution)/shard_map/ppermute | solution.py:17
  38.9 0.0 copy-start.1
  38.9 0.1 dynamic-slice_add_fusion
  39.0 0.7 collective-permute-start.1
  39.8 0.0 collective-permute-done.1
  39.8 0.1 add.49
  39.9 0.1 copy-done.1
  39.9 0.7 collective-permute-start.2
  40.7 0.0 collective-permute-done.2
  40.7 1.2 fusion.19
  41.9 1.3 collective-permute-start.3
  43.1 0.0 copy-start.4
  43.2 4.4 %copy.19 = bf16[48,8,32,128]{3,2,1,0:T(8,128)(2,1)} copy(bf16[48,8,32,128]{3,1,2,0:T(8,128)(2,1)} %bitcast.22) | data formatting | bytes 6291456
  47.6 0.0 copy-done.4
  47.6 2.0 %all_gather.3 = f32[4096]{0:T(1024)S(1)} all-gather(f32[2048]{0:T(1024)S(1)} %copy-done.4), channel_id=1, replica_groups=mesh['groups'=2,'ctx'=8,'dp'=2] {'dp'}, dimensions={0}, use_global_device_ids=true | all-gather | bytes 24576 | tf_op jit(solution)/shard_map/all_gather | solution.py:35
  49.6 62.5 %collective-permute-done.3 = f32[16,128,128]{2,1,0:T(8,128)} collective-permute-done((f32[16,128,128]{2,1,0:T(8,128)}, f32[16,128,128]{2,1,0:T(8,128)}, u32[]{:S(2)}, u32[]{:S(2)}) %collective-permute-start.3) | collective-permute-done | bytes 1048608 | tf_op jit(solution)/shard_map/ppermute | solution.py:22
  112.1 2.2 %add_convert_fusion = bf16[16,128,128]{2,1,0:T(8,128)(2,1)} fusion(f32[32,128,128]{2,1,0:T(8,128)S(1)} %fusion.10, s32[]{:T(128)S(6)} %select_n.44, pred[]{:T(512)S(6)} %eq.5, f32[16,128,128]{2,1,0:T(8,128)S(1)} %get-tuple-element.8, f32[16,128,128]{2,1,0:T(8,128)} %collective-permute-done.3), kind=kLoop, calls=%fused_computation.17 | loop fusion | flops 1048576 | bytes 3670021 | tf_op jit(solution)/shard_map/convert_element_type | solution.py:25
  114.3 0.5 collective-permute-start.4
  114.8 0.0 copy-start.2
  114.8 10.2 %fusion = f32[32,384,128]{1,2,0:T(8,128)} fusion(pred[384,384]{1,0:T(8,128)(4,1)S(1)} %iota_compare_fusion, bf16[384,32,128]{0,2,1:T(8,128)(2,1)} %bitcast.18, bf16[384,32,128]{2,1,0:T(8,128)(2,1)} %bitcast.15, bf16[384,32,128]{2,1,0:T(8,128)(2,1)} %bitcast.20), kind=kOutput, calls=%fused_computation.1 | convolution fusion | flops 2425356288 | bytes 15876096 | tf_op jit(solution)/shard_map/htu,uhe->the/dot_general | solution.py:44
  125.0 0.0 copy-start
  125.0 0.1 collective-permute-done.4
  125.1 0.0 copy-done.2
  125.1 1.7 %broadcast_select_fusion.1 = (bf16[16,128,128]{2,1,0:T(8,128)(2,1)S(1)}, bf16[16,128,128]{2,1,0:T(8,128)(2,1)S(1)}) fusion(bf16[16,128,128]{2,1,0:T(8,128)(2,1)S(1)} %collective-permute-done.4, pred[]{:T(512)S(6)} %eq.5, f32[16,128,128]{2,1,0:T(8,128)S(1)} %copy-done.2, f32[16,128,128]{2,1,0:T(8,128)S(1)} %get-tuple-element.8, ...), kind=kLoop, calls=%fused_computation.22 | loop fusion | flops 1310720 | bytes 4718593 | tf_op jit(solution)/shard_map/jit(_where)/select_n | solution.py:27
  126.8 0.1 broadcast_select_fusion
  126.9 0.4 copy-done
  127.2 8.0 %multiply_reduce_fusion = (f32[384]{0:T(512)S(1)}, f32[384,32,128]{0,2,1:T(8,128)}) fusion(bf16[384,32,128]{2,1,0:T(8,128)(2,1)S(1)} %bitcast.16, bf16[16,128,128]{2,1,0:T(8,128)(2,1)S(1)} %broadcast_select_fusion, bf16[16,128,128]{2,1,0:T(8,128)(2,1)S(1)} %get-tuple-element.5, f32[32,384,128]{1,2,0:T(8,128)} %fusion), kind=kOutput, calls=%fused_computation.6 | convolution fusion | flops 407895680 | bytes 16778752 | tf_op jit(solution)/shard_map/thd,hde->the/dot_general | solution.py:45
  135.2 6.6 %copy.16 = f32[1,384,4096]{2,1,0:T(8,128)} copy(f32[1,384,4096]{1,2,0:T(8,128)} %bitcast.14) | data formatting | bytes 12582912 | tf_op jit(solution)/shard_map/reshape | solution.py:46
  141.8 5.4 %multiply_convert_fusion = bf16[1,384,4096]{2,1,0:T(8,128)(2,1)} fusion(f32[1,384,4096]{2,1,0:T(8,128)} %copy.16, f32[4096]{0:T(1024)S(1)} %all_gather.3, f32[384]{0:T(512)S(1)} %add_rsqrt_fusion), kind=kLoop, calls=%fused_computation.5 | loop fusion | flops 4718592 | bytes 9455104 | tf_op jit(solution)/shard_map/convert_element_type | solution.py:48
  (2 shorter events, 0.0 us)
Async XLA Ops:
  0.0 4.9 %copy-start.3 = (bf16[1,384,4096]{2,1,0:T(8,128)(2,1)S(1)}, bf16[1,384,4096]{2,1,0:T(8,128)(2,1)}, u32[]{:S(2)}) copy-start(bf16[1,384,4096]{2,1,0:T(8,128)(2,1)} %param.6) | copy-start | bytes 9437188
  13.8 25.1 %collective-permute-start = (f32[16,128,128]{2,1,0:T(8,128)}, f32[16,128,128]{2,1,0:T(8,128)S(1)}, u32[]{:S(2)}, u32[]{:S(2)}) collective-permute-start(f32[16,128,128]{2,1,0:T(8,128)} %constant_dynamic-slice_fusion), channel_id=1, source_target_pairs={{0,2},{4,6},{8,10},{12,14},{2,0},{6,4},{10,8},{14,12},{1,3},{5,7},... | collective-permute-start | bytes 3145736 | tf_op jit(solution)/shard_map/ppermute | solution.py:17
  38.9 1.1 copy-start.1
  39.0 0.7 collective-permute-start.1
  39.9 0.7 collective-permute-start.2
  41.9 70.2 %collective-permute-start.3 = (f32[16,128,128]{2,1,0:T(8,128)}, f32[16,128,128]{2,1,0:T(8,128)}, u32[]{:S(2)}, u32[]{:S(2)}) collective-permute-start(f32[16,128,128]{2,1,0:T(8,128)} %get-tuple-element.7), channel_id=1, source_target_pairs={{8,12},{10,14},{9,13},{11,15},{24,28},{26,30},{25,29},{27,31}} | collective-permute-start | bytes 3145736 | tf_op jit(solution)/shard_map/ppermute | solution.py:22
  43.1 4.4 %copy-start.4 = (f32[2048]{0:T(1024)S(1)}, f32[2048]{0:T(1024)}, u32[]{:S(2)}) copy-start(f32[2048]{0:T(1024)} %param.7) | copy-start | bytes 24580
  114.3 10.8 %collective-permute-start.4 = (bf16[16,128,128]{2,1,0:T(8,128)(2,1)}, bf16[16,128,128]{2,1,0:T(8,128)(2,1)S(1)}, u32[]{:S(2)}, u32[]{:S(2)}) collective-permute-start(bf16[16,128,128]{2,1,0:T(8,128)(2,1)} %add_convert_fusion), channel_id=1, source_target_pairs={{0,2},{4,6},{8,10},{12,14},{2,0},{6,4},{10,8},{14,12},{1,3},{5,7},... | collective-permute-start | bytes 1572872 | tf_op jit(solution)/shard_map/ppermute | solution.py:26
  114.8 10.3 %copy-start.2 = (f32[16,128,128]{2,1,0:T(8,128)S(1)}, f32[16,128,128]{2,1,0:T(8,128)}, u32[]{:S(2)}) copy-start(f32[16,128,128]{2,1,0:T(8,128)} %copy-done.1) | copy-start | bytes 3145732
  125.0 2.2 %copy-start = (bf16[48,8,32,128]{3,2,1,0:T(8,128)(2,1)S(1)}, bf16[48,8,32,128]{3,2,1,0:T(8,128)(2,1)}, u32[]{:S(2)}) copy-start(bf16[48,8,32,128]{3,2,1,0:T(8,128)(2,1)} %copy.19) | copy-start | bytes 9437188

commit v2 on v1

--- a/solution.py
+++ b/solution.py
@@ -6,24 +6,30 @@
 H = 32
 
 
-def pair_chain_prefix(terms, axis):
+def pair_chain_prefix(terms, axis, pieces):
     count = lax.axis_size(axis)
     mine_at = lax.axis_index(axis) % 2
+    first = mine_at == 0
     half = terms.shape[0] // 2
     pairs = count // 2
-    mine = lax.dynamic_slice_in_dim(terms, mine_at * half, half, 0)
-    other = lax.dynamic_slice_in_dim(terms, (1 - mine_at) * half, half, 0)
+    mine_all = lax.dynamic_slice_in_dim(terms, mine_at * half, half, 0)
+    other_all = lax.dynamic_slice_in_dim(terms, (1 - mine_at) * half, half, 0)
     swap = [(2 * i, 2 * i + 1) for i in range(pairs)] + [(2 * i + 1, 2 * i) for i in range(pairs)]
-    got = lax.ppermute(other, axis, swap)
-    total = mine + got
-    carried = jnp.zeros_like(total)
-    for hop in range(1, pairs):
-        links = [(2 * (hop - 1) + side, 2 * hop + side) for side in range(2)]
-        carried = carried + lax.ppermute(carried + total, axis, links)
-    first = mine_at == 0
-    keep = (carried + jnp.where(first, 0.0, got)).astype(jnp.bfloat16)
-    send = (carried + jnp.where(first, mine, 0.0)).astype(jnp.bfloat16)
-    back = lax.ppermute(send, axis, swap)
+    step = half // pieces
+    keeps, backs = [], []
+    for piece in range(pieces):
+        mine = mine_all[piece * step:(piece + 1) * step]
+        got = lax.ppermute(other_all[piece * step:(piece + 1) * step], axis, swap)
+        total = mine + got
+        carried = jnp.zeros_like(total)
+        for hop in range(1, pairs):
+            links = [(2 * (hop - 1) + side, 2 * hop + side) for side in range(2)]
+            carried = carried + lax.ppermute(carried + total, axis, links)
+        keeps.append((carried + jnp.where(first, 0.0, got)).astype(jnp.bfloat16))
+        send = (carried + jnp.where(first, mine, 0.0)).astype(jnp.bfloat16)
+        backs.append(lax.ppermute(send, axis, swap))
+    keep = jnp.concatenate(keeps, axis=0)
+    back = jnp.concatenate(backs, axis=0)
     low = jnp.where(first, keep, back)
     high = jnp.where(first, back, keep)
     return jnp.concatenate([low, high], axis=0)
@@ -37,7 +43,7 @@
     keyset = key_rows.reshape(row_count, H, head_size)
     valset = value_rows.reshape(row_count, H, head_size)
     state_terms = jnp.einsum("thd,the->hde", keyset, valset, preferred_element_type=jnp.float32)
-    prefix_bf = pair_chain_prefix(state_terms, "ctx")
+    prefix_bf = pair_chain_prefix(state_terms, "ctx", 4)
     causal_mask = jnp.arange(row_count)[:, None] >= jnp.arange(row_count)[None, :]
     scores = jnp.einsum("thd,uhd->htu", query, keyset, preferred_element_type=jnp.float32)
     weights = jnp.where(causal_mask, scores, 0.0).astype(jnp.bfloat16)

time: 149 us -> 123 us (0.83)
  waiting for transfers between devices: 87.2 us -> 47 us
  starting transfers between devices: 3.72 us -> 17.7 us
  other arithmetic: 10.9 us -> 12.9 us
    ppermute x3 -> x12, waiting for transfers between devices: 62.5 us -> 17.8 us  [pair_chain_prefix(): carried = carried + lax.ppermute(carried + total, axis, links)]
    ppermute x3 -> x12, starting transfers between devices: 2.72 us -> 10.5 us  [pair_chain_prefix(): carried = carried + lax.ppermute(carried + total, axis, links)]
    ppermute x2 -> x8, starting transfers between devices: 0.99 us -> 7.21 us  [the longest x4 4.1 us: pair_chain_prefix(): backs.append(lax.ppermute(send, axis, swap))]
    ppermute x2 -> x8, waiting for transfers between devices: 24.7 us -> 29.2 us  [the longest x4 22.9 us: pair_chain_prefix(): got = lax.ppermute(other_all[piece * step:(piece + 1) * step], axis, swap)]
    add x2 -> x8, other arithmetic: 1.28 us -> 3.38 us  [pair_chain_prefix(): carried = carried + lax.ppermute(carried + total, axis, links)]
    select_n x1, other arithmetic: 1.67 us -> 0.1 us  [pair_chain_prefix(): low = jnp.where(first, keep, back)]
    unnamed x12 -> x29, local copies, waits for them, and re-layouts: 7.34 us -> 7.1 us
  transfers between devices with their start and end apart: 5 -> 20, of which waited for: 3 -> 10; matrix products, arithmetic and copies ran while one was open for 10% -> 16% of each run, Pallas kernels for 0% -> 0%
where the time goes in v2:
time: 123 us; the launch traced here: 122 us
  waiting for transfers between devices  47 us (38%)
  matrix products  23.6 us (19%)
  local copies, waits for them, and re-layouts  18.5 us (15%)
  starting transfers between devices  17.7 us (14%)
  other arithmetic  12.9 us (10%)
  blocking collectives  2.12 us (2%)
    ppermute x4, waiting for transfers between devices, pair_chain_prefix(): got = lax.ppermute(other_all[piece * step:(piece + 1) * step], axis, swap)  22.9 us
    ppermute x12, waiting for transfers between devices, pair_chain_prefix(): carried = carried + lax.ppermute(carried + total, axis, links)  17.8 us
    ppermute x12, starting transfers between devices, pair_chain_prefix(): carried = carried + lax.ppermute(carried + total, axis, links)  10.5 us
    dot_general x1, matrix products, shards(): jnp.einsum('htu,uhe->the', weights, valset, preferred_element_type=jnp.fl...  10.3 us
    dot_general x1, matrix products, shards(): jnp.einsum('thd,hde->the', query, prefix_bf, preferred_element_type=jnp.f...  8.02 us
    unnamed x29, local copies, waits for them, and re-layouts  7.1 us
    reshape x1, local copies, waits for them, and re-layouts, shards(): attended = (within + carried).reshape(seq_count, row_count, feat_count)  6.61 us
    ppermute x4, waiting for transfers between devices, pair_chain_prefix(): backs.append(lax.ppermute(send, axis, swap))  6.24 us
  transfers between devices with their start and end apart: 20, of which 10 were waited for; matrix products, arithmetic and copies ran while one was open for 16% of the time, Pallas kernels for 0%

profile of v2, /device:TPU:30, one launch (start us, length us, event | category | flops | bytes accessed | tf_op | source)
XLA Modules:
  0.0 122.2 jit_solution(8917186867232386033)
XLA Ops:
  0.0 4.8 %copy.18 = bf16[1,384,4096]{1,2,0:T(8,128)(2,1)} copy(bf16[1,384,4096]{2,1,0:T(8,128)(2,1)} %param.5) | data formatting | bytes 6291456 | tf_op jit(solution)/shard_map/reshape | solution.py:43
  4.8 2.5 %copy.20 = bf16[48,8,32,128]{3,2,1,0:T(8,128)(2,1)} copy(bf16[48,8,32,128]{3,1,2,0:T(8,128)(2,1)S(1)} %bitcast.21) | data formatting | bytes 6291456
  7.3 5.3 %fusion.10 = f32[32,128,128]{2,1,0:T(8,128)S(1)} fusion(bf16[384,32,128]{0,2,1:T(8,128)(2,1)} %bitcast.17, bf16[384,32,128]{2,1,0:T(8,128)(2,1)} %bitcast.19), kind=kOutput, calls=%fused_computation.12 | convolution fusion | flops 402653184 | bytes 8388608 | tf_op jit(solution)/shard_map/thd,the->hde/dot_general | solution.py:45
  12.7 0.6 collective-permute-start.12
  13.2 7.5 %collective-permute-done.12 = f32[4,128,128]{2,1,0:T(8,128)S(1)} collective-permute-done((f32[4,128,128]{2,1,0:T(8,128)S(1)}, f32[4,128,128]{2,1,0:T(8,128)S(1)}, u32[]{:S(2)}, u32[]{:S(2)}) %collective-permute-start.12) | collective-permute-done | bytes 262176 | tf_op jit(solution)/shard_map/ppermute | solution.py:22
  20.8 0.9 dynamic-slice_add_fusion
  21.7 0.5 collective-permute-start
  22.2 1.5 %collective-permute-start.4 = (f32[4,128,128]{2,1,0:T(8,128)}, f32[4,128,128]{2,1,0:T(8,128)S(1)}, u32[]{:S(2)}, u32[]{:S(2)}) collective-permute-start(f32[4,128,128]{2,1,0:T(8,128)} %get-tuple-element.19), channel_id=1, source_target_pairs={{0,2},{4,6},{8,10},{12,14},{2,0},{6,4},{10,8},{14,12},{1,3},{5,7},... | collective-permute-start | bytes 786440 | tf_op jit(solution)/shard_map/ppermute | solution.py:22
  23.7 0.5 collective-permute-start.8
  24.2 0.7 collective-permute-start.13
  24.9 6.2 %collective-permute-done = f32[4,128,128]{2,1,0:T(8,128)S(1)} collective-permute-done((f32[4,128,128]{2,1,0:T(8,128)}, f32[4,128,128]{2,1,0:T(8,128)S(1)}, u32[]{:S(2)}, u32[]{:S(2)}) %collective-permute-start) | collective-permute-done | bytes 262176 | tf_op jit(solution)/shard_map/ppermute | solution.py:22
  31.1 5.6 %collective-permute-done.4 = f32[4,128,128]{2,1,0:T(8,128)S(1)} collective-permute-done((f32[4,128,128]{2,1,0:T(8,128)}, f32[4,128,128]{2,1,0:T(8,128)S(1)}, u32[]{:S(2)}, u32[]{:S(2)}) %collective-permute-start.4) | collective-permute-done | bytes 262176 | tf_op jit(solution)/shard_map/ppermute | solution.py:22
  36.8 3.5 %collective-permute-done.8 = f32[4,128,128]{2,1,0:T(8,128)S(1)} collective-permute-done((f32[4,128,128]{2,1,0:T(8,128)S(1)}, f32[4,128,128]{2,1,0:T(8,128)S(1)}, u32[]{:S(2)}, u32[]{:S(2)}) %collective-permute-start.8) | collective-permute-done | bytes 262176 | tf_op jit(solution)/shard_map/ppermute | solution.py:22
  40.3 0.1 dynamic-slice_add_fusion.1
  40.4 0.7 collective-permute-start.9
  41.1 0.7 collective-permute-start.5
  41.8 0.7 collective-permute-start.1
  42.5 0.7 collective-permute-start.14
  43.2 0.7 collective-permute-start.10
  44.0 0.7 collective-permute-start.6
  44.7 0.7 collective-permute-start.2
  45.4 0.8 fusion.19
  46.2 1.3 %collective-permute-start.15 = (f32[4,128,128]{2,1,0:T(8,128)}, f32[4,128,128]{2,1,0:T(8,128)}, u32[]{:S(2)}, u32[]{:S(2)}) collective-permute-start(f32[4,128,128]{2,1,0:T(8,128)} %get-tuple-element.5), channel_id=1, source_target_pairs={{8,12},{10,14},{9,13},{11,15},{24,28},{26,30},{25,29},{27,31}} | collective-permute-start | bytes 786440 | tf_op jit(solution)/shard_map/ppermute | solution.py:27
  47.5 0.8 fusion.20
  48.2 1.3 %collective-permute-start.11 = (f32[4,128,128]{2,1,0:T(8,128)}, f32[4,128,128]{2,1,0:T(8,128)}, u32[]{:S(2)}, u32[]{:S(2)}) collective-permute-start(f32[4,128,128]{2,1,0:T(8,128)} %get-tuple-element.7), channel_id=1, source_target_pairs={{8,12},{10,14},{9,13},{11,15},{24,28},{26,30},{25,29},{27,31}} | collective-permute-start | bytes 786440 | tf_op jit(solution)/shard_map/ppermute | solution.py:27
  49.5 0.8 fusion.21
  50.4 1.3 %collective-permute-start.7 = (f32[4,128,128]{2,1,0:T(8,128)}, f32[4,128,128]{2,1,0:T(8,128)}, u32[]{:S(2)}, u32[]{:S(2)}) collective-permute-start(f32[4,128,128]{2,1,0:T(8,128)} %get-tuple-element.9), channel_id=1, source_target_pairs={{8,12},{10,14},{9,13},{11,15},{24,28},{26,30},{25,29},{27,31}} | collective-permute-start | bytes 786440 | tf_op jit(solution)/shard_map/ppermute | solution.py:27
  51.7 0.9 fusion.22
  52.5 1.3 %collective-permute-start.3 = (f32[4,128,128]{2,1,0:T(8,128)}, f32[4,128,128]{2,1,0:T(8,128)}, u32[]{:S(2)}, u32[]{:S(2)}) collective-permute-start(f32[4,128,128]{2,1,0:T(8,128)} %get-tuple-element.11), channel_id=1, source_target_pairs={{8,12},{10,14},{9,13},{11,15},{24,28},{26,30},{25,29},{27,31}} | collective-permute-start | bytes 786440 | tf_op jit(solution)/shard_map/ppermute | solution.py:27
  53.9 4.5 %copy.19 = bf16[48,8,32,128]{3,2,1,0:T(8,128)(2,1)} copy(bf16[48,8,32,128]{3,1,2,0:T(8,128)(2,1)} %bitcast.22) | data formatting | bytes 6291456
  58.3 0.7 iota_compare_fusion
  59.0 4.0 %collective-permute-done.15 = f32[4,128,128]{2,1,0:T(8,128)} collective-permute-done((f32[4,128,128]{2,1,0:T(8,128)}, f32[4,128,128]{2,1,0:T(8,128)}, u32[]{:S(2)}, u32[]{:S(2)}) %collective-permute-start.15) | collective-permute-done | bytes 262176 | tf_op jit(solution)/shard_map/ppermute | solution.py:27
  63.0 5.4 %collective-permute-done.11 = f32[4,128,128]{2,1,0:T(8,128)} collective-permute-done((f32[4,128,128]{2,1,0:T(8,128)}, f32[4,128,128]{2,1,0:T(8,128)}, u32[]{:S(2)}, u32[]{:S(2)}) %collective-permute-start.11) | collective-permute-done | bytes 262176 | tf_op jit(solution)/shard_map/ppermute | solution.py:27
  68.4 5.5 %collective-permute-done.7 = f32[4,128,128]{2,1,0:T(8,128)} collective-permute-done((f32[4,128,128]{2,1,0:T(8,128)}, f32[4,128,128]{2,1,0:T(8,128)}, u32[]{:S(2)}, u32[]{:S(2)}) %collective-permute-start.7) | collective-permute-done | bytes 262176 | tf_op jit(solution)/shard_map/ppermute | solution.py:27
  74.0 2.8 %collective-permute-done.3 = f32[4,128,128]{2,1,0:T(8,128)} collective-permute-done((f32[4,128,128]{2,1,0:T(8,128)}, f32[4,128,128]{2,1,0:T(8,128)}, u32[]{:S(2)}, u32[]{:S(2)}) %collective-permute-start.3) | collective-permute-done | bytes 262176 | tf_op jit(solution)/shard_map/ppermute | solution.py:27
  76.8 2.3 %add_convert_fusion = (bf16[4,128,128]{2,1,0:T(8,128)(2,1)}, bf16[4,128,128]{2,1,0:T(8,128)(2,1)}, bf16[4,128,128]{2,1,0:T(8,128)(2,1)}, bf16[4,128,128]{2,1,0:T...) fusion(f32[32,128,128]{2,1,0:T(8,128)S(1)} %fusion.10, ...), kind=kLoop, calls=%fused_computation.21 | loop fusion | flops 1835008 | bytes 5242897 | tf_op jit(solution)/shard_map/convert_element_type | solution.py:29
  79.1 0.5 collective-permute-start.16
  79.6 1.5 %collective-permute-start.17 = (bf16[4,128,128]{2,1,0:T(8,128)(2,1)}, bf16[4,128,128]{2,1,0:T(8,128)(2,1)S(1)}, u32[]{:S(2)}, u32[]{:S(2)}) collective-permute-start(bf16[4,128,128]{2,1,0:T(8,128)(2,1)} %get-tuple-element.15), channel_id=1, source_target_pairs={{0,2},{4,6},{8,10},{12,14},{2,0},{6,4},{10,8},{14,12},{1,3},{5,7},... | collective-permute-start | bytes 393224 | tf_op jit(solution)/shard_map/ppermute | solution.py:30
  81.2 10.3 %fusion = f32[32,384,128]{1,2,0:T(8,128)} fusion(pred[384,384]{1,0:T(8,128)(4,1)} %iota_compare_fusion, bf16[384,32,128]{0,2,1:T(8,128)(2,1)} %bitcast.18, bf16[384,32,128]{2,1,0:T(8,128)(2,1)} %bitcast.15, bf16[384,32,128]{2,1,0:T(8,128)(2,1)} %bitcast.20), kind=kOutput, calls=%fused_computation.1 | convolution fusion | flops 2425356288 | bytes 15876096 | tf_op jit(solution)/shard_map/htu,uhe->the/dot_general | solution.py:50
  91.4 2.1 %all_gather.3 = f32[4096]{0:T(1024)S(1)} all-gather(f32[2048]{0:T(1024)S(1)} %copy-done.11), channel_id=1, replica_groups=mesh['groups'=2,'ctx'=8,'dp'=2] {'dp'}, dimensions={0}, use_global_device_ids=true | all-gather | bytes 24576 | tf_op jit(solution)/shard_map/all_gather | solution.py:41
  93.6 0.5 collective-permute-start.18
  94.1 1.5 %collective-permute-start.19 = (bf16[4,128,128]{2,1,0:T(8,128)(2,1)S(1)}, bf16[4,128,128]{2,1,0:T(8,128)(2,1)S(1)}, u32[]{:S(2)}, u32[]{:S(2)}) collective-permute-start(bf16[4,128,128]{2,1,0:T(8,128)(2,1)S(1)} %copy-done.9), channel_id=1, source_target_pairs={{0,2},{4,6},{8,10},{12,14},{2,0},{6,4},{10,8},{14,12},{1,3},{5,7},... | collective-permute-start | bytes 393224 | tf_op jit(solution)/shard_map/ppermute | solution.py:30
  95.7 4.3 %collective-permute-done.18 = bf16[4,128,128]{2,1,0:T(8,128)(2,1)S(1)} collective-permute-done((bf16[4,128,128]{2,1,0:T(8,128)(2,1)S(1)}, bf16[4,128,128]{2,1,0:T(8,128)(2,1)S(1)}, u32[]{:S(2)}, u32[]{:S(2)}) %collective-permute-start.18) | collective-permute-done | bytes 131104 | tf_op jit(solution)/shard_map/ppermute | solution.py:30
  100.0 2.0 %collective-permute-done.19 = bf16[4,128,128]{2,1,0:T(8,128)(2,1)S(1)} collective-permute-done((bf16[4,128,128]{2,1,0:T(8,128)(2,1)S(1)}, bf16[4,128,128]{2,1,0:T(8,128)(2,1)S(1)}, u32[]{:S(2)}, u32[]{:S(2)}) %collective-permute-start.19) | collective-permute-done | bytes 131104 | tf_op jit(solution)/shard_map/ppermute | solution.py:30
  102.0 0.1 broadcast_select_fusion.1
  102.1 8.0 %multiply_reduce_fusion = (f32[384]{0:T(512)S(1)}, f32[384,32,128]{0,2,1:T(8,128)}) fusion(bf16[384,32,128]{2,1,0:T(8,128)(2,1)S(1)} %bitcast.16, bf16[16,128,128]{2,1,0:T(8,128)(2,1)S(1)} %get-tuple-element.25, bf16[16,128,128]{2,1,0:T(8,128)(2,1)S(1)} %get-tuple-element.24, f32[32,384,128]{1,2,0:T(8,128)} %fusion), kind=kOutput, calls=%fused_computation.6 | convolution fusion | flops 407895680 | bytes 16778752 | tf_op jit(solution)/shard_map/thd,hde->the/dot_general | solution.py:51
  110.2 6.6 %copy.16 = f32[1,384,4096]{2,1,0:T(8,128)} copy(f32[1,384,4096]{1,2,0:T(8,128)} %bitcast.14) | data formatting | bytes 12582912 | tf_op jit(solution)/shard_map/reshape | solution.py:52
  116.8 5.4 %multiply_convert_fusion = bf16[1,384,4096]{2,1,0:T(8,128)(2,1)} fusion(f32[1,384,4096]{2,1,0:T(8,128)} %copy.16, f32[4096]{0:T(1024)S(1)} %all_gather.3, f32[384]{0:T(512)S(1)} %add_rsqrt_fusion), kind=kLoop, calls=%fused_computation.5 | loop fusion | flops 4718592 | bytes 9455104 | tf_op jit(solution)/shard_map/convert_element_type | solution.py:54
  (44 shorter events, 0.3 us)
Async XLA Ops:
  0.0 4.8 %copy-start.1 = (bf16[1,384,4096]{2,1,0:T(8,128)(2,1)S(1)}, bf16[1,384,4096]{2,1,0:T(8,128)(2,1)}, u32[]{:S(2)}) copy-start(bf16[1,384,4096]{2,1,0:T(8,128)(2,1)} %param.6) | copy-start | bytes 9437188
  12.7 8.1 %collective-permute-start.12 = (f32[4,128,128]{2,1,0:T(8,128)S(1)}, f32[4,128,128]{2,1,0:T(8,128)S(1)}, u32[]{:S(2)}, u32[]{:S(2)}) collective-permute-start(f32[4,128,128]{2,1,0:T(8,128)S(1)} %constant_dynamic-slice_fusion.3), channel_id=1, source_target_pairs={{0,2},{4,6},{8,10},{12,14},{2,0},{6,4},{10,8},{14,12},{1,3},{5,7},... | collective-permute-start | bytes 786440 | tf_op jit(solution)/shard_map/ppermute | solution.py:22
  20.8 0.9 copy-start.4
  21.7 9.5 %collective-permute-start = (f32[4,128,128]{2,1,0:T(8,128)}, f32[4,128,128]{2,1,0:T(8,128)S(1)}, u32[]{:S(2)}, u32[]{:S(2)}) collective-permute-start(f32[4,128,128]{2,1,0:T(8,128)} %get-tuple-element.20), channel_id=1, source_target_pairs={{0,2},{4,6},{8,10},{12,14},{2,0},{6,4},{10,8},{14,12},{1,3},{5,7},... | collective-permute-start | bytes 786440 | tf_op jit(solution)/shard_map/ppermute | solution.py:22
  22.2 14.6 %collective-permute-start.4 = (f32[4,128,128]{2,1,0:T(8,128)}, f32[4,128,128]{2,1,0:T(8,128)S(1)}, u32[]{:S(2)}, u32[]{:S(2)}) collective-permute-start(f32[4,128,128]{2,1,0:T(8,128)} %get-tuple-element.19), channel_id=1, source_target_pairs={{0,2},{4,6},{8,10},{12,14},{2,0},{6,4},{10,8},{14,12},{1,3},{5,7},... | collective-permute-start | bytes 786440 | tf_op jit(solution)/shard_map/ppermute | solution.py:22
  23.7 16.6 %collective-permute-start.8 = (f32[4,128,128]{2,1,0:T(8,128)S(1)}, f32[4,128,128]{2,1,0:T(8,128)S(1)}, u32[]{:S(2)}, u32[]{:S(2)}) collective-permute-start(f32[4,128,128]{2,1,0:T(8,128)S(1)} %get-tuple-element.18), channel_id=1, source_target_pairs={{0,2},{4,6},{8,10},{12,14},{2,0},{6,4},{10,8},{14,12},{1,3},{5,7},... | collective-permute-start | bytes 786440 | tf_op jit(solution)/shard_map/ppermute | solution.py:22
  24.2 18.2 %collective-permute-start.13 = (f32[4,128,128]{2,1,0:T(8,128)S(1)}, f32[4,128,128]{2,1,0:T(8,128)S(1)}, u32[]{:S(2)}, u32[]{:S(2)}) collective-permute-start(f32[4,128,128]{2,1,0:T(8,128)S(1)} %get-tuple-element.17), channel_id=1, source_target_pairs={{0,4},{2,6},{1,5},{3,7},{16,20},{18,22},{17,21},{19,23}} | collective-permute-start | bytes 786440 | tf_op jit(solution)/shard_map/ppermute | solution.py:27
  40.4 2.8 %collective-permute-start.9 = (f32[4,128,128]{2,1,0:T(8,128)S(1)}, f32[4,128,128]{2,1,0:T(8,128)S(1)}, u32[]{:S(2)}, u32[]{:S(2)}) collective-permute-start(f32[4,128,128]{2,1,0:T(8,128)S(1)} %get-tuple-element.21), channel_id=1, source_target_pairs={{0,4},{2,6},{1,5},{3,7},{16,20},{18,22},{17,21},{19,23}} | collective-permute-start | bytes 786440 | tf_op jit(solution)/shard_map/ppermute | solution.py:27
  41.1 2.8 %collective-permute-start.5 = (f32[4,128,128]{2,1,0:T(8,128)S(1)}, f32[4,128,128]{2,1,0:T(8,128)S(1)}, u32[]{:S(2)}, u32[]{:S(2)}) collective-permute-start(f32[4,128,128]{2,1,0:T(8,128)S(1)} %get-tuple-element.22), channel_id=1, source_target_pairs={{0,4},{2,6},{1,5},{3,7},{16,20},{18,22},{17,21},{19,23}} | collective-permute-start | bytes 786440 | tf_op jit(solution)/shard_map/ppermute | solution.py:27
  41.8 2.9 %collective-permute-start.1 = (f32[4,128,128]{2,1,0:T(8,128)S(1)}, f32[4,128,128]{2,1,0:T(8,128)S(1)}, u32[]{:S(2)}, u32[]{:S(2)}) collective-permute-start(f32[4,128,128]{2,1,0:T(8,128)S(1)} %get-tuple-element.23), channel_id=1, source_target_pairs={{0,4},{2,6},{1,5},{3,7},{16,20},{18,22},{17,21},{19,23}} | collective-permute-start | bytes 786440 | tf_op jit(solution)/shard_map/ppermute | solution.py:27
  42.5 2.9 %collective-permute-start.14 = (f32[4,128,128]{2,1,0:T(8,128)S(1)}, f32[4,128,128]{2,1,0:T(8,128)S(1)}, u32[]{:S(2)}, u32[]{:S(2)}) collective-permute-start(f32[4,128,128]{2,1,0:T(8,128)S(1)} %add.130), channel_id=1, source_target_pairs={{4,8},{6,10},{5,9},{7,11},{20,24},{22,26},{21,25},{23,27}} | collective-permute-start | bytes 786440 | tf_op jit(solution)/shard_map/ppermute | solution.py:27
  43.2 4.2 %collective-permute-start.10 = (f32[4,128,128]{2,1,0:T(8,128)S(1)}, f32[4,128,128]{2,1,0:T(8,128)S(1)}, u32[]{:S(2)}, u32[]{:S(2)}) collective-permute-start(f32[4,128,128]{2,1,0:T(8,128)S(1)} %add.124), channel_id=1, source_target_pairs={{4,8},{6,10},{5,9},{7,11},{20,24},{22,26},{21,25},{23,27}} | collective-permute-start | bytes 786440 | tf_op jit(solution)/shard_map/ppermute | solution.py:27
  44.0 5.5 %collective-permute-start.6 = (f32[4,128,128]{2,1,0:T(8,128)S(1)}, f32[4,128,128]{2,1,0:T(8,128)S(1)}, u32[]{:S(2)}, u32[]{:S(2)}) collective-permute-start(f32[4,128,128]{2,1,0:T(8,128)S(1)} %add.118), channel_id=1, source_target_pairs={{4,8},{6,10},{5,9},{7,11},{20,24},{22,26},{21,25},{23,27}} | collective-permute-start | bytes 786440 | tf_op jit(solution)/shard_map/ppermute | solution.py:27
  44.7 7.0 %collective-permute-start.2 = (f32[4,128,128]{2,1,0:T(8,128)S(1)}, f32[4,128,128]{2,1,0:T(8,128)S(1)}, u32[]{:S(2)}, u32[]{:S(2)}) collective-permute-start(f32[4,128,128]{2,1,0:T(8,128)S(1)} %add.112), channel_id=1, source_target_pairs={{4,8},{6,10},{5,9},{7,11},{20,24},{22,26},{21,25},{23,27}} | collective-permute-start | bytes 786440 | tf_op jit(solution)/shard_map/ppermute | solution.py:27
  46.2 16.9 %collective-permute-start.15 = (f32[4,128,128]{2,1,0:T(8,128)}, f32[4,128,128]{2,1,0:T(8,128)}, u32[]{:S(2)}, u32[]{:S(2)}) collective-permute-start(f32[4,128,128]{2,1,0:T(8,128)} %get-tuple-element.5), channel_id=1, source_target_pairs={{8,12},{10,14},{9,13},{11,15},{24,28},{26,30},{25,29},{27,31}} | collective-permute-start | bytes 786440 | tf_op jit(solution)/shard_map/ppermute | solution.py:27
  48.2 20.2 %collective-permute-start.11 = (f32[4,128,128]{2,1,0:T(8,128)}, f32[4,128,128]{2,1,0:T(8,128)}, u32[]{:S(2)}, u32[]{:S(2)}) collective-permute-start(f32[4,128,128]{2,1,0:T(8,128)} %get-tuple-element.7), channel_id=1, source_target_pairs={{8,12},{10,14},{9,13},{11,15},{24,28},{26,30},{25,29},{27,31}} | collective-permute-start | bytes 786440 | tf_op jit(solution)/shard_map/ppermute | solution.py:27
  50.4 23.6 %collective-permute-start.7 = (f32[4,128,128]{2,1,0:T(8,128)}, f32[4,128,128]{2,1,0:T(8,128)}, u32[]{:S(2)}, u32[]{:S(2)}) collective-permute-start(f32[4,128,128]{2,1,0:T(8,128)} %get-tuple-element.9), channel_id=1, source_target_pairs={{8,12},{10,14},{9,13},{11,15},{24,28},{26,30},{25,29},{27,31}} | collective-permute-start | bytes 786440 | tf_op jit(solution)/shard_map/ppermute | solution.py:27
  52.5 24.3 %collective-permute-start.3 = (f32[4,128,128]{2,1,0:T(8,128)}, f32[4,128,128]{2,1,0:T(8,128)}, u32[]{:S(2)}, u32[]{:S(2)}) collective-permute-start(f32[4,128,128]{2,1,0:T(8,128)} %get-tuple-element.11), channel_id=1, source_target_pairs={{8,12},{10,14},{9,13},{11,15},{24,28},{26,30},{25,29},{27,31}} | collective-permute-start | bytes 786440 | tf_op jit(solution)/shard_map/ppermute | solution.py:27
  53.8 23.0 %copy-start.2 = (f32[4,128,128]{2,1,0:T(8,128)S(1)}, f32[4,128,128]{2,1,0:T(8,128)}, u32[]{:S(2)}) copy-start(f32[4,128,128]{2,1,0:T(8,128)} %get-tuple-element.10) | copy-start | bytes 786436
  53.8 23.0 %copy-start.3 = (f32[4,128,128]{2,1,0:T(8,128)S(1)}, f32[4,128,128]{2,1,0:T(8,128)}, u32[]{:S(2)}) copy-start(f32[4,128,128]{2,1,0:T(8,128)} %get-tuple-element.12) | copy-start | bytes 786436
  53.8 23.0 %copy-start.5 = (f32[4,128,128]{2,1,0:T(8,128)S(1)}, f32[4,128,128]{2,1,0:T(8,128)}, u32[]{:S(2)}) copy-start(f32[4,128,128]{2,1,0:T(8,128)} %copy-done.4) | copy-start | bytes 786436
  79.1 16.5 %collective-permute-start.16 = (bf16[4,128,128]{2,1,0:T(8,128)(2,1)}, bf16[4,128,128]{2,1,0:T(8,128)(2,1)S(1)}, u32[]{:S(2)}, u32[]{:S(2)}) collective-permute-start(bf16[4,128,128]{2,1,0:T(8,128)(2,1)} %get-tuple-element.14), channel_id=1, source_target_pairs={{0,2},{4,6},{8,10},{12,14},{2,0},{6,4},{10,8},{14,12},{1,3},{5,7},... | collective-permute-start | bytes 393224 | tf_op jit(solution)/shard_map/ppermute | solution.py:30
  79.6 16.0 %collective-permute-start.17 = (bf16[4,128,128]{2,1,0:T(8,128)(2,1)}, bf16[4,128,128]{2,1,0:T(8,128)(2,1)S(1)}, u32[]{:S(2)}, u32[]{:S(2)}) collective-permute-start(bf16[4,128,128]{2,1,0:T(8,128)(2,1)} %get-tuple-element.15), channel_id=1, source_target_pairs={{0,2},{4,6},{8,10},{12,14},{2,0},{6,4},{10,8},{14,12},{1,3},{5,7},... | collective-permute-start | bytes 393224 | tf_op jit(solution)/shard_map/ppermute | solution.py:30
  81.2 10.3 %copy-start.11 = (f32[2048]{0:T(1024)S(1)}, f32[2048]{0:T(1024)}, u32[]{:S(2)}) copy-start(f32[2048]{0:T(1024)} %param.7) | copy-start | bytes 24580
  81.2 12.4 %copy-start.10 = (bf16[4,128,128]{2,1,0:T(8,128)(2,1)S(1)}, bf16[4,128,128]{2,1,0:T(8,128)(2,1)}, u32[]{:S(2)}) copy-start(bf16[4,128,128]{2,1,0:T(8,128)(2,1)} %get-tuple-element.16) | copy-start | bytes 393220
  81.2 13.0 %copy-start.9 = (bf16[4,128,128]{2,1,0:T(8,128)(2,1)S(1)}, bf16[4,128,128]{2,1,0:T(8,128)(2,1)}, u32[]{:S(2)}) copy-start(bf16[4,128,128]{2,1,0:T(8,128)(2,1)} %get-tuple-element.13) | copy-start | bytes 393220
  81.2 20.8 %copy-start.6 = (bf16[4,128,128]{2,1,0:T(8,128)(2,1)S(1)}, bf16[4,128,128]{2,1,0:T(8,128)(2,1)}, u32[]{:S(2)}) copy-start(bf16[4,128,128]{2,1,0:T(8,128)(2,1)} %get-tuple-element.27) | copy-start | bytes 393220
  81.2 20.8 %copy-start.7 = (bf16[4,128,128]{2,1,0:T(8,128)(2,1)S(1)}, bf16[4,128,128]{2,1,0:T(8,128)(2,1)}, u32[]{:S(2)}) copy-start(bf16[4,128,128]{2,1,0:T(8,128)(2,1)} %get-tuple-element.28) | copy-start | bytes 393220
  81.2 20.8 %copy-start.8 = (bf16[4,128,128]{2,1,0:T(8,128)(2,1)S(1)}, bf16[4,128,128]{2,1,0:T(8,128)(2,1)}, u32[]{:S(2)}) copy-start(bf16[4,128,128]{2,1,0:T(8,128)(2,1)} %get-tuple-element.29) | copy-start | bytes 393220
  91.4 10.7 %copy-start = (bf16[48,8,32,128]{3,2,1,0:T(8,128)(2,1)S(1)}, bf16[48,8,32,128]{3,2,1,0:T(8,128)(2,1)}, u32[]{:S(2)}) copy-start(bf16[48,8,32,128]{3,2,1,0:T(8,128)(2,1)} %copy.19) | copy-start | bytes 9437188
  93.6 6.4 %collective-permute-start.18 = (bf16[4,128,128]{2,1,0:T(8,128)(2,1)S(1)}, bf16[4,128,128]{2,1,0:T(8,128)(2,1)S(1)}, u32[]{:S(2)}, u32[]{:S(2)}) collective-permute-start(bf16[4,128,128]{2,1,0:T(8,128)(2,1)S(1)} %copy-done.10), channel_id=1, source_target_pairs={{0,2},{4,6},{8,10},{12,14},{2,0},{6,4},{10,8},{14,12},{1,3},{5,7},... | collective-permute-start | bytes 393224 | tf_op jit(solution)/shard_map/ppermute | solution.py:30
  94.1 7.9 %collective-permute-start.19 = (bf16[4,128,128]{2,1,0:T(8,128)(2,1)S(1)}, bf16[4,128,128]{2,1,0:T(8,128)(2,1)S(1)}, u32[]{:S(2)}, u32[]{:S(2)}) collective-permute-start(bf16[4,128,128]{2,1,0:T(8,128)(2,1)S(1)} %copy-done.9), channel_id=1, source_target_pairs={{0,2},{4,6},{8,10},{12,14},{2,0},{6,4},{10,8},{14,12},{1,3},{5,7},... | collective-permute-start | bytes 393224 | tf_op jit(solution)/shard_map/ppermute | solution.py:30

commit v3 on v2

--- a/solution.py
+++ b/solution.py
@@ -1,6 +1,8 @@
 import jax
 import jax.numpy as jnp
 from jax import lax
+from jax.experimental import pallas as pl
+from jax.experimental.pallas import tpu as pltpu
 from jax.sharding import PartitionSpec as P
 
 H = 32
@@ -35,23 +37,92 @@
     return jnp.concatenate([low, high], axis=0)
 
 
+def state_kernel(key_ref, val_ref, out_ref):
+    heads, head_size, _ = out_ref.shape
+    for head in range(heads):
+        cols = slice(head * head_size, (head + 1) * head_size)
+        out_ref[head] = lax.dot_general(
+            key_ref[:, cols], val_ref[:, cols], (((0,), (0,)), ((), ())),
+            preferred_element_type=jnp.float32)
+
+
+def state_terms_of(keyset, valset, group):
+    row_count, feat_count = keyset.shape
+    head_size = feat_count // H
+    width = group * head_size
+    return pl.pallas_call(
+        state_kernel,
+        grid=(H // group,),
+        in_specs=[pl.BlockSpec((row_count, width), lambda g: (0, g)),
+                  pl.BlockSpec((row_count, width), lambda g: (0, g))],
+        out_specs=pl.BlockSpec((group, head_size, head_size), lambda g: (g, 0, 0)),
+        out_shape=jax.ShapeDtypeStruct((H, head_size, head_size), jnp.float32),
+    )(keyset, valset)
+
+
+def attend_kernel(query_ref, key_ref, val_ref, prefix_ref, gain_ref, out_ref, acc_ref, sumsq_ref):
+    step = pl.program_id(0)
+    row_count, width = query_ref.shape
+    heads, head_size, _ = prefix_ref.shape
+    causal = (lax.broadcasted_iota(jnp.int32, (row_count, row_count), 0)
+              >= lax.broadcasted_iota(jnp.int32, (row_count, row_count), 1))
+
+    @pl.when(step == 0)
+    def _():
+        sumsq_ref[...] = jnp.zeros_like(sumsq_ref)
+
+    sumsq = sumsq_ref[...]
+    for head in range(heads):
+        cols = slice(head * head_size, (head + 1) * head_size)
+        query = query_ref[:, cols]
+        scores = lax.dot_general(query, key_ref[:, cols], (((1,), (1,)), ((), ())),
+                                 preferred_element_type=jnp.float32)
+        weights = jnp.where(causal, scores, 0.0).astype(jnp.bfloat16)
+        within = jnp.dot(weights, val_ref[:, cols], preferred_element_type=jnp.float32)
+        carried = jnp.dot(query, prefix_ref[head], preferred_element_type=jnp.float32)
+        attended = within + carried
+        acc_ref[step, :, cols] = attended
+        sumsq = sumsq + jnp.sum(attended * attended, axis=1, keepdims=True)
+    sumsq_ref[...] = sumsq
+
+    @pl.when(step == pl.num_programs(0) - 1)
+    def _():
+        scale = lax.rsqrt(sumsq / (width * pl.num_programs(0)) + 1e-05)
+        for part in range(acc_ref.shape[0]):
+            cols = slice(part * width, (part + 1) * width)
+            out_ref[:, cols] = (acc_ref[part] * scale * gain_ref[:, cols]).astype(out_ref.dtype)
+
+
+def attend_of(query, keyset, valset, prefix_bf, full_gain, group):
+    row_count, feat_count = query.shape
+    head_size = feat_count // H
+    width = group * head_size
+    steps = H // group
+    return pl.pallas_call(
+        attend_kernel,
+        grid=(steps,),
+        in_specs=[pl.BlockSpec((row_count, width), lambda g: (0, g)),
+                  pl.BlockSpec((row_count, width), lambda g: (0, g)),
+                  pl.BlockSpec((row_count, width), lambda g: (0, g)),
+                  pl.BlockSpec((group, head_size, head_size), lambda g: (g, 0, 0)),
+                  pl.BlockSpec((1, feat_count), lambda g: (0, 0))],
+        out_specs=pl.BlockSpec((row_count, feat_count), lambda g: (0, 0)),
+        out_shape=jax.ShapeDtypeStruct((row_count, feat_count), jnp.bfloat16),
+        scratch_shapes=[pltpu.VMEM((steps, row_count, width), jnp.float32),
+                        pltpu.VMEM((row_count, 1), jnp.float32)],
+    )(query, keyset, valset, prefix_bf, full_gain)
+
+
 def shards(query_rows, key_rows, value_rows, gain):
     seq_count, row_count, feat_count = query_rows.shape
-    head_size = feat_count // H
-    full_gain = lax.all_gather(gain, "dp", axis=0, tiled=True)
-    query = query_rows.reshape(row_count, H, head_size)
-    keyset = key_rows.reshape(row_count, H, head_size)
-    valset = value_rows.reshape(row_count, H, head_size)
-    state_terms = jnp.einsum("thd,the->hde", keyset, valset, preferred_element_type=jnp.float32)
+    full_gain = lax.all_gather(gain, "dp", axis=0, tiled=True).reshape(1, feat_count)
+    query = query_rows.reshape(seq_count * row_count, feat_count)
+    keyset = key_rows.reshape(seq_count * row_count, feat_count)
+    valset = value_rows.reshape(seq_count * row_count, feat_count)
+    state_terms = state_terms_of(keyset, valset, 8)
     prefix_bf = pair_chain_prefix(state_terms, "ctx", 4)
-    causal_mask = jnp.arange(row_count)[:, None] >= jnp.arange(row_count)[None, :]
-    scores = jnp.einsum("thd,uhd->htu", query, keyset, preferred_element_type=jnp.float32)
-    weights = jnp.where(causal_mask, scores, 0.0).astype(jnp.bfloat16)
-    within = jnp.einsum("htu,uhe->the", weights, valset, preferred_element_type=jnp.float32)
-    carried = jnp.einsum("thd,hde->the", query, prefix_bf, preferred_element_type=jnp.float32)
-    attended = (within + carried).reshape(seq_count, row_count, feat_count)
-    scale = lax.rsqrt(jnp.mean(attended * attended, axis=-1, keepdims=True) + 1e-05)
-    return (attended * scale * full_gain).astype(jnp.bfloat16)
+    normed = attend_of(query, keyset, valset, prefix_bf, full_gain, 8)
+    return normed.reshape(seq_count, row_count, feat_count)
 
 
 def solution(mesh):

time: 123 us -> 100 us (0.81)
  matrix products: 23.6 us -> 0 us
  Pallas kernels: 0 us -> 17.6 us
  local copies, waits for them, and re-layouts: 18.5 us -> 1.19 us
  waiting for transfers between devices: 47 us -> 52.1 us
  other arithmetic: 12.9 us -> 8.73 us
    dot_general x3 -> x0, matrix products: 23.6 us -> none  [the longest x1 10.3 us: shards(): jnp.einsum('htu,uhe->the', weights, valset, preferred_element_type=jnp.fl...]
    pallas_call x0 -> x2, Pallas kernels: none -> 17.6 us  [the longest x1 12.3 us: attend_of(): pl.pallas_call(attend_kernel, grid=(steps,), in_specs=[pl.BlockSpec((row_...]
    reshape x2 -> x0, local copies, waits for them, and re-layouts: 11.4 us -> none  [the longest x1 6.61 us: shards(): attended = (within + carried).reshape(seq_count, row_count, feat_count)]
    unnamed x29 -> x9, local copies, waits for them, and re-layouts: 7.1 us -> 0.06 us
    convert_element_type x1 -> x0, other arithmetic: 5.42 us -> none  [shards(): return (attended * scale * full_gain).astype(jnp.bfloat16)]
    ppermute x12, waiting for transfers between devices: 17.8 us -> 22.9 us  [pair_chain_prefix(): carried = carried + lax.ppermute(carried + total, axis, links)]
    add x2, other arithmetic: 1 us -> 2.27 us  [pair_chain_prefix(): total = mine + got]
  transfers between devices with their start and end apart: 20 -> 20, of which waited for: 10 -> 11; matrix products, arithmetic and copies ran while one was open for 16% -> 4% of each run, Pallas kernels for 0% -> 0%
where the time goes in v3:
time: 100 us; the launch traced here: 99.6 us
  waiting for transfers between devices  52.1 us (52%)
  starting transfers between devices  17.8 us (18%)
  Pallas kernels  17.6 us (18%)
  other arithmetic  8.73 us (9%)
  blocking collectives  1.93 us (2%)
  local copies, waits for them, and re-layouts  1.19 us (1%)
    ppermute x4, waiting for transfers between devices, pair_chain_prefix(): got = lax.ppermute(other_all[piece * step:(piece + 1) * step], axis, swap)  22.9 us
    ppermute x12, waiting for transfers between devices, pair_chain_prefix(): carried = carried + lax.ppermute(carried + total, axis, links)  22.9 us
    pallas_call x1, Pallas kernels, attend_of(): pl.pallas_call(attend_kernel, grid=(steps,), in_specs=[pl.BlockSpec((row_...  12.3 us
    ppermute x12, starting transfers between devices, pair_chain_prefix(): carried = carried + lax.ppermute(carried + total, axis, links)  10.5 us
    ppermute x4, waiting for transfers between devices, pair_chain_prefix(): backs.append(lax.ppermute(send, axis, swap))  6.27 us
    pallas_call x1, Pallas kernels, state_terms_of(): pl.pallas_call(state_kernel, grid=(H // group,), in_specs=[pl.BlockSpec((...  5.36 us
    ppermute x4, starting transfers between devices, pair_chain_prefix(): backs.append(lax.ppermute(send, axis, swap))  4.16 us
    add x8, other arithmetic, pair_chain_prefix(): carried = carried + lax.ppermute(carried + total, axis, links)  3.44 us
  transfers between devices with their start and end apart: 20, of which 11 were waited for; matrix products, arithmetic and copies ran while one was open for 4% of the time, Pallas kernels for 0%

profile of v3, /device:TPU:30, one launch (start us, length us, event | category | flops | bytes accessed | tf_op | source)
XLA Modules:
  0.0 99.6 jit_solution(554721663142990139)
XLA Ops:
  0.0 5.4 %shard_map.46 = f32[32,128,128]{2,1,0:T(8,128)} custom-call(bf16[384,4096]{1,0:T(8,128)(2,1)} %bitcast.5, bf16[384,4096]{1,0:T(8,128)(2,1)} %bitcast.7), custom_call_target="tpu_custom_call" | custom-call | tf_op jit(solution)/shard_map/pallas_call | solution.py:53
  5.4 1.1 %constant_dynamic-slice_fusion.3 = f32[4,128,128]{2,1,0:T(8,128)S(1)} fusion(f32[32,128,128]{2,1,0:T(8,128)} %shard_map.46, s32[]{:T(128)S(6)} %add.130), kind=kLoop, calls=%fused_computation.23 | loop fusion | bytes 524292 | tf_op jit(solution)/shard_map/slice | solution.py:24
  6.5 0.6 collective-permute-start.12
  7.1 7.5 %collective-permute-done.12 = f32[4,128,128]{2,1,0:T(8,128)S(1)} collective-permute-done((f32[4,128,128]{2,1,0:T(8,128)S(1)}, f32[4,128,128]{2,1,0:T(8,128)S(1)}, u32[]{:S(2)}, u32[]{:S(2)}) %collective-permute-start.12) | collective-permute-done | bytes 262176 | tf_op jit(solution)/shard_map/ppermute | solution.py:24
  14.6 2.2 %dynamic-slice_add_fusion = (f32[4,128,128]{2,1,0:T(8,128)S(1)}, f32[4,128,128]{2,1,0:T(8,128)S(1)}, f32[4,128,128]{2,1,0:T(8,128)}, f32[4,128,128]{2,1,0:T(8,128)}) fusion(f32[4,128,128]{2,1,0:T(8,128)S(1)} %collective-permute-done.12, f32[32,128,128]{2,1,0:T(8,128)} %shard_map.46, s32[]{:T(128)S(6)} %add.129, s32[]{:T(128)S(6)} %add.128, s32[]{:T(128)S(6)} %add.126, ...), kind=kLoop, calls=%fused_computation.12 | loop fusion | flops 65536 | bytes 2359312 | tf_op jit(solution)/shard_map/add | solution.py:25
  16.8 0.5 collective-permute-start
  17.3 1.5 %collective-permute-start.4 = (f32[4,128,128]{2,1,0:T(8,128)}, f32[4,128,128]{2,1,0:T(8,128)S(1)}, u32[]{:S(2)}, u32[]{:S(2)}) collective-permute-start(f32[4,128,128]{2,1,0:T(8,128)} %get-tuple-element.19), channel_id=1, source_target_pairs={{0,2},{4,6},{8,10},{12,14},{2,0},{6,4},{10,8},{14,12},{1,3},{5,7},... | collective-permute-start | bytes 786440 | tf_op jit(solution)/shard_map/ppermute | solution.py:24
  18.8 0.5 collective-permute-start.8
  19.3 0.7 collective-permute-start.13
  20.0 6.2 %collective-permute-done = f32[4,128,128]{2,1,0:T(8,128)S(1)} collective-permute-done((f32[4,128,128]{2,1,0:T(8,128)}, f32[4,128,128]{2,1,0:T(8,128)S(1)}, u32[]{:S(2)}, u32[]{:S(2)}) %collective-permute-start) | collective-permute-done | bytes 262176 | tf_op jit(solution)/shard_map/ppermute | solution.py:24
  26.2 5.6 %collective-permute-done.4 = f32[4,128,128]{2,1,0:T(8,128)S(1)} collective-permute-done((f32[4,128,128]{2,1,0:T(8,128)}, f32[4,128,128]{2,1,0:T(8,128)S(1)}, u32[]{:S(2)}, u32[]{:S(2)}) %collective-permute-start.4) | collective-permute-done | bytes 262176 | tf_op jit(solution)/shard_map/ppermute | solution.py:24
  31.9 3.5 %collective-permute-done.8 = f32[4,128,128]{2,1,0:T(8,128)S(1)} collective-permute-done((f32[4,128,128]{2,1,0:T(8,128)S(1)}, f32[4,128,128]{2,1,0:T(8,128)S(1)}, u32[]{:S(2)}, u32[]{:S(2)}) %collective-permute-start.8) | collective-permute-done | bytes 262176 | tf_op jit(solution)/shard_map/ppermute | solution.py:24
  35.4 0.1 dynamic-slice_add_fusion.1
  35.5 0.7 collective-permute-start.9
  36.2 0.7 collective-permute-start.5
  36.9 0.7 collective-permute-start.1
  37.6 0.7 collective-permute-start.14
  38.3 0.0 collective-permute-done.9
  38.3 0.7 collective-permute-start.10
  39.0 0.0 collective-permute-done.5
  39.1 0.7 collective-permute-start.6
  39.8 0.7 collective-permute-start.2
  40.5 0.0 collective-permute-done.14
  40.5 0.8 fusion
  41.3 1.3 %collective-permute-start.15 = (f32[4,128,128]{2,1,0:T(8,128)}, f32[4,128,128]{2,1,0:T(8,128)}, u32[]{:S(2)}, u32[]{:S(2)}) collective-permute-start(f32[4,128,128]{2,1,0:T(8,128)} %get-tuple-element.5), channel_id=1, source_target_pairs={{8,12},{10,14},{9,13},{11,15},{24,28},{26,30},{25,29},{27,31}} | collective-permute-start | bytes 786440 | tf_op jit(solution)/shard_map/ppermute | solution.py:29
  42.5 0.0 collective-permute-done.10
  42.6 0.8 fusion.1
  43.3 1.3 %collective-permute-start.11 = (f32[4,128,128]{2,1,0:T(8,128)}, f32[4,128,128]{2,1,0:T(8,128)}, u32[]{:S(2)}, u32[]{:S(2)}) collective-permute-start(f32[4,128,128]{2,1,0:T(8,128)} %get-tuple-element.7), channel_id=1, source_target_pairs={{8,12},{10,14},{9,13},{11,15},{24,28},{26,30},{25,29},{27,31}} | collective-permute-start | bytes 786440 | tf_op jit(solution)/shard_map/ppermute | solution.py:29
  44.6 0.9 fusion.2
  45.5 1.3 %collective-permute-start.7 = (f32[4,128,128]{2,1,0:T(8,128)}, f32[4,128,128]{2,1,0:T(8,128)}, u32[]{:S(2)}, u32[]{:S(2)}) collective-permute-start(f32[4,128,128]{2,1,0:T(8,128)} %get-tuple-element.9), channel_id=1, source_target_pairs={{8,12},{10,14},{9,13},{11,15},{24,28},{26,30},{25,29},{27,31}} | collective-permute-start | bytes 786440 | tf_op jit(solution)/shard_map/ppermute | solution.py:29
  46.8 0.9 fusion.3
  47.7 1.3 %collective-permute-start.3 = (f32[4,128,128]{2,1,0:T(8,128)}, f32[4,128,128]{2,1,0:T(8,128)}, u32[]{:S(2)}, u32[]{:S(2)}) collective-permute-start(f32[4,128,128]{2,1,0:T(8,128)} %get-tuple-element.11), channel_id=1, source_target_pairs={{8,12},{10,14},{9,13},{11,15},{24,28},{26,30},{25,29},{27,31}} | collective-permute-start | bytes 786440 | tf_op jit(solution)/shard_map/ppermute | solution.py:29
  49.0 9.1 %collective-permute-done.15 = f32[4,128,128]{2,1,0:T(8,128)} collective-permute-done((f32[4,128,128]{2,1,0:T(8,128)}, f32[4,128,128]{2,1,0:T(8,128)}, u32[]{:S(2)}, u32[]{:S(2)}) %collective-permute-start.15) | collective-permute-done | bytes 262176 | tf_op jit(solution)/shard_map/ppermute | solution.py:29
  58.0 5.4 %collective-permute-done.11 = f32[4,128,128]{2,1,0:T(8,128)} collective-permute-done((f32[4,128,128]{2,1,0:T(8,128)}, f32[4,128,128]{2,1,0:T(8,128)}, u32[]{:S(2)}, u32[]{:S(2)}) %collective-permute-start.11) | collective-permute-done | bytes 262176 | tf_op jit(solution)/shard_map/ppermute | solution.py:29
  63.4 5.6 %collective-permute-done.7 = f32[4,128,128]{2,1,0:T(8,128)} collective-permute-done((f32[4,128,128]{2,1,0:T(8,128)}, f32[4,128,128]{2,1,0:T(8,128)}, u32[]{:S(2)}, u32[]{:S(2)}) %collective-permute-start.7) | collective-permute-done | bytes 262176 | tf_op jit(solution)/shard_map/ppermute | solution.py:29
  69.1 2.8 %collective-permute-done.3 = f32[4,128,128]{2,1,0:T(8,128)} collective-permute-done((f32[4,128,128]{2,1,0:T(8,128)}, f32[4,128,128]{2,1,0:T(8,128)}, u32[]{:S(2)}, u32[]{:S(2)}) %collective-permute-start.3) | collective-permute-done | bytes 262176 | tf_op jit(solution)/shard_map/ppermute | solution.py:29
  71.9 1.8 %add_convert_fusion = (bf16[4,128,128]{2,1,0:T(8,128)(2,1)S(1)}, bf16[4,128,128]{2,1,0:T(8,128)(2,1)S(1)}, bf16[4,128,128]{2,1,0:T(8,128)(2,1)S(1)}, bf16[4,128,...) fusion(f32[32,128,128]{2,1,0:T(8,128)S(1)} %copy-done, ...), kind=kLoop, calls=%fused_computation.4 | loop fusion | flops 1835008 | bytes 5242897 | tf_op jit(solution)/shard_map/convert_element_type | solution.py:31
  73.7 0.5 collective-permute-start.16
  74.2 1.6 %collective-permute-start.17 = (bf16[4,128,128]{2,1,0:T(8,128)(2,1)S(1)}, bf16[4,128,128]{2,1,0:T(8,128)(2,1)S(1)}, u32[]{:S(2)}, u32[]{:S(2)}) collective-permute-start(bf16[4,128,128]{2,1,0:T(8,128)(2,1)S(1)} %get-tuple-element.15), channel_id=1, source_target_pairs={{0,2},{4,6},{8,10},{12,14},{2,0},{6,4},{10,8},{14,12},{1,3},{5,7},... | collective-permute-start | bytes 393224 | tf_op jit(solution)/shard_map/ppermute | solution.py:32
  75.8 1.9 %all_gather.3 = f32[4096]{0:T(1024)} all-gather(f32[2048]{0:T(1024)S(1)} %copy-done.2), channel_id=1, replica_groups=mesh['groups'=2,'ctx'=8,'dp'=2] {'dp'}, dimensions={0}, use_global_device_ids=true | all-gather | bytes 24576 | tf_op jit(solution)/shard_map/all_gather | solution.py:118
  77.7 0.5 collective-permute-start.18
  78.2 1.6 %collective-permute-start.19 = (bf16[4,128,128]{2,1,0:T(8,128)(2,1)S(1)}, bf16[4,128,128]{2,1,0:T(8,128)(2,1)S(1)}, u32[]{:S(2)}, u32[]{:S(2)}) collective-permute-start(bf16[4,128,128]{2,1,0:T(8,128)(2,1)S(1)} %get-tuple-element.13), channel_id=1, source_target_pairs={{0,2},{4,6},{8,10},{12,14},{2,0},{6,4},{10,8},{14,12},{1,3},{5,7},... | collective-permute-start | bytes 393224 | tf_op jit(solution)/shard_map/ppermute | solution.py:32
  79.8 0.3 collective-permute-done.17
  80.2 4.0 %collective-permute-done.18 = bf16[4,128,128]{2,1,0:T(8,128)(2,1)S(1)} collective-permute-done((bf16[4,128,128]{2,1,0:T(8,128)(2,1)S(1)}, bf16[4,128,128]{2,1,0:T(8,128)(2,1)S(1)}, u32[]{:S(2)}, u32[]{:S(2)}) %collective-permute-start.18) | collective-permute-done | bytes 131104 | tf_op jit(solution)/shard_map/ppermute | solution.py:32
  84.2 2.0 %collective-permute-done.19 = bf16[4,128,128]{2,1,0:T(8,128)(2,1)S(1)} collective-permute-done((bf16[4,128,128]{2,1,0:T(8,128)(2,1)S(1)}, bf16[4,128,128]{2,1,0:T(8,128)(2,1)S(1)}, u32[]{:S(2)}, u32[]{:S(2)}) %collective-permute-start.19) | collective-permute-done | bytes 131104 | tf_op jit(solution)/shard_map/ppermute | solution.py:32
  86.2 0.1 broadcast_select_fusion.1
  86.3 1.1 %pad_maximum_fusion.prefix_ref = bf16[32,128,128]{2,1,0:T(8,128)(2,1)} fusion(bf16[16,128,128]{2,1,0:T(8,128)(2,1)S(1)} %get-tuple-element.25, bf16[16,128,128]{2,1,0:T(8,128)(2,1)S(1)} %get-tuple-element.24), kind=kLoop, calls=%fused_computation | loop fusion | flops 524288 | bytes 2097152 | tf_op jit(solution)/shard_map/concatenate | solution.py:37
  87.4 12.3 %shard_map.47 = bf16[384,4096]{1,0:T(8,128)(2,1)} custom-call(bf16[384,4096]{1,0:T(8,128)(2,1)} %bitcast.9, bf16[384,4096]{1,0:T(8,128)(2,1)} %bitcast.6, bf16[384,4096]{1,0:T(8,128)(2,1)} %bitcast.8, bf16[32,128,128]{2,1,0:T(8,128)(2,1)} %pad_maximum_fusion.prefix_ref, f32[1,4096]{1,0:T(1,128)} %bitcast.10), custom_call_target="tpu_custom_call" | custom-call | tf_op jit(solution)/shard_map/pallas_call | solution.py:101
  (19 shorter events, 0.2 us)
Async XLA Ops:
  5.4 30.0 %copy-start = (f32[32,128,128]{2,1,0:T(8,128)S(1)}, f32[32,128,128]{2,1,0:T(8,128)}, u32[]{:S(2)}) copy-start(f32[32,128,128]{2,1,0:T(8,128)} %shard_map.46) | copy-start | bytes 6291460
  6.5 8.1 %collective-permute-start.12 = (f32[4,128,128]{2,1,0:T(8,128)S(1)}, f32[4,128,128]{2,1,0:T(8,128)S(1)}, u32[]{:S(2)}, u32[]{:S(2)}) collective-permute-start(f32[4,128,128]{2,1,0:T(8,128)S(1)} %constant_dynamic-slice_fusion.3), channel_id=1, source_target_pairs={{0,2},{4,6},{8,10},{12,14},{2,0},{6,4},{10,8},{14,12},{1,3},{5,7},... | collective-permute-start | bytes 786440 | tf_op jit(solution)/shard_map/ppermute | solution.py:24
  14.6 2.2 %copy-start.1 = (f32[4,128,128]{2,1,0:T(8,128)}, f32[4,128,128]{2,1,0:T(8,128)S(1)}, u32[]{:S(2)}) copy-start(f32[4,128,128]{2,1,0:T(8,128)S(1)} %collective-permute-done.12) | copy-start | bytes 786436
  16.8 9.5 %collective-permute-start = (f32[4,128,128]{2,1,0:T(8,128)}, f32[4,128,128]{2,1,0:T(8,128)S(1)}, u32[]{:S(2)}, u32[]{:S(2)}) collective-permute-start(f32[4,128,128]{2,1,0:T(8,128)} %get-tuple-element.20), channel_id=1, source_target_pairs={{0,2},{4,6},{8,10},{12,14},{2,0},{6,4},{10,8},{14,12},{1,3},{5,7},... | collective-permute-start | bytes 786440 | tf_op jit(solution)/shard_map/ppermute | solution.py:24
  17.3 14.6 %collective-permute-start.4 = (f32[4,128,128]{2,1,0:T(8,128)}, f32[4,128,128]{2,1,0:T(8,128)S(1)}, u32[]{:S(2)}, u32[]{:S(2)}) collective-permute-start(f32[4,128,128]{2,1,0:T(8,128)} %get-tuple-element.19), channel_id=1, source_target_pairs={{0,2},{4,6},{8,10},{12,14},{2,0},{6,4},{10,8},{14,12},{1,3},{5,7},... | collective-permute-start | bytes 786440 | tf_op jit(solution)/shard_map/ppermute | solution.py:24
  18.8 16.6 %collective-permute-start.8 = (f32[4,128,128]{2,1,0:T(8,128)S(1)}, f32[4,128,128]{2,1,0:T(8,128)S(1)}, u32[]{:S(2)}, u32[]{:S(2)}) collective-permute-start(f32[4,128,128]{2,1,0:T(8,128)S(1)} %get-tuple-element.18), channel_id=1, source_target_pairs={{0,2},{4,6},{8,10},{12,14},{2,0},{6,4},{10,8},{14,12},{1,3},{5,7},... | collective-permute-start | bytes 786440 | tf_op jit(solution)/shard_map/ppermute | solution.py:24
  19.3 18.2 %collective-permute-start.13 = (f32[4,128,128]{2,1,0:T(8,128)S(1)}, f32[4,128,128]{2,1,0:T(8,128)S(1)}, u32[]{:S(2)}, u32[]{:S(2)}) collective-permute-start(f32[4,128,128]{2,1,0:T(8,128)S(1)} %get-tuple-element.17), channel_id=1, source_target_pairs={{0,4},{2,6},{1,5},{3,7},{16,20},{18,22},{17,21},{19,23}} | collective-permute-start | bytes 786440 | tf_op jit(solution)/shard_map/ppermute | solution.py:29
  35.5 2.8 %collective-permute-start.9 = (f32[4,128,128]{2,1,0:T(8,128)S(1)}, f32[4,128,128]{2,1,0:T(8,128)S(1)}, u32[]{:S(2)}, u32[]{:S(2)}) collective-permute-start(f32[4,128,128]{2,1,0:T(8,128)S(1)} %get-tuple-element.21), channel_id=1, source_target_pairs={{0,4},{2,6},{1,5},{3,7},{16,20},{18,22},{17,21},{19,23}} | collective-permute-start | bytes 786440 | tf_op jit(solution)/shard_map/ppermute | solution.py:29
  36.2 2.8 %collective-permute-start.5 = (f32[4,128,128]{2,1,0:T(8,128)S(1)}, f32[4,128,128]{2,1,0:T(8,128)S(1)}, u32[]{:S(2)}, u32[]{:S(2)}) collective-permute-start(f32[4,128,128]{2,1,0:T(8,128)S(1)} %get-tuple-element.22), channel_id=1, source_target_pairs={{0,4},{2,6},{1,5},{3,7},{16,20},{18,22},{17,21},{19,23}} | collective-permute-start | bytes 786440 | tf_op jit(solution)/shard_map/ppermute | solution.py:29
  36.9 2.9 %collective-permute-start.1 = (f32[4,128,128]{2,1,0:T(8,128)S(1)}, f32[4,128,128]{2,1,0:T(8,128)S(1)}, u32[]{:S(2)}, u32[]{:S(2)}) collective-permute-start(f32[4,128,128]{2,1,0:T(8,128)S(1)} %get-tuple-element.23), channel_id=1, source_target_pairs={{0,4},{2,6},{1,5},{3,7},{16,20},{18,22},{17,21},{19,23}} | collective-permute-start | bytes 786440 | tf_op jit(solution)/shard_map/ppermute | solution.py:29
  37.6 2.9 %collective-permute-start.14 = (f32[4,128,128]{2,1,0:T(8,128)S(1)}, f32[4,128,128]{2,1,0:T(8,128)S(1)}, u32[]{:S(2)}, u32[]{:S(2)}) collective-permute-start(f32[4,128,128]{2,1,0:T(8,128)S(1)} %add.116), channel_id=1, source_target_pairs={{4,8},{6,10},{5,9},{7,11},{20,24},{22,26},{21,25},{23,27}} | collective-permute-start | bytes 786440 | tf_op jit(solution)/shard_map/ppermute | solution.py:29
  38.3 4.2 %collective-permute-start.10 = (f32[4,128,128]{2,1,0:T(8,128)S(1)}, f32[4,128,128]{2,1,0:T(8,128)S(1)}, u32[]{:S(2)}, u32[]{:S(2)}) collective-permute-start(f32[4,128,128]{2,1,0:T(8,128)S(1)} %add.110), channel_id=1, source_target_pairs={{4,8},{6,10},{5,9},{7,11},{20,24},{22,26},{21,25},{23,27}} | collective-permute-start | bytes 786440 | tf_op jit(solution)/shard_map/ppermute | solution.py:29
  39.1 5.5 %collective-permute-start.6 = (f32[4,128,128]{2,1,0:T(8,128)S(1)}, f32[4,128,128]{2,1,0:T(8,128)S(1)}, u32[]{:S(2)}, u32[]{:S(2)}) collective-permute-start(f32[4,128,128]{2,1,0:T(8,128)S(1)} %add.104), channel_id=1, source_target_pairs={{4,8},{6,10},{5,9},{7,11},{20,24},{22,26},{21,25},{23,27}} | collective-permute-start | bytes 786440 | tf_op jit(solution)/shard_map/ppermute | solution.py:29
  39.8 7.0 %collective-permute-start.2 = (f32[4,128,128]{2,1,0:T(8,128)S(1)}, f32[4,128,128]{2,1,0:T(8,128)S(1)}, u32[]{:S(2)}, u32[]{:S(2)}) collective-permute-start(f32[4,128,128]{2,1,0:T(8,128)S(1)} %add.98), channel_id=1, source_target_pairs={{4,8},{6,10},{5,9},{7,11},{20,24},{22,26},{21,25},{23,27}} | collective-permute-start | bytes 786440 | tf_op jit(solution)/shard_map/ppermute | solution.py:29
  41.3 16.8 %collective-permute-start.15 = (f32[4,128,128]{2,1,0:T(8,128)}, f32[4,128,128]{2,1,0:T(8,128)}, u32[]{:S(2)}, u32[]{:S(2)}) collective-permute-start(f32[4,128,128]{2,1,0:T(8,128)} %get-tuple-element.5), channel_id=1, source_target_pairs={{8,12},{10,14},{9,13},{11,15},{24,28},{26,30},{25,29},{27,31}} | collective-permute-start | bytes 786440 | tf_op jit(solution)/shard_map/ppermute | solution.py:29
  43.3 20.1 %collective-permute-start.11 = (f32[4,128,128]{2,1,0:T(8,128)}, f32[4,128,128]{2,1,0:T(8,128)}, u32[]{:S(2)}, u32[]{:S(2)}) collective-permute-start(f32[4,128,128]{2,1,0:T(8,128)} %get-tuple-element.7), channel_id=1, source_target_pairs={{8,12},{10,14},{9,13},{11,15},{24,28},{26,30},{25,29},{27,31}} | collective-permute-start | bytes 786440 | tf_op jit(solution)/shard_map/ppermute | solution.py:29
  45.5 23.6 %collective-permute-start.7 = (f32[4,128,128]{2,1,0:T(8,128)}, f32[4,128,128]{2,1,0:T(8,128)}, u32[]{:S(2)}, u32[]{:S(2)}) collective-permute-start(f32[4,128,128]{2,1,0:T(8,128)} %get-tuple-element.9), channel_id=1, source_target_pairs={{8,12},{10,14},{9,13},{11,15},{24,28},{26,30},{25,29},{27,31}} | collective-permute-start | bytes 786440 | tf_op jit(solution)/shard_map/ppermute | solution.py:29
  47.7 24.2 %collective-permute-start.3 = (f32[4,128,128]{2,1,0:T(8,128)}, f32[4,128,128]{2,1,0:T(8,128)}, u32[]{:S(2)}, u32[]{:S(2)}) collective-permute-start(f32[4,128,128]{2,1,0:T(8,128)} %get-tuple-element.11), channel_id=1, source_target_pairs={{8,12},{10,14},{9,13},{11,15},{24,28},{26,30},{25,29},{27,31}} | collective-permute-start | bytes 786440 | tf_op jit(solution)/shard_map/ppermute | solution.py:29
  71.9 3.9 %copy-start.2 = (f32[2048]{0:T(1024)S(1)}, f32[2048]{0:T(1024)}, u32[]{:S(2)}) copy-start(f32[2048]{0:T(1024)} %param.7) | copy-start | bytes 24580
  73.7 6.1 %collective-permute-start.16 = (bf16[4,128,128]{2,1,0:T(8,128)(2,1)S(1)}, bf16[4,128,128]{2,1,0:T(8,128)(2,1)S(1)}, u32[]{:S(2)}, u32[]{:S(2)}) collective-permute-start(bf16[4,128,128]{2,1,0:T(8,128)(2,1)S(1)} %get-tuple-element.14), channel_id=1, source_target_pairs={{0,2},{4,6},{8,10},{12,14},{2,0},{6,4},{10,8},{14,12},{1,3},{5,7},... | collective-permute-start | bytes 393224 | tf_op jit(solution)/shard_map/ppermute | solution.py:32
  74.2 5.9 %collective-permute-start.17 = (bf16[4,128,128]{2,1,0:T(8,128)(2,1)S(1)}, bf16[4,128,128]{2,1,0:T(8,128)(2,1)S(1)}, u32[]{:S(2)}, u32[]{:S(2)}) collective-permute-start(bf16[4,128,128]{2,1,0:T(8,128)(2,1)S(1)} %get-tuple-element.15), channel_id=1, source_target_pairs={{0,2},{4,6},{8,10},{12,14},{2,0},{6,4},{10,8},{14,12},{1,3},{5,7},... | collective-permute-start | bytes 393224 | tf_op jit(solution)/shard_map/ppermute | solution.py:32
  77.7 6.4 %collective-permute-start.18 = (bf16[4,128,128]{2,1,0:T(8,128)(2,1)S(1)}, bf16[4,128,128]{2,1,0:T(8,128)(2,1)S(1)}, u32[]{:S(2)}, u32[]{:S(2)}) collective-permute-start(bf16[4,128,128]{2,1,0:T(8,128)(2,1)S(1)} %get-tuple-element.16), channel_id=1, source_target_pairs={{0,2},{4,6},{8,10},{12,14},{2,0},{6,4},{10,8},{14,12},{1,3},{5,7},... | collective-permute-start | bytes 393224 | tf_op jit(solution)/shard_map/ppermute | solution.py:32
  78.2 7.9 %collective-permute-start.19 = (bf16[4,128,128]{2,1,0:T(8,128)(2,1)S(1)}, bf16[4,128,128]{2,1,0:T(8,128)(2,1)S(1)}, u32[]{:S(2)}, u32[]{:S(2)}) collective-permute-start(bf16[4,128,128]{2,1,0:T(8,128)(2,1)S(1)} %get-tuple-element.13), channel_id=1, source_target_pairs={{0,2},{4,6},{8,10},{12,14},{2,0},{6,4},{10,8},{14,12},{1,3},{5,7},... | collective-permute-start | bytes 393224 | tf_op jit(solution)/shard_map/ppermute | solution.py:32

commit v4 on v3

--- a/solution.py
+++ b/solution.py
@@ -10,28 +10,49 @@
 
 def pair_chain_prefix(terms, axis, pieces):
     count = lax.axis_size(axis)
-    mine_at = lax.axis_index(axis) % 2
-    first = mine_at == 0
+    place = lax.axis_index(axis)
+    side = place % 2
+    level = place // 2
+    first = side == 0
     half = terms.shape[0] // 2
-    pairs = count // 2
-    mine_all = lax.dynamic_slice_in_dim(terms, mine_at * half, half, 0)
-    other_all = lax.dynamic_slice_in_dim(terms, (1 - mine_at) * half, half, 0)
-    swap = [(2 * i, 2 * i + 1) for i in range(pairs)] + [(2 * i + 1, 2 * i) for i in range(pairs)]
-    step = half // pieces
-    keeps, backs = [], []
-    for piece in range(pieces):
-        mine = mine_all[piece * step:(piece + 1) * step]
-        got = lax.ppermute(other_all[piece * step:(piece + 1) * step], axis, swap)
-        total = mine + got
-        carried = jnp.zeros_like(total)
-        for hop in range(1, pairs):
-            links = [(2 * (hop - 1) + side, 2 * hop + side) for side in range(2)]
-            carried = carried + lax.ppermute(carried + total, axis, links)
-        keeps.append((carried + jnp.where(first, 0.0, got)).astype(jnp.bfloat16))
+    levels = count // 2
+    shape = (pieces, half // pieces) + terms.shape[1:]
+    mine_all = lax.dynamic_slice_in_dim(terms, side * half, half, 0).reshape(shape)
+    other_all = lax.dynamic_slice_in_dim(terms, (1 - side) * half, half, 0).reshape(shape)
+
+    def swap_at(at):
+        return [(2 * lv, 2 * lv + 1) for lv in at] + [(2 * lv + 1, 2 * lv) for lv in at]
+
+    def put(buffer, index, valid, value):
+        value = jnp.where(valid, value, lax.dynamic_index_in_dim(buffer, index, 0, keepdims=False))
+        return lax.dynamic_update_index_in_dim(buffer, value, index, 0)
+
+    got_all = jnp.zeros_like(mine_all)
+    carried_all = jnp.zeros_like(mine_all)
+    keep_all = jnp.zeros(shape, jnp.bfloat16)
+    back_all = jnp.zeros(shape, jnp.bfloat16)
+    for t in range(pieces + levels - 1):
+        if t < pieces:
+            got_all = got_all.at[t].set(lax.ppermute(other_all[t], axis, swap_at(range(levels))))
+        active = [lv for lv in range(levels) if 0 <= t - lv < pieces]
+        piece = jnp.clip(t - level, 0, pieces - 1)
+        valid = (t - level >= 0) & (t - level < pieces)
+        carried = lax.dynamic_index_in_dim(carried_all, piece, 0, keepdims=False)
+        mine = lax.dynamic_index_in_dim(mine_all, piece, 0, keepdims=False)
+        got = lax.dynamic_index_in_dim(got_all, piece, 0, keepdims=False)
+        links = [(2 * lv + s, 2 * (lv + 1) + s) for lv in active if lv + 1 < levels for s in range(2)]
+        if links:
+            came = lax.ppermute(carried + mine + got, axis, links)
+            arrived = t - level + 1
+            came_ok = (arrived >= 0) & (arrived < pieces) & (level >= 1)
+            carried_all = put(carried_all, jnp.clip(arrived, 0, pieces - 1), came_ok, came)
+        keep = (carried + jnp.where(first, 0.0, got)).astype(jnp.bfloat16)
         send = (carried + jnp.where(first, mine, 0.0)).astype(jnp.bfloat16)
-        backs.append(lax.ppermute(send, axis, swap))
-    keep = jnp.concatenate(keeps, axis=0)
-    back = jnp.concatenate(backs, axis=0)
+        back = lax.ppermute(send, axis, swap_at(active))
+        keep_all = put(keep_all, piece, valid, keep)
+        back_all = put(back_all, piece, valid, back)
+    keep = keep_all.reshape((half,) + terms.shape[1:])
+    back = back_all.reshape((half,) + terms.shape[1:])
     low = jnp.where(first, keep, back)
     high = jnp.where(first, back, keep)
     return jnp.concatenate([low, high], axis=0)

time: 100 us -> 100 us (level)
  other arithmetic: 8.73 us -> 2.71 us
  starting transfers between devices: 17.8 us -> 22.5 us
  local copies, waits for them, and re-layouts: 1.19 us -> 3.25 us
  waiting for transfers between devices: 52.1 us -> 50.2 us
    add x10 -> x6, other arithmetic: 5.71 us -> 0.39 us  [pair_chain_prefix(): came = lax.ppermute(carried + mine + got, axis, links)]
    ppermute x20 -> x17, starting transfers between devices: 17.8 us -> 22.5 us  [the longest x7 11.8 us: pair_chain_prefix(): back = lax.ppermute(send, axis, swap_at(active))]
    ppermute x20 -> x17, waiting for transfers between devices: 52.1 us -> 50.2 us  [the longest x6 25.1 us: pair_chain_prefix(): came = lax.ppermute(carried + mine + got, axis, links)]
    convert_element_type x1 -> x2, other arithmetic: 1.83 us -> 0.08 us  [pair_chain_prefix(): send = (carried + jnp.where(first, mine, 0.0)).astype(jnp.bfloat16)]
    dynamic_slice x0 -> x12, local copies, waits for them, and re-layouts: none -> 1.55 us  [the longest x1 1.31 us: pair_chain_prefix(): lax.dynamic_slice_in_dim(terms, side * half, half, 0).reshape(shape)]
    dynamic_update_slice x0 -> x20, other arithmetic: none -> 1.09 us  [put(): return lax.dynamic_update_index_in_dim(buffer, value, index, 0)]
  transfers between devices with their start and end apart: 20 -> 17, of which waited for: 11 -> 12; matrix products, arithmetic and copies ran while one was open for 4% -> 3% of each run, Pallas kernels for 0% -> 0%
where the time goes in v4:
time: 100 us; the launch traced here: 98.8 us
  waiting for transfers between devices  50.2 us (50%)
  starting transfers between devices  22.5 us (22%)
  Pallas kernels  17.8 us (18%)
  local copies, waits for them, and re-layouts  3.25 us (3%)
  other arithmetic  2.71 us (3%)
  blocking collectives  1.93 us (2%)
    ppermute x6, waiting for transfers between devices, pair_chain_prefix(): came = lax.ppermute(carried + mine + got, axis, links)  25.1 us
    ppermute x4, waiting for transfers between devices, pair_chain_prefix(): lax.ppermute(other_all[t], axis, swap_at(range(levels)))  13.7 us
    pallas_call x1, Pallas kernels, attend_of(): pl.pallas_call(attend_kernel, grid=(steps,), in_specs=[pl.BlockSpec((row_...  12.4 us
    ppermute x7, starting transfers between devices, pair_chain_prefix(): back = lax.ppermute(send, axis, swap_at(active))  11.8 us
    ppermute x7, waiting for transfers between devices, pair_chain_prefix(): back = lax.ppermute(send, axis, swap_at(active))  11.5 us
    ppermute x6, starting transfers between devices, pair_chain_prefix(): came = lax.ppermute(carried + mine + got, axis, links)  6.52 us
    pallas_call x1, Pallas kernels, state_terms_of(): pl.pallas_call(state_kernel, grid=(H // group,), in_specs=[pl.BlockSpec((...  5.36 us
    ppermute x4, starting transfers between devices, pair_chain_prefix(): lax.ppermute(other_all[t], axis, swap_at(range(levels)))  4.12 us
  transfers between devices with their start and end apart: 17, of which 12 were waited for; matrix products, arithmetic and copies ran while one was open for 3% of the time, Pallas kernels for 0%

profile of v4, /device:TPU:30, one launch (start us, length us, event | category | flops | bytes accessed | tf_op | source)
XLA Modules:
  0.0 98.8 jit_solution(12417058343166588498)
XLA Ops:
  0.0 5.4 %shard_map.46 = f32[32,128,128]{2,1,0:T(8,128)} custom-call(bf16[384,4096]{1,0:T(8,128)(2,1)} %bitcast.161, bf16[384,4096]{1,0:T(8,128)(2,1)} %bitcast.163), custom_call_target="tpu_custom_call" | custom-call | tf_op jit(solution)/shard_map/pallas_call | solution.py:74
  5.4 1.3 %constant_dynamic-slice_fusion.14 = f32[16,128,128]{2,1,0:T(8,128)S(1)} fusion(f32[32,128,128]{2,1,0:T(8,128)} %shard_map.46, s32[]{:T(128)S(6)} %select_n.314), kind=kLoop, calls=%fused_computation.96 | loop fusion | bytes 2097156 | tf_op jit(solution)/shard_map/dynamic_slice | solution.py:20
  6.7 0.7 collective-permute-start.10
  7.4 1.3 %constant_dynamic-slice_fusion.15 = (f32[4,128,128]{2,1,0:T(8,128)S(1)}, f32[4,128,128]{2,1,0:T(8,128)S(1)}, f32[4,128,128]{2,1,0:T(8,128)S(1)}, f32[4,128,128]{2,1,0:T(8,128)S(1)}) fusion(f32[32,128,128]{2,1,0:T(8,128)} %shard_map.46, s32[]{:T(128)S(6)} %add.209, s32[]{:T(128)S(6)} %add.208, s32[]{:T(128)S(6)} %add.207, s32[]{:T(128)S(6)} %select_n.309), kind=kLoop, calls=%fused_computation.97 | loop fusion | bytes 2097168 | tf_op jit(solution)/shard_map/slice | solution.py:36
  8.7 0.6 collective-permute-start
  9.3 1.5 %collective-permute-start.2 = (f32[4,128,128]{2,1,0:T(8,128)S(1)}, f32[4,128,128]{2,1,0:T(8,128)S(1)}, u32[]{:S(2)}, u32[]{:S(2)}) collective-permute-start(f32[4,128,128]{2,1,0:T(8,128)S(1)} %get-tuple-element.61), channel_id=1, source_target_pairs={{0,2},{4,6},{8,10},{12,14},{2,0},{6,4},{10,8},{14,12},{1,3},{5,7},... | collective-permute-start | bytes 786440 | tf_op jit(solution)/shard_map/ppermute | solution.py:36
  10.8 0.5 collective-permute-start.4
  11.3 1.5 %collective-permute-start.6 = (f32[4,128,128]{2,1,0:T(8,128)S(1)}, f32[4,128,128]{2,1,0:T(8,128)S(1)}, u32[]{:S(2)}, u32[]{:S(2)}) collective-permute-start(f32[4,128,128]{2,1,0:T(8,128)S(1)} %get-tuple-element.59), channel_id=1, source_target_pairs={{0,2},{4,6},{8,10},{12,14},{2,0},{6,4},{10,8},{14,12},{1,3},{5,7},... | collective-permute-start | bytes 786440 | tf_op jit(solution)/shard_map/ppermute | solution.py:36
  12.8 1.9 %all_gather.3 = f32[4096]{0:T(1024)} all-gather(f32[2048]{0:T(1024)S(1)} %copy-done), channel_id=1, replica_groups=mesh['groups'=2,'ctx'=8,'dp'=2] {'dp'}, dimensions={0}, use_global_device_ids=true | all-gather | bytes 24576 | tf_op jit(solution)/shard_map/all_gather | solution.py:139
  14.7 0.1 broadcast.113.clone.1
  14.9 3.0 %collective-permute-done = f32[4,128,128]{2,1,0:T(8,128)S(1)} collective-permute-done((f32[4,128,128]{2,1,0:T(8,128)S(1)}, f32[4,128,128]{2,1,0:T(8,128)S(1)}, u32[]{:S(2)}, u32[]{:S(2)}) %collective-permute-start) | collective-permute-done | bytes 262176 | tf_op jit(solution)/shard_map/ppermute | solution.py:36
  18.0 0.7 collective-permute-start.1
  18.7 0.1 broadcast.113.clone
  18.8 0.1 scatter.14
  18.9 4.6 %collective-permute-done.2 = f32[4,128,128]{2,1,0:T(8,128)S(1)} collective-permute-done((f32[4,128,128]{2,1,0:T(8,128)S(1)}, f32[4,128,128]{2,1,0:T(8,128)S(1)}, u32[]{:S(2)}, u32[]{:S(2)}) %collective-permute-start.2) | collective-permute-done | bytes 262176 | tf_op jit(solution)/shard_map/ppermute | solution.py:36
  23.6 0.1 broadcast.114
  23.7 0.1 bitcast_add_fusion.8
  23.8 0.7 collective-permute-start.11
  24.5 0.7 collective-permute-start.3
  25.2 0.1 fusion.13
  25.2 3.9 %collective-permute-done.4 = f32[4,128,128]{2,1,0:T(8,128)S(1)} collective-permute-done((f32[4,128,128]{2,1,0:T(8,128)S(1)}, f32[4,128,128]{2,1,0:T(8,128)S(1)}, u32[]{:S(2)}, u32[]{:S(2)}) %collective-permute-start.4) | collective-permute-done | bytes 262176 | tf_op jit(solution)/shard_map/ppermute | solution.py:36
  29.4 0.1 bitcast_add_fusion.6
  29.5 0.7 collective-permute-start.12
  30.1 1.3 %collective-permute-start.5 = (f32[4,128,128]{2,1,0:T(8,128)S(1)}, f32[4,128,128]{2,1,0:T(8,128)S(1)}, u32[]{:S(2)}, u32[]{:S(2)}) collective-permute-start(f32[4,128,128]{2,1,0:T(8,128)S(1)} %get-tuple-element.63), channel_id=1, source_target_pairs={{0,4},{2,6},{4,8},{6,10},{8,12},{10,14},{1,5},{3,7},{5,9},{7,11},{... | collective-permute-start | bytes 786440 | tf_op jit(solution)/shard_map/ppermute | solution.py:45
  31.4 0.1 fusion.15
  31.5 2.1 %collective-permute-done.6 = f32[4,128,128]{2,1,0:T(8,128)S(1)} collective-permute-done((f32[4,128,128]{2,1,0:T(8,128)S(1)}, f32[4,128,128]{2,1,0:T(8,128)S(1)}, u32[]{:S(2)}, u32[]{:S(2)}) %collective-permute-start.6) | collective-permute-done | bytes 262176 | tf_op jit(solution)/shard_map/ppermute | solution.py:36
  33.8 12.5 %collective-permute-done.5 = f32[4,128,128]{2,1,0:T(8,128)S(1)} collective-permute-done((f32[4,128,128]{2,1,0:T(8,128)S(1)}, f32[4,128,128]{2,1,0:T(8,128)S(1)}, u32[]{:S(2)}, u32[]{:S(2)}) %collective-permute-start.5) | collective-permute-done | bytes 262176 | tf_op jit(solution)/shard_map/ppermute | solution.py:45
  46.4 0.1 bitcast_add_fusion.4
  46.4 0.7 collective-permute-start.13
  47.2 1.3 %collective-permute-start.7 = (f32[4,128,128]{2,1,0:T(8,128)S(1)}, f32[4,128,128]{2,1,0:T(8,128)S(1)}, u32[]{:S(2)}, u32[]{:S(2)}) collective-permute-start(f32[4,128,128]{2,1,0:T(8,128)S(1)} %get-tuple-element.57), channel_id=1, source_target_pairs={{0,4},{2,6},{4,8},{6,10},{8,12},{10,14},{1,5},{3,7},{5,9},{7,11},{... | collective-permute-start | bytes 786440 | tf_op jit(solution)/shard_map/ppermute | solution.py:45
  48.5 2.9 %collective-permute-done.13 = bf16[4,128,128]{2,1,0:T(8,128)(2,1)S(1)} collective-permute-done((bf16[4,128,128]{2,1,0:T(8,128)(2,1)S(1)}, bf16[4,128,128]{2,1,0:T(8,128)(2,1)S(1)}, u32[]{:S(2)}, u32[]{:S(2)}) %collective-permute-start.13) | collective-permute-done | bytes 131104 | tf_op jit(solution)/shard_map/ppermute | solution.py:51
  51.6 3.9 %collective-permute-done.7 = f32[4,128,128]{2,1,0:T(8,128)S(1)} collective-permute-done((f32[4,128,128]{2,1,0:T(8,128)S(1)}, f32[4,128,128]{2,1,0:T(8,128)S(1)}, u32[]{:S(2)}, u32[]{:S(2)}) %collective-permute-start.7) | collective-permute-done | bytes 262176 | tf_op jit(solution)/shard_map/ppermute | solution.py:45
  55.6 3.3 %collective-permute-start.14 = (bf16[4,128,128]{2,1,0:T(8,128)(2,1)S(1)}, bf16[4,128,128]{2,1,0:T(8,128)(2,1)S(1)}, u32[]{:S(2)}, u32[]{:S(2)}) collective-permute-start(bf16[4,128,128]{2,1,0:T(8,128)(2,1)S(1)} %get-tuple-element.56), channel_id=1, source_target_pairs={{4,6},{8,10},{12,14},{6,4},{10,8},{14,12},{5,7},{9,11},{13,15},{7,... | collective-permute-start | bytes 393224 | tf_op jit(solution)/shard_map/ppermute | solution.py:51
  58.9 0.1 fusion.19
  58.9 1.3 %collective-permute-start.8 = (f32[4,128,128]{2,1,0:T(8,128)S(1)}, f32[4,128,128]{2,1,0:T(8,128)S(1)}, u32[]{:S(2)}, u32[]{:S(2)}) collective-permute-start(f32[4,128,128]{2,1,0:T(8,128)S(1)} %get-tuple-element.55), channel_id=1, source_target_pairs={{4,8},{6,10},{8,12},{10,14},{5,9},{7,11},{9,13},{11,15},{20,24},{2... | collective-permute-start | bytes 786440 | tf_op jit(solution)/shard_map/ppermute | solution.py:45
  60.3 2.1 %collective-permute-done.14 = bf16[4,128,128]{2,1,0:T(8,128)(2,1)S(1)} collective-permute-done((bf16[4,128,128]{2,1,0:T(8,128)(2,1)S(1)}, bf16[4,128,128]{2,1,0:T(8,128)(2,1)S(1)}, u32[]{:S(2)}, u32[]{:S(2)}) %collective-permute-start.14) | collective-permute-done | bytes 131104 | tf_op jit(solution)/shard_map/ppermute | solution.py:51
  62.5 4.7 %collective-permute-done.8 = f32[4,128,128]{2,1,0:T(8,128)S(1)} collective-permute-done((f32[4,128,128]{2,1,0:T(8,128)S(1)}, f32[4,128,128]{2,1,0:T(8,128)S(1)}, u32[]{:S(2)}, u32[]{:S(2)}) %collective-permute-start.8) | collective-permute-done | bytes 262176 | tf_op jit(solution)/shard_map/ppermute | solution.py:45
  67.3 2.6 %collective-permute-start.15 = (bf16[4,128,128]{2,1,0:T(8,128)(2,1)S(1)}, bf16[4,128,128]{2,1,0:T(8,128)(2,1)S(1)}, u32[]{:S(2)}, u32[]{:S(2)}) collective-permute-start(bf16[4,128,128]{2,1,0:T(8,128)(2,1)S(1)} %get-tuple-element.54), channel_id=1, source_target_pairs={{8,10},{12,14},{10,8},{14,12},{9,11},{13,15},{11,9},{15,13},{24,26... | collective-permute-start | bytes 393224 | tf_op jit(solution)/shard_map/ppermute | solution.py:51
  69.9 1.3 %collective-permute-start.9 = (f32[4,128,128]{2,1,0:T(8,128)S(1)}, f32[4,128,128]{2,1,0:T(8,128)S(1)}, u32[]{:S(2)}, u32[]{:S(2)}) collective-permute-start(f32[4,128,128]{2,1,0:T(8,128)S(1)} %get-tuple-element.53), channel_id=1, source_target_pairs={{8,12},{10,14},{9,13},{11,15},{24,28},{26,30},{25,29},{27,31}} | collective-permute-start | bytes 786440 | tf_op jit(solution)/shard_map/ppermute | solution.py:45
  71.3 0.1 fusion.21
  71.3 2.8 %collective-permute-done.15 = bf16[4,128,128]{2,1,0:T(8,128)(2,1)S(1)} collective-permute-done((bf16[4,128,128]{2,1,0:T(8,128)(2,1)S(1)}, bf16[4,128,128]{2,1,0:T(8,128)(2,1)S(1)}, u32[]{:S(2)}, u32[]{:S(2)}) %collective-permute-start.15) | collective-permute-done | bytes 131104 | tf_op jit(solution)/shard_map/ppermute | solution.py:51
  74.2 4.0 %collective-permute-done.9 = f32[4,128,128]{2,1,0:T(8,128)S(1)} collective-permute-done((f32[4,128,128]{2,1,0:T(8,128)S(1)}, f32[4,128,128]{2,1,0:T(8,128)S(1)}, u32[]{:S(2)}, u32[]{:S(2)}) %collective-permute-start.9) | collective-permute-done | bytes 262176 | tf_op jit(solution)/shard_map/ppermute | solution.py:45
  78.3 3.2 %collective-permute-start.16 = (bf16[4,128,128]{2,1,0:T(8,128)(2,1)S(1)}, bf16[4,128,128]{2,1,0:T(8,128)(2,1)S(1)}, u32[]{:S(2)}, u32[]{:S(2)}) collective-permute-start(bf16[4,128,128]{2,1,0:T(8,128)(2,1)S(1)} %fusion.25), channel_id=1, source_target_pairs={{12,14},{14,12},{13,15},{15,13},{28,30},{30,28},{29,31},{31,29}} | collective-permute-start | bytes 393224 | tf_op jit(solution)/shard_map/ppermute | solution.py:51
  81.5 0.1 fusion.23
  81.6 3.5 %collective-permute-done.16 = bf16[4,128,128]{2,1,0:T(8,128)(2,1)S(1)} collective-permute-done((bf16[4,128,128]{2,1,0:T(8,128)(2,1)S(1)}, bf16[4,128,128]{2,1,0:T(8,128)(2,1)S(1)}, u32[]{:S(2)}, u32[]{:S(2)}) %collective-permute-start.16) | collective-permute-done | bytes 131104 | tf_op jit(solution)/shard_map/ppermute | solution.py:51
  85.2 0.1 broadcast_select_fusion.1
  85.3 1.1 %pad_maximum_fusion.prefix_ref = bf16[32,128,128]{2,1,0:T(8,128)(2,1)} fusion(bf16[16,128,128]{2,1,0:T(8,128)(2,1)S(1)} %bitcast.178, bf16[16,128,128]{2,1,0:T(8,128)(2,1)S(1)} %bitcast.177), kind=kLoop, calls=%fused_computation | loop fusion | flops 524288 | bytes 2097152 | tf_op jit(solution)/shard_map/concatenate | solution.py:58
  86.4 12.4 %shard_map.47 = bf16[384,4096]{1,0:T(8,128)(2,1)} custom-call(bf16[384,4096]{1,0:T(8,128)(2,1)} %bitcast.173, bf16[384,4096]{1,0:T(8,128)(2,1)} %bitcast.162, bf16[384,4096]{1,0:T(8,128)(2,1)} %bitcast.164, bf16[32,128,128]{2,1,0:T(8,128)(2,1)} %pad_maximum_fusion.prefix_ref, f32[1,4096]{1,0:T(1,128)} %bitcast.179), custom_call_target="tpu_custom_call" | custom-call | tf_op jit(solution)/shard_map/pallas_call | solution.py:122
  (41 shorter events, 1.3 us)
Async XLA Ops:
  5.4 7.4 %copy-start = (f32[2048]{0:T(1024)S(1)}, f32[2048]{0:T(1024)}, u32[]{:S(2)}) copy-start(f32[2048]{0:T(1024)} %param.15) | copy-start | bytes 24580
  6.7 8.0 %collective-permute-start.10 = (bf16[4,128,128]{2,1,0:T(8,128)(2,1)S(1)}, bf16[4,128,128]{2,1,0:T(8,128)(2,1)S(1)}, u32[]{:S(2)}, u32[]{:S(2)}) collective-permute-start(bf16[4,128,128]{2,1,0:T(8,128)(2,1)S(1)} %fusion.24), channel_id=1, source_target_pairs={{0,2},{2,0},{1,3},{3,1},{16,18},{18,16},{17,19},{19,17}} | collective-permute-start | bytes 393224 | tf_op jit(solution)/shard_map/ppermute | solution.py:51
  8.7 9.3 %collective-permute-start = (f32[4,128,128]{2,1,0:T(8,128)S(1)}, f32[4,128,128]{2,1,0:T(8,128)S(1)}, u32[]{:S(2)}, u32[]{:S(2)}) collective-permute-start(f32[4,128,128]{2,1,0:T(8,128)S(1)} %get-tuple-element.62), channel_id=1, source_target_pairs={{0,2},{4,6},{8,10},{12,14},{2,0},{6,4},{10,8},{14,12},{1,3},{5,7},... | collective-permute-start | bytes 786440 | tf_op jit(solution)/shard_map/ppermute | solution.py:36
  9.3 14.3 %collective-permute-start.2 = (f32[4,128,128]{2,1,0:T(8,128)S(1)}, f32[4,128,128]{2,1,0:T(8,128)S(1)}, u32[]{:S(2)}, u32[]{:S(2)}) collective-permute-start(f32[4,128,128]{2,1,0:T(8,128)S(1)} %get-tuple-element.61), channel_id=1, source_target_pairs={{0,2},{4,6},{8,10},{12,14},{2,0},{6,4},{10,8},{14,12},{1,3},{5,7},... | collective-permute-start | bytes 786440 | tf_op jit(solution)/shard_map/ppermute | solution.py:36
  10.8 18.4 %collective-permute-start.4 = (f32[4,128,128]{2,1,0:T(8,128)S(1)}, f32[4,128,128]{2,1,0:T(8,128)S(1)}, u32[]{:S(2)}, u32[]{:S(2)}) collective-permute-start(f32[4,128,128]{2,1,0:T(8,128)S(1)} %get-tuple-element.60), channel_id=1, source_target_pairs={{0,2},{4,6},{8,10},{12,14},{2,0},{6,4},{10,8},{14,12},{1,3},{5,7},... | collective-permute-start | bytes 786440 | tf_op jit(solution)/shard_map/ppermute | solution.py:36
  11.3 22.4 %collective-permute-start.6 = (f32[4,128,128]{2,1,0:T(8,128)S(1)}, f32[4,128,128]{2,1,0:T(8,128)S(1)}, u32[]{:S(2)}, u32[]{:S(2)}) collective-permute-start(f32[4,128,128]{2,1,0:T(8,128)S(1)} %get-tuple-element.59), channel_id=1, source_target_pairs={{0,2},{4,6},{8,10},{12,14},{2,0},{6,4},{10,8},{14,12},{1,3},{5,7},... | collective-permute-start | bytes 786440 | tf_op jit(solution)/shard_map/ppermute | solution.py:36
  18.0 5.6 %collective-permute-start.1 = (f32[4,128,128]{2,1,0:T(8,128)S(1)}, f32[4,128,128]{2,1,0:T(8,128)S(1)}, u32[]{:S(2)}, u32[]{:S(2)}) collective-permute-start(f32[4,128,128]{2,1,0:T(8,128)S(1)} %add_bitcast_fusion), channel_id=1, source_target_pairs={{0,4},{2,6},{1,5},{3,7},{16,20},{18,22},{17,21},{19,23}} | collective-permute-start | bytes 786440 | tf_op jit(solution)/shard_map/ppermute | solution.py:45
  23.8 5.4 %collective-permute-start.11 = (bf16[4,128,128]{2,1,0:T(8,128)(2,1)S(1)}, bf16[4,128,128]{2,1,0:T(8,128)(2,1)S(1)}, u32[]{:S(2)}, u32[]{:S(2)}) collective-permute-start(bf16[4,128,128]{2,1,0:T(8,128)(2,1)S(1)} %get-tuple-element.66), channel_id=1, source_target_pairs={{0,2},{4,6},{2,0},{6,4},{1,3},{5,7},{3,1},{7,5},{16,18},{20,22},{1... | collective-permute-start | bytes 393224 | tf_op jit(solution)/shard_map/ppermute | solution.py:51
  24.5 4.9 %collective-permute-start.3 = (f32[4,128,128]{2,1,0:T(8,128)S(1)}, f32[4,128,128]{2,1,0:T(8,128)S(1)}, u32[]{:S(2)}, u32[]{:S(2)}) collective-permute-start(f32[4,128,128]{2,1,0:T(8,128)S(1)} %get-tuple-element.65), channel_id=1, source_target_pairs={{0,4},{2,6},{4,8},{6,10},{1,5},{3,7},{5,9},{7,11},{16,20},{18,22},... | collective-permute-start | bytes 786440 | tf_op jit(solution)/shard_map/ppermute | solution.py:45
  29.5 4.2 %collective-permute-start.12 = (bf16[4,128,128]{2,1,0:T(8,128)(2,1)S(1)}, bf16[4,128,128]{2,1,0:T(8,128)(2,1)S(1)}, u32[]{:S(2)}, u32[]{:S(2)}) collective-permute-start(bf16[4,128,128]{2,1,0:T(8,128)(2,1)S(1)} %get-tuple-element.64), channel_id=1, source_target_pairs={{0,2},{4,6},{8,10},{2,0},{6,4},{10,8},{1,3},{5,7},{9,11},{3,1},{7,... | collective-permute-start | bytes 393224 | tf_op jit(solution)/shard_map/ppermute | solution.py:51
  30.1 16.2 %collective-permute-start.5 = (f32[4,128,128]{2,1,0:T(8,128)S(1)}, f32[4,128,128]{2,1,0:T(8,128)S(1)}, u32[]{:S(2)}, u32[]{:S(2)}) collective-permute-start(f32[4,128,128]{2,1,0:T(8,128)S(1)} %get-tuple-element.63), channel_id=1, source_target_pairs={{0,4},{2,6},{4,8},{6,10},{8,12},{10,14},{1,5},{3,7},{5,9},{7,11},{... | collective-permute-start | bytes 786440 | tf_op jit(solution)/shard_map/ppermute | solution.py:45
  46.4 5.0 %collective-permute-start.13 = (bf16[4,128,128]{2,1,0:T(8,128)(2,1)S(1)}, bf16[4,128,128]{2,1,0:T(8,128)(2,1)S(1)}, u32[]{:S(2)}, u32[]{:S(2)}) collective-permute-start(bf16[4,128,128]{2,1,0:T(8,128)(2,1)S(1)} %get-tuple-element.58), channel_id=1, source_target_pairs={{0,2},{4,6},{8,10},{12,14},{2,0},{6,4},{10,8},{14,12},{1,3},{5,7},... | collective-permute-start | bytes 393224 | tf_op jit(solution)/shard_map/ppermute | solution.py:51
  47.2 8.3 %collective-permute-start.7 = (f32[4,128,128]{2,1,0:T(8,128)S(1)}, f32[4,128,128]{2,1,0:T(8,128)S(1)}, u32[]{:S(2)}, u32[]{:S(2)}) collective-permute-start(f32[4,128,128]{2,1,0:T(8,128)S(1)} %get-tuple-element.57), channel_id=1, source_target_pairs={{0,4},{2,6},{4,8},{6,10},{8,12},{10,14},{1,5},{3,7},{5,9},{7,11},{... | collective-permute-start | bytes 786440 | tf_op jit(solution)/shard_map/ppermute | solution.py:45
  55.6 6.9 %collective-permute-start.14 = (bf16[4,128,128]{2,1,0:T(8,128)(2,1)S(1)}, bf16[4,128,128]{2,1,0:T(8,128)(2,1)S(1)}, u32[]{:S(2)}, u32[]{:S(2)}) collective-permute-start(bf16[4,128,128]{2,1,0:T(8,128)(2,1)S(1)} %get-tuple-element.56), channel_id=1, source_target_pairs={{4,6},{8,10},{12,14},{6,4},{10,8},{14,12},{5,7},{9,11},{13,15},{7,... | collective-permute-start | bytes 393224 | tf_op jit(solution)/shard_map/ppermute | solution.py:51
  58.9 8.3 %collective-permute-start.8 = (f32[4,128,128]{2,1,0:T(8,128)S(1)}, f32[4,128,128]{2,1,0:T(8,128)S(1)}, u32[]{:S(2)}, u32[]{:S(2)}) collective-permute-start(f32[4,128,128]{2,1,0:T(8,128)S(1)} %get-tuple-element.55), channel_id=1, source_target_pairs={{4,8},{6,10},{8,12},{10,14},{5,9},{7,11},{9,13},{11,15},{20,24},{2... | collective-permute-start | bytes 786440 | tf_op jit(solution)/shard_map/ppermute | solution.py:45
  67.3 6.9 %collective-permute-start.15 = (bf16[4,128,128]{2,1,0:T(8,128)(2,1)S(1)}, bf16[4,128,128]{2,1,0:T(8,128)(2,1)S(1)}, u32[]{:S(2)}, u32[]{:S(2)}) collective-permute-start(bf16[4,128,128]{2,1,0:T(8,128)(2,1)S(1)} %get-tuple-element.54), channel_id=1, source_target_pairs={{8,10},{12,14},{10,8},{14,12},{9,11},{13,15},{11,9},{15,13},{24,26... | collective-permute-start | bytes 393224 | tf_op jit(solution)/shard_map/ppermute | solution.py:51
  69.9 8.3 %collective-permute-start.9 = (f32[4,128,128]{2,1,0:T(8,128)S(1)}, f32[4,128,128]{2,1,0:T(8,128)S(1)}, u32[]{:S(2)}, u32[]{:S(2)}) collective-permute-start(f32[4,128,128]{2,1,0:T(8,128)S(1)} %get-tuple-element.53), channel_id=1, source_target_pairs={{8,12},{10,14},{9,13},{11,15},{24,28},{26,30},{25,29},{27,31}} | collective-permute-start | bytes 786440 | tf_op jit(solution)/shard_map/ppermute | solution.py:45
  78.3 6.9 %collective-permute-start.16 = (bf16[4,128,128]{2,1,0:T(8,128)(2,1)S(1)}, bf16[4,128,128]{2,1,0:T(8,128)(2,1)S(1)}, u32[]{:S(2)}, u32[]{:S(2)}) collective-permute-start(bf16[4,128,128]{2,1,0:T(8,128)(2,1)S(1)} %fusion.25), channel_id=1, source_target_pairs={{12,14},{14,12},{13,15},{15,13},{28,30},{30,28},{29,31},{31,29}} | collective-permute-start | bytes 393224 | tf_op jit(solution)/shard_map/ppermute | solution.py:51

commit v5 on v3

--- a/solution.py
+++ b/solution.py
@@ -1,3 +1,5 @@
+import functools
+
 import jax
 import jax.numpy as jnp
 from jax import lax
@@ -60,12 +62,35 @@
     )(keyset, valset)
 
 
-def attend_kernel(query_ref, key_ref, val_ref, prefix_ref, gain_ref, out_ref, acc_ref, sumsq_ref):
+def within_kernel(head_size, query_ref, key_ref, val_ref, out_ref):
+    row_count, width = query_ref.shape
+    causal = (lax.broadcasted_iota(jnp.int32, (row_count, row_count), 0)
+              >= lax.broadcasted_iota(jnp.int32, (row_count, row_count), 1))
+    for head in range(width // head_size):
+        cols = slice(head * head_size, (head + 1) * head_size)
+        scores = lax.dot_general(query_ref[:, cols], key_ref[:, cols], (((1,), (1,)), ((), ())),
+                                 preferred_element_type=jnp.float32)
+        weights = jnp.where(causal, scores, 0.0).astype(jnp.bfloat16)
+        out_ref[:, cols] = jnp.dot(weights, val_ref[:, cols], preferred_element_type=jnp.float32)
+
+
+def within_of(query, keyset, valset, group):
+    row_count, feat_count = query.shape
+    width = group * (feat_count // H)
+    spec = pl.BlockSpec((row_count, width), lambda g: (0, g))
+    return pl.pallas_call(
+        functools.partial(within_kernel, feat_count // H),
+        grid=(H // group,),
+        in_specs=[spec, spec, spec],
+        out_specs=spec,
+        out_shape=jax.ShapeDtypeStruct((row_count, feat_count), jnp.float32),
+    )(query, keyset, valset)
+
+
+def finish_kernel(query_ref, within_ref, prefix_ref, gain_ref, out_ref, acc_ref, sumsq_ref):
     step = pl.program_id(0)
     row_count, width = query_ref.shape
     heads, head_size, _ = prefix_ref.shape
-    causal = (lax.broadcasted_iota(jnp.int32, (row_count, row_count), 0)
-              >= lax.broadcasted_iota(jnp.int32, (row_count, row_count), 1))
 
     @pl.when(step == 0)
     def _():
@@ -74,13 +99,8 @@
     sumsq = sumsq_ref[...]
     for head in range(heads):
         cols = slice(head * head_size, (head + 1) * head_size)
-        query = query_ref[:, cols]
-        scores = lax.dot_general(query, key_ref[:, cols], (((1,), (1,)), ((), ())),
-                                 preferred_element_type=jnp.float32)
-        weights = jnp.where(causal, scores, 0.0).astype(jnp.bfloat16)
-        within = jnp.dot(weights, val_ref[:, cols], preferred_element_type=jnp.float32)
-        carried = jnp.dot(query, prefix_ref[head], preferred_element_type=jnp.float32)
-        attended = within + carried
+        carried = jnp.dot(query_ref[:, cols], prefix_ref[head], preferred_element_type=jnp.float32)
+        attended = within_ref[:, cols] + carried
         acc_ref[step, :, cols] = attended
         sumsq = sumsq + jnp.sum(attended * attended, axis=1, keepdims=True)
     sumsq_ref[...] = sumsq
@@ -93,24 +113,23 @@
             out_ref[:, cols] = (acc_ref[part] * scale * gain_ref[:, cols]).astype(out_ref.dtype)
 
 
-def attend_of(query, keyset, valset, prefix_bf, full_gain, group):
+def finish_of(query, within, prefix_bf, full_gain, group):
     row_count, feat_count = query.shape
     head_size = feat_count // H
     width = group * head_size
     steps = H // group
+    spec = pl.BlockSpec((row_count, width), lambda g: (0, g))
     return pl.pallas_call(
-        attend_kernel,
+        finish_kernel,
         grid=(steps,),
-        in_specs=[pl.BlockSpec((row_count, width), lambda g: (0, g)),
-                  pl.BlockSpec((row_count, width), lambda g: (0, g)),
-                  pl.BlockSpec((row_count, width), lambda g: (0, g)),
+        in_specs=[spec, spec,
                   pl.BlockSpec((group, head_size, head_size), lambda g: (g, 0, 0)),
                   pl.BlockSpec((1, feat_count), lambda g: (0, 0))],
         out_specs=pl.BlockSpec((row_count, feat_count), lambda g: (0, 0)),
         out_shape=jax.ShapeDtypeStruct((row_count, feat_count), jnp.bfloat16),
         scratch_shapes=[pltpu.VMEM((steps, row_count, width), jnp.float32),
                         pltpu.VMEM((row_count, 1), jnp.float32)],
-    )(query, keyset, valset, prefix_bf, full_gain)
+    )(query, within, prefix_bf, full_gain)
 
 
 def shards(query_rows, key_rows, value_rows, gain):
@@ -121,7 +140,8 @@
     valset = value_rows.reshape(seq_count * row_count, feat_count)
     state_terms = state_terms_of(keyset, valset, 8)
     prefix_bf = pair_chain_prefix(state_terms, "ctx", 4)
-    normed = attend_of(query, keyset, valset, prefix_bf, full_gain, 8)
+    within = within_of(query, keyset, valset, 8)
+    normed = finish_of(query, within, prefix_bf, full_gain, 8)
     return normed.reshape(seq_count, row_count, feat_count)
 
 

time: 100 us -> 108 us (1.080)
  Pallas kernels: 17.6 us -> 24.6 us
    pallas_call x1 -> x2, Pallas kernels: 12.3 us -> 19.2 us  [the longest x1 10.5 us: within_of(): pl.pallas_call(functools.partial(within_kernel, feat_count // H), grid=(H...]
  transfers between devices with their start and end apart: 20 -> 20, of which waited for: 11 -> 9; matrix products, arithmetic and copies ran while one was open for 4% -> 3% of each run, Pallas kernels for 0% -> 10%
where the time goes in v5:
time: 108 us; the launch traced here: 107 us
  waiting for transfers between devices  52.1 us (48%)
  Pallas kernels  24.6 us (23%)
  starting transfers between devices  17.7 us (16%)
  other arithmetic  9.36 us (9%)
  blocking collectives  1.93 us (2%)
  local copies, waits for them, and re-layouts  1.21 us (1%)
    ppermute x4, waiting for transfers between devices, pair_chain_prefix(): got = lax.ppermute(other_all[piece * step:(piece + 1) * step], axis, swap)  22.9 us
    ppermute x12, waiting for transfers between devices, pair_chain_prefix(): carried = carried + lax.ppermute(carried + total, axis, links)  22.9 us
    ppermute x12, starting transfers between devices, pair_chain_prefix(): carried = carried + lax.ppermute(carried + total, axis, links)  10.5 us
    pallas_call x1, Pallas kernels, within_of(): pl.pallas_call(functools.partial(within_kernel, feat_count // H), grid=(H...  10.5 us
    pallas_call x1, Pallas kernels, finish_of(): pl.pallas_call(finish_kernel, grid=(steps,), in_specs=[spec, spec, pl.Blo...  8.74 us
    ppermute x4, waiting for transfers between devices, pair_chain_prefix(): backs.append(lax.ppermute(send, axis, swap))  6.27 us
    pallas_call x1, Pallas kernels, state_terms_of(): pl.pallas_call(state_kernel, grid=(H // group,), in_specs=[pl.BlockSpec((...  5.35 us
    ppermute x4, starting transfers between devices, pair_chain_prefix(): backs.append(lax.ppermute(send, axis, swap))  4.11 us
  transfers between devices with their start and end apart: 20, of which 9 were waited for; matrix products, arithmetic and copies ran while one was open for 3% of the time, Pallas kernels for 10%

profile of v5, /device:TPU:30, one launch (start us, length us, event | category | flops | bytes accessed | tf_op | source)
XLA Modules:
  0.0 107.2 jit_solution(2569088997289797419)
XLA Ops:
  0.0 5.4 %shard_map.47 = f32[32,128,128]{2,1,0:T(8,128)} custom-call(bf16[384,4096]{1,0:T(8,128)(2,1)} %bitcast.5, bf16[384,4096]{1,0:T(8,128)(2,1)} %bitcast.7), custom_call_target="tpu_custom_call" | custom-call | tf_op jit(solution)/shard_map/pallas_call | solution.py:55
  5.4 1.1 %constant_dynamic-slice_fusion.3 = f32[4,128,128]{2,1,0:T(8,128)S(1)} fusion(f32[32,128,128]{2,1,0:T(8,128)} %shard_map.47, s32[]{:T(128)S(6)} %add.130), kind=kLoop, calls=%fused_computation.23 | loop fusion | bytes 524292 | tf_op jit(solution)/shard_map/slice | solution.py:26
  6.5 0.6 collective-permute-start.12
  7.0 7.5 %collective-permute-done.12 = f32[4,128,128]{2,1,0:T(8,128)S(1)} collective-permute-done((f32[4,128,128]{2,1,0:T(8,128)S(1)}, f32[4,128,128]{2,1,0:T(8,128)S(1)}, u32[]{:S(2)}, u32[]{:S(2)}) %collective-permute-start.12) | collective-permute-done | bytes 262176 | tf_op jit(solution)/shard_map/ppermute | solution.py:26
  14.6 2.2 %dynamic-slice_add_fusion = (f32[4,128,128]{2,1,0:T(8,128)S(1)}, f32[4,128,128]{2,1,0:T(8,128)}, f32[4,128,128]{2,1,0:T(8,128)}, f32[4,128,128]{2,1,0:T(8,128)S(1)}) fusion(f32[4,128,128]{2,1,0:T(8,128)S(1)} %collective-permute-done.12, f32[32,128,128]{2,1,0:T(8,128)} %shard_map.47, s32[]{:T(128)S(6)} %add.129, s32[]{:T(128)S(6)} %add.128, s32[]{:T(128)S(6)} %add.126, ...), kind=kLoop, calls=%fused_computation.12 | loop fusion | flops 65536 | bytes 2359312 | tf_op jit(solution)/shard_map/add | solution.py:27
  16.8 0.5 collective-permute-start.8
  17.3 1.5 %collective-permute-start.4 = (f32[4,128,128]{2,1,0:T(8,128)}, f32[4,128,128]{2,1,0:T(8,128)S(1)}, u32[]{:S(2)}, u32[]{:S(2)}) collective-permute-start(f32[4,128,128]{2,1,0:T(8,128)} %get-tuple-element.19), channel_id=1, source_target_pairs={{0,2},{4,6},{8,10},{12,14},{2,0},{6,4},{10,8},{14,12},{1,3},{5,7},... | collective-permute-start | bytes 786440 | tf_op jit(solution)/shard_map/ppermute | solution.py:26
  18.8 0.5 collective-permute-start
  19.3 0.7 collective-permute-start.13
  20.0 6.2 %collective-permute-done.8 = f32[4,128,128]{2,1,0:T(8,128)S(1)} collective-permute-done((f32[4,128,128]{2,1,0:T(8,128)}, f32[4,128,128]{2,1,0:T(8,128)S(1)}, u32[]{:S(2)}, u32[]{:S(2)}) %collective-permute-start.8) | collective-permute-done | bytes 262176 | tf_op jit(solution)/shard_map/ppermute | solution.py:26
  26.2 5.6 %collective-permute-done.4 = f32[4,128,128]{2,1,0:T(8,128)S(1)} collective-permute-done((f32[4,128,128]{2,1,0:T(8,128)}, f32[4,128,128]{2,1,0:T(8,128)S(1)}, u32[]{:S(2)}, u32[]{:S(2)}) %collective-permute-start.4) | collective-permute-done | bytes 262176 | tf_op jit(solution)/shard_map/ppermute | solution.py:26
  31.8 3.5 %collective-permute-done = f32[4,128,128]{2,1,0:T(8,128)S(1)} collective-permute-done((f32[4,128,128]{2,1,0:T(8,128)S(1)}, f32[4,128,128]{2,1,0:T(8,128)S(1)}, u32[]{:S(2)}, u32[]{:S(2)}) %collective-permute-start) | collective-permute-done | bytes 262176 | tf_op jit(solution)/shard_map/ppermute | solution.py:26
  35.4 0.1 dynamic-slice_add_fusion.1
  35.5 0.7 collective-permute-start.9
  36.2 0.7 collective-permute-start.5
  36.9 0.7 collective-permute-start.14
  37.6 0.7 collective-permute-start.1
  38.3 0.0 collective-permute-done.9
  38.3 0.7 collective-permute-start.10
  39.0 0.0 collective-permute-done.5
  39.1 0.7 collective-permute-start.6
  39.8 0.8 fusion
  40.5 1.3 %collective-permute-start.15 = (f32[4,128,128]{2,1,0:T(8,128)}, f32[4,128,128]{2,1,0:T(8,128)}, u32[]{:S(2)}, u32[]{:S(2)}) collective-permute-start(f32[4,128,128]{2,1,0:T(8,128)} %get-tuple-element.5), channel_id=1, source_target_pairs={{8,12},{10,14},{9,13},{11,15},{24,28},{26,30},{25,29},{27,31}} | collective-permute-start | bytes 786440 | tf_op jit(solution)/shard_map/ppermute | solution.py:31
  41.8 0.0 collective-permute-done.1
  41.8 0.7 collective-permute-start.2
  42.5 0.0 collective-permute-done.10
  42.5 0.8 fusion.1
  43.3 1.3 %collective-permute-start.11 = (f32[4,128,128]{2,1,0:T(8,128)}, f32[4,128,128]{2,1,0:T(8,128)}, u32[]{:S(2)}, u32[]{:S(2)}) collective-permute-start(f32[4,128,128]{2,1,0:T(8,128)} %get-tuple-element.7), channel_id=1, source_target_pairs={{8,12},{10,14},{9,13},{11,15},{24,28},{26,30},{25,29},{27,31}} | collective-permute-start | bytes 786440 | tf_op jit(solution)/shard_map/ppermute | solution.py:31
  44.6 0.0 collective-permute-done.6
  44.6 0.8 fusion.2
  45.4 1.3 %collective-permute-start.7 = (f32[4,128,128]{2,1,0:T(8,128)}, f32[4,128,128]{2,1,0:T(8,128)}, u32[]{:S(2)}, u32[]{:S(2)}) collective-permute-start(f32[4,128,128]{2,1,0:T(8,128)} %get-tuple-element.9), channel_id=1, source_target_pairs={{8,12},{10,14},{9,13},{11,15},{24,28},{26,30},{25,29},{27,31}} | collective-permute-start | bytes 786440 | tf_op jit(solution)/shard_map/ppermute | solution.py:31
  46.7 0.9 fusion.3
  47.7 1.3 %collective-permute-start.3 = (f32[4,128,128]{2,1,0:T(8,128)}, f32[4,128,128]{2,1,0:T(8,128)}, u32[]{:S(2)}, u32[]{:S(2)}) collective-permute-start(f32[4,128,128]{2,1,0:T(8,128)} %get-tuple-element.11), channel_id=1, source_target_pairs={{8,12},{10,14},{9,13},{11,15},{24,28},{26,30},{25,29},{27,31}} | collective-permute-start | bytes 786440 | tf_op jit(solution)/shard_map/ppermute | solution.py:31
  48.9 8.0 %collective-permute-done.15 = f32[4,128,128]{2,1,0:T(8,128)} collective-permute-done((f32[4,128,128]{2,1,0:T(8,128)}, f32[4,128,128]{2,1,0:T(8,128)}, u32[]{:S(2)}, u32[]{:S(2)}) %collective-permute-start.15) | collective-permute-done | bytes 262176 | tf_op jit(solution)/shard_map/ppermute | solution.py:31
  57.0 6.1 %collective-permute-done.11 = f32[4,128,128]{2,1,0:T(8,128)} collective-permute-done((f32[4,128,128]{2,1,0:T(8,128)}, f32[4,128,128]{2,1,0:T(8,128)}, u32[]{:S(2)}, u32[]{:S(2)}) %collective-permute-start.11) | collective-permute-done | bytes 262176 | tf_op jit(solution)/shard_map/ppermute | solution.py:31
  63.1 5.9 %collective-permute-done.7 = f32[4,128,128]{2,1,0:T(8,128)} collective-permute-done((f32[4,128,128]{2,1,0:T(8,128)}, f32[4,128,128]{2,1,0:T(8,128)}, u32[]{:S(2)}, u32[]{:S(2)}) %collective-permute-start.7) | collective-permute-done | bytes 262176 | tf_op jit(solution)/shard_map/ppermute | solution.py:31
  69.0 2.8 %collective-permute-done.3 = f32[4,128,128]{2,1,0:T(8,128)} collective-permute-done((f32[4,128,128]{2,1,0:T(8,128)}, f32[4,128,128]{2,1,0:T(8,128)}, u32[]{:S(2)}, u32[]{:S(2)}) %collective-permute-start.3) | collective-permute-done | bytes 262176 | tf_op jit(solution)/shard_map/ppermute | solution.py:31
  71.8 2.5 %add_convert_fusion = (bf16[4,128,128]{2,1,0:T(8,128)(2,1)}, bf16[4,128,128]{2,1,0:T(8,128)(2,1)}, bf16[4,128,128]{2,1,0:T(8,128)(2,1)}, bf16[4,128,128]{2,1,0:T...) fusion(f32[32,128,128]{2,1,0:T(8,128)S(1)} %copy-done, ...), kind=kLoop, calls=%fused_computation.4 | loop fusion | flops 1835008 | bytes 5242897 | tf_op jit(solution)/shard_map/convert_element_type | solution.py:33
  74.4 0.4 collective-permute-start.16
  74.7 1.6 %collective-permute-start.17 = (bf16[4,128,128]{2,1,0:T(8,128)(2,1)}, bf16[4,128,128]{2,1,0:T(8,128)(2,1)S(1)}, u32[]{:S(2)}, u32[]{:S(2)}) collective-permute-start(bf16[4,128,128]{2,1,0:T(8,128)(2,1)} %get-tuple-element.15), channel_id=1, source_target_pairs={{0,2},{4,6},{8,10},{12,14},{2,0},{6,4},{10,8},{14,12},{1,3},{5,7},... | collective-permute-start | bytes 393224 | tf_op jit(solution)/shard_map/ppermute | solution.py:34
  76.4 10.5 %shard_map.46.within_ref = f32[384,4096]{1,0:T(8,128)} custom-call(bf16[384,4096]{1,0:T(8,128)(2,1)} %bitcast.9, bf16[384,4096]{1,0:T(8,128)(2,1)} %bitcast.6, bf16[384,4096]{1,0:T(8,128)(2,1)} %bitcast.8), custom_call_target="tpu_custom_call" | custom-call | tf_op jit(solution)/shard_map/pallas_call | solution.py:81
  86.9 1.9 %all_gather.3 = f32[4096]{0:T(1024)} all-gather(f32[2048]{0:T(1024)S(1)} %copy-done.7), channel_id=1, replica_groups=mesh['groups'=2,'ctx'=8,'dp'=2] {'dp'}, dimensions={0}, use_global_device_ids=true | all-gather | bytes 24576 | tf_op jit(solution)/shard_map/all_gather | solution.py:137
  88.8 0.5 collective-permute-start.19
  89.3 1.6 %collective-permute-start.18 = (bf16[4,128,128]{2,1,0:T(8,128)(2,1)S(1)}, bf16[4,128,128]{2,1,0:T(8,128)(2,1)S(1)}, u32[]{:S(2)}, u32[]{:S(2)}) collective-permute-start(bf16[4,128,128]{2,1,0:T(8,128)(2,1)S(1)} %copy-done.6), channel_id=1, source_target_pairs={{0,2},{4,6},{8,10},{12,14},{2,0},{6,4},{10,8},{14,12},{1,3},{5,7},... | collective-permute-start | bytes 393224 | tf_op jit(solution)/shard_map/ppermute | solution.py:34
  91.0 6.3 %collective-permute-done.18 = bf16[4,128,128]{2,1,0:T(8,128)(2,1)S(1)} collective-permute-done((bf16[4,128,128]{2,1,0:T(8,128)(2,1)S(1)}, bf16[4,128,128]{2,1,0:T(8,128)(2,1)S(1)}, u32[]{:S(2)}, u32[]{:S(2)}) %collective-permute-start.18) | collective-permute-done | bytes 131104 | tf_op jit(solution)/shard_map/ppermute | solution.py:34
  97.3 0.1 broadcast_select_fusion.1
  97.4 1.1 pad_maximum_fusion.prefix_ref
  98.5 8.7 %shard_map.48 = bf16[384,4096]{1,0:T(8,128)(2,1)} custom-call(bf16[384,4096]{1,0:T(8,128)(2,1)} %bitcast.10, f32[384,4096]{1,0:T(8,128)} %shard_map.46.within_ref, bf16[32,128,128]{2,1,0:T(8,128)(2,1)} %pad_maximum_fusion.prefix_ref, f32[1,4096]{1,0:T(1,128)} %bitcast.11), custom_call_target="tpu_custom_call" | custom-call | tf_op jit(solution)/shard_map/pallas_call | solution.py:122
  (30 shorter events, 0.3 us)
Async XLA Ops:
  5.4 30.0 %copy-start = (f32[32,128,128]{2,1,0:T(8,128)S(1)}, f32[32,128,128]{2,1,0:T(8,128)}, u32[]{:S(2)}) copy-start(f32[32,128,128]{2,1,0:T(8,128)} %shard_map.47) | copy-start | bytes 6291460
  6.5 8.1 %collective-permute-start.12 = (f32[4,128,128]{2,1,0:T(8,128)S(1)}, f32[4,128,128]{2,1,0:T(8,128)S(1)}, u32[]{:S(2)}, u32[]{:S(2)}) collective-permute-start(f32[4,128,128]{2,1,0:T(8,128)S(1)} %constant_dynamic-slice_fusion.3), channel_id=1, source_target_pairs={{0,2},{4,6},{8,10},{12,14},{2,0},{6,4},{10,8},{14,12},{1,3},{5,7},... | collective-permute-start | bytes 786440 | tf_op jit(solution)/shard_map/ppermute | solution.py:26
  14.6 2.2 %copy-start.1 = (f32[4,128,128]{2,1,0:T(8,128)}, f32[4,128,128]{2,1,0:T(8,128)S(1)}, u32[]{:S(2)}) copy-start(f32[4,128,128]{2,1,0:T(8,128)S(1)} %collective-permute-done.12) | copy-start | bytes 786436
  16.8 9.5 %collective-permute-start.8 = (f32[4,128,128]{2,1,0:T(8,128)}, f32[4,128,128]{2,1,0:T(8,128)S(1)}, u32[]{:S(2)}, u32[]{:S(2)}) collective-permute-start(f32[4,128,128]{2,1,0:T(8,128)} %get-tuple-element.18), channel_id=1, source_target_pairs={{0,2},{4,6},{8,10},{12,14},{2,0},{6,4},{10,8},{14,12},{1,3},{5,7},... | collective-permute-start | bytes 786440 | tf_op jit(solution)/shard_map/ppermute | solution.py:26
  17.3 14.6 %collective-permute-start.4 = (f32[4,128,128]{2,1,0:T(8,128)}, f32[4,128,128]{2,1,0:T(8,128)S(1)}, u32[]{:S(2)}, u32[]{:S(2)}) collective-permute-start(f32[4,128,128]{2,1,0:T(8,128)} %get-tuple-element.19), channel_id=1, source_target_pairs={{0,2},{4,6},{8,10},{12,14},{2,0},{6,4},{10,8},{14,12},{1,3},{5,7},... | collective-permute-start | bytes 786440 | tf_op jit(solution)/shard_map/ppermute | solution.py:26
  18.8 16.6 %collective-permute-start = (f32[4,128,128]{2,1,0:T(8,128)S(1)}, f32[4,128,128]{2,1,0:T(8,128)S(1)}, u32[]{:S(2)}, u32[]{:S(2)}) collective-permute-start(f32[4,128,128]{2,1,0:T(8,128)S(1)} %get-tuple-element.20), channel_id=1, source_target_pairs={{0,2},{4,6},{8,10},{12,14},{2,0},{6,4},{10,8},{14,12},{1,3},{5,7},... | collective-permute-start | bytes 786440 | tf_op jit(solution)/shard_map/ppermute | solution.py:26
  19.3 17.5 %collective-permute-start.13 = (f32[4,128,128]{2,1,0:T(8,128)S(1)}, f32[4,128,128]{2,1,0:T(8,128)S(1)}, u32[]{:S(2)}, u32[]{:S(2)}) collective-permute-start(f32[4,128,128]{2,1,0:T(8,128)S(1)} %get-tuple-element.17), channel_id=1, source_target_pairs={{0,4},{2,6},{1,5},{3,7},{16,20},{18,22},{17,21},{19,23}} | collective-permute-start | bytes 786440 | tf_op jit(solution)/shard_map/ppermute | solution.py:31
  35.5 2.8 %collective-permute-start.9 = (f32[4,128,128]{2,1,0:T(8,128)S(1)}, f32[4,128,128]{2,1,0:T(8,128)S(1)}, u32[]{:S(2)}, u32[]{:S(2)}) collective-permute-start(f32[4,128,128]{2,1,0:T(8,128)S(1)} %get-tuple-element.21), channel_id=1, source_target_pairs={{0,4},{2,6},{1,5},{3,7},{16,20},{18,22},{17,21},{19,23}} | collective-permute-start | bytes 786440 | tf_op jit(solution)/shard_map/ppermute | solution.py:31
  36.2 2.8 %collective-permute-start.5 = (f32[4,128,128]{2,1,0:T(8,128)S(1)}, f32[4,128,128]{2,1,0:T(8,128)S(1)}, u32[]{:S(2)}, u32[]{:S(2)}) collective-permute-start(f32[4,128,128]{2,1,0:T(8,128)S(1)} %get-tuple-element.22), channel_id=1, source_target_pairs={{0,4},{2,6},{1,5},{3,7},{16,20},{18,22},{17,21},{19,23}} | collective-permute-start | bytes 786440 | tf_op jit(solution)/shard_map/ppermute | solution.py:31
  36.9 2.8 %collective-permute-start.14 = (f32[4,128,128]{2,1,0:T(8,128)S(1)}, f32[4,128,128]{2,1,0:T(8,128)S(1)}, u32[]{:S(2)}, u32[]{:S(2)}) collective-permute-start(f32[4,128,128]{2,1,0:T(8,128)S(1)} %add.116), channel_id=1, source_target_pairs={{4,8},{6,10},{5,9},{7,11},{20,24},{22,26},{21,25},{23,27}} | collective-permute-start | bytes 786440 | tf_op jit(solution)/shard_map/ppermute | solution.py:31
  37.6 4.2 %collective-permute-start.1 = (f32[4,128,128]{2,1,0:T(8,128)S(1)}, f32[4,128,128]{2,1,0:T(8,128)S(1)}, u32[]{:S(2)}, u32[]{:S(2)}) collective-permute-start(f32[4,128,128]{2,1,0:T(8,128)S(1)} %get-tuple-element.23), channel_id=1, source_target_pairs={{0,4},{2,6},{1,5},{3,7},{16,20},{18,22},{17,21},{19,23}} | collective-permute-start | bytes 786440 | tf_op jit(solution)/shard_map/ppermute | solution.py:31
  38.3 4.2 %collective-permute-start.10 = (f32[4,128,128]{2,1,0:T(8,128)S(1)}, f32[4,128,128]{2,1,0:T(8,128)S(1)}, u32[]{:S(2)}, u32[]{:S(2)}) collective-permute-start(f32[4,128,128]{2,1,0:T(8,128)S(1)} %add.110), channel_id=1, source_target_pairs={{4,8},{6,10},{5,9},{7,11},{20,24},{22,26},{21,25},{23,27}} | collective-permute-start | bytes 786440 | tf_op jit(solution)/shard_map/ppermute | solution.py:31
  39.1 5.5 %collective-permute-start.6 = (f32[4,128,128]{2,1,0:T(8,128)S(1)}, f32[4,128,128]{2,1,0:T(8,128)S(1)}, u32[]{:S(2)}, u32[]{:S(2)}) collective-permute-start(f32[4,128,128]{2,1,0:T(8,128)S(1)} %add.104), channel_id=1, source_target_pairs={{4,8},{6,10},{5,9},{7,11},{20,24},{22,26},{21,25},{23,27}} | collective-permute-start | bytes 786440 | tf_op jit(solution)/shard_map/ppermute | solution.py:31
  40.5 16.5 %collective-permute-start.15 = (f32[4,128,128]{2,1,0:T(8,128)}, f32[4,128,128]{2,1,0:T(8,128)}, u32[]{:S(2)}, u32[]{:S(2)}) collective-permute-start(f32[4,128,128]{2,1,0:T(8,128)} %get-tuple-element.5), channel_id=1, source_target_pairs={{8,12},{10,14},{9,13},{11,15},{24,28},{26,30},{25,29},{27,31}} | collective-permute-start | bytes 786440 | tf_op jit(solution)/shard_map/ppermute | solution.py:31
  41.8 4.9 %collective-permute-start.2 = (f32[4,128,128]{2,1,0:T(8,128)S(1)}, f32[4,128,128]{2,1,0:T(8,128)S(1)}, u32[]{:S(2)}, u32[]{:S(2)}) collective-permute-start(f32[4,128,128]{2,1,0:T(8,128)S(1)} %add.98), channel_id=1, source_target_pairs={{4,8},{6,10},{5,9},{7,11},{20,24},{22,26},{21,25},{23,27}} | collective-permute-start | bytes 786440 | tf_op jit(solution)/shard_map/ppermute | solution.py:31
  43.3 19.8 %collective-permute-start.11 = (f32[4,128,128]{2,1,0:T(8,128)}, f32[4,128,128]{2,1,0:T(8,128)}, u32[]{:S(2)}, u32[]{:S(2)}) collective-permute-start(f32[4,128,128]{2,1,0:T(8,128)} %get-tuple-element.7), channel_id=1, source_target_pairs={{8,12},{10,14},{9,13},{11,15},{24,28},{26,30},{25,29},{27,31}} | collective-permute-start | bytes 786440 | tf_op jit(solution)/shard_map/ppermute | solution.py:31
  45.4 23.6 %collective-permute-start.7 = (f32[4,128,128]{2,1,0:T(8,128)}, f32[4,128,128]{2,1,0:T(8,128)}, u32[]{:S(2)}, u32[]{:S(2)}) collective-permute-start(f32[4,128,128]{2,1,0:T(8,128)} %get-tuple-element.9), channel_id=1, source_target_pairs={{8,12},{10,14},{9,13},{11,15},{24,28},{26,30},{25,29},{27,31}} | collective-permute-start | bytes 786440 | tf_op jit(solution)/shard_map/ppermute | solution.py:31
  47.7 24.2 %collective-permute-start.3 = (f32[4,128,128]{2,1,0:T(8,128)}, f32[4,128,128]{2,1,0:T(8,128)}, u32[]{:S(2)}, u32[]{:S(2)}) collective-permute-start(f32[4,128,128]{2,1,0:T(8,128)} %get-tuple-element.11), channel_id=1, source_target_pairs={{8,12},{10,14},{9,13},{11,15},{24,28},{26,30},{25,29},{27,31}} | collective-permute-start | bytes 786440 | tf_op jit(solution)/shard_map/ppermute | solution.py:31
  74.4 16.6 %collective-permute-start.16 = (bf16[4,128,128]{2,1,0:T(8,128)(2,1)}, bf16[4,128,128]{2,1,0:T(8,128)(2,1)S(1)}, u32[]{:S(2)}, u32[]{:S(2)}) collective-permute-start(bf16[4,128,128]{2,1,0:T(8,128)(2,1)} %get-tuple-element.14), channel_id=1, source_target_pairs={{0,2},{4,6},{8,10},{12,14},{2,0},{6,4},{10,8},{14,12},{1,3},{5,7},... | collective-permute-start | bytes 393224 | tf_op jit(solution)/shard_map/ppermute | solution.py:34
  74.7 16.2 %collective-permute-start.17 = (bf16[4,128,128]{2,1,0:T(8,128)(2,1)}, bf16[4,128,128]{2,1,0:T(8,128)(2,1)S(1)}, u32[]{:S(2)}, u32[]{:S(2)}) collective-permute-start(bf16[4,128,128]{2,1,0:T(8,128)(2,1)} %get-tuple-element.15), channel_id=1, source_target_pairs={{0,2},{4,6},{8,10},{12,14},{2,0},{6,4},{10,8},{14,12},{1,3},{5,7},... | collective-permute-start | bytes 393224 | tf_op jit(solution)/shard_map/ppermute | solution.py:34
  76.4 10.5 %copy-start.7 = (f32[2048]{0:T(1024)S(1)}, f32[2048]{0:T(1024)}, u32[]{:S(2)}) copy-start(f32[2048]{0:T(1024)} %param.7) | copy-start | bytes 24580
  76.4 12.5 %copy-start.5 = (bf16[4,128,128]{2,1,0:T(8,128)(2,1)S(1)}, bf16[4,128,128]{2,1,0:T(8,128)(2,1)}, u32[]{:S(2)}) copy-start(bf16[4,128,128]{2,1,0:T(8,128)(2,1)} %get-tuple-element.13) | copy-start | bytes 393220
  76.4 12.9 %copy-start.6 = (bf16[4,128,128]{2,1,0:T(8,128)(2,1)S(1)}, bf16[4,128,128]{2,1,0:T(8,128)(2,1)}, u32[]{:S(2)}) copy-start(bf16[4,128,128]{2,1,0:T(8,128)(2,1)} %get-tuple-element.16) | copy-start | bytes 393220
  76.4 20.9 %copy-start.2 = (bf16[4,128,128]{2,1,0:T(8,128)(2,1)S(1)}, bf16[4,128,128]{2,1,0:T(8,128)(2,1)}, u32[]{:S(2)}) copy-start(bf16[4,128,128]{2,1,0:T(8,128)(2,1)} %get-tuple-element.27) | copy-start | bytes 393220
  76.4 20.9 %copy-start.3 = (bf16[4,128,128]{2,1,0:T(8,128)(2,1)S(1)}, bf16[4,128,128]{2,1,0:T(8,128)(2,1)}, u32[]{:S(2)}) copy-start(bf16[4,128,128]{2,1,0:T(8,128)(2,1)} %get-tuple-element.28) | copy-start | bytes 393220
  76.4 20.9 %copy-start.4 = (bf16[4,128,128]{2,1,0:T(8,128)(2,1)S(1)}, bf16[4,128,128]{2,1,0:T(8,128)(2,1)}, u32[]{:S(2)}) copy-start(bf16[4,128,128]{2,1,0:T(8,128)(2,1)} %get-tuple-element.29) | copy-start | bytes 393220
  88.8 8.4 %collective-permute-start.19 = (bf16[4,128,128]{2,1,0:T(8,128)(2,1)S(1)}, bf16[4,128,128]{2,1,0:T(8,128)(2,1)S(1)}, u32[]{:S(2)}, u32[]{:S(2)}) collective-permute-start(bf16[4,128,128]{2,1,0:T(8,128)(2,1)S(1)} %copy-done.5), channel_id=1, source_target_pairs={{0,2},{4,6},{8,10},{12,14},{2,0},{6,4},{10,8},{14,12},{1,3},{5,7},... | collective-permute-start | bytes 393224 | tf_op jit(solution)/shard_map/ppermute | solution.py:34
  89.3 7.9 %collective-permute-start.18 = (bf16[4,128,128]{2,1,0:T(8,128)(2,1)S(1)}, bf16[4,128,128]{2,1,0:T(8,128)(2,1)S(1)}, u32[]{:S(2)}, u32[]{:S(2)}) collective-permute-start(bf16[4,128,128]{2,1,0:T(8,128)(2,1)S(1)} %copy-done.6), channel_id=1, source_target_pairs={{0,2},{4,6},{8,10},{12,14},{2,0},{6,4},{10,8},{14,12},{1,3},{5,7},... | collective-permute-start | bytes 393224 | tf_op jit(solution)/shard_map/ppermute | solution.py:34

commit v6 on v3

--- a/solution.py
+++ b/solution.py
@@ -17,16 +17,20 @@
     mine_all = lax.dynamic_slice_in_dim(terms, mine_at * half, half, 0)
     other_all = lax.dynamic_slice_in_dim(terms, (1 - mine_at) * half, half, 0)
     swap = [(2 * i, 2 * i + 1) for i in range(pairs)] + [(2 * i + 1, 2 * i) for i in range(pairs)]
+    got_all = lax.ppermute(other_all, axis, swap)
     step = half // pieces
     keeps, backs = [], []
     for piece in range(pieces):
         mine = mine_all[piece * step:(piece + 1) * step]
-        got = lax.ppermute(other_all[piece * step:(piece + 1) * step], axis, swap)
+        got = got_all[piece * step:(piece + 1) * step]
         total = mine + got
         carried = jnp.zeros_like(total)
         for hop in range(1, pairs):
             links = [(2 * (hop - 1) + side, 2 * hop + side) for side in range(2)]
-            carried = carried + lax.ppermute(carried + total, axis, links)
+            send = carried + total
+            if hop == pairs - 1 and piece >= 2:
+                send, _ = lax.optimization_barrier((send, backs[piece - 2]))
+            carried = carried + lax.ppermute(send, axis, links)
         keeps.append((carried + jnp.where(first, 0.0, got)).astype(jnp.bfloat16))
         send = (carried + jnp.where(first, mine, 0.0)).astype(jnp.bfloat16)
         backs.append(lax.ppermute(send, axis, swap))

time: 100 us -> 109 us (1.090)
  waiting for transfers between devices: 52.1 us -> 61.4 us
  starting transfers between devices: 17.8 us -> 14.9 us
  local copies, waits for them, and re-layouts: 1.19 us -> 2.55 us
    ppermute x4, waiting for transfers between devices: 6.27 us -> 12.1 us  [pair_chain_prefix(): backs.append(lax.ppermute(send, axis, swap))]
    ppermute x16 -> x13, waiting for transfers between devices: 45.8 us -> 49.2 us  [the longest x12 24.6 us: pair_chain_prefix(): carried = carried + lax.ppermute(send, axis, links)]
    dynamic_slice x0 -> x1, local copies, waits for them, and re-layouts: none -> 2.46 us  [pair_chain_prefix(): other_all = lax.dynamic_slice_in_dim(terms, (1 - mine_at) * half, half, 0)]
    ppermute x4, starting transfers between devices: 4.16 us -> 2.34 us  [pair_chain_prefix(): backs.append(lax.ppermute(send, axis, swap))]
    add x8, other arithmetic: 3.44 us -> 4.99 us  [pair_chain_prefix(): send = carried + total]
    add x2 -> x1, other arithmetic: 2.27 us -> 0.91 us  [pair_chain_prefix(): total = mine + got]
    convert_element_type x0 -> x1, other arithmetic: none -> 1.24 us  [pair_chain_prefix(): keeps.append((carried + jnp.where(first, 0.0, got)).astype(jnp.bfloat16))]
    slice x1 -> x0, local copies, waits for them, and re-layouts: 1.12 us -> none  [pair_chain_prefix(): got = lax.ppermute(other_all[piece * step:(piece + 1) * step], axis, swap)]
  transfers between devices with their start and end apart: 20 -> 17, of which waited for: 11 -> 7; matrix products, arithmetic and copies ran while one was open for 4% -> 7% of each run, Pallas kernels for 0% -> 0%
where the time goes in v6:
time: 109 us; the launch traced here: 108 us
  waiting for transfers between devices  61.4 us (56%)
  Pallas kernels  17.7 us (16%)
  starting transfers between devices  14.9 us (14%)
  other arithmetic  9.43 us (9%)
  local copies, waits for them, and re-layouts  2.55 us (2%)
  blocking collectives  1.95 us (2%)
    ppermute x12, waiting for transfers between devices, pair_chain_prefix(): carried = carried + lax.ppermute(send, axis, links)  24.6 us
    ppermute x1, waiting for transfers between devices, pair_chain_prefix(): got_all = lax.ppermute(other_all, axis, swap)  24.6 us
    pallas_call x1, Pallas kernels, attend_of(): pl.pallas_call(attend_kernel, grid=(steps,), in_specs=[pl.BlockSpec((row_...  12.4 us
    ppermute x4, waiting for transfers between devices, pair_chain_prefix(): backs.append(lax.ppermute(send, axis, swap))  12.1 us
    ppermute x12, starting transfers between devices, pair_chain_prefix(): carried = carried + lax.ppermute(send, axis, links)  12.1 us
    pallas_call x1, Pallas kernels, state_terms_of(): pl.pallas_call(state_kernel, grid=(H // group,), in_specs=[pl.BlockSpec((...  5.36 us
    add x8, other arithmetic, pair_chain_prefix(): send = carried + total  4.99 us
    dynamic_slice x1, local copies, waits for them, and re-layouts, pair_chain_prefix(): other_all = lax.dynamic_slice_in_dim(terms, (1 - mine_at) * half, half, 0)  2.46 us
  transfers between devices with their start and end apart: 17, of which 7 were waited for; matrix products, arithmetic and copies ran while one was open for 7% of the time, Pallas kernels for 0%

profile of v6, /device:TPU:30, one launch (start us, length us, event | category | flops | bytes accessed | tf_op | source)
XLA Modules:
  0.0 108.2 jit_solution(6193412952032824163)
XLA Ops:
  0.0 5.4 %shard_map.46 = f32[32,128,128]{2,1,0:T(8,128)} custom-call(bf16[384,4096]{1,0:T(8,128)(2,1)} %bitcast.5, bf16[384,4096]{1,0:T(8,128)(2,1)} %bitcast.7), custom_call_target="tpu_custom_call" | custom-call | tf_op jit(solution)/shard_map/pallas_call | solution.py:57
  5.4 2.5 %constant_dynamic-slice_fusion = f32[16,128,128]{2,1,0:T(8,128)} fusion(f32[32,128,128]{2,1,0:T(8,128)} %shard_map.46, s32[]{:T(128)S(6)} %select_n.66), kind=kLoop, calls=%fused_computation.20 | loop fusion | bytes 2097156 | tf_op jit(solution)/shard_map/dynamic_slice | solution.py:18
  7.8 0.5 collective-permute-start
  8.3 24.6 %collective-permute-done = f32[16,128,128]{2,1,0:T(8,128)S(1)} collective-permute-done((f32[16,128,128]{2,1,0:T(8,128)}, f32[16,128,128]{2,1,0:T(8,128)S(1)}, u32[]{:S(2)}, u32[]{:S(2)}) %collective-permute-start) | collective-permute-done | bytes 1048608 | tf_op jit(solution)/shard_map/ppermute | solution.py:20
  32.9 0.9 slice_add_fusion
  33.8 0.7 collective-permute-start.4
  34.5 0.7 collective-permute-start.1
  35.2 0.0 collective-permute-done.4
  35.3 0.7 collective-permute-start.5
  35.9 1.4 %collective-permute-start.11 = (f32[4,128,128]{2,1,0:T(8,128)}, f32[4,128,128]{2,1,0:T(8,128)}, u32[]{:S(2)}, u32[]{:S(2)}) collective-permute-start(f32[4,128,128]{2,1,0:T(8,128)} %get-tuple-element.17), channel_id=1, source_target_pairs={{0,4},{2,6},{1,5},{3,7},{16,20},{18,22},{17,21},{19,23}} | collective-permute-start | bytes 786440 | tf_op jit(solution)/shard_map/ppermute | solution.py:33
  37.3 0.0 collective-permute-done.1
  37.3 0.8 add.98
  38.1 1.4 %collective-permute-start.2 = (f32[4,128,128]{2,1,0:T(8,128)}, f32[4,128,128]{2,1,0:T(8,128)}, u32[]{:S(2)}, u32[]{:S(2)}) collective-permute-start(f32[4,128,128]{2,1,0:T(8,128)} %add.98), channel_id=1, source_target_pairs={{4,8},{6,10},{5,9},{7,11},{20,24},{22,26},{21,25},{23,27}} | collective-permute-start | bytes 786440 | tf_op jit(solution)/shard_map/ppermute | solution.py:33
  39.5 0.0 collective-permute-done.5
  39.5 0.8 fusion.2
  40.3 1.3 %collective-permute-start.6 = (f32[4,128,128]{2,1,0:T(8,128)}, f32[4,128,128]{2,1,0:T(8,128)}, u32[]{:S(2)}, u32[]{:S(2)}) collective-permute-start(f32[4,128,128]{2,1,0:T(8,128)} %get-tuple-element.13), channel_id=1, source_target_pairs={{8,12},{10,14},{9,13},{11,15},{24,28},{26,30},{25,29},{27,31}} | collective-permute-start | bytes 786440 | tf_op jit(solution)/shard_map/ppermute | solution.py:33
  41.6 0.8 collective-permute-start.7
  42.4 0.0 collective-permute-done.11
  42.4 1.1 add.117
  43.5 0.7 collective-permute-start.12
  44.1 0.0 collective-permute-done.2
  44.1 1.2 %fusion.3 = (f32[4,128,128]{2,1,0:T(8,128)S(1)}, f32[4,128,128]{2,1,0:T(8,128)S(1)}) fusion(f32[4,128,128]{2,1,0:T(8,128)} %copy-done.2, f32[4,128,128]{2,1,0:T(8,128)} %copy-done.3, f32[4,128,128]{2,1,0:T(8,128)} %collective-permute-done.2), kind=kLoop, calls=%fused_computation.24 | loop fusion | flops 131072 | bytes 1310720 | tf_op jit(solution)/shard_map/add | solution.py:30
  45.3 1.3 %collective-permute-start.3 = (f32[4,128,128]{2,1,0:T(8,128)S(1)}, f32[4,128,128]{2,1,0:T(8,128)S(1)}, u32[]{:S(2)}, u32[]{:S(2)}) collective-permute-start(f32[4,128,128]{2,1,0:T(8,128)S(1)} %get-tuple-element.15), channel_id=1, source_target_pairs={{8,12},{10,14},{9,13},{11,15},{24,28},{26,30},{25,29},{27,31}} | collective-permute-start | bytes 786440 | tf_op jit(solution)/shard_map/ppermute | solution.py:33
  46.6 14.0 %collective-permute-done.6 = f32[4,128,128]{2,1,0:T(8,128)} collective-permute-done((f32[4,128,128]{2,1,0:T(8,128)}, f32[4,128,128]{2,1,0:T(8,128)}, u32[]{:S(2)}, u32[]{:S(2)}) %collective-permute-start.6) | collective-permute-done | bytes 262176 | tf_op jit(solution)/shard_map/ppermute | solution.py:33
  60.6 1.0 add_convert_fusion.3
  61.6 0.6 collective-permute-start.13
  62.2 0.0 collective-permute-done.12
  62.2 1.1 %fusion = (f32[4,128,128]{2,1,0:T(8,128)S(1)}, f32[4,128,128]{2,1,0:T(8,128)S(1)}) fusion(f32[4,128,128]{2,1,0:T(8,128)} %get-tuple-element.17, f32[4,128,128]{2,1,0:T(8,128)} %collective-permute-done.11, f32[4,128,128]{2,1,0:T(8,128)S(1)} %collective-permute-done.12), kind=kLoop, calls=%fused_computation.21 | loop fusion | flops 131072 | bytes 1310720 | tf_op jit(solution)/shard_map/add | solution.py:30
  63.3 0.0 copy-start.4
  63.3 3.3 %collective-permute-done.13 = bf16[4,128,128]{2,1,0:T(8,128)(2,1)S(1)} collective-permute-done((bf16[4,128,128]{2,1,0:T(8,128)(2,1)S(1)}, bf16[4,128,128]{2,1,0:T(8,128)(2,1)S(1)}, u32[]{:S(2)}, u32[]{:S(2)}) %collective-permute-start.13) | collective-permute-done | bytes 131104 | tf_op jit(solution)/shard_map/ppermute | solution.py:36
  66.6 1.3 %collective-permute-start.14 = (f32[4,128,128]{2,1,0:T(8,128)S(1)}, f32[4,128,128]{2,1,0:T(8,128)S(1)}, u32[]{:S(2)}, u32[]{:S(2)}) collective-permute-start(f32[4,128,128]{2,1,0:T(8,128)S(1)} %get-tuple-element.8), channel_id=1, source_target_pairs={{8,12},{10,14},{9,13},{11,15},{24,28},{26,30},{25,29},{27,31}} | collective-permute-start | bytes 786440 | tf_op jit(solution)/shard_map/ppermute | solution.py:33
  67.9 0.0 collective-permute-done.7
  68.0 0.7 collective-permute-start.8
  68.6 0.0 collective-permute-done.3
  68.6 6.2 %collective-permute-done.14 = f32[4,128,128]{2,1,0:T(8,128)S(1)} collective-permute-done((f32[4,128,128]{2,1,0:T(8,128)S(1)}, f32[4,128,128]{2,1,0:T(8,128)S(1)}, u32[]{:S(2)}, u32[]{:S(2)}) %collective-permute-start.14) | collective-permute-done | bytes 262176 | tf_op jit(solution)/shard_map/ppermute | solution.py:33
  74.9 0.1 add_convert_fusion
  75.0 0.6 collective-permute-start.9
  75.6 4.4 %collective-permute-done.9 = bf16[4,128,128]{2,1,0:T(8,128)(2,1)S(1)} collective-permute-done((bf16[4,128,128]{2,1,0:T(8,128)(2,1)S(1)}, bf16[4,128,128]{2,1,0:T(8,128)(2,1)S(1)}, u32[]{:S(2)}, u32[]{:S(2)}) %collective-permute-start.9) | collective-permute-done | bytes 131104 | tf_op jit(solution)/shard_map/ppermute | solution.py:36
  80.0 1.3 %collective-permute-start.10 = (f32[4,128,128]{2,1,0:T(8,128)S(1)}, f32[4,128,128]{2,1,0:T(8,128)S(1)}, u32[]{:S(2)}, u32[]{:S(2)}) collective-permute-start(f32[4,128,128]{2,1,0:T(8,128)S(1)} %get-tuple-element.7), channel_id=1, source_target_pairs={{8,12},{10,14},{9,13},{11,15},{24,28},{26,30},{25,29},{27,31}} | collective-permute-start | bytes 786440 | tf_op jit(solution)/shard_map/ppermute | solution.py:33
  81.3 1.9 %all_gather.3 = f32[4096]{0:T(1024)} all-gather(f32[2048]{0:T(1024)S(1)} %copy-done.4), channel_id=1, replica_groups=mesh['groups'=2,'ctx'=8,'dp'=2] {'dp'}, dimensions={0}, use_global_device_ids=true | all-gather | bytes 24576 | tf_op jit(solution)/shard_map/all_gather | solution.py:122
  83.3 0.6 collective-permute-start.16
  83.8 4.4 %collective-permute-done.10 = f32[4,128,128]{2,1,0:T(8,128)S(1)} collective-permute-done((f32[4,128,128]{2,1,0:T(8,128)S(1)}, f32[4,128,128]{2,1,0:T(8,128)S(1)}, u32[]{:S(2)}, u32[]{:S(2)}) %collective-permute-start.10) | collective-permute-done | bytes 262176 | tf_op jit(solution)/shard_map/ppermute | solution.py:33
  88.3 1.2 %add_convert_fusion.7 = (bf16[4,128,128]{2,1,0:T(8,128)(2,1)S(1)}, bf16[4,128,128]{2,1,0:T(8,128)(2,1)S(1)}, bf16[4,128,128]{2,1,0:T(8,128)(2,1)S(1)}, bf16[4,12...) fusion(f32[16,128,128]{2,1,0:T(8,128)S(1)} %collective-permute-done, pred[]{:T(512)S(6)} %eq.5, ...), kind=kLoop, calls=%fused_computation.11 | loop fusion | flops 1245184 | bytes 4063237 | tf_op jit(solution)/shard_map/convert_element_type | solution.py:34
  89.5 0.6 collective-permute-start.15
  90.1 4.4 %collective-permute-done.15 = bf16[4,128,128]{2,1,0:T(8,128)(2,1)S(1)} collective-permute-done((bf16[4,128,128]{2,1,0:T(8,128)(2,1)S(1)}, bf16[4,128,128]{2,1,0:T(8,128)(2,1)S(1)}, u32[]{:S(2)}, u32[]{:S(2)}) %collective-permute-start.15) | collective-permute-done | bytes 131104 | tf_op jit(solution)/shard_map/ppermute | solution.py:36
  94.6 0.1 broadcast_select_fusion.1
  94.7 1.1 %pad_maximum_fusion.prefix_ref = bf16[32,128,128]{2,1,0:T(8,128)(2,1)} fusion(bf16[16,128,128]{2,1,0:T(8,128)(2,1)S(1)} %get-tuple-element.24, bf16[16,128,128]{2,1,0:T(8,128)(2,1)S(1)} %get-tuple-element.23), kind=kLoop, calls=%fused_computation | loop fusion | flops 524288 | bytes 2097152 | tf_op jit(solution)/shard_map/concatenate | solution.py:41
  95.8 12.4 %shard_map.47 = bf16[384,4096]{1,0:T(8,128)(2,1)} custom-call(bf16[384,4096]{1,0:T(8,128)(2,1)} %bitcast.9, bf16[384,4096]{1,0:T(8,128)(2,1)} %bitcast.6, bf16[384,4096]{1,0:T(8,128)(2,1)} %bitcast.8, bf16[32,128,128]{2,1,0:T(8,128)(2,1)} %pad_maximum_fusion.prefix_ref, f32[1,4096]{1,0:T(1,128)} %bitcast.10), custom_call_target="tpu_custom_call" | custom-call | tf_op jit(solution)/shard_map/pallas_call | solution.py:105
  (18 shorter events, 0.2 us)
Async XLA Ops:
  5.4 27.6 %copy-start = (f32[32,128,128]{2,1,0:T(8,128)S(1)}, f32[32,128,128]{2,1,0:T(8,128)}, u32[]{:S(2)}) copy-start(f32[32,128,128]{2,1,0:T(8,128)} %shard_map.46) | copy-start | bytes 6291460
  7.8 25.1 %collective-permute-start = (f32[16,128,128]{2,1,0:T(8,128)}, f32[16,128,128]{2,1,0:T(8,128)S(1)}, u32[]{:S(2)}, u32[]{:S(2)}) collective-permute-start(f32[16,128,128]{2,1,0:T(8,128)} %constant_dynamic-slice_fusion), channel_id=1, source_target_pairs={{0,2},{4,6},{8,10},{12,14},{2,0},{6,4},{10,8},{14,12},{1,3},{5,7},... | collective-permute-start | bytes 3145736 | tf_op jit(solution)/shard_map/ppermute | solution.py:20
  33.8 5.6 %copy-start.2 = (f32[4,128,128]{2,1,0:T(8,128)}, f32[4,128,128]{2,1,0:T(8,128)S(1)}, u32[]{:S(2)}) copy-start(f32[4,128,128]{2,1,0:T(8,128)S(1)} %get-tuple-element.20) | copy-start | bytes 786436
  33.8 1.4 %collective-permute-start.4 = (f32[4,128,128]{2,1,0:T(8,128)S(1)}, f32[4,128,128]{2,1,0:T(8,128)S(1)}, u32[]{:S(2)}, u32[]{:S(2)}) collective-permute-start(f32[4,128,128]{2,1,0:T(8,128)S(1)} %get-tuple-element.19), channel_id=1, source_target_pairs={{0,4},{2,6},{1,5},{3,7},{16,20},{18,22},{17,21},{19,23}} | collective-permute-start | bytes 786440 | tf_op jit(solution)/shard_map/ppermute | solution.py:33
  34.5 2.8 %collective-permute-start.1 = (f32[4,128,128]{2,1,0:T(8,128)S(1)}, f32[4,128,128]{2,1,0:T(8,128)S(1)}, u32[]{:S(2)}, u32[]{:S(2)}) collective-permute-start(f32[4,128,128]{2,1,0:T(8,128)S(1)} %get-tuple-element.20), channel_id=1, source_target_pairs={{0,4},{2,6},{1,5},{3,7},{16,20},{18,22},{17,21},{19,23}} | collective-permute-start | bytes 786440 | tf_op jit(solution)/shard_map/ppermute | solution.py:33
  35.3 4.2 %collective-permute-start.5 = (f32[4,128,128]{2,1,0:T(8,128)S(1)}, f32[4,128,128]{2,1,0:T(8,128)S(1)}, u32[]{:S(2)}, u32[]{:S(2)}) collective-permute-start(f32[4,128,128]{2,1,0:T(8,128)S(1)} %add.104), channel_id=1, source_target_pairs={{4,8},{6,10},{5,9},{7,11},{20,24},{22,26},{21,25},{23,27}} | collective-permute-start | bytes 786440 | tf_op jit(solution)/shard_map/ppermute | solution.py:33
  35.9 6.4 %collective-permute-start.11 = (f32[4,128,128]{2,1,0:T(8,128)}, f32[4,128,128]{2,1,0:T(8,128)}, u32[]{:S(2)}, u32[]{:S(2)}) collective-permute-start(f32[4,128,128]{2,1,0:T(8,128)} %get-tuple-element.17), channel_id=1, source_target_pairs={{0,4},{2,6},{1,5},{3,7},{16,20},{18,22},{17,21},{19,23}} | collective-permute-start | bytes 786440 | tf_op jit(solution)/shard_map/ppermute | solution.py:33
  37.3 2.2 %copy-start.3 = (f32[4,128,128]{2,1,0:T(8,128)}, f32[4,128,128]{2,1,0:T(8,128)S(1)}, u32[]{:S(2)}) copy-start(f32[4,128,128]{2,1,0:T(8,128)S(1)} %collective-permute-done.1) | copy-start | bytes 786436
  38.1 6.0 %collective-permute-start.2 = (f32[4,128,128]{2,1,0:T(8,128)}, f32[4,128,128]{2,1,0:T(8,128)}, u32[]{:S(2)}, u32[]{:S(2)}) collective-permute-start(f32[4,128,128]{2,1,0:T(8,128)} %add.98), channel_id=1, source_target_pairs={{4,8},{6,10},{5,9},{7,11},{20,24},{22,26},{21,25},{23,27}} | collective-permute-start | bytes 786440 | tf_op jit(solution)/shard_map/ppermute | solution.py:33
  40.3 20.3 %collective-permute-start.6 = (f32[4,128,128]{2,1,0:T(8,128)}, f32[4,128,128]{2,1,0:T(8,128)}, u32[]{:S(2)}, u32[]{:S(2)}) collective-permute-start(f32[4,128,128]{2,1,0:T(8,128)} %get-tuple-element.13), channel_id=1, source_target_pairs={{8,12},{10,14},{9,13},{11,15},{24,28},{26,30},{25,29},{27,31}} | collective-permute-start | bytes 786440 | tf_op jit(solution)/shard_map/ppermute | solution.py:33
  41.6 26.4 %copy-start.1 = (f32[4,128,128]{2,1,0:T(8,128)S(1)}, f32[4,128,128]{2,1,0:T(8,128)}, u32[]{:S(2)}) copy-start(f32[4,128,128]{2,1,0:T(8,128)} %get-tuple-element.18) | copy-start | bytes 786436
  41.6 26.3 %collective-permute-start.7 = (f32[4,128,128]{2,1,0:T(8,128)}, f32[4,128,128]{2,1,0:T(8,128)S(1)}, u32[]{:S(2)}, u32[]{:S(2)}) collective-permute-start(f32[4,128,128]{2,1,0:T(8,128)} %get-tuple-element.18), channel_id=1, source_target_pairs={{0,4},{2,6},{1,5},{3,7},{16,20},{18,22},{17,21},{19,23}} | collective-permute-start | bytes 786440 | tf_op jit(solution)/shard_map/ppermute | solution.py:33
  43.5 18.7 %collective-permute-start.12 = (f32[4,128,128]{2,1,0:T(8,128)S(1)}, f32[4,128,128]{2,1,0:T(8,128)S(1)}, u32[]{:S(2)}, u32[]{:S(2)}) collective-permute-start(f32[4,128,128]{2,1,0:T(8,128)S(1)} %add.117), channel_id=1, source_target_pairs={{4,8},{6,10},{5,9},{7,11},{20,24},{22,26},{21,25},{23,27}} | collective-permute-start | bytes 786440 | tf_op jit(solution)/shard_map/ppermute | solution.py:33
  45.3 23.3 %collective-permute-start.3 = (f32[4,128,128]{2,1,0:T(8,128)S(1)}, f32[4,128,128]{2,1,0:T(8,128)S(1)}, u32[]{:S(2)}, u32[]{:S(2)}) collective-permute-start(f32[4,128,128]{2,1,0:T(8,128)S(1)} %get-tuple-element.15), channel_id=1, source_target_pairs={{8,12},{10,14},{9,13},{11,15},{24,28},{26,30},{25,29},{27,31}} | collective-permute-start | bytes 786440 | tf_op jit(solution)/shard_map/ppermute | solution.py:33
  61.6 5.0 %collective-permute-start.13 = (bf16[4,128,128]{2,1,0:T(8,128)(2,1)S(1)}, bf16[4,128,128]{2,1,0:T(8,128)(2,1)S(1)}, u32[]{:S(2)}, u32[]{:S(2)}) collective-permute-start(bf16[4,128,128]{2,1,0:T(8,128)(2,1)S(1)} %add_convert_fusion.3), channel_id=1, source_target_pairs={{0,2},{4,6},{8,10},{12,14},{2,0},{6,4},{10,8},{14,12},{1,3},{5,7},... | collective-permute-start | bytes 393224 | tf_op jit(solution)/shard_map/ppermute | solution.py:36
  63.3 18.0 %copy-start.4 = (f32[2048]{0:T(1024)S(1)}, f32[2048]{0:T(1024)}, u32[]{:S(2)}) copy-start(f32[2048]{0:T(1024)} %param.7) | copy-start | bytes 24580
  66.6 8.3 %collective-permute-start.14 = (f32[4,128,128]{2,1,0:T(8,128)S(1)}, f32[4,128,128]{2,1,0:T(8,128)S(1)}, u32[]{:S(2)}, u32[]{:S(2)}) collective-permute-start(f32[4,128,128]{2,1,0:T(8,128)S(1)} %get-tuple-element.8), channel_id=1, source_target_pairs={{8,12},{10,14},{9,13},{11,15},{24,28},{26,30},{25,29},{27,31}} | collective-permute-start | bytes 786440 | tf_op jit(solution)/shard_map/ppermute | solution.py:33
  68.0 7.6 %collective-permute-start.8 = (f32[4,128,128]{2,1,0:T(8,128)S(1)}, f32[4,128,128]{2,1,0:T(8,128)S(1)}, u32[]{:S(2)}, u32[]{:S(2)}) collective-permute-start(f32[4,128,128]{2,1,0:T(8,128)S(1)} %add.110), channel_id=1, source_target_pairs={{4,8},{6,10},{5,9},{7,11},{20,24},{22,26},{21,25},{23,27}} | collective-permute-start | bytes 786440 | tf_op jit(solution)/shard_map/ppermute | solution.py:33
  75.0 5.0 %collective-permute-start.9 = (bf16[4,128,128]{2,1,0:T(8,128)(2,1)S(1)}, bf16[4,128,128]{2,1,0:T(8,128)(2,1)S(1)}, u32[]{:S(2)}, u32[]{:S(2)}) collective-permute-start(bf16[4,128,128]{2,1,0:T(8,128)(2,1)S(1)} %get-tuple-element.22), channel_id=1, source_target_pairs={{0,2},{4,6},{8,10},{12,14},{2,0},{6,4},{10,8},{14,12},{1,3},{5,7},... | collective-permute-start | bytes 393224 | tf_op jit(solution)/shard_map/ppermute | solution.py:36
  80.0 8.3 %collective-permute-start.10 = (f32[4,128,128]{2,1,0:T(8,128)S(1)}, f32[4,128,128]{2,1,0:T(8,128)S(1)}, u32[]{:S(2)}, u32[]{:S(2)}) collective-permute-start(f32[4,128,128]{2,1,0:T(8,128)S(1)} %get-tuple-element.7), channel_id=1, source_target_pairs={{8,12},{10,14},{9,13},{11,15},{24,28},{26,30},{25,29},{27,31}} | collective-permute-start | bytes 786440 | tf_op jit(solution)/shard_map/ppermute | solution.py:33
  83.3 11.3 %collective-permute-start.16 = (bf16[4,128,128]{2,1,0:T(8,128)(2,1)S(1)}, bf16[4,128,128]{2,1,0:T(8,128)(2,1)S(1)}, u32[]{:S(2)}, u32[]{:S(2)}) collective-permute-start(bf16[4,128,128]{2,1,0:T(8,128)(2,1)S(1)} %get-tuple-element.21), channel_id=1, source_target_pairs={{0,2},{4,6},{8,10},{12,14},{2,0},{6,4},{10,8},{14,12},{1,3},{5,7},... | collective-permute-start | bytes 393224 | tf_op jit(solution)/shard_map/ppermute | solution.py:36
  89.5 5.0 %collective-permute-start.15 = (bf16[4,128,128]{2,1,0:T(8,128)(2,1)S(1)}, bf16[4,128,128]{2,1,0:T(8,128)(2,1)S(1)}, u32[]{:S(2)}, u32[]{:S(2)}) collective-permute-start(bf16[4,128,128]{2,1,0:T(8,128)(2,1)S(1)} %get-tuple-element.29), channel_id=1, source_target_pairs={{0,2},{4,6},{8,10},{12,14},{2,0},{6,4},{10,8},{14,12},{1,3},{5,7},... | collective-permute-start | bytes 393224 | tf_op jit(solution)/shard_map/ppermute | solution.py:36

commit v7 on v3

--- a/solution.py
+++ b/solution.py
@@ -8,14 +8,12 @@
 H = 32
 
 
-def pair_chain_prefix(terms, axis, pieces):
+def pair_chain_prefix(mine_all, other_all, axis, pieces):
     count = lax.axis_size(axis)
     mine_at = lax.axis_index(axis) % 2
     first = mine_at == 0
-    half = terms.shape[0] // 2
+    half = mine_all.shape[0]
     pairs = count // 2
-    mine_all = lax.dynamic_slice_in_dim(terms, mine_at * half, half, 0)
-    other_all = lax.dynamic_slice_in_dim(terms, (1 - mine_at) * half, half, 0)
     swap = [(2 * i, 2 * i + 1) for i in range(pairs)] + [(2 * i + 1, 2 * i) for i in range(pairs)]
     step = half // pieces
     keeps, backs = [], []
@@ -37,7 +35,7 @@
     return jnp.concatenate([low, high], axis=0)
 
 
-def state_kernel(key_ref, val_ref, out_ref):
+def state_kernel(at_ref, key_ref, val_ref, out_ref):
     heads, head_size, _ = out_ref.shape
     for head in range(heads):
         cols = slice(head * head_size, (head + 1) * head_size)
@@ -46,18 +44,20 @@
             preferred_element_type=jnp.float32)
 
 
-def state_terms_of(keyset, valset, group):
+def state_terms_of(keyset, valset, half_at):
     row_count, feat_count = keyset.shape
     head_size = feat_count // H
-    width = group * head_size
+    width = feat_count // 2
+    spec = pl.BlockSpec((row_count, width), lambda g, at: (0, at[0] + g))
     return pl.pallas_call(
         state_kernel,
-        grid=(H // group,),
-        in_specs=[pl.BlockSpec((row_count, width), lambda g: (0, g)),
-                  pl.BlockSpec((row_count, width), lambda g: (0, g))],
-        out_specs=pl.BlockSpec((group, head_size, head_size), lambda g: (g, 0, 0)),
-        out_shape=jax.ShapeDtypeStruct((H, head_size, head_size), jnp.float32),
-    )(keyset, valset)
+        grid_spec=pltpu.PrefetchScalarGridSpec(
+            num_scalar_prefetch=1,
+            grid=(1,),
+            in_specs=[spec, spec],
+            out_specs=pl.BlockSpec((H // 2, head_size, head_size), lambda g, at: (0, 0, 0))),
+        out_shape=jax.ShapeDtypeStruct((H // 2, head_size, head_size), jnp.float32),
+    )(jnp.reshape(half_at, (1,)).astype(jnp.int32), keyset, valset)
 
 
 def attend_kernel(query_ref, key_ref, val_ref, prefix_ref, gain_ref, out_ref, acc_ref, sumsq_ref):
@@ -119,8 +119,10 @@
     query = query_rows.reshape(seq_count * row_count, feat_count)
     keyset = key_rows.reshape(seq_count * row_count, feat_count)
     valset = value_rows.reshape(seq_count * row_count, feat_count)
-    state_terms = state_terms_of(keyset, valset, 8)
-    prefix_bf = pair_chain_prefix(state_terms, "ctx", 4)
+    mine_at = lax.axis_index("ctx") % 2
+    other_terms = state_terms_of(keyset, valset, 1 - mine_at)
+    mine_terms = state_terms_of(keyset, valset, mine_at)
+    prefix_bf = pair_chain_prefix(mine_terms, other_terms, "ctx", 4)
     normed = attend_of(query, keyset, valset, prefix_bf, full_gain, 8)
     return normed.reshape(seq_count, row_count, feat_count)
 

time: 100 us -> 103 us (1.030)
  other arithmetic: 8.73 us -> 6.62 us
  Pallas kernels: 17.6 us -> 19.3 us
  waiting for transfers between devices: 52.1 us -> 53.7 us
  starting transfers between devices: 17.8 us -> 19.1 us
    ppermute x12, waiting for transfers between devices: 22.9 us -> 30.1 us  [pair_chain_prefix(): carried = carried + lax.ppermute(carried + total, axis, links)]
    ppermute x4, waiting for transfers between devices: 22.9 us -> 17.4 us  [pair_chain_prefix(): got = lax.ppermute(other_all[piece * step:(piece + 1) * step], axis, swap)]
    pallas_call x1 -> x2, Pallas kernels: 5.36 us -> 6.97 us  [state_terms_of(): pl.pallas_call(state_kernel, grid_spec=pltpu.PrefetchScalarGridSpec(num_s...]
    add x2 -> x1, other arithmetic: 2.27 us -> 1.3 us  [pair_chain_prefix(): total = mine + got]
  transfers between devices with their start and end apart: 20 -> 20, of which waited for: 11 -> 11; matrix products, arithmetic and copies ran while one was open for 4% -> 3% of each run, Pallas kernels for 0% -> 3%
where the time goes in v7:
time: 103 us; the launch traced here: 102 us
  waiting for transfers between devices  53.7 us (52%)
  Pallas kernels  19.3 us (19%)
  starting transfers between devices  19.1 us (19%)
  other arithmetic  6.62 us (6%)
  blocking collectives  1.93 us (2%)
  local copies, waits for them, and re-layouts  1.33 us (1%)
    ppermute x12, waiting for transfers between devices, pair_chain_prefix(): carried = carried + lax.ppermute(carried + total, axis, links)  30.1 us
    ppermute x4, waiting for transfers between devices, pair_chain_prefix(): got = lax.ppermute(other_all[piece * step:(piece + 1) * step], axis, swap)  17.4 us
    pallas_call x1, Pallas kernels, attend_of(): pl.pallas_call(attend_kernel, grid=(steps,), in_specs=[pl.BlockSpec((row_...  12.4 us
    ppermute x12, starting transfers between devices, pair_chain_prefix(): carried = carried + lax.ppermute(carried + total, axis, links)  10.8 us
    pallas_call x2, Pallas kernels, state_terms_of(): pl.pallas_call(state_kernel, grid_spec=pltpu.PrefetchScalarGridSpec(num_s...  6.97 us
    ppermute x4, waiting for transfers between devices, pair_chain_prefix(): backs.append(lax.ppermute(send, axis, swap))  6.27 us
    ppermute x4, starting transfers between devices, pair_chain_prefix(): backs.append(lax.ppermute(send, axis, swap))  4.16 us
    ppermute x4, starting transfers between devices, pair_chain_prefix(): got = lax.ppermute(other_all[piece * step:(piece + 1) * step], axis, swap)  4.12 us
  transfers between devices with their start and end apart: 20, of which 11 were waited for; matrix products, arithmetic and copies ran while one was open for 3% of the time, Pallas kernels for 3%

profile of v7, /device:TPU:30, one launch (start us, length us, event | category | flops | bytes accessed | tf_op | source)
XLA Modules:
  0.0 102.3 jit_solution(6413586207251255864)
XLA Ops:
  0.0 3.5 %shard_map.47 = f32[16,128,128]{2,1,0:T(8,128)} custom-call(s32[1]{0:T(128)} %bitcast.4.at_ref, bf16[384,4096]{1,0:T(8,128)(2,1)} %bitcast.7, bf16[384,4096]{1,0:T(8,128)(2,1)} %bitcast.10), custom_call_target="tpu_custom_call" | custom-call | tf_op jit(solution)/shard_map/pallas_call | solution.py:52
  3.5 1.3 %fusion.4 = (f32[4,128,128]{2,1,0:T(8,128)S(1)}, f32[4,128,128]{2,1,0:T(8,128)S(1)}, f32[4,128,128]{2,1,0:T(8,128)S(1)}, f32[4,128,128]{2,1,0:T(8,128)S(1)}) fusion(f32[16,128,128]{2,1,0:T(8,128)} %shard_map.47), kind=kLoop, calls=%fused_computation.24 | loop fusion | bytes 2097152 | tf_op jit(solution)/shard_map/slice | solution.py:22
  4.7 0.6 collective-permute-start
  5.3 1.5 %collective-permute-start.12 = (f32[4,128,128]{2,1,0:T(8,128)S(1)}, f32[4,128,128]{2,1,0:T(8,128)S(1)}, u32[]{:S(2)}, u32[]{:S(2)}) collective-permute-start(f32[4,128,128]{2,1,0:T(8,128)S(1)} %get-tuple-element.23), channel_id=1, source_target_pairs={{0,2},{4,6},{8,10},{12,14},{2,0},{6,4},{10,8},{14,12},{1,3},{5,7},... | collective-permute-start | bytes 786440 | tf_op jit(solution)/shard_map/ppermute | solution.py:22
  6.8 0.5 collective-permute-start.4
  7.3 1.5 %collective-permute-start.8 = (f32[4,128,128]{2,1,0:T(8,128)S(1)}, f32[4,128,128]{2,1,0:T(8,128)S(1)}, u32[]{:S(2)}, u32[]{:S(2)}) collective-permute-start(f32[4,128,128]{2,1,0:T(8,128)S(1)} %get-tuple-element.24), channel_id=1, source_target_pairs={{0,2},{4,6},{8,10},{12,14},{2,0},{6,4},{10,8},{14,12},{1,3},{5,7},... | collective-permute-start | bytes 786440 | tf_op jit(solution)/shard_map/ppermute | solution.py:22
  8.9 3.5 %shard_map.46 = f32[16,128,128]{2,1,0:T(8,128)} custom-call(s32[1]{0:T(128)} %bitcast.3.at_ref, bf16[384,4096]{1,0:T(8,128)(2,1)} %bitcast.8, bf16[384,4096]{1,0:T(8,128)(2,1)} %bitcast.11), custom_call_target="tpu_custom_call" | custom-call | tf_op jit(solution)/shard_map/pallas_call | solution.py:52
  12.4 1.7 %collective-permute-done = f32[4,128,128]{2,1,0:T(8,128)S(1)} collective-permute-done((f32[4,128,128]{2,1,0:T(8,128)S(1)}, f32[4,128,128]{2,1,0:T(8,128)S(1)}, u32[]{:S(2)}, u32[]{:S(2)}) %collective-permute-start) | collective-permute-done | bytes 262176 | tf_op jit(solution)/shard_map/ppermute | solution.py:22
  14.0 5.6 %collective-permute-done.12 = f32[4,128,128]{2,1,0:T(8,128)S(1)} collective-permute-done((f32[4,128,128]{2,1,0:T(8,128)S(1)}, f32[4,128,128]{2,1,0:T(8,128)S(1)}, u32[]{:S(2)}, u32[]{:S(2)}) %collective-permute-start.12) | collective-permute-done | bytes 262176 | tf_op jit(solution)/shard_map/ppermute | solution.py:22
  19.6 5.6 %collective-permute-done.4 = f32[4,128,128]{2,1,0:T(8,128)S(1)} collective-permute-done((f32[4,128,128]{2,1,0:T(8,128)S(1)}, f32[4,128,128]{2,1,0:T(8,128)S(1)}, u32[]{:S(2)}, u32[]{:S(2)}) %collective-permute-start.4) | collective-permute-done | bytes 262176 | tf_op jit(solution)/shard_map/ppermute | solution.py:22
  25.2 4.5 %collective-permute-done.8 = f32[4,128,128]{2,1,0:T(8,128)S(1)} collective-permute-done((f32[4,128,128]{2,1,0:T(8,128)S(1)}, f32[4,128,128]{2,1,0:T(8,128)S(1)}, u32[]{:S(2)}, u32[]{:S(2)}) %collective-permute-start.8) | collective-permute-done | bytes 262176 | tf_op jit(solution)/shard_map/ppermute | solution.py:22
  29.7 1.3 %slice_add_fusion = (f32[4,128,128]{2,1,0:T(8,128)S(1)}, f32[4,128,128]{2,1,0:T(8,128)S(1)}, f32[4,128,128]{2,1,0:T(8,128)S(1)}, f32[4,128,128]{2,1,0:T(8,128)S(1)}) fusion(f32[4,128,128]{2,1,0:T(8,128)S(1)} %collective-permute-done.12, f32[16,128,128]{2,1,0:T(8,128)} %shard_map.46, f32[4,128,128]{2,1,0:T(8,128)S(1)} %collective-permute-done.8, ...), kind=kLoop, calls=%fused_computation.12 | loop fusion | flops 262144 | bytes 3145728 | tf_op jit(solution)/shard_map/add | solution.py:23
  31.0 0.7 collective-permute-start.9
  31.7 0.7 collective-permute-start.5
  32.4 0.7 collective-permute-start.1
  33.1 0.7 collective-permute-start.13
  33.8 0.7 collective-permute-start.10
  34.5 0.0 collective-permute-done.5
  34.5 0.7 collective-permute-start.6
  35.2 0.0 collective-permute-done.1
  35.3 0.0 copy-start
  35.3 0.8 collective-permute-start.2
  36.1 0.0 collective-permute-done.13
  36.2 0.7 collective-permute-start.14
  36.9 0.1 fusion.1
  36.9 1.3 %collective-permute-start.11 = (f32[4,128,128]{2,1,0:T(8,128)S(1)}, f32[4,128,128]{2,1,0:T(8,128)}, u32[]{:S(2)}, u32[]{:S(2)}) collective-permute-start(f32[4,128,128]{2,1,0:T(8,128)S(1)} %get-tuple-element.7), channel_id=1, source_target_pairs={{8,12},{10,14},{9,13},{11,15},{24,28},{26,30},{25,29},{27,31}} | collective-permute-start | bytes 786440 | tf_op jit(solution)/shard_map/ppermute | solution.py:27
  38.2 0.8 fusion.2
  39.0 1.3 %collective-permute-start.7 = (f32[4,128,128]{2,1,0:T(8,128)}, f32[4,128,128]{2,1,0:T(8,128)}, u32[]{:S(2)}, u32[]{:S(2)}) collective-permute-start(f32[4,128,128]{2,1,0:T(8,128)} %get-tuple-element.9), channel_id=1, source_target_pairs={{8,12},{10,14},{9,13},{11,15},{24,28},{26,30},{25,29},{27,31}} | collective-permute-start | bytes 786440 | tf_op jit(solution)/shard_map/ppermute | solution.py:27
  40.3 0.8 fusion.3
  41.0 1.4 %collective-permute-start.3 = (f32[4,128,128]{2,1,0:T(8,128)}, f32[4,128,128]{2,1,0:T(8,128)}, u32[]{:S(2)}, u32[]{:S(2)}) collective-permute-start(f32[4,128,128]{2,1,0:T(8,128)} %get-tuple-element.11), channel_id=1, source_target_pairs={{8,12},{10,14},{9,13},{11,15},{24,28},{26,30},{25,29},{27,31}} | collective-permute-start | bytes 786440 | tf_op jit(solution)/shard_map/ppermute | solution.py:27
  42.5 0.8 fusion
  43.3 1.3 %collective-permute-start.15 = (f32[4,128,128]{2,1,0:T(8,128)}, f32[4,128,128]{2,1,0:T(8,128)}, u32[]{:S(2)}, u32[]{:S(2)}) collective-permute-start(f32[4,128,128]{2,1,0:T(8,128)} %get-tuple-element.5), channel_id=1, source_target_pairs={{8,12},{10,14},{9,13},{11,15},{24,28},{26,30},{25,29},{27,31}} | collective-permute-start | bytes 786440 | tf_op jit(solution)/shard_map/ppermute | solution.py:27
  44.6 13.8 %collective-permute-done.11 = f32[4,128,128]{2,1,0:T(8,128)} collective-permute-done((f32[4,128,128]{2,1,0:T(8,128)S(1)}, f32[4,128,128]{2,1,0:T(8,128)}, u32[]{:S(2)}, u32[]{:S(2)}) %collective-permute-start.11) | collective-permute-done | bytes 262176 | tf_op jit(solution)/shard_map/ppermute | solution.py:27
  58.4 6.9 %collective-permute-done.7 = f32[4,128,128]{2,1,0:T(8,128)} collective-permute-done((f32[4,128,128]{2,1,0:T(8,128)}, f32[4,128,128]{2,1,0:T(8,128)}, u32[]{:S(2)}, u32[]{:S(2)}) %collective-permute-start.7) | collective-permute-done | bytes 262176 | tf_op jit(solution)/shard_map/ppermute | solution.py:27
  65.3 5.9 %collective-permute-done.3 = f32[4,128,128]{2,1,0:T(8,128)} collective-permute-done((f32[4,128,128]{2,1,0:T(8,128)}, f32[4,128,128]{2,1,0:T(8,128)}, u32[]{:S(2)}, u32[]{:S(2)}) %collective-permute-start.3) | collective-permute-done | bytes 262176 | tf_op jit(solution)/shard_map/ppermute | solution.py:27
  71.2 3.5 %collective-permute-done.15 = f32[4,128,128]{2,1,0:T(8,128)} collective-permute-done((f32[4,128,128]{2,1,0:T(8,128)}, f32[4,128,128]{2,1,0:T(8,128)}, u32[]{:S(2)}, u32[]{:S(2)}) %collective-permute-start.15) | collective-permute-done | bytes 262176 | tf_op jit(solution)/shard_map/ppermute | solution.py:27
  74.7 1.6 %add_convert_fusion = (bf16[4,128,128]{2,1,0:T(8,128)(2,1)S(1)}, bf16[4,128,128]{2,1,0:T(8,128)(2,1)S(1)}, bf16[4,128,128]{2,1,0:T(8,128)(2,1)S(1)}, bf16[4,128,...) fusion(f32[16,128,128]{2,1,0:T(8,128)S(1)} %copy-done, ...), kind=kLoop, calls=%fused_computation.4 | loop fusion | flops 1835008 | bytes 5242881 | tf_op jit(solution)/shard_map/convert_element_type | solution.py:29
  76.2 0.6 collective-permute-start.16
  76.8 1.5 %collective-permute-start.17 = (bf16[4,128,128]{2,1,0:T(8,128)(2,1)S(1)}, bf16[4,128,128]{2,1,0:T(8,128)(2,1)S(1)}, u32[]{:S(2)}, u32[]{:S(2)}) collective-permute-start(bf16[4,128,128]{2,1,0:T(8,128)(2,1)S(1)} %get-tuple-element.17), channel_id=1, source_target_pairs={{0,2},{4,6},{8,10},{12,14},{2,0},{6,4},{10,8},{14,12},{1,3},{5,7},... | collective-permute-start | bytes 393224 | tf_op jit(solution)/shard_map/ppermute | solution.py:30
  78.3 1.9 %all_gather.3 = f32[4096]{0:T(1024)} all-gather(f32[2048]{0:T(1024)S(1)} %copy-done.1), channel_id=1, replica_groups=mesh['groups'=2,'ctx'=8,'dp'=2] {'dp'}, dimensions={0}, use_global_device_ids=true | all-gather | bytes 24576 | tf_op jit(solution)/shard_map/all_gather | solution.py:118
  80.3 0.5 collective-permute-start.18
  80.8 1.5 %collective-permute-start.19 = (bf16[4,128,128]{2,1,0:T(8,128)(2,1)S(1)}, bf16[4,128,128]{2,1,0:T(8,128)(2,1)S(1)}, u32[]{:S(2)}, u32[]{:S(2)}) collective-permute-start(bf16[4,128,128]{2,1,0:T(8,128)(2,1)S(1)} %get-tuple-element.15), channel_id=1, source_target_pairs={{0,2},{4,6},{8,10},{12,14},{2,0},{6,4},{10,8},{14,12},{1,3},{5,7},... | collective-permute-start | bytes 393224 | tf_op jit(solution)/shard_map/ppermute | solution.py:30
  82.4 0.3 collective-permute-done.17
  82.7 4.0 %collective-permute-done.18 = bf16[4,128,128]{2,1,0:T(8,128)(2,1)S(1)} collective-permute-done((bf16[4,128,128]{2,1,0:T(8,128)(2,1)S(1)}, bf16[4,128,128]{2,1,0:T(8,128)(2,1)S(1)}, u32[]{:S(2)}, u32[]{:S(2)}) %collective-permute-start.18) | collective-permute-done | bytes 131104 | tf_op jit(solution)/shard_map/ppermute | solution.py:30
  86.7 2.0 %collective-permute-done.19 = bf16[4,128,128]{2,1,0:T(8,128)(2,1)S(1)} collective-permute-done((bf16[4,128,128]{2,1,0:T(8,128)(2,1)S(1)}, bf16[4,128,128]{2,1,0:T(8,128)(2,1)S(1)}, u32[]{:S(2)}, u32[]{:S(2)}) %collective-permute-start.19) | collective-permute-done | bytes 131104 | tf_op jit(solution)/shard_map/ppermute | solution.py:30
  88.7 0.1 broadcast_select_fusion.1
  88.8 1.1 %pad_maximum_fusion.prefix_ref = bf16[32,128,128]{2,1,0:T(8,128)(2,1)} fusion(bf16[16,128,128]{2,1,0:T(8,128)(2,1)S(1)} %get-tuple-element.14, bf16[16,128,128]{2,1,0:T(8,128)(2,1)S(1)} %get-tuple-element.13), kind=kLoop, calls=%fused_computation | loop fusion | flops 524288 | bytes 2097152 | tf_op jit(solution)/shard_map/concatenate | solution.py:35
  89.9 12.4 %shard_map.48 = bf16[384,4096]{1,0:T(8,128)(2,1)} custom-call(bf16[384,4096]{1,0:T(8,128)(2,1)} %bitcast.13, bf16[384,4096]{1,0:T(8,128)(2,1)} %bitcast.9, bf16[384,4096]{1,0:T(8,128)(2,1)} %bitcast.12, bf16[32,128,128]{2,1,0:T(8,128)(2,1)} %pad_maximum_fusion.prefix_ref, f32[1,4096]{1,0:T(1,128)} %bitcast.14), custom_call_target="tpu_custom_call" | custom-call | tf_op jit(solution)/shard_map/pallas_call | solution.py:101
  (17 shorter events, 0.3 us)
Async XLA Ops:
  4.7 9.3 %collective-permute-start = (f32[4,128,128]{2,1,0:T(8,128)S(1)}, f32[4,128,128]{2,1,0:T(8,128)S(1)}, u32[]{:S(2)}, u32[]{:S(2)}) collective-permute-start(f32[4,128,128]{2,1,0:T(8,128)S(1)} %get-tuple-element.26), channel_id=1, source_target_pairs={{0,2},{4,6},{8,10},{12,14},{2,0},{6,4},{10,8},{14,12},{1,3},{5,7},... | collective-permute-start | bytes 786440 | tf_op jit(solution)/shard_map/ppermute | solution.py:22
  5.3 14.3 %collective-permute-start.12 = (f32[4,128,128]{2,1,0:T(8,128)S(1)}, f32[4,128,128]{2,1,0:T(8,128)S(1)}, u32[]{:S(2)}, u32[]{:S(2)}) collective-permute-start(f32[4,128,128]{2,1,0:T(8,128)S(1)} %get-tuple-element.23), channel_id=1, source_target_pairs={{0,2},{4,6},{8,10},{12,14},{2,0},{6,4},{10,8},{14,12},{1,3},{5,7},... | collective-permute-start | bytes 786440 | tf_op jit(solution)/shard_map/ppermute | solution.py:22
  6.8 18.4 %collective-permute-start.4 = (f32[4,128,128]{2,1,0:T(8,128)S(1)}, f32[4,128,128]{2,1,0:T(8,128)S(1)}, u32[]{:S(2)}, u32[]{:S(2)}) collective-permute-start(f32[4,128,128]{2,1,0:T(8,128)S(1)} %get-tuple-element.25), channel_id=1, source_target_pairs={{0,2},{4,6},{8,10},{12,14},{2,0},{6,4},{10,8},{14,12},{1,3},{5,7},... | collective-permute-start | bytes 786440 | tf_op jit(solution)/shard_map/ppermute | solution.py:22
  7.3 22.4 %collective-permute-start.8 = (f32[4,128,128]{2,1,0:T(8,128)S(1)}, f32[4,128,128]{2,1,0:T(8,128)S(1)}, u32[]{:S(2)}, u32[]{:S(2)}) collective-permute-start(f32[4,128,128]{2,1,0:T(8,128)S(1)} %get-tuple-element.24), channel_id=1, source_target_pairs={{0,2},{4,6},{8,10},{12,14},{2,0},{6,4},{10,8},{14,12},{1,3},{5,7},... | collective-permute-start | bytes 786440 | tf_op jit(solution)/shard_map/ppermute | solution.py:22
  31.0 2.7 %collective-permute-start.9 = (f32[4,128,128]{2,1,0:T(8,128)S(1)}, f32[4,128,128]{2,1,0:T(8,128)S(1)}, u32[]{:S(2)}, u32[]{:S(2)}) collective-permute-start(f32[4,128,128]{2,1,0:T(8,128)S(1)} %get-tuple-element.20), channel_id=1, source_target_pairs={{0,4},{2,6},{1,5},{3,7},{16,20},{18,22},{17,21},{19,23}} | collective-permute-start | bytes 786440 | tf_op jit(solution)/shard_map/ppermute | solution.py:27
  31.7 2.8 %collective-permute-start.5 = (f32[4,128,128]{2,1,0:T(8,128)S(1)}, f32[4,128,128]{2,1,0:T(8,128)S(1)}, u32[]{:S(2)}, u32[]{:S(2)}) collective-permute-start(f32[4,128,128]{2,1,0:T(8,128)S(1)} %get-tuple-element.21), channel_id=1, source_target_pairs={{0,4},{2,6},{1,5},{3,7},{16,20},{18,22},{17,21},{19,23}} | collective-permute-start | bytes 786440 | tf_op jit(solution)/shard_map/ppermute | solution.py:27
  32.4 2.8 %collective-permute-start.1 = (f32[4,128,128]{2,1,0:T(8,128)S(1)}, f32[4,128,128]{2,1,0:T(8,128)S(1)}, u32[]{:S(2)}, u32[]{:S(2)}) collective-permute-start(f32[4,128,128]{2,1,0:T(8,128)S(1)} %get-tuple-element.22), channel_id=1, source_target_pairs={{0,4},{2,6},{1,5},{3,7},{16,20},{18,22},{17,21},{19,23}} | collective-permute-start | bytes 786440 | tf_op jit(solution)/shard_map/ppermute | solution.py:27
  33.1 3.0 %collective-permute-start.13 = (f32[4,128,128]{2,1,0:T(8,128)S(1)}, f32[4,128,128]{2,1,0:T(8,128)S(1)}, u32[]{:S(2)}, u32[]{:S(2)}) collective-permute-start(f32[4,128,128]{2,1,0:T(8,128)S(1)} %get-tuple-element.19), channel_id=1, source_target_pairs={{0,4},{2,6},{1,5},{3,7},{16,20},{18,22},{17,21},{19,23}} | collective-permute-start | bytes 786440 | tf_op jit(solution)/shard_map/ppermute | solution.py:27
  33.8 3.0 %collective-permute-start.10 = (f32[4,128,128]{2,1,0:T(8,128)S(1)}, f32[4,128,128]{2,1,0:T(8,128)S(1)}, u32[]{:S(2)}, u32[]{:S(2)}) collective-permute-start(f32[4,128,128]{2,1,0:T(8,128)S(1)} %add.103), channel_id=1, source_target_pairs={{4,8},{6,10},{5,9},{7,11},{20,24},{22,26},{21,25},{23,27}} | collective-permute-start | bytes 786440 | tf_op jit(solution)/shard_map/ppermute | solution.py:27
  34.5 3.7 %collective-permute-start.6 = (f32[4,128,128]{2,1,0:T(8,128)S(1)}, f32[4,128,128]{2,1,0:T(8,128)S(1)}, u32[]{:S(2)}, u32[]{:S(2)}) collective-permute-start(f32[4,128,128]{2,1,0:T(8,128)S(1)} %add.97), channel_id=1, source_target_pairs={{4,8},{6,10},{5,9},{7,11},{20,24},{22,26},{21,25},{23,27}} | collective-permute-start | bytes 786440 | tf_op jit(solution)/shard_map/ppermute | solution.py:27
  35.3 39.4 %copy-start = (f32[16,128,128]{2,1,0:T(8,128)S(1)}, f32[16,128,128]{2,1,0:T(8,128)}, u32[]{:S(2)}) copy-start(f32[16,128,128]{2,1,0:T(8,128)} %shard_map.46) | copy-start | bytes 3145732
  35.3 5.0 %collective-permute-start.2 = (f32[4,128,128]{2,1,0:T(8,128)S(1)}, f32[4,128,128]{2,1,0:T(8,128)S(1)}, u32[]{:S(2)}, u32[]{:S(2)}) collective-permute-start(f32[4,128,128]{2,1,0:T(8,128)S(1)} %add.91), channel_id=1, source_target_pairs={{4,8},{6,10},{5,9},{7,11},{20,24},{22,26},{21,25},{23,27}} | collective-permute-start | bytes 786440 | tf_op jit(solution)/shard_map/ppermute | solution.py:27
  36.2 6.3 %collective-permute-start.14 = (f32[4,128,128]{2,1,0:T(8,128)S(1)}, f32[4,128,128]{2,1,0:T(8,128)S(1)}, u32[]{:S(2)}, u32[]{:S(2)}) collective-permute-start(f32[4,128,128]{2,1,0:T(8,128)S(1)} %add.109), channel_id=1, source_target_pairs={{4,8},{6,10},{5,9},{7,11},{20,24},{22,26},{21,25},{23,27}} | collective-permute-start | bytes 786440 | tf_op jit(solution)/shard_map/ppermute | solution.py:27
  36.9 21.5 %collective-permute-start.11 = (f32[4,128,128]{2,1,0:T(8,128)S(1)}, f32[4,128,128]{2,1,0:T(8,128)}, u32[]{:S(2)}, u32[]{:S(2)}) collective-permute-start(f32[4,128,128]{2,1,0:T(8,128)S(1)} %get-tuple-element.7), channel_id=1, source_target_pairs={{8,12},{10,14},{9,13},{11,15},{24,28},{26,30},{25,29},{27,31}} | collective-permute-start | bytes 786440 | tf_op jit(solution)/shard_map/ppermute | solution.py:27
  39.0 26.3 %collective-permute-start.7 = (f32[4,128,128]{2,1,0:T(8,128)}, f32[4,128,128]{2,1,0:T(8,128)}, u32[]{:S(2)}, u32[]{:S(2)}) collective-permute-start(f32[4,128,128]{2,1,0:T(8,128)} %get-tuple-element.9), channel_id=1, source_target_pairs={{8,12},{10,14},{9,13},{11,15},{24,28},{26,30},{25,29},{27,31}} | collective-permute-start | bytes 786440 | tf_op jit(solution)/shard_map/ppermute | solution.py:27
  41.0 37.3 %copy-start.1 = (f32[2048]{0:T(1024)S(1)}, f32[2048]{0:T(1024)}, u32[]{:S(2)}) copy-start(f32[2048]{0:T(1024)} %param.7) | copy-start | bytes 24580
  41.0 30.1 %collective-permute-start.3 = (f32[4,128,128]{2,1,0:T(8,128)}, f32[4,128,128]{2,1,0:T(8,128)}, u32[]{:S(2)}, u32[]{:S(2)}) collective-permute-start(f32[4,128,128]{2,1,0:T(8,128)} %get-tuple-element.11), channel_id=1, source_target_pairs={{8,12},{10,14},{9,13},{11,15},{24,28},{26,30},{25,29},{27,31}} | collective-permute-start | bytes 786440 | tf_op jit(solution)/shard_map/ppermute | solution.py:27
  43.3 31.4 %collective-permute-start.15 = (f32[4,128,128]{2,1,0:T(8,128)}, f32[4,128,128]{2,1,0:T(8,128)}, u32[]{:S(2)}, u32[]{:S(2)}) collective-permute-start(f32[4,128,128]{2,1,0:T(8,128)} %get-tuple-element.5), channel_id=1, source_target_pairs={{8,12},{10,14},{9,13},{11,15},{24,28},{26,30},{25,29},{27,31}} | collective-permute-start | bytes 786440 | tf_op jit(solution)/shard_map/ppermute | solution.py:27
  76.2 6.1 %collective-permute-start.16 = (bf16[4,128,128]{2,1,0:T(8,128)(2,1)S(1)}, bf16[4,128,128]{2,1,0:T(8,128)(2,1)S(1)}, u32[]{:S(2)}, u32[]{:S(2)}) collective-permute-start(bf16[4,128,128]{2,1,0:T(8,128)(2,1)S(1)} %get-tuple-element.16), channel_id=1, source_target_pairs={{0,2},{4,6},{8,10},{12,14},{2,0},{6,4},{10,8},{14,12},{1,3},{5,7},... | collective-permute-start | bytes 393224 | tf_op jit(solution)/shard_map/ppermute | solution.py:30
  76.8 5.9 %collective-permute-start.17 = (bf16[4,128,128]{2,1,0:T(8,128)(2,1)S(1)}, bf16[4,128,128]{2,1,0:T(8,128)(2,1)S(1)}, u32[]{:S(2)}, u32[]{:S(2)}) collective-permute-start(bf16[4,128,128]{2,1,0:T(8,128)(2,1)S(1)} %get-tuple-element.17), channel_id=1, source_target_pairs={{0,2},{4,6},{8,10},{12,14},{2,0},{6,4},{10,8},{14,12},{1,3},{5,7},... | collective-permute-start | bytes 393224 | tf_op jit(solution)/shard_map/ppermute | solution.py:30
  80.3 6.4 %collective-permute-start.18 = (bf16[4,128,128]{2,1,0:T(8,128)(2,1)S(1)}, bf16[4,128,128]{2,1,0:T(8,128)(2,1)S(1)}, u32[]{:S(2)}, u32[]{:S(2)}) collective-permute-start(bf16[4,128,128]{2,1,0:T(8,128)(2,1)S(1)} %get-tuple-element.18), channel_id=1, source_target_pairs={{0,2},{4,6},{8,10},{12,14},{2,0},{6,4},{10,8},{14,12},{1,3},{5,7},... | collective-permute-start | bytes 393224 | tf_op jit(solution)/shard_map/ppermute | solution.py:30
  80.8 7.9 %collective-permute-start.19 = (bf16[4,128,128]{2,1,0:T(8,128)(2,1)S(1)}, bf16[4,128,128]{2,1,0:T(8,128)(2,1)S(1)}, u32[]{:S(2)}, u32[]{:S(2)}) collective-permute-start(bf16[4,128,128]{2,1,0:T(8,128)(2,1)S(1)} %get-tuple-element.15), channel_id=1, source_target_pairs={{0,2},{4,6},{8,10},{12,14},{2,0},{6,4},{10,8},{14,12},{1,3},{5,7},... | collective-permute-start | bytes 393224 | tf_op jit(solution)/shard_map/ppermute | solution.py:30

commit v8 on v3

--- a/solution.py
+++ b/solution.py
@@ -120,7 +120,7 @@
     keyset = key_rows.reshape(seq_count * row_count, feat_count)
     valset = value_rows.reshape(seq_count * row_count, feat_count)
     state_terms = state_terms_of(keyset, valset, 8)
-    prefix_bf = pair_chain_prefix(state_terms, "ctx", 4)
+    prefix_bf = pair_chain_prefix(state_terms, "ctx", 8)
     normed = attend_of(query, keyset, valset, prefix_bf, full_gain, 8)
     return normed.reshape(seq_count, row_count, feat_count)
 

time: 100 us -> 119 us (1.19)
  starting transfers between devices: 17.8 us -> 35.6 us
  waiting for transfers between devices: 52.1 us -> 47.1 us
  other arithmetic: 8.73 us -> 13 us
    ppermute x12 -> x24, starting transfers between devices: 10.5 us -> 21 us  [pair_chain_prefix(): carried = carried + lax.ppermute(carried + total, axis, links)]
    ppermute x4 -> x8, waiting for transfers between devices: 22.9 us -> 13.2 us  [pair_chain_prefix(): got = lax.ppermute(other_all[piece * step:(piece + 1) * step], axis, swap)]
    ppermute x12 -> x24, waiting for transfers between devices: 22.9 us -> 30.4 us  [pair_chain_prefix(): carried = carried + lax.ppermute(carried + total, axis, links)]
    ppermute x4 -> x8, starting transfers between devices: 3.11 us -> 7.29 us  [pair_chain_prefix(): got = lax.ppermute(other_all[piece * step:(piece + 1) * step], axis, swap)]
    unnamed x0 -> x7, other arithmetic: none -> 3.84 us
    ppermute x4 -> x8, starting transfers between devices: 4.16 us -> 7.39 us  [pair_chain_prefix(): backs.append(lax.ppermute(send, axis, swap))]
    ppermute x4 -> x8, waiting for transfers between devices: 6.27 us -> 3.44 us  [pair_chain_prefix(): backs.append(lax.ppermute(send, axis, swap))]
    add x2 -> x4, other arithmetic: 2.27 us -> 2.97 us  [pair_chain_prefix(): total = mine + got]
  transfers between devices with their start and end apart: 20 -> 40, of which waited for: 11 -> 15; matrix products, arithmetic and copies ran while one was open for 4% -> 8% of each run, Pallas kernels for 0% -> 0%
where the time goes in v8:
time: 119 us; the launch traced here: 118 us
  waiting for transfers between devices  47.1 us (40%)
  starting transfers between devices  35.6 us (30%)
  Pallas kernels  17.7 us (15%)
  other arithmetic  13 us (11%)
  blocking collectives  2.08 us (2%)
  local copies, waits for them, and re-layouts  1.92 us (2%)
    ppermute x24, waiting for transfers between devices, pair_chain_prefix(): carried = carried + lax.ppermute(carried + total, axis, links)  30.4 us
    ppermute x24, starting transfers between devices, pair_chain_prefix(): carried = carried + lax.ppermute(carried + total, axis, links)  21 us
    ppermute x8, waiting for transfers between devices, pair_chain_prefix(): got = lax.ppermute(other_all[piece * step:(piece + 1) * step], axis, swap)  13.2 us
    pallas_call x1, Pallas kernels, attend_of(): pl.pallas_call(attend_kernel, grid=(steps,), in_specs=[pl.BlockSpec((row_...  12.4 us
    ppermute x8, starting transfers between devices, pair_chain_prefix(): backs.append(lax.ppermute(send, axis, swap))  7.39 us
    ppermute x8, starting transfers between devices, pair_chain_prefix(): got = lax.ppermute(other_all[piece * step:(piece + 1) * step], axis, swap)  7.29 us
    pallas_call x1, Pallas kernels, state_terms_of(): pl.pallas_call(state_kernel, grid=(H // group,), in_specs=[pl.BlockSpec((...  5.36 us
    unnamed x7, other arithmetic  3.84 us
  transfers between devices with their start and end apart: 40, of which 15 were waited for; matrix products, arithmetic and copies ran while one was open for 8% of the time, Pallas kernels for 0%

profile of v8, /device:TPU:30, one launch (start us, length us, event | category | flops | bytes accessed | tf_op | source)
XLA Modules:
  0.0 118.1 jit_solution(3445267945872938557)
XLA Ops:
  0.0 5.4 %shard_map.46 = f32[32,128,128]{2,1,0:T(8,128)} custom-call(bf16[384,4096]{1,0:T(8,128)(2,1)} %bitcast.5, bf16[384,4096]{1,0:T(8,128)(2,1)} %bitcast.7), custom_call_target="tpu_custom_call" | custom-call | tf_op jit(solution)/shard_map/pallas_call | solution.py:53
  5.4 1.1 constant_dynamic-slice_fusion.7
  7.1 4.7 %collective-permute-done.16 = f32[2,128,128]{2,1,0:T(8,128)S(1)} collective-permute-done((f32[2,128,128]{2,1,0:T(8,128)S(1)}, f32[2,128,128]{2,1,0:T(8,128)S(1)}, u32[]{:S(2)}, u32[]{:S(2)}) %collective-permute-start.16) | collective-permute-done | bytes 131104 | tf_op jit(solution)/shard_map/ppermute | solution.py:24
  12.4 0.9 dynamic-slice_add_fusion.3
  13.4 0.7 collective-permute-start.17
  15.4 1.3 %collective-permute-start.19 = (f32[2,128,128]{2,1,0:T(8,128)S(1)}, f32[2,128,128]{2,1,0:T(8,128)S(1)}, u32[]{:S(2)}, u32[]{:S(2)}) collective-permute-start(f32[2,128,128]{2,1,0:T(8,128)S(1)} %get-tuple-element.11), channel_id=1, source_target_pairs={{8,12},{10,14},{9,13},{11,15},{24,28},{26,30},{25,29},{27,31}} | collective-permute-start | bytes 393224 | tf_op jit(solution)/shard_map/ppermute | solution.py:29
  16.7 3.1 %collective-permute-done.28 = f32[2,128,128]{2,1,0:T(8,128)S(1)} collective-permute-done((f32[2,128,128]{2,1,0:T(8,128)S(1)}, f32[2,128,128]{2,1,0:T(8,128)S(1)}, u32[]{:S(2)}, u32[]{:S(2)}) %collective-permute-start.28) | collective-permute-done | bytes 131104 | tf_op jit(solution)/shard_map/ppermute | solution.py:24
  19.8 9.8 %collective-permute-done.19 = f32[2,128,128]{2,1,0:T(8,128)S(1)} collective-permute-done((f32[2,128,128]{2,1,0:T(8,128)S(1)}, f32[2,128,128]{2,1,0:T(8,128)S(1)}, u32[]{:S(2)}, u32[]{:S(2)}) %collective-permute-start.19) | collective-permute-done | bytes 131104 | tf_op jit(solution)/shard_map/ppermute | solution.py:29
  29.6 2.0 %dynamic-slice_add_fusion = (f32[2,128,128]{2,1,0:T(8,128)S(1)}, bf16[2,128,128]{2,1,0:T(8,128)(2,1)}, f32[2,128,128]{2,1,0:T(8,128)S(1)}, f32[2,128,128]{2,1,0:...) fusion(f32[2,128,128]{2,1,0:T(8,128)S(1)} %collective-permute-done.28, f32[32,128,128]{2,1,0:T(8,128)} %shard_map.46, ...), kind=kLoop, calls=%fused_computation.19 | loop fusion | flops 163840 | bytes 1900569 | tf_op jit(solution)/shard_map/add | solution.py:25
  32.1 1.5 %collective-permute-start.12 = (f32[2,128,128]{2,1,0:T(8,128)S(1)}, f32[2,128,128]{2,1,0:T(8,128)S(1)}, u32[]{:S(2)}, u32[]{:S(2)}) collective-permute-start(f32[2,128,128]{2,1,0:T(8,128)S(1)} %get-tuple-element.30), channel_id=1, source_target_pairs={{0,2},{4,6},{8,10},{12,14},{2,0},{6,4},{10,8},{14,12},{1,3},{5,7},... | collective-permute-start | bytes 393224 | tf_op jit(solution)/shard_map/ppermute | solution.py:24
  34.1 1.5 %collective-permute-start.4 = (f32[2,128,128]{2,1,0:T(8,128)S(1)}, f32[2,128,128]{2,1,0:T(8,128)S(1)}, u32[]{:S(2)}, u32[]{:S(2)}) collective-permute-start(f32[2,128,128]{2,1,0:T(8,128)S(1)} %get-tuple-element.32), channel_id=1, source_target_pairs={{0,2},{4,6},{8,10},{12,14},{2,0},{6,4},{10,8},{14,12},{1,3},{5,7},... | collective-permute-start | bytes 393224 | tf_op jit(solution)/shard_map/ppermute | solution.py:24
  36.3 1.2 %collective-permute-done = f32[2,128,128]{2,1,0:T(8,128)S(1)} collective-permute-done((f32[2,128,128]{2,1,0:T(8,128)}, f32[2,128,128]{2,1,0:T(8,128)S(1)}, u32[]{:S(2)}, u32[]{:S(2)}) %collective-permute-start) | collective-permute-done | bytes 131104 | tf_op jit(solution)/shard_map/ppermute | solution.py:24
  37.5 1.4 %collective-permute-done.12 = f32[2,128,128]{2,1,0:T(8,128)S(1)} collective-permute-done((f32[2,128,128]{2,1,0:T(8,128)S(1)}, f32[2,128,128]{2,1,0:T(8,128)S(1)}, u32[]{:S(2)}, u32[]{:S(2)}) %collective-permute-start.12) | collective-permute-done | bytes 131104 | tf_op jit(solution)/shard_map/ppermute | solution.py:24
  38.9 1.4 %collective-permute-done.8 = f32[2,128,128]{2,1,0:T(8,128)S(1)} collective-permute-done((f32[2,128,128]{2,1,0:T(8,128)S(1)}, f32[2,128,128]{2,1,0:T(8,128)S(1)}, u32[]{:S(2)}, u32[]{:S(2)}) %collective-permute-start.8) | collective-permute-done | bytes 131104 | tf_op jit(solution)/shard_map/ppermute | solution.py:24
  40.3 1.4 %collective-permute-done.4 = f32[2,128,128]{2,1,0:T(8,128)S(1)} collective-permute-done((f32[2,128,128]{2,1,0:T(8,128)S(1)}, f32[2,128,128]{2,1,0:T(8,128)S(1)}, u32[]{:S(2)}, u32[]{:S(2)}) %collective-permute-start.4) | collective-permute-done | bytes 131104 | tf_op jit(solution)/shard_map/ppermute | solution.py:24
  48.1 0.7 fusion.8
  48.8 1.3 %collective-permute-start.31 = (f32[2,128,128]{2,1,0:T(8,128)}, f32[2,128,128]{2,1,0:T(8,128)S(1)}, u32[]{:S(2)}, u32[]{:S(2)}) collective-permute-start(f32[2,128,128]{2,1,0:T(8,128)} %get-tuple-element.5), channel_id=1, source_target_pairs={{8,12},{10,14},{9,13},{11,15},{24,28},{26,30},{25,29},{27,31}} | collective-permute-start | bytes 393224 | tf_op jit(solution)/shard_map/ppermute | solution.py:29
  50.1 0.7 fusion.15
  50.7 1.3 %collective-permute-start.3 = (f32[2,128,128]{2,1,0:T(8,128)}, f32[2,128,128]{2,1,0:T(8,128)}, u32[]{:S(2)}, u32[]{:S(2)}) collective-permute-start(f32[2,128,128]{2,1,0:T(8,128)} %get-tuple-element.19), channel_id=1, source_target_pairs={{8,12},{10,14},{9,13},{11,15},{24,28},{26,30},{25,29},{27,31}} | collective-permute-start | bytes 393224 | tf_op jit(solution)/shard_map/ppermute | solution.py:29
  52.0 0.7 fusion.14
  52.7 1.3 %collective-permute-start.7 = (f32[2,128,128]{2,1,0:T(8,128)}, f32[2,128,128]{2,1,0:T(8,128)}, u32[]{:S(2)}, u32[]{:S(2)}) collective-permute-start(f32[2,128,128]{2,1,0:T(8,128)} %get-tuple-element.17), channel_id=1, source_target_pairs={{8,12},{10,14},{9,13},{11,15},{24,28},{26,30},{25,29},{27,31}} | collective-permute-start | bytes 393224 | tf_op jit(solution)/shard_map/ppermute | solution.py:29
  54.0 0.7 fusion.13
  54.7 1.3 %collective-permute-start.11 = (f32[2,128,128]{2,1,0:T(8,128)}, f32[2,128,128]{2,1,0:T(8,128)}, u32[]{:S(2)}, u32[]{:S(2)}) collective-permute-start(f32[2,128,128]{2,1,0:T(8,128)} %get-tuple-element.15), channel_id=1, source_target_pairs={{8,12},{10,14},{9,13},{11,15},{24,28},{26,30},{25,29},{27,31}} | collective-permute-start | bytes 393224 | tf_op jit(solution)/shard_map/ppermute | solution.py:29
  56.0 0.7 fusion.12
  56.7 1.3 %collective-permute-start.15 = (f32[2,128,128]{2,1,0:T(8,128)}, f32[2,128,128]{2,1,0:T(8,128)}, u32[]{:S(2)}, u32[]{:S(2)}) collective-permute-start(f32[2,128,128]{2,1,0:T(8,128)} %get-tuple-element.13), channel_id=1, source_target_pairs={{8,12},{10,14},{9,13},{11,15},{24,28},{26,30},{25,29},{27,31}} | collective-permute-start | bytes 393224 | tf_op jit(solution)/shard_map/ppermute | solution.py:29
  58.0 2.1 %all_gather.3 = f32[4096]{0:T(1024)} all-gather(f32[2048]{0:T(1024)S(1)} %copy-done.7), channel_id=1, replica_groups=mesh['groups'=2,'ctx'=8,'dp'=2] {'dp'}, dimensions={0}, use_global_device_ids=true | all-gather | bytes 24576 | tf_op jit(solution)/shard_map/all_gather | solution.py:118
  60.6 1.3 %collective-permute-done.3 = f32[2,128,128]{2,1,0:T(8,128)} collective-permute-done((f32[2,128,128]{2,1,0:T(8,128)}, f32[2,128,128]{2,1,0:T(8,128)}, u32[]{:S(2)}, u32[]{:S(2)}) %collective-permute-start.3) | collective-permute-done | bytes 131104 | tf_op jit(solution)/shard_map/ppermute | solution.py:29
  61.9 1.7 %collective-permute-done.7 = f32[2,128,128]{2,1,0:T(8,128)} collective-permute-done((f32[2,128,128]{2,1,0:T(8,128)}, f32[2,128,128]{2,1,0:T(8,128)}, u32[]{:S(2)}, u32[]{:S(2)}) %collective-permute-start.7) | collective-permute-done | bytes 131104 | tf_op jit(solution)/shard_map/ppermute | solution.py:29
  63.5 1.6 %collective-permute-done.11 = f32[2,128,128]{2,1,0:T(8,128)} collective-permute-done((f32[2,128,128]{2,1,0:T(8,128)}, f32[2,128,128]{2,1,0:T(8,128)}, u32[]{:S(2)}, u32[]{:S(2)}) %collective-permute-start.11) | collective-permute-done | bytes 131104 | tf_op jit(solution)/shard_map/ppermute | solution.py:29
  65.2 2.6 %collective-permute-done.15 = f32[2,128,128]{2,1,0:T(8,128)} collective-permute-done((f32[2,128,128]{2,1,0:T(8,128)}, f32[2,128,128]{2,1,0:T(8,128)}, u32[]{:S(2)}, u32[]{:S(2)}) %collective-permute-start.15) | collective-permute-done | bytes 131104 | tf_op jit(solution)/shard_map/ppermute | solution.py:29
  67.8 1.3 %add_convert_fusion = (bf16[2,128,128]{2,1,0:T(8,128)(2,1)S(1)}, bf16[2,128,128]{2,1,0:T(8,128)(2,1)S(1)}, bf16[2,128,128]{2,1,0:T(8,128)(2,1)S(1)}, bf16[2,128,...) fusion(f32[32,128,128]{2,1,0:T(8,128)S(1)} %copy-done, ...), kind=kLoop, calls=%fused_computation.3 | loop fusion | flops 655360 | bytes 2818077 | tf_op jit(solution)/shard_map/convert_element_type | solution.py:31
  69.6 1.5 %collective-permute-start.24 = (f32[2,128,128]{2,1,0:T(8,128)S(1)}, f32[2,128,128]{2,1,0:T(8,128)S(1)}, u32[]{:S(2)}, u32[]{:S(2)}) collective-permute-start(f32[2,128,128]{2,1,0:T(8,128)S(1)} %get-tuple-element.26), channel_id=1, source_target_pairs={{0,2},{4,6},{8,10},{12,14},{2,0},{6,4},{10,8},{14,12},{1,3},{5,7},... | collective-permute-start | bytes 393224 | tf_op jit(solution)/shard_map/ppermute | solution.py:24
  71.6 1.5 %collective-permute-start.33 = (bf16[2,128,128]{2,1,0:T(8,128)(2,1)S(1)}, bf16[2,128,128]{2,1,0:T(8,128)(2,1)S(1)}, u32[]{:S(2)}, u32[]{:S(2)}) collective-permute-start(bf16[2,128,128]{2,1,0:T(8,128)(2,1)S(1)} %get-tuple-element.23), channel_id=1, source_target_pairs={{0,2},{4,6},{8,10},{12,14},{2,0},{6,4},{10,8},{14,12},{1,3},{5,7},... | collective-permute-start | bytes 196616 | tf_op jit(solution)/shard_map/ppermute | solution.py:32
  73.2 0.9 fusion
  74.1 0.9 fusion.1
  75.1 0.9 fusion.2
  76.0 0.9 fusion.3
  78.3 1.6 %collective-permute-start.35 = (bf16[2,128,128]{2,1,0:T(8,128)(2,1)S(1)}, bf16[2,128,128]{2,1,0:T(8,128)(2,1)S(1)}, u32[]{:S(2)}, u32[]{:S(2)}) collective-permute-start(bf16[2,128,128]{2,1,0:T(8,128)(2,1)S(1)} %get-tuple-element.25), channel_id=1, source_target_pairs={{0,2},{4,6},{8,10},{12,14},{2,0},{6,4},{10,8},{14,12},{1,3},{5,7},... | collective-permute-start | bytes 196616 | tf_op jit(solution)/shard_map/ppermute | solution.py:32
  82.6 1.3 %collective-permute-start.23 = (f32[2,128,128]{2,1,0:T(8,128)S(1)}, f32[2,128,128]{2,1,0:T(8,128)S(1)}, u32[]{:S(2)}, u32[]{:S(2)}) collective-permute-start(f32[2,128,128]{2,1,0:T(8,128)S(1)} %get-tuple-element.9), channel_id=1, source_target_pairs={{8,12},{10,14},{9,13},{11,15},{24,28},{26,30},{25,29},{27,31}} | collective-permute-start | bytes 393224 | tf_op jit(solution)/shard_map/ppermute | solution.py:29
  84.0 1.3 %collective-permute-start.27 = (f32[2,128,128]{2,1,0:T(8,128)S(1)}, f32[2,128,128]{2,1,0:T(8,128)S(1)}, u32[]{:S(2)}, u32[]{:S(2)}) collective-permute-start(f32[2,128,128]{2,1,0:T(8,128)S(1)} %get-tuple-element.7), channel_id=1, source_target_pairs={{8,12},{10,14},{9,13},{11,15},{24,28},{26,30},{25,29},{27,31}} | collective-permute-start | bytes 393224 | tf_op jit(solution)/shard_map/ppermute | solution.py:29
  85.3 9.5 %collective-permute-done.23 = f32[2,128,128]{2,1,0:T(8,128)S(1)} collective-permute-done((f32[2,128,128]{2,1,0:T(8,128)S(1)}, f32[2,128,128]{2,1,0:T(8,128)S(1)}, u32[]{:S(2)}, u32[]{:S(2)}) %collective-permute-start.23) | collective-permute-done | bytes 131104 | tf_op jit(solution)/shard_map/ppermute | solution.py:29
  94.8 3.9 %collective-permute-done.27 = f32[2,128,128]{2,1,0:T(8,128)S(1)} collective-permute-done((f32[2,128,128]{2,1,0:T(8,128)S(1)}, f32[2,128,128]{2,1,0:T(8,128)S(1)}, u32[]{:S(2)}, u32[]{:S(2)}) %collective-permute-start.27) | collective-permute-done | bytes 131104 | tf_op jit(solution)/shard_map/ppermute | solution.py:29
  98.8 1.4 %collective-permute-start.37 = (bf16[2,128,128]{2,1,0:T(8,128)(2,1)S(1)}, bf16[2,128,128]{2,1,0:T(8,128)(2,1)S(1)}, u32[]{:S(2)}, u32[]{:S(2)}) collective-permute-start(bf16[2,128,128]{2,1,0:T(8,128)(2,1)S(1)} %get-tuple-element.37), channel_id=1, source_target_pairs={{0,2},{4,6},{8,10},{12,14},{2,0},{6,4},{10,8},{14,12},{1,3},{5,7},... | collective-permute-start | bytes 196616 | tf_op jit(solution)/shard_map/ppermute | solution.py:32
  100.2 0.7 collective-permute-start.38
  101.0 2.1 %collective-permute-done.37 = bf16[2,128,128]{2,1,0:T(8,128)(2,1)S(1)} collective-permute-done((bf16[2,128,128]{2,1,0:T(8,128)(2,1)S(1)}, bf16[2,128,128]{2,1,0:T(8,128)(2,1)S(1)}, u32[]{:S(2)}, u32[]{:S(2)}) %collective-permute-start.37) | collective-permute-done | bytes 65568 | tf_op jit(solution)/shard_map/ppermute | solution.py:32
  103.1 1.3 %collective-permute-done.38 = bf16[2,128,128]{2,1,0:T(8,128)(2,1)S(1)} collective-permute-done((bf16[2,128,128]{2,1,0:T(8,128)(2,1)S(1)}, bf16[2,128,128]{2,1,0:T(8,128)(2,1)S(1)}, u32[]{:S(2)}, u32[]{:S(2)}) %collective-permute-start.38) | collective-permute-done | bytes 65568 | tf_op jit(solution)/shard_map/ppermute | solution.py:32
  104.5 1.1 pad_maximum_fusion.prefix_ref
  105.7 12.4 %shard_map.47 = bf16[384,4096]{1,0:T(8,128)(2,1)} custom-call(bf16[384,4096]{1,0:T(8,128)(2,1)} %bitcast.9, bf16[384,4096]{1,0:T(8,128)(2,1)} %bitcast.6, bf16[384,4096]{1,0:T(8,128)(2,1)} %bitcast.8, bf16[32,128,128]{2,1,0:T(8,128)(2,1)} %pad_maximum_fusion.prefix_ref, f32[1,4096]{1,0:T(1,128)} %bitcast.10), custom_call_target="tpu_custom_call" | custom-call | tf_op jit(solution)/shard_map/pallas_call | solution.py:101
  (92 shorter events, 16.3 us)
Async XLA Ops:
  5.4 36.3 %copy-start = (f32[32,128,128]{2,1,0:T(8,128)S(1)}, f32[32,128,128]{2,1,0:T(8,128)}, u32[]{:S(2)}) copy-start(f32[32,128,128]{2,1,0:T(8,128)} %shard_map.46) | copy-start | bytes 6291460
  6.5 5.3 %collective-permute-start.16 = (f32[2,128,128]{2,1,0:T(8,128)S(1)}, f32[2,128,128]{2,1,0:T(8,128)S(1)}, u32[]{:S(2)}, u32[]{:S(2)}) collective-permute-start(f32[2,128,128]{2,1,0:T(8,128)S(1)} %get-tuple-element.35), channel_id=1, source_target_pairs={{0,2},{4,6},{8,10},{12,14},{2,0},{6,4},{10,8},{14,12},{1,3},{5,7},... | collective-permute-start | bytes 393224 | tf_op jit(solution)/shard_map/ppermute | solution.py:24
  11.8 0.6 copy-start.5
  13.4 0.7 collective-permute-start.17
  14.1 1.3 %collective-permute-start.18 = (f32[2,128,128]{2,1,0:T(8,128)S(1)}, f32[2,128,128]{2,1,0:T(8,128)S(1)}, u32[]{:S(2)}, u32[]{:S(2)}) collective-permute-start(f32[2,128,128]{2,1,0:T(8,128)S(1)} %add.206), channel_id=1, source_target_pairs={{4,8},{6,10},{5,9},{7,11},{20,24},{22,26},{21,25},{23,27}} | collective-permute-start | bytes 393224 | tf_op jit(solution)/shard_map/ppermute | solution.py:29
  14.8 5.0 %collective-permute-start.28 = (f32[2,128,128]{2,1,0:T(8,128)S(1)}, f32[2,128,128]{2,1,0:T(8,128)S(1)}, u32[]{:S(2)}, u32[]{:S(2)}) collective-permute-start(f32[2,128,128]{2,1,0:T(8,128)S(1)} %get-tuple-element.34), channel_id=1, source_target_pairs={{0,2},{4,6},{8,10},{12,14},{2,0},{6,4},{10,8},{14,12},{1,3},{5,7},... | collective-permute-start | bytes 393224 | tf_op jit(solution)/shard_map/ppermute | solution.py:24
  15.4 14.3 %collective-permute-start.19 = (f32[2,128,128]{2,1,0:T(8,128)S(1)}, f32[2,128,128]{2,1,0:T(8,128)S(1)}, u32[]{:S(2)}, u32[]{:S(2)}) collective-permute-start(f32[2,128,128]{2,1,0:T(8,128)S(1)} %get-tuple-element.11), channel_id=1, source_target_pairs={{8,12},{10,14},{9,13},{11,15},{24,28},{26,30},{25,29},{27,31}} | collective-permute-start | bytes 393224 | tf_op jit(solution)/shard_map/ppermute | solution.py:29
  31.6 5.9 %collective-permute-start = (f32[2,128,128]{2,1,0:T(8,128)}, f32[2,128,128]{2,1,0:T(8,128)S(1)}, u32[]{:S(2)}, u32[]{:S(2)}) collective-permute-start(f32[2,128,128]{2,1,0:T(8,128)} %get-tuple-element.33), channel_id=1, source_target_pairs={{0,2},{4,6},{8,10},{12,14},{2,0},{6,4},{10,8},{14,12},{1,3},{5,7},... | collective-permute-start | bytes 393224 | tf_op jit(solution)/shard_map/ppermute | solution.py:24
  32.1 6.8 %collective-permute-start.12 = (f32[2,128,128]{2,1,0:T(8,128)S(1)}, f32[2,128,128]{2,1,0:T(8,128)S(1)}, u32[]{:S(2)}, u32[]{:S(2)}) collective-permute-start(f32[2,128,128]{2,1,0:T(8,128)S(1)} %get-tuple-element.30), channel_id=1, source_target_pairs={{0,2},{4,6},{8,10},{12,14},{2,0},{6,4},{10,8},{14,12},{1,3},{5,7},... | collective-permute-start | bytes 393224 | tf_op jit(solution)/shard_map/ppermute | solution.py:24
  33.6 6.7 %collective-permute-start.8 = (f32[2,128,128]{2,1,0:T(8,128)S(1)}, f32[2,128,128]{2,1,0:T(8,128)S(1)}, u32[]{:S(2)}, u32[]{:S(2)}) collective-permute-start(f32[2,128,128]{2,1,0:T(8,128)S(1)} %get-tuple-element.31), channel_id=1, source_target_pairs={{0,2},{4,6},{8,10},{12,14},{2,0},{6,4},{10,8},{14,12},{1,3},{5,7},... | collective-permute-start | bytes 393224 | tf_op jit(solution)/shard_map/ppermute | solution.py:24
  34.1 7.6 %collective-permute-start.4 = (f32[2,128,128]{2,1,0:T(8,128)S(1)}, f32[2,128,128]{2,1,0:T(8,128)S(1)}, u32[]{:S(2)}, u32[]{:S(2)}) collective-permute-start(f32[2,128,128]{2,1,0:T(8,128)S(1)} %get-tuple-element.32), channel_id=1, source_target_pairs={{0,2},{4,6},{8,10},{12,14},{2,0},{6,4},{10,8},{14,12},{1,3},{5,7},... | collective-permute-start | bytes 393224 | tf_op jit(solution)/shard_map/ppermute | solution.py:24
  35.6 8.8 %collective-permute-start.29 = (f32[2,128,128]{2,1,0:T(8,128)S(1)}, f32[2,128,128]{2,1,0:T(8,128)S(1)}, u32[]{:S(2)}, u32[]{:S(2)}) collective-permute-start(f32[2,128,128]{2,1,0:T(8,128)S(1)} %get-tuple-element.28), channel_id=1, source_target_pairs={{0,4},{2,6},{1,5},{3,7},{16,20},{18,22},{17,21},{19,23}} | collective-permute-start | bytes 393224 | tf_op jit(solution)/shard_map/ppermute | solution.py:29
  37.5 11.3 %copy-start.1 = (f32[2,128,128]{2,1,0:T(8,128)}, f32[2,128,128]{2,1,0:T(8,128)S(1)}, u32[]{:S(2)}) copy-start(f32[2,128,128]{2,1,0:T(8,128)S(1)} %collective-permute-done) | copy-start | bytes 393220
  41.7 6.3 %copy-start.3 = (f32[2,128,128]{2,1,0:T(8,128)}, f32[2,128,128]{2,1,0:T(8,128)S(1)}, u32[]{:S(2)}) copy-start(f32[2,128,128]{2,1,0:T(8,128)S(1)} %collective-permute-done.4) | copy-start | bytes 393220
  41.8 3.4 %collective-permute-start.1 = (f32[2,128,128]{2,1,0:T(8,128)S(1)}, f32[2,128,128]{2,1,0:T(8,128)S(1)}, u32[]{:S(2)}, u32[]{:S(2)}) collective-permute-start(f32[2,128,128]{2,1,0:T(8,128)S(1)} %get-tuple-element.43), channel_id=1, source_target_pairs={{0,4},{2,6},{1,5},{3,7},{16,20},{18,22},{17,21},{19,23}} | collective-permute-start | bytes 393224 | tf_op jit(solution)/shard_map/ppermute | solution.py:29
  42.4 3.5 %collective-permute-start.5 = (f32[2,128,128]{2,1,0:T(8,128)S(1)}, f32[2,128,128]{2,1,0:T(8,128)S(1)}, u32[]{:S(2)}, u32[]{:S(2)}) collective-permute-start(f32[2,128,128]{2,1,0:T(8,128)S(1)} %get-tuple-element.42), channel_id=1, source_target_pairs={{0,4},{2,6},{1,5},{3,7},{16,20},{18,22},{17,21},{19,23}} | collective-permute-start | bytes 393224 | tf_op jit(solution)/shard_map/ppermute | solution.py:29
  43.1 3.5 %collective-permute-start.9 = (f32[2,128,128]{2,1,0:T(8,128)S(1)}, f32[2,128,128]{2,1,0:T(8,128)S(1)}, u32[]{:S(2)}, u32[]{:S(2)}) collective-permute-start(f32[2,128,128]{2,1,0:T(8,128)S(1)} %get-tuple-element.41), channel_id=1, source_target_pairs={{0,4},{2,6},{1,5},{3,7},{16,20},{18,22},{17,21},{19,23}} | collective-permute-start | bytes 393224 | tf_op jit(solution)/shard_map/ppermute | solution.py:29
  43.8 3.5 %collective-permute-start.13 = (f32[2,128,128]{2,1,0:T(8,128)S(1)}, f32[2,128,128]{2,1,0:T(8,128)S(1)}, u32[]{:S(2)}, u32[]{:S(2)}) collective-permute-start(f32[2,128,128]{2,1,0:T(8,128)S(1)} %get-tuple-element.40), channel_id=1, source_target_pairs={{0,4},{2,6},{1,5},{3,7},{16,20},{18,22},{17,21},{19,23}} | collective-permute-start | bytes 393224 | tf_op jit(solution)/shard_map/ppermute | solution.py:29
  44.5 3.5 %collective-permute-start.30 = (f32[2,128,128]{2,1,0:T(8,128)S(1)}, f32[2,128,128]{2,1,0:T(8,128)S(1)}, u32[]{:S(2)}, u32[]{:S(2)}) collective-permute-start(f32[2,128,128]{2,1,0:T(8,128)S(1)} %add.224), channel_id=1, source_target_pairs={{4,8},{6,10},{5,9},{7,11},{20,24},{22,26},{21,25},{23,27}} | collective-permute-start | bytes 393224 | tf_op jit(solution)/shard_map/ppermute | solution.py:29
  45.2 4.8 %collective-permute-start.2 = (f32[2,128,128]{2,1,0:T(8,128)S(1)}, f32[2,128,128]{2,1,0:T(8,128)S(1)}, u32[]{:S(2)}, u32[]{:S(2)}) collective-permute-start(f32[2,128,128]{2,1,0:T(8,128)S(1)} %add.182), channel_id=1, source_target_pairs={{4,8},{6,10},{5,9},{7,11},{20,24},{22,26},{21,25},{23,27}} | collective-permute-start | bytes 393224 | tf_op jit(solution)/shard_map/ppermute | solution.py:29
  45.9 12.0 %copy-start.7 = (f32[2048]{0:T(1024)S(1)}, f32[2048]{0:T(1024)}, u32[]{:S(2)}) copy-start(f32[2048]{0:T(1024)} %param.7) | copy-start | bytes 24580
  45.9 6.1 %collective-permute-start.6 = (f32[2,128,128]{2,1,0:T(8,128)S(1)}, f32[2,128,128]{2,1,0:T(8,128)S(1)}, u32[]{:S(2)}, u32[]{:S(2)}) collective-permute-start(f32[2,128,128]{2,1,0:T(8,128)S(1)} %add.188), channel_id=1, source_target_pairs={{4,8},{6,10},{5,9},{7,11},{20,24},{22,26},{21,25},{23,27}} | collective-permute-start | bytes 393224 | tf_op jit(solution)/shard_map/ppermute | solution.py:29
  46.7 7.4 %collective-permute-start.10 = (f32[2,128,128]{2,1,0:T(8,128)S(1)}, f32[2,128,128]{2,1,0:T(8,128)S(1)}, u32[]{:S(2)}, u32[]{:S(2)}) collective-permute-start(f32[2,128,128]{2,1,0:T(8,128)S(1)} %add.194), channel_id=1, source_target_pairs={{4,8},{6,10},{5,9},{7,11},{20,24},{22,26},{21,25},{23,27}} | collective-permute-start | bytes 393224 | tf_op jit(solution)/shard_map/ppermute | solution.py:29
  47.4 8.6 %collective-permute-start.14 = (f32[2,128,128]{2,1,0:T(8,128)S(1)}, f32[2,128,128]{2,1,0:T(8,128)S(1)}, u32[]{:S(2)}, u32[]{:S(2)}) collective-permute-start(f32[2,128,128]{2,1,0:T(8,128)S(1)} %add.200), channel_id=1, source_target_pairs={{4,8},{6,10},{5,9},{7,11},{20,24},{22,26},{21,25},{23,27}} | collective-permute-start | bytes 393224 | tf_op jit(solution)/shard_map/ppermute | solution.py:29
  48.8 11.3 %collective-permute-start.31 = (f32[2,128,128]{2,1,0:T(8,128)}, f32[2,128,128]{2,1,0:T(8,128)S(1)}, u32[]{:S(2)}, u32[]{:S(2)}) collective-permute-start(f32[2,128,128]{2,1,0:T(8,128)} %get-tuple-element.5), channel_id=1, source_target_pairs={{8,12},{10,14},{9,13},{11,15},{24,28},{26,30},{25,29},{27,31}} | collective-permute-start | bytes 393224 | tf_op jit(solution)/shard_map/ppermute | solution.py:29
  50.7 11.1 %collective-permute-start.3 = (f32[2,128,128]{2,1,0:T(8,128)}, f32[2,128,128]{2,1,0:T(8,128)}, u32[]{:S(2)}, u32[]{:S(2)}) collective-permute-start(f32[2,128,128]{2,1,0:T(8,128)} %get-tuple-element.19), channel_id=1, source_target_pairs={{8,12},{10,14},{9,13},{11,15},{24,28},{26,30},{25,29},{27,31}} | collective-permute-start | bytes 393224 | tf_op jit(solution)/shard_map/ppermute | solution.py:29
  52.7 10.8 %collective-permute-start.7 = (f32[2,128,128]{2,1,0:T(8,128)}, f32[2,128,128]{2,1,0:T(8,128)}, u32[]{:S(2)}, u32[]{:S(2)}) collective-permute-start(f32[2,128,128]{2,1,0:T(8,128)} %get-tuple-element.17), channel_id=1, source_target_pairs={{8,12},{10,14},{9,13},{11,15},{24,28},{26,30},{25,29},{27,31}} | collective-permute-start | bytes 393224 | tf_op jit(solution)/shard_map/ppermute | solution.py:29
  54.7 10.5 %collective-permute-start.11 = (f32[2,128,128]{2,1,0:T(8,128)}, f32[2,128,128]{2,1,0:T(8,128)}, u32[]{:S(2)}, u32[]{:S(2)}) collective-permute-start(f32[2,128,128]{2,1,0:T(8,128)} %get-tuple-element.15), channel_id=1, source_target_pairs={{8,12},{10,14},{9,13},{11,15},{24,28},{26,30},{25,29},{27,31}} | collective-permute-start | bytes 393224 | tf_op jit(solution)/shard_map/ppermute | solution.py:29
  56.7 11.1 %collective-permute-start.15 = (f32[2,128,128]{2,1,0:T(8,128)}, f32[2,128,128]{2,1,0:T(8,128)}, u32[]{:S(2)}, u32[]{:S(2)}) collective-permute-start(f32[2,128,128]{2,1,0:T(8,128)} %get-tuple-element.13), channel_id=1, source_target_pairs={{8,12},{10,14},{9,13},{11,15},{24,28},{26,30},{25,29},{27,31}} | collective-permute-start | bytes 393224 | tf_op jit(solution)/shard_map/ppermute | solution.py:29
  58.0 15.2 %copy-start.2 = (f32[2,128,128]{2,1,0:T(8,128)S(1)}, f32[2,128,128]{2,1,0:T(8,128)}, u32[]{:S(2)}) copy-start(f32[2,128,128]{2,1,0:T(8,128)} %copy-done.1) | copy-start | bytes 393220
  58.0 16.1 %copy-start.4 = (f32[2,128,128]{2,1,0:T(8,128)S(1)}, f32[2,128,128]{2,1,0:T(8,128)}, u32[]{:S(2)}) copy-start(f32[2,128,128]{2,1,0:T(8,128)} %copy-done.3) | copy-start | bytes 393220
  60.1 25.2 %collective-permute-start.36 = (bf16[2,128,128]{2,1,0:T(8,128)(2,1)}, bf16[2,128,128]{2,1,0:T(8,128)(2,1)S(1)}, u32[]{:S(2)}, u32[]{:S(2)}) collective-permute-start(bf16[2,128,128]{2,1,0:T(8,128)(2,1)} %get-tuple-element.29), channel_id=1, source_target_pairs={{0,2},{4,6},{8,10},{12,14},{2,0},{6,4},{10,8},{14,12},{1,3},{5,7},... | collective-permute-start | bytes 196616 | tf_op jit(solution)/shard_map/ppermute | solution.py:32
  67.8 10.4 %copy-start.6 = (f32[2,128,128]{2,1,0:T(8,128)S(1)}, f32[2,128,128]{2,1,0:T(8,128)}, u32[]{:S(2)}) copy-start(f32[2,128,128]{2,1,0:T(8,128)} %copy-done.5) | copy-start | bytes 393220
  69.0 7.9 %collective-permute-start.20 = (f32[2,128,128]{2,1,0:T(8,128)S(1)}, f32[2,128,128]{2,1,0:T(8,128)S(1)}, u32[]{:S(2)}, u32[]{:S(2)}) collective-permute-start(f32[2,128,128]{2,1,0:T(8,128)S(1)} %get-tuple-element.27), channel_id=1, source_target_pairs={{0,2},{4,6},{8,10},{12,14},{2,0},{6,4},{10,8},{14,12},{1,3},{5,7},... | collective-permute-start | bytes 393224 | tf_op jit(solution)/shard_map/ppermute | solution.py:24
  69.6 7.9 %collective-permute-start.24 = (f32[2,128,128]{2,1,0:T(8,128)S(1)}, f32[2,128,128]{2,1,0:T(8,128)S(1)}, u32[]{:S(2)}, u32[]{:S(2)}) collective-permute-start(f32[2,128,128]{2,1,0:T(8,128)S(1)} %get-tuple-element.26), channel_id=1, source_target_pairs={{0,2},{4,6},{8,10},{12,14},{2,0},{6,4},{10,8},{14,12},{1,3},{5,7},... | collective-permute-start | bytes 393224 | tf_op jit(solution)/shard_map/ppermute | solution.py:24
  71.1 7.1 %collective-permute-start.32 = (bf16[2,128,128]{2,1,0:T(8,128)(2,1)S(1)}, bf16[2,128,128]{2,1,0:T(8,128)(2,1)S(1)}, u32[]{:S(2)}, u32[]{:S(2)}) collective-permute-start(bf16[2,128,128]{2,1,0:T(8,128)(2,1)S(1)} %get-tuple-element.22), channel_id=1, source_target_pairs={{0,2},{4,6},{8,10},{12,14},{2,0},{6,4},{10,8},{14,12},{1,3},{5,7},... | collective-permute-start | bytes 196616 | tf_op jit(solution)/shard_map/ppermute | solution.py:32
  71.6 9.0 %collective-permute-start.33 = (bf16[2,128,128]{2,1,0:T(8,128)(2,1)S(1)}, bf16[2,128,128]{2,1,0:T(8,128)(2,1)S(1)}, u32[]{:S(2)}, u32[]{:S(2)}) collective-permute-start(bf16[2,128,128]{2,1,0:T(8,128)(2,1)S(1)} %get-tuple-element.23), channel_id=1, source_target_pairs={{0,2},{4,6},{8,10},{12,14},{2,0},{6,4},{10,8},{14,12},{1,3},{5,7},... | collective-permute-start | bytes 196616 | tf_op jit(solution)/shard_map/ppermute | solution.py:32
  76.9 4.4 %collective-permute-start.34 = (bf16[2,128,128]{2,1,0:T(8,128)(2,1)S(1)}, bf16[2,128,128]{2,1,0:T(8,128)(2,1)S(1)}, u32[]{:S(2)}, u32[]{:S(2)}) collective-permute-start(bf16[2,128,128]{2,1,0:T(8,128)(2,1)S(1)} %get-tuple-element.24), channel_id=1, source_target_pairs={{0,2},{4,6},{8,10},{12,14},{2,0},{6,4},{10,8},{14,12},{1,3},{5,7},... | collective-permute-start | bytes 196616 | tf_op jit(solution)/shard_map/ppermute | solution.py:32
  77.5 2.3 %collective-permute-start.21 = (f32[2,128,128]{2,1,0:T(8,128)S(1)}, f32[2,128,128]{2,1,0:T(8,128)S(1)}, u32[]{:S(2)}, u32[]{:S(2)}) collective-permute-start(f32[2,128,128]{2,1,0:T(8,128)S(1)} %get-tuple-element.39), channel_id=1, source_target_pairs={{0,4},{2,6},{1,5},{3,7},{16,20},{18,22},{17,21},{19,23}} | collective-permute-start | bytes 393224 | tf_op jit(solution)/shard_map/ppermute | solution.py:29
  78.3 7.0 %collective-permute-start.35 = (bf16[2,128,128]{2,1,0:T(8,128)(2,1)S(1)}, bf16[2,128,128]{2,1,0:T(8,128)(2,1)S(1)}, u32[]{:S(2)}, u32[]{:S(2)}) collective-permute-start(bf16[2,128,128]{2,1,0:T(8,128)(2,1)S(1)} %get-tuple-element.25), channel_id=1, source_target_pairs={{0,2},{4,6},{8,10},{12,14},{2,0},{6,4},{10,8},{14,12},{1,3},{5,7},... | collective-permute-start | bytes 196616 | tf_op jit(solution)/shard_map/ppermute | solution.py:32
  79.9 2.0 %collective-permute-start.25 = (f32[2,128,128]{2,1,0:T(8,128)S(1)}, f32[2,128,128]{2,1,0:T(8,128)S(1)}, u32[]{:S(2)}, u32[]{:S(2)}) collective-permute-start(f32[2,128,128]{2,1,0:T(8,128)S(1)} %get-tuple-element.38), channel_id=1, source_target_pairs={{0,4},{2,6},{1,5},{3,7},{16,20},{18,22},{17,21},{19,23}} | collective-permute-start | bytes 393224 | tf_op jit(solution)/shard_map/ppermute | solution.py:29
  80.6 2.0 %collective-permute-start.22 = (f32[2,128,128]{2,1,0:T(8,128)S(1)}, f32[2,128,128]{2,1,0:T(8,128)S(1)}, u32[]{:S(2)}, u32[]{:S(2)}) collective-permute-start(f32[2,128,128]{2,1,0:T(8,128)S(1)} %add.212), channel_id=1, source_target_pairs={{4,8},{6,10},{5,9},{7,11},{20,24},{22,26},{21,25},{23,27}} | collective-permute-start | bytes 393224 | tf_op jit(solution)/shard_map/ppermute | solution.py:29
  81.3 23.1 %collective-permute-start.39 = (bf16[2,128,128]{2,1,0:T(8,128)(2,1)S(1)}, bf16[2,128,128]{2,1,0:T(8,128)(2,1)S(1)}, u32[]{:S(2)}, u32[]{:S(2)}) collective-permute-start(bf16[2,128,128]{2,1,0:T(8,128)(2,1)S(1)} %get-tuple-element.21), channel_id=1, source_target_pairs={{0,2},{4,6},{8,10},{12,14},{2,0},{6,4},{10,8},{14,12},{1,3},{5,7},... | collective-permute-start | bytes 196616 | tf_op jit(solution)/shard_map/ppermute | solution.py:32
  81.9 2.0 %collective-permute-start.26 = (f32[2,128,128]{2,1,0:T(8,128)S(1)}, f32[2,128,128]{2,1,0:T(8,128)S(1)}, u32[]{:S(2)}, u32[]{:S(2)}) collective-permute-start(f32[2,128,128]{2,1,0:T(8,128)S(1)} %add.218), channel_id=1, source_target_pairs={{4,8},{6,10},{5,9},{7,11},{20,24},{22,26},{21,25},{23,27}} | collective-permute-start | bytes 393224 | tf_op jit(solution)/shard_map/ppermute | solution.py:29
  82.6 12.2 %collective-permute-start.23 = (f32[2,128,128]{2,1,0:T(8,128)S(1)}, f32[2,128,128]{2,1,0:T(8,128)S(1)}, u32[]{:S(2)}, u32[]{:S(2)}) collective-permute-start(f32[2,128,128]{2,1,0:T(8,128)S(1)} %get-tuple-element.9), channel_id=1, source_target_pairs={{8,12},{10,14},{9,13},{11,15},{24,28},{26,30},{25,29},{27,31}} | collective-permute-start | bytes 393224 | tf_op jit(solution)/shard_map/ppermute | solution.py:29
  84.0 14.7 %collective-permute-start.27 = (f32[2,128,128]{2,1,0:T(8,128)S(1)}, f32[2,128,128]{2,1,0:T(8,128)S(1)}, u32[]{:S(2)}, u32[]{:S(2)}) collective-permute-start(f32[2,128,128]{2,1,0:T(8,128)S(1)} %get-tuple-element.7), channel_id=1, source_target_pairs={{8,12},{10,14},{9,13},{11,15},{24,28},{26,30},{25,29},{27,31}} | collective-permute-start | bytes 393224 | tf_op jit(solution)/shard_map/ppermute | solution.py:29
  98.8 4.3 %collective-permute-start.37 = (bf16[2,128,128]{2,1,0:T(8,128)(2,1)S(1)}, bf16[2,128,128]{2,1,0:T(8,128)(2,1)S(1)}, u32[]{:S(2)}, u32[]{:S(2)}) collective-permute-start(bf16[2,128,128]{2,1,0:T(8,128)(2,1)S(1)} %get-tuple-element.37), channel_id=1, source_target_pairs={{0,2},{4,6},{8,10},{12,14},{2,0},{6,4},{10,8},{14,12},{1,3},{5,7},... | collective-permute-start | bytes 196616 | tf_op jit(solution)/shard_map/ppermute | solution.py:32
  100.2 4.3 %collective-permute-start.38 = (bf16[2,128,128]{2,1,0:T(8,128)(2,1)S(1)}, bf16[2,128,128]{2,1,0:T(8,128)(2,1)S(1)}, u32[]{:S(2)}, u32[]{:S(2)}) collective-permute-start(bf16[2,128,128]{2,1,0:T(8,128)(2,1)S(1)} %get-tuple-element.36), channel_id=1, source_target_pairs={{0,2},{4,6},{8,10},{12,14},{2,0},{6,4},{10,8},{14,12},{1,3},{5,7},... | collective-permute-start | bytes 196616 | tf_op jit(solution)/shard_map/ppermute | solution.py:32

commit v9 on v8

--- a/solution.py
+++ b/solution.py
@@ -8,30 +8,26 @@
 H = 32
 
 
-def pair_chain_prefix(terms, axis, pieces):
-    count = lax.axis_size(axis)
-    mine_at = lax.axis_index(axis) % 2
+def pair_chain_prefix(terms, pieces):
+    levels = lax.axis_size("ctx_hi")
+    mine_at = lax.axis_index("ctx_lo")
     first = mine_at == 0
     half = terms.shape[0] // 2
-    pairs = count // 2
     mine_all = lax.dynamic_slice_in_dim(terms, mine_at * half, half, 0)
-    other_all = lax.dynamic_slice_in_dim(terms, (1 - mine_at) * half, half, 0)
-    swap = [(2 * i, 2 * i + 1) for i in range(pairs)] + [(2 * i + 1, 2 * i) for i in range(pairs)]
+    total_all = lax.psum_scatter(terms, "ctx_lo", scatter_dimension=0, tiled=True)
     step = half // pieces
-    keeps, backs = [], []
+    keeps, sends = [], []
     for piece in range(pieces):
         mine = mine_all[piece * step:(piece + 1) * step]
-        got = lax.ppermute(other_all[piece * step:(piece + 1) * step], axis, swap)
-        total = mine + got
+        total = total_all[piece * step:(piece + 1) * step]
         carried = jnp.zeros_like(total)
-        for hop in range(1, pairs):
-            links = [(2 * (hop - 1) + side, 2 * hop + side) for side in range(2)]
-            carried = carried + lax.ppermute(carried + total, axis, links)
-        keeps.append((carried + jnp.where(first, 0.0, got)).astype(jnp.bfloat16))
-        send = (carried + jnp.where(first, mine, 0.0)).astype(jnp.bfloat16)
-        backs.append(lax.ppermute(send, axis, swap))
+        for hop in range(1, levels):
+            carried = carried + lax.ppermute(carried + total, "ctx_hi", [(hop - 1, hop)])
+        keeps.append((carried + jnp.where(first, 0.0, total - mine)).astype(jnp.bfloat16))
+        sends.append((carried + jnp.where(first, mine, 0.0)).astype(jnp.bfloat16))
     keep = jnp.concatenate(keeps, axis=0)
-    back = jnp.concatenate(backs, axis=0)
+    both = lax.all_gather(jnp.concatenate(sends, axis=0), "ctx_lo", axis=0, tiled=False)
+    back = lax.dynamic_index_in_dim(both, 1 - mine_at, 0, keepdims=False)
     low = jnp.where(first, keep, back)
     high = jnp.where(first, back, keep)
     return jnp.concatenate([low, high], axis=0)
@@ -120,17 +116,18 @@
     keyset = key_rows.reshape(seq_count * row_count, feat_count)
     valset = value_rows.reshape(seq_count * row_count, feat_count)
     state_terms = state_terms_of(keyset, valset, 8)
-    prefix_bf = pair_chain_prefix(state_terms, "ctx", 8)
+    prefix_bf = pair_chain_prefix(state_terms, 4)
     normed = attend_of(query, keyset, valset, prefix_bf, full_gain, 8)
     return normed.reshape(seq_count, row_count, feat_count)
 
 
 def solution(mesh):
-    in_specs = (
-        P(("groups", "dp"), "ctx", None),
-        P(("groups", "dp"), "ctx", None),
-        P(("groups", "dp"), "ctx", None),
-        P("dp"),
-    )
-    out_specs = P(("groups", "dp"), "ctx", None)
-    return jax.shard_map(shards, mesh=mesh, in_specs=in_specs, out_specs=out_specs, check_vma=False)
+    devices = mesh.devices
+    sizes = dict(zip(mesh.axis_names, devices.shape))
+    ctx_at = mesh.axis_names.index("ctx")
+    split = devices.shape[:ctx_at] + (sizes["ctx"] // 2, 2) + devices.shape[ctx_at + 1:]
+    names = mesh.axis_names[:ctx_at] + ("ctx_hi", "ctx_lo") + mesh.axis_names[ctx_at + 1:]
+    paired = jax.sharding.Mesh(devices.reshape(split), names)
+    rows = P(("groups", "dp"), ("ctx_hi", "ctx_lo"), None)
+    in_specs = (rows, rows, rows, P("dp"))
+    return jax.shard_map(shards, mesh=paired, in_specs=in_specs, out_specs=rows, check_vma=False)

time: 119 us -> 163 us (1.37); the launches traced: 118 us -> 160 us
  waiting for transfers between devices: 47.1 us -> 106 us
  starting transfers between devices: 35.6 us -> 10.7 us
  between operations: 0.59 us -> 13.6 us
  other arithmetic: 13 us -> 9.09 us
    reduce_scatter x0 -> x1, waiting for transfers between devices: none -> 31.9 us  [pair_chain_prefix(): lax.psum_scatter(terms, 'ctx_lo', scatter_dimension=0, tiled=True)]
    ppermute x40 -> x12, starting transfers between devices: 35.6 us -> 10.7 us  [pair_chain_prefix(): lax.ppermute(carried + total, 'ctx_hi', [(hop - 1, hop)])]
    all_gather x0 -> x1, waiting for transfers between devices: none -> 19.6 us  [pair_chain_prefix(): lax.all_gather(jnp.concatenate(sends, axis=0), 'ctx_lo', axis=0, tiled=Fa...]
    ppermute x40 -> x12, waiting for transfers between devices: 47.1 us -> 54 us  [pair_chain_prefix(): lax.ppermute(carried + total, 'ctx_hi', [(hop - 1, hop)])]
    unnamed x7 -> x0, other arithmetic: 3.84 us -> none
    add x20 -> x3, other arithmetic: 6.61 us -> 3.36 us  [pair_chain_prefix(): carried + total]
  transfers between devices with their start and end apart: 40 -> 14, of which waited for: 15 -> 6; matrix products, arithmetic and copies ran while one was open for 8% -> 1% of each run, Pallas kernels for 0% -> 0%
where the time goes in v9:
time: 163 us; the launch traced here: 160 us
  waiting for transfers between devices  106 us (65%)
  Pallas kernels  17.7 us (11%)
  between operations  13.6 us (8%)
  starting transfers between devices  10.7 us (7%)
  other arithmetic  9.09 us (6%)
  blocking collectives  1.95 us (1%)
    ppermute x12, waiting for transfers between devices, pair_chain_prefix(): lax.ppermute(carried + total, 'ctx_hi', [(hop - 1, hop)])  54 us
    reduce_scatter x1, waiting for transfers between devices, pair_chain_prefix(): lax.psum_scatter(terms, 'ctx_lo', scatter_dimension=0, tiled=True)  31.9 us
    all_gather x1, waiting for transfers between devices, pair_chain_prefix(): lax.all_gather(jnp.concatenate(sends, axis=0), 'ctx_lo', axis=0, tiled=Fa...  19.6 us
    pallas_call x1, Pallas kernels, attend_of(): pl.pallas_call(attend_kernel, grid=(steps,), in_specs=[pl.BlockSpec((row_...  12.3 us
    ppermute x12, starting transfers between devices, pair_chain_prefix(): lax.ppermute(carried + total, 'ctx_hi', [(hop - 1, hop)])  10.7 us
    pallas_call x1, Pallas kernels, state_terms_of(): pl.pallas_call(state_kernel, grid=(H // group,), in_specs=[pl.BlockSpec((...  5.36 us
    add x3, other arithmetic, pair_chain_prefix(): carried + total  3.36 us
  transfers between devices with their start and end apart: 14, of which 6 were waited for; matrix products, arithmetic and copies ran while one was open for 1% of the time, Pallas kernels for 0%

profile of v9, /device:TPU:30, one launch (start us, length us, event | category | flops | bytes accessed | tf_op | source)
XLA Modules:
  0.0 159.7 jit_solution(5952071607643483371)
XLA Ops:
  6.5 0.0 reduce-scatter.2.cloned.1.call-start
  6.5 5.4 %shard_map.46 = f32[32,128,128]{2,1,0:T(8,128)} custom-call(bf16[384,4096]{1,0:T(8,128)(2,1)} %bitcast.9, bf16[384,4096]{1,0:T(8,128)(2,1)} %bitcast.11), custom_call_target="tpu_custom_call" | custom-call | tf_op jit(solution)/shard_map/pallas_call | solution.py:49
  11.9 0.0 reduce-scatter.2.cloned.1.call-update
  11.9 0.0 all-gather.3.cloned.1.call-start
  12.0 31.9 %reduce-scatter.2.cloned.1.call-done = f32[16,128,128]{2,1,0:T(8,128)} async-done(((f32[32,128,128]{2,1,0:T(8,128)}), f32[16,128,128]{2,1,0:T(8,128)}) %reduce-scatter.2.cloned.1.call-update) | async-done | bytes 1048592 | tf_op jit(solution)/shard_map/reduce_scatter | solution.py:17
  43.9 0.0 copy-start
  43.9 1.1 slice.32
  45.0 0.7 collective-permute-start
  45.6 0.0 collective-permute-done
  45.7 1.3 slice_add_fusion.7
  46.9 0.7 collective-permute-start.3
  47.6 0.7 collective-permute-start.6
  48.3 0.7 collective-permute-start.9
  49.0 0.0 copy-start.1
  49.0 0.8 collective-permute-start.1
  49.8 0.0 collective-permute-done.3
  49.8 0.0 collective-permute-done.6
  49.9 0.0 collective-permute-done.9
  49.9 0.0 collective-permute-done.1
  49.9 0.0 copy-done
  49.9 0.9 slice_add_fusion.6
  50.7 0.7 collective-permute-start.10
  51.4 0.7 collective-permute-start.4
  52.1 0.7 collective-permute-start.7
  52.8 1.3 collective-permute-start.2
  54.1 0.0 collective-permute-done.10
  54.1 0.0 collective-permute-done.4
  54.1 0.0 collective-permute-done.7
  54.1 1.2 slice_add_fusion.4
  55.3 1.3 collective-permute-start.11
  56.6 1.3 collective-permute-start.5
  57.9 1.3 collective-permute-start.8
  59.2 19.9 %collective-permute-done.2 = f32[4,128,128]{2,1,0:T(8,128)} collective-permute-done((f32[4,128,128]{2,1,0:T(8,128)}, f32[4,128,128]{2,1,0:T(8,128)}, u32[]{:S(2)}, u32[]{:S(2)}) %collective-permute-start.2) | collective-permute-done | bytes 262176 | tf_op jit(solution)/shard_map/ppermute | solution.py:25
  79.1 26.3 %collective-permute-done.11 = f32[4,128,128]{2,1,0:T(8,128)} collective-permute-done((f32[4,128,128]{2,1,0:T(8,128)}, f32[4,128,128]{2,1,0:T(8,128)}, u32[]{:S(2)}, u32[]{:S(2)}) %collective-permute-start.11) | collective-permute-done | bytes 262176 | tf_op jit(solution)/shard_map/ppermute | solution.py:25
  105.4 5.1 %collective-permute-done.5 = f32[4,128,128]{2,1,0:T(8,128)} collective-permute-done((f32[4,128,128]{2,1,0:T(8,128)}, f32[4,128,128]{2,1,0:T(8,128)}, u32[]{:S(2)}, u32[]{:S(2)}) %collective-permute-start.5) | collective-permute-done | bytes 262176 | tf_op jit(solution)/shard_map/ppermute | solution.py:25
  110.5 2.8 %collective-permute-done.8 = f32[4,128,128]{2,1,0:T(8,128)} collective-permute-done((f32[4,128,128]{2,1,0:T(8,128)}, f32[4,128,128]{2,1,0:T(8,128)}, u32[]{:S(2)}, u32[]{:S(2)}) %collective-permute-start.8) | collective-permute-done | bytes 262176 | tf_op jit(solution)/shard_map/ppermute | solution.py:25
  113.3 0.0 copy-done.1
  113.3 0.0 copy-start.2
  113.3 2.5 %add_convert_fusion.7 = (bf16[4,128,128]{2,1,0:T(8,128)(2,1)S(1)}, bf16[4,128,128]{2,1,0:T(8,128)(2,1)}, bf16[4,128,128]{2,1,0:T(8,128)(2,1)}, bf16[4,128,128]{2...) fusion(f32[32,128,128]{2,1,0:T(8,128)S(1)} %copy-done.1, ...), kind=kLoop, calls=%fused_computation.12 | loop fusion | flops 2097152 | bytes 5242897 | tf_op jit(solution)/shard_map/convert_element_type | solution.py:26
  115.8 0.9 pad_maximum_fusion.2
  116.7 0.0 all-gather.3.cloned.1.call-update
  116.7 0.0 copy-done.2
  116.7 1.9 %all_gather.11 = f32[4096]{0:T(1024)} all-gather(f32[2048]{0:T(1024)S(1)} %copy-done.2), channel_id=1, replica_groups=mesh['groups'=2,'ctx_hi'=4,'ctx_lo'=2,'dp'=2] {'dp'}, dimensions={0}, use_global_device_ids=true | all-gather | bytes 24576 | tf_op jit(solution)/shard_map/all_gather | solution.py:114
  118.6 19.6 %all-gather.3.cloned.1.call-done = bf16[32,128,128]{2,1,0:T(8,128)(2,1)} async-done(((bf16[16,128,128]{2,1,0:T(8,128)(2,1)}), bf16[32,128,128]{2,1,0:T(8,128)(2,1)}) %all-gather.3.cloned.1.call-update) | async-done | bytes 1048592 | tf_op jit(solution)/shard_map/all_gather | solution.py:29
  138.2 1.2 bitcast_select_fusion.1
  139.4 1.1 pad_maximum_fusion.prefix_ref
  140.5 12.3 %shard_map.47 = bf16[384,4096]{1,0:T(8,128)(2,1)} custom-call(bf16[384,4096]{1,0:T(8,128)(2,1)} %bitcast.13, bf16[384,4096]{1,0:T(8,128)(2,1)} %bitcast.10, bf16[384,4096]{1,0:T(8,128)(2,1)} %bitcast.12, bf16[32,128,128]{2,1,0:T(8,128)(2,1)} %pad_maximum_fusion.prefix_ref, f32[1,4096]{1,0:T(1,128)} %bitcast.15), custom_call_target="tpu_custom_call" | custom-call | tf_op jit(solution)/shard_map/pallas_call | solution.py:97
Async XLA Ops:
  6.5 37.4 %reduce-scatter.2.cloned.1.call-start = ((), (), s32[]{:S(2)}) async-start(), calls=%async_computation.1 | async-start | bytes 3145728 | tf_op jit(solution)/shard_map/reduce_scatter | solution.py:17
  11.9 126.3 %all-gather.3.cloned.1.call-start = ((), (), s32[]{:S(2)}) async-start(), calls=%async_computation.2 | async-start | bytes 1572864 | tf_op jit(solution)/shard_map/all_gather | solution.py:29
  43.9 6.0 %copy-start = (f32[16,128,128]{2,1,0:T(8,128)S(1)}, f32[16,128,128]{2,1,0:T(8,128)}, u32[]{:S(2)}) copy-start(f32[16,128,128]{2,1,0:T(8,128)} %reduce-scatter.2.cloned.1.call-done) | copy-start | bytes 3145732
  45.0 0.7 collective-permute-start
  46.9 2.9 %collective-permute-start.3 = (f32[4,128,128]{2,1,0:T(8,128)S(1)}, f32[4,128,128]{2,1,0:T(8,128)S(1)}, u32[]{:S(2)}, u32[]{:S(2)}) collective-permute-start(f32[4,128,128]{2,1,0:T(8,128)S(1)} %get-tuple-element.29), channel_id=1, source_target_pairs={{0,4},{1,5},{2,6},{3,7},{16,20},{17,21},{18,22},{19,23}} | collective-permute-start | bytes 786440 | tf_op jit(solution)/shard_map/ppermute | solution.py:25
  47.6 2.2 %collective-permute-start.6 = (f32[4,128,128]{2,1,0:T(8,128)S(1)}, f32[4,128,128]{2,1,0:T(8,128)S(1)}, u32[]{:S(2)}, u32[]{:S(2)}) collective-permute-start(f32[4,128,128]{2,1,0:T(8,128)S(1)} %get-tuple-element.28), channel_id=1, source_target_pairs={{0,4},{1,5},{2,6},{3,7},{16,20},{17,21},{18,22},{19,23}} | collective-permute-start | bytes 786440 | tf_op jit(solution)/shard_map/ppermute | solution.py:25
  48.3 1.5 collective-permute-start.9
  49.0 64.3 %copy-start.1 = (f32[32,128,128]{2,1,0:T(8,128)S(1)}, f32[32,128,128]{2,1,0:T(8,128)}, u32[]{:S(2)}) copy-start(f32[32,128,128]{2,1,0:T(8,128)} %shard_map.46) | copy-start | bytes 6291460
  49.0 0.9 collective-permute-start.1
  50.7 3.3 %collective-permute-start.10 = (f32[4,128,128]{2,1,0:T(8,128)S(1)}, f32[4,128,128]{2,1,0:T(8,128)S(1)}, u32[]{:S(2)}, u32[]{:S(2)}) collective-permute-start(f32[4,128,128]{2,1,0:T(8,128)S(1)} %get-tuple-element.25), channel_id=1, source_target_pairs={{4,8},{5,9},{6,10},{7,11},{20,24},{21,25},{22,26},{23,27}} | collective-permute-start | bytes 786440 | tf_op jit(solution)/shard_map/ppermute | solution.py:25
  51.4 2.7 %collective-permute-start.4 = (f32[4,128,128]{2,1,0:T(8,128)S(1)}, f32[4,128,128]{2,1,0:T(8,128)S(1)}, u32[]{:S(2)}, u32[]{:S(2)}) collective-permute-start(f32[4,128,128]{2,1,0:T(8,128)S(1)} %get-tuple-element.23), channel_id=1, source_target_pairs={{4,8},{5,9},{6,10},{7,11},{20,24},{21,25},{22,26},{23,27}} | collective-permute-start | bytes 786440 | tf_op jit(solution)/shard_map/ppermute | solution.py:25
  52.1 2.0 %collective-permute-start.7 = (f32[4,128,128]{2,1,0:T(8,128)S(1)}, f32[4,128,128]{2,1,0:T(8,128)S(1)}, u32[]{:S(2)}, u32[]{:S(2)}) collective-permute-start(f32[4,128,128]{2,1,0:T(8,128)S(1)} %get-tuple-element.24), channel_id=1, source_target_pairs={{4,8},{5,9},{6,10},{7,11},{20,24},{21,25},{22,26},{23,27}} | collective-permute-start | bytes 786440 | tf_op jit(solution)/shard_map/ppermute | solution.py:25
  52.8 26.3 %collective-permute-start.2 = (f32[4,128,128]{2,1,0:T(8,128)}, f32[4,128,128]{2,1,0:T(8,128)}, u32[]{:S(2)}, u32[]{:S(2)}) collective-permute-start(f32[4,128,128]{2,1,0:T(8,128)} %get-tuple-element.5), channel_id=1, source_target_pairs={{8,12},{9,13},{10,14},{11,15},{24,28},{25,29},{26,30},{27,31}} | collective-permute-start | bytes 786440 | tf_op jit(solution)/shard_map/ppermute | solution.py:25
  55.3 50.1 %collective-permute-start.11 = (f32[4,128,128]{2,1,0:T(8,128)}, f32[4,128,128]{2,1,0:T(8,128)}, u32[]{:S(2)}, u32[]{:S(2)}) collective-permute-start(f32[4,128,128]{2,1,0:T(8,128)} %get-tuple-element.32), channel_id=1, source_target_pairs={{8,12},{9,13},{10,14},{11,15},{24,28},{25,29},{26,30},{27,31}} | collective-permute-start | bytes 786440 | tf_op jit(solution)/shard_map/ppermute | solution.py:25
  56.6 53.8 %collective-permute-start.5 = (f32[4,128,128]{2,1,0:T(8,128)}, f32[4,128,128]{2,1,0:T(8,128)}, u32[]{:S(2)}, u32[]{:S(2)}) collective-permute-start(f32[4,128,128]{2,1,0:T(8,128)} %get-tuple-element.7), channel_id=1, source_target_pairs={{8,12},{9,13},{10,14},{11,15},{24,28},{25,29},{26,30},{27,31}} | collective-permute-start | bytes 786440 | tf_op jit(solution)/shard_map/ppermute | solution.py:25
  57.9 55.3 %collective-permute-start.8 = (f32[4,128,128]{2,1,0:T(8,128)}, f32[4,128,128]{2,1,0:T(8,128)}, u32[]{:S(2)}, u32[]{:S(2)}) collective-permute-start(f32[4,128,128]{2,1,0:T(8,128)} %get-tuple-element.30), channel_id=1, source_target_pairs={{8,12},{9,13},{10,14},{11,15},{24,28},{25,29},{26,30},{27,31}} | collective-permute-start | bytes 786440 | tf_op jit(solution)/shard_map/ppermute | solution.py:25
  113.3 3.4 %copy-start.2 = (f32[2048]{0:T(1024)S(1)}, f32[2048]{0:T(1024)}, u32[]{:S(2)}) copy-start(f32[2048]{0:T(1024)} %param.7) | copy-start | bytes 24580
Sparse Core Ops, SparseCore 0:
  12.0 31.8 reduce-scatter.1
  116.8 21.3 all-gather.2

commit v10 on v3

--- a/solution.py
+++ b/solution.py
@@ -78,16 +78,17 @@
         scores = lax.dot_general(query, key_ref[:, cols], (((1,), (1,)), ((), ())),
                                  preferred_element_type=jnp.float32)
         weights = jnp.where(causal, scores, 0.0).astype(jnp.bfloat16)
-        within = jnp.dot(weights, val_ref[:, cols], preferred_element_type=jnp.float32)
-        carried = jnp.dot(query, prefix_ref[head], preferred_element_type=jnp.float32)
-        attended = within + carried
+        lhs = jnp.concatenate([weights, query], axis=1)
+        rhs = jnp.concatenate([val_ref[:, cols], prefix_ref[head]], axis=0)
+        attended = jnp.dot(lhs, rhs, preferred_element_type=jnp.float32)
         acc_ref[step, :, cols] = attended
-        sumsq = sumsq + jnp.sum(attended * attended, axis=1, keepdims=True)
+        sumsq = sumsq + attended * attended
     sumsq_ref[...] = sumsq
 
     @pl.when(step == pl.num_programs(0) - 1)
     def _():
-        scale = lax.rsqrt(sumsq / (width * pl.num_programs(0)) + 1e-05)
+        total = jnp.sum(sumsq, axis=1, keepdims=True)
+        scale = lax.rsqrt(total / (width * pl.num_programs(0)) + 1e-05)
         for part in range(acc_ref.shape[0]):
             cols = slice(part * width, (part + 1) * width)
             out_ref[:, cols] = (acc_ref[part] * scale * gain_ref[:, cols]).astype(out_ref.dtype)
@@ -109,17 +110,24 @@
         out_specs=pl.BlockSpec((row_count, feat_count), lambda g: (0, 0)),
         out_shape=jax.ShapeDtypeStruct((row_count, feat_count), jnp.bfloat16),
         scratch_shapes=[pltpu.VMEM((steps, row_count, width), jnp.float32),
-                        pltpu.VMEM((row_count, 1), jnp.float32)],
+                        pltpu.VMEM((row_count, head_size), jnp.float32)],
     )(query, keyset, valset, prefix_bf, full_gain)
 
 
 def shards(query_rows, key_rows, value_rows, gain):
     seq_count, row_count, feat_count = query_rows.shape
-    full_gain = lax.all_gather(gain, "dp", axis=0, tiled=True).reshape(1, feat_count)
+    pair = [(0, 1), (1, 0)] if lax.axis_size("dp") == 2 else None
+    if pair is None:
+        full_gain = lax.all_gather(gain, "dp", axis=0, tiled=True).reshape(1, feat_count)
+    else:
+        other_gain = lax.ppermute(gain, "dp", pair)
+        low_first = lax.axis_index("dp") == 0
+        full_gain = jnp.concatenate([jnp.where(low_first, gain, other_gain),
+                                     jnp.where(low_first, other_gain, gain)]).reshape(1, feat_count)
     query = query_rows.reshape(seq_count * row_count, feat_count)
     keyset = key_rows.reshape(seq_count * row_count, feat_count)
     valset = value_rows.reshape(seq_count * row_count, feat_count)
-    state_terms = state_terms_of(keyset, valset, 8)
+    state_terms = state_terms_of(keyset, valset, 16)
     prefix_bf = pair_chain_prefix(state_terms, "ctx", 4)
     normed = attend_of(query, keyset, valset, prefix_bf, full_gain, 8)
     return normed.reshape(seq_count, row_count, feat_count)

time: 100 us -> 96.1 us (0.961)
  blocking collectives: 1.93 us -> 0 us
  Pallas kernels: 17.6 us -> 16 us
  waiting for transfers between devices: 52.1 us -> 50.7 us
    all_gather x1 -> x0, blocking collectives: 1.93 us -> none  [shards(): lax.all_gather(gain, 'dp', axis=0, tiled=True).reshape(1, feat_count)]
    ppermute x4, waiting for transfers between devices: 6.27 us -> 5.1 us  [pair_chain_prefix(): backs.append(lax.ppermute(send, axis, swap))]
  transfers between devices with their start and end apart: 20 -> 21, of which waited for: 11 -> 12; matrix products, arithmetic and copies ran while one was open for 4% -> 6% of each run, Pallas kernels for 0% -> 0%
where the time goes in v10:
time: 96.1 us; the launch traced here: 95.5 us
  waiting for transfers between devices  50.7 us (53%)
  starting transfers between devices  17.9 us (19%)
  Pallas kernels  16 us (17%)
  other arithmetic  9.3 us (10%)
  local copies, waits for them, and re-layouts  1.19 us (1%)
    ppermute x4, waiting for transfers between devices, pair_chain_prefix(): got = lax.ppermute(other_all[piece * step:(piece + 1) * step], axis, swap)  22.9 us
    ppermute x12, waiting for transfers between devices, pair_chain_prefix(): carried = carried + lax.ppermute(carried + total, axis, links)  22.7 us
    pallas_call x1, Pallas kernels, attend_of(): pl.pallas_call(attend_kernel, grid=(steps,), in_specs=[pl.BlockSpec((row_...  11.6 us
    ppermute x12, starting transfers between devices, pair_chain_prefix(): carried = carried + lax.ppermute(carried + total, axis, links)  10.7 us
    ppermute x4, waiting for transfers between devices, pair_chain_prefix(): backs.append(lax.ppermute(send, axis, swap))  5.1 us
    pallas_call x1, Pallas kernels, state_terms_of(): pl.pallas_call(state_kernel, grid=(H // group,), in_specs=[pl.BlockSpec((...  4.45 us
    ppermute x4, starting transfers between devices, pair_chain_prefix(): backs.append(lax.ppermute(send, axis, swap))  4.12 us
    add x8, other arithmetic, pair_chain_prefix(): carried = carried + lax.ppermute(carried + total, axis, links)  3.44 us
  transfers between devices with their start and end apart: 21, of which 12 were waited for; matrix products, arithmetic and copies ran while one was open for 6% of the time, Pallas kernels for 0%

profile of v10, /device:TPU:30, one launch (start us, length us, event | category | flops | bytes accessed | tf_op | source)
XLA Modules:
  0.0 95.5 jit_solution(4752398052181320357)
XLA Ops:
  0.0 4.4 %shard_map.46 = f32[32,128,128]{2,1,0:T(8,128)} custom-call(bf16[384,4096]{1,0:T(8,128)(2,1)} %bitcast.5, bf16[384,4096]{1,0:T(8,128)(2,1)} %bitcast.7), custom_call_target="tpu_custom_call" | custom-call | tf_op jit(solution)/shard_map/pallas_call | solution.py:53
  4.5 1.1 %constant_dynamic-slice_fusion.3 = f32[4,128,128]{2,1,0:T(8,128)S(1)} fusion(f32[32,128,128]{2,1,0:T(8,128)} %shard_map.46, s32[]{:T(128)S(6)} %add.130), kind=kLoop, calls=%fused_computation.26 | loop fusion | bytes 524292 | tf_op jit(solution)/shard_map/slice | solution.py:24
  5.6 0.6 collective-permute-start.12
  6.1 7.5 %collective-permute-done.12 = f32[4,128,128]{2,1,0:T(8,128)S(1)} collective-permute-done((f32[4,128,128]{2,1,0:T(8,128)S(1)}, f32[4,128,128]{2,1,0:T(8,128)S(1)}, u32[]{:S(2)}, u32[]{:S(2)}) %collective-permute-start.12) | collective-permute-done | bytes 262176 | tf_op jit(solution)/shard_map/ppermute | solution.py:24
  13.7 2.2 %dynamic-slice_add_fusion = (f32[4,128,128]{2,1,0:T(8,128)S(1)}, f32[4,128,128]{2,1,0:T(8,128)S(1)}, f32[4,128,128]{2,1,0:T(8,128)}, f32[4,128,128]{2,1,0:T(8,128)}) fusion(f32[4,128,128]{2,1,0:T(8,128)S(1)} %collective-permute-done.12, f32[32,128,128]{2,1,0:T(8,128)} %shard_map.46, s32[]{:T(128)S(6)} %add.129, s32[]{:T(128)S(6)} %add.128, s32[]{:T(128)S(6)} %add.126, ...), kind=kLoop, calls=%fused_computation.12 | loop fusion | flops 65536 | bytes 2359312 | tf_op jit(solution)/shard_map/add | solution.py:25
  15.9 0.5 collective-permute-start
  16.4 1.5 %collective-permute-start.4 = (f32[4,128,128]{2,1,0:T(8,128)}, f32[4,128,128]{2,1,0:T(8,128)S(1)}, u32[]{:S(2)}, u32[]{:S(2)}) collective-permute-start(f32[4,128,128]{2,1,0:T(8,128)} %get-tuple-element.19), channel_id=1, source_target_pairs={{0,2},{4,6},{8,10},{12,14},{2,0},{6,4},{10,8},{14,12},{1,3},{5,7},... | collective-permute-start | bytes 786440 | tf_op jit(solution)/shard_map/ppermute | solution.py:24
  17.9 0.5 collective-permute-start.8
  18.4 0.7 collective-permute-start.13
  19.1 6.2 %collective-permute-done = f32[4,128,128]{2,1,0:T(8,128)S(1)} collective-permute-done((f32[4,128,128]{2,1,0:T(8,128)}, f32[4,128,128]{2,1,0:T(8,128)S(1)}, u32[]{:S(2)}, u32[]{:S(2)}) %collective-permute-start) | collective-permute-done | bytes 262176 | tf_op jit(solution)/shard_map/ppermute | solution.py:24
  25.3 5.6 %collective-permute-done.4 = f32[4,128,128]{2,1,0:T(8,128)S(1)} collective-permute-done((f32[4,128,128]{2,1,0:T(8,128)}, f32[4,128,128]{2,1,0:T(8,128)S(1)}, u32[]{:S(2)}, u32[]{:S(2)}) %collective-permute-start.4) | collective-permute-done | bytes 262176 | tf_op jit(solution)/shard_map/ppermute | solution.py:24
  30.9 3.5 %collective-permute-done.8 = f32[4,128,128]{2,1,0:T(8,128)S(1)} collective-permute-done((f32[4,128,128]{2,1,0:T(8,128)S(1)}, f32[4,128,128]{2,1,0:T(8,128)S(1)}, u32[]{:S(2)}, u32[]{:S(2)}) %collective-permute-start.8) | collective-permute-done | bytes 262176 | tf_op jit(solution)/shard_map/ppermute | solution.py:24
  34.5 0.1 dynamic-slice_add_fusion.1
  34.6 0.7 collective-permute-start.9
  35.2 0.7 collective-permute-start.5
  35.9 0.7 collective-permute-start.1
  36.7 0.7 collective-permute-start.14
  37.4 0.0 collective-permute-done.9
  37.4 0.7 collective-permute-start.10
  38.1 0.0 collective-permute-done.5
  38.1 0.7 collective-permute-start.6
  38.9 0.7 collective-permute-start.2
  39.6 0.8 fusion
  40.3 1.4 %collective-permute-start.15 = (f32[4,128,128]{2,1,0:T(8,128)}, f32[4,128,128]{2,1,0:T(8,128)}, u32[]{:S(2)}, u32[]{:S(2)}) collective-permute-start(f32[4,128,128]{2,1,0:T(8,128)} %get-tuple-element.5), channel_id=1, source_target_pairs={{8,12},{10,14},{9,13},{11,15},{24,28},{26,30},{25,29},{27,31}} | collective-permute-start | bytes 786440 | tf_op jit(solution)/shard_map/ppermute | solution.py:29
  41.8 0.8 fusion.1
  42.5 1.3 %collective-permute-start.11 = (f32[4,128,128]{2,1,0:T(8,128)}, f32[4,128,128]{2,1,0:T(8,128)}, u32[]{:S(2)}, u32[]{:S(2)}) collective-permute-start(f32[4,128,128]{2,1,0:T(8,128)} %get-tuple-element.7), channel_id=1, source_target_pairs={{8,12},{10,14},{9,13},{11,15},{24,28},{26,30},{25,29},{27,31}} | collective-permute-start | bytes 786440 | tf_op jit(solution)/shard_map/ppermute | solution.py:29
  43.8 0.9 fusion.2
  44.7 1.3 %collective-permute-start.7 = (f32[4,128,128]{2,1,0:T(8,128)}, f32[4,128,128]{2,1,0:T(8,128)}, u32[]{:S(2)}, u32[]{:S(2)}) collective-permute-start(f32[4,128,128]{2,1,0:T(8,128)} %get-tuple-element.9), channel_id=1, source_target_pairs={{8,12},{10,14},{9,13},{11,15},{24,28},{26,30},{25,29},{27,31}} | collective-permute-start | bytes 786440 | tf_op jit(solution)/shard_map/ppermute | solution.py:29
  46.0 0.9 fusion.3
  46.9 1.3 %collective-permute-start.3 = (f32[4,128,128]{2,1,0:T(8,128)}, f32[4,128,128]{2,1,0:T(8,128)}, u32[]{:S(2)}, u32[]{:S(2)}) collective-permute-start(f32[4,128,128]{2,1,0:T(8,128)} %get-tuple-element.11), channel_id=1, source_target_pairs={{8,12},{10,14},{9,13},{11,15},{24,28},{26,30},{25,29},{27,31}} | collective-permute-start | bytes 786440 | tf_op jit(solution)/shard_map/ppermute | solution.py:29
  48.2 0.1 collective-permute-start.20
  48.3 8.7 %collective-permute-done.15 = f32[4,128,128]{2,1,0:T(8,128)} collective-permute-done((f32[4,128,128]{2,1,0:T(8,128)}, f32[4,128,128]{2,1,0:T(8,128)}, u32[]{:S(2)}, u32[]{:S(2)}) %collective-permute-start.15) | collective-permute-done | bytes 262176 | tf_op jit(solution)/shard_map/ppermute | solution.py:29
  57.0 5.5 %collective-permute-done.11 = f32[4,128,128]{2,1,0:T(8,128)} collective-permute-done((f32[4,128,128]{2,1,0:T(8,128)}, f32[4,128,128]{2,1,0:T(8,128)}, u32[]{:S(2)}, u32[]{:S(2)}) %collective-permute-start.11) | collective-permute-done | bytes 262176 | tf_op jit(solution)/shard_map/ppermute | solution.py:29
  62.5 5.7 %collective-permute-done.7 = f32[4,128,128]{2,1,0:T(8,128)} collective-permute-done((f32[4,128,128]{2,1,0:T(8,128)}, f32[4,128,128]{2,1,0:T(8,128)}, u32[]{:S(2)}, u32[]{:S(2)}) %collective-permute-start.7) | collective-permute-done | bytes 262176 | tf_op jit(solution)/shard_map/ppermute | solution.py:29
  68.1 2.8 %collective-permute-done.3 = f32[4,128,128]{2,1,0:T(8,128)} collective-permute-done((f32[4,128,128]{2,1,0:T(8,128)}, f32[4,128,128]{2,1,0:T(8,128)}, u32[]{:S(2)}, u32[]{:S(2)}) %collective-permute-start.3) | collective-permute-done | bytes 262176 | tf_op jit(solution)/shard_map/ppermute | solution.py:29
  70.9 1.8 %add_convert_fusion = (bf16[4,128,128]{2,1,0:T(8,128)(2,1)S(1)}, bf16[4,128,128]{2,1,0:T(8,128)(2,1)S(1)}, bf16[4,128,128]{2,1,0:T(8,128)(2,1)S(1)}, bf16[4,128,...) fusion(f32[32,128,128]{2,1,0:T(8,128)S(1)} %copy-done, ...), kind=kLoop, calls=%fused_computation.4 | loop fusion | flops 1835008 | bytes 5242897 | tf_op jit(solution)/shard_map/convert_element_type | solution.py:31
  72.8 0.5 collective-permute-start.16
  73.3 1.6 %collective-permute-start.17 = (bf16[4,128,128]{2,1,0:T(8,128)(2,1)S(1)}, bf16[4,128,128]{2,1,0:T(8,128)(2,1)S(1)}, u32[]{:S(2)}, u32[]{:S(2)}) collective-permute-start(bf16[4,128,128]{2,1,0:T(8,128)(2,1)S(1)} %get-tuple-element.15), channel_id=1, source_target_pairs={{0,2},{4,6},{8,10},{12,14},{2,0},{6,4},{10,8},{14,12},{1,3},{5,7},... | collective-permute-start | bytes 393224 | tf_op jit(solution)/shard_map/ppermute | solution.py:32
  74.9 0.6 pad_maximum_fusion.2
  75.5 0.5 collective-permute-start.18
  75.9 1.6 %collective-permute-start.19 = (bf16[4,128,128]{2,1,0:T(8,128)(2,1)S(1)}, bf16[4,128,128]{2,1,0:T(8,128)(2,1)S(1)}, u32[]{:S(2)}, u32[]{:S(2)}) collective-permute-start(bf16[4,128,128]{2,1,0:T(8,128)(2,1)S(1)} %get-tuple-element.13), channel_id=1, source_target_pairs={{0,2},{4,6},{8,10},{12,14},{2,0},{6,4},{10,8},{14,12},{1,3},{5,7},... | collective-permute-start | bytes 393224 | tf_op jit(solution)/shard_map/ppermute | solution.py:32
  77.5 0.9 collective-permute-done.16
  78.5 1.4 %collective-permute-done.17 = bf16[4,128,128]{2,1,0:T(8,128)(2,1)S(1)} collective-permute-done((bf16[4,128,128]{2,1,0:T(8,128)(2,1)S(1)}, bf16[4,128,128]{2,1,0:T(8,128)(2,1)S(1)}, u32[]{:S(2)}, u32[]{:S(2)}) %collective-permute-start.17) | collective-permute-done | bytes 131104 | tf_op jit(solution)/shard_map/ppermute | solution.py:32
  79.9 1.4 %collective-permute-done.18 = bf16[4,128,128]{2,1,0:T(8,128)(2,1)S(1)} collective-permute-done((bf16[4,128,128]{2,1,0:T(8,128)(2,1)S(1)}, bf16[4,128,128]{2,1,0:T(8,128)(2,1)S(1)}, u32[]{:S(2)}, u32[]{:S(2)}) %collective-permute-start.18) | collective-permute-done | bytes 131104 | tf_op jit(solution)/shard_map/ppermute | solution.py:32
  81.3 1.4 %collective-permute-done.19 = bf16[4,128,128]{2,1,0:T(8,128)(2,1)S(1)} collective-permute-done((bf16[4,128,128]{2,1,0:T(8,128)(2,1)S(1)}, bf16[4,128,128]{2,1,0:T(8,128)(2,1)S(1)}, u32[]{:S(2)}, u32[]{:S(2)}) %collective-permute-start.19) | collective-permute-done | bytes 131104 | tf_op jit(solution)/shard_map/ppermute | solution.py:32
  82.7 0.1 broadcast_select_fusion.1
  82.8 1.1 %pad_maximum_fusion.prefix_ref = bf16[32,128,128]{2,1,0:T(8,128)(2,1)} fusion(bf16[16,128,128]{2,1,0:T(8,128)(2,1)S(1)} %get-tuple-element.25, bf16[16,128,128]{2,1,0:T(8,128)(2,1)S(1)} %get-tuple-element.24), kind=kLoop, calls=%fused_computation | loop fusion | flops 524288 | bytes 2097152 | tf_op jit(solution)/shard_map/concatenate | solution.py:37
  83.9 11.6 %shard_map.47 = bf16[384,4096]{1,0:T(8,128)(2,1)} custom-call(bf16[384,4096]{1,0:T(8,128)(2,1)} %bitcast.9, bf16[384,4096]{1,0:T(8,128)(2,1)} %bitcast.6, bf16[384,4096]{1,0:T(8,128)(2,1)} %bitcast.8, bf16[32,128,128]{2,1,0:T(8,128)(2,1)} %pad_maximum_fusion.prefix_ref, f32[1,4096]{1,0:T(1,128)} %bitcast.10), custom_call_target="tpu_custom_call" | custom-call | tf_op jit(solution)/shard_map/pallas_call | solution.py:102
  (22 shorter events, 0.3 us)
Async XLA Ops:
  4.4 30.0 %copy-start = (f32[32,128,128]{2,1,0:T(8,128)S(1)}, f32[32,128,128]{2,1,0:T(8,128)}, u32[]{:S(2)}) copy-start(f32[32,128,128]{2,1,0:T(8,128)} %shard_map.46) | copy-start | bytes 6291460
  5.6 8.1 %collective-permute-start.12 = (f32[4,128,128]{2,1,0:T(8,128)S(1)}, f32[4,128,128]{2,1,0:T(8,128)S(1)}, u32[]{:S(2)}, u32[]{:S(2)}) collective-permute-start(f32[4,128,128]{2,1,0:T(8,128)S(1)} %constant_dynamic-slice_fusion.3), channel_id=1, source_target_pairs={{0,2},{4,6},{8,10},{12,14},{2,0},{6,4},{10,8},{14,12},{1,3},{5,7},... | collective-permute-start | bytes 786440 | tf_op jit(solution)/shard_map/ppermute | solution.py:24
  13.7 2.2 %copy-start.1 = (f32[4,128,128]{2,1,0:T(8,128)}, f32[4,128,128]{2,1,0:T(8,128)S(1)}, u32[]{:S(2)}) copy-start(f32[4,128,128]{2,1,0:T(8,128)S(1)} %collective-permute-done.12) | copy-start | bytes 786436
  15.9 9.5 %collective-permute-start = (f32[4,128,128]{2,1,0:T(8,128)}, f32[4,128,128]{2,1,0:T(8,128)S(1)}, u32[]{:S(2)}, u32[]{:S(2)}) collective-permute-start(f32[4,128,128]{2,1,0:T(8,128)} %get-tuple-element.20), channel_id=1, source_target_pairs={{0,2},{4,6},{8,10},{12,14},{2,0},{6,4},{10,8},{14,12},{1,3},{5,7},... | collective-permute-start | bytes 786440 | tf_op jit(solution)/shard_map/ppermute | solution.py:24
  16.4 14.6 %collective-permute-start.4 = (f32[4,128,128]{2,1,0:T(8,128)}, f32[4,128,128]{2,1,0:T(8,128)S(1)}, u32[]{:S(2)}, u32[]{:S(2)}) collective-permute-start(f32[4,128,128]{2,1,0:T(8,128)} %get-tuple-element.19), channel_id=1, source_target_pairs={{0,2},{4,6},{8,10},{12,14},{2,0},{6,4},{10,8},{14,12},{1,3},{5,7},... | collective-permute-start | bytes 786440 | tf_op jit(solution)/shard_map/ppermute | solution.py:24
  17.9 16.6 %collective-permute-start.8 = (f32[4,128,128]{2,1,0:T(8,128)S(1)}, f32[4,128,128]{2,1,0:T(8,128)S(1)}, u32[]{:S(2)}, u32[]{:S(2)}) collective-permute-start(f32[4,128,128]{2,1,0:T(8,128)S(1)} %get-tuple-element.18), channel_id=1, source_target_pairs={{0,2},{4,6},{8,10},{12,14},{2,0},{6,4},{10,8},{14,12},{1,3},{5,7},... | collective-permute-start | bytes 786440 | tf_op jit(solution)/shard_map/ppermute | solution.py:24
  18.4 18.2 %collective-permute-start.13 = (f32[4,128,128]{2,1,0:T(8,128)S(1)}, f32[4,128,128]{2,1,0:T(8,128)S(1)}, u32[]{:S(2)}, u32[]{:S(2)}) collective-permute-start(f32[4,128,128]{2,1,0:T(8,128)S(1)} %get-tuple-element.17), channel_id=1, source_target_pairs={{0,4},{2,6},{1,5},{3,7},{16,20},{18,22},{17,21},{19,23}} | collective-permute-start | bytes 786440 | tf_op jit(solution)/shard_map/ppermute | solution.py:29
  34.6 2.8 %collective-permute-start.9 = (f32[4,128,128]{2,1,0:T(8,128)S(1)}, f32[4,128,128]{2,1,0:T(8,128)S(1)}, u32[]{:S(2)}, u32[]{:S(2)}) collective-permute-start(f32[4,128,128]{2,1,0:T(8,128)S(1)} %get-tuple-element.21), channel_id=1, source_target_pairs={{0,4},{2,6},{1,5},{3,7},{16,20},{18,22},{17,21},{19,23}} | collective-permute-start | bytes 786440 | tf_op jit(solution)/shard_map/ppermute | solution.py:29
  35.2 2.8 %collective-permute-start.5 = (f32[4,128,128]{2,1,0:T(8,128)S(1)}, f32[4,128,128]{2,1,0:T(8,128)S(1)}, u32[]{:S(2)}, u32[]{:S(2)}) collective-permute-start(f32[4,128,128]{2,1,0:T(8,128)S(1)} %get-tuple-element.22), channel_id=1, source_target_pairs={{0,4},{2,6},{1,5},{3,7},{16,20},{18,22},{17,21},{19,23}} | collective-permute-start | bytes 786440 | tf_op jit(solution)/shard_map/ppermute | solution.py:29
  35.9 2.9 %collective-permute-start.1 = (f32[4,128,128]{2,1,0:T(8,128)S(1)}, f32[4,128,128]{2,1,0:T(8,128)S(1)}, u32[]{:S(2)}, u32[]{:S(2)}) collective-permute-start(f32[4,128,128]{2,1,0:T(8,128)S(1)} %get-tuple-element.23), channel_id=1, source_target_pairs={{0,4},{2,6},{1,5},{3,7},{16,20},{18,22},{17,21},{19,23}} | collective-permute-start | bytes 786440 | tf_op jit(solution)/shard_map/ppermute | solution.py:29
  36.7 2.9 %collective-permute-start.14 = (f32[4,128,128]{2,1,0:T(8,128)S(1)}, f32[4,128,128]{2,1,0:T(8,128)S(1)}, u32[]{:S(2)}, u32[]{:S(2)}) collective-permute-start(f32[4,128,128]{2,1,0:T(8,128)S(1)} %add.116), channel_id=1, source_target_pairs={{4,8},{6,10},{5,9},{7,11},{20,24},{22,26},{21,25},{23,27}} | collective-permute-start | bytes 786440 | tf_op jit(solution)/shard_map/ppermute | solution.py:29
  37.4 4.3 %collective-permute-start.10 = (f32[4,128,128]{2,1,0:T(8,128)S(1)}, f32[4,128,128]{2,1,0:T(8,128)S(1)}, u32[]{:S(2)}, u32[]{:S(2)}) collective-permute-start(f32[4,128,128]{2,1,0:T(8,128)S(1)} %add.110), channel_id=1, source_target_pairs={{4,8},{6,10},{5,9},{7,11},{20,24},{22,26},{21,25},{23,27}} | collective-permute-start | bytes 786440 | tf_op jit(solution)/shard_map/ppermute | solution.py:29
  38.1 5.7 %collective-permute-start.6 = (f32[4,128,128]{2,1,0:T(8,128)S(1)}, f32[4,128,128]{2,1,0:T(8,128)S(1)}, u32[]{:S(2)}, u32[]{:S(2)}) collective-permute-start(f32[4,128,128]{2,1,0:T(8,128)S(1)} %add.104), channel_id=1, source_target_pairs={{4,8},{6,10},{5,9},{7,11},{20,24},{22,26},{21,25},{23,27}} | collective-permute-start | bytes 786440 | tf_op jit(solution)/shard_map/ppermute | solution.py:29
  38.9 7.1 %collective-permute-start.2 = (f32[4,128,128]{2,1,0:T(8,128)S(1)}, f32[4,128,128]{2,1,0:T(8,128)S(1)}, u32[]{:S(2)}, u32[]{:S(2)}) collective-permute-start(f32[4,128,128]{2,1,0:T(8,128)S(1)} %add.98), channel_id=1, source_target_pairs={{4,8},{6,10},{5,9},{7,11},{20,24},{22,26},{21,25},{23,27}} | collective-permute-start | bytes 786440 | tf_op jit(solution)/shard_map/ppermute | solution.py:29
  40.3 7.8 %copy-start.2 = (f32[2048]{0:T(1024)S(1)}, f32[2048]{0:T(1024)}, u32[]{:S(2)}) copy-start(f32[2048]{0:T(1024)} %param.7) | copy-start | bytes 24580
  40.3 16.6 %collective-permute-start.15 = (f32[4,128,128]{2,1,0:T(8,128)}, f32[4,128,128]{2,1,0:T(8,128)}, u32[]{:S(2)}, u32[]{:S(2)}) collective-permute-start(f32[4,128,128]{2,1,0:T(8,128)} %get-tuple-element.5), channel_id=1, source_target_pairs={{8,12},{10,14},{9,13},{11,15},{24,28},{26,30},{25,29},{27,31}} | collective-permute-start | bytes 786440 | tf_op jit(solution)/shard_map/ppermute | solution.py:29
  42.5 19.9 %collective-permute-start.11 = (f32[4,128,128]{2,1,0:T(8,128)}, f32[4,128,128]{2,1,0:T(8,128)}, u32[]{:S(2)}, u32[]{:S(2)}) collective-permute-start(f32[4,128,128]{2,1,0:T(8,128)} %get-tuple-element.7), channel_id=1, source_target_pairs={{8,12},{10,14},{9,13},{11,15},{24,28},{26,30},{25,29},{27,31}} | collective-permute-start | bytes 786440 | tf_op jit(solution)/shard_map/ppermute | solution.py:29
  44.7 23.4 %collective-permute-start.7 = (f32[4,128,128]{2,1,0:T(8,128)}, f32[4,128,128]{2,1,0:T(8,128)}, u32[]{:S(2)}, u32[]{:S(2)}) collective-permute-start(f32[4,128,128]{2,1,0:T(8,128)} %get-tuple-element.9), channel_id=1, source_target_pairs={{8,12},{10,14},{9,13},{11,15},{24,28},{26,30},{25,29},{27,31}} | collective-permute-start | bytes 786440 | tf_op jit(solution)/shard_map/ppermute | solution.py:29
  46.9 24.1 %collective-permute-start.3 = (f32[4,128,128]{2,1,0:T(8,128)}, f32[4,128,128]{2,1,0:T(8,128)}, u32[]{:S(2)}, u32[]{:S(2)}) collective-permute-start(f32[4,128,128]{2,1,0:T(8,128)} %get-tuple-element.11), channel_id=1, source_target_pairs={{8,12},{10,14},{9,13},{11,15},{24,28},{26,30},{25,29},{27,31}} | collective-permute-start | bytes 786440 | tf_op jit(solution)/shard_map/ppermute | solution.py:29
  48.2 25.1 %collective-permute-start.20 = (f32[2048]{0:T(1024)S(1)}, f32[2048]{0:T(1024)S(1)}, u32[]{:S(2)}, u32[]{:S(2)}) collective-permute-start(f32[2048]{0:T(1024)S(1)} %copy-done.2), channel_id=1, source_target_pairs={{0,1},{1,0},{2,3},{3,2},{4,5},{5,4},{6,7},{7,6},{8,9},{9,8},{10,11... | collective-permute-start | bytes 24584 | tf_op jit(solution)/shard_map/ppermute | solution.py:123
  72.8 5.7 %collective-permute-start.16 = (bf16[4,128,128]{2,1,0:T(8,128)(2,1)S(1)}, bf16[4,128,128]{2,1,0:T(8,128)(2,1)S(1)}, u32[]{:S(2)}, u32[]{:S(2)}) collective-permute-start(bf16[4,128,128]{2,1,0:T(8,128)(2,1)S(1)} %get-tuple-element.14), channel_id=1, source_target_pairs={{0,2},{4,6},{8,10},{12,14},{2,0},{6,4},{10,8},{14,12},{1,3},{5,7},... | collective-permute-start | bytes 393224 | tf_op jit(solution)/shard_map/ppermute | solution.py:32
  73.3 6.5 %collective-permute-start.17 = (bf16[4,128,128]{2,1,0:T(8,128)(2,1)S(1)}, bf16[4,128,128]{2,1,0:T(8,128)(2,1)S(1)}, u32[]{:S(2)}, u32[]{:S(2)}) collective-permute-start(bf16[4,128,128]{2,1,0:T(8,128)(2,1)S(1)} %get-tuple-element.15), channel_id=1, source_target_pairs={{0,2},{4,6},{8,10},{12,14},{2,0},{6,4},{10,8},{14,12},{1,3},{5,7},... | collective-permute-start | bytes 393224 | tf_op jit(solution)/shard_map/ppermute | solution.py:32
  75.5 5.8 %collective-permute-start.18 = (bf16[4,128,128]{2,1,0:T(8,128)(2,1)S(1)}, bf16[4,128,128]{2,1,0:T(8,128)(2,1)S(1)}, u32[]{:S(2)}, u32[]{:S(2)}) collective-permute-start(bf16[4,128,128]{2,1,0:T(8,128)(2,1)S(1)} %get-tuple-element.16), channel_id=1, source_target_pairs={{0,2},{4,6},{8,10},{12,14},{2,0},{6,4},{10,8},{14,12},{1,3},{5,7},... | collective-permute-start | bytes 393224 | tf_op jit(solution)/shard_map/ppermute | solution.py:32
  75.9 6.7 %collective-permute-start.19 = (bf16[4,128,128]{2,1,0:T(8,128)(2,1)S(1)}, bf16[4,128,128]{2,1,0:T(8,128)(2,1)S(1)}, u32[]{:S(2)}, u32[]{:S(2)}) collective-permute-start(bf16[4,128,128]{2,1,0:T(8,128)(2,1)S(1)} %get-tuple-element.13), channel_id=1, source_target_pairs={{0,2},{4,6},{8,10},{12,14},{2,0},{6,4},{10,8},{14,12},{1,3},{5,7},... | collective-permute-start | bytes 393224 | tf_op jit(solution)/shard_map/ppermute | solution.py:32

commit v11 on v10

--- a/solution.py
+++ b/solution.py
@@ -26,7 +26,10 @@
         carried = jnp.zeros_like(total)
         for hop in range(1, pairs):
             links = [(2 * (hop - 1) + side, 2 * hop + side) for side in range(2)]
-            carried = carried + lax.ppermute(carried + total, axis, links)
+            came = lax.ppermute(carried + total, axis, links)
+            if hop == pairs - 1 and backs:
+                came, _ = lax.optimization_barrier((came, backs[-1]))
+            carried = carried + came
         keeps.append((carried + jnp.where(first, 0.0, got)).astype(jnp.bfloat16))
         send = (carried + jnp.where(first, mine, 0.0)).astype(jnp.bfloat16)
         backs.append(lax.ppermute(send, axis, swap))

time: 96.1 us -> 112 us (1.17)
  waiting for transfers between devices: 50.7 us -> 67.3 us
  starting transfers between devices: 17.9 us -> 16.5 us
    ppermute x12, waiting for transfers between devices: 22.7 us -> 34.6 us  [pair_chain_prefix(): came = lax.ppermute(carried + total, axis, links)]
    ppermute x4, waiting for transfers between devices: 5.1 us -> 14.4 us  [pair_chain_prefix(): backs.append(lax.ppermute(send, axis, swap))]
    ppermute x4, waiting for transfers between devices: 22.9 us -> 18.3 us  [pair_chain_prefix(): got = lax.ppermute(other_all[piece * step:(piece + 1) * step], axis, swap)]
    convert_element_type x1 -> x2, other arithmetic: 1.82 us -> 0.15 us  [pair_chain_prefix(): keeps.append((carried + jnp.where(first, 0.0, got)).astype(jnp.bfloat16))]
    add x2 -> x4, other arithmetic: 2.27 us -> 3.78 us  [pair_chain_prefix(): total = mine + got]
    ppermute x4, starting transfers between devices: 4.12 us -> 2.96 us  [pair_chain_prefix(): backs.append(lax.ppermute(send, axis, swap))]
  transfers between devices with their start and end apart: 21 -> 21, of which waited for: 12 -> 10; matrix products, arithmetic and copies ran while one was open for 6% -> 4% of each run, Pallas kernels for 0% -> 0%
where the time goes in v11:
time: 112 us; the launch traced here: 111 us
  waiting for transfers between devices  67.3 us (60%)
  starting transfers between devices  16.5 us (15%)
  Pallas kernels  16 us (14%)
  other arithmetic  9.1 us (8%)
  local copies, waits for them, and re-layouts  2.22 us (2%)
    ppermute x12, waiting for transfers between devices, pair_chain_prefix(): came = lax.ppermute(carried + total, axis, links)  34.6 us
    ppermute x4, waiting for transfers between devices, pair_chain_prefix(): got = lax.ppermute(other_all[piece * step:(piece + 1) * step], axis, swap)  18.3 us
    ppermute x4, waiting for transfers between devices, pair_chain_prefix(): backs.append(lax.ppermute(send, axis, swap))  14.4 us
    pallas_call x1, Pallas kernels, attend_of(): pl.pallas_call(attend_kernel, grid=(steps,), in_specs=[pl.BlockSpec((row_...  11.5 us
    ppermute x12, starting transfers between devices, pair_chain_prefix(): came = lax.ppermute(carried + total, axis, links)  11.5 us
    pallas_call x1, Pallas kernels, state_terms_of(): pl.pallas_call(state_kernel, grid=(H // group,), in_specs=[pl.BlockSpec((...  4.45 us
    add x4, other arithmetic, pair_chain_prefix(): total = mine + got  3.78 us
    add x8, other arithmetic, pair_chain_prefix(): came = lax.ppermute(carried + total, axis, links)  3.39 us
  transfers between devices with their start and end apart: 21, of which 10 were waited for; matrix products, arithmetic and copies ran while one was open for 4% of the time, Pallas kernels for 0%

profile of v11, /device:TPU:30, one launch (start us, length us, event | category | flops | bytes accessed | tf_op | source)
XLA Modules:
  0.0 111.4 jit_solution(1051115150685173442)
XLA Ops:
  0.0 4.4 %shard_map.46 = f32[32,128,128]{2,1,0:T(8,128)} custom-call(bf16[384,4096]{1,0:T(8,128)(2,1)} %bitcast.5, bf16[384,4096]{1,0:T(8,128)(2,1)} %bitcast.7), custom_call_target="tpu_custom_call" | custom-call | tf_op jit(solution)/shard_map/pallas_call | solution.py:56
  4.5 1.2 %constant_dynamic-slice_fusion.3 = (f32[4,128,128]{2,1,0:T(8,128)S(1)}, f32[4,128,128]{2,1,0:T(8,128)S(1)}) fusion(f32[32,128,128]{2,1,0:T(8,128)} %shard_map.46, s32[]{:T(128)S(6)} %add.130, s32[]{:T(128)S(6)} %select_n.78), kind=kLoop, calls=%fused_computation.26 | loop fusion | bytes 1048584 | tf_op jit(solution)/shard_map/slice | solution.py:24
  5.7 0.6 collective-permute-start
  6.2 7.5 %collective-permute-done = f32[4,128,128]{2,1,0:T(8,128)S(1)} collective-permute-done((f32[4,128,128]{2,1,0:T(8,128)S(1)}, f32[4,128,128]{2,1,0:T(8,128)S(1)}, u32[]{:S(2)}, u32[]{:S(2)}) %collective-permute-start) | collective-permute-done | bytes 262176 | tf_op jit(solution)/shard_map/ppermute | solution.py:24
  13.8 1.0 dynamic-slice_add_fusion.3
  14.8 0.7 collective-permute-start.1
  15.5 0.7 collective-permute-start.2
  16.2 0.6 collective-permute-start.14
  16.7 0.7 fusion.3
  17.5 1.3 %collective-permute-start.3 = (f32[4,128,128]{2,1,0:T(8,128)}, f32[4,128,128]{2,1,0:T(8,128)S(1)}, u32[]{:S(2)}, u32[]{:S(2)}) collective-permute-start(f32[4,128,128]{2,1,0:T(8,128)} %get-tuple-element.17), channel_id=1, source_target_pairs={{8,12},{10,14},{9,13},{11,15},{24,28},{26,30},{25,29},{27,31}} | collective-permute-start | bytes 786440 | tf_op jit(solution)/shard_map/ppermute | solution.py:29
  18.8 4.6 %collective-permute-done.14 = f32[4,128,128]{2,1,0:T(8,128)S(1)} collective-permute-done((f32[4,128,128]{2,1,0:T(8,128)S(1)}, f32[4,128,128]{2,1,0:T(8,128)S(1)}, u32[]{:S(2)}, u32[]{:S(2)}) %collective-permute-start.14) | collective-permute-done | bytes 262176 | tf_op jit(solution)/shard_map/ppermute | solution.py:24
  23.4 13.7 %collective-permute-done.3 = f32[4,128,128]{2,1,0:T(8,128)S(1)} collective-permute-done((f32[4,128,128]{2,1,0:T(8,128)}, f32[4,128,128]{2,1,0:T(8,128)S(1)}, u32[]{:S(2)}, u32[]{:S(2)}) %collective-permute-start.3) | collective-permute-done | bytes 262176 | tf_op jit(solution)/shard_map/ppermute | solution.py:29
  37.1 0.9 dynamic-slice_add_fusion
  38.0 0.5 collective-permute-start.4
  38.5 6.1 %collective-permute-done.4 = f32[4,128,128]{2,1,0:T(8,128)S(1)} collective-permute-done((f32[4,128,128]{2,1,0:T(8,128)}, f32[4,128,128]{2,1,0:T(8,128)S(1)}, u32[]{:S(2)}, u32[]{:S(2)}) %collective-permute-start.4) | collective-permute-done | bytes 262176 | tf_op jit(solution)/shard_map/ppermute | solution.py:24
  44.6 0.7 collective-permute-start.5
  45.4 0.7 collective-permute-start.6
  46.1 0.8 fusion.2
  46.8 1.3 %collective-permute-start.7 = (f32[4,128,128]{2,1,0:T(8,128)}, f32[4,128,128]{2,1,0:T(8,128)}, u32[]{:S(2)}, u32[]{:S(2)}) collective-permute-start(f32[4,128,128]{2,1,0:T(8,128)} %get-tuple-element.15), channel_id=1, source_target_pairs={{8,12},{10,14},{9,13},{11,15},{24,28},{26,30},{25,29},{27,31}} | collective-permute-start | bytes 786440 | tf_op jit(solution)/shard_map/ppermute | solution.py:29
  48.1 0.5 collective-permute-start.9
  48.7 1.6 %collective-permute-start.8 = (bf16[4,128,128]{2,1,0:T(8,128)(2,1)}, bf16[4,128,128]{2,1,0:T(8,128)(2,1)}, u32[]{:S(2)}, u32[]{:S(2)}) collective-permute-start(bf16[4,128,128]{2,1,0:T(8,128)(2,1)} %get-tuple-element.20), channel_id=1, source_target_pairs={{0,2},{4,6},{8,10},{12,14},{2,0},{6,4},{10,8},{14,12},{1,3},{5,7},... | collective-permute-start | bytes 393224 | tf_op jit(solution)/shard_map/ppermute | solution.py:35
  50.2 5.9 %collective-permute-done.8 = bf16[4,128,128]{2,1,0:T(8,128)(2,1)} collective-permute-done((bf16[4,128,128]{2,1,0:T(8,128)(2,1)}, bf16[4,128,128]{2,1,0:T(8,128)(2,1)}, u32[]{:S(2)}, u32[]{:S(2)}) %collective-permute-start.8) | collective-permute-done | bytes 131104 | tf_op jit(solution)/shard_map/ppermute | solution.py:35
  56.1 4.6 %collective-permute-done.7 = f32[4,128,128]{2,1,0:T(8,128)} collective-permute-done((f32[4,128,128]{2,1,0:T(8,128)}, f32[4,128,128]{2,1,0:T(8,128)}, u32[]{:S(2)}, u32[]{:S(2)}) %collective-permute-start.7) | collective-permute-done | bytes 262176 | tf_op jit(solution)/shard_map/ppermute | solution.py:29
  60.7 1.9 %dynamic-slice_add_fusion.1 = (f32[4,128,128]{2,1,0:T(8,128)S(1)}, bf16[4,128,128]{2,1,0:T(8,128)(2,1)}, bf16[4,128,128]{2,1,0:T(8,128)(2,1)}) fusion(f32[4,128,128]{2,1,0:T(8,128)S(1)} %collective-permute-done.9, f32[32,128,128]{2,1,0:T(8,128)S(1)} %copy-done, s32[]{:T(128)S(6)} %add.127, s32[]{:T(128)S(6)} %add.125, pred[]{:T(512)S(6)} %eq.8, ...), kind=kLoop, calls=%fused_computation.13 | loop fusion | flops 524288 | bytes 2097161 | tf_op jit(solution)/shard_map/add | solution.py:25
  62.6 0.7 collective-permute-start.10
  63.2 0.7 collective-permute-start.15
  63.9 0.7 add.111
  64.7 1.4 %collective-permute-start.11 = (f32[4,128,128]{2,1,0:T(8,128)}, f32[4,128,128]{2,1,0:T(8,128)}, u32[]{:S(2)}, u32[]{:S(2)}) collective-permute-start(f32[4,128,128]{2,1,0:T(8,128)} %add.111), channel_id=1, source_target_pairs={{4,8},{6,10},{5,9},{7,11},{20,24},{22,26},{21,25},{23,27}} | collective-permute-start | bytes 786440 | tf_op jit(solution)/shard_map/ppermute | solution.py:29
  66.1 0.8 collective-permute-start.16
  66.9 1.0 fusion.1
  67.9 1.3 %collective-permute-start.12 = (f32[4,128,128]{2,1,0:T(8,128)S(1)}, f32[4,128,128]{2,1,0:T(8,128)S(1)}, u32[]{:S(2)}, u32[]{:S(2)}) collective-permute-start(f32[4,128,128]{2,1,0:T(8,128)S(1)} %get-tuple-element.13), channel_id=1, source_target_pairs={{8,12},{10,14},{9,13},{11,15},{24,28},{26,30},{25,29},{27,31}} | collective-permute-start | bytes 786440 | tf_op jit(solution)/shard_map/ppermute | solution.py:29
  69.2 0.5 collective-permute-start.13
  69.7 0.1 fusion
  69.8 1.4 %collective-permute-start.17 = (f32[4,128,128]{2,1,0:T(8,128)S(1)}, f32[4,128,128]{2,1,0:T(8,128)S(1)}, u32[]{:S(2)}, u32[]{:S(2)}) collective-permute-start(f32[4,128,128]{2,1,0:T(8,128)S(1)} %get-tuple-element.11), channel_id=1, source_target_pairs={{8,12},{10,14},{9,13},{11,15},{24,28},{26,30},{25,29},{27,31}} | collective-permute-start | bytes 786440 | tf_op jit(solution)/shard_map/ppermute | solution.py:29
  71.2 4.0 %collective-permute-done.13 = bf16[4,128,128]{2,1,0:T(8,128)(2,1)S(1)} collective-permute-done((bf16[4,128,128]{2,1,0:T(8,128)(2,1)S(1)}, bf16[4,128,128]{2,1,0:T(8,128)(2,1)S(1)}, u32[]{:S(2)}, u32[]{:S(2)}) %collective-permute-start.13) | collective-permute-done | bytes 131104 | tf_op jit(solution)/shard_map/ppermute | solution.py:35
  75.2 13.3 %collective-permute-done.12 = f32[4,128,128]{2,1,0:T(8,128)S(1)} collective-permute-done((f32[4,128,128]{2,1,0:T(8,128)S(1)}, f32[4,128,128]{2,1,0:T(8,128)S(1)}, u32[]{:S(2)}, u32[]{:S(2)}) %collective-permute-start.12) | collective-permute-done | bytes 262176 | tf_op jit(solution)/shard_map/ppermute | solution.py:29
  88.5 0.1 add_convert_fusion.3
  88.5 0.5 collective-permute-start.18
  89.0 0.6 pad_maximum_fusion.2
  89.6 0.9 constant_dynamic-update-slice_fusion.3
  90.5 3.0 %collective-permute-done.17 = f32[4,128,128]{2,1,0:T(8,128)S(1)} collective-permute-done((f32[4,128,128]{2,1,0:T(8,128)S(1)}, f32[4,128,128]{2,1,0:T(8,128)S(1)}, u32[]{:S(2)}, u32[]{:S(2)}) %collective-permute-start.17) | collective-permute-done | bytes 262176 | tf_op jit(solution)/shard_map/ppermute | solution.py:29
  93.6 0.0 collective-permute-done.18
  93.6 0.1 add_convert_fusion.1
  93.7 0.5 collective-permute-start.19
  94.2 4.5 %collective-permute-done.19 = bf16[4,128,128]{2,1,0:T(8,128)(2,1)S(1)} collective-permute-done((bf16[4,128,128]{2,1,0:T(8,128)(2,1)S(1)}, bf16[4,128,128]{2,1,0:T(8,128)(2,1)S(1)}, u32[]{:S(2)}, u32[]{:S(2)}) %collective-permute-start.19) | collective-permute-done | bytes 131104 | tf_op jit(solution)/shard_map/ppermute | solution.py:35
  98.7 0.1 broadcast_select_fusion.1
  98.8 1.1 pad_maximum_fusion.prefix_ref
  99.9 11.5 %shard_map.47 = bf16[384,4096]{1,0:T(8,128)(2,1)} custom-call(bf16[384,4096]{1,0:T(8,128)(2,1)} %bitcast.9, bf16[384,4096]{1,0:T(8,128)(2,1)} %bitcast.6, bf16[384,4096]{1,0:T(8,128)(2,1)} %bitcast.8, bf16[32,128,128]{2,1,0:T(8,128)(2,1)} %pad_maximum_fusion.prefix_ref, f32[1,4096]{1,0:T(1,128)} %bitcast.10), custom_call_target="tpu_custom_call" | custom-call | tf_op jit(solution)/shard_map/pallas_call | solution.py:105
  (35 shorter events, 0.3 us)
Async XLA Ops:
  4.4 32.7 %copy-start = (f32[32,128,128]{2,1,0:T(8,128)S(1)}, f32[32,128,128]{2,1,0:T(8,128)}, u32[]{:S(2)}) copy-start(f32[32,128,128]{2,1,0:T(8,128)} %shard_map.46) | copy-start | bytes 6291460
  5.7 8.1 %collective-permute-start = (f32[4,128,128]{2,1,0:T(8,128)S(1)}, f32[4,128,128]{2,1,0:T(8,128)S(1)}, u32[]{:S(2)}, u32[]{:S(2)}) collective-permute-start(f32[4,128,128]{2,1,0:T(8,128)S(1)} %get-tuple-element.24), channel_id=1, source_target_pairs={{0,2},{4,6},{8,10},{12,14},{2,0},{6,4},{10,8},{14,12},{1,3},{5,7},... | collective-permute-start | bytes 786440 | tf_op jit(solution)/shard_map/ppermute | solution.py:24
  14.8 0.7 collective-permute-start.1
  15.5 1.3 %collective-permute-start.2 = (f32[4,128,128]{2,1,0:T(8,128)S(1)}, f32[4,128,128]{2,1,0:T(8,128)S(1)}, u32[]{:S(2)}, u32[]{:S(2)}) collective-permute-start(f32[4,128,128]{2,1,0:T(8,128)S(1)} %add.98), channel_id=1, source_target_pairs={{4,8},{6,10},{5,9},{7,11},{20,24},{22,26},{21,25},{23,27}} | collective-permute-start | bytes 786440 | tf_op jit(solution)/shard_map/ppermute | solution.py:29
  16.2 7.2 %collective-permute-start.14 = (f32[4,128,128]{2,1,0:T(8,128)S(1)}, f32[4,128,128]{2,1,0:T(8,128)S(1)}, u32[]{:S(2)}, u32[]{:S(2)}) collective-permute-start(f32[4,128,128]{2,1,0:T(8,128)S(1)} %get-tuple-element.23), channel_id=1, source_target_pairs={{0,2},{4,6},{8,10},{12,14},{2,0},{6,4},{10,8},{14,12},{1,3},{5,7},... | collective-permute-start | bytes 786440 | tf_op jit(solution)/shard_map/ppermute | solution.py:24
  17.5 19.6 %collective-permute-start.3 = (f32[4,128,128]{2,1,0:T(8,128)}, f32[4,128,128]{2,1,0:T(8,128)S(1)}, u32[]{:S(2)}, u32[]{:S(2)}) collective-permute-start(f32[4,128,128]{2,1,0:T(8,128)} %get-tuple-element.17), channel_id=1, source_target_pairs={{8,12},{10,14},{9,13},{11,15},{24,28},{26,30},{25,29},{27,31}} | collective-permute-start | bytes 786440 | tf_op jit(solution)/shard_map/ppermute | solution.py:29
  38.0 10.1 %copy-start.5 = (f32[4,128,128]{2,1,0:T(8,128)S(1)}, f32[4,128,128]{2,1,0:T(8,128)}, u32[]{:S(2)}) copy-start(f32[4,128,128]{2,1,0:T(8,128)} %get-tuple-element.21) | copy-start | bytes 786436
  38.0 6.6 %collective-permute-start.4 = (f32[4,128,128]{2,1,0:T(8,128)}, f32[4,128,128]{2,1,0:T(8,128)S(1)}, u32[]{:S(2)}, u32[]{:S(2)}) collective-permute-start(f32[4,128,128]{2,1,0:T(8,128)} %get-tuple-element.22), channel_id=1, source_target_pairs={{0,2},{4,6},{8,10},{12,14},{2,0},{6,4},{10,8},{14,12},{1,3},{5,7},... | collective-permute-start | bytes 786440 | tf_op jit(solution)/shard_map/ppermute | solution.py:24
  44.6 1.5 %copy-start.3 = (f32[4,128,128]{2,1,0:T(8,128)}, f32[4,128,128]{2,1,0:T(8,128)S(1)}, u32[]{:S(2)}) copy-start(f32[4,128,128]{2,1,0:T(8,128)S(1)} %collective-permute-done.4) | copy-start | bytes 786436
  44.6 0.7 collective-permute-start.5
  45.4 20.7 %copy-start.7 = (f32[2048]{0:T(1024)S(1)}, f32[2048]{0:T(1024)}, u32[]{:S(2)}) copy-start(f32[2048]{0:T(1024)} %param.7) | copy-start | bytes 24580
  45.4 0.7 collective-permute-start.6
  46.8 13.8 %collective-permute-start.7 = (f32[4,128,128]{2,1,0:T(8,128)}, f32[4,128,128]{2,1,0:T(8,128)}, u32[]{:S(2)}, u32[]{:S(2)}) collective-permute-start(f32[4,128,128]{2,1,0:T(8,128)} %get-tuple-element.15), channel_id=1, source_target_pairs={{8,12},{10,14},{9,13},{11,15},{24,28},{26,30},{25,29},{27,31}} | collective-permute-start | bytes 786440 | tf_op jit(solution)/shard_map/ppermute | solution.py:29
  48.1 12.5 %collective-permute-start.9 = (f32[4,128,128]{2,1,0:T(8,128)S(1)}, f32[4,128,128]{2,1,0:T(8,128)S(1)}, u32[]{:S(2)}, u32[]{:S(2)}) collective-permute-start(f32[4,128,128]{2,1,0:T(8,128)S(1)} %copy-done.5), channel_id=1, source_target_pairs={{0,2},{4,6},{8,10},{12,14},{2,0},{6,4},{10,8},{14,12},{1,3},{5,7},... | collective-permute-start | bytes 786440 | tf_op jit(solution)/shard_map/ppermute | solution.py:24
  48.7 7.4 %collective-permute-start.8 = (bf16[4,128,128]{2,1,0:T(8,128)(2,1)}, bf16[4,128,128]{2,1,0:T(8,128)(2,1)}, u32[]{:S(2)}, u32[]{:S(2)}) collective-permute-start(bf16[4,128,128]{2,1,0:T(8,128)(2,1)} %get-tuple-element.20), channel_id=1, source_target_pairs={{0,2},{4,6},{8,10},{12,14},{2,0},{6,4},{10,8},{14,12},{1,3},{5,7},... | collective-permute-start | bytes 393224 | tf_op jit(solution)/shard_map/ppermute | solution.py:35
  60.6 1.9 %copy-start.1 = (f32[4,128,128]{2,1,0:T(8,128)}, f32[4,128,128]{2,1,0:T(8,128)S(1)}, u32[]{:S(2)}) copy-start(f32[4,128,128]{2,1,0:T(8,128)S(1)} %collective-permute-done.9) | copy-start | bytes 786436
  62.6 1.4 %collective-permute-start.10 = (f32[4,128,128]{2,1,0:T(8,128)S(1)}, f32[4,128,128]{2,1,0:T(8,128)S(1)}, u32[]{:S(2)}, u32[]{:S(2)}) collective-permute-start(f32[4,128,128]{2,1,0:T(8,128)S(1)} %get-tuple-element.25), channel_id=1, source_target_pairs={{0,4},{2,6},{1,5},{3,7},{16,20},{18,22},{17,21},{19,23}} | collective-permute-start | bytes 786440 | tf_op jit(solution)/shard_map/ppermute | solution.py:29
  63.2 2.8 %collective-permute-start.15 = (f32[4,128,128]{2,1,0:T(8,128)S(1)}, f32[4,128,128]{2,1,0:T(8,128)S(1)}, u32[]{:S(2)}, u32[]{:S(2)}) collective-permute-start(f32[4,128,128]{2,1,0:T(8,128)S(1)} %get-tuple-element.19), channel_id=1, source_target_pairs={{0,4},{2,6},{1,5},{3,7},{16,20},{18,22},{17,21},{19,23}} | collective-permute-start | bytes 786440 | tf_op jit(solution)/shard_map/ppermute | solution.py:29
  64.7 2.2 %collective-permute-start.11 = (f32[4,128,128]{2,1,0:T(8,128)}, f32[4,128,128]{2,1,0:T(8,128)}, u32[]{:S(2)}, u32[]{:S(2)}) collective-permute-start(f32[4,128,128]{2,1,0:T(8,128)} %add.111), channel_id=1, source_target_pairs={{4,8},{6,10},{5,9},{7,11},{20,24},{22,26},{21,25},{23,27}} | collective-permute-start | bytes 786440 | tf_op jit(solution)/shard_map/ppermute | solution.py:29
  66.0 3.2 %collective-permute-start.20 = (f32[2048]{0:T(1024)S(1)}, f32[2048]{0:T(1024)S(1)}, u32[]{:S(2)}, u32[]{:S(2)}) collective-permute-start(f32[2048]{0:T(1024)S(1)} %copy-done.7), channel_id=1, source_target_pairs={{0,1},{1,0},{2,3},{3,2},{4,5},{5,4},{6,7},{7,6},{8,9},{9,8},{10,11... | collective-permute-start | bytes 24584 | tf_op jit(solution)/shard_map/ppermute | solution.py:126
  66.0 3.2 %copy-start.6 = (bf16[4,128,128]{2,1,0:T(8,128)(2,1)S(1)}, bf16[4,128,128]{2,1,0:T(8,128)(2,1)}, u32[]{:S(2)}) copy-start(bf16[4,128,128]{2,1,0:T(8,128)(2,1)} %get-tuple-element.26) | copy-start | bytes 393220
  66.0 22.4 %copy-start.2 = (f32[4,128,128]{2,1,0:T(8,128)S(1)}, f32[4,128,128]{2,1,0:T(8,128)}, u32[]{:S(2)}) copy-start(f32[4,128,128]{2,1,0:T(8,128)} %copy-done.1) | copy-start | bytes 786436
  66.1 3.6 %collective-permute-start.16 = (f32[4,128,128]{2,1,0:T(8,128)S(1)}, f32[4,128,128]{2,1,0:T(8,128)S(1)}, u32[]{:S(2)}, u32[]{:S(2)}) collective-permute-start(f32[4,128,128]{2,1,0:T(8,128)S(1)} %add.118), channel_id=1, source_target_pairs={{4,8},{6,10},{5,9},{7,11},{20,24},{22,26},{21,25},{23,27}} | collective-permute-start | bytes 786440 | tf_op jit(solution)/shard_map/ppermute | solution.py:29
  67.9 20.6 %collective-permute-start.12 = (f32[4,128,128]{2,1,0:T(8,128)S(1)}, f32[4,128,128]{2,1,0:T(8,128)S(1)}, u32[]{:S(2)}, u32[]{:S(2)}) collective-permute-start(f32[4,128,128]{2,1,0:T(8,128)S(1)} %get-tuple-element.13), channel_id=1, source_target_pairs={{8,12},{10,14},{9,13},{11,15},{24,28},{26,30},{25,29},{27,31}} | collective-permute-start | bytes 786440 | tf_op jit(solution)/shard_map/ppermute | solution.py:29
  69.2 6.0 %collective-permute-start.13 = (bf16[4,128,128]{2,1,0:T(8,128)(2,1)S(1)}, bf16[4,128,128]{2,1,0:T(8,128)(2,1)S(1)}, u32[]{:S(2)}, u32[]{:S(2)}) collective-permute-start(bf16[4,128,128]{2,1,0:T(8,128)(2,1)S(1)} %copy-done.6), channel_id=1, source_target_pairs={{0,2},{4,6},{8,10},{12,14},{2,0},{6,4},{10,8},{14,12},{1,3},{5,7},... | collective-permute-start | bytes 393224 | tf_op jit(solution)/shard_map/ppermute | solution.py:35
  69.8 28.9 %copy-start.4 = (bf16[4,128,128]{2,1,0:T(8,128)(2,1)S(1)}, bf16[4,128,128]{2,1,0:T(8,128)(2,1)}, u32[]{:S(2)}) copy-start(bf16[4,128,128]{2,1,0:T(8,128)(2,1)} %get-tuple-element.29) | copy-start | bytes 393220
  69.8 23.8 %collective-permute-start.17 = (f32[4,128,128]{2,1,0:T(8,128)S(1)}, f32[4,128,128]{2,1,0:T(8,128)S(1)}, u32[]{:S(2)}, u32[]{:S(2)}) collective-permute-start(f32[4,128,128]{2,1,0:T(8,128)S(1)} %get-tuple-element.11), channel_id=1, source_target_pairs={{8,12},{10,14},{9,13},{11,15},{24,28},{26,30},{25,29},{27,31}} | collective-permute-start | bytes 786440 | tf_op jit(solution)/shard_map/ppermute | solution.py:29
  88.5 5.0 %collective-permute-start.18 = (bf16[4,128,128]{2,1,0:T(8,128)(2,1)S(1)}, bf16[4,128,128]{2,1,0:T(8,128)(2,1)S(1)}, u32[]{:S(2)}, u32[]{:S(2)}) collective-permute-start(bf16[4,128,128]{2,1,0:T(8,128)(2,1)S(1)} %get-tuple-element.32), channel_id=1, source_target_pairs={{0,2},{4,6},{8,10},{12,14},{2,0},{6,4},{10,8},{14,12},{1,3},{5,7},... | collective-permute-start | bytes 393224 | tf_op jit(solution)/shard_map/ppermute | solution.py:35
  93.7 5.0 %collective-permute-start.19 = (bf16[4,128,128]{2,1,0:T(8,128)(2,1)S(1)}, bf16[4,128,128]{2,1,0:T(8,128)(2,1)S(1)}, u32[]{:S(2)}, u32[]{:S(2)}) collective-permute-start(bf16[4,128,128]{2,1,0:T(8,128)(2,1)S(1)} %get-tuple-element.34), channel_id=1, source_target_pairs={{0,2},{4,6},{8,10},{12,14},{2,0},{6,4},{10,8},{14,12},{1,3},{5,7},... | collective-permute-start | bytes 393224 | tf_op jit(solution)/shard_map/ppermute | solution.py:35

commit v12 on v10

--- a/solution.py
+++ b/solution.py
@@ -17,11 +17,12 @@
     mine_all = lax.dynamic_slice_in_dim(terms, mine_at * half, half, 0)
     other_all = lax.dynamic_slice_in_dim(terms, (1 - mine_at) * half, half, 0)
     swap = [(2 * i, 2 * i + 1) for i in range(pairs)] + [(2 * i + 1, 2 * i) for i in range(pairs)]
+    got_all = lax.ppermute(other_all, axis, swap)
     step = half // pieces
     keeps, backs = [], []
     for piece in range(pieces):
         mine = mine_all[piece * step:(piece + 1) * step]
-        got = lax.ppermute(other_all[piece * step:(piece + 1) * step], axis, swap)
+        got = got_all[piece * step:(piece + 1) * step]
         total = mine + got
         carried = jnp.zeros_like(total)
         for hop in range(1, pairs):

time: 96.1 us -> 103 us (1.072)
  waiting for transfers between devices: 50.7 us -> 60.8 us
  starting transfers between devices: 17.9 us -> 15.4 us
    ppermute x12, waiting for transfers between devices: 22.7 us -> 29.1 us  [pair_chain_prefix(): carried = carried + lax.ppermute(carried + total, axis, links)]
    ppermute x4 -> x1, starting transfers between devices: 3.09 us -> 0.56 us  [pair_chain_prefix(): got_all = lax.ppermute(other_all, axis, swap)]
    ppermute x4, waiting for transfers between devices: 5.1 us -> 7.3 us  [pair_chain_prefix(): backs.append(lax.ppermute(send, axis, swap))]
    ppermute x4 -> x1, waiting for transfers between devices: 22.9 us -> 24.4 us  [pair_chain_prefix(): got_all = lax.ppermute(other_all, axis, swap)]
    dynamic_slice x0 -> x1, local copies, waits for them, and re-layouts: none -> 1.29 us  [pair_chain_prefix(): other_all = lax.dynamic_slice_in_dim(terms, (1 - mine_at) * half, half, 0)]
    slice x1 -> x0, local copies, waits for them, and re-layouts: 1.12 us -> none  [pair_chain_prefix(): got = lax.ppermute(other_all[piece * step:(piece + 1) * step], axis, swap)]
    add x2 -> x1, other arithmetic: 2.27 us -> 1.3 us  [pair_chain_prefix(): total = mine + got]
  transfers between devices with their start and end apart: 21 -> 18, of which waited for: 12 -> 9; matrix products, arithmetic and copies ran while one was open for 6% -> 6% of each run, Pallas kernels for 0% -> 0%
where the time goes in v12:
time: 103 us; the launch traced here: 102 us
  waiting for transfers between devices  60.8 us (59%)
  Pallas kernels  15.9 us (15%)
  starting transfers between devices  15.4 us (15%)
  other arithmetic  8.46 us (8%)
  local copies, waits for them, and re-layouts  1.37 us (1%)
    ppermute x12, waiting for transfers between devices, pair_chain_prefix(): carried = carried + lax.ppermute(carried + total, axis, links)  29.1 us
    ppermute x1, waiting for transfers between devices, pair_chain_prefix(): got_all = lax.ppermute(other_all, axis, swap)  24.4 us
    pallas_call x1, Pallas kernels, attend_of(): pl.pallas_call(attend_kernel, grid=(steps,), in_specs=[pl.BlockSpec((row_...  11.5 us
    ppermute x12, starting transfers between devices, pair_chain_prefix(): carried = carried + lax.ppermute(carried + total, axis, links)  10.7 us
    ppermute x4, waiting for transfers between devices, pair_chain_prefix(): backs.append(lax.ppermute(send, axis, swap))  7.3 us
    pallas_call x1, Pallas kernels, state_terms_of(): pl.pallas_call(state_kernel, grid=(H // group,), in_specs=[pl.BlockSpec((...  4.45 us
    ppermute x4, starting transfers between devices, pair_chain_prefix(): backs.append(lax.ppermute(send, axis, swap))  4.12 us
    add x8, other arithmetic, pair_chain_prefix(): carried = carried + lax.ppermute(carried + total, axis, links)  3.51 us
  transfers between devices with their start and end apart: 18, of which 9 were waited for; matrix products, arithmetic and copies ran while one was open for 6% of the time, Pallas kernels for 0%

profile of v12, /device:TPU:30, one launch (start us, length us, event | category | flops | bytes accessed | tf_op | source)
XLA Modules:
  0.0 102.2 jit_solution(2257641941655534212)
XLA Ops:
  0.0 4.4 %shard_map.46 = f32[32,128,128]{2,1,0:T(8,128)} custom-call(bf16[384,4096]{1,0:T(8,128)(2,1)} %bitcast.5, bf16[384,4096]{1,0:T(8,128)(2,1)} %bitcast.7), custom_call_target="tpu_custom_call" | custom-call | tf_op jit(solution)/shard_map/pallas_call | solution.py:54
  4.4 1.3 %constant_dynamic-slice_fusion = f32[16,128,128]{2,1,0:T(8,128)S(1)} fusion(f32[32,128,128]{2,1,0:T(8,128)} %shard_map.46, s32[]{:T(128)S(6)} %select_n.78), kind=kLoop, calls=%fused_computation.23 | loop fusion | bytes 2097156 | tf_op jit(solution)/shard_map/dynamic_slice | solution.py:18
  5.7 0.6 collective-permute-start
  6.3 24.4 %collective-permute-done = f32[16,128,128]{2,1,0:T(8,128)S(1)} collective-permute-done((f32[16,128,128]{2,1,0:T(8,128)S(1)}, f32[16,128,128]{2,1,0:T(8,128)S(1)}, u32[]{:S(2)}, u32[]{:S(2)}) %collective-permute-start) | collective-permute-done | bytes 1048608 | tf_op jit(solution)/shard_map/ppermute | solution.py:20
  30.7 1.3 %slice_add_fusion = (f32[4,128,128]{2,1,0:T(8,128)S(1)}, f32[4,128,128]{2,1,0:T(8,128)S(1)}, f32[4,128,128]{2,1,0:T(8,128)S(1)}, f32[4,128,128]{2,1,0:T(8,128)S(1)}) fusion(f32[16,128,128]{2,1,0:T(8,128)S(1)} %collective-permute-done, f32[32,128,128]{2,1,0:T(8,128)} %shard_map.46, s32[]{:T(128)S(6)} %add.127, s32[]{:T(128)S(6)} %add.126, s32[]{:T(128)S(6)} %add.125, ...), kind=kLoop, calls=%fused_computation.12 | loop fusion | flops 262144 | bytes 3145744 | tf_op jit(solution)/shard_map/add | solution.py:26
  32.0 0.7 collective-permute-start.10
  32.7 0.7 collective-permute-start.7
  33.4 0.7 collective-permute-start.4
  34.1 0.7 collective-permute-start.1
  34.8 0.0 collective-permute-done.10
  34.8 0.7 collective-permute-start.11
  35.5 0.7 collective-permute-start.8
  36.2 0.0 collective-permute-done.4
  36.3 0.0 copy-start.1
  36.3 0.0 copy-start
  36.3 0.8 collective-permute-start.5
  37.2 0.7 collective-permute-start.2
  37.9 0.0 collective-permute-done.11
  37.9 0.8 fusion
  38.6 1.3 %collective-permute-start.12 = (f32[4,128,128]{2,1,0:T(8,128)}, f32[4,128,128]{2,1,0:T(8,128)}, u32[]{:S(2)}, u32[]{:S(2)}) collective-permute-start(f32[4,128,128]{2,1,0:T(8,128)} %get-tuple-element.5), channel_id=1, source_target_pairs={{8,12},{10,14},{9,13},{11,15},{24,28},{26,30},{25,29},{27,31}} | collective-permute-start | bytes 786440 | tf_op jit(solution)/shard_map/ppermute | solution.py:30
  39.9 0.0 collective-permute-done.8
  39.9 0.8 fusion.1
  40.8 1.3 %collective-permute-start.9 = (f32[4,128,128]{2,1,0:T(8,128)}, f32[4,128,128]{2,1,0:T(8,128)}, u32[]{:S(2)}, u32[]{:S(2)}) collective-permute-start(f32[4,128,128]{2,1,0:T(8,128)} %get-tuple-element.7), channel_id=1, source_target_pairs={{8,12},{10,14},{9,13},{11,15},{24,28},{26,30},{25,29},{27,31}} | collective-permute-start | bytes 786440 | tf_op jit(solution)/shard_map/ppermute | solution.py:30
  42.1 0.0 collective-permute-done.5
  42.1 0.9 fusion.2
  42.9 1.3 %collective-permute-start.6 = (f32[4,128,128]{2,1,0:T(8,128)}, f32[4,128,128]{2,1,0:T(8,128)}, u32[]{:S(2)}, u32[]{:S(2)}) collective-permute-start(f32[4,128,128]{2,1,0:T(8,128)} %get-tuple-element.9), channel_id=1, source_target_pairs={{8,12},{10,14},{9,13},{11,15},{24,28},{26,30},{25,29},{27,31}} | collective-permute-start | bytes 786440 | tf_op jit(solution)/shard_map/ppermute | solution.py:30
  44.2 0.0 collective-permute-done.2
  44.2 0.9 fusion.3
  45.1 1.3 %collective-permute-start.3 = (f32[4,128,128]{2,1,0:T(8,128)}, f32[4,128,128]{2,1,0:T(8,128)}, u32[]{:S(2)}, u32[]{:S(2)}) collective-permute-start(f32[4,128,128]{2,1,0:T(8,128)} %get-tuple-element.11), channel_id=1, source_target_pairs={{8,12},{10,14},{9,13},{11,15},{24,28},{26,30},{25,29},{27,31}} | collective-permute-start | bytes 786440 | tf_op jit(solution)/shard_map/ppermute | solution.py:30
  46.4 0.1 collective-permute-start.17
  46.5 14.5 %collective-permute-done.12 = f32[4,128,128]{2,1,0:T(8,128)} collective-permute-done((f32[4,128,128]{2,1,0:T(8,128)}, f32[4,128,128]{2,1,0:T(8,128)}, u32[]{:S(2)}, u32[]{:S(2)}) %collective-permute-start.12) | collective-permute-done | bytes 262176 | tf_op jit(solution)/shard_map/ppermute | solution.py:30
  61.0 5.6 %collective-permute-done.9 = f32[4,128,128]{2,1,0:T(8,128)} collective-permute-done((f32[4,128,128]{2,1,0:T(8,128)}, f32[4,128,128]{2,1,0:T(8,128)}, u32[]{:S(2)}, u32[]{:S(2)}) %collective-permute-start.9) | collective-permute-done | bytes 262176 | tf_op jit(solution)/shard_map/ppermute | solution.py:30
  66.6 5.3 %collective-permute-done.6 = f32[4,128,128]{2,1,0:T(8,128)} collective-permute-done((f32[4,128,128]{2,1,0:T(8,128)}, f32[4,128,128]{2,1,0:T(8,128)}, u32[]{:S(2)}, u32[]{:S(2)}) %collective-permute-start.6) | collective-permute-done | bytes 262176 | tf_op jit(solution)/shard_map/ppermute | solution.py:30
  71.9 3.7 %collective-permute-done.3 = f32[4,128,128]{2,1,0:T(8,128)} collective-permute-done((f32[4,128,128]{2,1,0:T(8,128)}, f32[4,128,128]{2,1,0:T(8,128)}, u32[]{:S(2)}, u32[]{:S(2)}) %collective-permute-start.3) | collective-permute-done | bytes 262176 | tf_op jit(solution)/shard_map/ppermute | solution.py:30
  75.6 1.8 %add_convert_fusion.7 = (bf16[4,128,128]{2,1,0:T(8,128)(2,1)S(1)}, bf16[4,128,128]{2,1,0:T(8,128)(2,1)S(1)}, bf16[4,128,128]{2,1,0:T(8,128)(2,1)S(1)}, bf16[4,12...) fusion(f32[16,128,128]{2,1,0:T(8,128)S(1)} %collective-permute-, ...), kind=kLoop, calls=%fused_computation.11 | loop fusion | flops 1835008 | bytes 5242897 | tf_op jit(solution)/shard_map/convert_element_type | solution.py:31
  77.4 0.6 collective-permute-start.13
  78.0 0.0 collective-permute-done.17
  78.0 1.5 %collective-permute-start.14 = (bf16[4,128,128]{2,1,0:T(8,128)(2,1)S(1)}, bf16[4,128,128]{2,1,0:T(8,128)(2,1)S(1)}, u32[]{:S(2)}, u32[]{:S(2)}) collective-permute-start(bf16[4,128,128]{2,1,0:T(8,128)(2,1)S(1)} %get-tuple-element.28), channel_id=1, source_target_pairs={{0,2},{4,6},{8,10},{12,14},{2,0},{6,4},{10,8},{14,12},{1,3},{5,7},... | collective-permute-start | bytes 393224 | tf_op jit(solution)/shard_map/ppermute | solution.py:33
  79.5 0.6 pad_maximum_fusion.2
  80.1 0.5 collective-permute-start.15
  80.7 1.5 %collective-permute-start.16 = (bf16[4,128,128]{2,1,0:T(8,128)(2,1)S(1)}, bf16[4,128,128]{2,1,0:T(8,128)(2,1)S(1)}, u32[]{:S(2)}, u32[]{:S(2)}) collective-permute-start(bf16[4,128,128]{2,1,0:T(8,128)(2,1)S(1)} %get-tuple-element.30), channel_id=1, source_target_pairs={{0,2},{4,6},{8,10},{12,14},{2,0},{6,4},{10,8},{14,12},{1,3},{5,7},... | collective-permute-start | bytes 393224 | tf_op jit(solution)/shard_map/ppermute | solution.py:33
  82.2 1.8 %collective-permute-done.13 = bf16[4,128,128]{2,1,0:T(8,128)(2,1)S(1)} collective-permute-done((bf16[4,128,128]{2,1,0:T(8,128)(2,1)S(1)}, bf16[4,128,128]{2,1,0:T(8,128)(2,1)S(1)}, u32[]{:S(2)}, u32[]{:S(2)}) %collective-permute-start.13) | collective-permute-done | bytes 131104 | tf_op jit(solution)/shard_map/ppermute | solution.py:33
  83.9 2.8 %collective-permute-done.14 = bf16[4,128,128]{2,1,0:T(8,128)(2,1)S(1)} collective-permute-done((bf16[4,128,128]{2,1,0:T(8,128)(2,1)S(1)}, bf16[4,128,128]{2,1,0:T(8,128)(2,1)S(1)}, u32[]{:S(2)}, u32[]{:S(2)}) %collective-permute-start.14) | collective-permute-done | bytes 131104 | tf_op jit(solution)/shard_map/ppermute | solution.py:33
  86.7 1.4 %collective-permute-done.15 = bf16[4,128,128]{2,1,0:T(8,128)(2,1)S(1)} collective-permute-done((bf16[4,128,128]{2,1,0:T(8,128)(2,1)S(1)}, bf16[4,128,128]{2,1,0:T(8,128)(2,1)S(1)}, u32[]{:S(2)}, u32[]{:S(2)}) %collective-permute-start.15) | collective-permute-done | bytes 131104 | tf_op jit(solution)/shard_map/ppermute | solution.py:33
  88.1 1.4 %collective-permute-done.16 = bf16[4,128,128]{2,1,0:T(8,128)(2,1)S(1)} collective-permute-done((bf16[4,128,128]{2,1,0:T(8,128)(2,1)S(1)}, bf16[4,128,128]{2,1,0:T(8,128)(2,1)S(1)}, u32[]{:S(2)}, u32[]{:S(2)}) %collective-permute-start.16) | collective-permute-done | bytes 131104 | tf_op jit(solution)/shard_map/ppermute | solution.py:33
  89.5 0.1 broadcast_select_fusion.1
  89.7 1.1 %pad_maximum_fusion.prefix_ref = bf16[32,128,128]{2,1,0:T(8,128)(2,1)} fusion(bf16[16,128,128]{2,1,0:T(8,128)(2,1)S(1)} %get-tuple-element.22, bf16[16,128,128]{2,1,0:T(8,128)(2,1)S(1)} %get-tuple-element.21), kind=kLoop, calls=%fused_computation | loop fusion | flops 524288 | bytes 2097152 | tf_op jit(solution)/shard_map/concatenate | solution.py:38
  90.8 11.5 %shard_map.47 = bf16[384,4096]{1,0:T(8,128)(2,1)} custom-call(bf16[384,4096]{1,0:T(8,128)(2,1)} %bitcast.9, bf16[384,4096]{1,0:T(8,128)(2,1)} %bitcast.6, bf16[384,4096]{1,0:T(8,128)(2,1)} %bitcast.8, bf16[32,128,128]{2,1,0:T(8,128)(2,1)} %pad_maximum_fusion.prefix_ref, f32[1,4096]{1,0:T(1,128)} %bitcast.10), custom_call_target="tpu_custom_call" | custom-call | tf_op jit(solution)/shard_map/pallas_call | solution.py:103
  (13 shorter events, 0.2 us)
Async XLA Ops:
  5.7 25.0 %collective-permute-start = (f32[16,128,128]{2,1,0:T(8,128)S(1)}, f32[16,128,128]{2,1,0:T(8,128)S(1)}, u32[]{:S(2)}, u32[]{:S(2)}) collective-permute-start(f32[16,128,128]{2,1,0:T(8,128)S(1)} %constant_dynamic-slice_fusion), channel_id=1, source_target_pairs={{0,2},{4,6},{8,10},{12,14},{2,0},{6,4},{10,8},{14,12},{1,3},{5,7},... | collective-permute-start | bytes 3145736 | tf_op jit(solution)/shard_map/ppermute | solution.py:20
  32.0 2.7 %collective-permute-start.10 = (f32[4,128,128]{2,1,0:T(8,128)S(1)}, f32[4,128,128]{2,1,0:T(8,128)S(1)}, u32[]{:S(2)}, u32[]{:S(2)}) collective-permute-start(f32[4,128,128]{2,1,0:T(8,128)S(1)} %get-tuple-element.13), channel_id=1, source_target_pairs={{0,4},{2,6},{1,5},{3,7},{16,20},{18,22},{17,21},{19,23}} | collective-permute-start | bytes 786440 | tf_op jit(solution)/shard_map/ppermute | solution.py:30
  32.7 2.8 %collective-permute-start.7 = (f32[4,128,128]{2,1,0:T(8,128)S(1)}, f32[4,128,128]{2,1,0:T(8,128)S(1)}, u32[]{:S(2)}, u32[]{:S(2)}) collective-permute-start(f32[4,128,128]{2,1,0:T(8,128)S(1)} %get-tuple-element.14), channel_id=1, source_target_pairs={{0,4},{2,6},{1,5},{3,7},{16,20},{18,22},{17,21},{19,23}} | collective-permute-start | bytes 786440 | tf_op jit(solution)/shard_map/ppermute | solution.py:30
  33.4 2.8 %collective-permute-start.4 = (f32[4,128,128]{2,1,0:T(8,128)S(1)}, f32[4,128,128]{2,1,0:T(8,128)S(1)}, u32[]{:S(2)}, u32[]{:S(2)}) collective-permute-start(f32[4,128,128]{2,1,0:T(8,128)S(1)} %get-tuple-element.15), channel_id=1, source_target_pairs={{0,4},{2,6},{1,5},{3,7},{16,20},{18,22},{17,21},{19,23}} | collective-permute-start | bytes 786440 | tf_op jit(solution)/shard_map/ppermute | solution.py:30
  34.1 3.1 %collective-permute-start.1 = (f32[4,128,128]{2,1,0:T(8,128)S(1)}, f32[4,128,128]{2,1,0:T(8,128)S(1)}, u32[]{:S(2)}, u32[]{:S(2)}) collective-permute-start(f32[4,128,128]{2,1,0:T(8,128)S(1)} %get-tuple-element.16), channel_id=1, source_target_pairs={{0,4},{2,6},{1,5},{3,7},{16,20},{18,22},{17,21},{19,23}} | collective-permute-start | bytes 786440 | tf_op jit(solution)/shard_map/ppermute | solution.py:30
  34.8 3.1 %collective-permute-start.11 = (f32[4,128,128]{2,1,0:T(8,128)S(1)}, f32[4,128,128]{2,1,0:T(8,128)S(1)}, u32[]{:S(2)}, u32[]{:S(2)}) collective-permute-start(f32[4,128,128]{2,1,0:T(8,128)S(1)} %add.116), channel_id=1, source_target_pairs={{4,8},{6,10},{5,9},{7,11},{20,24},{22,26},{21,25},{23,27}} | collective-permute-start | bytes 786440 | tf_op jit(solution)/shard_map/ppermute | solution.py:30
  35.5 4.4 %collective-permute-start.8 = (f32[4,128,128]{2,1,0:T(8,128)S(1)}, f32[4,128,128]{2,1,0:T(8,128)S(1)}, u32[]{:S(2)}, u32[]{:S(2)}) collective-permute-start(f32[4,128,128]{2,1,0:T(8,128)S(1)} %add.110), channel_id=1, source_target_pairs={{4,8},{6,10},{5,9},{7,11},{20,24},{22,26},{21,25},{23,27}} | collective-permute-start | bytes 786440 | tf_op jit(solution)/shard_map/ppermute | solution.py:30
  36.3 10.1 %copy-start.1 = (f32[2048]{0:T(1024)S(1)}, f32[2048]{0:T(1024)}, u32[]{:S(2)}) copy-start(f32[2048]{0:T(1024)} %param.7) | copy-start | bytes 24580
  36.3 39.3 %copy-start = (f32[32,128,128]{2,1,0:T(8,128)S(1)}, f32[32,128,128]{2,1,0:T(8,128)}, u32[]{:S(2)}) copy-start(f32[32,128,128]{2,1,0:T(8,128)} %shard_map.46) | copy-start | bytes 6291460
  36.3 5.8 %collective-permute-start.5 = (f32[4,128,128]{2,1,0:T(8,128)S(1)}, f32[4,128,128]{2,1,0:T(8,128)S(1)}, u32[]{:S(2)}, u32[]{:S(2)}) collective-permute-start(f32[4,128,128]{2,1,0:T(8,128)S(1)} %add.104), channel_id=1, source_target_pairs={{4,8},{6,10},{5,9},{7,11},{20,24},{22,26},{21,25},{23,27}} | collective-permute-start | bytes 786440 | tf_op jit(solution)/shard_map/ppermute | solution.py:30
  37.2 7.0 %collective-permute-start.2 = (f32[4,128,128]{2,1,0:T(8,128)S(1)}, f32[4,128,128]{2,1,0:T(8,128)S(1)}, u32[]{:S(2)}, u32[]{:S(2)}) collective-permute-start(f32[4,128,128]{2,1,0:T(8,128)S(1)} %add.98), channel_id=1, source_target_pairs={{4,8},{6,10},{5,9},{7,11},{20,24},{22,26},{21,25},{23,27}} | collective-permute-start | bytes 786440 | tf_op jit(solution)/shard_map/ppermute | solution.py:30
  38.6 22.3 %collective-permute-start.12 = (f32[4,128,128]{2,1,0:T(8,128)}, f32[4,128,128]{2,1,0:T(8,128)}, u32[]{:S(2)}, u32[]{:S(2)}) collective-permute-start(f32[4,128,128]{2,1,0:T(8,128)} %get-tuple-element.5), channel_id=1, source_target_pairs={{8,12},{10,14},{9,13},{11,15},{24,28},{26,30},{25,29},{27,31}} | collective-permute-start | bytes 786440 | tf_op jit(solution)/shard_map/ppermute | solution.py:30
  40.8 25.8 %collective-permute-start.9 = (f32[4,128,128]{2,1,0:T(8,128)}, f32[4,128,128]{2,1,0:T(8,128)}, u32[]{:S(2)}, u32[]{:S(2)}) collective-permute-start(f32[4,128,128]{2,1,0:T(8,128)} %get-tuple-element.7), channel_id=1, source_target_pairs={{8,12},{10,14},{9,13},{11,15},{24,28},{26,30},{25,29},{27,31}} | collective-permute-start | bytes 786440 | tf_op jit(solution)/shard_map/ppermute | solution.py:30
  42.9 29.0 %collective-permute-start.6 = (f32[4,128,128]{2,1,0:T(8,128)}, f32[4,128,128]{2,1,0:T(8,128)}, u32[]{:S(2)}, u32[]{:S(2)}) collective-permute-start(f32[4,128,128]{2,1,0:T(8,128)} %get-tuple-element.9), channel_id=1, source_target_pairs={{8,12},{10,14},{9,13},{11,15},{24,28},{26,30},{25,29},{27,31}} | collective-permute-start | bytes 786440 | tf_op jit(solution)/shard_map/ppermute | solution.py:30
  45.1 30.5 %collective-permute-start.3 = (f32[4,128,128]{2,1,0:T(8,128)}, f32[4,128,128]{2,1,0:T(8,128)}, u32[]{:S(2)}, u32[]{:S(2)}) collective-permute-start(f32[4,128,128]{2,1,0:T(8,128)} %get-tuple-element.11), channel_id=1, source_target_pairs={{8,12},{10,14},{9,13},{11,15},{24,28},{26,30},{25,29},{27,31}} | collective-permute-start | bytes 786440 | tf_op jit(solution)/shard_map/ppermute | solution.py:30
  46.4 31.6 %collective-permute-start.17 = (f32[2048]{0:T(1024)S(1)}, f32[2048]{0:T(1024)S(1)}, u32[]{:S(2)}, u32[]{:S(2)}) collective-permute-start(f32[2048]{0:T(1024)S(1)} %copy-done.1), channel_id=1, source_target_pairs={{0,1},{1,0},{2,3},{3,2},{4,5},{5,4},{6,7},{7,6},{8,9},{9,8},{10,11... | collective-permute-start | bytes 24584 | tf_op jit(solution)/shard_map/ppermute | solution.py:124
  77.4 6.5 %collective-permute-start.13 = (bf16[4,128,128]{2,1,0:T(8,128)(2,1)S(1)}, bf16[4,128,128]{2,1,0:T(8,128)(2,1)S(1)}, u32[]{:S(2)}, u32[]{:S(2)}) collective-permute-start(bf16[4,128,128]{2,1,0:T(8,128)(2,1)S(1)} %get-tuple-element.29), channel_id=1, source_target_pairs={{0,2},{4,6},{8,10},{12,14},{2,0},{6,4},{10,8},{14,12},{1,3},{5,7},... | collective-permute-start | bytes 393224 | tf_op jit(solution)/shard_map/ppermute | solution.py:33
  78.0 8.7 %collective-permute-start.14 = (bf16[4,128,128]{2,1,0:T(8,128)(2,1)S(1)}, bf16[4,128,128]{2,1,0:T(8,128)(2,1)S(1)}, u32[]{:S(2)}, u32[]{:S(2)}) collective-permute-start(bf16[4,128,128]{2,1,0:T(8,128)(2,1)S(1)} %get-tuple-element.28), channel_id=1, source_target_pairs={{0,2},{4,6},{8,10},{12,14},{2,0},{6,4},{10,8},{14,12},{1,3},{5,7},... | collective-permute-start | bytes 393224 | tf_op jit(solution)/shard_map/ppermute | solution.py:33
  80.1 8.0 %collective-permute-start.15 = (bf16[4,128,128]{2,1,0:T(8,128)(2,1)S(1)}, bf16[4,128,128]{2,1,0:T(8,128)(2,1)S(1)}, u32[]{:S(2)}, u32[]{:S(2)}) collective-permute-start(bf16[4,128,128]{2,1,0:T(8,128)(2,1)S(1)} %get-tuple-element.27), channel_id=1, source_target_pairs={{0,2},{4,6},{8,10},{12,14},{2,0},{6,4},{10,8},{14,12},{1,3},{5,7},... | collective-permute-start | bytes 393224 | tf_op jit(solution)/shard_map/ppermute | solution.py:33
  80.7 8.8 %collective-permute-start.16 = (bf16[4,128,128]{2,1,0:T(8,128)(2,1)S(1)}, bf16[4,128,128]{2,1,0:T(8,128)(2,1)S(1)}, u32[]{:S(2)}, u32[]{:S(2)}) collective-permute-start(bf16[4,128,128]{2,1,0:T(8,128)(2,1)S(1)} %get-tuple-element.30), channel_id=1, source_target_pairs={{0,2},{4,6},{8,10},{12,14},{2,0},{6,4},{10,8},{14,12},{1,3},{5,7},... | collective-permute-start | bytes 393224 | tf_op jit(solution)/shard_map/ppermute | solution.py:33

commit v13 on v10

--- a/solution.py
+++ b/solution.py
@@ -19,14 +19,22 @@
     swap = [(2 * i, 2 * i + 1) for i in range(pairs)] + [(2 * i + 1, 2 * i) for i in range(pairs)]
     step = half // pieces
     keeps, backs = [], []
+    got, came = None, [None] * pairs
     for piece in range(pieces):
         mine = mine_all[piece * step:(piece + 1) * step]
-        got = lax.ppermute(other_all[piece * step:(piece + 1) * step], axis, swap)
+        other = other_all[piece * step:(piece + 1) * step]
+        if got is not None:
+            other, _ = lax.optimization_barrier((other, got))
+        got = lax.ppermute(other, axis, swap)
         total = mine + got
         carried = jnp.zeros_like(total)
         for hop in range(1, pairs):
             links = [(2 * (hop - 1) + side, 2 * hop + side) for side in range(2)]
-            carried = carried + lax.ppermute(carried + total, axis, links)
+            send = carried + total
+            if came[hop] is not None:
+                send, _ = lax.optimization_barrier((send, came[hop]))
+            came[hop] = lax.ppermute(send, axis, links)
+            carried = carried + came[hop]
         keeps.append((carried + jnp.where(first, 0.0, got)).astype(jnp.bfloat16))
         send = (carried + jnp.where(first, mine, 0.0)).astype(jnp.bfloat16)
         backs.append(lax.ppermute(send, axis, swap))

time: 96.1 us -> 119 us (1.24)
  waiting for transfers between devices: 50.7 us -> 76.5 us
  other arithmetic: 9.3 us -> 6.11 us
    ppermute x16, waiting for transfers between devices: 45.6 us -> 72 us  [the longest x12 45.7 us: pair_chain_prefix(): came[hop] = lax.ppermute(send, axis, links)]
    add x8, other arithmetic: 3.44 us -> 1.1 us  [pair_chain_prefix(): send = carried + total]
  transfers between devices with their start and end apart: 21 -> 21, of which waited for: 12 -> 12; matrix products, arithmetic and copies ran while one was open for 6% -> 3% of each run, Pallas kernels for 0% -> 0%
where the time goes in v13:
time: 119 us; the launch traced here: 118 us
  waiting for transfers between devices  76.5 us (64%)
  starting transfers between devices  17 us (14%)
  Pallas kernels  15.9 us (13%)
  other arithmetic  6.11 us (5%)
  local copies, waits for them, and re-layouts  2.06 us (2%)
    ppermute x12, waiting for transfers between devices, pair_chain_prefix(): came[hop] = lax.ppermute(send, axis, links)  45.7 us
    ppermute x4, waiting for transfers between devices, pair_chain_prefix(): got = lax.ppermute(other, axis, swap)  26.4 us
    pallas_call x1, Pallas kernels, attend_of(): pl.pallas_call(attend_kernel, grid=(steps,), in_specs=[pl.BlockSpec((row_...  11.5 us
    ppermute x12, starting transfers between devices, pair_chain_prefix(): came[hop] = lax.ppermute(send, axis, links)  10.7 us
    ppermute x4, waiting for transfers between devices, pair_chain_prefix(): backs.append(lax.ppermute(send, axis, swap))  4.46 us
    pallas_call x1, Pallas kernels, state_terms_of(): pl.pallas_call(state_kernel, grid=(H // group,), in_specs=[pl.BlockSpec((...  4.45 us
    ppermute x4, starting transfers between devices, pair_chain_prefix(): backs.append(lax.ppermute(send, axis, swap))  4.12 us
  transfers between devices with their start and end apart: 21, of which 12 were waited for; matrix products, arithmetic and copies ran while one was open for 3% of the time, Pallas kernels for 0%

profile of v13, /device:TPU:30, one launch (start us, length us, event | category | flops | bytes accessed | tf_op | source)
XLA Modules:
  0.0 117.8 jit_solution(9736435886768877889)
XLA Ops:
  0.0 4.4 %shard_map.46 = f32[32,128,128]{2,1,0:T(8,128)} custom-call(bf16[384,4096]{1,0:T(8,128)(2,1)} %bitcast.5, bf16[384,4096]{1,0:T(8,128)(2,1)} %bitcast.7), custom_call_target="tpu_custom_call" | custom-call | tf_op jit(solution)/shard_map/pallas_call | solution.py:61
  4.4 1.3 %constant_dynamic-slice_fusion.3 = (f32[4,128,128]{2,1,0:T(8,128)S(1)}, f32[4,128,128]{2,1,0:T(8,128)S(1)}, f32[4,128,128]{2,1,0:T(8,128)S(1)}, f32[4,128,128]{2,1,0:T(8,128)S(1)}) fusion(f32[32,128,128]{2,1,0:T(8,128)} %shard_map.46, s32[]{:T(128)S(6)} %add.130, s32[]{:T(128)S(6)} %add.128, s32[]{:T(128)S(6)} %add.126, s32[]{:T(128)S(6)} %select_n.78), kind=kLoop, calls=%fused_computation.26 | loop fusion | bytes 2097168 | tf_op jit(solution)/shard_map/slice | solution.py:25
  5.7 0.6 collective-permute-start
  6.3 7.5 %collective-permute-done = f32[4,128,128]{2,1,0:T(8,128)S(1)} collective-permute-done((f32[4,128,128]{2,1,0:T(8,128)S(1)}, f32[4,128,128]{2,1,0:T(8,128)S(1)}, u32[]{:S(2)}, u32[]{:S(2)}) %collective-permute-start) | collective-permute-done | bytes 262176 | tf_op jit(solution)/shard_map/ppermute | solution.py:28
  13.8 0.5 collective-permute-start.4
  14.3 6.7 %collective-permute-done.4 = f32[4,128,128]{2,1,0:T(8,128)S(1)} collective-permute-done((f32[4,128,128]{2,1,0:T(8,128)S(1)}, f32[4,128,128]{2,1,0:T(8,128)S(1)}, u32[]{:S(2)}, u32[]{:S(2)}) %collective-permute-start.4) | collective-permute-done | bytes 262176 | tf_op jit(solution)/shard_map/ppermute | solution.py:28
  21.0 0.5 collective-permute-start.8
  21.5 6.3 %collective-permute-done.8 = f32[4,128,128]{2,1,0:T(8,128)S(1)} collective-permute-done((f32[4,128,128]{2,1,0:T(8,128)S(1)}, f32[4,128,128]{2,1,0:T(8,128)S(1)}, u32[]{:S(2)}, u32[]{:S(2)}) %collective-permute-start.8) | collective-permute-done | bytes 262176 | tf_op jit(solution)/shard_map/ppermute | solution.py:28
  27.8 0.5 collective-permute-start.12
  28.3 5.9 %collective-permute-done.12 = f32[4,128,128]{2,1,0:T(8,128)S(1)} collective-permute-done((f32[4,128,128]{2,1,0:T(8,128)S(1)}, f32[4,128,128]{2,1,0:T(8,128)S(1)}, u32[]{:S(2)}, u32[]{:S(2)}) %collective-permute-start.12) | collective-permute-done | bytes 262176 | tf_op jit(solution)/shard_map/ppermute | solution.py:28
  34.2 1.4 %dynamic-slice_add_fusion = (f32[4,128,128]{2,1,0:T(8,128)S(1)}, f32[4,128,128]{2,1,0:T(8,128)S(1)}, f32[4,128,128]{2,1,0:T(8,128)S(1)}, f32[4,128,128]{2,1,0:T(8,128)S(1)}) fusion(f32[4,128,128]{2,1,0:T(8,128)S(1)} %collective-permute-done.12, f32[32,128,128]{2,1,0:T(8,128)} %shard_map.46, s32[]{:T(128)S(6)} %add.129, ...), kind=kLoop, calls=%fused_computation.12 | loop fusion | flops 262144 | bytes 3145744 | tf_op jit(solution)/shard_map/add | solution.py:29
  35.6 0.7 collective-permute-start.1
  36.3 0.7 collective-permute-start.5
  37.0 0.7 collective-permute-start.2
  37.8 0.0 copy-start.7
  37.8 0.0 copy-start
  37.8 0.8 collective-permute-start.9
  38.6 0.7 collective-permute-start.6
  39.3 0.1 fusion.3
  39.4 1.3 %collective-permute-start.3 = (f32[4,128,128]{2,1,0:T(8,128)S(1)}, f32[4,128,128]{2,1,0:T(8,128)S(1)}, u32[]{:S(2)}, u32[]{:S(2)}) collective-permute-start(f32[4,128,128]{2,1,0:T(8,128)S(1)} %get-tuple-element.35), channel_id=1, source_target_pairs={{8,12},{10,14},{9,13},{11,15},{24,28},{26,30},{25,29},{27,31}} | collective-permute-start | bytes 786440 | tf_op jit(solution)/shard_map/ppermute | solution.py:36
  40.7 0.7 collective-permute-start.13
  41.4 0.7 collective-permute-start.10
  42.1 0.1 fusion.2
  42.2 22.1 %collective-permute-done.3 = f32[4,128,128]{2,1,0:T(8,128)S(1)} collective-permute-done((f32[4,128,128]{2,1,0:T(8,128)S(1)}, f32[4,128,128]{2,1,0:T(8,128)S(1)}, u32[]{:S(2)}, u32[]{:S(2)}) %collective-permute-start.3) | collective-permute-done | bytes 262176 | tf_op jit(solution)/shard_map/ppermute | solution.py:36
  64.2 1.3 %collective-permute-start.7 = (f32[4,128,128]{2,1,0:T(8,128)S(1)}, f32[4,128,128]{2,1,0:T(8,128)S(1)}, u32[]{:S(2)}, u32[]{:S(2)}) collective-permute-start(f32[4,128,128]{2,1,0:T(8,128)S(1)} %get-tuple-element.20), channel_id=1, source_target_pairs={{8,12},{10,14},{9,13},{11,15},{24,28},{26,30},{25,29},{27,31}} | collective-permute-start | bytes 786440 | tf_op jit(solution)/shard_map/ppermute | solution.py:36
  65.6 0.7 collective-permute-start.14
  66.3 0.1 fusion.1
  66.3 8.6 %collective-permute-done.7 = f32[4,128,128]{2,1,0:T(8,128)S(1)} collective-permute-done((f32[4,128,128]{2,1,0:T(8,128)S(1)}, f32[4,128,128]{2,1,0:T(8,128)S(1)}, u32[]{:S(2)}, u32[]{:S(2)}) %collective-permute-start.7) | collective-permute-done | bytes 262176 | tf_op jit(solution)/shard_map/ppermute | solution.py:36
  75.0 1.3 %collective-permute-start.11 = (f32[4,128,128]{2,1,0:T(8,128)S(1)}, f32[4,128,128]{2,1,0:T(8,128)S(1)}, u32[]{:S(2)}, u32[]{:S(2)}) collective-permute-start(f32[4,128,128]{2,1,0:T(8,128)S(1)} %get-tuple-element.24), channel_id=1, source_target_pairs={{8,12},{10,14},{9,13},{11,15},{24,28},{26,30},{25,29},{27,31}} | collective-permute-start | bytes 786440 | tf_op jit(solution)/shard_map/ppermute | solution.py:36
  76.3 0.8 fusion
  77.0 7.8 %collective-permute-done.11 = f32[4,128,128]{2,1,0:T(8,128)S(1)} collective-permute-done((f32[4,128,128]{2,1,0:T(8,128)S(1)}, f32[4,128,128]{2,1,0:T(8,128)S(1)}, u32[]{:S(2)}, u32[]{:S(2)}) %collective-permute-start.11) | collective-permute-done | bytes 262176 | tf_op jit(solution)/shard_map/ppermute | solution.py:36
  84.8 0.7 copy-done.6
  85.5 1.3 %collective-permute-start.15 = (f32[4,128,128]{2,1,0:T(8,128)}, f32[4,128,128]{2,1,0:T(8,128)}, u32[]{:S(2)}, u32[]{:S(2)}) collective-permute-start(f32[4,128,128]{2,1,0:T(8,128)} %get-tuple-element.28), channel_id=1, source_target_pairs={{8,12},{10,14},{9,13},{11,15},{24,28},{26,30},{25,29},{27,31}} | collective-permute-start | bytes 786440 | tf_op jit(solution)/shard_map/ppermute | solution.py:36
  86.8 0.1 collective-permute-start.20
  86.9 7.2 %collective-permute-done.15 = f32[4,128,128]{2,1,0:T(8,128)} collective-permute-done((f32[4,128,128]{2,1,0:T(8,128)}, f32[4,128,128]{2,1,0:T(8,128)}, u32[]{:S(2)}, u32[]{:S(2)}) %collective-permute-start.15) | collective-permute-done | bytes 262176 | tf_op jit(solution)/shard_map/ppermute | solution.py:36
  94.1 1.8 %add_convert_fusion = (bf16[4,128,128]{2,1,0:T(8,128)(2,1)S(1)}, bf16[4,128,128]{2,1,0:T(8,128)(2,1)S(1)}, bf16[4,128,128]{2,1,0:T(8,128)(2,1)S(1)}, bf16[4,128,...) fusion(f32[32,128,128]{2,1,0:T(8,128)S(1)} %copy-done, ...), kind=kLoop, calls=%fused_computation.4 | loop fusion | flops 1835008 | bytes 5242897 | tf_op jit(solution)/shard_map/convert_element_type | solution.py:39
  95.9 0.4 collective-permute-start.16
  96.3 1.7 %collective-permute-start.17 = (bf16[4,128,128]{2,1,0:T(8,128)(2,1)S(1)}, bf16[4,128,128]{2,1,0:T(8,128)(2,1)S(1)}, u32[]{:S(2)}, u32[]{:S(2)}) collective-permute-start(bf16[4,128,128]{2,1,0:T(8,128)(2,1)S(1)} %get-tuple-element.39), channel_id=1, source_target_pairs={{0,2},{4,6},{8,10},{12,14},{2,0},{6,4},{10,8},{14,12},{1,3},{5,7},... | collective-permute-start | bytes 393224 | tf_op jit(solution)/shard_map/ppermute | solution.py:40
  98.0 0.6 pad_maximum_fusion.2
  98.6 0.3 collective-permute-start.18
  98.9 1.7 %collective-permute-start.19 = (bf16[4,128,128]{2,1,0:T(8,128)(2,1)S(1)}, bf16[4,128,128]{2,1,0:T(8,128)(2,1)S(1)}, u32[]{:S(2)}, u32[]{:S(2)}) collective-permute-start(bf16[4,128,128]{2,1,0:T(8,128)(2,1)S(1)} %get-tuple-element.37), channel_id=1, source_target_pairs={{0,2},{4,6},{8,10},{12,14},{2,0},{6,4},{10,8},{14,12},{1,3},{5,7},... | collective-permute-start | bytes 393224 | tf_op jit(solution)/shard_map/ppermute | solution.py:40
  100.6 0.3 collective-permute-done.16
  100.9 1.4 %collective-permute-done.17 = bf16[4,128,128]{2,1,0:T(8,128)(2,1)S(1)} collective-permute-done((bf16[4,128,128]{2,1,0:T(8,128)(2,1)S(1)}, bf16[4,128,128]{2,1,0:T(8,128)(2,1)S(1)}, u32[]{:S(2)}, u32[]{:S(2)}) %collective-permute-start.17) | collective-permute-done | bytes 131104 | tf_op jit(solution)/shard_map/ppermute | solution.py:40
  102.4 1.4 %collective-permute-done.18 = bf16[4,128,128]{2,1,0:T(8,128)(2,1)S(1)} collective-permute-done((bf16[4,128,128]{2,1,0:T(8,128)(2,1)S(1)}, bf16[4,128,128]{2,1,0:T(8,128)(2,1)S(1)}, u32[]{:S(2)}, u32[]{:S(2)}) %collective-permute-start.18) | collective-permute-done | bytes 131104 | tf_op jit(solution)/shard_map/ppermute | solution.py:40
  103.8 1.4 %collective-permute-done.19 = bf16[4,128,128]{2,1,0:T(8,128)(2,1)S(1)} collective-permute-done((bf16[4,128,128]{2,1,0:T(8,128)(2,1)S(1)}, bf16[4,128,128]{2,1,0:T(8,128)(2,1)S(1)}, u32[]{:S(2)}, u32[]{:S(2)}) %collective-permute-start.19) | collective-permute-done | bytes 131104 | tf_op jit(solution)/shard_map/ppermute | solution.py:40
  105.2 0.1 broadcast_select_fusion.1
  105.3 1.1 pad_maximum_fusion.prefix_ref
  106.4 11.5 %shard_map.47 = bf16[384,4096]{1,0:T(8,128)(2,1)} custom-call(bf16[384,4096]{1,0:T(8,128)(2,1)} %bitcast.9, bf16[384,4096]{1,0:T(8,128)(2,1)} %bitcast.6, bf16[384,4096]{1,0:T(8,128)(2,1)} %bitcast.8, bf16[32,128,128]{2,1,0:T(8,128)(2,1)} %pad_maximum_fusion.prefix_ref, f32[1,4096]{1,0:T(1,128)} %bitcast.10), custom_call_target="tpu_custom_call" | custom-call | tf_op jit(solution)/shard_map/pallas_call | solution.py:110
  (31 shorter events, 0.3 us)
Async XLA Ops:
  5.7 8.1 %collective-permute-start = (f32[4,128,128]{2,1,0:T(8,128)S(1)}, f32[4,128,128]{2,1,0:T(8,128)S(1)}, u32[]{:S(2)}, u32[]{:S(2)}) collective-permute-start(f32[4,128,128]{2,1,0:T(8,128)S(1)} %get-tuple-element.48), channel_id=1, source_target_pairs={{0,2},{4,6},{8,10},{12,14},{2,0},{6,4},{10,8},{14,12},{1,3},{5,7},... | collective-permute-start | bytes 786440 | tf_op jit(solution)/shard_map/ppermute | solution.py:28
  13.8 7.2 %collective-permute-start.4 = (f32[4,128,128]{2,1,0:T(8,128)S(1)}, f32[4,128,128]{2,1,0:T(8,128)S(1)}, u32[]{:S(2)}, u32[]{:S(2)}) collective-permute-start(f32[4,128,128]{2,1,0:T(8,128)S(1)} %get-tuple-element.17), channel_id=1, source_target_pairs={{0,2},{4,6},{8,10},{12,14},{2,0},{6,4},{10,8},{14,12},{1,3},{5,7},... | collective-permute-start | bytes 786440 | tf_op jit(solution)/shard_map/ppermute | solution.py:28
  21.0 16.8 %copy-start.1 = (f32[4,128,128]{2,1,0:T(8,128)}, f32[4,128,128]{2,1,0:T(8,128)S(1)}, u32[]{:S(2)}) copy-start(f32[4,128,128]{2,1,0:T(8,128)S(1)} %collective-permute-done.4) | copy-start | bytes 786436
  21.0 6.8 %collective-permute-start.8 = (f32[4,128,128]{2,1,0:T(8,128)S(1)}, f32[4,128,128]{2,1,0:T(8,128)S(1)}, u32[]{:S(2)}, u32[]{:S(2)}) collective-permute-start(f32[4,128,128]{2,1,0:T(8,128)S(1)} %get-tuple-element.21), channel_id=1, source_target_pairs={{0,2},{4,6},{8,10},{12,14},{2,0},{6,4},{10,8},{14,12},{1,3},{5,7},... | collective-permute-start | bytes 786440 | tf_op jit(solution)/shard_map/ppermute | solution.py:28
  27.8 10.0 %copy-start.2 = (f32[4,128,128]{2,1,0:T(8,128)}, f32[4,128,128]{2,1,0:T(8,128)S(1)}, u32[]{:S(2)}) copy-start(f32[4,128,128]{2,1,0:T(8,128)S(1)} %collective-permute-done.8) | copy-start | bytes 786436
  27.8 6.4 %collective-permute-start.12 = (f32[4,128,128]{2,1,0:T(8,128)S(1)}, f32[4,128,128]{2,1,0:T(8,128)S(1)}, u32[]{:S(2)}, u32[]{:S(2)}) collective-permute-start(f32[4,128,128]{2,1,0:T(8,128)S(1)} %get-tuple-element.25), channel_id=1, source_target_pairs={{0,2},{4,6},{8,10},{12,14},{2,0},{6,4},{10,8},{14,12},{1,3},{5,7},... | collective-permute-start | bytes 786440 | tf_op jit(solution)/shard_map/ppermute | solution.py:28
  34.2 3.6 %copy-start.3 = (f32[4,128,128]{2,1,0:T(8,128)}, f32[4,128,128]{2,1,0:T(8,128)S(1)}, u32[]{:S(2)}) copy-start(f32[4,128,128]{2,1,0:T(8,128)S(1)} %collective-permute-done.12) | copy-start | bytes 786436
  35.6 0.7 collective-permute-start.1
  36.3 1.4 %collective-permute-start.5 = (f32[4,128,128]{2,1,0:T(8,128)S(1)}, f32[4,128,128]{2,1,0:T(8,128)S(1)}, u32[]{:S(2)}, u32[]{:S(2)}) collective-permute-start(f32[4,128,128]{2,1,0:T(8,128)S(1)} %get-tuple-element.18), channel_id=1, source_target_pairs={{0,4},{2,6},{1,5},{3,7},{16,20},{18,22},{17,21},{19,23}} | collective-permute-start | bytes 786440 | tf_op jit(solution)/shard_map/ppermute | solution.py:36
  37.0 0.7 collective-permute-start.2
  37.8 49.0 %copy-start.7 = (f32[2048]{0:T(1024)S(1)}, f32[2048]{0:T(1024)}, u32[]{:S(2)}) copy-start(f32[2048]{0:T(1024)} %param.7) | copy-start | bytes 24580
  37.8 56.3 %copy-start = (f32[32,128,128]{2,1,0:T(8,128)S(1)}, f32[32,128,128]{2,1,0:T(8,128)}, u32[]{:S(2)}) copy-start(f32[32,128,128]{2,1,0:T(8,128)} %shard_map.46) | copy-start | bytes 6291460
  37.8 2.9 %collective-permute-start.9 = (f32[4,128,128]{2,1,0:T(8,128)S(1)}, f32[4,128,128]{2,1,0:T(8,128)S(1)}, u32[]{:S(2)}, u32[]{:S(2)}) collective-permute-start(f32[4,128,128]{2,1,0:T(8,128)S(1)} %get-tuple-element.22), channel_id=1, source_target_pairs={{0,4},{2,6},{1,5},{3,7},{16,20},{18,22},{17,21},{19,23}} | collective-permute-start | bytes 786440 | tf_op jit(solution)/shard_map/ppermute | solution.py:36
  38.6 2.1 %collective-permute-start.6 = (f32[4,128,128]{2,1,0:T(8,128)S(1)}, f32[4,128,128]{2,1,0:T(8,128)S(1)}, u32[]{:S(2)}, u32[]{:S(2)}) collective-permute-start(f32[4,128,128]{2,1,0:T(8,128)S(1)} %add.104), channel_id=1, source_target_pairs={{4,8},{6,10},{5,9},{7,11},{20,24},{22,26},{21,25},{23,27}} | collective-permute-start | bytes 786440 | tf_op jit(solution)/shard_map/ppermute | solution.py:36
  39.4 24.9 %collective-permute-start.3 = (f32[4,128,128]{2,1,0:T(8,128)S(1)}, f32[4,128,128]{2,1,0:T(8,128)S(1)}, u32[]{:S(2)}, u32[]{:S(2)}) collective-permute-start(f32[4,128,128]{2,1,0:T(8,128)S(1)} %get-tuple-element.35), channel_id=1, source_target_pairs={{8,12},{10,14},{9,13},{11,15},{24,28},{26,30},{25,29},{27,31}} | collective-permute-start | bytes 786440 | tf_op jit(solution)/shard_map/ppermute | solution.py:36
  40.7 24.8 %collective-permute-start.13 = (f32[4,128,128]{2,1,0:T(8,128)S(1)}, f32[4,128,128]{2,1,0:T(8,128)S(1)}, u32[]{:S(2)}, u32[]{:S(2)}) collective-permute-start(f32[4,128,128]{2,1,0:T(8,128)S(1)} %get-tuple-element.26), channel_id=1, source_target_pairs={{0,4},{2,6},{1,5},{3,7},{16,20},{18,22},{17,21},{19,23}} | collective-permute-start | bytes 786440 | tf_op jit(solution)/shard_map/ppermute | solution.py:36
  41.4 24.2 %collective-permute-start.10 = (f32[4,128,128]{2,1,0:T(8,128)S(1)}, f32[4,128,128]{2,1,0:T(8,128)S(1)}, u32[]{:S(2)}, u32[]{:S(2)}) collective-permute-start(f32[4,128,128]{2,1,0:T(8,128)S(1)} %add.110), channel_id=1, source_target_pairs={{4,8},{6,10},{5,9},{7,11},{20,24},{22,26},{21,25},{23,27}} | collective-permute-start | bytes 786440 | tf_op jit(solution)/shard_map/ppermute | solution.py:36
  64.2 12.8 %copy-start.4 = (f32[4,128,128]{2,1,0:T(8,128)}, f32[4,128,128]{2,1,0:T(8,128)S(1)}, u32[]{:S(2)}) copy-start(f32[4,128,128]{2,1,0:T(8,128)S(1)} %collective-permute-done.3) | copy-start | bytes 786436
  64.2 10.7 %collective-permute-start.7 = (f32[4,128,128]{2,1,0:T(8,128)S(1)}, f32[4,128,128]{2,1,0:T(8,128)S(1)}, u32[]{:S(2)}, u32[]{:S(2)}) collective-permute-start(f32[4,128,128]{2,1,0:T(8,128)S(1)} %get-tuple-element.20), channel_id=1, source_target_pairs={{8,12},{10,14},{9,13},{11,15},{24,28},{26,30},{25,29},{27,31}} | collective-permute-start | bytes 786440 | tf_op jit(solution)/shard_map/ppermute | solution.py:36
  65.6 10.7 %collective-permute-start.14 = (f32[4,128,128]{2,1,0:T(8,128)S(1)}, f32[4,128,128]{2,1,0:T(8,128)S(1)}, u32[]{:S(2)}, u32[]{:S(2)}) collective-permute-start(f32[4,128,128]{2,1,0:T(8,128)S(1)} %add.116), channel_id=1, source_target_pairs={{4,8},{6,10},{5,9},{7,11},{20,24},{22,26},{21,25},{23,27}} | collective-permute-start | bytes 786440 | tf_op jit(solution)/shard_map/ppermute | solution.py:36
  75.0 9.8 %copy-start.5 = (f32[4,128,128]{2,1,0:T(8,128)}, f32[4,128,128]{2,1,0:T(8,128)S(1)}, u32[]{:S(2)}) copy-start(f32[4,128,128]{2,1,0:T(8,128)S(1)} %collective-permute-done.7) | copy-start | bytes 786436
  75.0 9.8 %collective-permute-start.11 = (f32[4,128,128]{2,1,0:T(8,128)S(1)}, f32[4,128,128]{2,1,0:T(8,128)S(1)}, u32[]{:S(2)}, u32[]{:S(2)}) collective-permute-start(f32[4,128,128]{2,1,0:T(8,128)S(1)} %get-tuple-element.24), channel_id=1, source_target_pairs={{8,12},{10,14},{9,13},{11,15},{24,28},{26,30},{25,29},{27,31}} | collective-permute-start | bytes 786440 | tf_op jit(solution)/shard_map/ppermute | solution.py:36
  84.8 0.7 copy-start.6
  85.5 8.6 %collective-permute-start.15 = (f32[4,128,128]{2,1,0:T(8,128)}, f32[4,128,128]{2,1,0:T(8,128)}, u32[]{:S(2)}, u32[]{:S(2)}) collective-permute-start(f32[4,128,128]{2,1,0:T(8,128)} %get-tuple-element.28), channel_id=1, source_target_pairs={{8,12},{10,14},{9,13},{11,15},{24,28},{26,30},{25,29},{27,31}} | collective-permute-start | bytes 786440 | tf_op jit(solution)/shard_map/ppermute | solution.py:36
  86.8 9.5 %collective-permute-start.20 = (f32[2048]{0:T(1024)S(1)}, f32[2048]{0:T(1024)S(1)}, u32[]{:S(2)}, u32[]{:S(2)}) collective-permute-start(f32[2048]{0:T(1024)S(1)} %copy-done.7), channel_id=1, source_target_pairs={{0,1},{1,0},{2,3},{3,2},{4,5},{5,4},{6,7},{7,6},{8,9},{9,8},{10,11... | collective-permute-start | bytes 24584 | tf_op jit(solution)/shard_map/ppermute | solution.py:131
  95.9 5.0 %collective-permute-start.16 = (bf16[4,128,128]{2,1,0:T(8,128)(2,1)S(1)}, bf16[4,128,128]{2,1,0:T(8,128)(2,1)S(1)}, u32[]{:S(2)}, u32[]{:S(2)}) collective-permute-start(bf16[4,128,128]{2,1,0:T(8,128)(2,1)S(1)} %get-tuple-element.38), channel_id=1, source_target_pairs={{0,2},{4,6},{8,10},{12,14},{2,0},{6,4},{10,8},{14,12},{1,3},{5,7},... | collective-permute-start | bytes 393224 | tf_op jit(solution)/shard_map/ppermute | solution.py:40
  96.3 6.0 %collective-permute-start.17 = (bf16[4,128,128]{2,1,0:T(8,128)(2,1)S(1)}, bf16[4,128,128]{2,1,0:T(8,128)(2,1)S(1)}, u32[]{:S(2)}, u32[]{:S(2)}) collective-permute-start(bf16[4,128,128]{2,1,0:T(8,128)(2,1)S(1)} %get-tuple-element.39), channel_id=1, source_target_pairs={{0,2},{4,6},{8,10},{12,14},{2,0},{6,4},{10,8},{14,12},{1,3},{5,7},... | collective-permute-start | bytes 393224 | tf_op jit(solution)/shard_map/ppermute | solution.py:40
  98.6 5.1 %collective-permute-start.18 = (bf16[4,128,128]{2,1,0:T(8,128)(2,1)S(1)}, bf16[4,128,128]{2,1,0:T(8,128)(2,1)S(1)}, u32[]{:S(2)}, u32[]{:S(2)}) collective-permute-start(bf16[4,128,128]{2,1,0:T(8,128)(2,1)S(1)} %get-tuple-element.40), channel_id=1, source_target_pairs={{0,2},{4,6},{8,10},{12,14},{2,0},{6,4},{10,8},{14,12},{1,3},{5,7},... | collective-permute-start | bytes 393224 | tf_op jit(solution)/shard_map/ppermute | solution.py:40
  98.9 6.2 %collective-permute-start.19 = (bf16[4,128,128]{2,1,0:T(8,128)(2,1)S(1)}, bf16[4,128,128]{2,1,0:T(8,128)(2,1)S(1)}, u32[]{:S(2)}, u32[]{:S(2)}) collective-permute-start(bf16[4,128,128]{2,1,0:T(8,128)(2,1)S(1)} %get-tuple-element.37), channel_id=1, source_target_pairs={{0,2},{4,6},{8,10},{12,14},{2,0},{6,4},{10,8},{14,12},{1,3},{5,7},... | collective-permute-start | bytes 393224 | tf_op jit(solution)/shard_map/ppermute | solution.py:40

commit v14 on v10

--- a/solution.py
+++ b/solution.py
@@ -128,7 +128,7 @@
     keyset = key_rows.reshape(seq_count * row_count, feat_count)
     valset = value_rows.reshape(seq_count * row_count, feat_count)
     state_terms = state_terms_of(keyset, valset, 16)
-    prefix_bf = pair_chain_prefix(state_terms, "ctx", 4)
+    prefix_bf = pair_chain_prefix(state_terms, "ctx", 2)
     normed = attend_of(query, keyset, valset, prefix_bf, full_gain, 8)
     return normed.reshape(seq_count, row_count, feat_count)
 

time: 96.1 us -> 98.5 us (1.025)
  waiting for transfers between devices: 50.7 us -> 64.2 us
  starting transfers between devices: 17.9 us -> 8.62 us
  other arithmetic: 9.3 us -> 7.07 us
    ppermute x12 -> x6, waiting for transfers between devices: 22.7 us -> 31.5 us  [pair_chain_prefix(): carried = carried + lax.ppermute(carried + total, axis, links)]
    ppermute x12 -> x6, starting transfers between devices: 10.7 us -> 5.32 us  [pair_chain_prefix(): carried = carried + lax.ppermute(carried + total, axis, links)]
    ppermute x4 -> x2, waiting for transfers between devices: 5.1 us -> 7.96 us  [pair_chain_prefix(): backs.append(lax.ppermute(send, axis, swap))]
    ppermute x4 -> x2, starting transfers between devices: 4.12 us -> 2.09 us  [pair_chain_prefix(): backs.append(lax.ppermute(send, axis, swap))]
    ppermute x4 -> x2, starting transfers between devices: 3.09 us -> 1.13 us  [pair_chain_prefix(): got = lax.ppermute(other_all[piece * step:(piece + 1) * step], axis, swap)]
    ppermute x4 -> x2, waiting for transfers between devices: 22.9 us -> 24.7 us  [pair_chain_prefix(): got = lax.ppermute(other_all[piece * step:(piece + 1) * step], axis, swap)]
    add x8 -> x4, other arithmetic: 3.44 us -> 2.08 us  [pair_chain_prefix(): carried = carried + lax.ppermute(carried + total, axis, links)]
  transfers between devices with their start and end apart: 21 -> 11, of which waited for: 12 -> 6; matrix products, arithmetic and copies ran while one was open for 6% -> 5% of each run, Pallas kernels for 0% -> 0%
where the time goes in v14:
time: 98.5 us; the launch traced here: 98 us
  waiting for transfers between devices  64.2 us (65%)
  Pallas kernels  15.9 us (16%)
  starting transfers between devices  8.62 us (9%)
  other arithmetic  7.07 us (7%)
  local copies, waits for them, and re-layouts  2.08 us (2%)
    ppermute x6, waiting for transfers between devices, pair_chain_prefix(): carried = carried + lax.ppermute(carried + total, axis, links)  31.5 us
    ppermute x2, waiting for transfers between devices, pair_chain_prefix(): got = lax.ppermute(other_all[piece * step:(piece + 1) * step], axis, swap)  24.7 us
    pallas_call x1, Pallas kernels, attend_of(): pl.pallas_call(attend_kernel, grid=(steps,), in_specs=[pl.BlockSpec((row_...  11.5 us
    ppermute x2, waiting for transfers between devices, pair_chain_prefix(): backs.append(lax.ppermute(send, axis, swap))  7.96 us
    ppermute x6, starting transfers between devices, pair_chain_prefix(): carried = carried + lax.ppermute(carried + total, axis, links)  5.32 us
    pallas_call x1, Pallas kernels, state_terms_of(): pl.pallas_call(state_kernel, grid=(H // group,), in_specs=[pl.BlockSpec((...  4.45 us
    ppermute x2, starting transfers between devices, pair_chain_prefix(): backs.append(lax.ppermute(send, axis, swap))  2.09 us
    add x4, other arithmetic, pair_chain_prefix(): carried = carried + lax.ppermute(carried + total, axis, links)  2.08 us
  transfers between devices with their start and end apart: 11, of which 6 were waited for; matrix products, arithmetic and copies ran while one was open for 5% of the time, Pallas kernels for 0%

profile of v14, /device:TPU:30, one launch (start us, length us, event | category | flops | bytes accessed | tf_op | source)
XLA Modules:
  0.0 98.0 jit_solution(3264321830842535379)
XLA Ops:
  0.0 4.4 %shard_map.46 = f32[32,128,128]{2,1,0:T(8,128)} custom-call(bf16[384,4096]{1,0:T(8,128)(2,1)} %bitcast.5, bf16[384,4096]{1,0:T(8,128)(2,1)} %bitcast.7), custom_call_target="tpu_custom_call" | custom-call | tf_op jit(solution)/shard_map/pallas_call | solution.py:53
  4.4 0.0 copy-start
  4.5 1.2 %constant_dynamic-slice_fusion.1 = f32[8,128,128]{2,1,0:T(8,128)S(1)} fusion(f32[32,128,128]{2,1,0:T(8,128)} %shard_map.46, s32[]{:T(128)S(6)} %add.70), kind=kLoop, calls=%fused_computation.16 | loop fusion | bytes 1048580 | tf_op jit(solution)/shard_map/slice | solution.py:24
  5.7 0.6 collective-permute-start.4
  6.2 13.2 %collective-permute-done.4 = f32[8,128,128]{2,1,0:T(8,128)S(1)} collective-permute-done((f32[8,128,128]{2,1,0:T(8,128)S(1)}, f32[8,128,128]{2,1,0:T(8,128)S(1)}, u32[]{:S(2)}, u32[]{:S(2)}) %collective-permute-start.4) | collective-permute-done | bytes 524320 | tf_op jit(solution)/shard_map/ppermute | solution.py:24
  19.4 1.3 %dynamic-slice_add_fusion = (f32[8,128,128]{2,1,0:T(8,128)S(1)}, f32[8,128,128]{2,1,0:T(8,128)S(1)}) fusion(f32[8,128,128]{2,1,0:T(8,128)S(1)} %collective-permute-done.4, f32[32,128,128]{2,1,0:T(8,128)} %shard_map.46, s32[]{:T(128)S(6)} %add.69, s32[]{:T(128)S(6)} %select_n.62), kind=kLoop, calls=%fused_computation.8 | loop fusion | flops 131072 | bytes 2621448 | tf_op jit(solution)/shard_map/add | solution.py:25
  20.7 0.6 collective-permute-start
  21.3 0.7 collective-permute-start.5
  22.0 11.6 %collective-permute-done = f32[8,128,128]{2,1,0:T(8,128)S(1)} collective-permute-done((f32[8,128,128]{2,1,0:T(8,128)S(1)}, f32[8,128,128]{2,1,0:T(8,128)S(1)}, u32[]{:S(2)}, u32[]{:S(2)}) %collective-permute-start) | collective-permute-done | bytes 524320 | tf_op jit(solution)/shard_map/ppermute | solution.py:24
  33.5 0.0 copy-start.1
  33.5 0.8 copy-done.1
  34.3 0.0 copy-done
  34.3 0.1 dynamic-slice_add_fusion.1
  34.4 0.7 collective-permute-start.1
  35.1 0.0 collective-permute-done.5
  35.1 0.1 add.62
  35.2 0.7 collective-permute-start.6
  35.9 0.0 collective-permute-done.1
  35.9 0.1 add.56
  36.0 0.0 copy-start.2
  36.0 0.7 collective-permute-start.2
  36.7 0.0 collective-permute-done.6
  36.7 0.9 fusion
  37.6 1.3 %collective-permute-start.7 = (f32[8,128,128]{2,1,0:T(8,128)}, f32[8,128,128]{2,1,0:T(8,128)}, u32[]{:S(2)}, u32[]{:S(2)}) collective-permute-start(f32[8,128,128]{2,1,0:T(8,128)} %get-tuple-element.5), channel_id=1, source_target_pairs={{8,12},{10,14},{9,13},{11,15},{24,28},{26,30},{25,29},{27,31}} | collective-permute-start | bytes 1572872 | tf_op jit(solution)/shard_map/ppermute | solution.py:29
  38.9 0.0 collective-permute-done.2
  38.9 1.1 %fusion.1 = (f32[8,128,128]{2,1,0:T(8,128)}, f32[8,128,128]{2,1,0:T(8,128)}) fusion(f32[8,128,128]{2,1,0:T(8,128)S(1)} %dynamic-slice_add_fusion.1, f32[8,128,128]{2,1,0:T(8,128)S(1)} %collective-permute-done.1, f32[8,128,128]{2,1,0:T(8,128)S(1)} %collective-permute-done.2), kind=kLoop, calls=%fused_computation.18 | loop fusion | flops 262144 | bytes 2621440 | tf_op jit(solution)/shard_map/add | solution.py:29
  40.0 1.3 %collective-permute-start.3 = (f32[8,128,128]{2,1,0:T(8,128)}, f32[8,128,128]{2,1,0:T(8,128)}, u32[]{:S(2)}, u32[]{:S(2)}) collective-permute-start(f32[8,128,128]{2,1,0:T(8,128)} %get-tuple-element.7), channel_id=1, source_target_pairs={{8,12},{10,14},{9,13},{11,15},{24,28},{26,30},{25,29},{27,31}} | collective-permute-start | bytes 1572872 | tf_op jit(solution)/shard_map/ppermute | solution.py:29
  41.2 0.0 copy-done.2
  41.2 0.1 collective-permute-start.10
  41.3 19.7 %collective-permute-done.7 = f32[8,128,128]{2,1,0:T(8,128)} collective-permute-done((f32[8,128,128]{2,1,0:T(8,128)}, f32[8,128,128]{2,1,0:T(8,128)}, u32[]{:S(2)}, u32[]{:S(2)}) %collective-permute-start.7) | collective-permute-done | bytes 524320 | tf_op jit(solution)/shard_map/ppermute | solution.py:29
  61.1 11.7 %collective-permute-done.3 = f32[8,128,128]{2,1,0:T(8,128)} collective-permute-done((f32[8,128,128]{2,1,0:T(8,128)}, f32[8,128,128]{2,1,0:T(8,128)}, u32[]{:S(2)}, u32[]{:S(2)}) %collective-permute-start.3) | collective-permute-done | bytes 524320 | tf_op jit(solution)/shard_map/ppermute | solution.py:29
  72.8 1.9 %add_convert_fusion = (bf16[8,128,128]{2,1,0:T(8,128)(2,1)S(1)}, bf16[8,128,128]{2,1,0:T(8,128)(2,1)S(1)}, bf16[8,128,128]{2,1,0:T(8,128)(2,1)S(1)}, bf16[8,128,128]{2,1,0:T(8,128)(2,1)S(1)}) fusion(f32[32,128,128]{2,1,0:T(8,128)S(1)} %copy-done, s32[]{:T(128)S(6)} %add.69, pred[]{:T(512)S(6)} %eq.8, f32[8,128,128]{2,1,0:T(8,128)S(1)} %get-tuple-element.6, ...), kind=kLoop, calls=%fused_computation.2 | loop fusion | flops 1835008 | bytes 5242889 | tf_op jit(solution)/shard_map/convert_element_type | solution.py:31
  74.7 0.5 collective-permute-start.8
  75.2 1.6 %collective-permute-start.9 = (bf16[8,128,128]{2,1,0:T(8,128)(2,1)S(1)}, bf16[8,128,128]{2,1,0:T(8,128)(2,1)S(1)}, u32[]{:S(2)}, u32[]{:S(2)}) collective-permute-start(bf16[8,128,128]{2,1,0:T(8,128)(2,1)S(1)} %get-tuple-element.9), channel_id=1, source_target_pairs={{0,2},{4,6},{8,10},{12,14},{2,0},{6,4},{10,8},{14,12},{1,3},{5,7},... | collective-permute-start | bytes 786440 | tf_op jit(solution)/shard_map/ppermute | solution.py:32
  76.8 0.0 collective-permute-done.10
  76.8 0.6 pad_maximum_fusion.2
  77.4 5.2 %collective-permute-done.8 = bf16[8,128,128]{2,1,0:T(8,128)(2,1)S(1)} collective-permute-done((bf16[8,128,128]{2,1,0:T(8,128)(2,1)S(1)}, bf16[8,128,128]{2,1,0:T(8,128)(2,1)S(1)}, u32[]{:S(2)}, u32[]{:S(2)}) %collective-permute-start.8) | collective-permute-done | bytes 262176 | tf_op jit(solution)/shard_map/ppermute | solution.py:32
  82.6 2.8 %collective-permute-done.9 = bf16[8,128,128]{2,1,0:T(8,128)(2,1)S(1)} collective-permute-done((bf16[8,128,128]{2,1,0:T(8,128)(2,1)S(1)}, bf16[8,128,128]{2,1,0:T(8,128)(2,1)S(1)}, u32[]{:S(2)}, u32[]{:S(2)}) %collective-permute-start.9) | collective-permute-done | bytes 262176 | tf_op jit(solution)/shard_map/ppermute | solution.py:32
  85.4 0.1 broadcast_select_fusion.1
  85.5 1.1 %pad_maximum_fusion.prefix_ref = bf16[32,128,128]{2,1,0:T(8,128)(2,1)} fusion(bf16[16,128,128]{2,1,0:T(8,128)(2,1)S(1)} %get-tuple-element.15, bf16[16,128,128]{2,1,0:T(8,128)(2,1)S(1)} %get-tuple-element.14), kind=kLoop, calls=%fused_computation | loop fusion | flops 524288 | bytes 2097152 | tf_op jit(solution)/shard_map/concatenate | solution.py:37
  86.6 11.5 %shard_map.47 = bf16[384,4096]{1,0:T(8,128)(2,1)} custom-call(bf16[384,4096]{1,0:T(8,128)(2,1)} %bitcast.9, bf16[384,4096]{1,0:T(8,128)(2,1)} %bitcast.6, bf16[384,4096]{1,0:T(8,128)(2,1)} %bitcast.8, bf16[32,128,128]{2,1,0:T(8,128)(2,1)} %pad_maximum_fusion.prefix_ref, f32[1,4096]{1,0:T(1,128)} %bitcast.10), custom_call_target="tpu_custom_call" | custom-call | tf_op jit(solution)/shard_map/pallas_call | solution.py:102
  (3 shorter events, 0.1 us)
Async XLA Ops:
  4.4 29.9 %copy-start = (f32[32,128,128]{2,1,0:T(8,128)S(1)}, f32[32,128,128]{2,1,0:T(8,128)}, u32[]{:S(2)}) copy-start(f32[32,128,128]{2,1,0:T(8,128)} %shard_map.46) | copy-start | bytes 6291460
  5.7 13.7 %collective-permute-start.4 = (f32[8,128,128]{2,1,0:T(8,128)S(1)}, f32[8,128,128]{2,1,0:T(8,128)S(1)}, u32[]{:S(2)}, u32[]{:S(2)}) collective-permute-start(f32[8,128,128]{2,1,0:T(8,128)S(1)} %constant_dynamic-slice_fusion.1), channel_id=1, source_target_pairs={{0,2},{4,6},{8,10},{12,14},{2,0},{6,4},{10,8},{14,12},{1,3},{5,7},... | collective-permute-start | bytes 1572872 | tf_op jit(solution)/shard_map/ppermute | solution.py:24
  20.7 12.8 %collective-permute-start = (f32[8,128,128]{2,1,0:T(8,128)S(1)}, f32[8,128,128]{2,1,0:T(8,128)S(1)}, u32[]{:S(2)}, u32[]{:S(2)}) collective-permute-start(f32[8,128,128]{2,1,0:T(8,128)S(1)} %get-tuple-element.12), channel_id=1, source_target_pairs={{0,2},{4,6},{8,10},{12,14},{2,0},{6,4},{10,8},{14,12},{1,3},{5,7},... | collective-permute-start | bytes 1572872 | tf_op jit(solution)/shard_map/ppermute | solution.py:24
  21.3 13.8 %collective-permute-start.5 = (f32[8,128,128]{2,1,0:T(8,128)S(1)}, f32[8,128,128]{2,1,0:T(8,128)S(1)}, u32[]{:S(2)}, u32[]{:S(2)}) collective-permute-start(f32[8,128,128]{2,1,0:T(8,128)S(1)} %get-tuple-element.11), channel_id=1, source_target_pairs={{0,4},{2,6},{1,5},{3,7},{16,20},{18,22},{17,21},{19,23}} | collective-permute-start | bytes 1572872 | tf_op jit(solution)/shard_map/ppermute | solution.py:29
  33.5 0.8 copy-start.1
  34.4 1.5 %collective-permute-start.1 = (f32[8,128,128]{2,1,0:T(8,128)S(1)}, f32[8,128,128]{2,1,0:T(8,128)S(1)}, u32[]{:S(2)}, u32[]{:S(2)}) collective-permute-start(f32[8,128,128]{2,1,0:T(8,128)S(1)} %dynamic-slice_add_fusion.1), channel_id=1, source_target_pairs={{0,4},{2,6},{1,5},{3,7},{16,20},{18,22},{17,21},{19,23}} | collective-permute-start | bytes 1572872 | tf_op jit(solution)/shard_map/ppermute | solution.py:29
  35.2 1.5 %collective-permute-start.6 = (f32[8,128,128]{2,1,0:T(8,128)S(1)}, f32[8,128,128]{2,1,0:T(8,128)S(1)}, u32[]{:S(2)}, u32[]{:S(2)}) collective-permute-start(f32[8,128,128]{2,1,0:T(8,128)S(1)} %add.62), channel_id=1, source_target_pairs={{4,8},{6,10},{5,9},{7,11},{20,24},{22,26},{21,25},{23,27}} | collective-permute-start | bytes 1572872 | tf_op jit(solution)/shard_map/ppermute | solution.py:29
  36.0 5.3 %copy-start.2 = (f32[2048]{0:T(1024)S(1)}, f32[2048]{0:T(1024)}, u32[]{:S(2)}) copy-start(f32[2048]{0:T(1024)} %param.7) | copy-start | bytes 24580
  36.0 2.9 %collective-permute-start.2 = (f32[8,128,128]{2,1,0:T(8,128)S(1)}, f32[8,128,128]{2,1,0:T(8,128)S(1)}, u32[]{:S(2)}, u32[]{:S(2)}) collective-permute-start(f32[8,128,128]{2,1,0:T(8,128)S(1)} %add.56), channel_id=1, source_target_pairs={{4,8},{6,10},{5,9},{7,11},{20,24},{22,26},{21,25},{23,27}} | collective-permute-start | bytes 1572872 | tf_op jit(solution)/shard_map/ppermute | solution.py:29
  37.6 23.5 %collective-permute-start.7 = (f32[8,128,128]{2,1,0:T(8,128)}, f32[8,128,128]{2,1,0:T(8,128)}, u32[]{:S(2)}, u32[]{:S(2)}) collective-permute-start(f32[8,128,128]{2,1,0:T(8,128)} %get-tuple-element.5), channel_id=1, source_target_pairs={{8,12},{10,14},{9,13},{11,15},{24,28},{26,30},{25,29},{27,31}} | collective-permute-start | bytes 1572872 | tf_op jit(solution)/shard_map/ppermute | solution.py:29
  40.0 32.8 %collective-permute-start.3 = (f32[8,128,128]{2,1,0:T(8,128)}, f32[8,128,128]{2,1,0:T(8,128)}, u32[]{:S(2)}, u32[]{:S(2)}) collective-permute-start(f32[8,128,128]{2,1,0:T(8,128)} %get-tuple-element.7), channel_id=1, source_target_pairs={{8,12},{10,14},{9,13},{11,15},{24,28},{26,30},{25,29},{27,31}} | collective-permute-start | bytes 1572872 | tf_op jit(solution)/shard_map/ppermute | solution.py:29
  41.2 35.5 %collective-permute-start.10 = (f32[2048]{0:T(1024)S(1)}, f32[2048]{0:T(1024)S(1)}, u32[]{:S(2)}, u32[]{:S(2)}) collective-permute-start(f32[2048]{0:T(1024)S(1)} %copy-done.2), channel_id=1, source_target_pairs={{0,1},{1,0},{2,3},{3,2},{4,5},{5,4},{6,7},{7,6},{8,9},{9,8},{10,11... | collective-permute-start | bytes 24584 | tf_op jit(solution)/shard_map/ppermute | solution.py:123
  74.7 7.9 %collective-permute-start.8 = (bf16[8,128,128]{2,1,0:T(8,128)(2,1)S(1)}, bf16[8,128,128]{2,1,0:T(8,128)(2,1)S(1)}, u32[]{:S(2)}, u32[]{:S(2)}) collective-permute-start(bf16[8,128,128]{2,1,0:T(8,128)(2,1)S(1)} %get-tuple-element.10), channel_id=1, source_target_pairs={{0,2},{4,6},{8,10},{12,14},{2,0},{6,4},{10,8},{14,12},{1,3},{5,7},... | collective-permute-start | bytes 786440 | tf_op jit(solution)/shard_map/ppermute | solution.py:32
  75.2 10.2 %collective-permute-start.9 = (bf16[8,128,128]{2,1,0:T(8,128)(2,1)S(1)}, bf16[8,128,128]{2,1,0:T(8,128)(2,1)S(1)}, u32[]{:S(2)}, u32[]{:S(2)}) collective-permute-start(bf16[8,128,128]{2,1,0:T(8,128)(2,1)S(1)} %get-tuple-element.9), channel_id=1, source_target_pairs={{0,2},{4,6},{8,10},{12,14},{2,0},{6,4},{10,8},{14,12},{1,3},{5,7},... | collective-permute-start | bytes 786440 | tf_op jit(solution)/shard_map/ppermute | solution.py:32

commit v15 on v14

--- a/solution.py
+++ b/solution.py
@@ -30,11 +30,7 @@
         keeps.append((carried + jnp.where(first, 0.0, got)).astype(jnp.bfloat16))
         send = (carried + jnp.where(first, mine, 0.0)).astype(jnp.bfloat16)
         backs.append(lax.ppermute(send, axis, swap))
-    keep = jnp.concatenate(keeps, axis=0)
-    back = jnp.concatenate(backs, axis=0)
-    low = jnp.where(first, keep, back)
-    high = jnp.where(first, back, keep)
-    return jnp.concatenate([low, high], axis=0)
+    return jnp.concatenate(keeps, axis=0), jnp.concatenate(backs, axis=0)
 
 
 def state_kernel(key_ref, val_ref, out_ref):
@@ -60,10 +56,12 @@
     )(keyset, valset)
 
 
-def attend_kernel(query_ref, key_ref, val_ref, prefix_ref, gain_ref, out_ref, acc_ref, sumsq_ref):
+def attend_kernel(mine_ref, query_ref, key_ref, val_ref, keep_ref, back_ref, gain_ref, out_ref, acc_ref,
+                  sumsq_ref):
     step = pl.program_id(0)
     row_count, width = query_ref.shape
-    heads, head_size, _ = prefix_ref.shape
+    heads, head_size, _ = keep_ref.shape
+    own = step // (pl.num_programs(0) // 2) == mine_ref[0]
     causal = (lax.broadcasted_iota(jnp.int32, (row_count, row_count), 0)
               >= lax.broadcasted_iota(jnp.int32, (row_count, row_count), 1))
 
@@ -79,7 +77,8 @@
                                  preferred_element_type=jnp.float32)
         weights = jnp.where(causal, scores, 0.0).astype(jnp.bfloat16)
         lhs = jnp.concatenate([weights, query], axis=1)
-        rhs = jnp.concatenate([val_ref[:, cols], prefix_ref[head]], axis=0)
+        prefix = jnp.where(own, keep_ref[head], back_ref[head])
+        rhs = jnp.concatenate([val_ref[:, cols], prefix], axis=0)
         attended = jnp.dot(lhs, rhs, preferred_element_type=jnp.float32)
         acc_ref[step, :, cols] = attended
         sumsq = sumsq + attended * attended
@@ -94,24 +93,25 @@
             out_ref[:, cols] = (acc_ref[part] * scale * gain_ref[:, cols]).astype(out_ref.dtype)
 
 
-def attend_of(query, keyset, valset, prefix_bf, full_gain, group):
+def attend_of(query, keyset, valset, keep, back, mine_at, full_gain, group):
     row_count, feat_count = query.shape
     head_size = feat_count // H
     width = group * head_size
     steps = H // group
+    spec = pl.BlockSpec((row_count, width), lambda g, at: (0, g))
+    half_spec = pl.BlockSpec((group, head_size, head_size), lambda g, at: (g % (steps // 2), 0, 0))
     return pl.pallas_call(
         attend_kernel,
-        grid=(steps,),
-        in_specs=[pl.BlockSpec((row_count, width), lambda g: (0, g)),
-                  pl.BlockSpec((row_count, width), lambda g: (0, g)),
-                  pl.BlockSpec((row_count, width), lambda g: (0, g)),
-                  pl.BlockSpec((group, head_size, head_size), lambda g: (g, 0, 0)),
-                  pl.BlockSpec((1, feat_count), lambda g: (0, 0))],
-        out_specs=pl.BlockSpec((row_count, feat_count), lambda g: (0, 0)),
+        grid_spec=pltpu.PrefetchScalarGridSpec(
+            num_scalar_prefetch=1,
+            grid=(steps,),
+            in_specs=[spec, spec, spec, half_spec, half_spec,
+                      pl.BlockSpec((1, feat_count), lambda g, at: (0, 0))],
+            out_specs=pl.BlockSpec((row_count, feat_count), lambda g, at: (0, 0)),
+            scratch_shapes=[pltpu.VMEM((steps, row_count, width), jnp.float32),
+                            pltpu.VMEM((row_count, head_size), jnp.float32)]),
         out_shape=jax.ShapeDtypeStruct((row_count, feat_count), jnp.bfloat16),
-        scratch_shapes=[pltpu.VMEM((steps, row_count, width), jnp.float32),
-                        pltpu.VMEM((row_count, head_size), jnp.float32)],
-    )(query, keyset, valset, prefix_bf, full_gain)
+    )(jnp.reshape(mine_at, (1,)).astype(jnp.int32), query, keyset, valset, keep, back, full_gain)
 
 
 def shards(query_rows, key_rows, value_rows, gain):
@@ -128,8 +128,8 @@
     keyset = key_rows.reshape(seq_count * row_count, feat_count)
     valset = value_rows.reshape(seq_count * row_count, feat_count)
     state_terms = state_terms_of(keyset, valset, 16)
-    prefix_bf = pair_chain_prefix(state_terms, "ctx", 2)
-    normed = attend_of(query, keyset, valset, prefix_bf, full_gain, 8)
+    keep, back = pair_chain_prefix(state_terms, "ctx", 4)
+    normed = attend_of(query, keyset, valset, keep, back, lax.axis_index("ctx") % 2, full_gain, 8)
     return normed.reshape(seq_count, row_count, feat_count)
 
 

time: 98.5 us -> 95.8 us (0.973)
  waiting for transfers between devices: 64.2 us -> 50 us
  starting transfers between devices: 8.62 us -> 17.9 us
  other arithmetic: 7.07 us -> 9.86 us
    ppermute x6 -> x12, waiting for transfers between devices: 31.5 us -> 21.6 us  [pair_chain_prefix(): carried = carried + lax.ppermute(carried + total, axis, links)]
    ppermute x6 -> x12, starting transfers between devices: 5.32 us -> 10.7 us  [pair_chain_prefix(): carried = carried + lax.ppermute(carried + total, axis, links)]
    ppermute x2 -> x4, waiting for transfers between devices: 7.96 us -> 4.31 us  [pair_chain_prefix(): backs.append(lax.ppermute(send, axis, swap))]
    ppermute x2 -> x4, starting transfers between devices: 2.09 us -> 4.12 us  [pair_chain_prefix(): backs.append(lax.ppermute(send, axis, swap))]
    ppermute x2 -> x4, starting transfers between devices: 1.13 us -> 3.09 us  [pair_chain_prefix(): got = lax.ppermute(other_all[piece * step:(piece + 1) * step], axis, swap)]
    ppermute x2 -> x4, waiting for transfers between devices: 24.7 us -> 22.9 us  [pair_chain_prefix(): got = lax.ppermute(other_all[piece * step:(piece + 1) * step], axis, swap)]
    add x4 -> x8, other arithmetic: 2.08 us -> 3.41 us  [pair_chain_prefix(): carried = carried + lax.ppermute(carried + total, axis, links)]
    ppermute x1, waiting for transfers between devices: 0.01 us -> 1.15 us  [shards(): other_gain = lax.ppermute(gain, 'dp', pair)]
  transfers between devices with their start and end apart: 11 -> 21, of which waited for: 6 -> 13; matrix products, arithmetic and copies ran while one was open for 5% -> 5% of each run, Pallas kernels for 0% -> 0%
where the time goes in v15:
time: 95.8 us; the launch traced here: 95.2 us
  waiting for transfers between devices  50 us (52%)
  starting transfers between devices  17.9 us (19%)
  Pallas kernels  16.1 us (17%)
  other arithmetic  9.86 us (10%)
  local copies, waits for them, and re-layouts  1.13 us (1%)
    ppermute x4, waiting for transfers between devices, pair_chain_prefix(): got = lax.ppermute(other_all[piece * step:(piece + 1) * step], axis, swap)  22.9 us
    ppermute x12, waiting for transfers between devices, pair_chain_prefix(): carried = carried + lax.ppermute(carried + total, axis, links)  21.6 us
    pallas_call x1, Pallas kernels, attend_of(): pl.pallas_call(attend_kernel, grid_spec=pltpu.PrefetchScalarGridSpec(num_...  11.6 us
    ppermute x12, starting transfers between devices, pair_chain_prefix(): carried = carried + lax.ppermute(carried + total, axis, links)  10.7 us
    pallas_call x1, Pallas kernels, state_terms_of(): pl.pallas_call(state_kernel, grid=(H // group,), in_specs=[pl.BlockSpec((...  4.45 us
    ppermute x4, waiting for transfers between devices, pair_chain_prefix(): backs.append(lax.ppermute(send, axis, swap))  4.31 us
    ppermute x4, starting transfers between devices, pair_chain_prefix(): backs.append(lax.ppermute(send, axis, swap))  4.12 us
    add x8, other arithmetic, pair_chain_prefix(): carried = carried + lax.ppermute(carried + total, axis, links)  3.41 us
  transfers between devices with their start and end apart: 21, of which 13 were waited for; matrix products, arithmetic and copies ran while one was open for 5% of the time, Pallas kernels for 0%

profile of v15, /device:TPU:30, one launch (start us, length us, event | category | flops | bytes accessed | tf_op | source)
XLA Modules:
  0.0 95.2 jit_solution(4543793963391994738)
XLA Ops:
  0.0 4.4 %shard_map.46 = f32[32,128,128]{2,1,0:T(8,128)} custom-call(bf16[384,4096]{1,0:T(8,128)(2,1)} %bitcast.6, bf16[384,4096]{1,0:T(8,128)(2,1)} %bitcast.8), custom_call_target="tpu_custom_call" | custom-call | tf_op jit(solution)/shard_map/pallas_call | solution.py:49
  4.5 1.1 %constant_dynamic-slice_fusion.2 = f32[4,128,128]{2,1,0:T(8,128)S(1)} fusion(f32[32,128,128]{2,1,0:T(8,128)} %shard_map.46, s32[]{:T(128)S(6)} %select_n.67), kind=kLoop, calls=%fused_computation.19 | loop fusion | bytes 524292 | tf_op jit(solution)/shard_map/slice | solution.py:24
  5.6 0.6 collective-permute-start
  6.1 7.5 %collective-permute-done = f32[4,128,128]{2,1,0:T(8,128)S(1)} collective-permute-done((f32[4,128,128]{2,1,0:T(8,128)S(1)}, f32[4,128,128]{2,1,0:T(8,128)S(1)}, u32[]{:S(2)}, u32[]{:S(2)}) %collective-permute-start) | collective-permute-done | bytes 262176 | tf_op jit(solution)/shard_map/ppermute | solution.py:24
  13.7 2.2 %dynamic-slice_add_fusion.3 = (f32[4,128,128]{2,1,0:T(8,128)S(1)}, f32[4,128,128]{2,1,0:T(8,128)S(1)}, f32[4,128,128]{2,1,0:T(8,128)}, f32[4,128,128]{2,1,0:T(8,128)}) fusion(f32[4,128,128]{2,1,0:T(8,128)S(1)} %collective-permute-done, f32[32,128,128]{2,1,0:T(8,128)} %shard_map.46, s32[]{:T(128)S(6)} %select_n.66, s32[]{:T(128)S(6)} %add.129, s32[]{:T(128)S(6)} %add.127, ...), kind=kLoop, calls=%fused_computation.13 | loop fusion | flops 65536 | bytes 2359312 | tf_op jit(solution)/shard_map/add | solution.py:25
  15.9 0.5 collective-permute-start.12
  16.4 1.5 %collective-permute-start.4 = (f32[4,128,128]{2,1,0:T(8,128)}, f32[4,128,128]{2,1,0:T(8,128)S(1)}, u32[]{:S(2)}, u32[]{:S(2)}) collective-permute-start(f32[4,128,128]{2,1,0:T(8,128)} %get-tuple-element.19), channel_id=1, source_target_pairs={{0,2},{4,6},{8,10},{12,14},{2,0},{6,4},{10,8},{14,12},{1,3},{5,7},... | collective-permute-start | bytes 786440 | tf_op jit(solution)/shard_map/ppermute | solution.py:24
  17.9 0.5 collective-permute-start.8
  18.4 0.7 collective-permute-start.1
  19.1 6.2 %collective-permute-done.12 = f32[4,128,128]{2,1,0:T(8,128)S(1)} collective-permute-done((f32[4,128,128]{2,1,0:T(8,128)}, f32[4,128,128]{2,1,0:T(8,128)S(1)}, u32[]{:S(2)}, u32[]{:S(2)}) %collective-permute-start.12) | collective-permute-done | bytes 262176 | tf_op jit(solution)/shard_map/ppermute | solution.py:24
  25.3 5.6 %collective-permute-done.4 = f32[4,128,128]{2,1,0:T(8,128)S(1)} collective-permute-done((f32[4,128,128]{2,1,0:T(8,128)}, f32[4,128,128]{2,1,0:T(8,128)S(1)}, u32[]{:S(2)}, u32[]{:S(2)}) %collective-permute-start.4) | collective-permute-done | bytes 262176 | tf_op jit(solution)/shard_map/ppermute | solution.py:24
  30.9 3.5 %collective-permute-done.8 = f32[4,128,128]{2,1,0:T(8,128)S(1)} collective-permute-done((f32[4,128,128]{2,1,0:T(8,128)S(1)}, f32[4,128,128]{2,1,0:T(8,128)S(1)}, u32[]{:S(2)}, u32[]{:S(2)}) %collective-permute-start.8) | collective-permute-done | bytes 262176 | tf_op jit(solution)/shard_map/ppermute | solution.py:24
  34.5 0.1 dynamic-slice_add_fusion.2
  34.6 0.7 collective-permute-start.13
  35.2 0.7 collective-permute-start.9
  35.9 0.7 collective-permute-start.5
  36.6 0.0 collective-permute-done.1
  36.7 0.7 collective-permute-start.2
  37.4 0.7 collective-permute-start.14
  38.1 0.7 collective-permute-start.10
  38.9 0.7 collective-permute-start.6
  39.6 0.8 fusion
  40.3 1.4 %collective-permute-start.3 = (f32[4,128,128]{2,1,0:T(8,128)}, f32[4,128,128]{2,1,0:T(8,128)}, u32[]{:S(2)}, u32[]{:S(2)}) collective-permute-start(f32[4,128,128]{2,1,0:T(8,128)} %get-tuple-element.5), channel_id=1, source_target_pairs={{8,12},{10,14},{9,13},{11,15},{24,28},{26,30},{25,29},{27,31}} | collective-permute-start | bytes 786440 | tf_op jit(solution)/shard_map/ppermute | solution.py:29
  41.8 0.8 fusion.3
  42.5 1.3 %collective-permute-start.15 = (f32[4,128,128]{2,1,0:T(8,128)}, f32[4,128,128]{2,1,0:T(8,128)}, u32[]{:S(2)}, u32[]{:S(2)}) collective-permute-start(f32[4,128,128]{2,1,0:T(8,128)} %get-tuple-element.11), channel_id=1, source_target_pairs={{8,12},{10,14},{9,13},{11,15},{24,28},{26,30},{25,29},{27,31}} | collective-permute-start | bytes 786440 | tf_op jit(solution)/shard_map/ppermute | solution.py:29
  43.8 0.9 fusion.2
  44.7 1.3 %collective-permute-start.11 = (f32[4,128,128]{2,1,0:T(8,128)}, f32[4,128,128]{2,1,0:T(8,128)}, u32[]{:S(2)}, u32[]{:S(2)}) collective-permute-start(f32[4,128,128]{2,1,0:T(8,128)} %get-tuple-element.9), channel_id=1, source_target_pairs={{8,12},{10,14},{9,13},{11,15},{24,28},{26,30},{25,29},{27,31}} | collective-permute-start | bytes 786440 | tf_op jit(solution)/shard_map/ppermute | solution.py:29
  46.0 0.9 fusion.1
  46.9 1.3 %collective-permute-start.7 = (f32[4,128,128]{2,1,0:T(8,128)}, f32[4,128,128]{2,1,0:T(8,128)}, u32[]{:S(2)}, u32[]{:S(2)}) collective-permute-start(f32[4,128,128]{2,1,0:T(8,128)} %get-tuple-element.7), channel_id=1, source_target_pairs={{8,12},{10,14},{9,13},{11,15},{24,28},{26,30},{25,29},{27,31}} | collective-permute-start | bytes 786440 | tf_op jit(solution)/shard_map/ppermute | solution.py:29
  48.2 0.1 collective-permute-start.20
  48.2 1.1 %collective-permute-done.20 = f32[2048]{0:T(1024)S(1)} collective-permute-done((f32[2048]{0:T(1024)S(1)}, f32[2048]{0:T(1024)S(1)}, u32[]{:S(2)}, u32[]{:S(2)}) %collective-permute-start.20) | collective-permute-done | bytes 8224 | tf_op jit(solution)/shard_map/ppermute | solution.py:123
  49.4 7.6 %collective-permute-done.3 = f32[4,128,128]{2,1,0:T(8,128)} collective-permute-done((f32[4,128,128]{2,1,0:T(8,128)}, f32[4,128,128]{2,1,0:T(8,128)}, u32[]{:S(2)}, u32[]{:S(2)}) %collective-permute-start.3) | collective-permute-done | bytes 262176 | tf_op jit(solution)/shard_map/ppermute | solution.py:29
  57.0 5.5 %collective-permute-done.15 = f32[4,128,128]{2,1,0:T(8,128)} collective-permute-done((f32[4,128,128]{2,1,0:T(8,128)}, f32[4,128,128]{2,1,0:T(8,128)}, u32[]{:S(2)}, u32[]{:S(2)}) %collective-permute-start.15) | collective-permute-done | bytes 262176 | tf_op jit(solution)/shard_map/ppermute | solution.py:29
  62.5 5.7 %collective-permute-done.11 = f32[4,128,128]{2,1,0:T(8,128)} collective-permute-done((f32[4,128,128]{2,1,0:T(8,128)}, f32[4,128,128]{2,1,0:T(8,128)}, u32[]{:S(2)}, u32[]{:S(2)}) %collective-permute-start.11) | collective-permute-done | bytes 262176 | tf_op jit(solution)/shard_map/ppermute | solution.py:29
  68.1 2.8 %collective-permute-done.7 = f32[4,128,128]{2,1,0:T(8,128)} collective-permute-done((f32[4,128,128]{2,1,0:T(8,128)}, f32[4,128,128]{2,1,0:T(8,128)}, u32[]{:S(2)}, u32[]{:S(2)}) %collective-permute-start.7) | collective-permute-done | bytes 262176 | tf_op jit(solution)/shard_map/ppermute | solution.py:29
  71.0 1.8 %add_convert_fusion.3 = (bf16[4,128,128]{2,1,0:T(8,128)(2,1)S(1)}, bf16[4,128,128]{2,1,0:T(8,128)(2,1)S(1)}, bf16[4,128,128]{2,1,0:T(8,128)(2,1)S(1)}, bf16[4,12...) fusion(f32[32,128,128]{2,1,0:T(8,128)S(1)} %copy-done, ...), kind=kLoop, calls=%fused_computation.5 | loop fusion | flops 1835008 | bytes 5242897 | tf_op jit(solution)/shard_map/convert_element_type | solution.py:31
  72.8 0.5 collective-permute-start.16
  73.3 1.6 %collective-permute-start.17 = (bf16[4,128,128]{2,1,0:T(8,128)(2,1)S(1)}, bf16[4,128,128]{2,1,0:T(8,128)(2,1)S(1)}, u32[]{:S(2)}, u32[]{:S(2)}) collective-permute-start(bf16[4,128,128]{2,1,0:T(8,128)(2,1)S(1)} %get-tuple-element.14), channel_id=1, source_target_pairs={{0,2},{4,6},{8,10},{12,14},{2,0},{6,4},{10,8},{14,12},{1,3},{5,7},... | collective-permute-start | bytes 393224 | tf_op jit(solution)/shard_map/ppermute | solution.py:32
  74.9 0.4 collective-permute-start.18
  75.3 1.6 %collective-permute-start.19 = (bf16[4,128,128]{2,1,0:T(8,128)(2,1)S(1)}, bf16[4,128,128]{2,1,0:T(8,128)(2,1)S(1)}, u32[]{:S(2)}, u32[]{:S(2)}) collective-permute-start(bf16[4,128,128]{2,1,0:T(8,128)(2,1)S(1)} %get-tuple-element.16), channel_id=1, source_target_pairs={{0,2},{4,6},{8,10},{12,14},{2,0},{6,4},{10,8},{14,12},{1,3},{5,7},... | collective-permute-start | bytes 393224 | tf_op jit(solution)/shard_map/ppermute | solution.py:32
  76.9 0.6 pad_maximum_fusion.2
  77.5 0.9 pad_maximum_fusion.keep_ref
  78.4 0.1 collective-permute-done.16
  78.5 1.4 %collective-permute-done.17 = bf16[4,128,128]{2,1,0:T(8,128)(2,1)S(1)} collective-permute-done((bf16[4,128,128]{2,1,0:T(8,128)(2,1)S(1)}, bf16[4,128,128]{2,1,0:T(8,128)(2,1)S(1)}, u32[]{:S(2)}, u32[]{:S(2)}) %collective-permute-start.17) | collective-permute-done | bytes 131104 | tf_op jit(solution)/shard_map/ppermute | solution.py:32
  79.9 1.4 %collective-permute-done.18 = bf16[4,128,128]{2,1,0:T(8,128)(2,1)S(1)} collective-permute-done((bf16[4,128,128]{2,1,0:T(8,128)(2,1)S(1)}, bf16[4,128,128]{2,1,0:T(8,128)(2,1)S(1)}, u32[]{:S(2)}, u32[]{:S(2)}) %collective-permute-start.18) | collective-permute-done | bytes 131104 | tf_op jit(solution)/shard_map/ppermute | solution.py:32
  81.3 1.4 %collective-permute-done.19 = bf16[4,128,128]{2,1,0:T(8,128)(2,1)S(1)} collective-permute-done((bf16[4,128,128]{2,1,0:T(8,128)(2,1)S(1)}, bf16[4,128,128]{2,1,0:T(8,128)(2,1)S(1)}, u32[]{:S(2)}, u32[]{:S(2)}) %collective-permute-start.19) | collective-permute-done | bytes 131104 | tf_op jit(solution)/shard_map/ppermute | solution.py:32
  82.7 0.9 pad_maximum_fusion.1.back_ref
  83.6 11.6 %shard_map.47 = bf16[384,4096]{1,0:T(8,128)(2,1)} custom-call(s32[1]{0:T(128)} %bitcast.mine_ref, bf16[384,4096]{1,0:T(8,128)(2,1)} %bitcast.10, bf16[384,4096]{1,0:T(8,128)(2,1)} %bitcast.7, bf16[384,4096]{1,0:T(8,128)(2,1)} %bitcast.9, bf16[16,128,128]{2,1,0:T(8,128)(2,1)} %pad_maximum_fusion.keep_ref, bf16[16,128,128]{2,1,0:T(8,128)(2,1)} %pad_maximum_fusion.1.back_ref, ...), custom_call_target="tpu_custom_call" | custom-call | tf_op jit(solution)/shard_map/pallas_call | solution.py:103
  (18 shorter events, 0.2 us)
Async XLA Ops:
  4.4 30.0 %copy-start = (f32[32,128,128]{2,1,0:T(8,128)S(1)}, f32[32,128,128]{2,1,0:T(8,128)}, u32[]{:S(2)}) copy-start(f32[32,128,128]{2,1,0:T(8,128)} %shard_map.46) | copy-start | bytes 6291460
  5.6 8.1 %collective-permute-start = (f32[4,128,128]{2,1,0:T(8,128)S(1)}, f32[4,128,128]{2,1,0:T(8,128)S(1)}, u32[]{:S(2)}, u32[]{:S(2)}) collective-permute-start(f32[4,128,128]{2,1,0:T(8,128)S(1)} %constant_dynamic-slice_fusion.2), channel_id=1, source_target_pairs={{0,2},{4,6},{8,10},{12,14},{2,0},{6,4},{10,8},{14,12},{1,3},{5,7},... | collective-permute-start | bytes 786440 | tf_op jit(solution)/shard_map/ppermute | solution.py:24
  13.7 2.2 %copy-start.1 = (f32[4,128,128]{2,1,0:T(8,128)}, f32[4,128,128]{2,1,0:T(8,128)S(1)}, u32[]{:S(2)}) copy-start(f32[4,128,128]{2,1,0:T(8,128)S(1)} %collective-permute-done) | copy-start | bytes 786436
  15.9 9.5 %collective-permute-start.12 = (f32[4,128,128]{2,1,0:T(8,128)}, f32[4,128,128]{2,1,0:T(8,128)S(1)}, u32[]{:S(2)}, u32[]{:S(2)}) collective-permute-start(f32[4,128,128]{2,1,0:T(8,128)} %get-tuple-element.20), channel_id=1, source_target_pairs={{0,2},{4,6},{8,10},{12,14},{2,0},{6,4},{10,8},{14,12},{1,3},{5,7},... | collective-permute-start | bytes 786440 | tf_op jit(solution)/shard_map/ppermute | solution.py:24
  16.4 14.6 %collective-permute-start.4 = (f32[4,128,128]{2,1,0:T(8,128)}, f32[4,128,128]{2,1,0:T(8,128)S(1)}, u32[]{:S(2)}, u32[]{:S(2)}) collective-permute-start(f32[4,128,128]{2,1,0:T(8,128)} %get-tuple-element.19), channel_id=1, source_target_pairs={{0,2},{4,6},{8,10},{12,14},{2,0},{6,4},{10,8},{14,12},{1,3},{5,7},... | collective-permute-start | bytes 786440 | tf_op jit(solution)/shard_map/ppermute | solution.py:24
  17.9 16.6 %collective-permute-start.8 = (f32[4,128,128]{2,1,0:T(8,128)S(1)}, f32[4,128,128]{2,1,0:T(8,128)S(1)}, u32[]{:S(2)}, u32[]{:S(2)}) collective-permute-start(f32[4,128,128]{2,1,0:T(8,128)S(1)} %get-tuple-element.18), channel_id=1, source_target_pairs={{0,2},{4,6},{8,10},{12,14},{2,0},{6,4},{10,8},{14,12},{1,3},{5,7},... | collective-permute-start | bytes 786440 | tf_op jit(solution)/shard_map/ppermute | solution.py:24
  18.4 18.2 %collective-permute-start.1 = (f32[4,128,128]{2,1,0:T(8,128)S(1)}, f32[4,128,128]{2,1,0:T(8,128)S(1)}, u32[]{:S(2)}, u32[]{:S(2)}) collective-permute-start(f32[4,128,128]{2,1,0:T(8,128)S(1)} %get-tuple-element.17), channel_id=1, source_target_pairs={{0,4},{2,6},{1,5},{3,7},{16,20},{18,22},{17,21},{19,23}} | collective-permute-start | bytes 786440 | tf_op jit(solution)/shard_map/ppermute | solution.py:29
  34.6 2.8 %collective-permute-start.13 = (f32[4,128,128]{2,1,0:T(8,128)S(1)}, f32[4,128,128]{2,1,0:T(8,128)S(1)}, u32[]{:S(2)}, u32[]{:S(2)}) collective-permute-start(f32[4,128,128]{2,1,0:T(8,128)S(1)} %get-tuple-element.23), channel_id=1, source_target_pairs={{0,4},{2,6},{1,5},{3,7},{16,20},{18,22},{17,21},{19,23}} | collective-permute-start | bytes 786440 | tf_op jit(solution)/shard_map/ppermute | solution.py:29
  35.2 2.8 %collective-permute-start.9 = (f32[4,128,128]{2,1,0:T(8,128)S(1)}, f32[4,128,128]{2,1,0:T(8,128)S(1)}, u32[]{:S(2)}, u32[]{:S(2)}) collective-permute-start(f32[4,128,128]{2,1,0:T(8,128)S(1)} %get-tuple-element.22), channel_id=1, source_target_pairs={{0,4},{2,6},{1,5},{3,7},{16,20},{18,22},{17,21},{19,23}} | collective-permute-start | bytes 786440 | tf_op jit(solution)/shard_map/ppermute | solution.py:29
  35.9 2.9 %collective-permute-start.5 = (f32[4,128,128]{2,1,0:T(8,128)S(1)}, f32[4,128,128]{2,1,0:T(8,128)S(1)}, u32[]{:S(2)}, u32[]{:S(2)}) collective-permute-start(f32[4,128,128]{2,1,0:T(8,128)S(1)} %get-tuple-element.21), channel_id=1, source_target_pairs={{0,4},{2,6},{1,5},{3,7},{16,20},{18,22},{17,21},{19,23}} | collective-permute-start | bytes 786440 | tf_op jit(solution)/shard_map/ppermute | solution.py:29
  36.7 2.9 %collective-permute-start.2 = (f32[4,128,128]{2,1,0:T(8,128)S(1)}, f32[4,128,128]{2,1,0:T(8,128)S(1)}, u32[]{:S(2)}, u32[]{:S(2)}) collective-permute-start(f32[4,128,128]{2,1,0:T(8,128)S(1)} %add.99), channel_id=1, source_target_pairs={{4,8},{6,10},{5,9},{7,11},{20,24},{22,26},{21,25},{23,27}} | collective-permute-start | bytes 786440 | tf_op jit(solution)/shard_map/ppermute | solution.py:29
  37.4 4.3 %collective-permute-start.14 = (f32[4,128,128]{2,1,0:T(8,128)S(1)}, f32[4,128,128]{2,1,0:T(8,128)S(1)}, u32[]{:S(2)}, u32[]{:S(2)}) collective-permute-start(f32[4,128,128]{2,1,0:T(8,128)S(1)} %add.117), channel_id=1, source_target_pairs={{4,8},{6,10},{5,9},{7,11},{20,24},{22,26},{21,25},{23,27}} | collective-permute-start | bytes 786440 | tf_op jit(solution)/shard_map/ppermute | solution.py:29
  38.1 5.7 %collective-permute-start.10 = (f32[4,128,128]{2,1,0:T(8,128)S(1)}, f32[4,128,128]{2,1,0:T(8,128)S(1)}, u32[]{:S(2)}, u32[]{:S(2)}) collective-permute-start(f32[4,128,128]{2,1,0:T(8,128)S(1)} %add.111), channel_id=1, source_target_pairs={{4,8},{6,10},{5,9},{7,11},{20,24},{22,26},{21,25},{23,27}} | collective-permute-start | bytes 786440 | tf_op jit(solution)/shard_map/ppermute | solution.py:29
  38.9 7.1 %collective-permute-start.6 = (f32[4,128,128]{2,1,0:T(8,128)S(1)}, f32[4,128,128]{2,1,0:T(8,128)S(1)}, u32[]{:S(2)}, u32[]{:S(2)}) collective-permute-start(f32[4,128,128]{2,1,0:T(8,128)S(1)} %add.105), channel_id=1, source_target_pairs={{4,8},{6,10},{5,9},{7,11},{20,24},{22,26},{21,25},{23,27}} | collective-permute-start | bytes 786440 | tf_op jit(solution)/shard_map/ppermute | solution.py:29
  40.3 7.8 %copy-start.2 = (f32[2048]{0:T(1024)S(1)}, f32[2048]{0:T(1024)}, u32[]{:S(2)}) copy-start(f32[2048]{0:T(1024)} %param.7) | copy-start | bytes 24580
  40.3 16.6 %collective-permute-start.3 = (f32[4,128,128]{2,1,0:T(8,128)}, f32[4,128,128]{2,1,0:T(8,128)}, u32[]{:S(2)}, u32[]{:S(2)}) collective-permute-start(f32[4,128,128]{2,1,0:T(8,128)} %get-tuple-element.5), channel_id=1, source_target_pairs={{8,12},{10,14},{9,13},{11,15},{24,28},{26,30},{25,29},{27,31}} | collective-permute-start | bytes 786440 | tf_op jit(solution)/shard_map/ppermute | solution.py:29
  42.5 19.9 %collective-permute-start.15 = (f32[4,128,128]{2,1,0:T(8,128)}, f32[4,128,128]{2,1,0:T(8,128)}, u32[]{:S(2)}, u32[]{:S(2)}) collective-permute-start(f32[4,128,128]{2,1,0:T(8,128)} %get-tuple-element.11), channel_id=1, source_target_pairs={{8,12},{10,14},{9,13},{11,15},{24,28},{26,30},{25,29},{27,31}} | collective-permute-start | bytes 786440 | tf_op jit(solution)/shard_map/ppermute | solution.py:29
  44.7 23.5 %collective-permute-start.11 = (f32[4,128,128]{2,1,0:T(8,128)}, f32[4,128,128]{2,1,0:T(8,128)}, u32[]{:S(2)}, u32[]{:S(2)}) collective-permute-start(f32[4,128,128]{2,1,0:T(8,128)} %get-tuple-element.9), channel_id=1, source_target_pairs={{8,12},{10,14},{9,13},{11,15},{24,28},{26,30},{25,29},{27,31}} | collective-permute-start | bytes 786440 | tf_op jit(solution)/shard_map/ppermute | solution.py:29
  46.9 24.1 %collective-permute-start.7 = (f32[4,128,128]{2,1,0:T(8,128)}, f32[4,128,128]{2,1,0:T(8,128)}, u32[]{:S(2)}, u32[]{:S(2)}) collective-permute-start(f32[4,128,128]{2,1,0:T(8,128)} %get-tuple-element.7), channel_id=1, source_target_pairs={{8,12},{10,14},{9,13},{11,15},{24,28},{26,30},{25,29},{27,31}} | collective-permute-start | bytes 786440 | tf_op jit(solution)/shard_map/ppermute | solution.py:29
  48.2 1.2 %collective-permute-start.20 = (f32[2048]{0:T(1024)S(1)}, f32[2048]{0:T(1024)S(1)}, u32[]{:S(2)}, u32[]{:S(2)}) collective-permute-start(f32[2048]{0:T(1024)S(1)} %copy-done.2), channel_id=1, source_target_pairs={{0,1},{1,0},{2,3},{3,2},{4,5},{5,4},{6,7},{7,6},{8,9},{9,8},{10,11... | collective-permute-start | bytes 24584 | tf_op jit(solution)/shard_map/ppermute | solution.py:123
  72.8 5.7 %collective-permute-start.16 = (bf16[4,128,128]{2,1,0:T(8,128)(2,1)S(1)}, bf16[4,128,128]{2,1,0:T(8,128)(2,1)S(1)}, u32[]{:S(2)}, u32[]{:S(2)}) collective-permute-start(bf16[4,128,128]{2,1,0:T(8,128)(2,1)S(1)} %get-tuple-element.13), channel_id=1, source_target_pairs={{0,2},{4,6},{8,10},{12,14},{2,0},{6,4},{10,8},{14,12},{1,3},{5,7},... | collective-permute-start | bytes 393224 | tf_op jit(solution)/shard_map/ppermute | solution.py:32
  73.3 6.6 %collective-permute-start.17 = (bf16[4,128,128]{2,1,0:T(8,128)(2,1)S(1)}, bf16[4,128,128]{2,1,0:T(8,128)(2,1)S(1)}, u32[]{:S(2)}, u32[]{:S(2)}) collective-permute-start(bf16[4,128,128]{2,1,0:T(8,128)(2,1)S(1)} %get-tuple-element.14), channel_id=1, source_target_pairs={{0,2},{4,6},{8,10},{12,14},{2,0},{6,4},{10,8},{14,12},{1,3},{5,7},... | collective-permute-start | bytes 393224 | tf_op jit(solution)/shard_map/ppermute | solution.py:32
  74.9 6.4 %collective-permute-start.18 = (bf16[4,128,128]{2,1,0:T(8,128)(2,1)S(1)}, bf16[4,128,128]{2,1,0:T(8,128)(2,1)S(1)}, u32[]{:S(2)}, u32[]{:S(2)}) collective-permute-start(bf16[4,128,128]{2,1,0:T(8,128)(2,1)S(1)} %get-tuple-element.15), channel_id=1, source_target_pairs={{0,2},{4,6},{8,10},{12,14},{2,0},{6,4},{10,8},{14,12},{1,3},{5,7},... | collective-permute-start | bytes 393224 | tf_op jit(solution)/shard_map/ppermute | solution.py:32
  75.3 7.4 %collective-permute-start.19 = (bf16[4,128,128]{2,1,0:T(8,128)(2,1)S(1)}, bf16[4,128,128]{2,1,0:T(8,128)(2,1)S(1)}, u32[]{:S(2)}, u32[]{:S(2)}) collective-permute-start(bf16[4,128,128]{2,1,0:T(8,128)(2,1)S(1)} %get-tuple-element.16), channel_id=1, source_target_pairs={{0,2},{4,6},{8,10},{12,14},{2,0},{6,4},{10,8},{14,12},{1,3},{5,7},... | collective-permute-start | bytes 393224 | tf_op jit(solution)/shard_map/ppermute | solution.py:32

commit v16 on v15

--- a/solution.py
+++ b/solution.py
@@ -10,26 +10,40 @@
 
 def pair_chain_prefix(terms, axis, pieces):
     count = lax.axis_size(axis)
-    mine_at = lax.axis_index(axis) % 2
+    place = lax.axis_index(axis)
+    mine_at = place % 2
     first = mine_at == 0
+    last = count // 2 - 1
+    at_last = place // 2 == last
     half = terms.shape[0] // 2
-    pairs = count // 2
     mine_all = lax.dynamic_slice_in_dim(terms, mine_at * half, half, 0)
     other_all = lax.dynamic_slice_in_dim(terms, (1 - mine_at) * half, half, 0)
-    swap = [(2 * i, 2 * i + 1) for i in range(pairs)] + [(2 * i + 1, 2 * i) for i in range(pairs)]
+    swap = [(2 * i, 2 * i + 1) for i in range(last)] + [(2 * i + 1, 2 * i) for i in range(last)]
+    behind = 2 * (last - 1)
+    kv_back = (lax.ppermute(mine_all, axis, [(2 * last, behind)])
+               + lax.ppermute(other_all, axis, [(2 * last, behind + 1)]))
+    ahead = [(behind, 2 * last), (behind + 1, 2 * last + 1)]
+    across = [(behind, 2 * last + 1), (behind + 1, 2 * last)]
     step = half // pieces
     keeps, backs = [], []
     for piece in range(pieces):
-        mine = mine_all[piece * step:(piece + 1) * step]
-        got = lax.ppermute(other_all[piece * step:(piece + 1) * step], axis, swap)
+        cut = slice(piece * step, (piece + 1) * step)
+        mine = mine_all[cut]
+        got = lax.ppermute(other_all[cut], axis, swap)
         total = mine + got
         carried = jnp.zeros_like(total)
-        for hop in range(1, pairs):
+        for hop in range(1, last):
             links = [(2 * (hop - 1) + side, 2 * hop + side) for side in range(2)]
             carried = carried + lax.ppermute(carried + total, axis, links)
-        keeps.append((carried + jnp.where(first, 0.0, got)).astype(jnp.bfloat16))
+        keep = (carried + jnp.where(first, 0.0, got)).astype(jnp.bfloat16)
         send = (carried + jnp.where(first, mine, 0.0)).astype(jnp.bfloat16)
-        backs.append(lax.ppermute(send, axis, swap))
+        back = lax.ppermute(send, axis, swap)
+        reach = carried + total
+        added = kv_back[cut]
+        straight = lax.ppermute((reach + jnp.where(first, 0.0, added)).astype(jnp.bfloat16), axis, ahead)
+        diagonal = lax.ppermute((reach + jnp.where(first, added, 0.0)).astype(jnp.bfloat16), axis, across)
+        keeps.append(jnp.where(at_last, straight, keep))
+        backs.append(jnp.where(at_last, diagonal, back))
     return jnp.concatenate(keeps, axis=0), jnp.concatenate(backs, axis=0)
 
 

time: 95.8 us -> 126 us (1.32); the launches traced: 95.2 us -> 124 us
  waiting for transfers between devices: 50 us -> 62.1 us
  starting transfers between devices: 17.9 us -> 28 us
  local copies, waits for them, and re-layouts: 1.13 us -> 4.99 us
  other arithmetic: 9.86 us -> 12.1 us
    ppermute x8 -> x18, waiting for transfers between devices: 27.3 us -> 62.1 us  [the longest x4 56.4 us: pair_chain_prefix(): lax.ppermute((reach + jnp.where(first, 0.0, added)).astype(jnp.bfloat16),...]
    ppermute x12 -> x8, waiting for transfers between devices: 21.6 us -> 0.02 us  [pair_chain_prefix(): carried = carried + lax.ppermute(carried + total, axis, links)]
    ppermute x8 -> x18, starting transfers between devices: 7.21 us -> 19.8 us  [the longest x4 5.28 us: pair_chain_prefix(): lax.ppermute((reach + jnp.where(first, 0.0, added)).astype(jnp.bfloat16),...]
    dynamic_slice x0 -> x1, local copies, waits for them, and re-layouts: none -> 3.23 us  [pair_chain_prefix(): other_all = lax.dynamic_slice_in_dim(terms, (1 - mine_at) * half, half, 0)]
    ppermute x12 -> x8, starting transfers between devices: 10.7 us -> 8.18 us  [pair_chain_prefix(): carried = carried + lax.ppermute(carried + total, axis, links)]
    add x0 -> x1, other arithmetic: none -> 1.71 us  [pair_chain_prefix(): lax.ppermute(mine_all, axis, [(2 * last, behind)])]
    add x8 -> x4, other arithmetic: 3.41 us -> 2.97 us  [pair_chain_prefix(): carried = carried + lax.ppermute(carried + total, axis, links)]
  transfers between devices with their start and end apart: 21 -> 27, of which waited for: 13 -> 6; matrix products, arithmetic and copies ran while one was open for 5% -> 12% of each run, Pallas kernels for 0% -> 0%
where the time goes in v16:
time: 126 us; the launch traced here: 124 us
  waiting for transfers between devices  62.1 us (49%)
  starting transfers between devices  28 us (22%)
  Pallas kernels  16 us (13%)
  other arithmetic  12.1 us (10%)
  local copies, waits for them, and re-layouts  4.99 us (4%)
    ppermute x4, waiting for transfers between devices, pair_chain_prefix(): lax.ppermute((reach + jnp.where(first, 0.0, added)).astype(jnp.bfloat16),...  56.4 us
    pallas_call x1, Pallas kernels, attend_of(): pl.pallas_call(attend_kernel, grid_spec=pltpu.PrefetchScalarGridSpec(num_...  11.5 us
    ppermute x8, starting transfers between devices, pair_chain_prefix(): carried = carried + lax.ppermute(carried + total, axis, links)  8.18 us
    ppermute x4, waiting for transfers between devices, pair_chain_prefix(): lax.ppermute((reach + jnp.where(first, added, 0.0)).astype(jnp.bfloat16),...  5.65 us
    ppermute x4, starting transfers between devices, pair_chain_prefix(): lax.ppermute((reach + jnp.where(first, 0.0, added)).astype(jnp.bfloat16),...  5.28 us
    ppermute x4, starting transfers between devices, pair_chain_prefix(): lax.ppermute((reach + jnp.where(first, added, 0.0)).astype(jnp.bfloat16),...  5.14 us
    pallas_call x1, Pallas kernels, state_terms_of(): pl.pallas_call(state_kernel, grid=(H // group,), in_specs=[pl.BlockSpec((...  4.45 us
    ppermute x4, starting transfers between devices, pair_chain_prefix(): got = lax.ppermute(other_all[cut], axis, swap)  3.41 us
  transfers between devices with their start and end apart: 27, of which 6 were waited for; matrix products, arithmetic and copies ran while one was open for 12% of the time, Pallas kernels for 0%

profile of v16, /device:TPU:30, one launch (start us, length us, event | category | flops | bytes accessed | tf_op | source)
XLA Modules:
  0.0 123.7 jit_solution(4227865783866151411)
XLA Ops:
  0.0 4.4 %shard_map.46 = f32[32,128,128]{2,1,0:T(8,128)} custom-call(bf16[384,4096]{1,0:T(8,128)(2,1)} %bitcast.6, bf16[384,4096]{1,0:T(8,128)(2,1)} %bitcast.8), custom_call_target="tpu_custom_call" | custom-call | tf_op jit(solution)/shard_map/pallas_call | solution.py:63
  4.4 1.0 constant_dynamic-slice_fusion.3
  5.4 0.7 collective-permute-start
  6.1 3.2 %constant_dynamic-slice_fusion.4 = (f32[16,128,128]{2,1,0:T(8,128)}, f32[16,128,128]{2,1,0:T(8,128)}) fusion(f32[32,128,128]{2,1,0:T(8,128)} %shard_map.46, s32[]{:T(128)S(6)} %select_n.141, s32[]{:T(128)S(6)} %select_n.140), kind=kLoop, calls=%fused_computation.37 | loop fusion | bytes 4194312 | tf_op jit(solution)/shard_map/dynamic_slice | solution.py:20
  9.4 1.6 %collective-permute-start.3 = (f32[16,128,128]{2,1,0:T(8,128)}, f32[16,128,128]{2,1,0:T(8,128)}, u32[]{:S(2)}, u32[]{:S(2)}) collective-permute-start(f32[16,128,128]{2,1,0:T(8,128)} %get-tuple-element.27), channel_id=1, source_target_pairs={{12,8},{13,9},{28,24},{29,25}} | collective-permute-start | bytes 3145736 | tf_op jit(solution)/shard_map/ppermute | solution.py:23
  11.0 0.8 dynamic-slice_add_fusion.3
  11.8 0.7 collective-permute-start.10
  12.5 0.7 collective-permute-start.14
  13.2 1.4 %collective-permute-start.6 = (f32[4,128,128]{2,1,0:T(8,128)S(1)}, f32[4,128,128]{2,1,0:T(8,128)}, u32[]{:S(2)}, u32[]{:S(2)}) collective-permute-start(f32[4,128,128]{2,1,0:T(8,128)S(1)} %get-tuple-element.22), channel_id=1, source_target_pairs={{0,2},{4,6},{8,10},{2,0},{6,4},{10,8},{1,3},{5,7},{9,11},{3,1},{7,... | collective-permute-start | bytes 786440 | tf_op jit(solution)/shard_map/ppermute | solution.py:32
  14.6 1.6 %collective-permute-start.4 = (f32[16,128,128]{2,1,0:T(8,128)}, f32[16,128,128]{2,1,0:T(8,128)}, u32[]{:S(2)}, u32[]{:S(2)}) collective-permute-start(f32[16,128,128]{2,1,0:T(8,128)} %get-tuple-element.26), channel_id=1, source_target_pairs={{12,10},{13,11},{28,26},{29,27}} | collective-permute-start | bytes 3145736 | tf_op jit(solution)/shard_map/ppermute | solution.py:24
  16.2 0.7 collective-permute-start.1
  16.9 0.7 copy-done.7
  17.6 1.2 dynamic-slice_add_fusion.2
  18.9 0.7 collective-permute-start.15
  19.5 0.7 collective-permute-start.11
  20.2 0.7 collective-permute-start.7
  20.9 0.7 add.115
  21.7 1.4 %collective-permute-start.2 = (f32[4,128,128]{2,1,0:T(8,128)}, f32[4,128,128]{2,1,0:T(8,128)}, u32[]{:S(2)}, u32[]{:S(2)}) collective-permute-start(f32[4,128,128]{2,1,0:T(8,128)} %add.115), channel_id=1, source_target_pairs={{4,8},{6,10},{5,9},{7,11},{20,24},{22,26},{21,25},{23,27}} | collective-permute-start | bytes 786440 | tf_op jit(solution)/shard_map/ppermute | solution.py:37
  23.0 0.7 add.134
  23.8 1.4 %collective-permute-start.16 = (f32[4,128,128]{2,1,0:T(8,128)}, f32[4,128,128]{2,1,0:T(8,128)}, u32[]{:S(2)}, u32[]{:S(2)}) collective-permute-start(f32[4,128,128]{2,1,0:T(8,128)} %add.134), channel_id=1, source_target_pairs={{4,8},{6,10},{5,9},{7,11},{20,24},{22,26},{21,25},{23,27}} | collective-permute-start | bytes 786440 | tf_op jit(solution)/shard_map/ppermute | solution.py:37
  25.1 0.7 add.128
  25.9 1.4 %collective-permute-start.12 = (f32[4,128,128]{2,1,0:T(8,128)}, f32[4,128,128]{2,1,0:T(8,128)}, u32[]{:S(2)}, u32[]{:S(2)}) collective-permute-start(f32[4,128,128]{2,1,0:T(8,128)} %add.128), channel_id=1, source_target_pairs={{4,8},{6,10},{5,9},{7,11},{20,24},{22,26},{21,25},{23,27}} | collective-permute-start | bytes 786440 | tf_op jit(solution)/shard_map/ppermute | solution.py:37
  27.3 0.8 add.122
  28.0 1.4 %collective-permute-start.8 = (f32[4,128,128]{2,1,0:T(8,128)}, f32[4,128,128]{2,1,0:T(8,128)}, u32[]{:S(2)}, u32[]{:S(2)}) collective-permute-start(f32[4,128,128]{2,1,0:T(8,128)} %add.122), channel_id=1, source_target_pairs={{4,8},{6,10},{5,9},{7,11},{20,24},{22,26},{21,25},{23,27}} | collective-permute-start | bytes 786440 | tf_op jit(solution)/shard_map/ppermute | solution.py:37
  29.5 1.7 %add.118 = f32[16,128,128]{2,1,0:T(8,128)S(1)} add(f32[16,128,128]{2,1,0:T(8,128)} %collective-permute-done.3, f32[16,128,128]{2,1,0:T(8,128)} %collective-permute-done.4) | non-fusion elementwise | flops 262144 | bytes 3145728 | tf_op jit(solution)/shard_map/add | solution.py:23
  31.3 1.5 %add_convert_fusion.6 = (bf16[4,128,128]{2,1,0:T(8,128)(2,1)S(1)}, f32[4,128,128]{2,1,0:T(8,128)S(1)}, bf16[4,128,128]{2,1,0:T(8,128)(2,1)S(1)}, f32[4,128,128]{...) fusion(f32[32,128,128]{2,1,0:T(8,128)S(1)} %copy-done, ...), kind=kLoop, calls=%fused_computation.8 | loop fusion | flops 1048576 | bytes 4718609 | tf_op jit(solution)/shard_map/convert_element_type | solution.py:39
  33.1 1.3 %collective-permute-start.5 = (bf16[4,128,128]{2,1,0:T(8,128)(2,1)S(1)}, bf16[4,128,128]{2,1,0:T(8,128)(2,1)S(1)}, u32[]{:S(2)}, u32[]{:S(2)}) collective-permute-start(bf16[4,128,128]{2,1,0:T(8,128)(2,1)S(1)} %get-tuple-element.29), channel_id=1, source_target_pairs={{8,12},{10,14},{9,13},{11,15},{24,28},{26,30},{25,29},{27,31}} | collective-permute-start | bytes 393224 | tf_op jit(solution)/shard_map/ppermute | solution.py:43
  35.1 1.3 %collective-permute-start.18 = (bf16[4,128,128]{2,1,0:T(8,128)(2,1)S(1)}, bf16[4,128,128]{2,1,0:T(8,128)(2,1)S(1)}, u32[]{:S(2)}, u32[]{:S(2)}) collective-permute-start(bf16[4,128,128]{2,1,0:T(8,128)(2,1)S(1)} %get-tuple-element.28), channel_id=1, source_target_pairs={{8,14},{10,12},{9,15},{11,13},{24,30},{26,28},{25,31},{27,29}} | collective-permute-start | bytes 393224 | tf_op jit(solution)/shard_map/ppermute | solution.py:44
  36.4 0.7 collective-permute-start.19
  37.0 1.3 %collective-permute-start.20 = (bf16[4,128,128]{2,1,0:T(8,128)(2,1)S(1)}, bf16[4,128,128]{2,1,0:T(8,128)(2,1)S(1)}, u32[]{:S(2)}, u32[]{:S(2)}) collective-permute-start(bf16[4,128,128]{2,1,0:T(8,128)(2,1)S(1)} %get-tuple-element.37), channel_id=1, source_target_pairs={{8,14},{10,12},{9,15},{11,13},{24,30},{26,28},{25,31},{27,29}} | collective-permute-start | bytes 393224 | tf_op jit(solution)/shard_map/ppermute | solution.py:44
  38.3 0.7 collective-permute-start.21
  39.0 39.0 %collective-permute-done.5 = bf16[4,128,128]{2,1,0:T(8,128)(2,1)S(1)} collective-permute-done((bf16[4,128,128]{2,1,0:T(8,128)(2,1)S(1)}, bf16[4,128,128]{2,1,0:T(8,128)(2,1)S(1)}, u32[]{:S(2)}, u32[]{:S(2)}) %collective-permute-start.5) | collective-permute-done | bytes 131104 | tf_op jit(solution)/shard_map/ppermute | solution.py:43
  78.0 1.3 %collective-permute-start.9 = (bf16[4,128,128]{2,1,0:T(8,128)(2,1)S(1)}, bf16[4,128,128]{2,1,0:T(8,128)(2,1)S(1)}, u32[]{:S(2)}, u32[]{:S(2)}) collective-permute-start(bf16[4,128,128]{2,1,0:T(8,128)(2,1)S(1)} %get-tuple-element.36), channel_id=1, source_target_pairs={{8,12},{10,14},{9,13},{11,15},{24,28},{26,30},{25,29},{27,31}} | collective-permute-start | bytes 393224 | tf_op jit(solution)/shard_map/ppermute | solution.py:43
  79.4 8.8 %collective-permute-done.9 = bf16[4,128,128]{2,1,0:T(8,128)(2,1)S(1)} collective-permute-done((bf16[4,128,128]{2,1,0:T(8,128)(2,1)S(1)}, bf16[4,128,128]{2,1,0:T(8,128)(2,1)S(1)}, u32[]{:S(2)}, u32[]{:S(2)}) %collective-permute-start.9) | collective-permute-done | bytes 131104 | tf_op jit(solution)/shard_map/ppermute | solution.py:43
  88.2 1.4 %collective-permute-start.13 = (bf16[4,128,128]{2,1,0:T(8,128)(2,1)S(1)}, bf16[4,128,128]{2,1,0:T(8,128)(2,1)S(1)}, u32[]{:S(2)}, u32[]{:S(2)}) collective-permute-start(bf16[4,128,128]{2,1,0:T(8,128)(2,1)S(1)} %get-tuple-element.38), channel_id=1, source_target_pairs={{8,12},{10,14},{9,13},{11,15},{24,28},{26,30},{25,29},{27,31}} | collective-permute-start | bytes 393224 | tf_op jit(solution)/shard_map/ppermute | solution.py:43
  89.6 1.0 fusion.1
  90.6 5.6 %collective-permute-done.13 = bf16[4,128,128]{2,1,0:T(8,128)(2,1)S(1)} collective-permute-done((bf16[4,128,128]{2,1,0:T(8,128)(2,1)S(1)}, bf16[4,128,128]{2,1,0:T(8,128)(2,1)S(1)}, u32[]{:S(2)}, u32[]{:S(2)}) %collective-permute-start.13) | collective-permute-done | bytes 131104 | tf_op jit(solution)/shard_map/ppermute | solution.py:43
  96.3 1.3 %collective-permute-start.22 = (bf16[4,128,128]{2,1,0:T(8,128)(2,1)S(1)}, bf16[4,128,128]{2,1,0:T(8,128)(2,1)S(1)}, u32[]{:S(2)}, u32[]{:S(2)}) collective-permute-start(bf16[4,128,128]{2,1,0:T(8,128)(2,1)S(1)} %get-tuple-element.39), channel_id=1, source_target_pairs={{8,14},{10,12},{9,15},{11,13},{24,30},{26,28},{25,31},{27,29}} | collective-permute-start | bytes 393224 | tf_op jit(solution)/shard_map/ppermute | solution.py:44
  97.6 0.7 collective-permute-start.23
  98.3 1.3 %collective-permute-start.24 = (bf16[4,128,128]{2,1,0:T(8,128)(2,1)S(1)}, bf16[4,128,128]{2,1,0:T(8,128)(2,1)S(1)}, u32[]{:S(2)}, u32[]{:S(2)}) collective-permute-start(bf16[4,128,128]{2,1,0:T(8,128)(2,1)S(1)} %get-tuple-element.41), channel_id=1, source_target_pairs={{8,14},{10,12},{9,15},{11,13},{24,30},{26,28},{25,31},{27,29}} | collective-permute-start | bytes 393224 | tf_op jit(solution)/shard_map/ppermute | solution.py:44
  99.7 0.7 collective-permute-start.25
  100.3 1.3 %collective-permute-start.17 = (bf16[4,128,128]{2,1,0:T(8,128)(2,1)S(1)}, bf16[4,128,128]{2,1,0:T(8,128)(2,1)S(1)}, u32[]{:S(2)}, u32[]{:S(2)}) collective-permute-start(bf16[4,128,128]{2,1,0:T(8,128)(2,1)S(1)} %get-tuple-element.40), channel_id=1, source_target_pairs={{8,12},{10,14},{9,13},{11,15},{24,28},{26,30},{25,29},{27,31}} | collective-permute-start | bytes 393224 | tf_op jit(solution)/shard_map/ppermute | solution.py:43
  101.7 2.3 %collective-permute-done.22 = bf16[4,128,128]{2,1,0:T(8,128)(2,1)S(1)} collective-permute-done((bf16[4,128,128]{2,1,0:T(8,128)(2,1)S(1)}, bf16[4,128,128]{2,1,0:T(8,128)(2,1)S(1)}, u32[]{:S(2)}, u32[]{:S(2)}) %collective-permute-start.22) | collective-permute-done | bytes 131104 | tf_op jit(solution)/shard_map/ppermute | solution.py:44
  104.0 3.3 %collective-permute-done.24 = bf16[4,128,128]{2,1,0:T(8,128)(2,1)S(1)} collective-permute-done((bf16[4,128,128]{2,1,0:T(8,128)(2,1)S(1)}, bf16[4,128,128]{2,1,0:T(8,128)(2,1)S(1)}, u32[]{:S(2)}, u32[]{:S(2)}) %collective-permute-start.24) | collective-permute-done | bytes 131104 | tf_op jit(solution)/shard_map/ppermute | solution.py:44
  107.4 0.9 pad_maximum_fusion.1.back_ref
  108.2 2.9 %collective-permute-done.17 = bf16[4,128,128]{2,1,0:T(8,128)(2,1)S(1)} collective-permute-done((bf16[4,128,128]{2,1,0:T(8,128)(2,1)S(1)}, bf16[4,128,128]{2,1,0:T(8,128)(2,1)S(1)}, u32[]{:S(2)}, u32[]{:S(2)}) %collective-permute-start.17) | collective-permute-done | bytes 131104 | tf_op jit(solution)/shard_map/ppermute | solution.py:43
  111.2 0.9 pad_maximum_fusion.keep_ref
  112.1 11.5 %shard_map.47 = bf16[384,4096]{1,0:T(8,128)(2,1)} custom-call(s32[1]{0:T(128)} %bitcast.mine_ref, bf16[384,4096]{1,0:T(8,128)(2,1)} %bitcast.10, bf16[384,4096]{1,0:T(8,128)(2,1)} %bitcast.7, bf16[384,4096]{1,0:T(8,128)(2,1)} %bitcast.9, bf16[16,128,128]{2,1,0:T(8,128)(2,1)} %pad_maximum_fusion.keep_ref, bf16[16,128,128]{2,1,0:T(8,128)(2,1)} %pad_maximum_fusion.1.back_ref, ...), custom_call_target="tpu_custom_call" | custom-call | tf_op jit(solution)/shard_map/pallas_call | solution.py:117
  (59 shorter events, 1.4 us)
Async XLA Ops:
  5.4 5.6 %collective-permute-start = (f32[4,128,128]{2,1,0:T(8,128)S(1)}, f32[4,128,128]{2,1,0:T(8,128)S(1)}, u32[]{:S(2)}, u32[]{:S(2)}) collective-permute-start(f32[4,128,128]{2,1,0:T(8,128)S(1)} %constant_dynamic-slice_fusion.3), channel_id=1, source_target_pairs={{0,2},{4,6},{8,10},{2,0},{6,4},{10,8},{1,3},{5,7},{9,11},{3,1},{7,... | collective-permute-start | bytes 786440 | tf_op jit(solution)/shard_map/ppermute | solution.py:32
  6.1 4.9 %copy-start = (f32[32,128,128]{2,1,0:T(8,128)S(1)}, f32[32,128,128]{2,1,0:T(8,128)}, u32[]{:S(2)}) copy-start(f32[32,128,128]{2,1,0:T(8,128)} %shard_map.46) | copy-start | bytes 6291460
  9.4 18.7 %collective-permute-start.3 = (f32[16,128,128]{2,1,0:T(8,128)}, f32[16,128,128]{2,1,0:T(8,128)}, u32[]{:S(2)}, u32[]{:S(2)}) collective-permute-start(f32[16,128,128]{2,1,0:T(8,128)} %get-tuple-element.27), channel_id=1, source_target_pairs={{12,8},{13,9},{28,24},{29,25}} | collective-permute-start | bytes 3145736 | tf_op jit(solution)/shard_map/ppermute | solution.py:23
  11.0 1.5 %copy-start.11 = (f32[4,128,128]{2,1,0:T(8,128)}, f32[4,128,128]{2,1,0:T(8,128)S(1)}, u32[]{:S(2)}) copy-start(f32[4,128,128]{2,1,0:T(8,128)S(1)} %collective-permute-done) | copy-start | bytes 786436
  11.8 4.4 %collective-permute-start.10 = (f32[4,128,128]{2,1,0:T(8,128)S(1)}, f32[4,128,128]{2,1,0:T(8,128)S(1)}, u32[]{:S(2)}, u32[]{:S(2)}) collective-permute-start(f32[4,128,128]{2,1,0:T(8,128)S(1)} %get-tuple-element.21), channel_id=1, source_target_pairs={{0,2},{4,6},{8,10},{2,0},{6,4},{10,8},{1,3},{5,7},{9,11},{3,1},{7,... | collective-permute-start | bytes 786440 | tf_op jit(solution)/shard_map/ppermute | solution.py:32
  12.5 4.4 %collective-permute-start.14 = (f32[4,128,128]{2,1,0:T(8,128)}, f32[4,128,128]{2,1,0:T(8,128)S(1)}, u32[]{:S(2)}, u32[]{:S(2)}) collective-permute-start(f32[4,128,128]{2,1,0:T(8,128)} %get-tuple-element.20), channel_id=1, source_target_pairs={{0,2},{4,6},{8,10},{2,0},{6,4},{10,8},{1,3},{5,7},{9,11},{3,1},{7,... | collective-permute-start | bytes 786440 | tf_op jit(solution)/shard_map/ppermute | solution.py:32
  13.2 4.5 %collective-permute-start.6 = (f32[4,128,128]{2,1,0:T(8,128)S(1)}, f32[4,128,128]{2,1,0:T(8,128)}, u32[]{:S(2)}, u32[]{:S(2)}) collective-permute-start(f32[4,128,128]{2,1,0:T(8,128)S(1)} %get-tuple-element.22), channel_id=1, source_target_pairs={{0,2},{4,6},{8,10},{2,0},{6,4},{10,8},{1,3},{5,7},{9,11},{3,1},{7,... | collective-permute-start | bytes 786440 | tf_op jit(solution)/shard_map/ppermute | solution.py:32
  14.6 14.8 %collective-permute-start.4 = (f32[16,128,128]{2,1,0:T(8,128)}, f32[16,128,128]{2,1,0:T(8,128)}, u32[]{:S(2)}, u32[]{:S(2)}) collective-permute-start(f32[16,128,128]{2,1,0:T(8,128)} %get-tuple-element.26), channel_id=1, source_target_pairs={{12,10},{13,11},{28,26},{29,27}} | collective-permute-start | bytes 3145736 | tf_op jit(solution)/shard_map/ppermute | solution.py:24
  16.2 0.7 copy-start.9
  16.2 4.0 %collective-permute-start.1 = (f32[4,128,128]{2,1,0:T(8,128)S(1)}, f32[4,128,128]{2,1,0:T(8,128)S(1)}, u32[]{:S(2)}, u32[]{:S(2)}) collective-permute-start(f32[4,128,128]{2,1,0:T(8,128)S(1)} %get-tuple-element.19), channel_id=1, source_target_pairs={{0,4},{2,6},{1,5},{3,7},{16,20},{18,22},{17,21},{19,23}} | collective-permute-start | bytes 786440 | tf_op jit(solution)/shard_map/ppermute | solution.py:37
  16.9 0.7 copy-start.7
  18.8 10.6 %copy-start.13 = (f32[2048]{0:T(1024)S(1)}, f32[2048]{0:T(1024)}, u32[]{:S(2)}) copy-start(f32[2048]{0:T(1024)} %param.7) | copy-start | bytes 24580
  18.9 2.8 %collective-permute-start.15 = (f32[4,128,128]{2,1,0:T(8,128)S(1)}, f32[4,128,128]{2,1,0:T(8,128)S(1)}, u32[]{:S(2)}, u32[]{:S(2)}) collective-permute-start(f32[4,128,128]{2,1,0:T(8,128)S(1)} %get-tuple-element.24), channel_id=1, source_target_pairs={{0,4},{2,6},{1,5},{3,7},{16,20},{18,22},{17,21},{19,23}} | collective-permute-start | bytes 786440 | tf_op jit(solution)/shard_map/ppermute | solution.py:37
  19.5 4.2 %collective-permute-start.11 = (f32[4,128,128]{2,1,0:T(8,128)S(1)}, f32[4,128,128]{2,1,0:T(8,128)S(1)}, u32[]{:S(2)}, u32[]{:S(2)}) collective-permute-start(f32[4,128,128]{2,1,0:T(8,128)S(1)} %get-tuple-element.25), channel_id=1, source_target_pairs={{0,4},{2,6},{1,5},{3,7},{16,20},{18,22},{17,21},{19,23}} | collective-permute-start | bytes 786440 | tf_op jit(solution)/shard_map/ppermute | solution.py:37
  20.2 5.6 %collective-permute-start.7 = (f32[4,128,128]{2,1,0:T(8,128)S(1)}, f32[4,128,128]{2,1,0:T(8,128)S(1)}, u32[]{:S(2)}, u32[]{:S(2)}) collective-permute-start(f32[4,128,128]{2,1,0:T(8,128)S(1)} %get-tuple-element.23), channel_id=1, source_target_pairs={{0,4},{2,6},{1,5},{3,7},{16,20},{18,22},{17,21},{19,23}} | collective-permute-start | bytes 786440 | tf_op jit(solution)/shard_map/ppermute | solution.py:37
  21.7 4.2 %copy-start.1 = (f32[4,128,128]{2,1,0:T(8,128)}, f32[4,128,128]{2,1,0:T(8,128)S(1)}, u32[]{:S(2)}) copy-start(f32[4,128,128]{2,1,0:T(8,128)S(1)} %collective-permute-done.15) | copy-start | bytes 786436
  21.7 9.6 %collective-permute-start.2 = (f32[4,128,128]{2,1,0:T(8,128)}, f32[4,128,128]{2,1,0:T(8,128)}, u32[]{:S(2)}, u32[]{:S(2)}) collective-permute-start(f32[4,128,128]{2,1,0:T(8,128)} %add.115), channel_id=1, source_target_pairs={{4,8},{6,10},{5,9},{7,11},{20,24},{22,26},{21,25},{23,27}} | collective-permute-start | bytes 786440 | tf_op jit(solution)/shard_map/ppermute | solution.py:37
  23.8 3.5 %copy-start.3 = (f32[4,128,128]{2,1,0:T(8,128)}, f32[4,128,128]{2,1,0:T(8,128)S(1)}, u32[]{:S(2)}) copy-start(f32[4,128,128]{2,1,0:T(8,128)S(1)} %collective-permute-done.11) | copy-start | bytes 786436
  23.8 7.5 %collective-permute-start.16 = (f32[4,128,128]{2,1,0:T(8,128)}, f32[4,128,128]{2,1,0:T(8,128)}, u32[]{:S(2)}, u32[]{:S(2)}) collective-permute-start(f32[4,128,128]{2,1,0:T(8,128)} %add.134), channel_id=1, source_target_pairs={{4,8},{6,10},{5,9},{7,11},{20,24},{22,26},{21,25},{23,27}} | collective-permute-start | bytes 786440 | tf_op jit(solution)/shard_map/ppermute | solution.py:37
  25.9 2.1 %copy-start.5 = (f32[4,128,128]{2,1,0:T(8,128)}, f32[4,128,128]{2,1,0:T(8,128)S(1)}, u32[]{:S(2)}) copy-start(f32[4,128,128]{2,1,0:T(8,128)S(1)} %collective-permute-done.7) | copy-start | bytes 786436
  25.9 5.4 %collective-permute-start.12 = (f32[4,128,128]{2,1,0:T(8,128)}, f32[4,128,128]{2,1,0:T(8,128)}, u32[]{:S(2)}, u32[]{:S(2)}) collective-permute-start(f32[4,128,128]{2,1,0:T(8,128)} %add.128), channel_id=1, source_target_pairs={{4,8},{6,10},{5,9},{7,11},{20,24},{22,26},{21,25},{23,27}} | collective-permute-start | bytes 786440 | tf_op jit(solution)/shard_map/ppermute | solution.py:37
  28.0 3.2 %collective-permute-start.8 = (f32[4,128,128]{2,1,0:T(8,128)}, f32[4,128,128]{2,1,0:T(8,128)}, u32[]{:S(2)}, u32[]{:S(2)}) collective-permute-start(f32[4,128,128]{2,1,0:T(8,128)} %add.122), channel_id=1, source_target_pairs={{4,8},{6,10},{5,9},{7,11},{20,24},{22,26},{21,25},{23,27}} | collective-permute-start | bytes 786440 | tf_op jit(solution)/shard_map/ppermute | solution.py:37
  29.4 1.9 %copy-start.2 = (f32[4,128,128]{2,1,0:T(8,128)S(1)}, f32[4,128,128]{2,1,0:T(8,128)}, u32[]{:S(2)}) copy-start(f32[4,128,128]{2,1,0:T(8,128)} %copy-done.1) | copy-start | bytes 786436
  29.4 1.9 %copy-start.4 = (f32[4,128,128]{2,1,0:T(8,128)S(1)}, f32[4,128,128]{2,1,0:T(8,128)}, u32[]{:S(2)}) copy-start(f32[4,128,128]{2,1,0:T(8,128)} %copy-done.3) | copy-start | bytes 786436
  29.4 1.9 %copy-start.6 = (f32[4,128,128]{2,1,0:T(8,128)S(1)}, f32[4,128,128]{2,1,0:T(8,128)}, u32[]{:S(2)}) copy-start(f32[4,128,128]{2,1,0:T(8,128)} %copy-done.5) | copy-start | bytes 786436
  29.4 5.0 %collective-permute-start.26 = (f32[2048]{0:T(1024)S(1)}, f32[2048]{0:T(1024)S(1)}, u32[]{:S(2)}, u32[]{:S(2)}) collective-permute-start(f32[2048]{0:T(1024)S(1)} %copy-done.13), channel_id=1, source_target_pairs={{0,1},{1,0},{2,3},{3,2},{4,5},{5,4},{6,7},{7,6},{8,9},{9,8},{10,11... | collective-permute-start | bytes 24584 | tf_op jit(solution)/shard_map/ppermute | solution.py:137
  32.8 46.5 %copy-start.12 = (f32[4,128,128]{2,1,0:T(8,128)S(1)}, f32[4,128,128]{2,1,0:T(8,128)}, u32[]{:S(2)}) copy-start(f32[4,128,128]{2,1,0:T(8,128)} %copy-done.11) | copy-start | bytes 786436
  32.8 64.8 %copy-start.10 = (f32[4,128,128]{2,1,0:T(8,128)S(1)}, f32[4,128,128]{2,1,0:T(8,128)}, u32[]{:S(2)}) copy-start(f32[4,128,128]{2,1,0:T(8,128)} %copy-done.9) | copy-start | bytes 786436
  33.1 44.9 %collective-permute-start.5 = (bf16[4,128,128]{2,1,0:T(8,128)(2,1)S(1)}, bf16[4,128,128]{2,1,0:T(8,128)(2,1)S(1)}, u32[]{:S(2)}, u32[]{:S(2)}) collective-permute-start(bf16[4,128,128]{2,1,0:T(8,128)(2,1)S(1)} %get-tuple-element.29), channel_id=1, source_target_pairs={{8,12},{10,14},{9,13},{11,15},{24,28},{26,30},{25,29},{27,31}} | collective-permute-start | bytes 393224 | tf_op jit(solution)/shard_map/ppermute | solution.py:43
  35.1 62.5 %collective-permute-start.18 = (bf16[4,128,128]{2,1,0:T(8,128)(2,1)S(1)}, bf16[4,128,128]{2,1,0:T(8,128)(2,1)S(1)}, u32[]{:S(2)}, u32[]{:S(2)}) collective-permute-start(bf16[4,128,128]{2,1,0:T(8,128)(2,1)S(1)} %get-tuple-element.28), channel_id=1, source_target_pairs={{8,14},{10,12},{9,15},{11,13},{24,30},{26,28},{25,31},{27,29}} | collective-permute-start | bytes 393224 | tf_op jit(solution)/shard_map/ppermute | solution.py:44
  36.4 61.9 %collective-permute-start.19 = (bf16[4,128,128]{2,1,0:T(8,128)(2,1)S(1)}, bf16[4,128,128]{2,1,0:T(8,128)(2,1)S(1)}, u32[]{:S(2)}, u32[]{:S(2)}) collective-permute-start(bf16[4,128,128]{2,1,0:T(8,128)(2,1)S(1)} %get-tuple-element.5), channel_id=1, source_target_pairs={{0,2},{4,6},{8,10},{2,0},{6,4},{10,8},{1,3},{5,7},{9,11},{3,1},{7,... | collective-permute-start | bytes 393224 | tf_op jit(solution)/shard_map/ppermute | solution.py:40
  37.0 62.6 %collective-permute-start.20 = (bf16[4,128,128]{2,1,0:T(8,128)(2,1)S(1)}, bf16[4,128,128]{2,1,0:T(8,128)(2,1)S(1)}, u32[]{:S(2)}, u32[]{:S(2)}) collective-permute-start(bf16[4,128,128]{2,1,0:T(8,128)(2,1)S(1)} %get-tuple-element.37), channel_id=1, source_target_pairs={{8,14},{10,12},{9,15},{11,13},{24,30},{26,28},{25,31},{27,29}} | collective-permute-start | bytes 393224 | tf_op jit(solution)/shard_map/ppermute | solution.py:44
  38.3 62.0 %collective-permute-start.21 = (bf16[4,128,128]{2,1,0:T(8,128)(2,1)S(1)}, bf16[4,128,128]{2,1,0:T(8,128)(2,1)S(1)}, u32[]{:S(2)}, u32[]{:S(2)}) collective-permute-start(bf16[4,128,128]{2,1,0:T(8,128)(2,1)S(1)} %get-tuple-element.13), channel_id=1, source_target_pairs={{0,2},{4,6},{8,10},{2,0},{6,4},{10,8},{1,3},{5,7},{9,11},{3,1},{7,... | collective-permute-start | bytes 393224 | tf_op jit(solution)/shard_map/ppermute | solution.py:40
  78.0 10.2 %collective-permute-start.9 = (bf16[4,128,128]{2,1,0:T(8,128)(2,1)S(1)}, bf16[4,128,128]{2,1,0:T(8,128)(2,1)S(1)}, u32[]{:S(2)}, u32[]{:S(2)}) collective-permute-start(bf16[4,128,128]{2,1,0:T(8,128)(2,1)S(1)} %get-tuple-element.36), channel_id=1, source_target_pairs={{8,12},{10,14},{9,13},{11,15},{24,28},{26,30},{25,29},{27,31}} | collective-permute-start | bytes 393224 | tf_op jit(solution)/shard_map/ppermute | solution.py:43
  88.2 23.0 %copy-start.8 = (f32[4,128,128]{2,1,0:T(8,128)S(1)}, f32[4,128,128]{2,1,0:T(8,128)}, u32[]{:S(2)}) copy-start(f32[4,128,128]{2,1,0:T(8,128)} %copy-done.7) | copy-start | bytes 786436
  88.2 8.1 %collective-permute-start.13 = (bf16[4,128,128]{2,1,0:T(8,128)(2,1)S(1)}, bf16[4,128,128]{2,1,0:T(8,128)(2,1)S(1)}, u32[]{:S(2)}, u32[]{:S(2)}) collective-permute-start(bf16[4,128,128]{2,1,0:T(8,128)(2,1)S(1)} %get-tuple-element.38), channel_id=1, source_target_pairs={{8,12},{10,14},{9,13},{11,15},{24,28},{26,30},{25,29},{27,31}} | collective-permute-start | bytes 393224 | tf_op jit(solution)/shard_map/ppermute | solution.py:43
  96.3 7.7 %collective-permute-start.22 = (bf16[4,128,128]{2,1,0:T(8,128)(2,1)S(1)}, bf16[4,128,128]{2,1,0:T(8,128)(2,1)S(1)}, u32[]{:S(2)}, u32[]{:S(2)}) collective-permute-start(bf16[4,128,128]{2,1,0:T(8,128)(2,1)S(1)} %get-tuple-element.39), channel_id=1, source_target_pairs={{8,14},{10,12},{9,15},{11,13},{24,30},{26,28},{25,31},{27,29}} | collective-permute-start | bytes 393224 | tf_op jit(solution)/shard_map/ppermute | solution.py:44
  97.6 6.4 %collective-permute-start.23 = (bf16[4,128,128]{2,1,0:T(8,128)(2,1)S(1)}, bf16[4,128,128]{2,1,0:T(8,128)(2,1)S(1)}, u32[]{:S(2)}, u32[]{:S(2)}) collective-permute-start(bf16[4,128,128]{2,1,0:T(8,128)(2,1)S(1)} %get-tuple-element.15), channel_id=1, source_target_pairs={{0,2},{4,6},{8,10},{2,0},{6,4},{10,8},{1,3},{5,7},{9,11},{3,1},{7,... | collective-permute-start | bytes 393224 | tf_op jit(solution)/shard_map/ppermute | solution.py:40
  98.3 9.0 %collective-permute-start.24 = (bf16[4,128,128]{2,1,0:T(8,128)(2,1)S(1)}, bf16[4,128,128]{2,1,0:T(8,128)(2,1)S(1)}, u32[]{:S(2)}, u32[]{:S(2)}) collective-permute-start(bf16[4,128,128]{2,1,0:T(8,128)(2,1)S(1)} %get-tuple-element.41), channel_id=1, source_target_pairs={{8,14},{10,12},{9,15},{11,13},{24,30},{26,28},{25,31},{27,29}} | collective-permute-start | bytes 393224 | tf_op jit(solution)/shard_map/ppermute | solution.py:44
  99.7 7.7 %collective-permute-start.25 = (bf16[4,128,128]{2,1,0:T(8,128)(2,1)S(1)}, bf16[4,128,128]{2,1,0:T(8,128)(2,1)S(1)}, u32[]{:S(2)}, u32[]{:S(2)}) collective-permute-start(bf16[4,128,128]{2,1,0:T(8,128)(2,1)S(1)} %get-tuple-element.17), channel_id=1, source_target_pairs={{0,2},{4,6},{8,10},{2,0},{6,4},{10,8},{1,3},{5,7},{9,11},{3,1},{7,... | collective-permute-start | bytes 393224 | tf_op jit(solution)/shard_map/ppermute | solution.py:40
  100.3 10.8 %collective-permute-start.17 = (bf16[4,128,128]{2,1,0:T(8,128)(2,1)S(1)}, bf16[4,128,128]{2,1,0:T(8,128)(2,1)S(1)}, u32[]{:S(2)}, u32[]{:S(2)}) collective-permute-start(bf16[4,128,128]{2,1,0:T(8,128)(2,1)S(1)} %get-tuple-element.40), channel_id=1, source_target_pairs={{8,12},{10,14},{9,13},{11,15},{24,28},{26,30},{25,29},{27,31}} | collective-permute-start | bytes 393224 | tf_op jit(solution)/shard_map/ppermute | solution.py:43

commit v17 on v15

--- a/solution.py
+++ b/solution.py
@@ -28,9 +28,9 @@
             links = [(2 * (hop - 1) + side, 2 * hop + side) for side in range(2)]
             carried = carried + lax.ppermute(carried + total, axis, links)
         keeps.append((carried + jnp.where(first, 0.0, got)).astype(jnp.bfloat16))
-        send = (carried + jnp.where(first, mine, 0.0)).astype(jnp.bfloat16)
-        backs.append(lax.ppermute(send, axis, swap))
-    return jnp.concatenate(keeps, axis=0), jnp.concatenate(backs, axis=0)
+        backs.append((carried + jnp.where(first, mine, 0.0)).astype(jnp.bfloat16))
+    back = lax.ppermute(jnp.concatenate(backs, axis=0), axis, swap)
+    return jnp.concatenate(keeps, axis=0), back
 
 
 def state_kernel(key_ref, val_ref, out_ref):

time: 95.8 us -> 96.4 us (level)
  starting transfers between devices: 17.9 us -> 14.1 us
  waiting for transfers between devices: 50 us -> 52.7 us
    ppermute x4 -> x1, starting transfers between devices: 4.12 us -> 0.51 us  [pair_chain_prefix(): back = lax.ppermute(jnp.concatenate(backs, axis=0), axis, swap)]
    ppermute x12, waiting for transfers between devices: 21.6 us -> 22.9 us  [pair_chain_prefix(): carried = carried + lax.ppermute(carried + total, axis, links)]
    ppermute x4 -> x1, waiting for transfers between devices: 4.31 us -> 5.67 us  [pair_chain_prefix(): back = lax.ppermute(jnp.concatenate(backs, axis=0), axis, swap)]
  transfers between devices with their start and end apart: 21 -> 18, of which waited for: 13 -> 10; matrix products, arithmetic and copies ran while one was open for 5% -> 6% of each run, Pallas kernels for 0% -> 0%
where the time goes in v17:
time: 96.4 us; the launch traced here: 95.8 us
  waiting for transfers between devices  52.7 us (55%)
  Pallas kernels  16.1 us (17%)
  starting transfers between devices  14.1 us (15%)
  other arithmetic  10.7 us (11%)
  local copies, waits for them, and re-layouts  1.94 us (2%)
    ppermute x12, waiting for transfers between devices, pair_chain_prefix(): carried = carried + lax.ppermute(carried + total, axis, links)  22.9 us
    ppermute x4, waiting for transfers between devices, pair_chain_prefix(): got = lax.ppermute(other_all[piece * step:(piece + 1) * step], axis, swap)  22.9 us
    pallas_call x1, Pallas kernels, attend_of(): pl.pallas_call(attend_kernel, grid_spec=pltpu.PrefetchScalarGridSpec(num_...  11.6 us
    ppermute x12, starting transfers between devices, pair_chain_prefix(): carried = carried + lax.ppermute(carried + total, axis, links)  10.5 us
    ppermute x1, waiting for transfers between devices, pair_chain_prefix(): back = lax.ppermute(jnp.concatenate(backs, axis=0), axis, swap)  5.67 us
    pallas_call x1, Pallas kernels, state_terms_of(): pl.pallas_call(state_kernel, grid=(H // group,), in_specs=[pl.BlockSpec((...  4.45 us
    add x8, other arithmetic, pair_chain_prefix(): carried = carried + lax.ppermute(carried + total, axis, links)  3.39 us
    ppermute x4, starting transfers between devices, pair_chain_prefix(): got = lax.ppermute(other_all[piece * step:(piece + 1) * step], axis, swap)  3.09 us
  transfers between devices with their start and end apart: 18, of which 10 were waited for; matrix products, arithmetic and copies ran while one was open for 6% of the time, Pallas kernels for 0%

profile of v17, /device:TPU:30, one launch (start us, length us, event | category | flops | bytes accessed | tf_op | source)
XLA Modules:
  0.0 95.8 jit_solution(6951679581215435591)
XLA Ops:
  0.0 4.4 %shard_map.46 = f32[32,128,128]{2,1,0:T(8,128)} custom-call(bf16[384,4096]{1,0:T(8,128)(2,1)} %bitcast.6, bf16[384,4096]{1,0:T(8,128)(2,1)} %bitcast.8), custom_call_target="tpu_custom_call" | custom-call | tf_op jit(solution)/shard_map/pallas_call | solution.py:49
  4.5 1.1 %constant_dynamic-slice_fusion.2 = f32[4,128,128]{2,1,0:T(8,128)S(1)} fusion(f32[32,128,128]{2,1,0:T(8,128)} %shard_map.46, s32[]{:T(128)S(6)} %select_n.67), kind=kLoop, calls=%fused_computation.19 | loop fusion | bytes 524292 | tf_op jit(solution)/shard_map/slice | solution.py:24
  5.6 0.6 collective-permute-start
  6.1 7.5 %collective-permute-done = f32[4,128,128]{2,1,0:T(8,128)S(1)} collective-permute-done((f32[4,128,128]{2,1,0:T(8,128)S(1)}, f32[4,128,128]{2,1,0:T(8,128)S(1)}, u32[]{:S(2)}, u32[]{:S(2)}) %collective-permute-start) | collective-permute-done | bytes 262176 | tf_op jit(solution)/shard_map/ppermute | solution.py:24
  13.7 2.2 %dynamic-slice_add_fusion.3 = (f32[4,128,128]{2,1,0:T(8,128)S(1)}, f32[4,128,128]{2,1,0:T(8,128)S(1)}, f32[4,128,128]{2,1,0:T(8,128)}, f32[4,128,128]{2,1,0:T(8,128)}) fusion(f32[4,128,128]{2,1,0:T(8,128)S(1)} %collective-permute-done, f32[32,128,128]{2,1,0:T(8,128)} %shard_map.46, s32[]{:T(128)S(6)} %select_n.66, s32[]{:T(128)S(6)} %add.129, s32[]{:T(128)S(6)} %add.127, ...), kind=kLoop, calls=%fused_computation.13 | loop fusion | flops 65536 | bytes 2359312 | tf_op jit(solution)/shard_map/add | solution.py:25
  15.9 0.5 collective-permute-start.12
  16.4 1.5 %collective-permute-start.4 = (f32[4,128,128]{2,1,0:T(8,128)}, f32[4,128,128]{2,1,0:T(8,128)S(1)}, u32[]{:S(2)}, u32[]{:S(2)}) collective-permute-start(f32[4,128,128]{2,1,0:T(8,128)} %get-tuple-element.19), channel_id=1, source_target_pairs={{0,2},{4,6},{8,10},{12,14},{2,0},{6,4},{10,8},{14,12},{1,3},{5,7},... | collective-permute-start | bytes 786440 | tf_op jit(solution)/shard_map/ppermute | solution.py:24
  17.9 0.5 collective-permute-start.8
  18.4 0.7 collective-permute-start.1
  19.1 6.2 %collective-permute-done.12 = f32[4,128,128]{2,1,0:T(8,128)S(1)} collective-permute-done((f32[4,128,128]{2,1,0:T(8,128)}, f32[4,128,128]{2,1,0:T(8,128)S(1)}, u32[]{:S(2)}, u32[]{:S(2)}) %collective-permute-start.12) | collective-permute-done | bytes 262176 | tf_op jit(solution)/shard_map/ppermute | solution.py:24
  25.3 5.6 %collective-permute-done.4 = f32[4,128,128]{2,1,0:T(8,128)S(1)} collective-permute-done((f32[4,128,128]{2,1,0:T(8,128)}, f32[4,128,128]{2,1,0:T(8,128)S(1)}, u32[]{:S(2)}, u32[]{:S(2)}) %collective-permute-start.4) | collective-permute-done | bytes 262176 | tf_op jit(solution)/shard_map/ppermute | solution.py:24
  30.9 3.5 %collective-permute-done.8 = f32[4,128,128]{2,1,0:T(8,128)S(1)} collective-permute-done((f32[4,128,128]{2,1,0:T(8,128)S(1)}, f32[4,128,128]{2,1,0:T(8,128)S(1)}, u32[]{:S(2)}, u32[]{:S(2)}) %collective-permute-start.8) | collective-permute-done | bytes 262176 | tf_op jit(solution)/shard_map/ppermute | solution.py:24
  34.5 0.1 dynamic-slice_add_fusion.2
  34.6 0.7 collective-permute-start.13
  35.2 0.7 collective-permute-start.9
  35.9 0.7 collective-permute-start.5
  36.6 0.0 collective-permute-done.1
  36.7 0.7 collective-permute-start.2
  37.3 0.0 collective-permute-done.13
  37.4 0.7 collective-permute-start.14
  38.1 0.0 collective-permute-done.9
  38.1 0.7 collective-permute-start.10
  38.8 0.0 collective-permute-done.5
  38.9 0.7 collective-permute-start.6
  39.6 0.0 collective-permute-done.2
  39.6 0.8 fusion
  40.3 1.3 %collective-permute-start.3 = (f32[4,128,128]{2,1,0:T(8,128)}, f32[4,128,128]{2,1,0:T(8,128)}, u32[]{:S(2)}, u32[]{:S(2)}) collective-permute-start(f32[4,128,128]{2,1,0:T(8,128)} %get-tuple-element.5), channel_id=1, source_target_pairs={{8,12},{10,14},{9,13},{11,15},{24,28},{26,30},{25,29},{27,31}} | collective-permute-start | bytes 786440 | tf_op jit(solution)/shard_map/ppermute | solution.py:29
  41.6 0.0 collective-permute-done.14
  41.6 0.8 fusion.3
  42.4 1.3 %collective-permute-start.15 = (f32[4,128,128]{2,1,0:T(8,128)}, f32[4,128,128]{2,1,0:T(8,128)}, u32[]{:S(2)}, u32[]{:S(2)}) collective-permute-start(f32[4,128,128]{2,1,0:T(8,128)} %get-tuple-element.11), channel_id=1, source_target_pairs={{8,12},{10,14},{9,13},{11,15},{24,28},{26,30},{25,29},{27,31}} | collective-permute-start | bytes 786440 | tf_op jit(solution)/shard_map/ppermute | solution.py:29
  43.7 0.9 fusion.2
  44.5 1.3 %collective-permute-start.11 = (f32[4,128,128]{2,1,0:T(8,128)}, f32[4,128,128]{2,1,0:T(8,128)}, u32[]{:S(2)}, u32[]{:S(2)}) collective-permute-start(f32[4,128,128]{2,1,0:T(8,128)} %get-tuple-element.9), channel_id=1, source_target_pairs={{8,12},{10,14},{9,13},{11,15},{24,28},{26,30},{25,29},{27,31}} | collective-permute-start | bytes 786440 | tf_op jit(solution)/shard_map/ppermute | solution.py:29
  45.8 0.9 fusion.1
  46.7 1.3 %collective-permute-start.7 = (f32[4,128,128]{2,1,0:T(8,128)}, f32[4,128,128]{2,1,0:T(8,128)}, u32[]{:S(2)}, u32[]{:S(2)}) collective-permute-start(f32[4,128,128]{2,1,0:T(8,128)} %get-tuple-element.7), channel_id=1, source_target_pairs={{8,12},{10,14},{9,13},{11,15},{24,28},{26,30},{25,29},{27,31}} | collective-permute-start | bytes 786440 | tf_op jit(solution)/shard_map/ppermute | solution.py:29
  48.0 8.9 %collective-permute-done.3 = f32[4,128,128]{2,1,0:T(8,128)} collective-permute-done((f32[4,128,128]{2,1,0:T(8,128)}, f32[4,128,128]{2,1,0:T(8,128)}, u32[]{:S(2)}, u32[]{:S(2)}) %collective-permute-start.3) | collective-permute-done | bytes 262176 | tf_op jit(solution)/shard_map/ppermute | solution.py:29
  56.9 5.5 %collective-permute-done.15 = f32[4,128,128]{2,1,0:T(8,128)} collective-permute-done((f32[4,128,128]{2,1,0:T(8,128)}, f32[4,128,128]{2,1,0:T(8,128)}, u32[]{:S(2)}, u32[]{:S(2)}) %collective-permute-start.15) | collective-permute-done | bytes 262176 | tf_op jit(solution)/shard_map/ppermute | solution.py:29
  62.5 5.7 %collective-permute-done.11 = f32[4,128,128]{2,1,0:T(8,128)} collective-permute-done((f32[4,128,128]{2,1,0:T(8,128)}, f32[4,128,128]{2,1,0:T(8,128)}, u32[]{:S(2)}, u32[]{:S(2)}) %collective-permute-start.11) | collective-permute-done | bytes 262176 | tf_op jit(solution)/shard_map/ppermute | solution.py:29
  68.1 2.8 %collective-permute-done.7 = f32[4,128,128]{2,1,0:T(8,128)} collective-permute-done((f32[4,128,128]{2,1,0:T(8,128)}, f32[4,128,128]{2,1,0:T(8,128)}, u32[]{:S(2)}, u32[]{:S(2)}) %collective-permute-start.7) | collective-permute-done | bytes 262176 | tf_op jit(solution)/shard_map/ppermute | solution.py:29
  70.9 2.5 %add_convert_fusion.3 = (bf16[4,128,128]{2,1,0:T(8,128)(2,1)S(1)}, bf16[4,128,128]{2,1,0:T(8,128)(2,1)S(1)}, bf16[4,128,128]{2,1,0:T(8,128)(2,1)S(1)}, bf16[4,12...) fusion(f32[32,128,128]{2,1,0:T(8,128)S(1)} %copy-done, ...), kind=kLoop, calls=%fused_computation.5 | loop fusion | flops 1835008 | bytes 5242897 | tf_op jit(solution)/shard_map/convert_element_type | solution.py:31
  73.4 0.1 pad_maximum_fusion.1
  73.5 0.5 collective-permute-start.16
  74.0 0.0 collective-permute-start.17
  74.0 1.2 %collective-permute-done.17 = f32[2048]{0:T(1024)S(1)} collective-permute-done((f32[2048]{0:T(1024)S(1)}, f32[2048]{0:T(1024)S(1)}, u32[]{:S(2)}, u32[]{:S(2)}) %collective-permute-start.17) | collective-permute-done | bytes 8224 | tf_op jit(solution)/shard_map/ppermute | solution.py:123
  75.2 0.6 pad_maximum_fusion.2
  75.8 1.9 %pad_maximum_fusion.keep_ref = bf16[16,128,128]{2,1,0:T(8,128)(2,1)} fusion(bf16[4,128,128]{2,1,0:T(8,128)(2,1)S(1)} %get-tuple-element.24, bf16[4,128,128]{2,1,0:T(8,128)(2,1)} %get-tuple-element.25, bf16[4,128,128]{2,1,0:T(8,128)(2,1)} %get-tuple-element.26, bf16[4,128,128]{2,1,0:T(8,128)(2,1)} %get-tuple-element.27), kind=kLoop, calls=%fused_computation | loop fusion | flops 786432 | bytes 1048576 | tf_op jit(solution)/shard_map/concatenate | solution.py:33
  77.7 5.7 %collective-permute-done.16.back_ref = bf16[16,128,128]{2,1,0:T(8,128)(2,1)S(1)} collective-permute-done((bf16[16,128,128]{2,1,0:T(8,128)(2,1)S(1)}, bf16[16,128,128]{2,1,0:T(8,128)(2,1)S(1)}, u32[]{:S(2)}, u32[]{:S(2)}) %collective-permute-start.16) | collective-permute-done | bytes 524320 | tf_op jit(solution)/shard_map/ppermute | solution.py:32
  83.4 0.8 copy-done.2
  84.2 11.6 %shard_map.47 = bf16[384,4096]{1,0:T(8,128)(2,1)} custom-call(s32[1]{0:T(128)} %bitcast.mine_ref, bf16[384,4096]{1,0:T(8,128)(2,1)} %bitcast.10, bf16[384,4096]{1,0:T(8,128)(2,1)} %bitcast.7, bf16[384,4096]{1,0:T(8,128)(2,1)} %bitcast.9, bf16[16,128,128]{2,1,0:T(8,128)(2,1)} %pad_maximum_fusion.keep_ref, bf16[16,128,128]{2,1,0:T(8,128)(2,1)} %copy-done.2, ...), custom_call_target="tpu_custom_call" | custom-call | tf_op jit(solution)/shard_map/pallas_call | solution.py:103
  (14 shorter events, 0.2 us)
Async XLA Ops:
  4.4 30.0 %copy-start = (f32[32,128,128]{2,1,0:T(8,128)S(1)}, f32[32,128,128]{2,1,0:T(8,128)}, u32[]{:S(2)}) copy-start(f32[32,128,128]{2,1,0:T(8,128)} %shard_map.46) | copy-start | bytes 6291460
  5.6 8.1 %collective-permute-start = (f32[4,128,128]{2,1,0:T(8,128)S(1)}, f32[4,128,128]{2,1,0:T(8,128)S(1)}, u32[]{:S(2)}, u32[]{:S(2)}) collective-permute-start(f32[4,128,128]{2,1,0:T(8,128)S(1)} %constant_dynamic-slice_fusion.2), channel_id=1, source_target_pairs={{0,2},{4,6},{8,10},{12,14},{2,0},{6,4},{10,8},{14,12},{1,3},{5,7},... | collective-permute-start | bytes 786440 | tf_op jit(solution)/shard_map/ppermute | solution.py:24
  13.7 2.2 %copy-start.1 = (f32[4,128,128]{2,1,0:T(8,128)}, f32[4,128,128]{2,1,0:T(8,128)S(1)}, u32[]{:S(2)}) copy-start(f32[4,128,128]{2,1,0:T(8,128)S(1)} %collective-permute-done) | copy-start | bytes 786436
  15.9 9.5 %collective-permute-start.12 = (f32[4,128,128]{2,1,0:T(8,128)}, f32[4,128,128]{2,1,0:T(8,128)S(1)}, u32[]{:S(2)}, u32[]{:S(2)}) collective-permute-start(f32[4,128,128]{2,1,0:T(8,128)} %get-tuple-element.20), channel_id=1, source_target_pairs={{0,2},{4,6},{8,10},{12,14},{2,0},{6,4},{10,8},{14,12},{1,3},{5,7},... | collective-permute-start | bytes 786440 | tf_op jit(solution)/shard_map/ppermute | solution.py:24
  16.4 14.6 %collective-permute-start.4 = (f32[4,128,128]{2,1,0:T(8,128)}, f32[4,128,128]{2,1,0:T(8,128)S(1)}, u32[]{:S(2)}, u32[]{:S(2)}) collective-permute-start(f32[4,128,128]{2,1,0:T(8,128)} %get-tuple-element.19), channel_id=1, source_target_pairs={{0,2},{4,6},{8,10},{12,14},{2,0},{6,4},{10,8},{14,12},{1,3},{5,7},... | collective-permute-start | bytes 786440 | tf_op jit(solution)/shard_map/ppermute | solution.py:24
  17.9 16.6 %collective-permute-start.8 = (f32[4,128,128]{2,1,0:T(8,128)S(1)}, f32[4,128,128]{2,1,0:T(8,128)S(1)}, u32[]{:S(2)}, u32[]{:S(2)}) collective-permute-start(f32[4,128,128]{2,1,0:T(8,128)S(1)} %get-tuple-element.18), channel_id=1, source_target_pairs={{0,2},{4,6},{8,10},{12,14},{2,0},{6,4},{10,8},{14,12},{1,3},{5,7},... | collective-permute-start | bytes 786440 | tf_op jit(solution)/shard_map/ppermute | solution.py:24
  18.4 18.2 %collective-permute-start.1 = (f32[4,128,128]{2,1,0:T(8,128)S(1)}, f32[4,128,128]{2,1,0:T(8,128)S(1)}, u32[]{:S(2)}, u32[]{:S(2)}) collective-permute-start(f32[4,128,128]{2,1,0:T(8,128)S(1)} %get-tuple-element.17), channel_id=1, source_target_pairs={{0,4},{2,6},{1,5},{3,7},{16,20},{18,22},{17,21},{19,23}} | collective-permute-start | bytes 786440 | tf_op jit(solution)/shard_map/ppermute | solution.py:29
  34.6 2.8 %collective-permute-start.13 = (f32[4,128,128]{2,1,0:T(8,128)S(1)}, f32[4,128,128]{2,1,0:T(8,128)S(1)}, u32[]{:S(2)}, u32[]{:S(2)}) collective-permute-start(f32[4,128,128]{2,1,0:T(8,128)S(1)} %get-tuple-element.23), channel_id=1, source_target_pairs={{0,4},{2,6},{1,5},{3,7},{16,20},{18,22},{17,21},{19,23}} | collective-permute-start | bytes 786440 | tf_op jit(solution)/shard_map/ppermute | solution.py:29
  35.2 2.8 %collective-permute-start.9 = (f32[4,128,128]{2,1,0:T(8,128)S(1)}, f32[4,128,128]{2,1,0:T(8,128)S(1)}, u32[]{:S(2)}, u32[]{:S(2)}) collective-permute-start(f32[4,128,128]{2,1,0:T(8,128)S(1)} %get-tuple-element.22), channel_id=1, source_target_pairs={{0,4},{2,6},{1,5},{3,7},{16,20},{18,22},{17,21},{19,23}} | collective-permute-start | bytes 786440 | tf_op jit(solution)/shard_map/ppermute | solution.py:29
  35.9 2.9 %collective-permute-start.5 = (f32[4,128,128]{2,1,0:T(8,128)S(1)}, f32[4,128,128]{2,1,0:T(8,128)S(1)}, u32[]{:S(2)}, u32[]{:S(2)}) collective-permute-start(f32[4,128,128]{2,1,0:T(8,128)S(1)} %get-tuple-element.21), channel_id=1, source_target_pairs={{0,4},{2,6},{1,5},{3,7},{16,20},{18,22},{17,21},{19,23}} | collective-permute-start | bytes 786440 | tf_op jit(solution)/shard_map/ppermute | solution.py:29
  36.7 2.9 %collective-permute-start.2 = (f32[4,128,128]{2,1,0:T(8,128)S(1)}, f32[4,128,128]{2,1,0:T(8,128)S(1)}, u32[]{:S(2)}, u32[]{:S(2)}) collective-permute-start(f32[4,128,128]{2,1,0:T(8,128)S(1)} %add.99), channel_id=1, source_target_pairs={{4,8},{6,10},{5,9},{7,11},{20,24},{22,26},{21,25},{23,27}} | collective-permute-start | bytes 786440 | tf_op jit(solution)/shard_map/ppermute | solution.py:29
  37.4 4.2 %collective-permute-start.14 = (f32[4,128,128]{2,1,0:T(8,128)S(1)}, f32[4,128,128]{2,1,0:T(8,128)S(1)}, u32[]{:S(2)}, u32[]{:S(2)}) collective-permute-start(f32[4,128,128]{2,1,0:T(8,128)S(1)} %add.117), channel_id=1, source_target_pairs={{4,8},{6,10},{5,9},{7,11},{20,24},{22,26},{21,25},{23,27}} | collective-permute-start | bytes 786440 | tf_op jit(solution)/shard_map/ppermute | solution.py:29
  38.1 5.5 %collective-permute-start.10 = (f32[4,128,128]{2,1,0:T(8,128)S(1)}, f32[4,128,128]{2,1,0:T(8,128)S(1)}, u32[]{:S(2)}, u32[]{:S(2)}) collective-permute-start(f32[4,128,128]{2,1,0:T(8,128)S(1)} %add.111), channel_id=1, source_target_pairs={{4,8},{6,10},{5,9},{7,11},{20,24},{22,26},{21,25},{23,27}} | collective-permute-start | bytes 786440 | tf_op jit(solution)/shard_map/ppermute | solution.py:29
  38.9 7.0 %collective-permute-start.6 = (f32[4,128,128]{2,1,0:T(8,128)S(1)}, f32[4,128,128]{2,1,0:T(8,128)S(1)}, u32[]{:S(2)}, u32[]{:S(2)}) collective-permute-start(f32[4,128,128]{2,1,0:T(8,128)S(1)} %add.105), channel_id=1, source_target_pairs={{4,8},{6,10},{5,9},{7,11},{20,24},{22,26},{21,25},{23,27}} | collective-permute-start | bytes 786440 | tf_op jit(solution)/shard_map/ppermute | solution.py:29
  40.3 16.6 %collective-permute-start.3 = (f32[4,128,128]{2,1,0:T(8,128)}, f32[4,128,128]{2,1,0:T(8,128)}, u32[]{:S(2)}, u32[]{:S(2)}) collective-permute-start(f32[4,128,128]{2,1,0:T(8,128)} %get-tuple-element.5), channel_id=1, source_target_pairs={{8,12},{10,14},{9,13},{11,15},{24,28},{26,30},{25,29},{27,31}} | collective-permute-start | bytes 786440 | tf_op jit(solution)/shard_map/ppermute | solution.py:29
  42.4 20.1 %collective-permute-start.15 = (f32[4,128,128]{2,1,0:T(8,128)}, f32[4,128,128]{2,1,0:T(8,128)}, u32[]{:S(2)}, u32[]{:S(2)}) collective-permute-start(f32[4,128,128]{2,1,0:T(8,128)} %get-tuple-element.11), channel_id=1, source_target_pairs={{8,12},{10,14},{9,13},{11,15},{24,28},{26,30},{25,29},{27,31}} | collective-permute-start | bytes 786440 | tf_op jit(solution)/shard_map/ppermute | solution.py:29
  44.5 23.6 %collective-permute-start.11 = (f32[4,128,128]{2,1,0:T(8,128)}, f32[4,128,128]{2,1,0:T(8,128)}, u32[]{:S(2)}, u32[]{:S(2)}) collective-permute-start(f32[4,128,128]{2,1,0:T(8,128)} %get-tuple-element.9), channel_id=1, source_target_pairs={{8,12},{10,14},{9,13},{11,15},{24,28},{26,30},{25,29},{27,31}} | collective-permute-start | bytes 786440 | tf_op jit(solution)/shard_map/ppermute | solution.py:29
  46.7 24.2 %collective-permute-start.7 = (f32[4,128,128]{2,1,0:T(8,128)}, f32[4,128,128]{2,1,0:T(8,128)}, u32[]{:S(2)}, u32[]{:S(2)}) collective-permute-start(f32[4,128,128]{2,1,0:T(8,128)} %get-tuple-element.7), channel_id=1, source_target_pairs={{8,12},{10,14},{9,13},{11,15},{24,28},{26,30},{25,29},{27,31}} | collective-permute-start | bytes 786440 | tf_op jit(solution)/shard_map/ppermute | solution.py:29
  70.9 3.1 %copy-start.3 = (f32[2048]{0:T(1024)S(1)}, f32[2048]{0:T(1024)}, u32[]{:S(2)}) copy-start(f32[2048]{0:T(1024)} %param.7) | copy-start | bytes 24580
  73.5 9.9 %collective-permute-start.16 = (bf16[16,128,128]{2,1,0:T(8,128)(2,1)S(1)}, bf16[16,128,128]{2,1,0:T(8,128)(2,1)S(1)}, u32[]{:S(2)}, u32[]{:S(2)}) collective-permute-start(bf16[16,128,128]{2,1,0:T(8,128)(2,1)S(1)} %pad_maximum_fusion.1), channel_id=1, source_target_pairs={{0,2},{4,6},{8,10},{12,14},{2,0},{6,4},{10,8},{14,12},{1,3},{5,7},... | collective-permute-start | bytes 1572872 | tf_op jit(solution)/shard_map/ppermute | solution.py:32
  74.0 1.2 %collective-permute-start.17 = (f32[2048]{0:T(1024)S(1)}, f32[2048]{0:T(1024)S(1)}, u32[]{:S(2)}, u32[]{:S(2)}) collective-permute-start(f32[2048]{0:T(1024)S(1)} %copy-done.3), channel_id=1, source_target_pairs={{0,1},{1,0},{2,3},{3,2},{4,5},{5,4},{6,7},{7,6},{8,9},{9,8},{10,11... | collective-permute-start | bytes 24584 | tf_op jit(solution)/shard_map/ppermute | solution.py:123
  83.4 0.8 copy-start.2

commit v18 on v15

--- a/solution.py
+++ b/solution.py
@@ -17,11 +17,11 @@
     mine_all = lax.dynamic_slice_in_dim(terms, mine_at * half, half, 0)
     other_all = lax.dynamic_slice_in_dim(terms, (1 - mine_at) * half, half, 0)
     swap = [(2 * i, 2 * i + 1) for i in range(pairs)] + [(2 * i + 1, 2 * i) for i in range(pairs)]
-    step = half // pieces
+    ends = [sum(pieces[:n + 1]) * half // sum(pieces) for n in range(len(pieces))]
     keeps, backs = [], []
-    for piece in range(pieces):
-        mine = mine_all[piece * step:(piece + 1) * step]
-        got = lax.ppermute(other_all[piece * step:(piece + 1) * step], axis, swap)
+    for start, end in zip([0] + ends[:-1], ends):
+        mine = mine_all[start:end]
+        got = lax.ppermute(other_all[start:end], axis, swap)
         total = mine + got
         carried = jnp.zeros_like(total)
         for hop in range(1, pairs):
@@ -128,7 +128,7 @@
     keyset = key_rows.reshape(seq_count * row_count, feat_count)
     valset = value_rows.reshape(seq_count * row_count, feat_count)
     state_terms = state_terms_of(keyset, valset, 16)
-    keep, back = pair_chain_prefix(state_terms, "ctx", 4)
+    keep, back = pair_chain_prefix(state_terms, "ctx", (8, 4, 2, 2))
     normed = attend_of(query, keyset, valset, keep, back, lax.axis_index("ctx") % 2, full_gain, 8)
     return normed.reshape(seq_count, row_count, feat_count)
 

time: 95.8 us -> 97.5 us (1.018)
  local copies, waits for them, and re-layouts: 1.13 us -> 4.63 us
  waiting for transfers between devices: 50 us -> 46.6 us
  other arithmetic: 9.86 us -> 11.4 us
    ppermute x12, waiting for transfers between devices: 21.6 us -> 28.4 us  [pair_chain_prefix(): carried = carried + lax.ppermute(carried + total, axis, links)]
    ppermute x4, waiting for transfers between devices: 22.9 us -> 16.1 us  [pair_chain_prefix(): got = lax.ppermute(other_all[start:end], axis, swap)]
    slice x1 -> x3, local copies, waits for them, and re-layouts: 1.12 us -> 3.82 us  [pair_chain_prefix(): got = lax.ppermute(other_all[start:end], axis, swap)]
    add x2 -> x4, other arithmetic: 2.26 us -> 4.58 us  [pair_chain_prefix(): total = mine + got]
    ppermute x4, waiting for transfers between devices: 4.31 us -> 2.08 us  [pair_chain_prefix(): backs.append(lax.ppermute(send, axis, swap))]
    ppermute x4, starting transfers between devices: 4.12 us -> 2.52 us  [pair_chain_prefix(): backs.append(lax.ppermute(send, axis, swap))]
    add x8, other arithmetic: 3.41 us -> 2.24 us  [pair_chain_prefix(): carried = carried + lax.ppermute(carried + total, axis, links)]
    ppermute x1, waiting for transfers between devices: 1.15 us -> 0.01 us  [shards(): other_gain = lax.ppermute(gain, 'dp', pair)]
  transfers between devices with their start and end apart: 21 -> 21, of which waited for: 13 -> 9; matrix products, arithmetic and copies ran while one was open for 5% -> 14% of each run, Pallas kernels for 0% -> 0%
where the time goes in v18:
time: 97.5 us; the launch traced here: 96.1 us
  waiting for transfers between devices  46.6 us (48%)
  starting transfers between devices  17.1 us (18%)
  Pallas kernels  16 us (16%)
  other arithmetic  11.4 us (12%)
  local copies, waits for them, and re-layouts  4.63 us (5%)
    ppermute x12, waiting for transfers between devices, pair_chain_prefix(): carried = carried + lax.ppermute(carried + total, axis, links)  28.4 us
    ppermute x4, waiting for transfers between devices, pair_chain_prefix(): got = lax.ppermute(other_all[start:end], axis, swap)  16.1 us
    pallas_call x1, Pallas kernels, attend_of(): pl.pallas_call(attend_kernel, grid_spec=pltpu.PrefetchScalarGridSpec(num_...  11.6 us
    ppermute x12, starting transfers between devices, pair_chain_prefix(): carried = carried + lax.ppermute(carried + total, axis, links)  11.4 us
    add x4, other arithmetic, pair_chain_prefix(): total = mine + got  4.58 us
    pallas_call x1, Pallas kernels, state_terms_of(): pl.pallas_call(state_kernel, grid=(H // group,), in_specs=[pl.BlockSpec((...  4.45 us
    slice x3, local copies, waits for them, and re-layouts, pair_chain_prefix(): got = lax.ppermute(other_all[start:end], axis, swap)  3.82 us
    ppermute x4, starting transfers between devices, pair_chain_prefix(): got = lax.ppermute(other_all[start:end], axis, swap)  3.16 us
  transfers between devices with their start and end apart: 21, of which 9 were waited for; matrix products, arithmetic and copies ran while one was open for 14% of the time, Pallas kernels for 0%

profile of v18, /device:TPU:30, one launch (start us, length us, event | category | flops | bytes accessed | tf_op | source)
XLA Modules:
  0.0 96.1 jit_solution(16298036384440395187)
XLA Ops:
  0.0 4.4 %shard_map.46 = f32[32,128,128]{2,1,0:T(8,128)} custom-call(bf16[384,4096]{1,0:T(8,128)(2,1)} %bitcast.6, bf16[384,4096]{1,0:T(8,128)(2,1)} %bitcast.8), custom_call_target="tpu_custom_call" | custom-call | tf_op jit(solution)/shard_map/pallas_call | solution.py:49
  4.5 1.2 %constant_dynamic-slice_fusion.2 = f32[8,128,128]{2,1,0:T(8,128)S(1)} fusion(f32[32,128,128]{2,1,0:T(8,128)} %shard_map.46, s32[]{:T(128)S(6)} %select_n.79), kind=kLoop, calls=%fused_computation.19 | loop fusion | bytes 1048580 | tf_op jit(solution)/shard_map/slice | solution.py:24
  5.7 0.6 collective-permute-start
  6.3 1.7 %constant_dynamic-slice_fusion.1 = f32[4,128,128]{2,1,0:T(8,128)} fusion(f32[32,128,128]{2,1,0:T(8,128)} %shard_map.46, s32[]{:T(128)S(6)} %add.127), kind=kLoop, calls=%fused_computation.18 | loop fusion | bytes 524292 | tf_op jit(solution)/shard_map/slice | solution.py:24
  7.9 1.5 %collective-permute-start.4 = (f32[4,128,128]{2,1,0:T(8,128)}, f32[4,128,128]{2,1,0:T(8,128)}, u32[]{:S(2)}, u32[]{:S(2)}) collective-permute-start(f32[4,128,128]{2,1,0:T(8,128)} %constant_dynamic-slice_fusion.1), channel_id=1, source_target_pairs={{0,2},{4,6},{8,10},{12,14},{2,0},{6,4},{10,8},{14,12},{1,3},{5,7},... | collective-permute-start | bytes 786440 | tf_op jit(solution)/shard_map/ppermute | solution.py:24
  9.5 0.9 constant_dynamic-slice_fusion
  10.4 0.6 collective-permute-start.8
  10.9 9.6 %collective-permute-done = f32[8,128,128]{2,1,0:T(8,128)S(1)} collective-permute-done((f32[8,128,128]{2,1,0:T(8,128)S(1)}, f32[8,128,128]{2,1,0:T(8,128)S(1)}, u32[]{:S(2)}, u32[]{:S(2)}) %collective-permute-start) | collective-permute-done | bytes 524320 | tf_op jit(solution)/shard_map/ppermute | solution.py:24
  20.6 0.8 copy-done.1
  21.4 1.1 %dynamic-slice_add_fusion = f32[8,128,128]{2,1,0:T(8,128)S(1)} fusion(f32[8,128,128]{2,1,0:T(8,128)S(1)} %collective-permute-done, f32[32,128,128]{2,1,0:T(8,128)} %shard_map.46, s32[]{:T(128)S(6)} %select_n.78), kind=kLoop, calls=%fused_computation.4 | loop fusion | flops 131072 | bytes 1572868 | tf_op jit(solution)/shard_map/add | solution.py:25
  22.5 0.7 collective-permute-start.1
  23.2 4.8 %collective-permute-done.8 = f32[2,128,128]{2,1,0:T(8,128)} collective-permute-done((f32[2,128,128]{2,1,0:T(8,128)S(1)}, f32[2,128,128]{2,1,0:T(8,128)}, u32[]{:S(2)}, u32[]{:S(2)}) %collective-permute-start.8) | collective-permute-done | bytes 131104 | tf_op jit(solution)/shard_map/ppermute | solution.py:24
  27.9 1.6 %dynamic-slice_add_fusion.3 = (f32[2,128,128]{2,1,0:T(8,128)S(1)}, f32[2,128,128]{2,1,0:T(8,128)}) fusion(f32[2,128,128]{2,1,0:T(8,128)} %collective-permute-done.8, f32[32,128,128]{2,1,0:T(8,128)S(1)} %copy-done, s32[]{:T(128)S(6)} %add.128, s32[]{:T(128)S(6)} %add.131), kind=kLoop, calls=%fused_computation.13 | loop fusion | flops 32768 | bytes 655368 | tf_op jit(solution)/shard_map/add | solution.py:25
  29.5 0.5 collective-permute-start.12
  30.0 1.0 %dynamic-slice_add_fusion.1 = f32[4,128,128]{2,1,0:T(8,128)S(1)} fusion(f32[4,128,128]{2,1,0:T(8,128)} %collective-permute-done.4, f32[32,128,128]{2,1,0:T(8,128)S(1)} %copy-done, s32[]{:T(128)S(6)} %add.126), kind=kLoop, calls=%fused_computation.7 | loop fusion | flops 65536 | bytes 786436 | tf_op jit(solution)/shard_map/add | solution.py:25
  31.0 1.4 %collective-permute-start.5 = (f32[4,128,128]{2,1,0:T(8,128)S(1)}, f32[4,128,128]{2,1,0:T(8,128)}, u32[]{:S(2)}, u32[]{:S(2)}) collective-permute-start(f32[4,128,128]{2,1,0:T(8,128)S(1)} %dynamic-slice_add_fusion.1), channel_id=1, source_target_pairs={{0,4},{2,6},{1,5},{3,7},{16,20},{18,22},{17,21},{19,23}} | collective-permute-start | bytes 786440 | tf_op jit(solution)/shard_map/ppermute | solution.py:29
  32.4 0.7 collective-permute-start.9
  33.1 1.7 %collective-permute-done.12 = f32[2,128,128]{2,1,0:T(8,128)} collective-permute-done((f32[2,128,128]{2,1,0:T(8,128)}, f32[2,128,128]{2,1,0:T(8,128)}, u32[]{:S(2)}, u32[]{:S(2)}) %collective-permute-start.12) | collective-permute-done | bytes 131104 | tf_op jit(solution)/shard_map/ppermute | solution.py:24
  34.8 0.9 dynamic-slice_add_fusion.2
  35.7 0.7 collective-permute-start.13
  36.4 1.0 %add.105 = f32[4,128,128]{2,1,0:T(8,128)S(1)} add(f32[4,128,128]{2,1,0:T(8,128)} %collective-permute-done.5, f32[4,128,128]{2,1,0:T(8,128)S(1)} %dynamic-slice_add_fusion.1) | non-fusion elementwise | flops 65536 | bytes 786432 | tf_op jit(solution)/shard_map/add | solution.py:29
  37.4 0.7 collective-permute-start.6
  38.2 0.7 collective-permute-start.2
  38.9 0.6 pad_maximum_fusion.2
  39.5 0.7 collective-permute-start.10
  40.2 0.7 collective-permute-start.14
  40.9 1.0 %fusion.1 = (f32[4,128,128]{2,1,0:T(8,128)S(1)}, f32[4,128,128]{2,1,0:T(8,128)S(1)}) fusion(f32[4,128,128]{2,1,0:T(8,128)S(1)} %dynamic-slice_add_fusion.1, f32[4,128,128]{2,1,0:T(8,128)} %collective-permute-done.5, f32[4,128,128]{2,1,0:T(8,128)S(1)} %collective-permute-done.6), kind=kLoop, calls=%fused_computation.22 | loop fusion | flops 131072 | bytes 1310720 | tf_op jit(solution)/shard_map/add | solution.py:29
  41.9 1.4 %collective-permute-start.7 = (f32[4,128,128]{2,1,0:T(8,128)S(1)}, f32[4,128,128]{2,1,0:T(8,128)S(1)}, u32[]{:S(2)}, u32[]{:S(2)}) collective-permute-start(f32[4,128,128]{2,1,0:T(8,128)S(1)} %get-tuple-element.7), channel_id=1, source_target_pairs={{8,12},{10,14},{9,13},{11,15},{24,28},{26,30},{25,29},{27,31}} | collective-permute-start | bytes 786440 | tf_op jit(solution)/shard_map/ppermute | solution.py:29
  43.4 0.1 fusion
  43.5 1.3 %collective-permute-start.3 = (f32[8,128,128]{2,1,0:T(8,128)S(1)}, f32[8,128,128]{2,1,0:T(8,128)S(1)}, u32[]{:S(2)}, u32[]{:S(2)}) collective-permute-start(f32[8,128,128]{2,1,0:T(8,128)S(1)} %get-tuple-element.5), channel_id=1, source_target_pairs={{8,12},{10,14},{9,13},{11,15},{24,28},{26,30},{25,29},{27,31}} | collective-permute-start | bytes 1572872 | tf_op jit(solution)/shard_map/ppermute | solution.py:29
  44.8 1.3 %collective-permute-start.11 = (f32[2,128,128]{2,1,0:T(8,128)S(1)}, f32[2,128,128]{2,1,0:T(8,128)S(1)}, u32[]{:S(2)}, u32[]{:S(2)}) collective-permute-start(f32[2,128,128]{2,1,0:T(8,128)S(1)} %get-tuple-element.9), channel_id=1, source_target_pairs={{8,12},{10,14},{9,13},{11,15},{24,28},{26,30},{25,29},{27,31}} | collective-permute-start | bytes 393224 | tf_op jit(solution)/shard_map/ppermute | solution.py:29
  46.2 1.3 %collective-permute-start.15 = (f32[2,128,128]{2,1,0:T(8,128)S(1)}, f32[2,128,128]{2,1,0:T(8,128)S(1)}, u32[]{:S(2)}, u32[]{:S(2)}) collective-permute-start(f32[2,128,128]{2,1,0:T(8,128)S(1)} %get-tuple-element.11), channel_id=1, source_target_pairs={{8,12},{10,14},{9,13},{11,15},{24,28},{26,30},{25,29},{27,31}} | collective-permute-start | bytes 393224 | tf_op jit(solution)/shard_map/ppermute | solution.py:29
  47.5 14.6 %collective-permute-done.7 = f32[4,128,128]{2,1,0:T(8,128)S(1)} collective-permute-done((f32[4,128,128]{2,1,0:T(8,128)S(1)}, f32[4,128,128]{2,1,0:T(8,128)S(1)}, u32[]{:S(2)}, u32[]{:S(2)}) %collective-permute-start.7) | collective-permute-done | bytes 262176 | tf_op jit(solution)/shard_map/ppermute | solution.py:29
  62.1 1.0 %add_convert_fusion.2 = (bf16[4,128,128]{2,1,0:T(8,128)(2,1)S(1)}, bf16[4,128,128]{2,1,0:T(8,128)(2,1)S(1)}) fusion(f32[32,128,128]{2,1,0:T(8,128)S(1)} %copy-done, s32[]{:T(128)S(6)} %add.126, pred[]{:T(512)S(6)} %eq.9, f32[4,128,128]{2,1,0:T(8,128)S(1)} %get-tuple-element.8, f32[4,128,128]{2,1,0:T(8,128)S(1)} %collective-permute-done.7, ...), kind=kLoop, calls=%fused_computation.5 | loop fusion | flops 458752 | bytes 1310725 | tf_op jit(solution)/shard_map/convert_element_type | solution.py:31
  63.1 0.1 collective-permute-start.17
  63.2 11.5 %collective-permute-done.3 = f32[8,128,128]{2,1,0:T(8,128)S(1)} collective-permute-done((f32[8,128,128]{2,1,0:T(8,128)S(1)}, f32[8,128,128]{2,1,0:T(8,128)S(1)}, u32[]{:S(2)}, u32[]{:S(2)}) %collective-permute-start.3) | collective-permute-done | bytes 524320 | tf_op jit(solution)/shard_map/ppermute | solution.py:29
  74.7 0.1 add_convert_fusion
  74.8 0.4 collective-permute-start.16
  75.2 0.9 collective-permute-done.11
  76.1 1.4 %collective-permute-done.15 = f32[2,128,128]{2,1,0:T(8,128)S(1)} collective-permute-done((f32[2,128,128]{2,1,0:T(8,128)S(1)}, f32[2,128,128]{2,1,0:T(8,128)S(1)}, u32[]{:S(2)}, u32[]{:S(2)}) %collective-permute-start.15) | collective-permute-done | bytes 131104 | tf_op jit(solution)/shard_map/ppermute | solution.py:29
  77.5 1.0 %add_convert_fusion.5 = (bf16[2,128,128]{2,1,0:T(8,128)(2,1)S(1)}, bf16[2,128,128]{2,1,0:T(8,128)(2,1)S(1)}, bf16[2,128,128]{2,1,0:T(8,128)(2,1)S(1)}, bf16[2,128,128]{2,1,0:T(8,128)(2,1)S(1)}) fusion(f32[32,128,128]{2,1,0:T(8,128)S(1)} %copy-done, s32[]{:T(128)S(6)} %add.128, pred[]{:T(512)S(6)} %eq.9, f32[2,128,128]{2,1,0:T(8,128)S(1)} %get-tuple-element.10, ...), kind=kLoop, calls=%fused_computation.9 | loop fusion | flops 458752 | bytes 1310729 | tf_op jit(solution)/shard_map/convert_element_type | solution.py:31
  78.5 0.1 collective-permute-start.18
  78.6 2.0 %collective-permute-start.19 = (bf16[2,128,128]{2,1,0:T(8,128)(2,1)S(1)}, bf16[2,128,128]{2,1,0:T(8,128)(2,1)S(1)}, u32[]{:S(2)}, u32[]{:S(2)}) collective-permute-start(bf16[2,128,128]{2,1,0:T(8,128)(2,1)S(1)} %get-tuple-element.14), channel_id=1, source_target_pairs={{0,2},{4,6},{8,10},{12,14},{2,0},{6,4},{10,8},{14,12},{1,3},{5,7},... | collective-permute-start | bytes 196616 | tf_op jit(solution)/shard_map/ppermute | solution.py:32
  80.6 0.9 pad_maximum_fusion.keep_ref
  81.5 1.4 %collective-permute-done.18 = bf16[2,128,128]{2,1,0:T(8,128)(2,1)S(1)} collective-permute-done((bf16[2,128,128]{2,1,0:T(8,128)(2,1)S(1)}, bf16[2,128,128]{2,1,0:T(8,128)(2,1)S(1)}, u32[]{:S(2)}, u32[]{:S(2)}) %collective-permute-start.18) | collective-permute-done | bytes 65568 | tf_op jit(solution)/shard_map/ppermute | solution.py:32
  82.9 0.7 collective-permute-done.19
  83.6 0.9 pad_maximum_fusion.1.back_ref
  84.5 11.6 %shard_map.47 = bf16[384,4096]{1,0:T(8,128)(2,1)} custom-call(s32[1]{0:T(128)} %bitcast.mine_ref, bf16[384,4096]{1,0:T(8,128)(2,1)} %bitcast.10, bf16[384,4096]{1,0:T(8,128)(2,1)} %bitcast.7, bf16[384,4096]{1,0:T(8,128)(2,1)} %bitcast.9, bf16[16,128,128]{2,1,0:T(8,128)(2,1)} %pad_maximum_fusion.keep_ref, bf16[16,128,128]{2,1,0:T(8,128)(2,1)} %pad_maximum_fusion.1.back_ref, ...), custom_call_target="tpu_custom_call" | custom-call | tf_op jit(solution)/shard_map/pallas_call | solution.py:103
  (26 shorter events, 0.2 us)
Async XLA Ops:
  4.4 23.5 %copy-start = (f32[32,128,128]{2,1,0:T(8,128)S(1)}, f32[32,128,128]{2,1,0:T(8,128)}, u32[]{:S(2)}) copy-start(f32[32,128,128]{2,1,0:T(8,128)} %shard_map.46) | copy-start | bytes 6291460
  5.7 26.7 %copy-start.3 = (f32[2048]{0:T(1024)S(1)}, f32[2048]{0:T(1024)}, u32[]{:S(2)}) copy-start(f32[2048]{0:T(1024)} %param.7) | copy-start | bytes 24580
  5.7 14.9 %collective-permute-start = (f32[8,128,128]{2,1,0:T(8,128)S(1)}, f32[8,128,128]{2,1,0:T(8,128)S(1)}, u32[]{:S(2)}, u32[]{:S(2)}) collective-permute-start(f32[8,128,128]{2,1,0:T(8,128)S(1)} %constant_dynamic-slice_fusion.2), channel_id=1, source_target_pairs={{0,2},{4,6},{8,10},{12,14},{2,0},{6,4},{10,8},{14,12},{1,3},{5,7},... | collective-permute-start | bytes 1572872 | tf_op jit(solution)/shard_map/ppermute | solution.py:24
  7.9 22.1 %collective-permute-start.4 = (f32[4,128,128]{2,1,0:T(8,128)}, f32[4,128,128]{2,1,0:T(8,128)}, u32[]{:S(2)}, u32[]{:S(2)}) collective-permute-start(f32[4,128,128]{2,1,0:T(8,128)} %constant_dynamic-slice_fusion.1), channel_id=1, source_target_pairs={{0,2},{4,6},{8,10},{12,14},{2,0},{6,4},{10,8},{14,12},{1,3},{5,7},... | collective-permute-start | bytes 786440 | tf_op jit(solution)/shard_map/ppermute | solution.py:24
  10.4 17.6 %collective-permute-start.8 = (f32[2,128,128]{2,1,0:T(8,128)S(1)}, f32[2,128,128]{2,1,0:T(8,128)}, u32[]{:S(2)}, u32[]{:S(2)}) collective-permute-start(f32[2,128,128]{2,1,0:T(8,128)S(1)} %constant_dynamic-slice_fusion), channel_id=1, source_target_pairs={{0,2},{4,6},{8,10},{12,14},{2,0},{6,4},{10,8},{14,12},{1,3},{5,7},... | collective-permute-start | bytes 393224 | tf_op jit(solution)/shard_map/ppermute | solution.py:24
  20.6 0.8 copy-start.1
  22.5 15.6 %collective-permute-start.1 = (f32[8,128,128]{2,1,0:T(8,128)S(1)}, f32[8,128,128]{2,1,0:T(8,128)S(1)}, u32[]{:S(2)}, u32[]{:S(2)}) collective-permute-start(f32[8,128,128]{2,1,0:T(8,128)S(1)} %dynamic-slice_add_fusion), channel_id=1, source_target_pairs={{0,4},{2,6},{1,5},{3,7},{16,20},{18,22},{17,21},{19,23}} | collective-permute-start | bytes 1572872 | tf_op jit(solution)/shard_map/ppermute | solution.py:29
  29.5 5.3 %collective-permute-start.12 = (f32[2,128,128]{2,1,0:T(8,128)}, f32[2,128,128]{2,1,0:T(8,128)}, u32[]{:S(2)}, u32[]{:S(2)}) collective-permute-start(f32[2,128,128]{2,1,0:T(8,128)} %get-tuple-element.16), channel_id=1, source_target_pairs={{0,2},{4,6},{8,10},{12,14},{2,0},{6,4},{10,8},{14,12},{1,3},{5,7},... | collective-permute-start | bytes 393224 | tf_op jit(solution)/shard_map/ppermute | solution.py:24
  31.0 5.4 %collective-permute-start.5 = (f32[4,128,128]{2,1,0:T(8,128)S(1)}, f32[4,128,128]{2,1,0:T(8,128)}, u32[]{:S(2)}, u32[]{:S(2)}) collective-permute-start(f32[4,128,128]{2,1,0:T(8,128)S(1)} %dynamic-slice_add_fusion.1), channel_id=1, source_target_pairs={{0,4},{2,6},{1,5},{3,7},{16,20},{18,22},{17,21},{19,23}} | collective-permute-start | bytes 786440 | tf_op jit(solution)/shard_map/ppermute | solution.py:29
  32.4 6.5 %collective-permute-start.20 = (f32[2048]{0:T(1024)S(1)}, f32[2048]{0:T(1024)S(1)}, u32[]{:S(2)}, u32[]{:S(2)}) collective-permute-start(f32[2048]{0:T(1024)S(1)} %copy-done.3), channel_id=1, source_target_pairs={{0,1},{1,0},{2,3},{3,2},{4,5},{5,4},{6,7},{7,6},{8,9},{9,8},{10,11... | collective-permute-start | bytes 24584 | tf_op jit(solution)/shard_map/ppermute | solution.py:123
  32.4 7.1 %collective-permute-start.9 = (f32[2,128,128]{2,1,0:T(8,128)S(1)}, f32[2,128,128]{2,1,0:T(8,128)S(1)}, u32[]{:S(2)}, u32[]{:S(2)}) collective-permute-start(f32[2,128,128]{2,1,0:T(8,128)S(1)} %get-tuple-element.15), channel_id=1, source_target_pairs={{0,4},{2,6},{1,5},{3,7},{16,20},{18,22},{17,21},{19,23}} | collective-permute-start | bytes 393224 | tf_op jit(solution)/shard_map/ppermute | solution.py:29
  35.7 4.5 %collective-permute-start.13 = (f32[2,128,128]{2,1,0:T(8,128)S(1)}, f32[2,128,128]{2,1,0:T(8,128)S(1)}, u32[]{:S(2)}, u32[]{:S(2)}) collective-permute-start(f32[2,128,128]{2,1,0:T(8,128)S(1)} %dynamic-slice_add_fusion.2), channel_id=1, source_target_pairs={{0,4},{2,6},{1,5},{3,7},{16,20},{18,22},{17,21},{19,23}} | collective-permute-start | bytes 393224 | tf_op jit(solution)/shard_map/ppermute | solution.py:29
  37.4 3.5 %collective-permute-start.6 = (f32[4,128,128]{2,1,0:T(8,128)S(1)}, f32[4,128,128]{2,1,0:T(8,128)S(1)}, u32[]{:S(2)}, u32[]{:S(2)}) collective-permute-start(f32[4,128,128]{2,1,0:T(8,128)S(1)} %add.105), channel_id=1, source_target_pairs={{4,8},{6,10},{5,9},{7,11},{20,24},{22,26},{21,25},{23,27}} | collective-permute-start | bytes 786440 | tf_op jit(solution)/shard_map/ppermute | solution.py:29
  38.2 5.2 %collective-permute-start.2 = (f32[8,128,128]{2,1,0:T(8,128)S(1)}, f32[8,128,128]{2,1,0:T(8,128)S(1)}, u32[]{:S(2)}, u32[]{:S(2)}) collective-permute-start(f32[8,128,128]{2,1,0:T(8,128)S(1)} %add.99), channel_id=1, source_target_pairs={{4,8},{6,10},{5,9},{7,11},{20,24},{22,26},{21,25},{23,27}} | collective-permute-start | bytes 1572872 | tf_op jit(solution)/shard_map/ppermute | solution.py:29
  39.5 5.3 %collective-permute-start.10 = (f32[2,128,128]{2,1,0:T(8,128)S(1)}, f32[2,128,128]{2,1,0:T(8,128)S(1)}, u32[]{:S(2)}, u32[]{:S(2)}) collective-permute-start(f32[2,128,128]{2,1,0:T(8,128)S(1)} %add.111), channel_id=1, source_target_pairs={{4,8},{6,10},{5,9},{7,11},{20,24},{22,26},{21,25},{23,27}} | collective-permute-start | bytes 393224 | tf_op jit(solution)/shard_map/ppermute | solution.py:29
  40.2 5.9 %collective-permute-start.14 = (f32[2,128,128]{2,1,0:T(8,128)S(1)}, f32[2,128,128]{2,1,0:T(8,128)S(1)}, u32[]{:S(2)}, u32[]{:S(2)}) collective-permute-start(f32[2,128,128]{2,1,0:T(8,128)S(1)} %add.117), channel_id=1, source_target_pairs={{4,8},{6,10},{5,9},{7,11},{20,24},{22,26},{21,25},{23,27}} | collective-permute-start | bytes 393224 | tf_op jit(solution)/shard_map/ppermute | solution.py:29
  41.9 32.8 %copy-start.2 = (f32[8,128,128]{2,1,0:T(8,128)S(1)}, f32[8,128,128]{2,1,0:T(8,128)}, u32[]{:S(2)}) copy-start(f32[8,128,128]{2,1,0:T(8,128)} %copy-done.1) | copy-start | bytes 1572868
  41.9 20.2 %collective-permute-start.7 = (f32[4,128,128]{2,1,0:T(8,128)S(1)}, f32[4,128,128]{2,1,0:T(8,128)S(1)}, u32[]{:S(2)}, u32[]{:S(2)}) collective-permute-start(f32[4,128,128]{2,1,0:T(8,128)S(1)} %get-tuple-element.7), channel_id=1, source_target_pairs={{8,12},{10,14},{9,13},{11,15},{24,28},{26,30},{25,29},{27,31}} | collective-permute-start | bytes 786440 | tf_op jit(solution)/shard_map/ppermute | solution.py:29
  43.5 31.2 %collective-permute-start.3 = (f32[8,128,128]{2,1,0:T(8,128)S(1)}, f32[8,128,128]{2,1,0:T(8,128)S(1)}, u32[]{:S(2)}, u32[]{:S(2)}) collective-permute-start(f32[8,128,128]{2,1,0:T(8,128)S(1)} %get-tuple-element.5), channel_id=1, source_target_pairs={{8,12},{10,14},{9,13},{11,15},{24,28},{26,30},{25,29},{27,31}} | collective-permute-start | bytes 1572872 | tf_op jit(solution)/shard_map/ppermute | solution.py:29
  44.8 31.2 %collective-permute-start.11 = (f32[2,128,128]{2,1,0:T(8,128)S(1)}, f32[2,128,128]{2,1,0:T(8,128)S(1)}, u32[]{:S(2)}, u32[]{:S(2)}) collective-permute-start(f32[2,128,128]{2,1,0:T(8,128)S(1)} %get-tuple-element.9), channel_id=1, source_target_pairs={{8,12},{10,14},{9,13},{11,15},{24,28},{26,30},{25,29},{27,31}} | collective-permute-start | bytes 393224 | tf_op jit(solution)/shard_map/ppermute | solution.py:29
  46.2 31.3 %collective-permute-start.15 = (f32[2,128,128]{2,1,0:T(8,128)S(1)}, f32[2,128,128]{2,1,0:T(8,128)S(1)}, u32[]{:S(2)}, u32[]{:S(2)}) collective-permute-start(f32[2,128,128]{2,1,0:T(8,128)S(1)} %get-tuple-element.11), channel_id=1, source_target_pairs={{8,12},{10,14},{9,13},{11,15},{24,28},{26,30},{25,29},{27,31}} | collective-permute-start | bytes 393224 | tf_op jit(solution)/shard_map/ppermute | solution.py:29
  63.1 20.4 %collective-permute-start.17 = (bf16[4,128,128]{2,1,0:T(8,128)(2,1)S(1)}, bf16[4,128,128]{2,1,0:T(8,128)(2,1)S(1)}, u32[]{:S(2)}, u32[]{:S(2)}) collective-permute-start(bf16[4,128,128]{2,1,0:T(8,128)(2,1)S(1)} %get-tuple-element.19), channel_id=1, source_target_pairs={{0,2},{4,6},{8,10},{12,14},{2,0},{6,4},{10,8},{14,12},{1,3},{5,7},... | collective-permute-start | bytes 393224 | tf_op jit(solution)/shard_map/ppermute | solution.py:32
  74.8 8.7 %collective-permute-start.16 = (bf16[8,128,128]{2,1,0:T(8,128)(2,1)S(1)}, bf16[8,128,128]{2,1,0:T(8,128)(2,1)S(1)}, u32[]{:S(2)}, u32[]{:S(2)}) collective-permute-start(bf16[8,128,128]{2,1,0:T(8,128)(2,1)S(1)} %get-tuple-element.17), channel_id=1, source_target_pairs={{0,2},{4,6},{8,10},{12,14},{2,0},{6,4},{10,8},{14,12},{1,3},{5,7},... | collective-permute-start | bytes 786440 | tf_op jit(solution)/shard_map/ppermute | solution.py:32
  78.5 4.3 %collective-permute-start.18 = (bf16[2,128,128]{2,1,0:T(8,128)(2,1)S(1)}, bf16[2,128,128]{2,1,0:T(8,128)(2,1)S(1)}, u32[]{:S(2)}, u32[]{:S(2)}) collective-permute-start(bf16[2,128,128]{2,1,0:T(8,128)(2,1)S(1)} %get-tuple-element.13), channel_id=1, source_target_pairs={{0,2},{4,6},{8,10},{12,14},{2,0},{6,4},{10,8},{14,12},{1,3},{5,7},... | collective-permute-start | bytes 196616 | tf_op jit(solution)/shard_map/ppermute | solution.py:32
  78.6 5.0 %collective-permute-start.19 = (bf16[2,128,128]{2,1,0:T(8,128)(2,1)S(1)}, bf16[2,128,128]{2,1,0:T(8,128)(2,1)S(1)}, u32[]{:S(2)}, u32[]{:S(2)}) collective-permute-start(bf16[2,128,128]{2,1,0:T(8,128)(2,1)S(1)} %get-tuple-element.14), channel_id=1, source_target_pairs={{0,2},{4,6},{8,10},{12,14},{2,0},{6,4},{10,8},{14,12},{1,3},{5,7},... | collective-permute-start | bytes 196616 | tf_op jit(solution)/shard_map/ppermute | solution.py:32

commit v19 on v15

--- a/solution.py
+++ b/solution.py
@@ -56,20 +56,11 @@
     )(keyset, valset)
 
 
-def attend_kernel(mine_ref, query_ref, key_ref, val_ref, keep_ref, back_ref, gain_ref, out_ref, acc_ref,
-                  sumsq_ref):
-    step = pl.program_id(0)
-    row_count, width = query_ref.shape
-    heads, head_size, _ = keep_ref.shape
-    own = step // (pl.num_programs(0) // 2) == mine_ref[0]
+def attend_heads(query_ref, key_ref, val_ref, prefix_ref, store, sumsq):
+    row_count = query_ref.shape[0]
+    heads, head_size, _ = prefix_ref.shape
     causal = (lax.broadcasted_iota(jnp.int32, (row_count, row_count), 0)
               >= lax.broadcasted_iota(jnp.int32, (row_count, row_count), 1))
-
-    @pl.when(step == 0)
-    def _():
-        sumsq_ref[...] = jnp.zeros_like(sumsq_ref)
-
-    sumsq = sumsq_ref[...]
     for head in range(heads):
         cols = slice(head * head_size, (head + 1) * head_size)
         query = query_ref[:, cols]
@@ -77,41 +68,90 @@
                                  preferred_element_type=jnp.float32)
         weights = jnp.where(causal, scores, 0.0).astype(jnp.bfloat16)
         lhs = jnp.concatenate([weights, query], axis=1)
-        prefix = jnp.where(own, keep_ref[head], back_ref[head])
-        rhs = jnp.concatenate([val_ref[:, cols], prefix], axis=0)
+        rhs = jnp.concatenate([val_ref[:, cols], prefix_ref[head]], axis=0)
         attended = jnp.dot(lhs, rhs, preferred_element_type=jnp.float32)
+        store(cols, attended)
+        sumsq = sumsq + attended * attended
+    return sumsq
+
+
+def own_kernel(mine_ref, query_ref, key_ref, val_ref, keep_ref, att_ref, sumsq_ref):
+    @pl.when(pl.program_id(0) == 0)
+    def _():
+        sumsq_ref[...] = jnp.zeros_like(sumsq_ref)
+
+    def store(cols, attended):
+        att_ref[:, cols] = attended
+
+    sumsq_ref[...] = attend_heads(query_ref, key_ref, val_ref, keep_ref, store, sumsq_ref[...])
+
+
+def other_kernel(mine_ref, query_ref, key_ref, val_ref, back_ref, own_ref, own_sumsq_ref, gain_ref, out_ref,
+                 acc_ref, sumsq_ref):
+    step = pl.program_id(0)
+    row_count, width = query_ref.shape
+
+    @pl.when(step == 0)
+    def _():
+        sumsq_ref[...] = own_sumsq_ref[...]
+
+    def store(cols, attended):
         acc_ref[step, :, cols] = attended
-        sumsq = sumsq + attended * attended
+
+    sumsq = attend_heads(query_ref, key_ref, val_ref, back_ref, store, sumsq_ref[...])
     sumsq_ref[...] = sumsq
 
     @pl.when(step == pl.num_programs(0) - 1)
     def _():
         total = jnp.sum(sumsq, axis=1, keepdims=True)
-        scale = lax.rsqrt(total / (width * pl.num_programs(0)) + 1e-05)
-        for part in range(acc_ref.shape[0]):
-            cols = slice(part * width, (part + 1) * width)
-            out_ref[:, cols] = (acc_ref[part] * scale * gain_ref[:, cols]).astype(out_ref.dtype)
+        feat_count = out_ref.shape[1]
+        scale = lax.rsqrt(total / feat_count + 1e-05)
+        half = feat_count // 2
+        for own_at in range(2):
+            @pl.when(mine_ref[0] == own_at)
+            def _():
+                own = slice(own_at * half, (own_at + 1) * half)
+                out_ref[:, own] = (own_ref[...] * scale * gain_ref[:, own]).astype(out_ref.dtype)
+                for part in range(acc_ref.shape[0]):
+                    at = (1 - own_at) * half + part * width
+                    cols = slice(at, at + width)
+                    out_ref[:, cols] = (acc_ref[part] * scale * gain_ref[:, cols]).astype(out_ref.dtype)
 
 
 def attend_of(query, keyset, valset, keep, back, mine_at, full_gain, group):
     row_count, feat_count = query.shape
     head_size = feat_count // H
     width = group * head_size
-    steps = H // group
-    spec = pl.BlockSpec((row_count, width), lambda g, at: (0, g))
-    half_spec = pl.BlockSpec((group, head_size, head_size), lambda g, at: (g % (steps // 2), 0, 0))
-    return pl.pallas_call(
-        attend_kernel,
+    steps = H // group // 2
+    mine = jnp.reshape(mine_at, (1,)).astype(jnp.int32)
+    own_spec = pl.BlockSpec((row_count, width), lambda g, at: (0, at[0] * steps + g))
+    other_spec = pl.BlockSpec((row_count, width), lambda g, at: (0, (1 - at[0]) * steps + g))
+    half_spec = pl.BlockSpec((group, head_size, head_size), lambda g, at: (g, 0, 0))
+    sumsq_spec = pl.BlockSpec((row_count, head_size), lambda g, at: (0, 0))
+    own, own_sumsq = pl.pallas_call(
+        own_kernel,
         grid_spec=pltpu.PrefetchScalarGridSpec(
             num_scalar_prefetch=1,
             grid=(steps,),
-            in_specs=[spec, spec, spec, half_spec, half_spec,
+            in_specs=[own_spec, own_spec, own_spec, half_spec],
+            out_specs=[pl.BlockSpec((row_count, width), lambda g, at: (0, g)), sumsq_spec]),
+        out_shape=[jax.ShapeDtypeStruct((row_count, feat_count // 2), jnp.float32),
+                   jax.ShapeDtypeStruct((row_count, head_size), jnp.float32)],
+    )(mine, query, keyset, valset, keep)
+    return pl.pallas_call(
+        other_kernel,
+        grid_spec=pltpu.PrefetchScalarGridSpec(
+            num_scalar_prefetch=1,
+            grid=(steps,),
+            in_specs=[other_spec, other_spec, other_spec, half_spec,
+                      pl.BlockSpec((row_count, feat_count // 2), lambda g, at: (0, 0)),
+                      sumsq_spec,
                       pl.BlockSpec((1, feat_count), lambda g, at: (0, 0))],
             out_specs=pl.BlockSpec((row_count, feat_count), lambda g, at: (0, 0)),
             scratch_shapes=[pltpu.VMEM((steps, row_count, width), jnp.float32),
                             pltpu.VMEM((row_count, head_size), jnp.float32)]),
         out_shape=jax.ShapeDtypeStruct((row_count, feat_count), jnp.bfloat16),
-    )(jnp.reshape(mine_at, (1,)).astype(jnp.int32), query, keyset, valset, keep, back, full_gain)
+    )(mine, query, keyset, valset, back, own, own_sumsq, full_gain)
 
 
 def shards(query_rows, key_rows, value_rows, gain):

time: 95.8 us -> 95.1 us (level)
  waiting for transfers between devices: 50 us -> 45.8 us
  Pallas kernels: 16.1 us -> 19.3 us
    ppermute x4, waiting for transfers between devices: 4.31 us -> 0.01 us  [pair_chain_prefix(): backs.append(lax.ppermute(send, axis, swap))]
    pallas_call x1 -> x2, Pallas kernels: 11.6 us -> 14.8 us  [the longest x1 8.61 us: attend_of(): pl.pallas_call(other_kernel, grid_spec=pltpu.PrefetchScalarGridSpec(num_s...]
  transfers between devices with their start and end apart: 21 -> 21, of which waited for: 13 -> 9; matrix products, arithmetic and copies ran while one was open for 5% -> 5% of each run, Pallas kernels for 0% -> 7%
where the time goes in v19:
time: 95.1 us; the launch traced here: 94.7 us
  waiting for transfers between devices  45.8 us (48%)
  Pallas kernels  19.3 us (20%)
  starting transfers between devices  17.7 us (19%)
  other arithmetic  10.5 us (11%)
  local copies, waits for them, and re-layouts  1.13 us (1%)
    ppermute x4, waiting for transfers between devices, pair_chain_prefix(): got = lax.ppermute(other_all[piece * step:(piece + 1) * step], axis, swap)  22.9 us
    ppermute x12, waiting for transfers between devices, pair_chain_prefix(): carried = carried + lax.ppermute(carried + total, axis, links)  21.7 us
    ppermute x12, starting transfers between devices, pair_chain_prefix(): carried = carried + lax.ppermute(carried + total, axis, links)  10.5 us
    pallas_call x1, Pallas kernels, attend_of(): pl.pallas_call(other_kernel, grid_spec=pltpu.PrefetchScalarGridSpec(num_s...  8.61 us
    pallas_call x1, Pallas kernels, attend_of(): pl.pallas_call(own_kernel, grid_spec=pltpu.PrefetchScalarGridSpec(num_sca...  6.23 us
    pallas_call x1, Pallas kernels, state_terms_of(): pl.pallas_call(state_kernel, grid=(H // group,), in_specs=[pl.BlockSpec((...  4.45 us
    ppermute x4, starting transfers between devices, pair_chain_prefix(): backs.append(lax.ppermute(send, axis, swap))  4.05 us
    add x8, other arithmetic, pair_chain_prefix(): carried = carried + lax.ppermute(carried + total, axis, links)  3.44 us
  transfers between devices with their start and end apart: 21, of which 9 were waited for; matrix products, arithmetic and copies ran while one was open for 5% of the time, Pallas kernels for 7%

profile of v19, /device:TPU:30, one launch (start us, length us, event | category | flops | bytes accessed | tf_op | source)
XLA Modules:
  0.0 94.7 jit_solution(17939915309012567151)
XLA Ops:
  0.0 4.4 %shard_map.46 = f32[32,128,128]{2,1,0:T(8,128)} custom-call(bf16[384,4096]{1,0:T(8,128)(2,1)} %bitcast.6, bf16[384,4096]{1,0:T(8,128)(2,1)} %bitcast.9), custom_call_target="tpu_custom_call" | custom-call | tf_op jit(solution)/shard_map/pallas_call | solution.py:49
  4.5 1.1 %constant_dynamic-slice_fusion.2 = f32[4,128,128]{2,1,0:T(8,128)S(1)} fusion(f32[32,128,128]{2,1,0:T(8,128)} %shard_map.46, s32[]{:T(128)S(6)} %select_n.67), kind=kLoop, calls=%fused_computation.19 | loop fusion | bytes 524292 | tf_op jit(solution)/shard_map/slice | solution.py:24
  5.6 0.6 collective-permute-start
  6.1 7.5 %collective-permute-done = f32[4,128,128]{2,1,0:T(8,128)S(1)} collective-permute-done((f32[4,128,128]{2,1,0:T(8,128)S(1)}, f32[4,128,128]{2,1,0:T(8,128)S(1)}, u32[]{:S(2)}, u32[]{:S(2)}) %collective-permute-start) | collective-permute-done | bytes 262176 | tf_op jit(solution)/shard_map/ppermute | solution.py:24
  13.7 2.2 %dynamic-slice_add_fusion.3 = (f32[4,128,128]{2,1,0:T(8,128)S(1)}, f32[4,128,128]{2,1,0:T(8,128)}, f32[4,128,128]{2,1,0:T(8,128)}, f32[4,128,128]{2,1,0:T(8,128)S(1)}) fusion(f32[4,128,128]{2,1,0:T(8,128)S(1)} %collective-permute-done, f32[32,128,128]{2,1,0:T(8,128)} %shard_map.46, s32[]{:T(128)S(6)} %select_n.66, s32[]{:T(128)S(6)} %add.129, s32[]{:T(128)S(6)} %add.127, ...), kind=kLoop, calls=%fused_computation.13 | loop fusion | flops 65536 | bytes 2359312 | tf_op jit(solution)/shard_map/add | solution.py:25
  15.9 0.5 collective-permute-start.10
  16.4 1.5 %collective-permute-start.5 = (f32[4,128,128]{2,1,0:T(8,128)}, f32[4,128,128]{2,1,0:T(8,128)S(1)}, u32[]{:S(2)}, u32[]{:S(2)}) collective-permute-start(f32[4,128,128]{2,1,0:T(8,128)} %get-tuple-element.23), channel_id=1, source_target_pairs={{0,2},{4,6},{8,10},{12,14},{2,0},{6,4},{10,8},{14,12},{1,3},{5,7},... | collective-permute-start | bytes 786440 | tf_op jit(solution)/shard_map/ppermute | solution.py:24
  17.9 0.5 collective-permute-start.15
  18.4 0.7 collective-permute-start.1
  19.1 6.2 %collective-permute-done.10 = f32[4,128,128]{2,1,0:T(8,128)S(1)} collective-permute-done((f32[4,128,128]{2,1,0:T(8,128)}, f32[4,128,128]{2,1,0:T(8,128)S(1)}, u32[]{:S(2)}, u32[]{:S(2)}) %collective-permute-start.10) | collective-permute-done | bytes 262176 | tf_op jit(solution)/shard_map/ppermute | solution.py:24
  25.3 5.6 %collective-permute-done.5 = f32[4,128,128]{2,1,0:T(8,128)S(1)} collective-permute-done((f32[4,128,128]{2,1,0:T(8,128)}, f32[4,128,128]{2,1,0:T(8,128)S(1)}, u32[]{:S(2)}, u32[]{:S(2)}) %collective-permute-start.5) | collective-permute-done | bytes 262176 | tf_op jit(solution)/shard_map/ppermute | solution.py:24
  30.9 3.5 %collective-permute-done.15 = f32[4,128,128]{2,1,0:T(8,128)S(1)} collective-permute-done((f32[4,128,128]{2,1,0:T(8,128)S(1)}, f32[4,128,128]{2,1,0:T(8,128)S(1)}, u32[]{:S(2)}, u32[]{:S(2)}) %collective-permute-start.15) | collective-permute-done | bytes 262176 | tf_op jit(solution)/shard_map/ppermute | solution.py:24
  34.5 0.1 dynamic-slice_add_fusion.2
  34.6 0.7 collective-permute-start.6
  35.2 0.7 collective-permute-start.11
  35.9 0.0 collective-permute-done.1
  36.0 0.7 collective-permute-start.2
  36.7 0.7 collective-permute-start.16
  37.4 0.0 collective-permute-done.6
  37.4 0.7 collective-permute-start.7
  38.1 0.0 copy-start.2
  38.2 0.7 collective-permute-start.12
  38.9 0.8 fusion
  39.6 1.3 %collective-permute-start.3 = (f32[4,128,128]{2,1,0:T(8,128)}, f32[4,128,128]{2,1,0:T(8,128)}, u32[]{:S(2)}, u32[]{:S(2)}) collective-permute-start(f32[4,128,128]{2,1,0:T(8,128)} %get-tuple-element.9), channel_id=1, source_target_pairs={{8,12},{10,14},{9,13},{11,15},{24,28},{26,30},{25,29},{27,31}} | collective-permute-start | bytes 786440 | tf_op jit(solution)/shard_map/ppermute | solution.py:29
  40.9 0.7 collective-permute-start.17
  41.6 0.0 collective-permute-done.7
  41.6 0.8 fusion.1
  42.4 1.3 %collective-permute-start.8 = (f32[4,128,128]{2,1,0:T(8,128)}, f32[4,128,128]{2,1,0:T(8,128)}, u32[]{:S(2)}, u32[]{:S(2)}) collective-permute-start(f32[4,128,128]{2,1,0:T(8,128)} %get-tuple-element.11), channel_id=1, source_target_pairs={{8,12},{10,14},{9,13},{11,15},{24,28},{26,30},{25,29},{27,31}} | collective-permute-start | bytes 786440 | tf_op jit(solution)/shard_map/ppermute | solution.py:29
  43.7 0.9 fusion.2
  44.6 1.3 %collective-permute-start.13 = (f32[4,128,128]{2,1,0:T(8,128)}, f32[4,128,128]{2,1,0:T(8,128)}, u32[]{:S(2)}, u32[]{:S(2)}) collective-permute-start(f32[4,128,128]{2,1,0:T(8,128)} %get-tuple-element.13), channel_id=1, source_target_pairs={{8,12},{10,14},{9,13},{11,15},{24,28},{26,30},{25,29},{27,31}} | collective-permute-start | bytes 786440 | tf_op jit(solution)/shard_map/ppermute | solution.py:29
  45.9 0.9 fusion.3
  46.8 1.3 %collective-permute-start.18 = (f32[4,128,128]{2,1,0:T(8,128)}, f32[4,128,128]{2,1,0:T(8,128)}, u32[]{:S(2)}, u32[]{:S(2)}) collective-permute-start(f32[4,128,128]{2,1,0:T(8,128)} %get-tuple-element.15), channel_id=1, source_target_pairs={{8,12},{10,14},{9,13},{11,15},{24,28},{26,30},{25,29},{27,31}} | collective-permute-start | bytes 786440 | tf_op jit(solution)/shard_map/ppermute | solution.py:29
  48.1 0.1 collective-permute-start.20
  48.2 1.1 %collective-permute-done.20 = f32[2048]{0:T(1024)S(1)} collective-permute-done((f32[2048]{0:T(1024)S(1)}, f32[2048]{0:T(1024)S(1)}, u32[]{:S(2)}, u32[]{:S(2)}) %collective-permute-start.20) | collective-permute-done | bytes 8224 | tf_op jit(solution)/shard_map/ppermute | solution.py:163
  49.3 6.7 %collective-permute-done.3 = f32[4,128,128]{2,1,0:T(8,128)} collective-permute-done((f32[4,128,128]{2,1,0:T(8,128)}, f32[4,128,128]{2,1,0:T(8,128)}, u32[]{:S(2)}, u32[]{:S(2)}) %collective-permute-start.3) | collective-permute-done | bytes 262176 | tf_op jit(solution)/shard_map/ppermute | solution.py:29
  56.0 6.4 %collective-permute-done.8 = f32[4,128,128]{2,1,0:T(8,128)} collective-permute-done((f32[4,128,128]{2,1,0:T(8,128)}, f32[4,128,128]{2,1,0:T(8,128)}, u32[]{:S(2)}, u32[]{:S(2)}) %collective-permute-start.8) | collective-permute-done | bytes 262176 | tf_op jit(solution)/shard_map/ppermute | solution.py:29
  62.3 5.8 %collective-permute-done.13 = f32[4,128,128]{2,1,0:T(8,128)} collective-permute-done((f32[4,128,128]{2,1,0:T(8,128)}, f32[4,128,128]{2,1,0:T(8,128)}, u32[]{:S(2)}, u32[]{:S(2)}) %collective-permute-start.13) | collective-permute-done | bytes 262176 | tf_op jit(solution)/shard_map/ppermute | solution.py:29
  68.1 2.8 %collective-permute-done.18 = f32[4,128,128]{2,1,0:T(8,128)} collective-permute-done((f32[4,128,128]{2,1,0:T(8,128)}, f32[4,128,128]{2,1,0:T(8,128)}, u32[]{:S(2)}, u32[]{:S(2)}) %collective-permute-start.18) | collective-permute-done | bytes 262176 | tf_op jit(solution)/shard_map/ppermute | solution.py:29
  71.0 2.5 %add_convert_fusion.7 = (bf16[4,128,128]{2,1,0:T(8,128)(2,1)}, bf16[4,128,128]{2,1,0:T(8,128)(2,1)}, bf16[4,128,128]{2,1,0:T(8,128)(2,1)}, bf16[4,128,128]{2,1,0...) fusion(f32[32,128,128]{2,1,0:T(8,128)S(1)} %copy-done, ...), kind=kLoop, calls=%fused_computation.9 | loop fusion | flops 1835008 | bytes 5242897 | tf_op jit(solution)/shard_map/convert_element_type | solution.py:31
  73.4 0.3 collective-permute-start.4
  73.8 1.7 %collective-permute-start.9 = (bf16[4,128,128]{2,1,0:T(8,128)(2,1)}, bf16[4,128,128]{2,1,0:T(8,128)(2,1)S(1)}, u32[]{:S(2)}, u32[]{:S(2)}) collective-permute-start(bf16[4,128,128]{2,1,0:T(8,128)(2,1)} %get-tuple-element.18), channel_id=1, source_target_pairs={{0,2},{4,6},{8,10},{12,14},{2,0},{6,4},{10,8},{14,12},{1,3},{5,7},... | collective-permute-start | bytes 393224 | tf_op jit(solution)/shard_map/ppermute | solution.py:32
  75.5 0.3 collective-permute-start.14
  75.8 1.7 %collective-permute-start.19 = (bf16[4,128,128]{2,1,0:T(8,128)(2,1)S(1)}, bf16[4,128,128]{2,1,0:T(8,128)(2,1)S(1)}, u32[]{:S(2)}, u32[]{:S(2)}) collective-permute-start(bf16[4,128,128]{2,1,0:T(8,128)(2,1)S(1)} %get-tuple-element.20), channel_id=1, source_target_pairs={{0,2},{4,6},{8,10},{12,14},{2,0},{6,4},{10,8},{14,12},{1,3},{5,7},... | collective-permute-start | bytes 393224 | tf_op jit(solution)/shard_map/ppermute | solution.py:32
  77.5 0.6 pad_maximum_fusion.2
  78.1 0.9 pad_maximum_fusion.1.keep_ref
  79.0 6.2 %shard_map.47 = (f32[384,2048]{1,0:T(8,128)}, f32[384,128]{1,0:T(8,128)}) custom-call(s32[1]{0:T(128)} %bitcast.mine_ref, bf16[384,4096]{1,0:T(8,128)(2,1)} %bitcast.12, bf16[384,4096]{1,0:T(8,128)(2,1)} %bitcast.7, bf16[384,4096]{1,0:T(8,128)(2,1)} %bitcast.10, bf16[16,128,128]{2,1,0:T(8,128)(2,1)} %pad_maximum_fusion.1.keep_ref), custom_call_target="tpu_custom_call" | custom-call | tf_op jit(solution)/shard_map/pallas_call | solution.py:131
  85.2 0.9 pad_maximum_fusion.back_ref
  86.1 8.6 %shard_map.48 = bf16[384,4096]{1,0:T(8,128)(2,1)} custom-call(s32[1]{0:T(128)} %bitcast.mine_ref, bf16[384,4096]{1,0:T(8,128)(2,1)} %bitcast.13, bf16[384,4096]{1,0:T(8,128)(2,1)} %bitcast.8, bf16[384,4096]{1,0:T(8,128)(2,1)} %bitcast.11, bf16[16,128,128]{2,1,0:T(8,128)(2,1)} %pad_maximum_fusion.back_ref, f32[384,2048]{1,0:T(8,128)} %get-tuple-element.7.own_ref, ...), custom_call_target="tpu_custom_call" | custom-call | tf_op jit(solution)/shard_map/pallas_call | solution.py:141
  (19 shorter events, 0.2 us)
Async XLA Ops:
  4.4 30.0 %copy-start = (f32[32,128,128]{2,1,0:T(8,128)S(1)}, f32[32,128,128]{2,1,0:T(8,128)}, u32[]{:S(2)}) copy-start(f32[32,128,128]{2,1,0:T(8,128)} %shard_map.46) | copy-start | bytes 6291460
  5.6 8.1 %collective-permute-start = (f32[4,128,128]{2,1,0:T(8,128)S(1)}, f32[4,128,128]{2,1,0:T(8,128)S(1)}, u32[]{:S(2)}, u32[]{:S(2)}) collective-permute-start(f32[4,128,128]{2,1,0:T(8,128)S(1)} %constant_dynamic-slice_fusion.2), channel_id=1, source_target_pairs={{0,2},{4,6},{8,10},{12,14},{2,0},{6,4},{10,8},{14,12},{1,3},{5,7},... | collective-permute-start | bytes 786440 | tf_op jit(solution)/shard_map/ppermute | solution.py:24
  13.7 2.2 %copy-start.1 = (f32[4,128,128]{2,1,0:T(8,128)}, f32[4,128,128]{2,1,0:T(8,128)S(1)}, u32[]{:S(2)}) copy-start(f32[4,128,128]{2,1,0:T(8,128)S(1)} %collective-permute-done) | copy-start | bytes 786436
  15.9 9.5 %collective-permute-start.10 = (f32[4,128,128]{2,1,0:T(8,128)}, f32[4,128,128]{2,1,0:T(8,128)S(1)}, u32[]{:S(2)}, u32[]{:S(2)}) collective-permute-start(f32[4,128,128]{2,1,0:T(8,128)} %get-tuple-element.22), channel_id=1, source_target_pairs={{0,2},{4,6},{8,10},{12,14},{2,0},{6,4},{10,8},{14,12},{1,3},{5,7},... | collective-permute-start | bytes 786440 | tf_op jit(solution)/shard_map/ppermute | solution.py:24
  16.4 14.6 %collective-permute-start.5 = (f32[4,128,128]{2,1,0:T(8,128)}, f32[4,128,128]{2,1,0:T(8,128)S(1)}, u32[]{:S(2)}, u32[]{:S(2)}) collective-permute-start(f32[4,128,128]{2,1,0:T(8,128)} %get-tuple-element.23), channel_id=1, source_target_pairs={{0,2},{4,6},{8,10},{12,14},{2,0},{6,4},{10,8},{14,12},{1,3},{5,7},... | collective-permute-start | bytes 786440 | tf_op jit(solution)/shard_map/ppermute | solution.py:24
  17.9 16.6 %collective-permute-start.15 = (f32[4,128,128]{2,1,0:T(8,128)S(1)}, f32[4,128,128]{2,1,0:T(8,128)S(1)}, u32[]{:S(2)}, u32[]{:S(2)}) collective-permute-start(f32[4,128,128]{2,1,0:T(8,128)S(1)} %get-tuple-element.24), channel_id=1, source_target_pairs={{0,2},{4,6},{8,10},{12,14},{2,0},{6,4},{10,8},{14,12},{1,3},{5,7},... | collective-permute-start | bytes 786440 | tf_op jit(solution)/shard_map/ppermute | solution.py:24
  18.4 17.5 %collective-permute-start.1 = (f32[4,128,128]{2,1,0:T(8,128)S(1)}, f32[4,128,128]{2,1,0:T(8,128)S(1)}, u32[]{:S(2)}, u32[]{:S(2)}) collective-permute-start(f32[4,128,128]{2,1,0:T(8,128)S(1)} %get-tuple-element.21), channel_id=1, source_target_pairs={{0,4},{2,6},{1,5},{3,7},{16,20},{18,22},{17,21},{19,23}} | collective-permute-start | bytes 786440 | tf_op jit(solution)/shard_map/ppermute | solution.py:29
  34.6 2.8 %collective-permute-start.6 = (f32[4,128,128]{2,1,0:T(8,128)S(1)}, f32[4,128,128]{2,1,0:T(8,128)S(1)}, u32[]{:S(2)}, u32[]{:S(2)}) collective-permute-start(f32[4,128,128]{2,1,0:T(8,128)S(1)} %get-tuple-element.25), channel_id=1, source_target_pairs={{0,4},{2,6},{1,5},{3,7},{16,20},{18,22},{17,21},{19,23}} | collective-permute-start | bytes 786440 | tf_op jit(solution)/shard_map/ppermute | solution.py:29
  35.2 2.8 %collective-permute-start.11 = (f32[4,128,128]{2,1,0:T(8,128)S(1)}, f32[4,128,128]{2,1,0:T(8,128)S(1)}, u32[]{:S(2)}, u32[]{:S(2)}) collective-permute-start(f32[4,128,128]{2,1,0:T(8,128)S(1)} %get-tuple-element.26), channel_id=1, source_target_pairs={{0,4},{2,6},{1,5},{3,7},{16,20},{18,22},{17,21},{19,23}} | collective-permute-start | bytes 786440 | tf_op jit(solution)/shard_map/ppermute | solution.py:29
  36.0 2.9 %collective-permute-start.2 = (f32[4,128,128]{2,1,0:T(8,128)S(1)}, f32[4,128,128]{2,1,0:T(8,128)S(1)}, u32[]{:S(2)}, u32[]{:S(2)}) collective-permute-start(f32[4,128,128]{2,1,0:T(8,128)S(1)} %add.99), channel_id=1, source_target_pairs={{4,8},{6,10},{5,9},{7,11},{20,24},{22,26},{21,25},{23,27}} | collective-permute-start | bytes 786440 | tf_op jit(solution)/shard_map/ppermute | solution.py:29
  36.7 4.2 %collective-permute-start.16 = (f32[4,128,128]{2,1,0:T(8,128)S(1)}, f32[4,128,128]{2,1,0:T(8,128)S(1)}, u32[]{:S(2)}, u32[]{:S(2)}) collective-permute-start(f32[4,128,128]{2,1,0:T(8,128)S(1)} %get-tuple-element.27), channel_id=1, source_target_pairs={{0,4},{2,6},{1,5},{3,7},{16,20},{18,22},{17,21},{19,23}} | collective-permute-start | bytes 786440 | tf_op jit(solution)/shard_map/ppermute | solution.py:29
  37.4 4.2 %collective-permute-start.7 = (f32[4,128,128]{2,1,0:T(8,128)S(1)}, f32[4,128,128]{2,1,0:T(8,128)S(1)}, u32[]{:S(2)}, u32[]{:S(2)}) collective-permute-start(f32[4,128,128]{2,1,0:T(8,128)S(1)} %add.105), channel_id=1, source_target_pairs={{4,8},{6,10},{5,9},{7,11},{20,24},{22,26},{21,25},{23,27}} | collective-permute-start | bytes 786440 | tf_op jit(solution)/shard_map/ppermute | solution.py:29
  38.1 9.9 %copy-start.2 = (f32[2048]{0:T(1024)S(1)}, f32[2048]{0:T(1024)}, u32[]{:S(2)}) copy-start(f32[2048]{0:T(1024)} %param.7) | copy-start | bytes 24580
  38.2 5.5 %collective-permute-start.12 = (f32[4,128,128]{2,1,0:T(8,128)S(1)}, f32[4,128,128]{2,1,0:T(8,128)S(1)}, u32[]{:S(2)}, u32[]{:S(2)}) collective-permute-start(f32[4,128,128]{2,1,0:T(8,128)S(1)} %add.111), channel_id=1, source_target_pairs={{4,8},{6,10},{5,9},{7,11},{20,24},{22,26},{21,25},{23,27}} | collective-permute-start | bytes 786440 | tf_op jit(solution)/shard_map/ppermute | solution.py:29
  39.6 16.4 %collective-permute-start.3 = (f32[4,128,128]{2,1,0:T(8,128)}, f32[4,128,128]{2,1,0:T(8,128)}, u32[]{:S(2)}, u32[]{:S(2)}) collective-permute-start(f32[4,128,128]{2,1,0:T(8,128)} %get-tuple-element.9), channel_id=1, source_target_pairs={{8,12},{10,14},{9,13},{11,15},{24,28},{26,30},{25,29},{27,31}} | collective-permute-start | bytes 786440 | tf_op jit(solution)/shard_map/ppermute | solution.py:29
  40.9 4.9 %collective-permute-start.17 = (f32[4,128,128]{2,1,0:T(8,128)S(1)}, f32[4,128,128]{2,1,0:T(8,128)S(1)}, u32[]{:S(2)}, u32[]{:S(2)}) collective-permute-start(f32[4,128,128]{2,1,0:T(8,128)S(1)} %add.117), channel_id=1, source_target_pairs={{4,8},{6,10},{5,9},{7,11},{20,24},{22,26},{21,25},{23,27}} | collective-permute-start | bytes 786440 | tf_op jit(solution)/shard_map/ppermute | solution.py:29
  42.4 19.9 %collective-permute-start.8 = (f32[4,128,128]{2,1,0:T(8,128)}, f32[4,128,128]{2,1,0:T(8,128)}, u32[]{:S(2)}, u32[]{:S(2)}) collective-permute-start(f32[4,128,128]{2,1,0:T(8,128)} %get-tuple-element.11), channel_id=1, source_target_pairs={{8,12},{10,14},{9,13},{11,15},{24,28},{26,30},{25,29},{27,31}} | collective-permute-start | bytes 786440 | tf_op jit(solution)/shard_map/ppermute | solution.py:29
  44.6 23.6 %collective-permute-start.13 = (f32[4,128,128]{2,1,0:T(8,128)}, f32[4,128,128]{2,1,0:T(8,128)}, u32[]{:S(2)}, u32[]{:S(2)}) collective-permute-start(f32[4,128,128]{2,1,0:T(8,128)} %get-tuple-element.13), channel_id=1, source_target_pairs={{8,12},{10,14},{9,13},{11,15},{24,28},{26,30},{25,29},{27,31}} | collective-permute-start | bytes 786440 | tf_op jit(solution)/shard_map/ppermute | solution.py:29
  46.8 24.2 %collective-permute-start.18 = (f32[4,128,128]{2,1,0:T(8,128)}, f32[4,128,128]{2,1,0:T(8,128)}, u32[]{:S(2)}, u32[]{:S(2)}) collective-permute-start(f32[4,128,128]{2,1,0:T(8,128)} %get-tuple-element.15), channel_id=1, source_target_pairs={{8,12},{10,14},{9,13},{11,15},{24,28},{26,30},{25,29},{27,31}} | collective-permute-start | bytes 786440 | tf_op jit(solution)/shard_map/ppermute | solution.py:29
  48.1 1.2 %collective-permute-start.20 = (f32[2048]{0:T(1024)S(1)}, f32[2048]{0:T(1024)S(1)}, u32[]{:S(2)}, u32[]{:S(2)}) collective-permute-start(f32[2048]{0:T(1024)S(1)} %copy-done.2), channel_id=1, source_target_pairs={{0,1},{1,0},{2,3},{3,2},{4,5},{5,4},{6,7},{7,6},{8,9},{9,8},{10,11... | collective-permute-start | bytes 24584 | tf_op jit(solution)/shard_map/ppermute | solution.py:163
  73.4 11.8 %collective-permute-start.4 = (bf16[4,128,128]{2,1,0:T(8,128)(2,1)}, bf16[4,128,128]{2,1,0:T(8,128)(2,1)S(1)}, u32[]{:S(2)}, u32[]{:S(2)}) collective-permute-start(bf16[4,128,128]{2,1,0:T(8,128)(2,1)} %get-tuple-element.17), channel_id=1, source_target_pairs={{0,2},{4,6},{8,10},{12,14},{2,0},{6,4},{10,8},{14,12},{1,3},{5,7},... | collective-permute-start | bytes 393224 | tf_op jit(solution)/shard_map/ppermute | solution.py:32
  73.8 11.4 %collective-permute-start.9 = (bf16[4,128,128]{2,1,0:T(8,128)(2,1)}, bf16[4,128,128]{2,1,0:T(8,128)(2,1)S(1)}, u32[]{:S(2)}, u32[]{:S(2)}) collective-permute-start(bf16[4,128,128]{2,1,0:T(8,128)(2,1)} %get-tuple-element.18), channel_id=1, source_target_pairs={{0,2},{4,6},{8,10},{12,14},{2,0},{6,4},{10,8},{14,12},{1,3},{5,7},... | collective-permute-start | bytes 393224 | tf_op jit(solution)/shard_map/ppermute | solution.py:32
  75.5 9.7 %collective-permute-start.14 = (bf16[4,128,128]{2,1,0:T(8,128)(2,1)}, bf16[4,128,128]{2,1,0:T(8,128)(2,1)S(1)}, u32[]{:S(2)}, u32[]{:S(2)}) collective-permute-start(bf16[4,128,128]{2,1,0:T(8,128)(2,1)} %get-tuple-element.19), channel_id=1, source_target_pairs={{0,2},{4,6},{8,10},{12,14},{2,0},{6,4},{10,8},{14,12},{1,3},{5,7},... | collective-permute-start | bytes 393224 | tf_op jit(solution)/shard_map/ppermute | solution.py:32
  75.8 9.4 %collective-permute-start.19 = (bf16[4,128,128]{2,1,0:T(8,128)(2,1)S(1)}, bf16[4,128,128]{2,1,0:T(8,128)(2,1)S(1)}, u32[]{:S(2)}, u32[]{:S(2)}) collective-permute-start(bf16[4,128,128]{2,1,0:T(8,128)(2,1)S(1)} %get-tuple-element.20), channel_id=1, source_target_pairs={{0,2},{4,6},{8,10},{12,14},{2,0},{6,4},{10,8},{14,12},{1,3},{5,7},... | collective-permute-start | bytes 393224 | tf_op jit(solution)/shard_map/ppermute | solution.py:32

commit v20 on v19

--- a/solution.py
+++ b/solution.py
@@ -30,7 +30,7 @@
         keeps.append((carried + jnp.where(first, 0.0, got)).astype(jnp.bfloat16))
         send = (carried + jnp.where(first, mine, 0.0)).astype(jnp.bfloat16)
         backs.append(lax.ppermute(send, axis, swap))
-    return jnp.concatenate(keeps, axis=0), jnp.concatenate(backs, axis=0)
+    return jnp.concatenate(keeps, axis=0), backs
 
 
 def state_kernel(key_ref, val_ref, out_ref):
@@ -56,9 +56,9 @@
     )(keyset, valset)
 
 
-def attend_heads(query_ref, key_ref, val_ref, prefix_ref, store, sumsq):
-    row_count = query_ref.shape[0]
-    heads, head_size, _ = prefix_ref.shape
+def attend_heads(query_ref, key_ref, val_ref, prefix_of, heads, store, sumsq):
+    row_count, width = query_ref.shape
+    head_size = width // heads
     causal = (lax.broadcasted_iota(jnp.int32, (row_count, row_count), 0)
               >= lax.broadcasted_iota(jnp.int32, (row_count, row_count), 1))
     for head in range(heads):
@@ -68,7 +68,7 @@
                                  preferred_element_type=jnp.float32)
         weights = jnp.where(causal, scores, 0.0).astype(jnp.bfloat16)
         lhs = jnp.concatenate([weights, query], axis=1)
-        rhs = jnp.concatenate([val_ref[:, cols], prefix_ref[head]], axis=0)
+        rhs = jnp.concatenate([val_ref[:, cols], prefix_of(head)], axis=0)
         attended = jnp.dot(lhs, rhs, preferred_element_type=jnp.float32)
         store(cols, attended)
         sumsq = sumsq + attended * attended
@@ -83,13 +83,24 @@
     def store(cols, attended):
         att_ref[:, cols] = attended
 
-    sumsq_ref[...] = attend_heads(query_ref, key_ref, val_ref, keep_ref, store, sumsq_ref[...])
+    sumsq_ref[...] = attend_heads(query_ref, key_ref, val_ref, lambda head: keep_ref[head],
+                                  keep_ref.shape[0], store, sumsq_ref[...])
 
 
-def other_kernel(mine_ref, query_ref, key_ref, val_ref, back_ref, own_ref, own_sumsq_ref, gain_ref, out_ref,
-                 acc_ref, sumsq_ref):
+def other_kernel(mine_ref, query_ref, key_ref, val_ref, *refs):
+    back_refs = refs[:-6]
+    own_ref, own_sumsq_ref, gain_ref, out_ref, acc_ref, sumsq_ref = refs[-6:]
     step = pl.program_id(0)
     row_count, width = query_ref.shape
+    per_piece = back_refs[0].shape[0]
+    heads = width // (out_ref.shape[1] // H)
+    per_step = heads // per_piece
+
+    def prefix_of(head):
+        pick = back_refs[head // per_piece][head % per_piece]
+        for g in range(1, pl.num_programs(0)):
+            pick = jnp.where(step == g, back_refs[g * per_step + head // per_piece][head % per_piece], pick)
+        return pick
 
     @pl.when(step == 0)
     def _():
@@ -98,7 +109,7 @@
     def store(cols, attended):
         acc_ref[step, :, cols] = attended
 
-    sumsq = attend_heads(query_ref, key_ref, val_ref, back_ref, store, sumsq_ref[...])
+    sumsq = attend_heads(query_ref, key_ref, val_ref, prefix_of, heads, store, sumsq_ref[...])
     sumsq_ref[...] = sumsq
 
     @pl.when(step == pl.num_programs(0) - 1)
@@ -118,7 +129,7 @@
                     out_ref[:, cols] = (acc_ref[part] * scale * gain_ref[:, cols]).astype(out_ref.dtype)
 
 
-def attend_of(query, keyset, valset, keep, back, mine_at, full_gain, group):
+def attend_of(query, keyset, valset, keep, backs, mine_at, full_gain, group):
     row_count, feat_count = query.shape
     head_size = feat_count // H
     width = group * head_size
@@ -143,7 +154,8 @@
         grid_spec=pltpu.PrefetchScalarGridSpec(
             num_scalar_prefetch=1,
             grid=(steps,),
-            in_specs=[other_spec, other_spec, other_spec, half_spec,
+            in_specs=[other_spec, other_spec, other_spec]
+                     + [pl.BlockSpec(piece.shape, lambda g, at: (0, 0, 0)) for piece in backs] + [
                       pl.BlockSpec((row_count, feat_count // 2), lambda g, at: (0, 0)),
                       sumsq_spec,
                       pl.BlockSpec((1, feat_count), lambda g, at: (0, 0))],
@@ -151,7 +163,7 @@
             scratch_shapes=[pltpu.VMEM((steps, row_count, width), jnp.float32),
                             pltpu.VMEM((row_count, head_size), jnp.float32)]),
         out_shape=jax.ShapeDtypeStruct((row_count, feat_count), jnp.bfloat16),
-    )(mine, query, keyset, valset, back, own, own_sumsq, full_gain)
+    )(mine, query, keyset, valset, *backs, own, own_sumsq, full_gain)
 
 
 def shards(query_rows, key_rows, value_rows, gain):
@@ -168,8 +180,8 @@
     keyset = key_rows.reshape(seq_count * row_count, feat_count)
     valset = value_rows.reshape(seq_count * row_count, feat_count)
     state_terms = state_terms_of(keyset, valset, 16)
-    keep, back = pair_chain_prefix(state_terms, "ctx", 4)
-    normed = attend_of(query, keyset, valset, keep, back, lax.axis_index("ctx") % 2, full_gain, 8)
+    keep, backs = pair_chain_prefix(state_terms, "ctx", 4)
+    normed = attend_of(query, keyset, valset, keep, backs, lax.axis_index("ctx") % 2, full_gain, 8)
     return normed.reshape(seq_count, row_count, feat_count)
 
 

time: 95.1 us -> 95.1 us (level)
  no operation moved by 1% of the time
where the time goes in v20:
time: 95.1 us; the launch traced here: 94.8 us
  waiting for transfers between devices  45.8 us (48%)
  Pallas kernels  19.4 us (20%)
  starting transfers between devices  17.7 us (19%)
  other arithmetic  9.66 us (10%)
  local copies, waits for them, and re-layouts  1.88 us (2%)
    ppermute x4, waiting for transfers between devices, pair_chain_prefix(): got = lax.ppermute(other_all[piece * step:(piece + 1) * step], axis, swap)  22.9 us
    ppermute x12, waiting for transfers between devices, pair_chain_prefix(): carried = carried + lax.ppermute(carried + total, axis, links)  21.7 us
    ppermute x12, starting transfers between devices, pair_chain_prefix(): carried = carried + lax.ppermute(carried + total, axis, links)  10.5 us
    pallas_call x1, Pallas kernels, attend_of(): pl.pallas_call(other_kernel, grid_spec=pltpu.PrefetchScalarGridSpec(num_s...  8.71 us
    pallas_call x1, Pallas kernels, attend_of(): pl.pallas_call(own_kernel, grid_spec=pltpu.PrefetchScalarGridSpec(num_sca...  6.24 us
    pallas_call x1, Pallas kernels, state_terms_of(): pl.pallas_call(state_kernel, grid=(H // group,), in_specs=[pl.BlockSpec((...  4.45 us
    ppermute x4, starting transfers between devices, pair_chain_prefix(): backs.append(lax.ppermute(send, axis, swap))  4.05 us
    add x8, other arithmetic, pair_chain_prefix(): carried = carried + lax.ppermute(carried + total, axis, links)  3.43 us
  transfers between devices with their start and end apart: 21, of which 9 were waited for; matrix products, arithmetic and copies ran while one was open for 5% of the time, Pallas kernels for 7%

profile of v20, /device:TPU:30, one launch (start us, length us, event | category | flops | bytes accessed | tf_op | source)
XLA Modules:
  0.0 94.8 jit_solution(13667700897298649222)
XLA Ops:
  0.0 4.4 %shard_map.46 = f32[32,128,128]{2,1,0:T(8,128)} custom-call(bf16[384,4096]{1,0:T(8,128)(2,1)} %bitcast.6, bf16[384,4096]{1,0:T(8,128)(2,1)} %bitcast.9), custom_call_target="tpu_custom_call" | custom-call | tf_op jit(solution)/shard_map/pallas_call | solution.py:49
  4.5 1.1 %constant_dynamic-slice_fusion.3 = f32[4,128,128]{2,1,0:T(8,128)S(1)} fusion(f32[32,128,128]{2,1,0:T(8,128)} %shard_map.46, s32[]{:T(128)S(6)} %add.131), kind=kLoop, calls=%fused_computation.19 | loop fusion | bytes 524292 | tf_op jit(solution)/shard_map/slice | solution.py:24
  5.6 0.6 collective-permute-start.15
  6.1 7.5 %collective-permute-done.15 = f32[4,128,128]{2,1,0:T(8,128)S(1)} collective-permute-done((f32[4,128,128]{2,1,0:T(8,128)S(1)}, f32[4,128,128]{2,1,0:T(8,128)S(1)}, u32[]{:S(2)}, u32[]{:S(2)}) %collective-permute-start.15) | collective-permute-done | bytes 262176 | tf_op jit(solution)/shard_map/ppermute | solution.py:24
  13.7 2.2 %dynamic-slice_add_fusion = (f32[4,128,128]{2,1,0:T(8,128)S(1)}, f32[4,128,128]{2,1,0:T(8,128)}, f32[4,128,128]{2,1,0:T(8,128)}, f32[4,128,128]{2,1,0:T(8,128)}) fusion(f32[4,128,128]{2,1,0:T(8,128)S(1)} %collective-permute-done.15, f32[32,128,128]{2,1,0:T(8,128)} %shard_map.46, s32[]{:T(128)S(6)} %add.130, s32[]{:T(128)S(6)} %add.129, s32[]{:T(128)S(6)} %add.127, ...), kind=kLoop, calls=%fused_computation.9 | loop fusion | flops 65536 | bytes 2359312 | tf_op jit(solution)/shard_map/add | solution.py:25
  15.9 0.5 collective-permute-start.10
  16.4 1.5 %collective-permute-start.5 = (f32[4,128,128]{2,1,0:T(8,128)}, f32[4,128,128]{2,1,0:T(8,128)S(1)}, u32[]{:S(2)}, u32[]{:S(2)}) collective-permute-start(f32[4,128,128]{2,1,0:T(8,128)} %get-tuple-element.23), channel_id=1, source_target_pairs={{0,2},{4,6},{8,10},{12,14},{2,0},{6,4},{10,8},{14,12},{1,3},{5,7},... | collective-permute-start | bytes 786440 | tf_op jit(solution)/shard_map/ppermute | solution.py:24
  17.9 0.5 collective-permute-start
  18.4 0.7 collective-permute-start.16
  19.1 6.2 %collective-permute-done.10 = f32[4,128,128]{2,1,0:T(8,128)S(1)} collective-permute-done((f32[4,128,128]{2,1,0:T(8,128)}, f32[4,128,128]{2,1,0:T(8,128)S(1)}, u32[]{:S(2)}, u32[]{:S(2)}) %collective-permute-start.10) | collective-permute-done | bytes 262176 | tf_op jit(solution)/shard_map/ppermute | solution.py:24
  25.3 5.6 %collective-permute-done.5 = f32[4,128,128]{2,1,0:T(8,128)S(1)} collective-permute-done((f32[4,128,128]{2,1,0:T(8,128)}, f32[4,128,128]{2,1,0:T(8,128)S(1)}, u32[]{:S(2)}, u32[]{:S(2)}) %collective-permute-start.5) | collective-permute-done | bytes 262176 | tf_op jit(solution)/shard_map/ppermute | solution.py:24
  31.0 3.5 %collective-permute-done = f32[4,128,128]{2,1,0:T(8,128)S(1)} collective-permute-done((f32[4,128,128]{2,1,0:T(8,128)}, f32[4,128,128]{2,1,0:T(8,128)S(1)}, u32[]{:S(2)}, u32[]{:S(2)}) %collective-permute-start) | collective-permute-done | bytes 262176 | tf_op jit(solution)/shard_map/ppermute | solution.py:24
  34.5 0.1 dynamic-slice_add_fusion.1
  34.6 0.7 collective-permute-start.11
  35.3 0.7 collective-permute-start.6
  36.0 0.7 collective-permute-start.17
  36.7 0.7 collective-permute-start.1
  37.4 0.7 collective-permute-start.12
  38.2 0.0 copy-start.6
  38.2 0.7 collective-permute-start.7
  38.9 0.8 fusion
  39.6 1.3 %collective-permute-start.18 = (f32[4,128,128]{2,1,0:T(8,128)}, f32[4,128,128]{2,1,0:T(8,128)}, u32[]{:S(2)}, u32[]{:S(2)}) collective-permute-start(f32[4,128,128]{2,1,0:T(8,128)} %get-tuple-element.9), channel_id=1, source_target_pairs={{8,12},{10,14},{9,13},{11,15},{24,28},{26,30},{25,29},{27,31}} | collective-permute-start | bytes 786440 | tf_op jit(solution)/shard_map/ppermute | solution.py:29
  41.0 0.7 collective-permute-start.2
  41.7 0.8 fusion.1
  42.4 1.3 %collective-permute-start.13 = (f32[4,128,128]{2,1,0:T(8,128)}, f32[4,128,128]{2,1,0:T(8,128)}, u32[]{:S(2)}, u32[]{:S(2)}) collective-permute-start(f32[4,128,128]{2,1,0:T(8,128)} %get-tuple-element.11), channel_id=1, source_target_pairs={{8,12},{10,14},{9,13},{11,15},{24,28},{26,30},{25,29},{27,31}} | collective-permute-start | bytes 786440 | tf_op jit(solution)/shard_map/ppermute | solution.py:29
  43.7 0.9 fusion.2
  44.6 1.3 %collective-permute-start.8 = (f32[4,128,128]{2,1,0:T(8,128)}, f32[4,128,128]{2,1,0:T(8,128)}, u32[]{:S(2)}, u32[]{:S(2)}) collective-permute-start(f32[4,128,128]{2,1,0:T(8,128)} %get-tuple-element.13), channel_id=1, source_target_pairs={{8,12},{10,14},{9,13},{11,15},{24,28},{26,30},{25,29},{27,31}} | collective-permute-start | bytes 786440 | tf_op jit(solution)/shard_map/ppermute | solution.py:29
  45.9 0.9 fusion.3
  46.8 1.3 %collective-permute-start.3 = (f32[4,128,128]{2,1,0:T(8,128)}, f32[4,128,128]{2,1,0:T(8,128)}, u32[]{:S(2)}, u32[]{:S(2)}) collective-permute-start(f32[4,128,128]{2,1,0:T(8,128)} %get-tuple-element.15), channel_id=1, source_target_pairs={{8,12},{10,14},{9,13},{11,15},{24,28},{26,30},{25,29},{27,31}} | collective-permute-start | bytes 786440 | tf_op jit(solution)/shard_map/ppermute | solution.py:29
  48.1 0.1 collective-permute-start.20
  48.2 1.1 %collective-permute-done.20 = f32[2048]{0:T(1024)S(1)} collective-permute-done((f32[2048]{0:T(1024)S(1)}, f32[2048]{0:T(1024)S(1)}, u32[]{:S(2)}, u32[]{:S(2)}) %collective-permute-start.20) | collective-permute-done | bytes 8224 | tf_op jit(solution)/shard_map/ppermute | solution.py:175
  49.3 6.7 %collective-permute-done.18 = f32[4,128,128]{2,1,0:T(8,128)} collective-permute-done((f32[4,128,128]{2,1,0:T(8,128)}, f32[4,128,128]{2,1,0:T(8,128)}, u32[]{:S(2)}, u32[]{:S(2)}) %collective-permute-start.18) | collective-permute-done | bytes 262176 | tf_op jit(solution)/shard_map/ppermute | solution.py:29
  56.0 6.3 %collective-permute-done.13 = f32[4,128,128]{2,1,0:T(8,128)} collective-permute-done((f32[4,128,128]{2,1,0:T(8,128)}, f32[4,128,128]{2,1,0:T(8,128)}, u32[]{:S(2)}, u32[]{:S(2)}) %collective-permute-start.13) | collective-permute-done | bytes 262176 | tf_op jit(solution)/shard_map/ppermute | solution.py:29
  62.3 5.9 %collective-permute-done.8 = f32[4,128,128]{2,1,0:T(8,128)} collective-permute-done((f32[4,128,128]{2,1,0:T(8,128)}, f32[4,128,128]{2,1,0:T(8,128)}, u32[]{:S(2)}, u32[]{:S(2)}) %collective-permute-start.8) | collective-permute-done | bytes 262176 | tf_op jit(solution)/shard_map/ppermute | solution.py:29
  68.2 2.8 %collective-permute-done.3 = f32[4,128,128]{2,1,0:T(8,128)} collective-permute-done((f32[4,128,128]{2,1,0:T(8,128)}, f32[4,128,128]{2,1,0:T(8,128)}, u32[]{:S(2)}, u32[]{:S(2)}) %collective-permute-start.3) | collective-permute-done | bytes 262176 | tf_op jit(solution)/shard_map/ppermute | solution.py:29
  71.0 2.5 %add_convert_fusion.4 = (bf16[4,128,128]{2,1,0:T(8,128)(2,1)}, bf16[4,128,128]{2,1,0:T(8,128)(2,1)}, bf16[4,128,128]{2,1,0:T(8,128)(2,1)}, bf16[4,128,128]{2,1,0...) fusion(f32[32,128,128]{2,1,0:T(8,128)S(1)} %copy-done, ...), kind=kLoop, calls=%fused_computation.5 | loop fusion | flops 1835008 | bytes 5242897 | tf_op jit(solution)/shard_map/convert_element_type | solution.py:31
  73.5 0.3 collective-permute-start.19
  73.8 1.7 %collective-permute-start.4 = (bf16[4,128,128]{2,1,0:T(8,128)(2,1)}, bf16[4,128,128]{2,1,0:T(8,128)(2,1)S(1)}, u32[]{:S(2)}, u32[]{:S(2)}) collective-permute-start(bf16[4,128,128]{2,1,0:T(8,128)(2,1)} %get-tuple-element.18), channel_id=1, source_target_pairs={{0,2},{4,6},{8,10},{12,14},{2,0},{6,4},{10,8},{14,12},{1,3},{5,7},... | collective-permute-start | bytes 393224 | tf_op jit(solution)/shard_map/ppermute | solution.py:32
  75.5 0.3 collective-permute-start.9
  75.8 1.7 %collective-permute-start.14 = (bf16[4,128,128]{2,1,0:T(8,128)(2,1)S(1)}, bf16[4,128,128]{2,1,0:T(8,128)(2,1)S(1)}, u32[]{:S(2)}, u32[]{:S(2)}) collective-permute-start(bf16[4,128,128]{2,1,0:T(8,128)(2,1)S(1)} %get-tuple-element.20), channel_id=1, source_target_pairs={{0,2},{4,6},{8,10},{12,14},{2,0},{6,4},{10,8},{14,12},{1,3},{5,7},... | collective-permute-start | bytes 393224 | tf_op jit(solution)/shard_map/ppermute | solution.py:32
  77.5 0.6 pad_maximum_fusion.1
  78.1 0.9 pad_maximum_fusion.keep_ref
  79.0 6.2 %shard_map.47 = (f32[384,2048]{1,0:T(8,128)}, f32[384,128]{1,0:T(8,128)}) custom-call(s32[1]{0:T(128)} %bitcast.mine_ref, bf16[384,4096]{1,0:T(8,128)(2,1)} %bitcast.12, bf16[384,4096]{1,0:T(8,128)(2,1)} %bitcast.7, bf16[384,4096]{1,0:T(8,128)(2,1)} %bitcast.10, bf16[16,128,128]{2,1,0:T(8,128)(2,1)} %pad_maximum_fusion.keep_ref), custom_call_target="tpu_custom_call" | custom-call | tf_op jit(solution)/shard_map/pallas_call | solution.py:142
  85.3 0.6 copy-done.2
  85.9 0.1 copy-done.3
  85.9 0.0 copy-done.4
  86.0 0.1 copy-done.5
  86.0 8.7 %shard_map.48 = bf16[384,4096]{1,0:T(8,128)(2,1)} custom-call(s32[1]{0:T(128)} %bitcast.mine_ref, bf16[384,4096]{1,0:T(8,128)(2,1)} %bitcast.13, bf16[384,4096]{1,0:T(8,128)(2,1)} %bitcast.8, bf16[384,4096]{1,0:T(8,128)(2,1)} %bitcast.11, bf16[4,128,128]{2,1,0:T(8,128)(2,1)} %copy-done.3, bf16[4,128,128]{2,1,0:T(8,128)(2,1)} %copy-done.4, ...), custom_call_target="tpu_custom_call" | custom-call | tf_op jit(solution)/shard_map/pallas_call | solution.py:152
  (26 shorter events, 0.2 us)
Async XLA Ops:
  4.4 30.1 %copy-start = (f32[32,128,128]{2,1,0:T(8,128)S(1)}, f32[32,128,128]{2,1,0:T(8,128)}, u32[]{:S(2)}) copy-start(f32[32,128,128]{2,1,0:T(8,128)} %shard_map.46) | copy-start | bytes 6291460
  5.6 8.1 %collective-permute-start.15 = (f32[4,128,128]{2,1,0:T(8,128)S(1)}, f32[4,128,128]{2,1,0:T(8,128)S(1)}, u32[]{:S(2)}, u32[]{:S(2)}) collective-permute-start(f32[4,128,128]{2,1,0:T(8,128)S(1)} %constant_dynamic-slice_fusion.3), channel_id=1, source_target_pairs={{0,2},{4,6},{8,10},{12,14},{2,0},{6,4},{10,8},{14,12},{1,3},{5,7},... | collective-permute-start | bytes 786440 | tf_op jit(solution)/shard_map/ppermute | solution.py:24
  13.7 23.8 %copy-start.1 = (f32[4,128,128]{2,1,0:T(8,128)}, f32[4,128,128]{2,1,0:T(8,128)S(1)}, u32[]{:S(2)}) copy-start(f32[4,128,128]{2,1,0:T(8,128)S(1)} %collective-permute-done.15) | copy-start | bytes 786436
  15.9 9.5 %collective-permute-start.10 = (f32[4,128,128]{2,1,0:T(8,128)}, f32[4,128,128]{2,1,0:T(8,128)S(1)}, u32[]{:S(2)}, u32[]{:S(2)}) collective-permute-start(f32[4,128,128]{2,1,0:T(8,128)} %get-tuple-element.22), channel_id=1, source_target_pairs={{0,2},{4,6},{8,10},{12,14},{2,0},{6,4},{10,8},{14,12},{1,3},{5,7},... | collective-permute-start | bytes 786440 | tf_op jit(solution)/shard_map/ppermute | solution.py:24
  16.4 14.6 %collective-permute-start.5 = (f32[4,128,128]{2,1,0:T(8,128)}, f32[4,128,128]{2,1,0:T(8,128)S(1)}, u32[]{:S(2)}, u32[]{:S(2)}) collective-permute-start(f32[4,128,128]{2,1,0:T(8,128)} %get-tuple-element.23), channel_id=1, source_target_pairs={{0,2},{4,6},{8,10},{12,14},{2,0},{6,4},{10,8},{14,12},{1,3},{5,7},... | collective-permute-start | bytes 786440 | tf_op jit(solution)/shard_map/ppermute | solution.py:24
  17.9 16.6 %collective-permute-start = (f32[4,128,128]{2,1,0:T(8,128)}, f32[4,128,128]{2,1,0:T(8,128)S(1)}, u32[]{:S(2)}, u32[]{:S(2)}) collective-permute-start(f32[4,128,128]{2,1,0:T(8,128)} %get-tuple-element.24), channel_id=1, source_target_pairs={{0,2},{4,6},{8,10},{12,14},{2,0},{6,4},{10,8},{14,12},{1,3},{5,7},... | collective-permute-start | bytes 786440 | tf_op jit(solution)/shard_map/ppermute | solution.py:24
  18.4 17.5 %collective-permute-start.16 = (f32[4,128,128]{2,1,0:T(8,128)S(1)}, f32[4,128,128]{2,1,0:T(8,128)S(1)}, u32[]{:S(2)}, u32[]{:S(2)}) collective-permute-start(f32[4,128,128]{2,1,0:T(8,128)S(1)} %get-tuple-element.21), channel_id=1, source_target_pairs={{0,4},{2,6},{1,5},{3,7},{16,20},{18,22},{17,21},{19,23}} | collective-permute-start | bytes 786440 | tf_op jit(solution)/shard_map/ppermute | solution.py:29
  34.6 2.8 %collective-permute-start.11 = (f32[4,128,128]{2,1,0:T(8,128)S(1)}, f32[4,128,128]{2,1,0:T(8,128)S(1)}, u32[]{:S(2)}, u32[]{:S(2)}) collective-permute-start(f32[4,128,128]{2,1,0:T(8,128)S(1)} %get-tuple-element.25), channel_id=1, source_target_pairs={{0,4},{2,6},{1,5},{3,7},{16,20},{18,22},{17,21},{19,23}} | collective-permute-start | bytes 786440 | tf_op jit(solution)/shard_map/ppermute | solution.py:29
  35.3 2.9 %collective-permute-start.6 = (f32[4,128,128]{2,1,0:T(8,128)S(1)}, f32[4,128,128]{2,1,0:T(8,128)S(1)}, u32[]{:S(2)}, u32[]{:S(2)}) collective-permute-start(f32[4,128,128]{2,1,0:T(8,128)S(1)} %get-tuple-element.26), channel_id=1, source_target_pairs={{0,4},{2,6},{1,5},{3,7},{16,20},{18,22},{17,21},{19,23}} | collective-permute-start | bytes 786440 | tf_op jit(solution)/shard_map/ppermute | solution.py:29
  36.0 2.9 %collective-permute-start.17 = (f32[4,128,128]{2,1,0:T(8,128)S(1)}, f32[4,128,128]{2,1,0:T(8,128)S(1)}, u32[]{:S(2)}, u32[]{:S(2)}) collective-permute-start(f32[4,128,128]{2,1,0:T(8,128)S(1)} %add.117), channel_id=1, source_target_pairs={{4,8},{6,10},{5,9},{7,11},{20,24},{22,26},{21,25},{23,27}} | collective-permute-start | bytes 786440 | tf_op jit(solution)/shard_map/ppermute | solution.py:29
  36.7 4.2 %collective-permute-start.1 = (f32[4,128,128]{2,1,0:T(8,128)S(1)}, f32[4,128,128]{2,1,0:T(8,128)S(1)}, u32[]{:S(2)}, u32[]{:S(2)}) collective-permute-start(f32[4,128,128]{2,1,0:T(8,128)S(1)} %get-tuple-element.27), channel_id=1, source_target_pairs={{0,4},{2,6},{1,5},{3,7},{16,20},{18,22},{17,21},{19,23}} | collective-permute-start | bytes 786440 | tf_op jit(solution)/shard_map/ppermute | solution.py:29
  37.4 4.2 %collective-permute-start.12 = (f32[4,128,128]{2,1,0:T(8,128)S(1)}, f32[4,128,128]{2,1,0:T(8,128)S(1)}, u32[]{:S(2)}, u32[]{:S(2)}) collective-permute-start(f32[4,128,128]{2,1,0:T(8,128)S(1)} %add.111), channel_id=1, source_target_pairs={{4,8},{6,10},{5,9},{7,11},{20,24},{22,26},{21,25},{23,27}} | collective-permute-start | bytes 786440 | tf_op jit(solution)/shard_map/ppermute | solution.py:29
  38.2 9.9 %copy-start.6 = (f32[2048]{0:T(1024)S(1)}, f32[2048]{0:T(1024)}, u32[]{:S(2)}) copy-start(f32[2048]{0:T(1024)} %param.7) | copy-start | bytes 24580
  38.2 5.5 %collective-permute-start.7 = (f32[4,128,128]{2,1,0:T(8,128)S(1)}, f32[4,128,128]{2,1,0:T(8,128)S(1)}, u32[]{:S(2)}, u32[]{:S(2)}) collective-permute-start(f32[4,128,128]{2,1,0:T(8,128)S(1)} %add.105), channel_id=1, source_target_pairs={{4,8},{6,10},{5,9},{7,11},{20,24},{22,26},{21,25},{23,27}} | collective-permute-start | bytes 786440 | tf_op jit(solution)/shard_map/ppermute | solution.py:29
  39.6 16.4 %collective-permute-start.18 = (f32[4,128,128]{2,1,0:T(8,128)}, f32[4,128,128]{2,1,0:T(8,128)}, u32[]{:S(2)}, u32[]{:S(2)}) collective-permute-start(f32[4,128,128]{2,1,0:T(8,128)} %get-tuple-element.9), channel_id=1, source_target_pairs={{8,12},{10,14},{9,13},{11,15},{24,28},{26,30},{25,29},{27,31}} | collective-permute-start | bytes 786440 | tf_op jit(solution)/shard_map/ppermute | solution.py:29
  41.0 4.9 %collective-permute-start.2 = (f32[4,128,128]{2,1,0:T(8,128)S(1)}, f32[4,128,128]{2,1,0:T(8,128)S(1)}, u32[]{:S(2)}, u32[]{:S(2)}) collective-permute-start(f32[4,128,128]{2,1,0:T(8,128)S(1)} %add.99), channel_id=1, source_target_pairs={{4,8},{6,10},{5,9},{7,11},{20,24},{22,26},{21,25},{23,27}} | collective-permute-start | bytes 786440 | tf_op jit(solution)/shard_map/ppermute | solution.py:29
  42.4 19.9 %collective-permute-start.13 = (f32[4,128,128]{2,1,0:T(8,128)}, f32[4,128,128]{2,1,0:T(8,128)}, u32[]{:S(2)}, u32[]{:S(2)}) collective-permute-start(f32[4,128,128]{2,1,0:T(8,128)} %get-tuple-element.11), channel_id=1, source_target_pairs={{8,12},{10,14},{9,13},{11,15},{24,28},{26,30},{25,29},{27,31}} | collective-permute-start | bytes 786440 | tf_op jit(solution)/shard_map/ppermute | solution.py:29
  44.6 23.6 %collective-permute-start.8 = (f32[4,128,128]{2,1,0:T(8,128)}, f32[4,128,128]{2,1,0:T(8,128)}, u32[]{:S(2)}, u32[]{:S(2)}) collective-permute-start(f32[4,128,128]{2,1,0:T(8,128)} %get-tuple-element.13), channel_id=1, source_target_pairs={{8,12},{10,14},{9,13},{11,15},{24,28},{26,30},{25,29},{27,31}} | collective-permute-start | bytes 786440 | tf_op jit(solution)/shard_map/ppermute | solution.py:29
  46.8 24.2 %collective-permute-start.3 = (f32[4,128,128]{2,1,0:T(8,128)}, f32[4,128,128]{2,1,0:T(8,128)}, u32[]{:S(2)}, u32[]{:S(2)}) collective-permute-start(f32[4,128,128]{2,1,0:T(8,128)} %get-tuple-element.15), channel_id=1, source_target_pairs={{8,12},{10,14},{9,13},{11,15},{24,28},{26,30},{25,29},{27,31}} | collective-permute-start | bytes 786440 | tf_op jit(solution)/shard_map/ppermute | solution.py:29
  48.1 1.2 %collective-permute-start.20 = (f32[2048]{0:T(1024)S(1)}, f32[2048]{0:T(1024)S(1)}, u32[]{:S(2)}, u32[]{:S(2)}) collective-permute-start(f32[2048]{0:T(1024)S(1)} %copy-done.6), channel_id=1, source_target_pairs={{0,1},{1,0},{2,3},{3,2},{4,5},{5,4},{6,7},{7,6},{8,9},{9,8},{10,11... | collective-permute-start | bytes 24584 | tf_op jit(solution)/shard_map/ppermute | solution.py:175
  73.5 11.8 %collective-permute-start.19 = (bf16[4,128,128]{2,1,0:T(8,128)(2,1)}, bf16[4,128,128]{2,1,0:T(8,128)(2,1)S(1)}, u32[]{:S(2)}, u32[]{:S(2)}) collective-permute-start(bf16[4,128,128]{2,1,0:T(8,128)(2,1)} %get-tuple-element.17), channel_id=1, source_target_pairs={{0,2},{4,6},{8,10},{12,14},{2,0},{6,4},{10,8},{14,12},{1,3},{5,7},... | collective-permute-start | bytes 393224 | tf_op jit(solution)/shard_map/ppermute | solution.py:32
  73.8 11.4 %collective-permute-start.4 = (bf16[4,128,128]{2,1,0:T(8,128)(2,1)}, bf16[4,128,128]{2,1,0:T(8,128)(2,1)S(1)}, u32[]{:S(2)}, u32[]{:S(2)}) collective-permute-start(bf16[4,128,128]{2,1,0:T(8,128)(2,1)} %get-tuple-element.18), channel_id=1, source_target_pairs={{0,2},{4,6},{8,10},{12,14},{2,0},{6,4},{10,8},{14,12},{1,3},{5,7},... | collective-permute-start | bytes 393224 | tf_op jit(solution)/shard_map/ppermute | solution.py:32
  75.5 9.8 %collective-permute-start.9 = (bf16[4,128,128]{2,1,0:T(8,128)(2,1)}, bf16[4,128,128]{2,1,0:T(8,128)(2,1)S(1)}, u32[]{:S(2)}, u32[]{:S(2)}) collective-permute-start(bf16[4,128,128]{2,1,0:T(8,128)(2,1)} %get-tuple-element.19), channel_id=1, source_target_pairs={{0,2},{4,6},{8,10},{12,14},{2,0},{6,4},{10,8},{14,12},{1,3},{5,7},... | collective-permute-start | bytes 393224 | tf_op jit(solution)/shard_map/ppermute | solution.py:32
  75.8 9.5 %collective-permute-start.14 = (bf16[4,128,128]{2,1,0:T(8,128)(2,1)S(1)}, bf16[4,128,128]{2,1,0:T(8,128)(2,1)S(1)}, u32[]{:S(2)}, u32[]{:S(2)}) collective-permute-start(bf16[4,128,128]{2,1,0:T(8,128)(2,1)S(1)} %get-tuple-element.20), channel_id=1, source_target_pairs={{0,2},{4,6},{8,10},{12,14},{2,0},{6,4},{10,8},{14,12},{1,3},{5,7},... | collective-permute-start | bytes 393224 | tf_op jit(solution)/shard_map/ppermute | solution.py:32
  85.2 0.7 copy-start.2
  85.3 0.7 copy-start.3
  85.3 0.7 copy-start.4
  85.3 0.7 copy-start.5

commit v21 on v20

--- a/solution.py
+++ b/solution.py
@@ -88,9 +88,14 @@
 
 
 def other_kernel(mine_ref, query_ref, key_ref, val_ref, *refs):
-    back_refs = refs[:-6]
-    own_ref, own_sumsq_ref, gain_ref, out_ref, acc_ref, sumsq_ref = refs[-6:]
+    back_refs = refs[:-8]
+    own_hbm, own_sumsq_ref, gain_ref, out_ref, acc_ref, sumsq_ref, own_ref, own_sem = refs[-8:]
     step = pl.program_id(0)
+    own_copy = pltpu.make_async_copy(own_hbm, own_ref, own_sem)
+
+    @pl.when(step == 0)
+    def _():
+        own_copy.start()
     row_count, width = query_ref.shape
     per_piece = back_refs[0].shape[0]
     heads = width // (out_ref.shape[1] // H)
@@ -118,6 +123,7 @@
         feat_count = out_ref.shape[1]
         scale = lax.rsqrt(total / feat_count + 1e-05)
         half = feat_count // 2
+        own_copy.wait()
         for own_at in range(2):
             @pl.when(mine_ref[0] == own_at)
             def _():
@@ -156,12 +162,14 @@
             grid=(steps,),
             in_specs=[other_spec, other_spec, other_spec]
                      + [pl.BlockSpec(piece.shape, lambda g, at: (0, 0, 0)) for piece in backs] + [
-                      pl.BlockSpec((row_count, feat_count // 2), lambda g, at: (0, 0)),
+                      pl.BlockSpec(memory_space=pl.ANY),
                       sumsq_spec,
                       pl.BlockSpec((1, feat_count), lambda g, at: (0, 0))],
             out_specs=pl.BlockSpec((row_count, feat_count), lambda g, at: (0, 0)),
             scratch_shapes=[pltpu.VMEM((steps, row_count, width), jnp.float32),
-                            pltpu.VMEM((row_count, head_size), jnp.float32)]),
+                            pltpu.VMEM((row_count, head_size), jnp.float32),
+                            pltpu.VMEM((row_count, feat_count // 2), jnp.float32),
+                            pltpu.SemaphoreType.DMA]),
         out_shape=jax.ShapeDtypeStruct((row_count, feat_count), jnp.bfloat16),
     )(mine, query, keyset, valset, *backs, own, own_sumsq, full_gain)
 

time: 95.1 us -> 94.1 us (0.989)
  Pallas kernels: 19.4 us -> 18.4 us
    pallas_call x1, Pallas kernels: 8.71 us -> 7.73 us  [attend_of(): pl.pallas_call(other_kernel, grid_spec=pltpu.PrefetchScalarGridSpec(num_s...]
where the time goes in v21:
time: 94.1 us; the launch traced here: 93.8 us
  waiting for transfers between devices  45.8 us (49%)
  Pallas kernels  18.4 us (20%)
  starting transfers between devices  17.7 us (19%)
  other arithmetic  9.66 us (10%)
  local copies, waits for them, and re-layouts  1.88 us (2%)
    ppermute x4, waiting for transfers between devices, pair_chain_prefix(): got = lax.ppermute(other_all[piece * step:(piece + 1) * step], axis, swap)  22.9 us
    ppermute x12, waiting for transfers between devices, pair_chain_prefix(): carried = carried + lax.ppermute(carried + total, axis, links)  21.7 us
    ppermute x12, starting transfers between devices, pair_chain_prefix(): carried = carried + lax.ppermute(carried + total, axis, links)  10.5 us
    pallas_call x1, Pallas kernels, attend_of(): pl.pallas_call(other_kernel, grid_spec=pltpu.PrefetchScalarGridSpec(num_s...  7.73 us
    pallas_call x1, Pallas kernels, attend_of(): pl.pallas_call(own_kernel, grid_spec=pltpu.PrefetchScalarGridSpec(num_sca...  6.24 us
    pallas_call x1, Pallas kernels, state_terms_of(): pl.pallas_call(state_kernel, grid=(H // group,), in_specs=[pl.BlockSpec((...  4.45 us
    ppermute x4, starting transfers between devices, pair_chain_prefix(): backs.append(lax.ppermute(send, axis, swap))  4.05 us
    add x8, other arithmetic, pair_chain_prefix(): carried = carried + lax.ppermute(carried + total, axis, links)  3.43 us
  transfers between devices with their start and end apart: 21, of which 9 were waited for; matrix products, arithmetic and copies ran while one was open for 5% of the time, Pallas kernels for 7%

profile of v21, /device:TPU:30, one launch (start us, length us, event | category | flops | bytes accessed | tf_op | source)
XLA Modules:
  0.0 93.8 jit_solution(13482146460463988482)
XLA Ops:
  0.0 4.4 %shard_map.46 = f32[32,128,128]{2,1,0:T(8,128)} custom-call(bf16[384,4096]{1,0:T(8,128)(2,1)} %bitcast.6, bf16[384,4096]{1,0:T(8,128)(2,1)} %bitcast.9), custom_call_target="tpu_custom_call" | custom-call | tf_op jit(solution)/shard_map/pallas_call | solution.py:49
  4.5 1.1 %constant_dynamic-slice_fusion.3 = f32[4,128,128]{2,1,0:T(8,128)S(1)} fusion(f32[32,128,128]{2,1,0:T(8,128)} %shard_map.46, s32[]{:T(128)S(6)} %add.131), kind=kLoop, calls=%fused_computation.19 | loop fusion | bytes 524292 | tf_op jit(solution)/shard_map/slice | solution.py:24
  5.6 0.6 collective-permute-start.15
  6.1 7.5 %collective-permute-done.15 = f32[4,128,128]{2,1,0:T(8,128)S(1)} collective-permute-done((f32[4,128,128]{2,1,0:T(8,128)S(1)}, f32[4,128,128]{2,1,0:T(8,128)S(1)}, u32[]{:S(2)}, u32[]{:S(2)}) %collective-permute-start.15) | collective-permute-done | bytes 262176 | tf_op jit(solution)/shard_map/ppermute | solution.py:24
  13.7 2.2 %dynamic-slice_add_fusion = (f32[4,128,128]{2,1,0:T(8,128)S(1)}, f32[4,128,128]{2,1,0:T(8,128)}, f32[4,128,128]{2,1,0:T(8,128)}, f32[4,128,128]{2,1,0:T(8,128)}) fusion(f32[4,128,128]{2,1,0:T(8,128)S(1)} %collective-permute-done.15, f32[32,128,128]{2,1,0:T(8,128)} %shard_map.46, s32[]{:T(128)S(6)} %add.130, s32[]{:T(128)S(6)} %add.129, s32[]{:T(128)S(6)} %add.127, ...), kind=kLoop, calls=%fused_computation.9 | loop fusion | flops 65536 | bytes 2359312 | tf_op jit(solution)/shard_map/add | solution.py:25
  15.9 0.5 collective-permute-start.10
  16.4 1.5 %collective-permute-start.5 = (f32[4,128,128]{2,1,0:T(8,128)}, f32[4,128,128]{2,1,0:T(8,128)S(1)}, u32[]{:S(2)}, u32[]{:S(2)}) collective-permute-start(f32[4,128,128]{2,1,0:T(8,128)} %get-tuple-element.23), channel_id=1, source_target_pairs={{0,2},{4,6},{8,10},{12,14},{2,0},{6,4},{10,8},{14,12},{1,3},{5,7},... | collective-permute-start | bytes 786440 | tf_op jit(solution)/shard_map/ppermute | solution.py:24
  17.9 0.5 collective-permute-start
  18.4 0.7 collective-permute-start.16
  19.1 6.2 %collective-permute-done.10 = f32[4,128,128]{2,1,0:T(8,128)S(1)} collective-permute-done((f32[4,128,128]{2,1,0:T(8,128)}, f32[4,128,128]{2,1,0:T(8,128)S(1)}, u32[]{:S(2)}, u32[]{:S(2)}) %collective-permute-start.10) | collective-permute-done | bytes 262176 | tf_op jit(solution)/shard_map/ppermute | solution.py:24
  25.3 5.6 %collective-permute-done.5 = f32[4,128,128]{2,1,0:T(8,128)S(1)} collective-permute-done((f32[4,128,128]{2,1,0:T(8,128)}, f32[4,128,128]{2,1,0:T(8,128)S(1)}, u32[]{:S(2)}, u32[]{:S(2)}) %collective-permute-start.5) | collective-permute-done | bytes 262176 | tf_op jit(solution)/shard_map/ppermute | solution.py:24
  31.0 3.5 %collective-permute-done = f32[4,128,128]{2,1,0:T(8,128)S(1)} collective-permute-done((f32[4,128,128]{2,1,0:T(8,128)}, f32[4,128,128]{2,1,0:T(8,128)S(1)}, u32[]{:S(2)}, u32[]{:S(2)}) %collective-permute-start) | collective-permute-done | bytes 262176 | tf_op jit(solution)/shard_map/ppermute | solution.py:24
  34.5 0.1 dynamic-slice_add_fusion.1
  34.6 0.7 collective-permute-start.11
  35.3 0.7 collective-permute-start.6
  36.0 0.7 collective-permute-start.17
  36.7 0.7 collective-permute-start.1
  37.4 0.7 collective-permute-start.12
  38.2 0.0 copy-start.6
  38.2 0.7 collective-permute-start.7
  38.9 0.8 fusion
  39.6 1.3 %collective-permute-start.18 = (f32[4,128,128]{2,1,0:T(8,128)}, f32[4,128,128]{2,1,0:T(8,128)}, u32[]{:S(2)}, u32[]{:S(2)}) collective-permute-start(f32[4,128,128]{2,1,0:T(8,128)} %get-tuple-element.9), channel_id=1, source_target_pairs={{8,12},{10,14},{9,13},{11,15},{24,28},{26,30},{25,29},{27,31}} | collective-permute-start | bytes 786440 | tf_op jit(solution)/shard_map/ppermute | solution.py:29
  41.0 0.7 collective-permute-start.2
  41.7 0.8 fusion.1
  42.4 1.3 %collective-permute-start.13 = (f32[4,128,128]{2,1,0:T(8,128)}, f32[4,128,128]{2,1,0:T(8,128)}, u32[]{:S(2)}, u32[]{:S(2)}) collective-permute-start(f32[4,128,128]{2,1,0:T(8,128)} %get-tuple-element.11), channel_id=1, source_target_pairs={{8,12},{10,14},{9,13},{11,15},{24,28},{26,30},{25,29},{27,31}} | collective-permute-start | bytes 786440 | tf_op jit(solution)/shard_map/ppermute | solution.py:29
  43.7 0.9 fusion.2
  44.6 1.3 %collective-permute-start.8 = (f32[4,128,128]{2,1,0:T(8,128)}, f32[4,128,128]{2,1,0:T(8,128)}, u32[]{:S(2)}, u32[]{:S(2)}) collective-permute-start(f32[4,128,128]{2,1,0:T(8,128)} %get-tuple-element.13), channel_id=1, source_target_pairs={{8,12},{10,14},{9,13},{11,15},{24,28},{26,30},{25,29},{27,31}} | collective-permute-start | bytes 786440 | tf_op jit(solution)/shard_map/ppermute | solution.py:29
  45.9 0.9 fusion.3
  46.8 1.3 %collective-permute-start.3 = (f32[4,128,128]{2,1,0:T(8,128)}, f32[4,128,128]{2,1,0:T(8,128)}, u32[]{:S(2)}, u32[]{:S(2)}) collective-permute-start(f32[4,128,128]{2,1,0:T(8,128)} %get-tuple-element.15), channel_id=1, source_target_pairs={{8,12},{10,14},{9,13},{11,15},{24,28},{26,30},{25,29},{27,31}} | collective-permute-start | bytes 786440 | tf_op jit(solution)/shard_map/ppermute | solution.py:29
  48.1 0.1 collective-permute-start.20
  48.2 1.1 %collective-permute-done.20 = f32[2048]{0:T(1024)S(1)} collective-permute-done((f32[2048]{0:T(1024)S(1)}, f32[2048]{0:T(1024)S(1)}, u32[]{:S(2)}, u32[]{:S(2)}) %collective-permute-start.20) | collective-permute-done | bytes 8224 | tf_op jit(solution)/shard_map/ppermute | solution.py:183
  49.3 6.7 %collective-permute-done.18 = f32[4,128,128]{2,1,0:T(8,128)} collective-permute-done((f32[4,128,128]{2,1,0:T(8,128)}, f32[4,128,128]{2,1,0:T(8,128)}, u32[]{:S(2)}, u32[]{:S(2)}) %collective-permute-start.18) | collective-permute-done | bytes 262176 | tf_op jit(solution)/shard_map/ppermute | solution.py:29
  56.0 6.3 %collective-permute-done.13 = f32[4,128,128]{2,1,0:T(8,128)} collective-permute-done((f32[4,128,128]{2,1,0:T(8,128)}, f32[4,128,128]{2,1,0:T(8,128)}, u32[]{:S(2)}, u32[]{:S(2)}) %collective-permute-start.13) | collective-permute-done | bytes 262176 | tf_op jit(solution)/shard_map/ppermute | solution.py:29
  62.3 5.9 %collective-permute-done.8 = f32[4,128,128]{2,1,0:T(8,128)} collective-permute-done((f32[4,128,128]{2,1,0:T(8,128)}, f32[4,128,128]{2,1,0:T(8,128)}, u32[]{:S(2)}, u32[]{:S(2)}) %collective-permute-start.8) | collective-permute-done | bytes 262176 | tf_op jit(solution)/shard_map/ppermute | solution.py:29
  68.2 2.8 %collective-permute-done.3 = f32[4,128,128]{2,1,0:T(8,128)} collective-permute-done((f32[4,128,128]{2,1,0:T(8,128)}, f32[4,128,128]{2,1,0:T(8,128)}, u32[]{:S(2)}, u32[]{:S(2)}) %collective-permute-start.3) | collective-permute-done | bytes 262176 | tf_op jit(solution)/shard_map/ppermute | solution.py:29
  71.0 2.5 %add_convert_fusion.4 = (bf16[4,128,128]{2,1,0:T(8,128)(2,1)}, bf16[4,128,128]{2,1,0:T(8,128)(2,1)}, bf16[4,128,128]{2,1,0:T(8,128)(2,1)}, bf16[4,128,128]{2,1,0...) fusion(f32[32,128,128]{2,1,0:T(8,128)S(1)} %copy-done, ...), kind=kLoop, calls=%fused_computation.5 | loop fusion | flops 1835008 | bytes 5242897 | tf_op jit(solution)/shard_map/convert_element_type | solution.py:31
  73.5 0.3 collective-permute-start.19
  73.8 1.7 %collective-permute-start.4 = (bf16[4,128,128]{2,1,0:T(8,128)(2,1)}, bf16[4,128,128]{2,1,0:T(8,128)(2,1)S(1)}, u32[]{:S(2)}, u32[]{:S(2)}) collective-permute-start(bf16[4,128,128]{2,1,0:T(8,128)(2,1)} %get-tuple-element.18), channel_id=1, source_target_pairs={{0,2},{4,6},{8,10},{12,14},{2,0},{6,4},{10,8},{14,12},{1,3},{5,7},... | collective-permute-start | bytes 393224 | tf_op jit(solution)/shard_map/ppermute | solution.py:32
  75.5 0.3 collective-permute-start.9
  75.8 1.7 %collective-permute-start.14 = (bf16[4,128,128]{2,1,0:T(8,128)(2,1)S(1)}, bf16[4,128,128]{2,1,0:T(8,128)(2,1)S(1)}, u32[]{:S(2)}, u32[]{:S(2)}) collective-permute-start(bf16[4,128,128]{2,1,0:T(8,128)(2,1)S(1)} %get-tuple-element.20), channel_id=1, source_target_pairs={{0,2},{4,6},{8,10},{12,14},{2,0},{6,4},{10,8},{14,12},{1,3},{5,7},... | collective-permute-start | bytes 393224 | tf_op jit(solution)/shard_map/ppermute | solution.py:32
  77.5 0.6 pad_maximum_fusion.1
  78.1 0.9 pad_maximum_fusion.keep_ref
  79.0 6.2 %shard_map.47 = (f32[384,2048]{1,0:T(8,128)}, f32[384,128]{1,0:T(8,128)}) custom-call(s32[1]{0:T(128)} %bitcast.mine_ref, bf16[384,4096]{1,0:T(8,128)(2,1)} %bitcast.12, bf16[384,4096]{1,0:T(8,128)(2,1)} %bitcast.7, bf16[384,4096]{1,0:T(8,128)(2,1)} %bitcast.10, bf16[16,128,128]{2,1,0:T(8,128)(2,1)} %pad_maximum_fusion.keep_ref), custom_call_target="tpu_custom_call" | custom-call | tf_op jit(solution)/shard_map/pallas_call | solution.py:148
  85.3 0.6 copy-done.2
  85.9 0.1 copy-done.3
  85.9 0.0 copy-done.4
  86.0 0.1 copy-done.5
  86.0 7.7 %shard_map.48 = bf16[384,4096]{1,0:T(8,128)(2,1)} custom-call(s32[1]{0:T(128)} %bitcast.mine_ref, bf16[384,4096]{1,0:T(8,128)(2,1)} %bitcast.13, bf16[384,4096]{1,0:T(8,128)(2,1)} %bitcast.8, bf16[384,4096]{1,0:T(8,128)(2,1)} %bitcast.11, bf16[4,128,128]{2,1,0:T(8,128)(2,1)} %copy-done.3, bf16[4,128,128]{2,1,0:T(8,128)(2,1)} %copy-done.4, ...), custom_call_target="tpu_custom_call" | custom-call | tf_op jit(solution)/shard_map/pallas_call | solution.py:158
  (26 shorter events, 0.2 us)
Async XLA Ops:
  4.4 30.1 %copy-start = (f32[32,128,128]{2,1,0:T(8,128)S(1)}, f32[32,128,128]{2,1,0:T(8,128)}, u32[]{:S(2)}) copy-start(f32[32,128,128]{2,1,0:T(8,128)} %shard_map.46) | copy-start | bytes 6291460
  5.6 8.1 %collective-permute-start.15 = (f32[4,128,128]{2,1,0:T(8,128)S(1)}, f32[4,128,128]{2,1,0:T(8,128)S(1)}, u32[]{:S(2)}, u32[]{:S(2)}) collective-permute-start(f32[4,128,128]{2,1,0:T(8,128)S(1)} %constant_dynamic-slice_fusion.3), channel_id=1, source_target_pairs={{0,2},{4,6},{8,10},{12,14},{2,0},{6,4},{10,8},{14,12},{1,3},{5,7},... | collective-permute-start | bytes 786440 | tf_op jit(solution)/shard_map/ppermute | solution.py:24
  13.7 23.8 %copy-start.1 = (f32[4,128,128]{2,1,0:T(8,128)}, f32[4,128,128]{2,1,0:T(8,128)S(1)}, u32[]{:S(2)}) copy-start(f32[4,128,128]{2,1,0:T(8,128)S(1)} %collective-permute-done.15) | copy-start | bytes 786436
  15.9 9.5 %collective-permute-start.10 = (f32[4,128,128]{2,1,0:T(8,128)}, f32[4,128,128]{2,1,0:T(8,128)S(1)}, u32[]{:S(2)}, u32[]{:S(2)}) collective-permute-start(f32[4,128,128]{2,1,0:T(8,128)} %get-tuple-element.22), channel_id=1, source_target_pairs={{0,2},{4,6},{8,10},{12,14},{2,0},{6,4},{10,8},{14,12},{1,3},{5,7},... | collective-permute-start | bytes 786440 | tf_op jit(solution)/shard_map/ppermute | solution.py:24
  16.4 14.6 %collective-permute-start.5 = (f32[4,128,128]{2,1,0:T(8,128)}, f32[4,128,128]{2,1,0:T(8,128)S(1)}, u32[]{:S(2)}, u32[]{:S(2)}) collective-permute-start(f32[4,128,128]{2,1,0:T(8,128)} %get-tuple-element.23), channel_id=1, source_target_pairs={{0,2},{4,6},{8,10},{12,14},{2,0},{6,4},{10,8},{14,12},{1,3},{5,7},... | collective-permute-start | bytes 786440 | tf_op jit(solution)/shard_map/ppermute | solution.py:24
  17.9 16.6 %collective-permute-start = (f32[4,128,128]{2,1,0:T(8,128)}, f32[4,128,128]{2,1,0:T(8,128)S(1)}, u32[]{:S(2)}, u32[]{:S(2)}) collective-permute-start(f32[4,128,128]{2,1,0:T(8,128)} %get-tuple-element.24), channel_id=1, source_target_pairs={{0,2},{4,6},{8,10},{12,14},{2,0},{6,4},{10,8},{14,12},{1,3},{5,7},... | collective-permute-start | bytes 786440 | tf_op jit(solution)/shard_map/ppermute | solution.py:24
  18.4 17.5 %collective-permute-start.16 = (f32[4,128,128]{2,1,0:T(8,128)S(1)}, f32[4,128,128]{2,1,0:T(8,128)S(1)}, u32[]{:S(2)}, u32[]{:S(2)}) collective-permute-start(f32[4,128,128]{2,1,0:T(8,128)S(1)} %get-tuple-element.21), channel_id=1, source_target_pairs={{0,4},{2,6},{1,5},{3,7},{16,20},{18,22},{17,21},{19,23}} | collective-permute-start | bytes 786440 | tf_op jit(solution)/shard_map/ppermute | solution.py:29
  34.6 2.8 %collective-permute-start.11 = (f32[4,128,128]{2,1,0:T(8,128)S(1)}, f32[4,128,128]{2,1,0:T(8,128)S(1)}, u32[]{:S(2)}, u32[]{:S(2)}) collective-permute-start(f32[4,128,128]{2,1,0:T(8,128)S(1)} %get-tuple-element.25), channel_id=1, source_target_pairs={{0,4},{2,6},{1,5},{3,7},{16,20},{18,22},{17,21},{19,23}} | collective-permute-start | bytes 786440 | tf_op jit(solution)/shard_map/ppermute | solution.py:29
  35.3 2.9 %collective-permute-start.6 = (f32[4,128,128]{2,1,0:T(8,128)S(1)}, f32[4,128,128]{2,1,0:T(8,128)S(1)}, u32[]{:S(2)}, u32[]{:S(2)}) collective-permute-start(f32[4,128,128]{2,1,0:T(8,128)S(1)} %get-tuple-element.26), channel_id=1, source_target_pairs={{0,4},{2,6},{1,5},{3,7},{16,20},{18,22},{17,21},{19,23}} | collective-permute-start | bytes 786440 | tf_op jit(solution)/shard_map/ppermute | solution.py:29
  36.0 2.9 %collective-permute-start.17 = (f32[4,128,128]{2,1,0:T(8,128)S(1)}, f32[4,128,128]{2,1,0:T(8,128)S(1)}, u32[]{:S(2)}, u32[]{:S(2)}) collective-permute-start(f32[4,128,128]{2,1,0:T(8,128)S(1)} %add.117), channel_id=1, source_target_pairs={{4,8},{6,10},{5,9},{7,11},{20,24},{22,26},{21,25},{23,27}} | collective-permute-start | bytes 786440 | tf_op jit(solution)/shard_map/ppermute | solution.py:29
  36.7 4.2 %collective-permute-start.1 = (f32[4,128,128]{2,1,0:T(8,128)S(1)}, f32[4,128,128]{2,1,0:T(8,128)S(1)}, u32[]{:S(2)}, u32[]{:S(2)}) collective-permute-start(f32[4,128,128]{2,1,0:T(8,128)S(1)} %get-tuple-element.27), channel_id=1, source_target_pairs={{0,4},{2,6},{1,5},{3,7},{16,20},{18,22},{17,21},{19,23}} | collective-permute-start | bytes 786440 | tf_op jit(solution)/shard_map/ppermute | solution.py:29
  37.4 4.2 %collective-permute-start.12 = (f32[4,128,128]{2,1,0:T(8,128)S(1)}, f32[4,128,128]{2,1,0:T(8,128)S(1)}, u32[]{:S(2)}, u32[]{:S(2)}) collective-permute-start(f32[4,128,128]{2,1,0:T(8,128)S(1)} %add.111), channel_id=1, source_target_pairs={{4,8},{6,10},{5,9},{7,11},{20,24},{22,26},{21,25},{23,27}} | collective-permute-start | bytes 786440 | tf_op jit(solution)/shard_map/ppermute | solution.py:29
  38.2 9.9 %copy-start.6 = (f32[2048]{0:T(1024)S(1)}, f32[2048]{0:T(1024)}, u32[]{:S(2)}) copy-start(f32[2048]{0:T(1024)} %param.7) | copy-start | bytes 24580
  38.2 5.5 %collective-permute-start.7 = (f32[4,128,128]{2,1,0:T(8,128)S(1)}, f32[4,128,128]{2,1,0:T(8,128)S(1)}, u32[]{:S(2)}, u32[]{:S(2)}) collective-permute-start(f32[4,128,128]{2,1,0:T(8,128)S(1)} %add.105), channel_id=1, source_target_pairs={{4,8},{6,10},{5,9},{7,11},{20,24},{22,26},{21,25},{23,27}} | collective-permute-start | bytes 786440 | tf_op jit(solution)/shard_map/ppermute | solution.py:29
  39.6 16.4 %collective-permute-start.18 = (f32[4,128,128]{2,1,0:T(8,128)}, f32[4,128,128]{2,1,0:T(8,128)}, u32[]{:S(2)}, u32[]{:S(2)}) collective-permute-start(f32[4,128,128]{2,1,0:T(8,128)} %get-tuple-element.9), channel_id=1, source_target_pairs={{8,12},{10,14},{9,13},{11,15},{24,28},{26,30},{25,29},{27,31}} | collective-permute-start | bytes 786440 | tf_op jit(solution)/shard_map/ppermute | solution.py:29
  41.0 4.9 %collective-permute-start.2 = (f32[4,128,128]{2,1,0:T(8,128)S(1)}, f32[4,128,128]{2,1,0:T(8,128)S(1)}, u32[]{:S(2)}, u32[]{:S(2)}) collective-permute-start(f32[4,128,128]{2,1,0:T(8,128)S(1)} %add.99), channel_id=1, source_target_pairs={{4,8},{6,10},{5,9},{7,11},{20,24},{22,26},{21,25},{23,27}} | collective-permute-start | bytes 786440 | tf_op jit(solution)/shard_map/ppermute | solution.py:29
  42.4 19.9 %collective-permute-start.13 = (f32[4,128,128]{2,1,0:T(8,128)}, f32[4,128,128]{2,1,0:T(8,128)}, u32[]{:S(2)}, u32[]{:S(2)}) collective-permute-start(f32[4,128,128]{2,1,0:T(8,128)} %get-tuple-element.11), channel_id=1, source_target_pairs={{8,12},{10,14},{9,13},{11,15},{24,28},{26,30},{25,29},{27,31}} | collective-permute-start | bytes 786440 | tf_op jit(solution)/shard_map/ppermute | solution.py:29
  44.6 23.6 %collective-permute-start.8 = (f32[4,128,128]{2,1,0:T(8,128)}, f32[4,128,128]{2,1,0:T(8,128)}, u32[]{:S(2)}, u32[]{:S(2)}) collective-permute-start(f32[4,128,128]{2,1,0:T(8,128)} %get-tuple-element.13), channel_id=1, source_target_pairs={{8,12},{10,14},{9,13},{11,15},{24,28},{26,30},{25,29},{27,31}} | collective-permute-start | bytes 786440 | tf_op jit(solution)/shard_map/ppermute | solution.py:29
  46.8 24.2 %collective-permute-start.3 = (f32[4,128,128]{2,1,0:T(8,128)}, f32[4,128,128]{2,1,0:T(8,128)}, u32[]{:S(2)}, u32[]{:S(2)}) collective-permute-start(f32[4,128,128]{2,1,0:T(8,128)} %get-tuple-element.15), channel_id=1, source_target_pairs={{8,12},{10,14},{9,13},{11,15},{24,28},{26,30},{25,29},{27,31}} | collective-permute-start | bytes 786440 | tf_op jit(solution)/shard_map/ppermute | solution.py:29
  48.1 1.2 %collective-permute-start.20 = (f32[2048]{0:T(1024)S(1)}, f32[2048]{0:T(1024)S(1)}, u32[]{:S(2)}, u32[]{:S(2)}) collective-permute-start(f32[2048]{0:T(1024)S(1)} %copy-done.6), channel_id=1, source_target_pairs={{0,1},{1,0},{2,3},{3,2},{4,5},{5,4},{6,7},{7,6},{8,9},{9,8},{10,11... | collective-permute-start | bytes 24584 | tf_op jit(solution)/shard_map/ppermute | solution.py:183
  73.5 11.8 %collective-permute-start.19 = (bf16[4,128,128]{2,1,0:T(8,128)(2,1)}, bf16[4,128,128]{2,1,0:T(8,128)(2,1)S(1)}, u32[]{:S(2)}, u32[]{:S(2)}) collective-permute-start(bf16[4,128,128]{2,1,0:T(8,128)(2,1)} %get-tuple-element.17), channel_id=1, source_target_pairs={{0,2},{4,6},{8,10},{12,14},{2,0},{6,4},{10,8},{14,12},{1,3},{5,7},... | collective-permute-start | bytes 393224 | tf_op jit(solution)/shard_map/ppermute | solution.py:32
  73.8 11.4 %collective-permute-start.4 = (bf16[4,128,128]{2,1,0:T(8,128)(2,1)}, bf16[4,128,128]{2,1,0:T(8,128)(2,1)S(1)}, u32[]{:S(2)}, u32[]{:S(2)}) collective-permute-start(bf16[4,128,128]{2,1,0:T(8,128)(2,1)} %get-tuple-element.18), channel_id=1, source_target_pairs={{0,2},{4,6},{8,10},{12,14},{2,0},{6,4},{10,8},{14,12},{1,3},{5,7},... | collective-permute-start | bytes 393224 | tf_op jit(solution)/shard_map/ppermute | solution.py:32
  75.5 9.8 %collective-permute-start.9 = (bf16[4,128,128]{2,1,0:T(8,128)(2,1)}, bf16[4,128,128]{2,1,0:T(8,128)(2,1)S(1)}, u32[]{:S(2)}, u32[]{:S(2)}) collective-permute-start(bf16[4,128,128]{2,1,0:T(8,128)(2,1)} %get-tuple-element.19), channel_id=1, source_target_pairs={{0,2},{4,6},{8,10},{12,14},{2,0},{6,4},{10,8},{14,12},{1,3},{5,7},... | collective-permute-start | bytes 393224 | tf_op jit(solution)/shard_map/ppermute | solution.py:32
  75.8 9.5 %collective-permute-start.14 = (bf16[4,128,128]{2,1,0:T(8,128)(2,1)S(1)}, bf16[4,128,128]{2,1,0:T(8,128)(2,1)S(1)}, u32[]{:S(2)}, u32[]{:S(2)}) collective-permute-start(bf16[4,128,128]{2,1,0:T(8,128)(2,1)S(1)} %get-tuple-element.20), channel_id=1, source_target_pairs={{0,2},{4,6},{8,10},{12,14},{2,0},{6,4},{10,8},{14,12},{1,3},{5,7},... | collective-permute-start | bytes 393224 | tf_op jit(solution)/shard_map/ppermute | solution.py:32
  85.2 0.7 copy-start.2
  85.3 0.7 copy-start.3
  85.3 0.7 copy-start.4
  85.3 0.7 copy-start.5

commit v22 on v21

--- a/solution.py
+++ b/solution.py
@@ -30,7 +30,7 @@
         keeps.append((carried + jnp.where(first, 0.0, got)).astype(jnp.bfloat16))
         send = (carried + jnp.where(first, mine, 0.0)).astype(jnp.bfloat16)
         backs.append(lax.ppermute(send, axis, swap))
-    return jnp.concatenate(keeps, axis=0), backs
+    return keeps, backs
 
 
 def state_kernel(key_ref, val_ref, out_ref):
@@ -75,7 +75,25 @@
     return sumsq
 
 
-def own_kernel(mine_ref, query_ref, key_ref, val_ref, keep_ref, att_ref, sumsq_ref):
+def pick_piece(refs, heads):
+    step = pl.program_id(0)
+    per_piece = refs[0].shape[0]
+    per_step = heads // per_piece
+
+    def prefix_of(head):
+        pick = refs[head // per_piece][head % per_piece]
+        for g in range(1, pl.num_programs(0)):
+            pick = jnp.where(step == g, refs[g * per_step + head // per_piece][head % per_piece], pick)
+        return pick
+
+    return prefix_of
+
+
+def own_kernel(mine_ref, query_ref, key_ref, val_ref, *refs):
+    keep_refs = refs[:-2]
+    att_ref, sumsq_ref = refs[-2:]
+    heads = att_ref.shape[1] // keep_refs[0].shape[1]
+
     @pl.when(pl.program_id(0) == 0)
     def _():
         sumsq_ref[...] = jnp.zeros_like(sumsq_ref)
@@ -83,8 +101,8 @@
     def store(cols, attended):
         att_ref[:, cols] = attended
 
-    sumsq_ref[...] = attend_heads(query_ref, key_ref, val_ref, lambda head: keep_ref[head],
-                                  keep_ref.shape[0], store, sumsq_ref[...])
+    sumsq_ref[...] = attend_heads(query_ref, key_ref, val_ref, pick_piece(keep_refs, heads),
+                                  heads, store, sumsq_ref[...])
 
 
 def other_kernel(mine_ref, query_ref, key_ref, val_ref, *refs):
@@ -97,15 +115,8 @@
     def _():
         own_copy.start()
     row_count, width = query_ref.shape
-    per_piece = back_refs[0].shape[0]
     heads = width // (out_ref.shape[1] // H)
-    per_step = heads // per_piece
-
-    def prefix_of(head):
-        pick = back_refs[head // per_piece][head % per_piece]
-        for g in range(1, pl.num_programs(0)):
-            pick = jnp.where(step == g, back_refs[g * per_step + head // per_piece][head % per_piece], pick)
-        return pick
+    prefix_of = pick_piece(back_refs, heads)
 
     @pl.when(step == 0)
     def _():
@@ -135,7 +146,7 @@
                     out_ref[:, cols] = (acc_ref[part] * scale * gain_ref[:, cols]).astype(out_ref.dtype)
 
 
-def attend_of(query, keyset, valset, keep, backs, mine_at, full_gain, group):
+def attend_of(query, keyset, valset, keeps, backs, mine_at, full_gain, group):
     row_count, feat_count = query.shape
     head_size = feat_count // H
     width = group * head_size
@@ -150,11 +161,12 @@
         grid_spec=pltpu.PrefetchScalarGridSpec(
             num_scalar_prefetch=1,
             grid=(steps,),
-            in_specs=[own_spec, own_spec, own_spec, half_spec],
+            in_specs=[own_spec, own_spec, own_spec]
+                     + [pl.BlockSpec(piece.shape, lambda g, at: (0, 0, 0)) for piece in keeps],
             out_specs=[pl.BlockSpec((row_count, width), lambda g, at: (0, g)), sumsq_spec]),
         out_shape=[jax.ShapeDtypeStruct((row_count, feat_count // 2), jnp.float32),
                    jax.ShapeDtypeStruct((row_count, head_size), jnp.float32)],
-    )(mine, query, keyset, valset, keep)
+    )(mine, query, keyset, valset, *keeps)
     return pl.pallas_call(
         other_kernel,
         grid_spec=pltpu.PrefetchScalarGridSpec(
@@ -188,8 +200,8 @@
     keyset = key_rows.reshape(seq_count * row_count, feat_count)
     valset = value_rows.reshape(seq_count * row_count, feat_count)
     state_terms = state_terms_of(keyset, valset, 16)
-    keep, backs = pair_chain_prefix(state_terms, "ctx", 4)
-    normed = attend_of(query, keyset, valset, keep, backs, lax.axis_index("ctx") % 2, full_gain, 8)
+    keeps, backs = pair_chain_prefix(state_terms, "ctx", 4)
+    normed = attend_of(query, keyset, valset, keeps, backs, lax.axis_index("ctx") % 2, full_gain, 8)
     return normed.reshape(seq_count, row_count, feat_count)
 
 

time: 94.1 us -> 93.7 us (level)
    ppermute x12, waiting for transfers between devices: 21.7 us -> 22.8 us  [pair_chain_prefix(): carried = carried + lax.ppermute(carried + total, axis, links)]
    ppermute x1, waiting for transfers between devices: 1.15 us -> 0.01 us  [shards(): other_gain = lax.ppermute(gain, 'dp', pair)]
  transfers between devices with their start and end apart: 21 -> 21, of which waited for: 9 -> 8; matrix products, arithmetic and copies ran while one was open for 5% -> 7% of each run, Pallas kernels for 7% -> 7%
where the time goes in v22:
time: 93.7 us; the launch traced here: 93.3 us
  waiting for transfers between devices  45.8 us (49%)
  Pallas kernels  18.7 us (20%)
  starting transfers between devices  17.7 us (19%)
  other arithmetic  8.85 us (9%)
  local copies, waits for them, and re-layouts  1.88 us (2%)
    ppermute x4, waiting for transfers between devices, pair_chain_prefix(): got = lax.ppermute(other_all[piece * step:(piece + 1) * step], axis, swap)  22.9 us
    ppermute x12, waiting for transfers between devices, pair_chain_prefix(): carried = carried + lax.ppermute(carried + total, axis, links)  22.8 us
    ppermute x12, starting transfers between devices, pair_chain_prefix(): carried = carried + lax.ppermute(carried + total, axis, links)  10.5 us
    pallas_call x1, Pallas kernels, attend_of(): pl.pallas_call(other_kernel, grid_spec=pltpu.PrefetchScalarGridSpec(num_s...  7.73 us
    pallas_call x1, Pallas kernels, attend_of(): pl.pallas_call(own_kernel, grid_spec=pltpu.PrefetchScalarGridSpec(num_sca...  6.56 us
    pallas_call x1, Pallas kernels, state_terms_of(): pl.pallas_call(state_kernel, grid=(H // group,), in_specs=[pl.BlockSpec((...  4.45 us
    ppermute x4, starting transfers between devices, pair_chain_prefix(): backs.append(lax.ppermute(send, axis, swap))  4.05 us
    add x8, other arithmetic, pair_chain_prefix(): carried = carried + lax.ppermute(carried + total, axis, links)  3.43 us
  transfers between devices with their start and end apart: 21, of which 8 were waited for; matrix products, arithmetic and copies ran while one was open for 7% of the time, Pallas kernels for 7%

profile of v22, /device:TPU:30, one launch (start us, length us, event | category | flops | bytes accessed | tf_op | source)
XLA Modules:
  0.0 93.3 jit_solution(15797295078186964327)
XLA Ops:
  0.0 4.4 %shard_map.46 = f32[32,128,128]{2,1,0:T(8,128)} custom-call(bf16[384,4096]{1,0:T(8,128)(2,1)} %bitcast.6, bf16[384,4096]{1,0:T(8,128)(2,1)} %bitcast.9), custom_call_target="tpu_custom_call" | custom-call | tf_op jit(solution)/shard_map/pallas_call | solution.py:49
  4.5 1.1 %constant_dynamic-slice_fusion.3 = f32[4,128,128]{2,1,0:T(8,128)S(1)} fusion(f32[32,128,128]{2,1,0:T(8,128)} %shard_map.46, s32[]{:T(128)S(6)} %add.131), kind=kLoop, calls=%fused_computation.18 | loop fusion | bytes 524292 | tf_op jit(solution)/shard_map/slice | solution.py:24
  5.6 0.6 collective-permute-start.15
  6.1 7.5 %collective-permute-done.15 = f32[4,128,128]{2,1,0:T(8,128)S(1)} collective-permute-done((f32[4,128,128]{2,1,0:T(8,128)S(1)}, f32[4,128,128]{2,1,0:T(8,128)S(1)}, u32[]{:S(2)}, u32[]{:S(2)}) %collective-permute-start.15) | collective-permute-done | bytes 262176 | tf_op jit(solution)/shard_map/ppermute | solution.py:24
  13.7 2.2 %dynamic-slice_add_fusion = (f32[4,128,128]{2,1,0:T(8,128)S(1)}, f32[4,128,128]{2,1,0:T(8,128)}, f32[4,128,128]{2,1,0:T(8,128)}, f32[4,128,128]{2,1,0:T(8,128)S(1)}) fusion(f32[4,128,128]{2,1,0:T(8,128)S(1)} %collective-permute-done.15, f32[32,128,128]{2,1,0:T(8,128)} %shard_map.46, s32[]{:T(128)S(6)} %add.130, s32[]{:T(128)S(6)} %add.129, s32[]{:T(128)S(6)} %add.127, ...), kind=kLoop, calls=%fused_computation.8 | loop fusion | flops 65536 | bytes 2359312 | tf_op jit(solution)/shard_map/add | solution.py:25
  15.9 0.5 collective-permute-start.10
  16.4 1.5 %collective-permute-start.5 = (f32[4,128,128]{2,1,0:T(8,128)}, f32[4,128,128]{2,1,0:T(8,128)S(1)}, u32[]{:S(2)}, u32[]{:S(2)}) collective-permute-start(f32[4,128,128]{2,1,0:T(8,128)} %get-tuple-element.23), channel_id=1, source_target_pairs={{0,2},{4,6},{8,10},{12,14},{2,0},{6,4},{10,8},{14,12},{1,3},{5,7},... | collective-permute-start | bytes 786440 | tf_op jit(solution)/shard_map/ppermute | solution.py:24
  17.9 0.5 collective-permute-start
  18.4 0.7 collective-permute-start.16
  19.1 6.2 %collective-permute-done.10 = f32[4,128,128]{2,1,0:T(8,128)S(1)} collective-permute-done((f32[4,128,128]{2,1,0:T(8,128)}, f32[4,128,128]{2,1,0:T(8,128)S(1)}, u32[]{:S(2)}, u32[]{:S(2)}) %collective-permute-start.10) | collective-permute-done | bytes 262176 | tf_op jit(solution)/shard_map/ppermute | solution.py:24
  25.3 5.6 %collective-permute-done.5 = f32[4,128,128]{2,1,0:T(8,128)S(1)} collective-permute-done((f32[4,128,128]{2,1,0:T(8,128)}, f32[4,128,128]{2,1,0:T(8,128)S(1)}, u32[]{:S(2)}, u32[]{:S(2)}) %collective-permute-start.5) | collective-permute-done | bytes 262176 | tf_op jit(solution)/shard_map/ppermute | solution.py:24
  30.9 3.5 %collective-permute-done = f32[4,128,128]{2,1,0:T(8,128)S(1)} collective-permute-done((f32[4,128,128]{2,1,0:T(8,128)S(1)}, f32[4,128,128]{2,1,0:T(8,128)S(1)}, u32[]{:S(2)}, u32[]{:S(2)}) %collective-permute-start) | collective-permute-done | bytes 262176 | tf_op jit(solution)/shard_map/ppermute | solution.py:24
  34.5 0.1 dynamic-slice_add_fusion.1
  34.6 0.7 collective-permute-start.11
  35.3 0.7 collective-permute-start.6
  36.0 0.7 collective-permute-start.17
  36.7 0.7 collective-permute-start.1
  37.4 0.0 collective-permute-done.11
  37.4 0.7 collective-permute-start.12
  38.1 0.0 collective-permute-done.6
  38.1 0.0 copy-start.6
  38.2 0.7 collective-permute-start.7
  38.9 0.8 fusion
  39.6 1.3 %collective-permute-start.18 = (f32[4,128,128]{2,1,0:T(8,128)}, f32[4,128,128]{2,1,0:T(8,128)}, u32[]{:S(2)}, u32[]{:S(2)}) collective-permute-start(f32[4,128,128]{2,1,0:T(8,128)} %get-tuple-element.9), channel_id=1, source_target_pairs={{8,12},{10,14},{9,13},{11,15},{24,28},{26,30},{25,29},{27,31}} | collective-permute-start | bytes 786440 | tf_op jit(solution)/shard_map/ppermute | solution.py:29
  40.9 0.7 collective-permute-start.2
  41.6 0.8 fusion.1
  42.4 1.3 %collective-permute-start.13 = (f32[4,128,128]{2,1,0:T(8,128)}, f32[4,128,128]{2,1,0:T(8,128)}, u32[]{:S(2)}, u32[]{:S(2)}) collective-permute-start(f32[4,128,128]{2,1,0:T(8,128)} %get-tuple-element.11), channel_id=1, source_target_pairs={{8,12},{10,14},{9,13},{11,15},{24,28},{26,30},{25,29},{27,31}} | collective-permute-start | bytes 786440 | tf_op jit(solution)/shard_map/ppermute | solution.py:29
  43.7 0.9 fusion.2
  44.6 1.3 %collective-permute-start.8 = (f32[4,128,128]{2,1,0:T(8,128)}, f32[4,128,128]{2,1,0:T(8,128)}, u32[]{:S(2)}, u32[]{:S(2)}) collective-permute-start(f32[4,128,128]{2,1,0:T(8,128)} %get-tuple-element.13), channel_id=1, source_target_pairs={{8,12},{10,14},{9,13},{11,15},{24,28},{26,30},{25,29},{27,31}} | collective-permute-start | bytes 786440 | tf_op jit(solution)/shard_map/ppermute | solution.py:29
  45.9 0.9 fusion.3
  46.8 1.3 %collective-permute-start.3 = (f32[4,128,128]{2,1,0:T(8,128)}, f32[4,128,128]{2,1,0:T(8,128)}, u32[]{:S(2)}, u32[]{:S(2)}) collective-permute-start(f32[4,128,128]{2,1,0:T(8,128)} %get-tuple-element.15), channel_id=1, source_target_pairs={{8,12},{10,14},{9,13},{11,15},{24,28},{26,30},{25,29},{27,31}} | collective-permute-start | bytes 786440 | tf_op jit(solution)/shard_map/ppermute | solution.py:29
  48.1 0.1 collective-permute-start.20
  48.1 7.8 %collective-permute-done.18 = f32[4,128,128]{2,1,0:T(8,128)} collective-permute-done((f32[4,128,128]{2,1,0:T(8,128)}, f32[4,128,128]{2,1,0:T(8,128)}, u32[]{:S(2)}, u32[]{:S(2)}) %collective-permute-start.18) | collective-permute-done | bytes 262176 | tf_op jit(solution)/shard_map/ppermute | solution.py:29
  56.0 6.3 %collective-permute-done.13 = f32[4,128,128]{2,1,0:T(8,128)} collective-permute-done((f32[4,128,128]{2,1,0:T(8,128)}, f32[4,128,128]{2,1,0:T(8,128)}, u32[]{:S(2)}, u32[]{:S(2)}) %collective-permute-start.13) | collective-permute-done | bytes 262176 | tf_op jit(solution)/shard_map/ppermute | solution.py:29
  62.3 5.8 %collective-permute-done.8 = f32[4,128,128]{2,1,0:T(8,128)} collective-permute-done((f32[4,128,128]{2,1,0:T(8,128)}, f32[4,128,128]{2,1,0:T(8,128)}, u32[]{:S(2)}, u32[]{:S(2)}) %collective-permute-start.8) | collective-permute-done | bytes 262176 | tf_op jit(solution)/shard_map/ppermute | solution.py:29
  68.2 2.8 %collective-permute-done.3 = f32[4,128,128]{2,1,0:T(8,128)} collective-permute-done((f32[4,128,128]{2,1,0:T(8,128)}, f32[4,128,128]{2,1,0:T(8,128)}, u32[]{:S(2)}, u32[]{:S(2)}) %collective-permute-start.3) | collective-permute-done | bytes 262176 | tf_op jit(solution)/shard_map/ppermute | solution.py:29
  71.0 2.5 %add_convert_fusion.4 = (bf16[4,128,128]{2,1,0:T(8,128)(2,1)}, bf16[4,128,128]{2,1,0:T(8,128)(2,1)}, bf16[4,128,128]{2,1,0:T(8,128)(2,1)}, bf16[4,128,128]{2,1,0...) fusion(f32[32,128,128]{2,1,0:T(8,128)S(1)} %copy-done, ...), kind=kLoop, calls=%fused_computation.4 | loop fusion | flops 1835008 | bytes 5242897 | tf_op jit(solution)/shard_map/convert_element_type | solution.py:31
  73.5 0.3 collective-permute-start.19
  73.8 1.7 %collective-permute-start.4 = (bf16[4,128,128]{2,1,0:T(8,128)(2,1)}, bf16[4,128,128]{2,1,0:T(8,128)(2,1)S(1)}, u32[]{:S(2)}, u32[]{:S(2)}) collective-permute-start(bf16[4,128,128]{2,1,0:T(8,128)(2,1)} %get-tuple-element.18), channel_id=1, source_target_pairs={{0,2},{4,6},{8,10},{12,14},{2,0},{6,4},{10,8},{14,12},{1,3},{5,7},... | collective-permute-start | bytes 393224 | tf_op jit(solution)/shard_map/ppermute | solution.py:32
  75.5 0.3 collective-permute-start.9
  75.9 1.7 %collective-permute-start.14 = (bf16[4,128,128]{2,1,0:T(8,128)(2,1)S(1)}, bf16[4,128,128]{2,1,0:T(8,128)(2,1)S(1)}, u32[]{:S(2)}, u32[]{:S(2)}) collective-permute-start(bf16[4,128,128]{2,1,0:T(8,128)(2,1)S(1)} %get-tuple-element.20), channel_id=1, source_target_pairs={{0,2},{4,6},{8,10},{12,14},{2,0},{6,4},{10,8},{14,12},{1,3},{5,7},... | collective-permute-start | bytes 393224 | tf_op jit(solution)/shard_map/ppermute | solution.py:32
  77.6 0.6 pad_maximum_fusion
  78.2 6.6 %shard_map.47 = (f32[384,2048]{1,0:T(8,128)}, f32[384,128]{1,0:T(8,128)}) custom-call(s32[1]{0:T(128)} %bitcast.mine_ref, bf16[384,4096]{1,0:T(8,128)(2,1)} %bitcast.12, bf16[384,4096]{1,0:T(8,128)(2,1)} %bitcast.7, bf16[384,4096]{1,0:T(8,128)(2,1)} %bitcast.10, bf16[4,128,128]{2,1,0:T(8,128)(2,1)} %get-tuple-element.30.refs_0_, ...), custom_call_target="tpu_custom_call" | custom-call | tf_op jit(solution)/shard_map/pallas_call | solution.py:159
  84.8 0.6 copy-done.2
  85.4 0.1 copy-done.3
  85.5 0.0 copy-done.4
  85.5 0.1 copy-done.5
  85.6 7.7 %shard_map.48 = bf16[384,4096]{1,0:T(8,128)(2,1)} custom-call(s32[1]{0:T(128)} %bitcast.mine_ref, bf16[384,4096]{1,0:T(8,128)(2,1)} %bitcast.13, bf16[384,4096]{1,0:T(8,128)(2,1)} %bitcast.8, bf16[384,4096]{1,0:T(8,128)(2,1)} %bitcast.11, bf16[4,128,128]{2,1,0:T(8,128)(2,1)} %copy-done.3, bf16[4,128,128]{2,1,0:T(8,128)(2,1)} %copy-done.4, ...), custom_call_target="tpu_custom_call" | custom-call | tf_op jit(solution)/shard_map/pallas_call | solution.py:170
  (25 shorter events, 0.2 us)
Async XLA Ops:
  4.4 30.0 %copy-start = (f32[32,128,128]{2,1,0:T(8,128)S(1)}, f32[32,128,128]{2,1,0:T(8,128)}, u32[]{:S(2)}) copy-start(f32[32,128,128]{2,1,0:T(8,128)} %shard_map.46) | copy-start | bytes 6291460
  5.6 8.1 %collective-permute-start.15 = (f32[4,128,128]{2,1,0:T(8,128)S(1)}, f32[4,128,128]{2,1,0:T(8,128)S(1)}, u32[]{:S(2)}, u32[]{:S(2)}) collective-permute-start(f32[4,128,128]{2,1,0:T(8,128)S(1)} %constant_dynamic-slice_fusion.3), channel_id=1, source_target_pairs={{0,2},{4,6},{8,10},{12,14},{2,0},{6,4},{10,8},{14,12},{1,3},{5,7},... | collective-permute-start | bytes 786440 | tf_op jit(solution)/shard_map/ppermute | solution.py:24
  13.7 2.2 %copy-start.1 = (f32[4,128,128]{2,1,0:T(8,128)}, f32[4,128,128]{2,1,0:T(8,128)S(1)}, u32[]{:S(2)}) copy-start(f32[4,128,128]{2,1,0:T(8,128)S(1)} %collective-permute-done.15) | copy-start | bytes 786436
  15.9 9.5 %collective-permute-start.10 = (f32[4,128,128]{2,1,0:T(8,128)}, f32[4,128,128]{2,1,0:T(8,128)S(1)}, u32[]{:S(2)}, u32[]{:S(2)}) collective-permute-start(f32[4,128,128]{2,1,0:T(8,128)} %get-tuple-element.22), channel_id=1, source_target_pairs={{0,2},{4,6},{8,10},{12,14},{2,0},{6,4},{10,8},{14,12},{1,3},{5,7},... | collective-permute-start | bytes 786440 | tf_op jit(solution)/shard_map/ppermute | solution.py:24
  16.4 14.6 %collective-permute-start.5 = (f32[4,128,128]{2,1,0:T(8,128)}, f32[4,128,128]{2,1,0:T(8,128)S(1)}, u32[]{:S(2)}, u32[]{:S(2)}) collective-permute-start(f32[4,128,128]{2,1,0:T(8,128)} %get-tuple-element.23), channel_id=1, source_target_pairs={{0,2},{4,6},{8,10},{12,14},{2,0},{6,4},{10,8},{14,12},{1,3},{5,7},... | collective-permute-start | bytes 786440 | tf_op jit(solution)/shard_map/ppermute | solution.py:24
  17.9 16.6 %collective-permute-start = (f32[4,128,128]{2,1,0:T(8,128)S(1)}, f32[4,128,128]{2,1,0:T(8,128)S(1)}, u32[]{:S(2)}, u32[]{:S(2)}) collective-permute-start(f32[4,128,128]{2,1,0:T(8,128)S(1)} %get-tuple-element.24), channel_id=1, source_target_pairs={{0,2},{4,6},{8,10},{12,14},{2,0},{6,4},{10,8},{14,12},{1,3},{5,7},... | collective-permute-start | bytes 786440 | tf_op jit(solution)/shard_map/ppermute | solution.py:24
  18.4 17.5 %collective-permute-start.16 = (f32[4,128,128]{2,1,0:T(8,128)S(1)}, f32[4,128,128]{2,1,0:T(8,128)S(1)}, u32[]{:S(2)}, u32[]{:S(2)}) collective-permute-start(f32[4,128,128]{2,1,0:T(8,128)S(1)} %get-tuple-element.21), channel_id=1, source_target_pairs={{0,4},{2,6},{1,5},{3,7},{16,20},{18,22},{17,21},{19,23}} | collective-permute-start | bytes 786440 | tf_op jit(solution)/shard_map/ppermute | solution.py:29
  34.6 2.8 %collective-permute-start.11 = (f32[4,128,128]{2,1,0:T(8,128)S(1)}, f32[4,128,128]{2,1,0:T(8,128)S(1)}, u32[]{:S(2)}, u32[]{:S(2)}) collective-permute-start(f32[4,128,128]{2,1,0:T(8,128)S(1)} %get-tuple-element.25), channel_id=1, source_target_pairs={{0,4},{2,6},{1,5},{3,7},{16,20},{18,22},{17,21},{19,23}} | collective-permute-start | bytes 786440 | tf_op jit(solution)/shard_map/ppermute | solution.py:29
  35.3 2.8 %collective-permute-start.6 = (f32[4,128,128]{2,1,0:T(8,128)S(1)}, f32[4,128,128]{2,1,0:T(8,128)S(1)}, u32[]{:S(2)}, u32[]{:S(2)}) collective-permute-start(f32[4,128,128]{2,1,0:T(8,128)S(1)} %get-tuple-element.26), channel_id=1, source_target_pairs={{0,4},{2,6},{1,5},{3,7},{16,20},{18,22},{17,21},{19,23}} | collective-permute-start | bytes 786440 | tf_op jit(solution)/shard_map/ppermute | solution.py:29
  36.0 2.9 %collective-permute-start.17 = (f32[4,128,128]{2,1,0:T(8,128)S(1)}, f32[4,128,128]{2,1,0:T(8,128)S(1)}, u32[]{:S(2)}, u32[]{:S(2)}) collective-permute-start(f32[4,128,128]{2,1,0:T(8,128)S(1)} %add.117), channel_id=1, source_target_pairs={{4,8},{6,10},{5,9},{7,11},{20,24},{22,26},{21,25},{23,27}} | collective-permute-start | bytes 786440 | tf_op jit(solution)/shard_map/ppermute | solution.py:29
  36.7 4.2 %collective-permute-start.1 = (f32[4,128,128]{2,1,0:T(8,128)S(1)}, f32[4,128,128]{2,1,0:T(8,128)S(1)}, u32[]{:S(2)}, u32[]{:S(2)}) collective-permute-start(f32[4,128,128]{2,1,0:T(8,128)S(1)} %get-tuple-element.27), channel_id=1, source_target_pairs={{0,4},{2,6},{1,5},{3,7},{16,20},{18,22},{17,21},{19,23}} | collective-permute-start | bytes 786440 | tf_op jit(solution)/shard_map/ppermute | solution.py:29
  37.4 4.2 %collective-permute-start.12 = (f32[4,128,128]{2,1,0:T(8,128)S(1)}, f32[4,128,128]{2,1,0:T(8,128)S(1)}, u32[]{:S(2)}, u32[]{:S(2)}) collective-permute-start(f32[4,128,128]{2,1,0:T(8,128)S(1)} %add.111), channel_id=1, source_target_pairs={{4,8},{6,10},{5,9},{7,11},{20,24},{22,26},{21,25},{23,27}} | collective-permute-start | bytes 786440 | tf_op jit(solution)/shard_map/ppermute | solution.py:29
  38.1 9.9 %copy-start.6 = (f32[2048]{0:T(1024)S(1)}, f32[2048]{0:T(1024)}, u32[]{:S(2)}) copy-start(f32[2048]{0:T(1024)} %param.7) | copy-start | bytes 24580
  38.2 5.5 %collective-permute-start.7 = (f32[4,128,128]{2,1,0:T(8,128)S(1)}, f32[4,128,128]{2,1,0:T(8,128)S(1)}, u32[]{:S(2)}, u32[]{:S(2)}) collective-permute-start(f32[4,128,128]{2,1,0:T(8,128)S(1)} %add.105), channel_id=1, source_target_pairs={{4,8},{6,10},{5,9},{7,11},{20,24},{22,26},{21,25},{23,27}} | collective-permute-start | bytes 786440 | tf_op jit(solution)/shard_map/ppermute | solution.py:29
  39.6 16.4 %collective-permute-start.18 = (f32[4,128,128]{2,1,0:T(8,128)}, f32[4,128,128]{2,1,0:T(8,128)}, u32[]{:S(2)}, u32[]{:S(2)}) collective-permute-start(f32[4,128,128]{2,1,0:T(8,128)} %get-tuple-element.9), channel_id=1, source_target_pairs={{8,12},{10,14},{9,13},{11,15},{24,28},{26,30},{25,29},{27,31}} | collective-permute-start | bytes 786440 | tf_op jit(solution)/shard_map/ppermute | solution.py:29
  40.9 4.9 %collective-permute-start.2 = (f32[4,128,128]{2,1,0:T(8,128)S(1)}, f32[4,128,128]{2,1,0:T(8,128)S(1)}, u32[]{:S(2)}, u32[]{:S(2)}) collective-permute-start(f32[4,128,128]{2,1,0:T(8,128)S(1)} %add.99), channel_id=1, source_target_pairs={{4,8},{6,10},{5,9},{7,11},{20,24},{22,26},{21,25},{23,27}} | collective-permute-start | bytes 786440 | tf_op jit(solution)/shard_map/ppermute | solution.py:29
  42.4 19.9 %collective-permute-start.13 = (f32[4,128,128]{2,1,0:T(8,128)}, f32[4,128,128]{2,1,0:T(8,128)}, u32[]{:S(2)}, u32[]{:S(2)}) collective-permute-start(f32[4,128,128]{2,1,0:T(8,128)} %get-tuple-element.11), channel_id=1, source_target_pairs={{8,12},{10,14},{9,13},{11,15},{24,28},{26,30},{25,29},{27,31}} | collective-permute-start | bytes 786440 | tf_op jit(solution)/shard_map/ppermute | solution.py:29
  44.6 23.6 %collective-permute-start.8 = (f32[4,128,128]{2,1,0:T(8,128)}, f32[4,128,128]{2,1,0:T(8,128)}, u32[]{:S(2)}, u32[]{:S(2)}) collective-permute-start(f32[4,128,128]{2,1,0:T(8,128)} %get-tuple-element.13), channel_id=1, source_target_pairs={{8,12},{10,14},{9,13},{11,15},{24,28},{26,30},{25,29},{27,31}} | collective-permute-start | bytes 786440 | tf_op jit(solution)/shard_map/ppermute | solution.py:29
  46.8 24.2 %collective-permute-start.3 = (f32[4,128,128]{2,1,0:T(8,128)}, f32[4,128,128]{2,1,0:T(8,128)}, u32[]{:S(2)}, u32[]{:S(2)}) collective-permute-start(f32[4,128,128]{2,1,0:T(8,128)} %get-tuple-element.15), channel_id=1, source_target_pairs={{8,12},{10,14},{9,13},{11,15},{24,28},{26,30},{25,29},{27,31}} | collective-permute-start | bytes 786440 | tf_op jit(solution)/shard_map/ppermute | solution.py:29
  48.1 29.5 %collective-permute-start.20 = (f32[2048]{0:T(1024)S(1)}, f32[2048]{0:T(1024)S(1)}, u32[]{:S(2)}, u32[]{:S(2)}) collective-permute-start(f32[2048]{0:T(1024)S(1)} %copy-done.6), channel_id=1, source_target_pairs={{0,1},{1,0},{2,3},{3,2},{4,5},{5,4},{6,7},{7,6},{8,9},{9,8},{10,11... | collective-permute-start | bytes 24584 | tf_op jit(solution)/shard_map/ppermute | solution.py:195
  73.5 11.2 %collective-permute-start.19 = (bf16[4,128,128]{2,1,0:T(8,128)(2,1)}, bf16[4,128,128]{2,1,0:T(8,128)(2,1)S(1)}, u32[]{:S(2)}, u32[]{:S(2)}) collective-permute-start(bf16[4,128,128]{2,1,0:T(8,128)(2,1)} %get-tuple-element.17), channel_id=1, source_target_pairs={{0,2},{4,6},{8,10},{12,14},{2,0},{6,4},{10,8},{14,12},{1,3},{5,7},... | collective-permute-start | bytes 393224 | tf_op jit(solution)/shard_map/ppermute | solution.py:32
  73.8 10.9 %collective-permute-start.4 = (bf16[4,128,128]{2,1,0:T(8,128)(2,1)}, bf16[4,128,128]{2,1,0:T(8,128)(2,1)S(1)}, u32[]{:S(2)}, u32[]{:S(2)}) collective-permute-start(bf16[4,128,128]{2,1,0:T(8,128)(2,1)} %get-tuple-element.18), channel_id=1, source_target_pairs={{0,2},{4,6},{8,10},{12,14},{2,0},{6,4},{10,8},{14,12},{1,3},{5,7},... | collective-permute-start | bytes 393224 | tf_op jit(solution)/shard_map/ppermute | solution.py:32
  75.5 9.2 %collective-permute-start.9 = (bf16[4,128,128]{2,1,0:T(8,128)(2,1)}, bf16[4,128,128]{2,1,0:T(8,128)(2,1)S(1)}, u32[]{:S(2)}, u32[]{:S(2)}) collective-permute-start(bf16[4,128,128]{2,1,0:T(8,128)(2,1)} %get-tuple-element.19), channel_id=1, source_target_pairs={{0,2},{4,6},{8,10},{12,14},{2,0},{6,4},{10,8},{14,12},{1,3},{5,7},... | collective-permute-start | bytes 393224 | tf_op jit(solution)/shard_map/ppermute | solution.py:32
  75.9 8.9 %collective-permute-start.14 = (bf16[4,128,128]{2,1,0:T(8,128)(2,1)S(1)}, bf16[4,128,128]{2,1,0:T(8,128)(2,1)S(1)}, u32[]{:S(2)}, u32[]{:S(2)}) collective-permute-start(bf16[4,128,128]{2,1,0:T(8,128)(2,1)S(1)} %get-tuple-element.20), channel_id=1, source_target_pairs={{0,2},{4,6},{8,10},{12,14},{2,0},{6,4},{10,8},{14,12},{1,3},{5,7},... | collective-permute-start | bytes 393224 | tf_op jit(solution)/shard_map/ppermute | solution.py:32
  84.7 0.7 copy-start.2
  84.8 0.7 copy-start.3
  84.8 0.7 copy-start.4
  84.8 0.7 copy-start.5

commit v23 on v22

--- a/solution.py
+++ b/solution.py
@@ -27,7 +27,7 @@
         for hop in range(1, pairs):
             links = [(2 * (hop - 1) + side, 2 * hop + side) for side in range(2)]
             carried = carried + lax.ppermute(carried + total, axis, links)
-        keeps.append((carried + jnp.where(first, 0.0, got)).astype(jnp.bfloat16))
+        keeps.append((carried, got))
         send = (carried + jnp.where(first, mine, 0.0)).astype(jnp.bfloat16)
         backs.append(lax.ppermute(send, axis, swap))
     return keeps, backs
@@ -90,9 +90,16 @@
 
 
 def own_kernel(mine_ref, query_ref, key_ref, val_ref, *refs):
-    keep_refs = refs[:-2]
+    pieces = (len(refs) - 2) // 2
+    carried_refs, got_refs = refs[:pieces], refs[pieces:2 * pieces]
     att_ref, sumsq_ref = refs[-2:]
-    heads = att_ref.shape[1] // keep_refs[0].shape[1]
+    heads = att_ref.shape[1] // carried_refs[0].shape[1]
+    carried_of = pick_piece(carried_refs, heads)
+    got_of = pick_piece(got_refs, heads)
+    second = mine_ref[0] == 1
+
+    def keep_of(head):
+        return (carried_of(head) + jnp.where(second, got_of(head), 0.0)).astype(jnp.bfloat16)
 
     @pl.when(pl.program_id(0) == 0)
     def _():
@@ -101,8 +108,7 @@
     def store(cols, attended):
         att_ref[:, cols] = attended
 
-    sumsq_ref[...] = attend_heads(query_ref, key_ref, val_ref, pick_piece(keep_refs, heads),
-                                  heads, store, sumsq_ref[...])
+    sumsq_ref[...] = attend_heads(query_ref, key_ref, val_ref, keep_of, heads, store, sumsq_ref[...])
 
 
 def other_kernel(mine_ref, query_ref, key_ref, val_ref, *refs):
@@ -162,11 +168,11 @@
             num_scalar_prefetch=1,
             grid=(steps,),
             in_specs=[own_spec, own_spec, own_spec]
-                     + [pl.BlockSpec(piece.shape, lambda g, at: (0, 0, 0)) for piece in keeps],
+                     + [pl.BlockSpec(piece.shape, lambda g, at: (0, 0, 0)) for pair in keeps for piece in pair],
             out_specs=[pl.BlockSpec((row_count, width), lambda g, at: (0, g)), sumsq_spec]),
         out_shape=[jax.ShapeDtypeStruct((row_count, feat_count // 2), jnp.float32),
                    jax.ShapeDtypeStruct((row_count, head_size), jnp.float32)],
-    )(mine, query, keyset, valset, *keeps)
+    )(mine, query, keyset, valset, *[pair[0] for pair in keeps], *[pair[1] for pair in keeps])
     return pl.pallas_call(
         other_kernel,
         grid_spec=pltpu.PrefetchScalarGridSpec(

time: 93.7 us -> 93.6 us (level)
  transfers between devices with their start and end apart: 21 -> 21, of which waited for: 8 -> 8; matrix products, arithmetic and copies ran while one was open for 7% -> 7% of each run, Pallas kernels for 7% -> 8%
where the time goes in v23:
time: 93.6 us; the launch traced here: 93.3 us
  waiting for transfers between devices  45.9 us (49%)
  Pallas kernels  19.1 us (20%)
  starting transfers between devices  17.7 us (19%)
  other arithmetic  8.27 us (9%)
  local copies, waits for them, and re-layouts  1.86 us (2%)
    ppermute x12, waiting for transfers between devices, pair_chain_prefix(): carried = carried + lax.ppermute(carried + total, axis, links)  23 us
    ppermute x4, waiting for transfers between devices, pair_chain_prefix(): got = lax.ppermute(other_all[piece * step:(piece + 1) * step], axis, swap)  22.9 us
    ppermute x12, starting transfers between devices, pair_chain_prefix(): carried = carried + lax.ppermute(carried + total, axis, links)  10.5 us
    pallas_call x1, Pallas kernels, attend_of(): pl.pallas_call(other_kernel, grid_spec=pltpu.PrefetchScalarGridSpec(num_s...  7.66 us
    pallas_call x1, Pallas kernels, attend_of(): pl.pallas_call(own_kernel, grid_spec=pltpu.PrefetchScalarGridSpec(num_sca...  7.02 us
    pallas_call x1, Pallas kernels, state_terms_of(): pl.pallas_call(state_kernel, grid=(H // group,), in_specs=[pl.BlockSpec((...  4.45 us
    ppermute x4, starting transfers between devices, pair_chain_prefix(): backs.append(lax.ppermute(send, axis, swap))  4.05 us
    add x8, other arithmetic, pair_chain_prefix(): carried = carried + lax.ppermute(carried + total, axis, links)  3.16 us
  transfers between devices with their start and end apart: 21, of which 8 were waited for; matrix products, arithmetic and copies ran while one was open for 7% of the time, Pallas kernels for 8%

profile of v23, /device:TPU:30, one launch (start us, length us, event | category | flops | bytes accessed | tf_op | source)
XLA Modules:
  0.0 93.3 jit_solution(18300098140837925871)
XLA Ops:
  0.0 4.4 %shard_map.46 = f32[32,128,128]{2,1,0:T(8,128)} custom-call(bf16[384,4096]{1,0:T(8,128)(2,1)} %bitcast.6, bf16[384,4096]{1,0:T(8,128)(2,1)} %bitcast.9), custom_call_target="tpu_custom_call" | custom-call | tf_op jit(solution)/shard_map/pallas_call | solution.py:49
  4.5 1.1 %constant_dynamic-slice_fusion.3 = f32[4,128,128]{2,1,0:T(8,128)S(1)} fusion(f32[32,128,128]{2,1,0:T(8,128)} %shard_map.46, s32[]{:T(128)S(6)} %add.115), kind=kLoop, calls=%fused_computation.14 | loop fusion | bytes 524292 | tf_op jit(solution)/shard_map/slice | solution.py:24
  5.6 0.6 collective-permute-start.15
  6.1 7.5 %collective-permute-done.15.refs_7_ = f32[4,128,128]{2,1,0:T(8,128)S(1)} collective-permute-done((f32[4,128,128]{2,1,0:T(8,128)S(1)}, f32[4,128,128]{2,1,0:T(8,128)S(1)}, u32[]{:S(2)}, u32[]{:S(2)}) %collective-permute-start.15) | collective-permute-done | bytes 262176 | tf_op jit(solution)/shard_map/ppermute | solution.py:24
  13.7 2.2 %dynamic-slice_add_fusion = (f32[4,128,128]{2,1,0:T(8,128)S(1)}, f32[4,128,128]{2,1,0:T(8,128)}, f32[4,128,128]{2,1,0:T(8,128)}, f32[4,128,128]{2,1,0:T(8,128)S(1)}) fusion(f32[4,128,128]{2,1,0:T(8,128)S(1)} %collective-permute-done.15.refs_7_, f32[32,128,128]{2,1,0:T(8,128)} %shard_map.46, s32[]{:T(128)S(6)} %add.114, s32[]{:T(128)S(6)} %add.113, ...), kind=kLoop, calls=%fused_computation.4 | loop fusion | flops 65536 | bytes 2359312 | tf_op jit(solution)/shard_map/add | solution.py:25
  15.9 0.5 collective-permute-start.10
  16.4 1.5 %collective-permute-start.5 = (f32[4,128,128]{2,1,0:T(8,128)}, f32[4,128,128]{2,1,0:T(8,128)S(1)}, u32[]{:S(2)}, u32[]{:S(2)}) collective-permute-start(f32[4,128,128]{2,1,0:T(8,128)} %get-tuple-element.33), channel_id=1, source_target_pairs={{0,2},{4,6},{8,10},{12,14},{2,0},{6,4},{10,8},{14,12},{1,3},{5,7},... | collective-permute-start | bytes 786440 | tf_op jit(solution)/shard_map/ppermute | solution.py:24
  17.9 0.5 collective-permute-start
  18.4 0.7 collective-permute-start.16
  19.1 6.2 %collective-permute-done.10.refs_6_ = f32[4,128,128]{2,1,0:T(8,128)S(1)} collective-permute-done((f32[4,128,128]{2,1,0:T(8,128)}, f32[4,128,128]{2,1,0:T(8,128)S(1)}, u32[]{:S(2)}, u32[]{:S(2)}) %collective-permute-start.10) | collective-permute-done | bytes 262176 | tf_op jit(solution)/shard_map/ppermute | solution.py:24
  25.3 5.6 %collective-permute-done.5.refs_5_ = f32[4,128,128]{2,1,0:T(8,128)S(1)} collective-permute-done((f32[4,128,128]{2,1,0:T(8,128)}, f32[4,128,128]{2,1,0:T(8,128)S(1)}, u32[]{:S(2)}, u32[]{:S(2)}) %collective-permute-start.5) | collective-permute-done | bytes 262176 | tf_op jit(solution)/shard_map/ppermute | solution.py:24
  30.9 3.5 %collective-permute-done.refs_4_ = f32[4,128,128]{2,1,0:T(8,128)S(1)} collective-permute-done((f32[4,128,128]{2,1,0:T(8,128)S(1)}, f32[4,128,128]{2,1,0:T(8,128)S(1)}, u32[]{:S(2)}, u32[]{:S(2)}) %collective-permute-start) | collective-permute-done | bytes 262176 | tf_op jit(solution)/shard_map/ppermute | solution.py:24
  34.5 0.1 dynamic-slice_add_fusion.1
  34.6 0.7 collective-permute-start.11
  35.2 0.7 collective-permute-start.6
  36.0 0.7 collective-permute-start.17
  36.7 0.7 collective-permute-start.1
  37.3 0.0 collective-permute-done.11
  37.4 0.7 collective-permute-start.12
  38.1 0.0 collective-permute-done.6
  38.1 0.0 copy-start.9
  38.2 0.7 collective-permute-start.7
  38.8 0.8 fusion
  39.6 1.3 %collective-permute-start.18 = (f32[4,128,128]{2,1,0:T(8,128)}, f32[4,128,128]{2,1,0:T(8,128)}, u32[]{:S(2)}, u32[]{:S(2)}) collective-permute-start(f32[4,128,128]{2,1,0:T(8,128)} %get-tuple-element.11), channel_id=1, source_target_pairs={{8,12},{10,14},{9,13},{11,15},{24,28},{26,30},{25,29},{27,31}} | collective-permute-start | bytes 786440 | tf_op jit(solution)/shard_map/ppermute | solution.py:29
  41.0 0.7 collective-permute-start.2
  41.7 0.7 fusion.1
  42.4 1.3 %collective-permute-start.13 = (f32[4,128,128]{2,1,0:T(8,128)}, f32[4,128,128]{2,1,0:T(8,128)S(1)}, u32[]{:S(2)}, u32[]{:S(2)}) collective-permute-start(f32[4,128,128]{2,1,0:T(8,128)} %get-tuple-element.15), channel_id=1, source_target_pairs={{8,12},{10,14},{9,13},{11,15},{24,28},{26,30},{25,29},{27,31}} | collective-permute-start | bytes 786440 | tf_op jit(solution)/shard_map/ppermute | solution.py:29
  43.7 0.7 fusion.2
  44.5 1.3 %collective-permute-start.8 = (f32[4,128,128]{2,1,0:T(8,128)}, f32[4,128,128]{2,1,0:T(8,128)}, u32[]{:S(2)}, u32[]{:S(2)}) collective-permute-start(f32[4,128,128]{2,1,0:T(8,128)} %get-tuple-element.19), channel_id=1, source_target_pairs={{8,12},{10,14},{9,13},{11,15},{24,28},{26,30},{25,29},{27,31}} | collective-permute-start | bytes 786440 | tf_op jit(solution)/shard_map/ppermute | solution.py:29
  45.8 0.8 fusion.3
  46.5 1.3 %collective-permute-start.3 = (f32[4,128,128]{2,1,0:T(8,128)}, f32[4,128,128]{2,1,0:T(8,128)}, u32[]{:S(2)}, u32[]{:S(2)}) collective-permute-start(f32[4,128,128]{2,1,0:T(8,128)} %get-tuple-element.23), channel_id=1, source_target_pairs={{8,12},{10,14},{9,13},{11,15},{24,28},{26,30},{25,29},{27,31}} | collective-permute-start | bytes 786440 | tf_op jit(solution)/shard_map/ppermute | solution.py:29
  47.8 0.1 collective-permute-start.20
  47.9 8.2 %collective-permute-done.18 = f32[4,128,128]{2,1,0:T(8,128)} collective-permute-done((f32[4,128,128]{2,1,0:T(8,128)}, f32[4,128,128]{2,1,0:T(8,128)}, u32[]{:S(2)}, u32[]{:S(2)}) %collective-permute-start.18) | collective-permute-done | bytes 262176 | tf_op jit(solution)/shard_map/ppermute | solution.py:29
  56.1 6.0 %collective-permute-done.13 = f32[4,128,128]{2,1,0:T(8,128)S(1)} collective-permute-done((f32[4,128,128]{2,1,0:T(8,128)}, f32[4,128,128]{2,1,0:T(8,128)S(1)}, u32[]{:S(2)}, u32[]{:S(2)}) %collective-permute-start.13) | collective-permute-done | bytes 262176 | tf_op jit(solution)/shard_map/ppermute | solution.py:29
  62.1 5.9 %collective-permute-done.8 = f32[4,128,128]{2,1,0:T(8,128)} collective-permute-done((f32[4,128,128]{2,1,0:T(8,128)}, f32[4,128,128]{2,1,0:T(8,128)}, u32[]{:S(2)}, u32[]{:S(2)}) %collective-permute-start.8) | collective-permute-done | bytes 262176 | tf_op jit(solution)/shard_map/ppermute | solution.py:29
  68.1 2.8 %collective-permute-done.3 = f32[4,128,128]{2,1,0:T(8,128)} collective-permute-done((f32[4,128,128]{2,1,0:T(8,128)}, f32[4,128,128]{2,1,0:T(8,128)}, u32[]{:S(2)}, u32[]{:S(2)}) %collective-permute-start.3) | collective-permute-done | bytes 262176 | tf_op jit(solution)/shard_map/ppermute | solution.py:29
  70.9 2.2 %add_convert_fusion = (bf16[4,128,128]{2,1,0:T(8,128)(2,1)}, f32[4,128,128]{2,1,0:T(8,128)}, bf16[4,128,128]{2,1,0:T(8,128)(2,1)}, f32[4,128,128]{2,1,0:T(8,128)...) fusion(f32[32,128,128]{2,1,0:T(8,128)S(1)} %copy-done, ...), kind=kLoop, calls=%fused_computation | loop fusion | flops 1048576 | bytes 4718609 | tf_op jit(solution)/shard_map/convert_element_type | solution.py:31
  73.1 0.5 collective-permute-start.19
  73.6 1.6 %collective-permute-start.4 = (bf16[4,128,128]{2,1,0:T(8,128)(2,1)}, bf16[4,128,128]{2,1,0:T(8,128)(2,1)S(1)}, u32[]{:S(2)}, u32[]{:S(2)}) collective-permute-start(bf16[4,128,128]{2,1,0:T(8,128)(2,1)} %get-tuple-element.25), channel_id=1, source_target_pairs={{0,2},{4,6},{8,10},{12,14},{2,0},{6,4},{10,8},{14,12},{1,3},{5,7},... | collective-permute-start | bytes 393224 | tf_op jit(solution)/shard_map/ppermute | solution.py:32
  75.1 0.5 collective-permute-start.9
  75.6 1.6 %collective-permute-start.14 = (bf16[4,128,128]{2,1,0:T(8,128)(2,1)S(1)}, bf16[4,128,128]{2,1,0:T(8,128)(2,1)S(1)}, u32[]{:S(2)}, u32[]{:S(2)}) collective-permute-start(bf16[4,128,128]{2,1,0:T(8,128)(2,1)S(1)} %get-tuple-element.29), channel_id=1, source_target_pairs={{0,2},{4,6},{8,10},{12,14},{2,0},{6,4},{10,8},{14,12},{1,3},{5,7},... | collective-permute-start | bytes 393224 | tf_op jit(solution)/shard_map/ppermute | solution.py:32
  77.2 0.6 pad_maximum_fusion
  77.8 7.0 %shard_map.47 = (f32[384,2048]{1,0:T(8,128)}, f32[384,128]{1,0:T(8,128)}) custom-call(s32[1]{0:T(128)} %bitcast.mine_ref, bf16[384,4096]{1,0:T(8,128)(2,1)} %bitcast.12, bf16[384,4096]{1,0:T(8,128)(2,1)} %bitcast.7, bf16[384,4096]{1,0:T(8,128)(2,1)} %bitcast.10, f32[4,128,128]{2,1,0:T(8,128)} %get-tuple-element.26.refs_0_, ...), custom_call_target="tpu_custom_call" | custom-call | tf_op jit(solution)/shard_map/pallas_call | solution.py:165
  84.9 0.6 copy-done.5
  85.5 0.0 copy-done.6
  85.5 0.1 copy-done.7
  85.6 0.0 copy-done.8
  85.6 7.7 %shard_map.48 = bf16[384,4096]{1,0:T(8,128)(2,1)} custom-call(s32[1]{0:T(128)} %bitcast.mine_ref, bf16[384,4096]{1,0:T(8,128)(2,1)} %bitcast.13, bf16[384,4096]{1,0:T(8,128)(2,1)} %bitcast.8, bf16[384,4096]{1,0:T(8,128)(2,1)} %bitcast.11, bf16[4,128,128]{2,1,0:T(8,128)(2,1)} %copy-done.6, bf16[4,128,128]{2,1,0:T(8,128)(2,1)} %copy-done.7, ...), custom_call_target="tpu_custom_call" | custom-call | tf_op jit(solution)/shard_map/pallas_call | solution.py:176
  (31 shorter events, 0.2 us)
Async XLA Ops:
  4.4 30.0 %copy-start = (f32[32,128,128]{2,1,0:T(8,128)S(1)}, f32[32,128,128]{2,1,0:T(8,128)}, u32[]{:S(2)}) copy-start(f32[32,128,128]{2,1,0:T(8,128)} %shard_map.46) | copy-start | bytes 6291460
  5.6 8.1 %collective-permute-start.15 = (f32[4,128,128]{2,1,0:T(8,128)S(1)}, f32[4,128,128]{2,1,0:T(8,128)S(1)}, u32[]{:S(2)}, u32[]{:S(2)}) collective-permute-start(f32[4,128,128]{2,1,0:T(8,128)S(1)} %constant_dynamic-slice_fusion.3), channel_id=1, source_target_pairs={{0,2},{4,6},{8,10},{12,14},{2,0},{6,4},{10,8},{14,12},{1,3},{5,7},... | collective-permute-start | bytes 786440 | tf_op jit(solution)/shard_map/ppermute | solution.py:24
  13.7 2.2 %copy-start.4 = (f32[4,128,128]{2,1,0:T(8,128)}, f32[4,128,128]{2,1,0:T(8,128)S(1)}, u32[]{:S(2)}) copy-start(f32[4,128,128]{2,1,0:T(8,128)S(1)} %collective-permute-done.15.refs_7_) | copy-start | bytes 786436
  15.9 9.5 %collective-permute-start.10 = (f32[4,128,128]{2,1,0:T(8,128)}, f32[4,128,128]{2,1,0:T(8,128)S(1)}, u32[]{:S(2)}, u32[]{:S(2)}) collective-permute-start(f32[4,128,128]{2,1,0:T(8,128)} %get-tuple-element.32), channel_id=1, source_target_pairs={{0,2},{4,6},{8,10},{12,14},{2,0},{6,4},{10,8},{14,12},{1,3},{5,7},... | collective-permute-start | bytes 786440 | tf_op jit(solution)/shard_map/ppermute | solution.py:24
  16.4 14.6 %collective-permute-start.5 = (f32[4,128,128]{2,1,0:T(8,128)}, f32[4,128,128]{2,1,0:T(8,128)S(1)}, u32[]{:S(2)}, u32[]{:S(2)}) collective-permute-start(f32[4,128,128]{2,1,0:T(8,128)} %get-tuple-element.33), channel_id=1, source_target_pairs={{0,2},{4,6},{8,10},{12,14},{2,0},{6,4},{10,8},{14,12},{1,3},{5,7},... | collective-permute-start | bytes 786440 | tf_op jit(solution)/shard_map/ppermute | solution.py:24
  17.9 16.6 %collective-permute-start = (f32[4,128,128]{2,1,0:T(8,128)S(1)}, f32[4,128,128]{2,1,0:T(8,128)S(1)}, u32[]{:S(2)}, u32[]{:S(2)}) collective-permute-start(f32[4,128,128]{2,1,0:T(8,128)S(1)} %get-tuple-element.34), channel_id=1, source_target_pairs={{0,2},{4,6},{8,10},{12,14},{2,0},{6,4},{10,8},{14,12},{1,3},{5,7},... | collective-permute-start | bytes 786440 | tf_op jit(solution)/shard_map/ppermute | solution.py:24
  18.4 17.5 %collective-permute-start.16 = (f32[4,128,128]{2,1,0:T(8,128)S(1)}, f32[4,128,128]{2,1,0:T(8,128)S(1)}, u32[]{:S(2)}, u32[]{:S(2)}) collective-permute-start(f32[4,128,128]{2,1,0:T(8,128)S(1)} %get-tuple-element.31), channel_id=1, source_target_pairs={{0,4},{2,6},{1,5},{3,7},{16,20},{18,22},{17,21},{19,23}} | collective-permute-start | bytes 786440 | tf_op jit(solution)/shard_map/ppermute | solution.py:29
  25.3 15.6 %copy-start.1 = (f32[4,128,128]{2,1,0:T(8,128)}, f32[4,128,128]{2,1,0:T(8,128)S(1)}, u32[]{:S(2)}) copy-start(f32[4,128,128]{2,1,0:T(8,128)S(1)} %collective-permute-done.10.refs_6_) | copy-start | bytes 786436
  30.9 10.0 %copy-start.2 = (f32[4,128,128]{2,1,0:T(8,128)}, f32[4,128,128]{2,1,0:T(8,128)S(1)}, u32[]{:S(2)}) copy-start(f32[4,128,128]{2,1,0:T(8,128)S(1)} %collective-permute-done.5.refs_5_) | copy-start | bytes 786436
  34.5 6.5 %copy-start.3 = (f32[4,128,128]{2,1,0:T(8,128)}, f32[4,128,128]{2,1,0:T(8,128)S(1)}, u32[]{:S(2)}) copy-start(f32[4,128,128]{2,1,0:T(8,128)S(1)} %collective-permute-done.refs_4_) | copy-start | bytes 786436
  34.6 2.8 %collective-permute-start.11 = (f32[4,128,128]{2,1,0:T(8,128)S(1)}, f32[4,128,128]{2,1,0:T(8,128)S(1)}, u32[]{:S(2)}, u32[]{:S(2)}) collective-permute-start(f32[4,128,128]{2,1,0:T(8,128)S(1)} %get-tuple-element.35), channel_id=1, source_target_pairs={{0,4},{2,6},{1,5},{3,7},{16,20},{18,22},{17,21},{19,23}} | collective-permute-start | bytes 786440 | tf_op jit(solution)/shard_map/ppermute | solution.py:29
  35.2 2.8 %collective-permute-start.6 = (f32[4,128,128]{2,1,0:T(8,128)S(1)}, f32[4,128,128]{2,1,0:T(8,128)S(1)}, u32[]{:S(2)}, u32[]{:S(2)}) collective-permute-start(f32[4,128,128]{2,1,0:T(8,128)S(1)} %get-tuple-element.36), channel_id=1, source_target_pairs={{0,4},{2,6},{1,5},{3,7},{16,20},{18,22},{17,21},{19,23}} | collective-permute-start | bytes 786440 | tf_op jit(solution)/shard_map/ppermute | solution.py:29
  36.0 2.9 %collective-permute-start.17 = (f32[4,128,128]{2,1,0:T(8,128)S(1)}, f32[4,128,128]{2,1,0:T(8,128)S(1)}, u32[]{:S(2)}, u32[]{:S(2)}) collective-permute-start(f32[4,128,128]{2,1,0:T(8,128)S(1)} %add.105), channel_id=1, source_target_pairs={{4,8},{6,10},{5,9},{7,11},{20,24},{22,26},{21,25},{23,27}} | collective-permute-start | bytes 786440 | tf_op jit(solution)/shard_map/ppermute | solution.py:29
  36.7 4.2 %collective-permute-start.1 = (f32[4,128,128]{2,1,0:T(8,128)S(1)}, f32[4,128,128]{2,1,0:T(8,128)S(1)}, u32[]{:S(2)}, u32[]{:S(2)}) collective-permute-start(f32[4,128,128]{2,1,0:T(8,128)S(1)} %get-tuple-element.37), channel_id=1, source_target_pairs={{0,4},{2,6},{1,5},{3,7},{16,20},{18,22},{17,21},{19,23}} | collective-permute-start | bytes 786440 | tf_op jit(solution)/shard_map/ppermute | solution.py:29
  37.4 4.3 %collective-permute-start.12 = (f32[4,128,128]{2,1,0:T(8,128)S(1)}, f32[4,128,128]{2,1,0:T(8,128)S(1)}, u32[]{:S(2)}, u32[]{:S(2)}) collective-permute-start(f32[4,128,128]{2,1,0:T(8,128)S(1)} %add.99), channel_id=1, source_target_pairs={{4,8},{6,10},{5,9},{7,11},{20,24},{22,26},{21,25},{23,27}} | collective-permute-start | bytes 786440 | tf_op jit(solution)/shard_map/ppermute | solution.py:29
  38.1 9.7 %copy-start.9 = (f32[2048]{0:T(1024)S(1)}, f32[2048]{0:T(1024)}, u32[]{:S(2)}) copy-start(f32[2048]{0:T(1024)} %param.7) | copy-start | bytes 24580
  38.2 5.5 %collective-permute-start.7 = (f32[4,128,128]{2,1,0:T(8,128)S(1)}, f32[4,128,128]{2,1,0:T(8,128)S(1)}, u32[]{:S(2)}, u32[]{:S(2)}) collective-permute-start(f32[4,128,128]{2,1,0:T(8,128)S(1)} %add.93), channel_id=1, source_target_pairs={{4,8},{6,10},{5,9},{7,11},{20,24},{22,26},{21,25},{23,27}} | collective-permute-start | bytes 786440 | tf_op jit(solution)/shard_map/ppermute | solution.py:29
  39.6 16.5 %collective-permute-start.18 = (f32[4,128,128]{2,1,0:T(8,128)}, f32[4,128,128]{2,1,0:T(8,128)}, u32[]{:S(2)}, u32[]{:S(2)}) collective-permute-start(f32[4,128,128]{2,1,0:T(8,128)} %get-tuple-element.11), channel_id=1, source_target_pairs={{8,12},{10,14},{9,13},{11,15},{24,28},{26,30},{25,29},{27,31}} | collective-permute-start | bytes 786440 | tf_op jit(solution)/shard_map/ppermute | solution.py:29
  41.0 4.8 %collective-permute-start.2 = (f32[4,128,128]{2,1,0:T(8,128)S(1)}, f32[4,128,128]{2,1,0:T(8,128)S(1)}, u32[]{:S(2)}, u32[]{:S(2)}) collective-permute-start(f32[4,128,128]{2,1,0:T(8,128)S(1)} %add.87), channel_id=1, source_target_pairs={{4,8},{6,10},{5,9},{7,11},{20,24},{22,26},{21,25},{23,27}} | collective-permute-start | bytes 786440 | tf_op jit(solution)/shard_map/ppermute | solution.py:29
  42.4 19.7 %collective-permute-start.13 = (f32[4,128,128]{2,1,0:T(8,128)}, f32[4,128,128]{2,1,0:T(8,128)S(1)}, u32[]{:S(2)}, u32[]{:S(2)}) collective-permute-start(f32[4,128,128]{2,1,0:T(8,128)} %get-tuple-element.15), channel_id=1, source_target_pairs={{8,12},{10,14},{9,13},{11,15},{24,28},{26,30},{25,29},{27,31}} | collective-permute-start | bytes 786440 | tf_op jit(solution)/shard_map/ppermute | solution.py:29
  44.5 23.6 %collective-permute-start.8 = (f32[4,128,128]{2,1,0:T(8,128)}, f32[4,128,128]{2,1,0:T(8,128)}, u32[]{:S(2)}, u32[]{:S(2)}) collective-permute-start(f32[4,128,128]{2,1,0:T(8,128)} %get-tuple-element.19), channel_id=1, source_target_pairs={{8,12},{10,14},{9,13},{11,15},{24,28},{26,30},{25,29},{27,31}} | collective-permute-start | bytes 786440 | tf_op jit(solution)/shard_map/ppermute | solution.py:29
  46.5 24.3 %collective-permute-start.3 = (f32[4,128,128]{2,1,0:T(8,128)}, f32[4,128,128]{2,1,0:T(8,128)}, u32[]{:S(2)}, u32[]{:S(2)}) collective-permute-start(f32[4,128,128]{2,1,0:T(8,128)} %get-tuple-element.23), channel_id=1, source_target_pairs={{8,12},{10,14},{9,13},{11,15},{24,28},{26,30},{25,29},{27,31}} | collective-permute-start | bytes 786440 | tf_op jit(solution)/shard_map/ppermute | solution.py:29
  47.8 29.4 %collective-permute-start.20 = (f32[2048]{0:T(1024)S(1)}, f32[2048]{0:T(1024)S(1)}, u32[]{:S(2)}, u32[]{:S(2)}) collective-permute-start(f32[2048]{0:T(1024)S(1)} %copy-done.9), channel_id=1, source_target_pairs={{0,1},{1,0},{2,3},{3,2},{4,5},{5,4},{6,7},{7,6},{8,9},{9,8},{10,11... | collective-permute-start | bytes 24584 | tf_op jit(solution)/shard_map/ppermute | solution.py:201
  73.1 11.7 %collective-permute-start.19 = (bf16[4,128,128]{2,1,0:T(8,128)(2,1)}, bf16[4,128,128]{2,1,0:T(8,128)(2,1)S(1)}, u32[]{:S(2)}, u32[]{:S(2)}) collective-permute-start(bf16[4,128,128]{2,1,0:T(8,128)(2,1)} %get-tuple-element.9), channel_id=1, source_target_pairs={{0,2},{4,6},{8,10},{12,14},{2,0},{6,4},{10,8},{14,12},{1,3},{5,7},... | collective-permute-start | bytes 393224 | tf_op jit(solution)/shard_map/ppermute | solution.py:32
  73.6 11.2 %collective-permute-start.4 = (bf16[4,128,128]{2,1,0:T(8,128)(2,1)}, bf16[4,128,128]{2,1,0:T(8,128)(2,1)S(1)}, u32[]{:S(2)}, u32[]{:S(2)}) collective-permute-start(bf16[4,128,128]{2,1,0:T(8,128)(2,1)} %get-tuple-element.25), channel_id=1, source_target_pairs={{0,2},{4,6},{8,10},{12,14},{2,0},{6,4},{10,8},{14,12},{1,3},{5,7},... | collective-permute-start | bytes 393224 | tf_op jit(solution)/shard_map/ppermute | solution.py:32
  75.1 9.7 %collective-permute-start.9 = (bf16[4,128,128]{2,1,0:T(8,128)(2,1)}, bf16[4,128,128]{2,1,0:T(8,128)(2,1)S(1)}, u32[]{:S(2)}, u32[]{:S(2)}) collective-permute-start(bf16[4,128,128]{2,1,0:T(8,128)(2,1)} %get-tuple-element.27), channel_id=1, source_target_pairs={{0,2},{4,6},{8,10},{12,14},{2,0},{6,4},{10,8},{14,12},{1,3},{5,7},... | collective-permute-start | bytes 393224 | tf_op jit(solution)/shard_map/ppermute | solution.py:32
  75.6 9.3 %collective-permute-start.14 = (bf16[4,128,128]{2,1,0:T(8,128)(2,1)S(1)}, bf16[4,128,128]{2,1,0:T(8,128)(2,1)S(1)}, u32[]{:S(2)}, u32[]{:S(2)}) collective-permute-start(bf16[4,128,128]{2,1,0:T(8,128)(2,1)S(1)} %get-tuple-element.29), channel_id=1, source_target_pairs={{0,2},{4,6},{8,10},{12,14},{2,0},{6,4},{10,8},{14,12},{1,3},{5,7},... | collective-permute-start | bytes 393224 | tf_op jit(solution)/shard_map/ppermute | solution.py:32
  84.8 0.6 copy-start.5
  84.8 0.7 copy-start.6
  84.9 0.7 copy-start.7
  84.9 0.7 copy-start.8

commit v24 on v22

--- a/solution.py
+++ b/solution.py
@@ -28,9 +28,9 @@
             links = [(2 * (hop - 1) + side, 2 * hop + side) for side in range(2)]
             carried = carried + lax.ppermute(carried + total, axis, links)
         keeps.append((carried + jnp.where(first, 0.0, got)).astype(jnp.bfloat16))
-        send = (carried + jnp.where(first, mine, 0.0)).astype(jnp.bfloat16)
-        backs.append(lax.ppermute(send, axis, swap))
-    return keeps, backs
+        backs.append((carried + jnp.where(first, mine, 0.0)).astype(jnp.bfloat16))
+    joined = [jnp.concatenate(backs[at:at + 2], axis=0) for at in range(0, len(backs), 2)]
+    return keeps, [lax.ppermute(send, axis, swap) for send in joined]
 
 
 def state_kernel(key_ref, val_ref, out_ref):

time: 93.7 us -> 92.2 us (0.984)
  starting transfers between devices: 17.7 us -> 15.8 us
    ppermute x4 -> x2, starting transfers between devices: 4.05 us -> 2.16 us  [pair_chain_prefix(): return (keeps, [lax.ppermute(send, axis, swap) for send in joined])]
  transfers between devices with their start and end apart: 21 -> 19, of which waited for: 8 -> 9; matrix products, arithmetic and copies ran while one was open for 7% -> 7% of each run, Pallas kernels for 7% -> 7%
where the time goes in v24:
time: 92.2 us; the launch traced here: 91.8 us
  waiting for transfers between devices  46.3 us (50%)
  Pallas kernels  18.7 us (20%)
  starting transfers between devices  15.8 us (17%)
  other arithmetic  8.87 us (10%)
  local copies, waits for them, and re-layouts  1.84 us (2%)
    ppermute x4, waiting for transfers between devices, pair_chain_prefix(): got = lax.ppermute(other_all[piece * step:(piece + 1) * step], axis, swap)  22.9 us
    ppermute x12, waiting for transfers between devices, pair_chain_prefix(): carried = carried + lax.ppermute(carried + total, axis, links)  22.8 us
    ppermute x12, starting transfers between devices, pair_chain_prefix(): carried = carried + lax.ppermute(carried + total, axis, links)  10.5 us
    pallas_call x1, Pallas kernels, attend_of(): pl.pallas_call(other_kernel, grid_spec=pltpu.PrefetchScalarGridSpec(num_s...  7.7 us
    pallas_call x1, Pallas kernels, attend_of(): pl.pallas_call(own_kernel, grid_spec=pltpu.PrefetchScalarGridSpec(num_sca...  6.55 us
    pallas_call x1, Pallas kernels, state_terms_of(): pl.pallas_call(state_kernel, grid=(H // group,), in_specs=[pl.BlockSpec((...  4.45 us
    add x8, other arithmetic, pair_chain_prefix(): carried = carried + lax.ppermute(carried + total, axis, links)  3.44 us
    ppermute x4, starting transfers between devices, pair_chain_prefix(): got = lax.ppermute(other_all[piece * step:(piece + 1) * step], axis, swap)  3.09 us
  transfers between devices with their start and end apart: 19, of which 9 were waited for; matrix products, arithmetic and copies ran while one was open for 7% of the time, Pallas kernels for 7%

profile of v24, /device:TPU:30, one launch (start us, length us, event | category | flops | bytes accessed | tf_op | source)
XLA Modules:
  0.0 91.8 jit_solution(16623258407910528607)
XLA Ops:
  0.0 4.4 %shard_map.46 = f32[32,128,128]{2,1,0:T(8,128)} custom-call(bf16[384,4096]{1,0:T(8,128)(2,1)} %bitcast.6, bf16[384,4096]{1,0:T(8,128)(2,1)} %bitcast.9), custom_call_target="tpu_custom_call" | custom-call | tf_op jit(solution)/shard_map/pallas_call | solution.py:49
  4.5 1.1 %constant_dynamic-slice_fusion = f32[4,128,128]{2,1,0:T(8,128)S(1)} fusion(f32[32,128,128]{2,1,0:T(8,128)} %shard_map.46, s32[]{:T(128)S(6)} %add.129), kind=kLoop, calls=%fused_computation.17 | loop fusion | bytes 524292 | tf_op jit(solution)/shard_map/slice | solution.py:24
  5.6 0.6 collective-permute-start.9
  6.1 7.5 %collective-permute-done.9 = f32[4,128,128]{2,1,0:T(8,128)S(1)} collective-permute-done((f32[4,128,128]{2,1,0:T(8,128)S(1)}, f32[4,128,128]{2,1,0:T(8,128)S(1)}, u32[]{:S(2)}, u32[]{:S(2)}) %collective-permute-start.9) | collective-permute-done | bytes 262176 | tf_op jit(solution)/shard_map/ppermute | solution.py:24
  13.7 2.2 %dynamic-slice_add_fusion.1 = (f32[4,128,128]{2,1,0:T(8,128)S(1)}, f32[4,128,128]{2,1,0:T(8,128)}, f32[4,128,128]{2,1,0:T(8,128)}, f32[4,128,128]{2,1,0:T(8,128)S(1)}) fusion(f32[4,128,128]{2,1,0:T(8,128)S(1)} %collective-permute-done.9, f32[32,128,128]{2,1,0:T(8,128)} %shard_map.46, s32[]{:T(128)S(6)} %add.128, s32[]{:T(128)S(6)} %add.127, ...), kind=kLoop, calls=%fused_computation.11 | loop fusion | flops 65536 | bytes 2359312 | tf_op jit(solution)/shard_map/add | solution.py:25
  15.9 0.5 collective-permute-start.4
  16.4 1.5 %collective-permute-start = (f32[4,128,128]{2,1,0:T(8,128)}, f32[4,128,128]{2,1,0:T(8,128)S(1)}, u32[]{:S(2)}, u32[]{:S(2)}) collective-permute-start(f32[4,128,128]{2,1,0:T(8,128)} %get-tuple-element.23), channel_id=1, source_target_pairs={{0,2},{4,6},{8,10},{12,14},{2,0},{6,4},{10,8},{14,12},{1,3},{5,7},... | collective-permute-start | bytes 786440 | tf_op jit(solution)/shard_map/ppermute | solution.py:24
  17.9 0.5 collective-permute-start.13
  18.4 0.7 collective-permute-start.10
  19.1 6.2 %collective-permute-done.4 = f32[4,128,128]{2,1,0:T(8,128)S(1)} collective-permute-done((f32[4,128,128]{2,1,0:T(8,128)}, f32[4,128,128]{2,1,0:T(8,128)S(1)}, u32[]{:S(2)}, u32[]{:S(2)}) %collective-permute-start.4) | collective-permute-done | bytes 262176 | tf_op jit(solution)/shard_map/ppermute | solution.py:24
  25.3 5.6 %collective-permute-done = f32[4,128,128]{2,1,0:T(8,128)S(1)} collective-permute-done((f32[4,128,128]{2,1,0:T(8,128)}, f32[4,128,128]{2,1,0:T(8,128)S(1)}, u32[]{:S(2)}, u32[]{:S(2)}) %collective-permute-start) | collective-permute-done | bytes 262176 | tf_op jit(solution)/shard_map/ppermute | solution.py:24
  30.9 3.5 %collective-permute-done.13 = f32[4,128,128]{2,1,0:T(8,128)S(1)} collective-permute-done((f32[4,128,128]{2,1,0:T(8,128)S(1)}, f32[4,128,128]{2,1,0:T(8,128)S(1)}, u32[]{:S(2)}, u32[]{:S(2)}) %collective-permute-start.13) | collective-permute-done | bytes 262176 | tf_op jit(solution)/shard_map/ppermute | solution.py:24
  34.5 0.1 dynamic-slice_add_fusion
  34.6 0.7 collective-permute-start.14
  35.2 0.7 collective-permute-start.5
  35.9 0.0 collective-permute-done.10
  36.0 0.7 collective-permute-start.11
  36.7 0.7 collective-permute-start.1
  37.4 0.7 collective-permute-start.15
  38.1 0.0 collective-permute-done.5
  38.1 0.0 copy-start.4
  38.2 0.7 collective-permute-start.6
  38.8 0.0 collective-permute-done.11
  38.9 0.8 fusion
  39.6 1.3 %collective-permute-start.12 = (f32[4,128,128]{2,1,0:T(8,128)}, f32[4,128,128]{2,1,0:T(8,128)}, u32[]{:S(2)}, u32[]{:S(2)}) collective-permute-start(f32[4,128,128]{2,1,0:T(8,128)} %get-tuple-element.9), channel_id=1, source_target_pairs={{8,12},{10,14},{9,13},{11,15},{24,28},{26,30},{25,29},{27,31}} | collective-permute-start | bytes 786440 | tf_op jit(solution)/shard_map/ppermute | solution.py:29
  40.9 0.0 collective-permute-done.1
  40.9 0.7 collective-permute-start.2
  41.6 0.8 fusion.1
  42.4 1.3 %collective-permute-start.16 = (f32[4,128,128]{2,1,0:T(8,128)}, f32[4,128,128]{2,1,0:T(8,128)}, u32[]{:S(2)}, u32[]{:S(2)}) collective-permute-start(f32[4,128,128]{2,1,0:T(8,128)} %get-tuple-element.11), channel_id=1, source_target_pairs={{8,12},{10,14},{9,13},{11,15},{24,28},{26,30},{25,29},{27,31}} | collective-permute-start | bytes 786440 | tf_op jit(solution)/shard_map/ppermute | solution.py:29
  43.7 0.9 fusion.3
  44.6 1.3 %collective-permute-start.7 = (f32[4,128,128]{2,1,0:T(8,128)}, f32[4,128,128]{2,1,0:T(8,128)}, u32[]{:S(2)}, u32[]{:S(2)}) collective-permute-start(f32[4,128,128]{2,1,0:T(8,128)} %get-tuple-element.15), channel_id=1, source_target_pairs={{8,12},{10,14},{9,13},{11,15},{24,28},{26,30},{25,29},{27,31}} | collective-permute-start | bytes 786440 | tf_op jit(solution)/shard_map/ppermute | solution.py:29
  45.9 0.9 fusion.2
  46.8 1.3 %collective-permute-start.3 = (f32[4,128,128]{2,1,0:T(8,128)}, f32[4,128,128]{2,1,0:T(8,128)}, u32[]{:S(2)}, u32[]{:S(2)}) collective-permute-start(f32[4,128,128]{2,1,0:T(8,128)} %get-tuple-element.13), channel_id=1, source_target_pairs={{8,12},{10,14},{9,13},{11,15},{24,28},{26,30},{25,29},{27,31}} | collective-permute-start | bytes 786440 | tf_op jit(solution)/shard_map/ppermute | solution.py:29
  48.1 0.1 collective-permute-start.18
  48.2 7.8 %collective-permute-done.12 = f32[4,128,128]{2,1,0:T(8,128)} collective-permute-done((f32[4,128,128]{2,1,0:T(8,128)}, f32[4,128,128]{2,1,0:T(8,128)}, u32[]{:S(2)}, u32[]{:S(2)}) %collective-permute-start.12) | collective-permute-done | bytes 262176 | tf_op jit(solution)/shard_map/ppermute | solution.py:29
  56.0 6.4 %collective-permute-done.16 = f32[4,128,128]{2,1,0:T(8,128)} collective-permute-done((f32[4,128,128]{2,1,0:T(8,128)}, f32[4,128,128]{2,1,0:T(8,128)}, u32[]{:S(2)}, u32[]{:S(2)}) %collective-permute-start.16) | collective-permute-done | bytes 262176 | tf_op jit(solution)/shard_map/ppermute | solution.py:29
  62.3 5.8 %collective-permute-done.7 = f32[4,128,128]{2,1,0:T(8,128)} collective-permute-done((f32[4,128,128]{2,1,0:T(8,128)}, f32[4,128,128]{2,1,0:T(8,128)}, u32[]{:S(2)}, u32[]{:S(2)}) %collective-permute-start.7) | collective-permute-done | bytes 262176 | tf_op jit(solution)/shard_map/ppermute | solution.py:29
  68.1 2.8 %collective-permute-done.3 = f32[4,128,128]{2,1,0:T(8,128)} collective-permute-done((f32[4,128,128]{2,1,0:T(8,128)}, f32[4,128,128]{2,1,0:T(8,128)}, u32[]{:S(2)}, u32[]{:S(2)}) %collective-permute-start.3) | collective-permute-done | bytes 262176 | tf_op jit(solution)/shard_map/ppermute | solution.py:29
  71.0 2.5 %add_convert_fusion.5 = (bf16[4,128,128]{2,1,0:T(8,128)(2,1)S(1)}, bf16[4,128,128]{2,1,0:T(8,128)(2,1)S(1)}, bf16[4,128,128]{2,1,0:T(8,128)(2,1)S(1)}, bf16[4,12...) fusion(f32[32,128,128]{2,1,0:T(8,128)S(1)} %copy-done, ...), kind=kLoop, calls=%fused_computation.7 | loop fusion | flops 1835008 | bytes 5242897 | tf_op jit(solution)/shard_map/convert_element_type | solution.py:31
  73.5 0.4 collective-permute-start.8
  73.9 1.8 %collective-permute-start.17 = (bf16[8,128,128]{2,1,0:T(8,128)(2,1)S(1)}, bf16[8,128,128]{2,1,0:T(8,128)(2,1)S(1)}, u32[]{:S(2)}, u32[]{:S(2)}) collective-permute-start(bf16[8,128,128]{2,1,0:T(8,128)(2,1)S(1)} %pad_maximum_fusion.1), channel_id=1, source_target_pairs={{0,2},{4,6},{8,10},{12,14},{2,0},{6,4},{10,8},{14,12},{1,3},{5,7},... | collective-permute-start | bytes 786440 | tf_op jit(solution)/shard_map/ppermute | solution.py:33
  75.7 0.0 collective-permute-done.18
  75.7 0.6 pad_maximum_fusion.2
  76.3 6.6 %shard_map.47 = (f32[384,2048]{1,0:T(8,128)}, f32[384,128]{1,0:T(8,128)}) custom-call(s32[1]{0:T(128)} %bitcast.mine_ref, bf16[384,4096]{1,0:T(8,128)(2,1)} %bitcast.12, bf16[384,4096]{1,0:T(8,128)(2,1)} %bitcast.7, bf16[384,4096]{1,0:T(8,128)(2,1)} %bitcast.10, bf16[4,128,128]{2,1,0:T(8,128)(2,1)} %get-tuple-element.30.refs_0_, ...), custom_call_target="tpu_custom_call" | custom-call | tf_op jit(solution)/shard_map/pallas_call | solution.py:159
  82.9 0.5 collective-permute-done.17.refs_1_
  83.4 0.2 copy-done.2
  83.5 0.5 copy-done.3
  84.1 7.7 %shard_map.48 = bf16[384,4096]{1,0:T(8,128)(2,1)} custom-call(s32[1]{0:T(128)} %bitcast.mine_ref, bf16[384,4096]{1,0:T(8,128)(2,1)} %bitcast.13, bf16[384,4096]{1,0:T(8,128)(2,1)} %bitcast.8, bf16[384,4096]{1,0:T(8,128)(2,1)} %bitcast.11, bf16[8,128,128]{2,1,0:T(8,128)(2,1)} %copy-done.2, bf16[8,128,128]{2,1,0:T(8,128)(2,1)} %copy-done.3, ...), custom_call_target="tpu_custom_call" | custom-call | tf_op jit(solution)/shard_map/pallas_call | solution.py:170
  (19 shorter events, 0.2 us)
Async XLA Ops:
  4.4 30.0 %copy-start = (f32[32,128,128]{2,1,0:T(8,128)S(1)}, f32[32,128,128]{2,1,0:T(8,128)}, u32[]{:S(2)}) copy-start(f32[32,128,128]{2,1,0:T(8,128)} %shard_map.46) | copy-start | bytes 6291460
  5.6 8.1 %collective-permute-start.9 = (f32[4,128,128]{2,1,0:T(8,128)S(1)}, f32[4,128,128]{2,1,0:T(8,128)S(1)}, u32[]{:S(2)}, u32[]{:S(2)}) collective-permute-start(f32[4,128,128]{2,1,0:T(8,128)S(1)} %constant_dynamic-slice_fusion), channel_id=1, source_target_pairs={{0,2},{4,6},{8,10},{12,14},{2,0},{6,4},{10,8},{14,12},{1,3},{5,7},... | collective-permute-start | bytes 786440 | tf_op jit(solution)/shard_map/ppermute | solution.py:24
  13.7 2.2 %copy-start.1 = (f32[4,128,128]{2,1,0:T(8,128)}, f32[4,128,128]{2,1,0:T(8,128)S(1)}, u32[]{:S(2)}) copy-start(f32[4,128,128]{2,1,0:T(8,128)S(1)} %collective-permute-done.9) | copy-start | bytes 786436
  15.9 9.5 %collective-permute-start.4 = (f32[4,128,128]{2,1,0:T(8,128)}, f32[4,128,128]{2,1,0:T(8,128)S(1)}, u32[]{:S(2)}, u32[]{:S(2)}) collective-permute-start(f32[4,128,128]{2,1,0:T(8,128)} %get-tuple-element.22), channel_id=1, source_target_pairs={{0,2},{4,6},{8,10},{12,14},{2,0},{6,4},{10,8},{14,12},{1,3},{5,7},... | collective-permute-start | bytes 786440 | tf_op jit(solution)/shard_map/ppermute | solution.py:24
  16.4 14.6 %collective-permute-start = (f32[4,128,128]{2,1,0:T(8,128)}, f32[4,128,128]{2,1,0:T(8,128)S(1)}, u32[]{:S(2)}, u32[]{:S(2)}) collective-permute-start(f32[4,128,128]{2,1,0:T(8,128)} %get-tuple-element.23), channel_id=1, source_target_pairs={{0,2},{4,6},{8,10},{12,14},{2,0},{6,4},{10,8},{14,12},{1,3},{5,7},... | collective-permute-start | bytes 786440 | tf_op jit(solution)/shard_map/ppermute | solution.py:24
  17.9 16.6 %collective-permute-start.13 = (f32[4,128,128]{2,1,0:T(8,128)S(1)}, f32[4,128,128]{2,1,0:T(8,128)S(1)}, u32[]{:S(2)}, u32[]{:S(2)}) collective-permute-start(f32[4,128,128]{2,1,0:T(8,128)S(1)} %get-tuple-element.24), channel_id=1, source_target_pairs={{0,2},{4,6},{8,10},{12,14},{2,0},{6,4},{10,8},{14,12},{1,3},{5,7},... | collective-permute-start | bytes 786440 | tf_op jit(solution)/shard_map/ppermute | solution.py:24
  18.4 17.5 %collective-permute-start.10 = (f32[4,128,128]{2,1,0:T(8,128)S(1)}, f32[4,128,128]{2,1,0:T(8,128)S(1)}, u32[]{:S(2)}, u32[]{:S(2)}) collective-permute-start(f32[4,128,128]{2,1,0:T(8,128)S(1)} %get-tuple-element.21), channel_id=1, source_target_pairs={{0,4},{2,6},{1,5},{3,7},{16,20},{18,22},{17,21},{19,23}} | collective-permute-start | bytes 786440 | tf_op jit(solution)/shard_map/ppermute | solution.py:29
  34.6 2.8 %collective-permute-start.14 = (f32[4,128,128]{2,1,0:T(8,128)S(1)}, f32[4,128,128]{2,1,0:T(8,128)S(1)}, u32[]{:S(2)}, u32[]{:S(2)}) collective-permute-start(f32[4,128,128]{2,1,0:T(8,128)S(1)} %get-tuple-element.25), channel_id=1, source_target_pairs={{0,4},{2,6},{1,5},{3,7},{16,20},{18,22},{17,21},{19,23}} | collective-permute-start | bytes 786440 | tf_op jit(solution)/shard_map/ppermute | solution.py:29
  35.2 2.8 %collective-permute-start.5 = (f32[4,128,128]{2,1,0:T(8,128)S(1)}, f32[4,128,128]{2,1,0:T(8,128)S(1)}, u32[]{:S(2)}, u32[]{:S(2)}) collective-permute-start(f32[4,128,128]{2,1,0:T(8,128)S(1)} %get-tuple-element.26), channel_id=1, source_target_pairs={{0,4},{2,6},{1,5},{3,7},{16,20},{18,22},{17,21},{19,23}} | collective-permute-start | bytes 786440 | tf_op jit(solution)/shard_map/ppermute | solution.py:29
  36.0 2.9 %collective-permute-start.11 = (f32[4,128,128]{2,1,0:T(8,128)S(1)}, f32[4,128,128]{2,1,0:T(8,128)S(1)}, u32[]{:S(2)}, u32[]{:S(2)}) collective-permute-start(f32[4,128,128]{2,1,0:T(8,128)S(1)} %add.111), channel_id=1, source_target_pairs={{4,8},{6,10},{5,9},{7,11},{20,24},{22,26},{21,25},{23,27}} | collective-permute-start | bytes 786440 | tf_op jit(solution)/shard_map/ppermute | solution.py:29
  36.7 4.2 %collective-permute-start.1 = (f32[4,128,128]{2,1,0:T(8,128)S(1)}, f32[4,128,128]{2,1,0:T(8,128)S(1)}, u32[]{:S(2)}, u32[]{:S(2)}) collective-permute-start(f32[4,128,128]{2,1,0:T(8,128)S(1)} %get-tuple-element.27), channel_id=1, source_target_pairs={{0,4},{2,6},{1,5},{3,7},{16,20},{18,22},{17,21},{19,23}} | collective-permute-start | bytes 786440 | tf_op jit(solution)/shard_map/ppermute | solution.py:29
  37.4 4.2 %collective-permute-start.15 = (f32[4,128,128]{2,1,0:T(8,128)S(1)}, f32[4,128,128]{2,1,0:T(8,128)S(1)}, u32[]{:S(2)}, u32[]{:S(2)}) collective-permute-start(f32[4,128,128]{2,1,0:T(8,128)S(1)} %add.117), channel_id=1, source_target_pairs={{4,8},{6,10},{5,9},{7,11},{20,24},{22,26},{21,25},{23,27}} | collective-permute-start | bytes 786440 | tf_op jit(solution)/shard_map/ppermute | solution.py:29
  38.1 9.9 %copy-start.4 = (f32[2048]{0:T(1024)S(1)}, f32[2048]{0:T(1024)}, u32[]{:S(2)}) copy-start(f32[2048]{0:T(1024)} %param.7) | copy-start | bytes 24580
  38.2 5.5 %collective-permute-start.6 = (f32[4,128,128]{2,1,0:T(8,128)S(1)}, f32[4,128,128]{2,1,0:T(8,128)S(1)}, u32[]{:S(2)}, u32[]{:S(2)}) collective-permute-start(f32[4,128,128]{2,1,0:T(8,128)S(1)} %add.105), channel_id=1, source_target_pairs={{4,8},{6,10},{5,9},{7,11},{20,24},{22,26},{21,25},{23,27}} | collective-permute-start | bytes 786440 | tf_op jit(solution)/shard_map/ppermute | solution.py:29
  39.6 16.4 %collective-permute-start.12 = (f32[4,128,128]{2,1,0:T(8,128)}, f32[4,128,128]{2,1,0:T(8,128)}, u32[]{:S(2)}, u32[]{:S(2)}) collective-permute-start(f32[4,128,128]{2,1,0:T(8,128)} %get-tuple-element.9), channel_id=1, source_target_pairs={{8,12},{10,14},{9,13},{11,15},{24,28},{26,30},{25,29},{27,31}} | collective-permute-start | bytes 786440 | tf_op jit(solution)/shard_map/ppermute | solution.py:29
  40.9 4.9 %collective-permute-start.2 = (f32[4,128,128]{2,1,0:T(8,128)S(1)}, f32[4,128,128]{2,1,0:T(8,128)S(1)}, u32[]{:S(2)}, u32[]{:S(2)}) collective-permute-start(f32[4,128,128]{2,1,0:T(8,128)S(1)} %add.99), channel_id=1, source_target_pairs={{4,8},{6,10},{5,9},{7,11},{20,24},{22,26},{21,25},{23,27}} | collective-permute-start | bytes 786440 | tf_op jit(solution)/shard_map/ppermute | solution.py:29
  42.4 19.9 %collective-permute-start.16 = (f32[4,128,128]{2,1,0:T(8,128)}, f32[4,128,128]{2,1,0:T(8,128)}, u32[]{:S(2)}, u32[]{:S(2)}) collective-permute-start(f32[4,128,128]{2,1,0:T(8,128)} %get-tuple-element.11), channel_id=1, source_target_pairs={{8,12},{10,14},{9,13},{11,15},{24,28},{26,30},{25,29},{27,31}} | collective-permute-start | bytes 786440 | tf_op jit(solution)/shard_map/ppermute | solution.py:29
  44.6 23.6 %collective-permute-start.7 = (f32[4,128,128]{2,1,0:T(8,128)}, f32[4,128,128]{2,1,0:T(8,128)}, u32[]{:S(2)}, u32[]{:S(2)}) collective-permute-start(f32[4,128,128]{2,1,0:T(8,128)} %get-tuple-element.15), channel_id=1, source_target_pairs={{8,12},{10,14},{9,13},{11,15},{24,28},{26,30},{25,29},{27,31}} | collective-permute-start | bytes 786440 | tf_op jit(solution)/shard_map/ppermute | solution.py:29
  46.8 24.2 %collective-permute-start.3 = (f32[4,128,128]{2,1,0:T(8,128)}, f32[4,128,128]{2,1,0:T(8,128)}, u32[]{:S(2)}, u32[]{:S(2)}) collective-permute-start(f32[4,128,128]{2,1,0:T(8,128)} %get-tuple-element.13), channel_id=1, source_target_pairs={{8,12},{10,14},{9,13},{11,15},{24,28},{26,30},{25,29},{27,31}} | collective-permute-start | bytes 786440 | tf_op jit(solution)/shard_map/ppermute | solution.py:29
  48.1 27.6 %collective-permute-start.18 = (f32[2048]{0:T(1024)S(1)}, f32[2048]{0:T(1024)S(1)}, u32[]{:S(2)}, u32[]{:S(2)}) collective-permute-start(f32[2048]{0:T(1024)S(1)} %copy-done.4), channel_id=1, source_target_pairs={{0,1},{1,0},{2,3},{3,2},{4,5},{5,4},{6,7},{7,6},{8,9},{9,8},{10,11... | collective-permute-start | bytes 24584 | tf_op jit(solution)/shard_map/ppermute | solution.py:195
  73.5 9.3 %collective-permute-start.8 = (bf16[8,128,128]{2,1,0:T(8,128)(2,1)S(1)}, bf16[8,128,128]{2,1,0:T(8,128)(2,1)S(1)}, u32[]{:S(2)}, u32[]{:S(2)}) collective-permute-start(bf16[8,128,128]{2,1,0:T(8,128)(2,1)S(1)} %pad_maximum_fusion), channel_id=1, source_target_pairs={{0,2},{4,6},{8,10},{12,14},{2,0},{6,4},{10,8},{14,12},{1,3},{5,7},... | collective-permute-start | bytes 786440 | tf_op jit(solution)/shard_map/ppermute | solution.py:33
  73.9 9.5 %collective-permute-start.17 = (bf16[8,128,128]{2,1,0:T(8,128)(2,1)S(1)}, bf16[8,128,128]{2,1,0:T(8,128)(2,1)S(1)}, u32[]{:S(2)}, u32[]{:S(2)}) collective-permute-start(bf16[8,128,128]{2,1,0:T(8,128)(2,1)S(1)} %pad_maximum_fusion.1), channel_id=1, source_target_pairs={{0,2},{4,6},{8,10},{12,14},{2,0},{6,4},{10,8},{14,12},{1,3},{5,7},... | collective-permute-start | bytes 786440 | tf_op jit(solution)/shard_map/ppermute | solution.py:33
  82.9 0.7 copy-start.2
  83.4 0.7 copy-start.3

commit v25 on v24

--- a/solution.py
+++ b/solution.py
@@ -29,7 +29,7 @@
             carried = carried + lax.ppermute(carried + total, axis, links)
         keeps.append((carried + jnp.where(first, 0.0, got)).astype(jnp.bfloat16))
         backs.append((carried + jnp.where(first, mine, 0.0)).astype(jnp.bfloat16))
-    joined = [jnp.concatenate(backs[at:at + 2], axis=0) for at in range(0, len(backs), 2)]
+    joined = [jnp.concatenate(backs, axis=0)]
     return keeps, [lax.ppermute(send, axis, swap) for send in joined]
 
 
@@ -81,6 +81,8 @@
     per_step = heads // per_piece
 
     def prefix_of(head):
+        if len(refs) == 1:
+            return refs[0][step * heads + head]
         pick = refs[head // per_piece][head % per_piece]
         for g in range(1, pl.num_programs(0)):
             pick = jnp.where(step == g, refs[g * per_step + head // per_piece][head % per_piece], pick)

time: 92.2 us -> 92.6 us (level)
  waiting for transfers between devices: 46.3 us -> 48.3 us
  starting transfers between devices: 15.8 us -> 14 us
    ppermute x2 -> x1, starting transfers between devices: 2.16 us -> 0.39 us  [pair_chain_prefix(): return (keeps, [lax.ppermute(send, axis, swap) for send in joined])]
    ppermute x1, waiting for transfers between devices: 0.01 us -> 1.17 us  [shards(): other_gain = lax.ppermute(gain, 'dp', pair)]
  transfers between devices with their start and end apart: 19 -> 18, of which waited for: 9 -> 10; matrix products, arithmetic and copies ran while one was open for 7% -> 4% of each run, Pallas kernels for 7% -> 7%
where the time goes in v25:
time: 92.6 us; the launch traced here: 92 us
  waiting for transfers between devices  48.3 us (52%)
  Pallas kernels  18.7 us (20%)
  starting transfers between devices  14 us (15%)
  other arithmetic  8.91 us (10%)
  local copies, waits for them, and re-layouts  1.94 us (2%)
    ppermute x4, waiting for transfers between devices, pair_chain_prefix(): got = lax.ppermute(other_all[piece * step:(piece + 1) * step], axis, swap)  22.9 us
    ppermute x12, waiting for transfers between devices, pair_chain_prefix(): carried = carried + lax.ppermute(carried + total, axis, links)  22.9 us
    ppermute x12, starting transfers between devices, pair_chain_prefix(): carried = carried + lax.ppermute(carried + total, axis, links)  10.5 us
    pallas_call x1, Pallas kernels, attend_of(): pl.pallas_call(other_kernel, grid_spec=pltpu.PrefetchScalarGridSpec(num_s...  7.72 us
    pallas_call x1, Pallas kernels, attend_of(): pl.pallas_call(own_kernel, grid_spec=pltpu.PrefetchScalarGridSpec(num_sca...  6.5 us
    pallas_call x1, Pallas kernels, state_terms_of(): pl.pallas_call(state_kernel, grid=(H // group,), in_specs=[pl.BlockSpec((...  4.45 us
    add x8, other arithmetic, pair_chain_prefix(): carried = carried + lax.ppermute(carried + total, axis, links)  3.45 us
    ppermute x4, starting transfers between devices, pair_chain_prefix(): got = lax.ppermute(other_all[piece * step:(piece + 1) * step], axis, swap)  3.09 us
  transfers between devices with their start and end apart: 18, of which 10 were waited for; matrix products, arithmetic and copies ran while one was open for 4% of the time, Pallas kernels for 7%

profile of v25, /device:TPU:30, one launch (start us, length us, event | category | flops | bytes accessed | tf_op | source)
XLA Modules:
  0.0 92.0 jit_solution(5967775962132305307)
XLA Ops:
  0.0 4.4 %shard_map.46 = f32[32,128,128]{2,1,0:T(8,128)} custom-call(bf16[384,4096]{1,0:T(8,128)(2,1)} %bitcast.6, bf16[384,4096]{1,0:T(8,128)(2,1)} %bitcast.9), custom_call_target="tpu_custom_call" | custom-call | tf_op jit(solution)/shard_map/pallas_call | solution.py:49
  4.5 1.1 %constant_dynamic-slice_fusion.2 = f32[4,128,128]{2,1,0:T(8,128)S(1)} fusion(f32[32,128,128]{2,1,0:T(8,128)} %shard_map.46, s32[]{:T(128)S(6)} %select_n.67), kind=kLoop, calls=%fused_computation.18 | loop fusion | bytes 524292 | tf_op jit(solution)/shard_map/slice | solution.py:24
  5.6 0.6 collective-permute-start
  6.1 7.5 %collective-permute-done = f32[4,128,128]{2,1,0:T(8,128)S(1)} collective-permute-done((f32[4,128,128]{2,1,0:T(8,128)S(1)}, f32[4,128,128]{2,1,0:T(8,128)S(1)}, u32[]{:S(2)}, u32[]{:S(2)}) %collective-permute-start) | collective-permute-done | bytes 262176 | tf_op jit(solution)/shard_map/ppermute | solution.py:24
  13.7 2.2 %dynamic-slice_add_fusion.3 = (f32[4,128,128]{2,1,0:T(8,128)S(1)}, f32[4,128,128]{2,1,0:T(8,128)}, f32[4,128,128]{2,1,0:T(8,128)}, f32[4,128,128]{2,1,0:T(8,128)S(1)}) fusion(f32[4,128,128]{2,1,0:T(8,128)S(1)} %collective-permute-done, f32[32,128,128]{2,1,0:T(8,128)} %shard_map.46, s32[]{:T(128)S(6)} %select_n.66, s32[]{:T(128)S(6)} %add.129, s32[]{:T(128)S(6)} %add.127, ...), kind=kLoop, calls=%fused_computation.12 | loop fusion | flops 65536 | bytes 2359312 | tf_op jit(solution)/shard_map/add | solution.py:25
  15.9 0.5 collective-permute-start.8
  16.4 1.5 %collective-permute-start.4 = (f32[4,128,128]{2,1,0:T(8,128)}, f32[4,128,128]{2,1,0:T(8,128)S(1)}, u32[]{:S(2)}, u32[]{:S(2)}) collective-permute-start(f32[4,128,128]{2,1,0:T(8,128)} %get-tuple-element.23), channel_id=1, source_target_pairs={{0,2},{4,6},{8,10},{12,14},{2,0},{6,4},{10,8},{14,12},{1,3},{5,7},... | collective-permute-start | bytes 786440 | tf_op jit(solution)/shard_map/ppermute | solution.py:24
  17.9 0.5 collective-permute-start.12
  18.4 0.7 collective-permute-start.1
  19.1 6.2 %collective-permute-done.8 = f32[4,128,128]{2,1,0:T(8,128)S(1)} collective-permute-done((f32[4,128,128]{2,1,0:T(8,128)}, f32[4,128,128]{2,1,0:T(8,128)S(1)}, u32[]{:S(2)}, u32[]{:S(2)}) %collective-permute-start.8) | collective-permute-done | bytes 262176 | tf_op jit(solution)/shard_map/ppermute | solution.py:24
  25.3 5.6 %collective-permute-done.4 = f32[4,128,128]{2,1,0:T(8,128)S(1)} collective-permute-done((f32[4,128,128]{2,1,0:T(8,128)}, f32[4,128,128]{2,1,0:T(8,128)S(1)}, u32[]{:S(2)}, u32[]{:S(2)}) %collective-permute-start.4) | collective-permute-done | bytes 262176 | tf_op jit(solution)/shard_map/ppermute | solution.py:24
  30.9 3.5 %collective-permute-done.12 = f32[4,128,128]{2,1,0:T(8,128)S(1)} collective-permute-done((f32[4,128,128]{2,1,0:T(8,128)S(1)}, f32[4,128,128]{2,1,0:T(8,128)S(1)}, u32[]{:S(2)}, u32[]{:S(2)}) %collective-permute-start.12) | collective-permute-done | bytes 262176 | tf_op jit(solution)/shard_map/ppermute | solution.py:24
  34.5 0.1 dynamic-slice_add_fusion.2
  34.6 0.7 collective-permute-start.5
  35.3 0.7 collective-permute-start.9
  35.9 0.0 collective-permute-done.1
  36.0 0.7 collective-permute-start.2
  36.7 0.7 collective-permute-start.13
  37.4 0.0 collective-permute-done.5
  37.4 0.7 collective-permute-start.6
  38.1 0.0 collective-permute-done.9
  38.1 0.7 collective-permute-start.10
  38.8 0.0 collective-permute-done.2
  38.8 0.8 fusion
  39.6 1.3 %collective-permute-start.3 = (f32[4,128,128]{2,1,0:T(8,128)}, f32[4,128,128]{2,1,0:T(8,128)}, u32[]{:S(2)}, u32[]{:S(2)}) collective-permute-start(f32[4,128,128]{2,1,0:T(8,128)} %get-tuple-element.9), channel_id=1, source_target_pairs={{8,12},{10,14},{9,13},{11,15},{24,28},{26,30},{25,29},{27,31}} | collective-permute-start | bytes 786440 | tf_op jit(solution)/shard_map/ppermute | solution.py:29
  40.9 0.0 collective-permute-done.13
  40.9 0.7 collective-permute-start.14
  41.6 0.8 fusion.1
  42.4 1.3 %collective-permute-start.7 = (f32[4,128,128]{2,1,0:T(8,128)}, f32[4,128,128]{2,1,0:T(8,128)}, u32[]{:S(2)}, u32[]{:S(2)}) collective-permute-start(f32[4,128,128]{2,1,0:T(8,128)} %get-tuple-element.11), channel_id=1, source_target_pairs={{8,12},{10,14},{9,13},{11,15},{24,28},{26,30},{25,29},{27,31}} | collective-permute-start | bytes 786440 | tf_op jit(solution)/shard_map/ppermute | solution.py:29
  43.7 0.0 collective-permute-done.10
  43.7 0.9 fusion.2
  44.6 1.3 %collective-permute-start.11 = (f32[4,128,128]{2,1,0:T(8,128)}, f32[4,128,128]{2,1,0:T(8,128)}, u32[]{:S(2)}, u32[]{:S(2)}) collective-permute-start(f32[4,128,128]{2,1,0:T(8,128)} %get-tuple-element.13), channel_id=1, source_target_pairs={{8,12},{10,14},{9,13},{11,15},{24,28},{26,30},{25,29},{27,31}} | collective-permute-start | bytes 786440 | tf_op jit(solution)/shard_map/ppermute | solution.py:29
  45.9 0.9 fusion.3
  46.8 1.3 %collective-permute-start.15 = (f32[4,128,128]{2,1,0:T(8,128)}, f32[4,128,128]{2,1,0:T(8,128)}, u32[]{:S(2)}, u32[]{:S(2)}) collective-permute-start(f32[4,128,128]{2,1,0:T(8,128)} %get-tuple-element.15), channel_id=1, source_target_pairs={{8,12},{10,14},{9,13},{11,15},{24,28},{26,30},{25,29},{27,31}} | collective-permute-start | bytes 786440 | tf_op jit(solution)/shard_map/ppermute | solution.py:29
  48.1 7.9 %collective-permute-done.3 = f32[4,128,128]{2,1,0:T(8,128)} collective-permute-done((f32[4,128,128]{2,1,0:T(8,128)}, f32[4,128,128]{2,1,0:T(8,128)}, u32[]{:S(2)}, u32[]{:S(2)}) %collective-permute-start.3) | collective-permute-done | bytes 262176 | tf_op jit(solution)/shard_map/ppermute | solution.py:29
  56.0 6.3 %collective-permute-done.7 = f32[4,128,128]{2,1,0:T(8,128)} collective-permute-done((f32[4,128,128]{2,1,0:T(8,128)}, f32[4,128,128]{2,1,0:T(8,128)}, u32[]{:S(2)}, u32[]{:S(2)}) %collective-permute-start.7) | collective-permute-done | bytes 262176 | tf_op jit(solution)/shard_map/ppermute | solution.py:29
  62.3 5.9 %collective-permute-done.11 = f32[4,128,128]{2,1,0:T(8,128)} collective-permute-done((f32[4,128,128]{2,1,0:T(8,128)}, f32[4,128,128]{2,1,0:T(8,128)}, u32[]{:S(2)}, u32[]{:S(2)}) %collective-permute-start.11) | collective-permute-done | bytes 262176 | tf_op jit(solution)/shard_map/ppermute | solution.py:29
  68.2 2.8 %collective-permute-done.15 = f32[4,128,128]{2,1,0:T(8,128)} collective-permute-done((f32[4,128,128]{2,1,0:T(8,128)}, f32[4,128,128]{2,1,0:T(8,128)}, u32[]{:S(2)}, u32[]{:S(2)}) %collective-permute-start.15) | collective-permute-done | bytes 262176 | tf_op jit(solution)/shard_map/ppermute | solution.py:29
  71.0 2.5 %add_convert_fusion.7 = (bf16[4,128,128]{2,1,0:T(8,128)(2,1)S(1)}, bf16[4,128,128]{2,1,0:T(8,128)(2,1)S(1)}, bf16[4,128,128]{2,1,0:T(8,128)(2,1)S(1)}, bf16[4,12...) fusion(f32[32,128,128]{2,1,0:T(8,128)S(1)} %copy-done, ...), kind=kLoop, calls=%fused_computation.8 | loop fusion | flops 1835008 | bytes 5242897 | tf_op jit(solution)/shard_map/convert_element_type | solution.py:31
  73.5 0.1 pad_maximum_fusion
  73.6 0.4 collective-permute-start.16
  74.0 0.0 collective-permute-start.17
  74.0 1.2 %collective-permute-done.17 = f32[2048]{0:T(1024)S(1)} collective-permute-done((f32[2048]{0:T(1024)S(1)}, f32[2048]{0:T(1024)S(1)}, u32[]{:S(2)}, u32[]{:S(2)}) %collective-permute-start.17) | collective-permute-done | bytes 8224 | tf_op jit(solution)/shard_map/ppermute | solution.py:197
  75.1 0.6 pad_maximum_fusion.1
  75.7 6.5 %shard_map.47 = (f32[384,2048]{1,0:T(8,128)}, f32[384,128]{1,0:T(8,128)}) custom-call(s32[1]{0:T(128)} %bitcast.mine_ref, bf16[384,4096]{1,0:T(8,128)(2,1)} %bitcast.12, bf16[384,4096]{1,0:T(8,128)(2,1)} %bitcast.7, bf16[384,4096]{1,0:T(8,128)(2,1)} %bitcast.10, bf16[4,128,128]{2,1,0:T(8,128)(2,1)} %get-tuple-element.31.refs_0_, ...), custom_call_target="tpu_custom_call" | custom-call | tf_op jit(solution)/shard_map/pallas_call | solution.py:161
  82.2 1.2 %collective-permute-done.16.refs_0_ = bf16[16,128,128]{2,1,0:T(8,128)(2,1)S(1)} collective-permute-done((bf16[16,128,128]{2,1,0:T(8,128)(2,1)S(1)}, bf16[16,128,128]{2,1,0:T(8,128)(2,1)S(1)}, u32[]{:S(2)}, u32[]{:S(2)}) %collective-permute-start.16) | collective-permute-done | bytes 524320 | tf_op jit(solution)/shard_map/ppermute | solution.py:33
  83.5 0.8 copy-done.2
  84.3 7.7 %shard_map.48 = bf16[384,4096]{1,0:T(8,128)(2,1)} custom-call(s32[1]{0:T(128)} %bitcast.mine_ref, bf16[384,4096]{1,0:T(8,128)(2,1)} %bitcast.13, bf16[384,4096]{1,0:T(8,128)(2,1)} %bitcast.8, bf16[384,4096]{1,0:T(8,128)(2,1)} %bitcast.11, bf16[16,128,128]{2,1,0:T(8,128)(2,1)} %copy-done.2, f32[384,2048]{1,0:T(8,128)} %get-tuple-element.7.refs_1_, ...), custom_call_target="tpu_custom_call" | custom-call | tf_op jit(solution)/shard_map/pallas_call | solution.py:172
  (14 shorter events, 0.2 us)
Async XLA Ops:
  4.4 30.0 %copy-start = (f32[32,128,128]{2,1,0:T(8,128)S(1)}, f32[32,128,128]{2,1,0:T(8,128)}, u32[]{:S(2)}) copy-start(f32[32,128,128]{2,1,0:T(8,128)} %shard_map.46) | copy-start | bytes 6291460
  5.6 8.1 %collective-permute-start = (f32[4,128,128]{2,1,0:T(8,128)S(1)}, f32[4,128,128]{2,1,0:T(8,128)S(1)}, u32[]{:S(2)}, u32[]{:S(2)}) collective-permute-start(f32[4,128,128]{2,1,0:T(8,128)S(1)} %constant_dynamic-slice_fusion.2), channel_id=1, source_target_pairs={{0,2},{4,6},{8,10},{12,14},{2,0},{6,4},{10,8},{14,12},{1,3},{5,7},... | collective-permute-start | bytes 786440 | tf_op jit(solution)/shard_map/ppermute | solution.py:24
  13.7 2.2 %copy-start.1 = (f32[4,128,128]{2,1,0:T(8,128)}, f32[4,128,128]{2,1,0:T(8,128)S(1)}, u32[]{:S(2)}) copy-start(f32[4,128,128]{2,1,0:T(8,128)S(1)} %collective-permute-done) | copy-start | bytes 786436
  15.9 9.5 %collective-permute-start.8 = (f32[4,128,128]{2,1,0:T(8,128)}, f32[4,128,128]{2,1,0:T(8,128)S(1)}, u32[]{:S(2)}, u32[]{:S(2)}) collective-permute-start(f32[4,128,128]{2,1,0:T(8,128)} %get-tuple-element.22), channel_id=1, source_target_pairs={{0,2},{4,6},{8,10},{12,14},{2,0},{6,4},{10,8},{14,12},{1,3},{5,7},... | collective-permute-start | bytes 786440 | tf_op jit(solution)/shard_map/ppermute | solution.py:24
  16.4 14.6 %collective-permute-start.4 = (f32[4,128,128]{2,1,0:T(8,128)}, f32[4,128,128]{2,1,0:T(8,128)S(1)}, u32[]{:S(2)}, u32[]{:S(2)}) collective-permute-start(f32[4,128,128]{2,1,0:T(8,128)} %get-tuple-element.23), channel_id=1, source_target_pairs={{0,2},{4,6},{8,10},{12,14},{2,0},{6,4},{10,8},{14,12},{1,3},{5,7},... | collective-permute-start | bytes 786440 | tf_op jit(solution)/shard_map/ppermute | solution.py:24
  17.9 16.6 %collective-permute-start.12 = (f32[4,128,128]{2,1,0:T(8,128)S(1)}, f32[4,128,128]{2,1,0:T(8,128)S(1)}, u32[]{:S(2)}, u32[]{:S(2)}) collective-permute-start(f32[4,128,128]{2,1,0:T(8,128)S(1)} %get-tuple-element.24), channel_id=1, source_target_pairs={{0,2},{4,6},{8,10},{12,14},{2,0},{6,4},{10,8},{14,12},{1,3},{5,7},... | collective-permute-start | bytes 786440 | tf_op jit(solution)/shard_map/ppermute | solution.py:24
  18.4 17.5 %collective-permute-start.1 = (f32[4,128,128]{2,1,0:T(8,128)S(1)}, f32[4,128,128]{2,1,0:T(8,128)S(1)}, u32[]{:S(2)}, u32[]{:S(2)}) collective-permute-start(f32[4,128,128]{2,1,0:T(8,128)S(1)} %get-tuple-element.21), channel_id=1, source_target_pairs={{0,4},{2,6},{1,5},{3,7},{16,20},{18,22},{17,21},{19,23}} | collective-permute-start | bytes 786440 | tf_op jit(solution)/shard_map/ppermute | solution.py:29
  34.6 2.8 %collective-permute-start.5 = (f32[4,128,128]{2,1,0:T(8,128)S(1)}, f32[4,128,128]{2,1,0:T(8,128)S(1)}, u32[]{:S(2)}, u32[]{:S(2)}) collective-permute-start(f32[4,128,128]{2,1,0:T(8,128)S(1)} %get-tuple-element.25), channel_id=1, source_target_pairs={{0,4},{2,6},{1,5},{3,7},{16,20},{18,22},{17,21},{19,23}} | collective-permute-start | bytes 786440 | tf_op jit(solution)/shard_map/ppermute | solution.py:29
  35.3 2.8 %collective-permute-start.9 = (f32[4,128,128]{2,1,0:T(8,128)S(1)}, f32[4,128,128]{2,1,0:T(8,128)S(1)}, u32[]{:S(2)}, u32[]{:S(2)}) collective-permute-start(f32[4,128,128]{2,1,0:T(8,128)S(1)} %get-tuple-element.26), channel_id=1, source_target_pairs={{0,4},{2,6},{1,5},{3,7},{16,20},{18,22},{17,21},{19,23}} | collective-permute-start | bytes 786440 | tf_op jit(solution)/shard_map/ppermute | solution.py:29
  36.0 2.8 %collective-permute-start.2 = (f32[4,128,128]{2,1,0:T(8,128)S(1)}, f32[4,128,128]{2,1,0:T(8,128)S(1)}, u32[]{:S(2)}, u32[]{:S(2)}) collective-permute-start(f32[4,128,128]{2,1,0:T(8,128)S(1)} %add.99), channel_id=1, source_target_pairs={{4,8},{6,10},{5,9},{7,11},{20,24},{22,26},{21,25},{23,27}} | collective-permute-start | bytes 786440 | tf_op jit(solution)/shard_map/ppermute | solution.py:29
  36.7 4.2 %collective-permute-start.13 = (f32[4,128,128]{2,1,0:T(8,128)S(1)}, f32[4,128,128]{2,1,0:T(8,128)S(1)}, u32[]{:S(2)}, u32[]{:S(2)}) collective-permute-start(f32[4,128,128]{2,1,0:T(8,128)S(1)} %get-tuple-element.27), channel_id=1, source_target_pairs={{0,4},{2,6},{1,5},{3,7},{16,20},{18,22},{17,21},{19,23}} | collective-permute-start | bytes 786440 | tf_op jit(solution)/shard_map/ppermute | solution.py:29
  37.4 4.2 %collective-permute-start.6 = (f32[4,128,128]{2,1,0:T(8,128)S(1)}, f32[4,128,128]{2,1,0:T(8,128)S(1)}, u32[]{:S(2)}, u32[]{:S(2)}) collective-permute-start(f32[4,128,128]{2,1,0:T(8,128)S(1)} %add.105), channel_id=1, source_target_pairs={{4,8},{6,10},{5,9},{7,11},{20,24},{22,26},{21,25},{23,27}} | collective-permute-start | bytes 786440 | tf_op jit(solution)/shard_map/ppermute | solution.py:29
  38.1 5.5 %collective-permute-start.10 = (f32[4,128,128]{2,1,0:T(8,128)S(1)}, f32[4,128,128]{2,1,0:T(8,128)S(1)}, u32[]{:S(2)}, u32[]{:S(2)}) collective-permute-start(f32[4,128,128]{2,1,0:T(8,128)S(1)} %add.111), channel_id=1, source_target_pairs={{4,8},{6,10},{5,9},{7,11},{20,24},{22,26},{21,25},{23,27}} | collective-permute-start | bytes 786440 | tf_op jit(solution)/shard_map/ppermute | solution.py:29
  39.6 16.4 %collective-permute-start.3 = (f32[4,128,128]{2,1,0:T(8,128)}, f32[4,128,128]{2,1,0:T(8,128)}, u32[]{:S(2)}, u32[]{:S(2)}) collective-permute-start(f32[4,128,128]{2,1,0:T(8,128)} %get-tuple-element.9), channel_id=1, source_target_pairs={{8,12},{10,14},{9,13},{11,15},{24,28},{26,30},{25,29},{27,31}} | collective-permute-start | bytes 786440 | tf_op jit(solution)/shard_map/ppermute | solution.py:29
  40.9 4.9 %collective-permute-start.14 = (f32[4,128,128]{2,1,0:T(8,128)S(1)}, f32[4,128,128]{2,1,0:T(8,128)S(1)}, u32[]{:S(2)}, u32[]{:S(2)}) collective-permute-start(f32[4,128,128]{2,1,0:T(8,128)S(1)} %add.117), channel_id=1, source_target_pairs={{4,8},{6,10},{5,9},{7,11},{20,24},{22,26},{21,25},{23,27}} | collective-permute-start | bytes 786440 | tf_op jit(solution)/shard_map/ppermute | solution.py:29
  42.4 19.9 %collective-permute-start.7 = (f32[4,128,128]{2,1,0:T(8,128)}, f32[4,128,128]{2,1,0:T(8,128)}, u32[]{:S(2)}, u32[]{:S(2)}) collective-permute-start(f32[4,128,128]{2,1,0:T(8,128)} %get-tuple-element.11), channel_id=1, source_target_pairs={{8,12},{10,14},{9,13},{11,15},{24,28},{26,30},{25,29},{27,31}} | collective-permute-start | bytes 786440 | tf_op jit(solution)/shard_map/ppermute | solution.py:29
  44.6 23.6 %collective-permute-start.11 = (f32[4,128,128]{2,1,0:T(8,128)}, f32[4,128,128]{2,1,0:T(8,128)}, u32[]{:S(2)}, u32[]{:S(2)}) collective-permute-start(f32[4,128,128]{2,1,0:T(8,128)} %get-tuple-element.13), channel_id=1, source_target_pairs={{8,12},{10,14},{9,13},{11,15},{24,28},{26,30},{25,29},{27,31}} | collective-permute-start | bytes 786440 | tf_op jit(solution)/shard_map/ppermute | solution.py:29
  46.8 24.2 %collective-permute-start.15 = (f32[4,128,128]{2,1,0:T(8,128)}, f32[4,128,128]{2,1,0:T(8,128)}, u32[]{:S(2)}, u32[]{:S(2)}) collective-permute-start(f32[4,128,128]{2,1,0:T(8,128)} %get-tuple-element.15), channel_id=1, source_target_pairs={{8,12},{10,14},{9,13},{11,15},{24,28},{26,30},{25,29},{27,31}} | collective-permute-start | bytes 786440 | tf_op jit(solution)/shard_map/ppermute | solution.py:29
  71.0 3.0 %copy-start.3 = (f32[2048]{0:T(1024)S(1)}, f32[2048]{0:T(1024)}, u32[]{:S(2)}) copy-start(f32[2048]{0:T(1024)} %param.7) | copy-start | bytes 24580
  73.6 9.9 %collective-permute-start.16 = (bf16[16,128,128]{2,1,0:T(8,128)(2,1)S(1)}, bf16[16,128,128]{2,1,0:T(8,128)(2,1)S(1)}, u32[]{:S(2)}, u32[]{:S(2)}) collective-permute-start(bf16[16,128,128]{2,1,0:T(8,128)(2,1)S(1)} %pad_maximum_fusion), channel_id=1, source_target_pairs={{0,2},{4,6},{8,10},{12,14},{2,0},{6,4},{10,8},{14,12},{1,3},{5,7},... | collective-permute-start | bytes 1572872 | tf_op jit(solution)/shard_map/ppermute | solution.py:33
  74.0 1.2 %collective-permute-start.17 = (f32[2048]{0:T(1024)S(1)}, f32[2048]{0:T(1024)S(1)}, u32[]{:S(2)}, u32[]{:S(2)}) collective-permute-start(f32[2048]{0:T(1024)S(1)} %copy-done.3), channel_id=1, source_target_pairs={{0,1},{1,0},{2,3},{3,2},{4,5},{5,4},{6,7},{7,6},{8,9},{9,8},{10,11... | collective-permute-start | bytes 24584 | tf_op jit(solution)/shard_map/ppermute | solution.py:197
  83.5 0.8 copy-start.2
